TPU v7x, 32 devices: a whole 2x2x4 slice. The times are simulated.
32 devices in a mesh: tm: 4 (over y, x), series: 8 (over z, core).
Axes of the slice: x: 2, y: 2, z: 4, core: 2. Of those that a mesh axis runs over, the one named last changes fastest.
Arguments:
- codes: int32 [8, 512], P(None, ('tm', 'series')), may hold values from 0 to 916478, as said below
- owner_slot: int32 [8], replicated, may hold values from 0 to 7, each once
- edges: int32 [4096], replicated, may hold values from 0 to 2096640, as said below
- w_in: bfloat16 [128, 2304], replicated, may hold values from -0.09375 to 0.09375
- w_dt: bfloat16 [128, 32], replicated, may hold values from -0.5 to 0.5
- dt_bias: float32 [32], replicated, may hold values from -1 to 1
- decay_rate: float32 [32], replicated, may hold values from 1e-05 to 0.1
- grad_out: bfloat16 [8, 512, 2048], P('series', 'tm'), may hold values from -6 to 6
Outputs:
- ssd_output: bfloat16 [8, 512, 2048], P('series', 'tm')
- grad_in: float32 [128, 2304], replicated
Inputs may be any that keep to these rules, and one draw needn't show every extreme that they name: `codes`: each row is one series in the order of ingestion slots. edges[0] is 0 and edges rise strictly.
All inputs are finite; a program needn't handle non-finite values.
Results may differ from a plain program's by a relative error of at most 0.0062.
The roundings to bfloat16 on the way count: a program that leaves them out, or rounds other values in their place, can miss the bound.
Values sent between devices are 32-bit elements; how exact they have to be, the bound alone decides.
No kernel may reach another device: no remote copies, remote signals or barrier semaphores. Data moves between devices by JAX's collectives and lax.ppermute only.
A program may use at most 128 MiB of HBM per device.

v0:
```python
import math

import jax
import jax.numpy as jnp
from jax import lax
from jax.sharding import PartitionSpec as P

code_ceiling = 2097152.0


def carried_in(array, axis, combine, identity, reverse):
    count, position = (lax.axis_size(axis), lax.axis_index(axis))
    everything = jax.tree.map(lambda part: lax.all_gather(part, axis), array)
    start = jax.tree.map(
        lambda part, zero: jnp.broadcast_to(jnp.asarray(zero, part.dtype), part.shape),
        array,
        identity,
    )

    def lap(k, before):
        at = count - 1 - k if reverse else k
        reached = at > position if reverse else at < position
        new = combine(before, jax.tree.map(lambda part: part[at], everything))
        return jax.tree.map(lambda a, b: jnp.where(reached, a, b), new, before)

    return lax.fori_loop(0, count, lap, start)


def decay_matrix(cum_decay):
    row_count = cum_decay.shape[0]
    causal = jnp.arange(row_count)[:, None] >= jnp.arange(row_count)[None, :]
    log_span = cum_decay.T[:, :, None] - cum_decay.T[:, None, :]
    return jnp.where(causal[None], jnp.exp(jnp.where(causal[None], log_span, -60.0)), 0.0)


def carry_combine(earlier, later):
    return (earlier[0] * later[0], later[0][:, None, None] * earlier[1] + later[1])


def on_device(codes, owner_slot, edges, w_in, w_dt, dt_bias, decay_rate, grad_out):
    fl = jnp.float32
    half = jnp.bfloat16
    tok_rows = grad_out.shape[1]
    head_count = dt_bias.shape[0]
    inner_width = grad_out.shape[2]
    head_dim = inner_width // head_count
    state_dim = (w_in.shape[1] - inner_width) // 2
    seq_len = tok_rows * lax.axis_size("tm")
    series_count = lax.axis_size("series")
    ordered = jnp.take(codes, owner_slot, axis=0).astype(fl)
    own_series = lax.all_to_all(ordered, "series", split_axis=0, concat_axis=1, tiled=True)
    reading = own_series[0]
    edge_float = edges.astype(fl)
    upper_edge = jnp.concatenate([edge_float[1:], jnp.full((1,), code_ceiling, fl)])
    onehot = (
        (edge_float[None, :] <= reading[:, None]) & (upper_edge[None, :] > reading[:, None])
    ).astype(fl)
    counts = lax.psum(jnp.sum(onehot, axis=0), "tm")
    before = jnp.cumsum(counts) - counts
    bin_table = jnp.stack([before, counts, edge_float, upper_edge - edge_float], axis=1)
    picked = jnp.dot(onehot, bin_table, precision=lax.Precision.HIGHEST)
    within_bin = (reading - picked[:, 2]) / picked[:, 3]
    quantile = (picked[:, 0] + picked[:, 1] * within_bin) / seq_len
    frequency = (jnp.arange(w_in.shape[0], dtype=fl) + 0.5) * math.pi
    features = jnp.cos(quantile[:, None] * frequency).astype(half)
    projected = jnp.dot(features, w_in, preferred_element_type=fl).astype(half)
    x_heads = projected[:, :inner_width].reshape(tok_rows, head_count, head_dim)
    b_proj = projected[:, inner_width : inner_width + state_dim]
    c_proj = projected[:, inner_width + state_dim :]
    step_size = jax.nn.softplus(dt_bias + jnp.dot(features, w_dt, preferred_element_type=fl))
    cum_decay = jnp.cumsum(-step_size * decay_rate, axis=0)
    tail_factor = jnp.exp(cum_decay[-1][None, :] - cum_decay) * step_size
    head_factor = jnp.exp(cum_decay)
    grad_heads = grad_out[0].reshape(tok_rows, head_count, head_dim)
    masked = decay_matrix(cum_decay) * step_size.T[:, None, :]
    scores = jnp.dot(c_proj, b_proj.T, preferred_element_type=fl)
    weights = (scores[None] * masked).astype(half)
    x_weighted = (x_heads * tail_factor[:, :, None]).astype(half)
    state_local = jnp.einsum("thp,tn->hpn", x_weighted, b_proj, preferred_element_type=fl)
    block_gate = jnp.exp(cum_decay[-1])
    grad_weighted = (grad_heads * head_factor[:, :, None]).astype(half)
    adjoint_local = jnp.einsum("thp,tn->hpn", grad_weighted, c_proj, preferred_element_type=fl)
    identity = (jnp.ones((head_count,), fl), jnp.zeros((head_count, head_dim, state_dim), fl))
    _, state_in = carried_in((block_gate, state_local), "tm", carry_combine, identity, False)
    _, adjoint_in = carried_in((block_gate, adjoint_local), "tm", carry_combine, identity, True)
    state_half = state_in.astype(half)
    adjoint_half = adjoint_in.astype(half)
    output = jnp.einsum("hts,shp->thp", weights, x_heads, preferred_element_type=fl)
    output = (
        output
        + jnp.einsum("tn,hpn->thp", c_proj, state_half, preferred_element_type=fl)
        * head_factor[:, :, None]
    )
    ssd_output = output.reshape(1, tok_rows, inner_width).astype(half)
    grad_x = jnp.einsum("hts,thp->shp", weights, grad_heads, preferred_element_type=fl)
    grad_x = (
        grad_x
        + jnp.einsum("sn,hpn->shp", b_proj, adjoint_half, preferred_element_type=fl)
        * tail_factor[:, :, None]
    )
    pair_scores = jnp.einsum("thp,shp->hts", grad_heads, x_heads, preferred_element_type=fl)
    pair_mixed = jnp.sum(pair_scores * masked, axis=0).astype(half)
    grad_b = jnp.dot(pair_mixed.T, c_proj, preferred_element_type=fl)
    grad_b = grad_b + jnp.einsum("shp,hpn->sn", x_weighted, adjoint_half, preferred_element_type=fl)
    grad_c = jnp.dot(pair_mixed, b_proj, preferred_element_type=fl)
    grad_c = grad_c + jnp.einsum(
        "thp,hpn->tn", grad_weighted, state_half, preferred_element_type=fl
    )
    grad_rows = jnp.concatenate(
        [
            grad_x.reshape(tok_rows, inner_width).astype(half),
            grad_b.astype(half),
            grad_c.astype(half),
        ],
        axis=1,
    )
    local_grad = jnp.einsum("tf,tw->fw", features, grad_rows, preferred_element_type=fl)
    share_grad = lax.psum_scatter(local_grad, "series", scatter_dimension=1, tiled=True)
    share_grad = lax.psum(share_grad, "tm")
    total_grad = lax.all_gather(share_grad, "series", axis=1, tiled=True)
    grad_in = total_grad / math.sqrt(series_count * seq_len)
    return (ssd_output, grad_in)


def solution(mesh):
    return jax.shard_map(
        on_device,
        mesh=mesh,
        in_specs=(P(None, ("tm", "series")), P(), P(), P(), P(), P(), P(), P("series", "tm", None)),
        out_specs=(P("series", "tm", None), P()),
        check_vma=False,
    )
```

profile of v0, /device:TPU:1, one launch (start us, length us, event | category | flops | bytes accessed | tf_op | source)
XLA Modules:
  0.0 266.8 jit_solution(18337310911339434361)
XLA Ops:
  7.2 0.7 compare_select_fusion.2
  7.9 0.7 compare_and_fusion.2
  8.6 1.2 gather_fusion
  9.8 0.7 fusion.61
  10.5 6.4 %all-to-all-start = ((f32[8,1,16]{2,1,0:T(1,128)}), f32[8,1,16]{2,1,0:T(1,128)S(1)}, u32[]{:S(2)}, u32[]{:S(2)}) async-start(f32[8,1,16]{2,1,0:T(1,128)} %bitcast.1), calls=%async_computation | async-start | bytes 8192 | tf_op jit(solution)/shard_map/all_to_all | solution.py:51
  16.9 0.7 convert_element_type.72
  17.7 0.8 convert_subtract_fusion
  18.5 1.3 copy.58
  19.8 1.8 all-to-all-done
  21.6 0.5 broadcast.88
  22.2 0.7 reduce.7
  22.9 0.4 convert_reduce_fusion
  23.4 12.3 %psum.14 = f32[4096]{0:T(1024)S(1)} all-reduce(f32[4096]{0:T(1024)S(1)} %convert_reduce_fusion), channel_id=1, replica_groups=mesh['tm'=4,'series'=8] {'tm'}, use_global_device_ids=true, to_apply=%region_1.2 | all-reduce | flops 4096 | bytes 32768 | tf_op jit(solution)/shard_map/psum | solution.py:58
  36.3 1.2 fusion.3
  37.6 0.6 convolution_convert_fusion
  38.2 0.4 compare_select_fusion
  39.1 1.3 fusion.22
  41.0 1.3 fusion.21
  42.5 5.0 %all-gather.2 = f32[4,1,32]{2,1,0:T(1,128)S(1)} all-gather(f32[1,1,32]{2,1,0:T(1,128)S(1)} %get-tuple-element.295), channel_id=1, replica_groups=mesh['tm'=4,'series'=8] {'tm'}, dimensions={0}, use_global_device_ids=true | all-gather | bytes 640 | tf_op jit(solution)/shard_map/all_gather | solution.py:13
  47.5 0.9 fusion.48
  48.4 2.6 fusion.2
  51.0 1.0 fusion.51
  52.0 1.0 fusion.45
  52.9 2.3 convolution_bitcast_fusion
  55.3 38.8 %all-gather.11.cloned.1.call-done = f32[128,64,128]{2,1,0:T(8,128)} async-done(((f32[32,64,128]{2,1,0:T(8,128)}), f32[128,64,128]{2,1,0:T(8,128)}) %all-gather.11.cloned.1.call-update) | async-done | bytes 4194320 | tf_op jit(solution)/shard_map/all_gather | solution.py:13
  94.1 6.0 %while.31 = (s32[]{:T(128)}, f32[32,64,128]{2,1,0:T(8,128)S(1)}, s32[]{:T(128)}, f32[4,32]{1,0:T(4,128)S(1)}, f32[4,32,64,128]{3,2,1,0:T(8,128)}, /*index=5*/s32[]{:T(128)}, s32[]{:T(128)}, s32[]{:T(128)}, s32[]{:T(128)}) while((s32[]{:T(128)}, f32[32,64,128]{2,1,0:T(8,128)S(1)}, s32[]{:T(128)}, f32[4,32]{1,0:T(4,128)S(1)}, ...), condition=%wide.region_8.9_spmd.clone, body=%wide.region_7.8_spmd.clone.sunk | while | flops 1048584 | bytes 3146279 | solution.py:26
  94.1 1.5 fusion.79
  95.6 1.5 fusion.79
  97.1 1.5 fusion.79
  98.6 1.5 fusion.79
  100.1 1.5 fusion.10
  101.6 1.9 fusion.7
  103.5 45.2 %all-gather.9.cloned.1.call-done = f32[128,64,128]{2,1,0:T(8,128)} async-done(((f32[32,64,128]{2,1,0:T(8,128)}), f32[128,64,128]{2,1,0:T(8,128)}) %all-gather.9.cloned.1.call-update) | async-done | bytes 4194320 | tf_op jit(solution)/shard_map/all_gather | solution.py:13
  148.7 6.0 %while.30 = (s32[]{:T(128)}, f32[32,64,128]{2,1,0:T(8,128)S(1)}, s32[]{:T(128)}, f32[4,32]{1,0:T(4,128)S(1)}, f32[4,32,64,128]{3,2,1,0:T(8,128)}, /*index=5*/s32[]{:T(128)}, s32[]{:T(128)}) while((s32[]{:T(128)}, f32[32,64,128]{2,1,0:T(8,128)S(1)}, s32[]{:T(128)}, f32[4,32]{1,0:T(4,128)S(1)}, f32[4,32,64,128]{3,2,1,0:T(8,128)}, ...), condition=%wide.region_6.7_spmd.clone, body=%wide.region_5.6_spmd.clone.sunk | while | flops 1048580 | bytes 3146217 | solution.py:26
  148.7 1.5 fusion.78
  150.2 1.5 fusion.78
  151.7 1.5 fusion.78
  153.2 1.5 fusion.78
  154.7 0.4 fusion.11
  155.1 1.6 fusion.15
  156.8 29.4 %reduce-scatter.2.cloned.1.call-done = f32[128,288]{0,1:T(8,128)} async-done(((f32[128,2304]{0,1:T(8,128)}), f32[128,288]{0,1:T(8,128)}) %reduce-scatter.2.cloned.1.call-update) | async-done | bytes 147472 | tf_op jit(solution)/shard_map/reduce_scatter | solution.py:118
  186.3 46.2 %all-reduce.2.cloned.1.call-done = f32[128,288]{0,1:T(8,128)} async-done(((f32[128,288]{0,1:T(8,128)}), f32[128,288]{0,1:T(8,128)}) %all-reduce.2.cloned.1.call-update) | async-done | bytes 147472 | tf_op jit(solution)/shard_map/psum | solution.py:119
  232.5 1.3 convolution_bitcast_fusion.1
  233.8 1.1 fusion.6
  234.8 1.0 copy.60
  235.8 21.7 %all-gather.7.cloned.1.call-done = f32[128,2304]{0,1:T(8,128)} async-done(((f32[128,288]{0,1:T(8,128)}), f32[128,2304]{0,1:T(8,128)}) %all-gather.7.cloned.1.call-update) | async-done | bytes 1179664 | tf_op jit(solution)/shard_map/all_gather | solution.py:120
  257.6 1.3 broadcast_multiply_fusion
  258.9 1.4 copy.61
  (61 shorter events, 2.2 us)
Async XLA Ops:
  7.2 30.4 %copy-start = (bf16[128,2304]{1,0:T(8,128)(2,1)S(1)}, bf16[128,2304]{1,0:T(8,128)(2,1)}, u32[]{:S(2)}) copy-start(bf16[128,2304]{1,0:T(8,128)(2,1)} %param.15) | copy-start | bytes 1769476
  10.5 11.2 %all-to-all-start = ((f32[8,1,16]{2,1,0:T(1,128)}), f32[8,1,16]{2,1,0:T(1,128)S(1)}, u32[]{:S(2)}, u32[]{:S(2)}) async-start(f32[8,1,16]{2,1,0:T(1,128)} %bitcast.1), calls=%async_computation | async-start | bytes 8192 | tf_op jit(solution)/shard_map/all_to_all | solution.py:51
  16.9 77.2 %all-gather.11.cloned.1.call-start = ((), (), s32[]{:S(2)}) async-start(), calls=%async_computation.6 | async-start | bytes 5242880 | tf_op jit(solution)/shard_map/all_gather | solution.py:13
  18.5 19.7 %copy-start.7 = (bf16[128,32]{0,1:T(8,128)(2,1)S(1)}, bf16[128,32]{0,1:T(8,128)(2,1)}, u32[]{:S(2)}) copy-start(bf16[128,32]{0,1:T(8,128)(2,1)} %param.16) | copy-start | bytes 24580
  18.5 19.7 %copy-start.8 = (f32[32]{0:T(128)S(1)}, f32[32]{0:T(128)}, u32[]{:S(2)}) copy-start(f32[32]{0:T(128)} %param.17) | copy-start | bytes 388
  18.5 20.2 %copy-start.6 = (f32[32]{0:T(128)S(1)}, f32[32]{0:T(128)}, u32[]{:S(2)}) copy-start(f32[32]{0:T(128)} %param.18) | copy-start | bytes 388
  38.2 2.7 %copy-start.3 = (bf16[128,2304]{1,0:T(8,128)(2,1)}, bf16[128,2304]{1,0:T(8,128)(2,1)S(1)}, u32[]{:S(2)}) copy-start(bf16[128,2304]{1,0:T(8,128)(2,1)S(1)} %convolution_convert_fusion) | copy-start | bytes 1769476
  40.4 108.3 %all-gather.9.cloned.1.call-start = ((), (), s32[]{:S(2)}) async-start(), calls=%async_computation.5 | async-start | bytes 5242880 | tf_op jit(solution)/shard_map/all_gather | solution.py:13
  40.8 1.5 copy-start.1
  42.3 143.9 %reduce-scatter.2.cloned.1.call-start = ((), (), s32[]{:S(2)}) async-start(), calls=%async_computation.2 | async-start | bytes 1327104 | tf_op jit(solution)/shard_map/reduce_scatter | solution.py:118
  100.1 1.5 copy-start.5
  148.7 6.4 %copy-start.4 = (bf16[128,32,64]{0,2,1:T(8,128)(2,1)S(1)}, bf16[128,32,64]{0,2,1:T(8,128)(2,1)}, u32[]{:S(2)}) copy-start(bf16[128,32,64]{0,2,1:T(8,128)(2,1)} %fusion.7) | copy-start | bytes 1572868
  154.7 77.7 %copy-start.2 = (bf16[128,2048]{0,1:T(8,128)(2,1)S(1)}, bf16[128,2048]{0,1:T(8,128)(2,1)}, u32[]{:S(2)}) copy-start(bf16[128,2048]{0,1:T(8,128)(2,1)} %copy-done.1) | copy-start | bytes 1572868
  156.7 75.7 %all-reduce.2.cloned.1.call-start = ((), (), s32[]{:S(2)}) async-start(), calls=%async_computation.3 | async-start | bytes 294912 | tf_op jit(solution)/shard_map/psum | solution.py:119
  186.2 71.4 %all-gather.7.cloned.1.call-start = ((), (), s32[]{:S(2)}) async-start(), calls=%async_computation.4 | async-start | bytes 1327104 | tf_op jit(solution)/shard_map/all_gather | solution.py:120
Sparse Core Ops, SparseCore 0:
  40.5 53.5 all-gather.10
  95.9 52.6 all-gather.8
  156.8 29.3 reduce-scatter.1
  189.0 43.4 all-reduce.1
  234.0 23.5 all-gather.6
where the time goes:
time: 268 us; the launch traced here: 267 us
  waiting for transfers between devices  183 us (68%)
  matrix products  20.3 us (8%)
  other arithmetic  18.5 us (7%)
  blocking collectives  17.3 us (6%)
  between operations  14.1 us (5%)
  local copies, waits for them, and re-layouts  6.62 us (2%)
  starting transfers between devices  6.54 us (2%)
    all_gather x2, waiting for transfers between devices, carried_in(): everything = jax.tree.map(lambda part: lax.all_gather(part, axis), array)  84 us
    psum x1, waiting for transfers between devices, on_device(): share_grad = lax.psum(share_grad, 'tm')  46.2 us
    reduce_scatter x1, waiting for transfers between devices, on_device(): lax.psum_scatter(local_grad, 'series', scatter_dimension=1, tiled=True)  29.4 us
    all_gather x1, waiting for transfers between devices, on_device(): total_grad = lax.all_gather(share_grad, 'series', axis=1, tiled=True)  21.7 us
    psum x1, blocking collectives, on_device(): counts = lax.psum(jnp.sum(onehot, axis=0), 'tm')  12.3 us
    select_n x8, other arithmetic, lap(): return jax.tree.map(lambda a, b: jnp.where(reached, a, b), new, before)  11.7 us
    all_to_all x1, starting transfers between devices, on_device(): lax.all_to_all(ordered, 'series', split_axis=0, concat_axis=1, tiled=True)  6.38 us
  transfers between devices with their start and end apart: 6, of which 6 were waited for; matrix products, arithmetic and copies ran while one was open for 9% of the time, Pallas kernels for 0%

commit v1 on v0

v1 whole, which is shorter than its diff:
```python
import math

import jax
import jax.numpy as jnp
from jax import lax
from jax.sharding import PartitionSpec as P

code_ceiling = 2097152.0


def decay_matrix(cum_decay):
    row_count = cum_decay.shape[0]
    causal = jnp.arange(row_count)[:, None] >= jnp.arange(row_count)[None, :]
    log_span = cum_decay.T[:, :, None] - cum_decay.T[:, None, :]
    return jnp.where(causal[None], jnp.exp(jnp.where(causal[None], log_span, -60.0)), 0.0)


def on_device(codes, owner_slot, edges, w_in, w_dt, dt_bias, decay_rate, grad_out):
    fl = jnp.float32
    half = jnp.bfloat16
    tok_rows = grad_out.shape[1]
    head_count = dt_bias.shape[0]
    inner_width = grad_out.shape[2]
    head_dim = inner_width // head_count
    state_dim = (w_in.shape[1] - inner_width) // 2
    n_blocks = lax.axis_size("tm")
    seq_len = tok_rows * n_blocks
    series_count = lax.axis_size("series")
    my_block = lax.axis_index("tm")
    my_series = lax.axis_index("series")

    all_codes = lax.all_gather(codes, ("tm", "series"), axis=1, tiled=True)
    row = lax.dynamic_index_in_dim(all_codes, owner_slot[my_series], axis=0, keepdims=False)
    reading = row.astype(fl)
    edge_float = edges.astype(fl)
    upper_edge = jnp.concatenate([edge_float[1:], jnp.full((1,), code_ceiling, fl)])
    onehot = (
        (edge_float[None, :] <= reading[:, None]) & (upper_edge[None, :] > reading[:, None])
    ).astype(fl)
    counts = jnp.sum(onehot, axis=0)
    before = jnp.cumsum(counts) - counts
    bin_table = jnp.stack([before, counts, edge_float, upper_edge - edge_float], axis=1)
    picked = jnp.dot(onehot, bin_table, precision=lax.Precision.HIGHEST)
    within_bin = (reading - picked[:, 2]) / picked[:, 3]
    quantile = (picked[:, 0] + picked[:, 1] * within_bin) / seq_len
    frequency = (jnp.arange(w_in.shape[0], dtype=fl) + 0.5) * math.pi
    features_all = jnp.cos(quantile[:, None] * frequency).astype(half)

    projected_all = jnp.dot(features_all, w_in, preferred_element_type=fl).astype(half)
    projected_all = projected_all.reshape(n_blocks, tok_rows, -1)
    x_all = projected_all[:, :, :inner_width].reshape(n_blocks, tok_rows, head_count, head_dim)
    b_all = projected_all[:, :, inner_width : inner_width + state_dim]
    c_all = projected_all[:, :, inner_width + state_dim :]
    step_all = jax.nn.softplus(
        dt_bias + jnp.dot(features_all, w_dt, preferred_element_type=fl)
    ).reshape(n_blocks, tok_rows, head_count)
    cum_all = jnp.cumsum(-step_all * decay_rate, axis=1)
    gate_all = jnp.exp(cum_all[:, -1])
    tail_all = jnp.exp(cum_all[:, -1:, :] - cum_all) * step_all
    xw_all = (x_all * tail_all[..., None]).astype(half)
    state_local_all = jnp.einsum("bthp,btn->bhpn", xw_all, b_all, preferred_element_type=fl)

    state_in = jnp.zeros((head_count, head_dim, state_dim), fl)
    for k in range(n_blocks - 1):
        new = gate_all[k][:, None, None] * state_in + state_local_all[k]
        state_in = jnp.where(k < my_block, new, state_in)

    def mine(a):
        return lax.dynamic_index_in_dim(a, my_block, axis=0, keepdims=False)

    features = mine(features_all.reshape(n_blocks, tok_rows, -1))
    x_heads = mine(x_all)
    b_proj = mine(b_all)
    c_proj = mine(c_all)
    step_size = mine(step_all)
    cum_decay = mine(cum_all)
    tail_factor = mine(tail_all)
    x_weighted = mine(xw_all)
    head_factor = jnp.exp(cum_decay)

    grad_heads = grad_out[0].reshape(tok_rows, head_count, head_dim)
    grad_weighted = (grad_heads * head_factor[:, :, None]).astype(half)
    adjoint_local = jnp.einsum("thp,tn->hpn", grad_weighted, c_proj, preferred_element_type=fl)
    adjoint_all = lax.all_gather(adjoint_local, "tm")
    adjoint_in = jnp.zeros((head_count, head_dim, state_dim), fl)
    for k in range(n_blocks - 1, 0, -1):
        new = gate_all[k][:, None, None] * adjoint_in + adjoint_all[k]
        adjoint_in = jnp.where(k > my_block, new, adjoint_in)

    masked = decay_matrix(cum_decay) * step_size.T[:, None, :]
    scores = jnp.dot(c_proj, b_proj.T, preferred_element_type=fl)
    weights = (scores[None] * masked).astype(half)
    state_half = state_in.astype(half)
    adjoint_half = adjoint_in.astype(half)
    output = jnp.einsum("hts,shp->thp", weights, x_heads, preferred_element_type=fl)
    output = (
        output
        + jnp.einsum("tn,hpn->thp", c_proj, state_half, preferred_element_type=fl)
        * head_factor[:, :, None]
    )
    ssd_output = output.reshape(1, tok_rows, inner_width).astype(half)
    grad_x = jnp.einsum("hts,thp->shp", weights, grad_heads, preferred_element_type=fl)
    grad_x = (
        grad_x
        + jnp.einsum("sn,hpn->shp", b_proj, adjoint_half, preferred_element_type=fl)
        * tail_factor[:, :, None]
    )
    pair_scores = jnp.einsum("thp,shp->hts", grad_heads, x_heads, preferred_element_type=fl)
    pair_mixed = jnp.sum(pair_scores * masked, axis=0).astype(half)
    grad_b = jnp.dot(pair_mixed.T, c_proj, preferred_element_type=fl)
    grad_b = grad_b + jnp.einsum("shp,hpn->sn", x_weighted, adjoint_half, preferred_element_type=fl)
    grad_c = jnp.dot(pair_mixed, b_proj, preferred_element_type=fl)
    grad_c = grad_c + jnp.einsum(
        "thp,hpn->tn", grad_weighted, state_half, preferred_element_type=fl
    )
    grad_rows = jnp.concatenate(
        [
            grad_x.reshape(tok_rows, inner_width).astype(half),
            grad_b.astype(half),
            grad_c.astype(half),
        ],
        axis=1,
    )
    local_grad = jnp.einsum("tf,tw->fw", features, grad_rows, preferred_element_type=fl)
    share_grad = lax.psum_scatter(local_grad, "series", scatter_dimension=1, tiled=True)
    share_grad = lax.psum(share_grad, "tm")
    total_grad = lax.all_gather(share_grad, "series", axis=1, tiled=True)
    grad_in = total_grad / math.sqrt(series_count * seq_len)
    return (ssd_output, grad_in)


def solution(mesh):
    return jax.shard_map(
        on_device,
        mesh=mesh,
        in_specs=(P(None, ("tm", "series")), P(), P(), P(), P(), P(), P(), P("series", "tm", None)),
        out_specs=(P("series", "tm", None), P()),
        check_vma=False,
    )
```

time: 268 us -> 245 us (0.914)
  waiting for transfers between devices: 183 us -> 118 us
  blocking collectives: 17.3 us -> 43.9 us
  local copies, waits for them, and re-layouts: 6.62 us -> 21.2 us
  matrix products: 20.3 us -> 27.7 us
  starting transfers between devices: 6.54 us -> 0.34 us
  other arithmetic: 18.5 us -> 15.3 us
    all_gather x2 -> x1, waiting for transfers between devices: 84 us -> 22.8 us  [on_device(): adjoint_all = lax.all_gather(adjoint_local, 'tm')]
    all_gather x1, blocking collectives: 5 us -> 43.9 us  [on_device(): all_codes = lax.all_gather(codes, ('tm', 'series'), axis=1, tiled=True)]
    select_n x9 -> x0, other arithmetic: 12.5 us -> none  [the longest x8 11.7 us: lap(): return jax.tree.map(lambda a, b: jnp.where(reached, a, b), new, before)]
    psum x1 -> x0, blocking collectives: 12.3 us -> none  [on_device(): counts = lax.psum(jnp.sum(onehot, axis=0), 'tm')]
    all_to_all x1 -> x0, starting transfers between devices: 6.38 us -> none  [on_device(): lax.all_to_all(ordered, 'series', split_axis=0, concat_axis=1, tiled=True)]
    dynamic_slice x0 -> x7, local copies, waits for them, and re-layouts: none -> 6.15 us  [the longest x6 4.86 us: mine(): return lax.dynamic_index_in_dim(a, my_block, axis=0, keepdims=False)]
    slice x3 -> x5, local copies, waits for them, and re-layouts: 0.41 us -> 6.29 us  [the longest x2 4.86 us: on_device(): projected_all[:, :, :inner_width]]
    convert_element_type x1 -> x4, other arithmetic: 0.67 us -> 5.43 us  [the longest x1 3.6 us: on_device(): adjoint_half = adjoint_in.astype(half)]
  transfers between devices with their start and end apart: 6 -> 4, of which waited for: 6 -> 4; matrix products, arithmetic and copies ran while one was open for 9% -> 13% of each run, Pallas kernels for 0% -> 0%
where the time goes in v1:
time: 245 us; the launch traced here: 243 us
  waiting for transfers between devices  118 us (48%)
  blocking collectives  43.9 us (18%)
  matrix products  27.7 us (11%)
  local copies, waits for them, and re-layouts  21.2 us (9%)
  between operations  16.2 us (7%)
  other arithmetic  15.3 us (6%)
    psum x1, waiting for transfers between devices, on_device(): share_grad = lax.psum(share_grad, 'tm')  46.4 us
    all_gather x1, blocking collectives, on_device(): all_codes = lax.all_gather(codes, ('tm', 'series'), axis=1, tiled=True)  43.9 us
    reduce_scatter x1, waiting for transfers between devices, on_device(): lax.psum_scatter(local_grad, 'series', scatter_dimension=1, tiled=True)  29.4 us
    all_gather x1, waiting for transfers between devices, on_device(): adjoint_all = lax.all_gather(adjoint_local, 'tm')  22.8 us
    all_gather x1, waiting for transfers between devices, on_device(): total_grad = lax.all_gather(share_grad, 'series', axis=1, tiled=True)  19.7 us
    unnamed x62, local copies, waits for them, and re-layouts  5.44 us
  transfers between devices with their start and end apart: 4, of which 4 were waited for; matrix products, arithmetic and copies ran while one was open for 13% of the time, Pallas kernels for 0%

profile of v1, /device:TPU:1, one launch (start us, length us, event | category | flops | bytes accessed | tf_op | source)
XLA Modules:
  0.0 243.2 jit_solution(498775291195324287)
XLA Ops:
  7.2 1.3 dynamic_slice.34
  9.8 43.9 %all-gather.1 = s32[32,16,8]{1,2,0:T(8,128)S(1)} all-gather(s32[1,16,8]{1,2,0:T(8,128)} %bitcast.172), channel_id=1, replica_groups=mesh['tm'=4,'series'=8] {'tm','series'}, dimensions={0}, use_global_device_ids=true | all-gather | bytes 16896 | tf_op jit(solution)/shard_map/all_gather | solution.py:32
  53.8 0.7 convert_element_type.97
  55.3 0.8 convert_subtract_fusion
  56.1 1.4 convert_reduce_fusion
  58.2 4.1 %fusion = f32[512,4]{0,1:T(4,128)S(1)} fusion(f32[4096]{0:T(1024)S(1)} %get-tuple-element.13, f32[4096]{0:T(1024)S(1)} %convert_element_type.97, f32[512]{0:T(512)S(1)} %bitcast.168, f32[4096,1]{0,1:T(1,128)S(1)} %bitcast.166, f32[4096,1]{0,1:T(1,128)S(1)} %bitcast.155, f32[4096,1]{0,1:T(1,128)S(1)} %bitcast.154, f32[4096,1]{0,1:T(1,128)S(1)} %sub.42), kind=kOutput, calls=%fused_computation.2 | convolution fusion | flops 107003904 | bytes 108544 | tf_op jit(solution)/shard_map/dot_general | solution.py:43
  62.4 1.6 convolution_convert_fusion
  64.1 1.1 compare_select_fusion
  65.4 0.7 negate_multiply_fusion
  66.1 1.2 reduce_window_sum.35
  67.3 0.8 fusion.97
  68.1 0.6 constant_dynamic-slice_fusion.3
  68.8 1.5 copy.57
  70.3 0.7 bitcast_exponential_fusion
  71.0 2.0 copy.61
  73.1 1.1 fusion.24
  74.2 0.8 copy-done.4
  75.0 2.0 fusion.59
  77.3 1.6 slice.98
  78.9 0.5 slice.101
  79.4 3.2 %copy.54 = bf16[4,128,2048]{1,2,0:T(8,128)(2,1)S(1)} copy(bf16[4,128,2048]{2,1,0:T(8,128)(2,1)} %slice.98) | data formatting | bytes 4194304 | tf_op jit(solution)/shard_map/slice | solution.py:51
  82.7 1.2 exp.26
  83.9 1.7 exponential_multiply_fusion
  85.6 1.0 copy.60
  86.7 0.9 constant_dynamic-slice_fusion
  87.5 0.7 copy.64
  88.2 1.2 constant_dynamic-slice_fusion.1
  89.4 0.9 fusion.64
  90.3 1.4 multiply_bitcast_fusion
  91.8 2.4 fusion.4
  94.2 1.0 fusion.66
  95.1 1.0 fusion.62
  96.2 2.3 convolution_bitcast_fusion
  98.5 0.7 multiply_convert_fusion
  99.2 3.6 %fusion.41 = f32[4,32,64,128]{3,2,1,0:T(8,128)} fusion(bf16[4,128,32,64]{1,3,2,0:T(8,128)(2,1)S(1)} %multiply_convert_fusion, bf16[4,128,2304]{2,1,0:T(8,128)(2,1)} %bitcast.143), kind=kOutput, calls=%fused_computation.67 | convolution fusion | flops 268435456 | bytes 6422528 | tf_op jit(solution)/shard_map/bthp,btn->bhpn/dot_general | solution.py:61
  102.8 22.8 %all-gather.7.cloned.1.call-done = f32[128,64,128]{2,1,0:T(8,128)} async-done(((f32[32,64,128]{2,1,0:T(8,128)}), f32[128,64,128]{2,1,0:T(8,128)}) %all-gather.7.cloned.1.call-update) | async-done | bytes 4194320 | tf_op jit(solution)/shard_map/all_gather | solution.py:84
  125.7 3.6 %fusion.15 = (bf16[1,32,64,128]{3,2,1,0:T(8,128)(2,1)S(1)}, bf16[1,32,64,128]{3,2,1,0:T(8,128)(2,1)S(1)}) fusion(f32[128,64,128]{2,1,0:T(8,128)} %all-gather.7.cloned.1.call-done, f32[32]{0:T(128)S(1)} %copy-done.19, f32[32]{0:T(128)S(1)} %copy-done.21, f32[32]{0:T(128)S(1)} %copy-done.22, pred[]{:T(512)S(6)} %lt.34, pred[]{:T(512)S(6)} %lt.33, pred[]{:T(512)S(6)} %lt.32, ...), kind=kLoop, calls=%fused_computation.30 | loop fusion | flops 4718592 | bytes 7340550 | tf_op jit(solution)/shard_map/convert_element_type | solution.py:94
  129.3 0.4 fusion.11
  129.7 1.1 fusion.8
  131.2 1.6 fusion.25
  132.9 29.4 %reduce-scatter.2.cloned.1.call-done = f32[128,288]{0,1:T(8,128)} async-done(((f32[128,2304]{0,1:T(8,128)}), f32[128,288]{0,1:T(8,128)}) %reduce-scatter.2.cloned.1.call-update) | async-done | bytes 147472 | tf_op jit(solution)/shard_map/reduce_scatter | solution.py:125
  162.3 46.4 %all-reduce.2.cloned.1.call-done = f32[128,288]{0,1:T(8,128)} async-done(((f32[128,288]{0,1:T(8,128)}), f32[128,288]{0,1:T(8,128)}) %all-reduce.2.cloned.1.call-update) | async-done | bytes 147472 | tf_op jit(solution)/shard_map/psum | solution.py:126
  208.8 3.3 %convolution_bitcast_fusion.1 = f32[128,32,64]{0,2,1:T(8,128)S(1)} fusion(f32[32,128]{1,0:T(8,128)S(1)} %bitcast.165, f32[32,128]{1,0:T(8,128)S(1)} %bitcast.159, f32[128,128]{0,1:T(8,128)S(1)} %copy-done.13, pred[128,128]{0,1:T(8,128)(4,1)S(1)} %copy-done.17, bf16[4,128,32,64]{1,3,2,0:T(8,128)(2,1)} %bitcast.145, s32[]{:T(128)S(6)} %select_n.83), kind=kOutput, calls=%fused_computation.17 | convolution fusion | flops 70254592 | bytes 1703940 | tf_op jit(solution)/shard_map/hts,shp->thp/dot_general | solution.py:95
  212.1 1.1 fusion.7
  213.2 1.0 copy.65
  214.2 19.7 %all-gather.5.cloned.1.call-done = f32[128,2304]{0,1:T(8,128)} async-done(((f32[128,288]{0,1:T(8,128)}), f32[128,2304]{0,1:T(8,128)}) %all-gather.5.cloned.1.call-update) | async-done | bytes 1179664 | tf_op jit(solution)/shard_map/all_gather | solution.py:127
  233.9 1.3 broadcast_multiply_fusion
  235.2 1.4 copy.66
  (82 shorter events, 2.0 us)
Async XLA Ops:
  7.2 55.2 %copy-start = (bf16[128,2304]{1,0:T(8,128)(2,1)S(1)}, bf16[128,2304]{1,0:T(8,128)(2,1)}, u32[]{:S(2)}) copy-start(bf16[128,2304]{1,0:T(8,128)(2,1)} %param.11) | copy-start | bytes 1769476
  7.2 118.5 %all-gather.7.cloned.1.call-start = ((), (), s32[]{:S(2)}) async-start(), calls=%async_computation.4 | async-start | bytes 5242880 | tf_op jit(solution)/shard_map/all_gather | solution.py:84
  9.8 54.2 %copy-start.23 = (f32[128]{0:T(128)}, f32[128]{0:T(128)S(1)}, u32[]{:S(2)}) copy-start(f32[128]{0:T(128)S(1)} %add_multiply_fusion) | copy-start | bytes 1540
  62.3 1.7 copy-start.27
  62.3 1.7 copy-start.28
  62.3 3.0 %copy-start.25 = (f32[32]{0:T(128)S(1)}, f32[32]{0:T(128)}, u32[]{:S(2)}) copy-start(f32[32]{0:T(128)} %param.14) | copy-start | bytes 388
  62.4 2.8 %copy-start.18 = (f32[512,1]{0,1:T(1,128)}, f32[512,1]{0,1:T(1,128)S(1)}, u32[]{:S(2)}) copy-start(f32[512,1]{0,1:T(1,128)S(1)} %fusion.89) | copy-start | bytes 6148
  64.1 13.2 %copy-start.1 = (bf16[512,2304]{1,0:T(8,128)(2,1)}, bf16[512,2304]{1,0:T(8,128)(2,1)S(1)}, u32[]{:S(2)}) copy-start(bf16[512,2304]{1,0:T(8,128)(2,1)S(1)} %convolution_convert_fusion) | copy-start | bytes 7077892
  67.3 11.6 %copy-start.7 = (f32[4,128,32]{2,1,0:T(8,128)}, f32[4,128,32]{2,1,0:T(8,128)S(1)}, u32[]{:S(2)}) copy-start(f32[4,128,32]{2,1,0:T(8,128)S(1)} %reduce_window_sum.35) | copy-start | bytes 196612
  74.2 0.8 copy-start.4
  77.0 85.2 %reduce-scatter.2.cloned.1.call-start = ((), (), s32[]{:S(2)}) async-start(), calls=%async_computation.1 | async-start | bytes 1327104 | tf_op jit(solution)/shard_map/reduce_scatter | solution.py:125
  79.4 12.3 %copy-start.6 = (bf16[1,128,2048]{1,2,0:T(8,128)(2,1)S(1)}, bf16[1,128,2048]{1,2,0:T(8,128)(2,1)}, u32[]{:S(2)}) copy-start(bf16[1,128,2048]{1,2,0:T(8,128)(2,1)} %copy.61) | copy-start | bytes 1572868
  82.7 11.5 %copy-start.2 = (bf16[4,128,2048]{1,2,0:T(8,128)(2,1)}, bf16[4,128,2048]{1,2,0:T(8,128)(2,1)S(1)}, u32[]{:S(2)}) copy-start(bf16[4,128,2048]{1,2,0:T(8,128)(2,1)S(1)} %copy.54) | copy-start | bytes 6291460
  89.4 6.7 %copy-start.14 = (f32[1,128,32]{1,0,2:T(1,128)}, f32[1,128,32]{1,0,2:T(1,128)S(1)}, u32[]{:S(2)}) copy-start(f32[1,128,32]{1,0,2:T(1,128)S(1)} %constant_dynamic-slice_fusion.2) | copy-start | bytes 49156
  89.4 6.7 %copy-start.16 = (pred[128,128]{0,1:T(8,128)(4,1)}, pred[128,128]{0,1:T(8,128)(4,1)S(1)}, u32[]{:S(2)}) copy-start(pred[128,128]{0,1:T(8,128)(4,1)S(1)} %iota_compare_fusion) | copy-start | bytes 49156
  90.3 5.8 %copy-start.12 = (f32[128,128]{0,1:T(8,128)}, f32[128,128]{0,1:T(8,128)S(1)}, u32[]{:S(2)}) copy-start(f32[128,128]{0,1:T(8,128)S(1)} %fusion.64) | copy-start | bytes 196612
  91.8 4.4 %copy-start.10 = (f32[1,128,32]{1,2,0:T(8,128)S(1)}, f32[1,128,32]{1,2,0:T(8,128)}, u32[]{:S(2)}) copy-start(f32[1,128,32]{1,2,0:T(8,128)} %copy.57) | copy-start | bytes 49156
  96.2 2.4 copy-start.3
  99.2 26.5 %copy-start.19 = (f32[32]{0:T(128)S(1)}, f32[32]{0:T(128)}, u32[]{:S(2)}) copy-start(f32[32]{0:T(128)} %get-tuple-element.14) | copy-start | bytes 388
  99.2 26.5 %copy-start.20 = (f32[32]{0:T(128)S(1)}, f32[32]{0:T(128)}, u32[]{:S(2)}) copy-start(f32[32]{0:T(128)} %get-tuple-element.15) | copy-start | bytes 388
  99.2 26.5 %copy-start.21 = (f32[32]{0:T(128)S(1)}, f32[32]{0:T(128)}, u32[]{:S(2)}) copy-start(f32[32]{0:T(128)} %get-tuple-element.16) | copy-start | bytes 388
  99.2 26.5 %copy-start.22 = (f32[32]{0:T(128)S(1)}, f32[32]{0:T(128)}, u32[]{:S(2)}) copy-start(f32[32]{0:T(128)} %get-tuple-element.17) | copy-start | bytes 388
  125.7 4.0 %copy-start.8 = (f32[128,32,64]{0,2,1:T(8,128)S(1)}, f32[128,32,64]{0,2,1:T(8,128)}, u32[]{:S(2)}) copy-start(f32[128,32,64]{0,2,1:T(8,128)} %convolution_bitcast_fusion) | copy-start | bytes 3145732
  125.7 4.0 %copy-start.9 = (f32[1,128,32]{1,2,0:T(8,128)S(1)}, f32[1,128,32]{1,2,0:T(8,128)}, u32[]{:S(2)}) copy-start(f32[1,128,32]{1,2,0:T(8,128)} %copy.64) | copy-start | bytes 49156
  129.3 1.5 copy-start.5
  129.3 1.9 copy-start.24
  129.3 1.9 copy-start.26
  130.8 78.0 %copy-start.11 = (f32[1,128,32]{1,2,0:T(8,128)S(1)}, f32[1,128,32]{1,2,0:T(8,128)}, u32[]{:S(2)}) copy-start(f32[1,128,32]{1,2,0:T(8,128)} %copy.57) | copy-start | bytes 49156
  130.8 78.0 %copy-start.13 = (f32[128,128]{0,1:T(8,128)S(1)}, f32[128,128]{0,1:T(8,128)}, u32[]{:S(2)}) copy-start(f32[128,128]{0,1:T(8,128)} %copy-done.12) | copy-start | bytes 196612
  130.8 78.0 %copy-start.15 = (f32[1,128,32]{1,0,2:T(1,128)S(1)}, f32[1,128,32]{1,0,2:T(1,128)}, u32[]{:S(2)}) copy-start(f32[1,128,32]{1,0,2:T(1,128)} %copy-done.14) | copy-start | bytes 49156
  130.8 78.0 %copy-start.17 = (pred[128,128]{0,1:T(8,128)(4,1)S(1)}, pred[128,128]{0,1:T(8,128)(4,1)}, u32[]{:S(2)}) copy-start(pred[128,128]{0,1:T(8,128)(4,1)} %copy-done.16) | copy-start | bytes 49156
  132.8 75.9 %all-reduce.2.cloned.1.call-start = ((), (), s32[]{:S(2)}) async-start(), calls=%async_computation.2 | async-start | bytes 294912 | tf_op jit(solution)/shard_map/psum | solution.py:126
  162.3 71.6 %all-gather.5.cloned.1.call-start = ((), (), s32[]{:S(2)}) async-start(), calls=%async_computation.3 | async-start | bytes 1327104 | tf_op jit(solution)/shard_map/all_gather | solution.py:127
Sparse Core Ops, SparseCore 0:
  77.1 48.4 all-gather.6
  132.9 29.2 reduce-scatter.1
  165.2 43.5 all-reduce.1
  210.3 23.5 all-gather.4

commit v2 on v1

--- a/solution.py
+++ b/solution.py
@@ -27,11 +27,10 @@
     seq_len = tok_rows * n_blocks
     series_count = lax.axis_size("series")
     my_block = lax.axis_index("tm")
-    my_series = lax.axis_index("series")
 
-    all_codes = lax.all_gather(codes, ("tm", "series"), axis=1, tiled=True)
-    row = lax.dynamic_index_in_dim(all_codes, owner_slot[my_series], axis=0, keepdims=False)
-    reading = row.astype(fl)
+    ordered = jnp.take(codes, owner_slot, axis=0).astype(fl)
+    own_block = lax.all_to_all(ordered, "series", split_axis=0, concat_axis=1, tiled=True)
+    reading = lax.all_gather(own_block, "tm", axis=1, tiled=True)[0]
     edge_float = edges.astype(fl)
     upper_edge = jnp.concatenate([edge_float[1:], jnp.full((1,), code_ceiling, fl)])
     onehot = (
@@ -46,11 +45,25 @@
     frequency = (jnp.arange(w_in.shape[0], dtype=fl) + 0.5) * math.pi
     features_all = jnp.cos(quantile[:, None] * frequency).astype(half)
 
+    def mine(a):
+        return lax.dynamic_index_in_dim(a, my_block, axis=0, keepdims=False)
+
+    features_blocks = features_all.reshape(n_blocks, tok_rows, -1)
+    features = mine(features_blocks)
+    projected = jnp.dot(features, w_in, preferred_element_type=fl).astype(half)
+    x_heads = projected[:, :inner_width].reshape(tok_rows, head_count, head_dim)
+    b_proj = projected[:, inner_width : inner_width + state_dim]
+    c_proj = projected[:, inner_width + state_dim :]
+    step_size = jax.nn.softplus(dt_bias + jnp.dot(features, w_dt, preferred_element_type=fl))
+    cum_decay = jnp.cumsum(-step_size * decay_rate, axis=0)
+    tail_factor = jnp.exp(cum_decay[-1][None, :] - cum_decay) * step_size
+    head_factor = jnp.exp(cum_decay)
+    x_weighted = (x_heads * tail_factor[:, :, None]).astype(half)
+
     projected_all = jnp.dot(features_all, w_in, preferred_element_type=fl).astype(half)
     projected_all = projected_all.reshape(n_blocks, tok_rows, -1)
     x_all = projected_all[:, :, :inner_width].reshape(n_blocks, tok_rows, head_count, head_dim)
     b_all = projected_all[:, :, inner_width : inner_width + state_dim]
-    c_all = projected_all[:, :, inner_width + state_dim :]
     step_all = jax.nn.softplus(
         dt_bias + jnp.dot(features_all, w_dt, preferred_element_type=fl)
     ).reshape(n_blocks, tok_rows, head_count)
@@ -64,19 +77,6 @@
     for k in range(n_blocks - 1):
         new = gate_all[k][:, None, None] * state_in + state_local_all[k]
         state_in = jnp.where(k < my_block, new, state_in)
-
-    def mine(a):
-        return lax.dynamic_index_in_dim(a, my_block, axis=0, keepdims=False)
-
-    features = mine(features_all.reshape(n_blocks, tok_rows, -1))
-    x_heads = mine(x_all)
-    b_proj = mine(b_all)
-    c_proj = mine(c_all)
-    step_size = mine(step_all)
-    cum_decay = mine(cum_all)
-    tail_factor = mine(tail_all)
-    x_weighted = mine(xw_all)
-    head_factor = jnp.exp(cum_decay)
 
     grad_heads = grad_out[0].reshape(tok_rows, head_count, head_dim)
     grad_weighted = (grad_heads * head_factor[:, :, None]).astype(half)

time: 245 us -> 210 us (0.86)
  blocking collectives: 43.9 us -> 5.9 us
  starting transfers between devices: 0.34 us -> 6.9 us
  local copies, waits for them, and re-layouts: 21.2 us -> 25.3 us
  waiting for transfers between devices: 118 us -> 114 us
    all_gather x1, blocking collectives: 43.9 us -> 5.9 us  [on_device(): reading = lax.all_gather(own_block, 'tm', axis=1, tiled=True)[0]]
    convert_element_type x0 -> x2, local copies, waits for them, and re-layouts: none -> 7.71 us  [the longest x1 5.66 us: on_device(): xw_all = (x_all * tail_all[..., None]).astype(half)]
    all_gather x1, waiting for transfers between devices: 22.8 us -> 15.7 us  [on_device(): adjoint_all = lax.all_gather(adjoint_local, 'tm')]
    all_to_all x0 -> x1, starting transfers between devices: none -> 6.38 us  [on_device(): lax.all_to_all(ordered, 'series', split_axis=0, concat_axis=1, tiled=True)]
    dynamic_slice x6 -> x1, local copies, waits for them, and re-layouts: 4.86 us -> 0.01 us  [mine(): return lax.dynamic_index_in_dim(a, my_block, axis=0, keepdims=False)]
    slice x4, local copies, waits for them, and re-layouts: 5.75 us -> 1.08 us  [the longest x3 1 us: on_device(): x_heads = projected[:, :inner_width].reshape(tok_rows, head_count, head_dim)]
    mul x0 -> x3, local copies, waits for them, and re-layouts: none -> 3.76 us  [the longest x2 3.67 us: on_device(): jnp.einsum('sn,hpn->shp', b_proj, adjoint_half, preferred_element_type=fl)]
    dot_general x1, matrix products: 3.59 us -> 0.7 us  [on_device(): jnp.einsum('bthp,btn->bhpn', xw_all, b_all, preferred_element_type=fl)]
  transfers between devices with their start and end apart: 4 -> 5, of which waited for: 4 -> 5; matrix products, arithmetic and copies ran while one was open for 13% -> 20% of each run, Pallas kernels for 0% -> 0%
where the time goes in v2:
time: 210 us; the launch traced here: 209 us
  waiting for transfers between devices  114 us (54%)
  matrix products  26.5 us (13%)
  local copies, waits for them, and re-layouts  25.3 us (12%)
  other arithmetic  16.4 us (8%)
  between operations  14.3 us (7%)
  starting transfers between devices  6.9 us (3%)
  blocking collectives  5.9 us (3%)
    psum x1, waiting for transfers between devices, on_device(): share_grad = lax.psum(share_grad, 'tm')  46 us
    reduce_scatter x1, waiting for transfers between devices, on_device(): lax.psum_scatter(local_grad, 'series', scatter_dimension=1, tiled=True)  29.5 us
    all_gather x1, waiting for transfers between devices, on_device(): total_grad = lax.all_gather(share_grad, 'series', axis=1, tiled=True)  20.4 us
    all_gather x1, waiting for transfers between devices, on_device(): adjoint_all = lax.all_gather(adjoint_local, 'tm')  15.7 us
    all_to_all x1, starting transfers between devices, on_device(): lax.all_to_all(ordered, 'series', split_axis=0, concat_axis=1, tiled=True)  6.38 us
    unnamed x79, local copies, waits for them, and re-layouts  6.36 us
    all_gather x1, blocking collectives, on_device(): reading = lax.all_gather(own_block, 'tm', axis=1, tiled=True)[0]  5.9 us
    convert_element_type x1, local copies, waits for them, and re-layouts, on_device(): xw_all = (x_all * tail_all[..., None]).astype(half)  5.66 us
  transfers between devices with their start and end apart: 5, of which 5 were waited for; matrix products, arithmetic and copies ran while one was open for 20% of the time, Pallas kernels for 0%

profile of v2, /device:TPU:1, one launch (start us, length us, event | category | flops | bytes accessed | tf_op | source)
XLA Modules:
  0.0 208.9 jit_solution(4456451901641016910)
XLA Ops:
  7.2 0.7 compare_select_fusion.3
  7.9 0.7 compare_and_fusion.2
  8.6 1.2 gather_fusion
  9.8 0.7 fusion.90
  10.5 6.4 %all-to-all-start = ((f32[8,1,16]{2,1,0:T(1,128)}), f32[8,1,16]{2,1,0:T(1,128)S(1)}, u32[]{:S(2)}, u32[]{:S(2)}) async-start(f32[8,1,16]{2,1,0:T(1,128)} %bitcast.1), calls=%async_computation | async-start | bytes 8192 | tf_op jit(solution)/shard_map/all_to_all | solution.py:32
  16.9 0.7 convert_element_type.109
  17.7 0.8 convert_subtract_fusion
  18.5 1.3 copy.80
  19.8 1.9 all-to-all-done
  22.2 0.7 reduce.5
  22.9 5.9 %all_gather.12 = f32[1,512]{1,0:T(1,128)S(1)} all-gather(f32[1,128]{1,0:T(1,128)S(1)} %all_to_all.11), channel_id=1, replica_groups=mesh['tm'=4,'series'=8] {'tm'}, dimensions={1}, use_global_device_ids=true | all-gather | bytes 2560 | tf_op jit(solution)/shard_map/all_gather | solution.py:33
  28.8 1.4 convert_reduce_fusion
  30.9 4.1 %fusion = f32[512,4]{0,1:T(4,128)S(1)} fusion(f32[4096]{0:T(1024)S(1)} %get-tuple-element.11, f32[4096]{0:T(1024)S(1)} %convert_element_type.109, f32[512]{0:T(512)S(1)} %bitcast.189, f32[4096,1]{0,1:T(1,128)S(1)} %bitcast.190, f32[4096,1]{0,1:T(1,128)S(1)} %bitcast.184, f32[4096,1]{0,1:T(1,128)S(1)} %bitcast.183, f32[4096,1]{0,1:T(1,128)S(1)} %sub.52), kind=kOutput, calls=%fused_computation.3 | convolution fusion | flops 107003904 | bytes 108544 | tf_op jit(solution)/shard_map/dot_general | solution.py:42
  35.8 1.0 compare_select_fusion.1
  37.8 1.3 fusion.30
  40.0 0.9 fusion.15
  40.9 0.7 copy.82
  41.6 1.1 compare_select_fusion
  43.7 0.7 copy.78
  44.5 1.6 convolution_convert_fusion
  46.1 2.5 %slice_convert_fusion = f32[4,128,2048]{2,1,0:T(8,128)} fusion(bf16[4,128,2304]{2,1,0:T(8,128)(2,1)S(1)} %bitcast.166), kind=kLoop, calls=%fused_computation.11 | loop fusion | flops 1048576 | bytes 6291456 | tf_op jit(solution)/shard_map/convert_element_type | solution.py:73
  48.6 5.7 %copy.76 = f32[4,128,2048]{1,2,0:T(8,128)} copy(f32[4,128,2048]{2,1,0:T(8,128)} %slice_convert_fusion) | data formatting | bytes 8388608 | tf_op jit(solution)/shard_map/convert_element_type | solution.py:73
  54.3 1.0 copy.69
  55.3 1.6 copy.72
  56.9 0.7 slice_bitcast_fusion.2
  57.5 0.8 exponential_multiply_fusion.1
  59.0 1.0 mul.245
  60.0 2.6 %copy.83 = f32[128,2048]{1,0:T(8,128)} copy(f32[128,2048]{0,1:T(8,128)} %bitcast.171) | data formatting | bytes 2097152 | tf_op jit(solution)/shard_map/mul | solution.py:105
  62.6 2.1 %multiply_convert_fusion.3 = bf16[128,2048]{1,0:T(8,128)(2,1)} fusion(f32[128,2048]{1,0:T(8,128)} %copy.83, bf16[128,2304]{1,0:T(8,128)(2,1)S(1)} %copy-done.3), kind=kLoop, calls=%fused_computation.50 | loop fusion | flops 786432 | bytes 2097152 | tf_op jit(solution)/shard_map/convert_element_type | solution.py:61
  64.8 2.0 copy.84
  66.8 1.4 multiply_bitcast_fusion
  68.2 2.9 %fusion.5 = bf16[128,128]{0,1:T(8,128)(2,1)S(1)} fusion(bf16[128,32,64]{0,2,1:T(8,128)(2,1)} %bitcast.176, bf16[128,32,64]{0,2,1:T(8,128)(2,1)} %bitcast.169, f32[32,128]{1,0:T(8,128)} %get-tuple-element.16, f32[32,128]{1,0:T(8,128)} %copy.72, pred[128,128]{0,1:T(8,128)(4,1)} %iota_compare_fusion), kind=kOutput, calls=%fused_computation.13 | convolution fusion | flops 70238208 | bytes 1130496 | tf_op jit(solution)/shard_map/thp,shp->hts/dot_general | solution.py:108
  71.3 0.9 fusion.80
  72.3 0.7 fusion.4
  74.0 1.0 copy-done.6
  75.1 1.3 convolution_bitcast_fusion
  76.4 15.7 %all-gather.6.cloned.1.call-done = f32[128,64,128]{2,1,0:T(8,128)} async-done(((f32[32,64,128]{2,1,0:T(8,128)}), f32[128,64,128]{2,1,0:T(8,128)}) %all-gather.6.cloned.1.call-update) | async-done | bytes 4194320 | tf_op jit(solution)/shard_map/all_gather | solution.py:84
  92.2 2.4 %fusion.10 = bf16[128,32,64]{0,2,1:T(8,128)(2,1)S(1)} fusion(f32[128,32,64]{0,2,1:T(8,128)S(1)} %convolution_bitcast_fusion, f32[128,64,128]{2,1,0:T(8,128)} %all-gather.6.cloned.1.call-done, f32[128,32]{0,1:T(8,128)S(1)} %copy-done.13, f32[32]{0:T(128)S(1)} %copy-done.34, f32[32]{0:T(128)S(1)} %copy-done.31, f32[32]{0:T(128)S(1)} %copy-done.33, ...), kind=kOutput, calls=%fused_computation.24 | convolution fusion | flops 70254592 | bytes 4769283 | tf_op jit(solution)/shard_map/sn,hpn->shp/dot_general | solution.py:105
  94.6 2.4 %fusion.13 = bf16[128,128]{0,1:T(8,128)(2,1)S(1)} fusion(f32[128,128]{0,1:T(8,128)S(1)} %copy-done.17, bf16[128,32,64]{0,2,1:T(8,128)(2,1)S(1)} %bitcast.179, f32[128,64,128]{2,1,0:T(8,128)} %all-gather.6.cloned.1.call-done, f32[32]{0:T(128)S(1)} %copy-done.34, f32[32]{0:T(128)S(1)} %copy-done.33, f32[32]{0:T(128)S(1)} %copy-done.31, pred[]{:T(512)S(6)} %lt.21, ...), kind=kOutput, calls=%fused_computation.30 | convolution fusion | flops 69500928 | bytes 3768707 | tf_op jit(solution)/shard_map/shp,hpn->sn/dot_general | solution.py:111
  97.0 1.6 fusion.24
  98.7 29.5 %reduce-scatter.2.cloned.1.call-done = f32[128,288]{0,1:T(8,128)} async-done(((f32[128,2304]{0,1:T(8,128)}), f32[128,288]{0,1:T(8,128)}) %reduce-scatter.2.cloned.1.call-update) | async-done | bytes 147472 | tf_op jit(solution)/shard_map/reduce_scatter | solution.py:125
  128.5 46.0 %all-reduce.2.cloned.1.call-done = f32[128,288]{0,1:T(8,128)} async-done(((f32[128,288]{0,1:T(8,128)}), f32[128,288]{0,1:T(8,128)}) %all-reduce.2.cloned.1.call-update) | async-done | bytes 147472 | tf_op jit(solution)/shard_map/psum | solution.py:126
  174.6 1.3 convolution_bitcast_fusion.1
  175.9 2.4 %fusion.9 = bf16[128,32,64]{0,2,1:T(8,128)(2,1)S(1)} fusion(f32[128,32,64]{0,2,1:T(8,128)S(1)} %convolution_bitcast_fusion.1, f32[4,32,64,128]{3,2,1,0:T(8,128)} %copy-done.6, f32[128,32]{0,1:T(8,128)S(1)} %copy.79, f32[32]{0:T(128)S(1)} %copy-done.29, f32[32]{0:T(128)S(1)} %copy-done.31, f32[32]{0:T(128)S(1)} %copy-done.33, pred[]{:T(512)S(6)} %gt.24, ...), kind=kOutput, calls=%fused_computation.23 | convolution fusion | flops 70254592 | bytes 4769283 | tf_op jit(solution)/shard_map/tn,hpn->thp/dot_general | solution.py:98
  178.2 1.0 copy.86
  179.2 20.4 %all-gather.4.cloned.1.call-done = f32[128,2304]{0,1:T(8,128)} async-done(((f32[128,288]{0,1:T(8,128)}), f32[128,2304]{0,1:T(8,128)}) %all-gather.4.cloned.1.call-update) | async-done | bytes 1179664 | tf_op jit(solution)/shard_map/all_gather | solution.py:127
  199.6 1.3 broadcast_multiply_fusion
  201.0 1.4 copy.87
  (114 shorter events, 7.1 us)
Async XLA Ops:
  7.2 28.0 %copy-start = (bf16[128,2304]{1,0:T(8,128)(2,1)S(1)}, bf16[128,2304]{1,0:T(8,128)(2,1)}, u32[]{:S(2)}) copy-start(bf16[128,2304]{1,0:T(8,128)(2,1)} %param.11) | copy-start | bytes 1769476
  10.5 11.2 %all-to-all-start = ((f32[8,1,16]{2,1,0:T(1,128)}), f32[8,1,16]{2,1,0:T(1,128)S(1)}, u32[]{:S(2)}, u32[]{:S(2)}) async-start(f32[8,1,16]{2,1,0:T(1,128)} %bitcast.1), calls=%async_computation | async-start | bytes 8192 | tf_op jit(solution)/shard_map/all_to_all | solution.py:32
  16.9 75.3 %all-gather.6.cloned.1.call-start = ((), (), s32[]{:S(2)}) async-start(), calls=%async_computation.5 | async-start | bytes 5242880 | tf_op jit(solution)/shard_map/all_gather | solution.py:84
  18.5 23.1 %copy-start.22 = (f32[128]{0:T(128)}, f32[128]{0:T(128)S(1)}, u32[]{:S(2)}) copy-start(f32[128]{0:T(128)S(1)} %add_multiply_fusion) | copy-start | bytes 1540
  19.8 20.2 %copy-start.4 = (bf16[1,128,2048]{1,2,0:T(8,128)(2,1)}, bf16[1,128,2048]{1,2,0:T(8,128)(2,1)S(1)}, u32[]{:S(2)}) copy-start(bf16[1,128,2048]{1,2,0:T(8,128)(2,1)S(1)} %copy.80) | copy-start | bytes 1572868
  30.9 4.9 %copy-start.35 = (bf16[128,32]{0,1:T(8,128)(2,1)S(1)}, bf16[128,32]{0,1:T(8,128)(2,1)}, u32[]{:S(2)}) copy-start(bf16[128,32]{0,1:T(8,128)(2,1)} %param.12) | copy-start | bytes 24580
  30.9 4.9 %copy-start.36 = (f32[32]{0:T(128)S(1)}, f32[32]{0:T(128)}, u32[]{:S(2)}) copy-start(f32[32]{0:T(128)} %param.13) | copy-start | bytes 388
  30.9 5.9 %copy-start.25 = (f32[32]{0:T(128)S(1)}, f32[32]{0:T(128)}, u32[]{:S(2)}) copy-start(f32[32]{0:T(128)} %param.14) | copy-start | bytes 388
  35.1 6.5 %copy-start.20 = (f32[512,1]{0,1:T(1,128)}, f32[512,1]{0,1:T(1,128)S(1)}, u32[]{:S(2)}) copy-start(f32[512,1]{0,1:T(1,128)S(1)} %fusion.92) | copy-start | bytes 6148
  35.2 1.6 copy-start.26
  35.8 4.2 %copy-start.2 = (bf16[128,2304]{1,0:T(8,128)(2,1)}, bf16[128,2304]{1,0:T(8,128)(2,1)S(1)}, u32[]{:S(2)}) copy-start(bf16[128,2304]{1,0:T(8,128)(2,1)S(1)} %convolution_convert_fusion.1) | copy-start | bytes 1769476
  36.8 0.6 copy-start.14
  37.7 3.2 %copy-start.7 = (f32[128,32]{1,0:T(8,128)}, f32[128,32]{1,0:T(8,128)S(1)}, u32[]{:S(2)}) copy-start(f32[128,32]{1,0:T(8,128)S(1)} %reduce_window_sum.46) | copy-start | bytes 49156
  39.1 89.1 %reduce-scatter.2.cloned.1.call-start = ((), (), s32[]{:S(2)}) async-start(), calls=%async_computation.2 | async-start | bytes 1327104 | tf_op jit(solution)/shard_map/reduce_scatter | solution.py:125
  42.7 1.8 copy-start.21
  42.7 1.8 copy-start.23
  48.6 5.7 %slice-start = ((bf16[128,2304]{1,0:T(8,128)(2,1)}), bf16[128,2048]{1,0:T(8,128)(2,1)S(1)}, s32[]{:S(2)}) async-start(bf16[128,2304]{1,0:T(8,128)(2,1)} %copy-done.2), calls=%async_computation.6 | async-start | bytes 1048576 | tf_op jit(solution)/shard_map/slice | solution.py:54
  55.3 7.3 %copy-start.3 = (bf16[128,2304]{1,0:T(8,128)(2,1)S(1)}, bf16[128,2304]{1,0:T(8,128)(2,1)}, u32[]{:S(2)}) copy-start(bf16[128,2304]{1,0:T(8,128)(2,1)} %copy-done.2) | copy-start | bytes 1769476
  58.4 0.6 copy-start.12
  68.2 4.9 %copy-start.28 = (f32[32]{0:T(128)}, f32[32]{0:T(128)S(1)}, u32[]{:S(2)}) copy-start(f32[32]{0:T(128)S(1)} %get-tuple-element.13) | copy-start | bytes 388
  68.2 4.9 %copy-start.30 = (f32[32]{0:T(128)}, f32[32]{0:T(128)S(1)}, u32[]{:S(2)}) copy-start(f32[32]{0:T(128)S(1)} %get-tuple-element.14) | copy-start | bytes 388
  68.2 4.9 %copy-start.32 = (f32[32]{0:T(128)}, f32[32]{0:T(128)S(1)}, u32[]{:S(2)}) copy-start(f32[32]{0:T(128)S(1)} %get-tuple-element.15) | copy-start | bytes 388
  68.2 4.1 %copy-start.1 = (f32[4,128,2048]{1,2,0:T(8,128)S(1)}, f32[4,128,2048]{1,2,0:T(8,128)}, u32[]{:S(2)}) copy-start(f32[4,128,2048]{1,2,0:T(8,128)} %copy.76) | copy-start | bytes 12582916
  68.2 4.1 %copy-start.11 = (f32[4,128,32]{1,2,0:T(8,128)S(1)}, f32[4,128,32]{1,2,0:T(8,128)}, u32[]{:S(2)}) copy-start(f32[4,128,32]{1,2,0:T(8,128)} %copy.78) | copy-start | bytes 196612
  72.2 1.7 copy-start.15
  72.3 1.1 copy-start.9
  73.0 2.0 copy-start.6
  73.4 1.7 copy-start.5
  73.4 1.7 copy-start.18
  73.4 1.7 copy-start.19
  73.4 1.7 copy-start.37
  75.0 17.1 %copy-start.13 = (f32[128,32]{0,1:T(8,128)S(1)}, f32[128,32]{0,1:T(8,128)}, u32[]{:S(2)}) copy-start(f32[128,32]{0,1:T(8,128)} %copy-done.12) | copy-start | bytes 49156
  75.0 17.1 %copy-start.31 = (f32[32]{0:T(128)S(1)}, f32[32]{0:T(128)}, u32[]{:S(2)}) copy-start(f32[32]{0:T(128)} %copy-done.30) | copy-start | bytes 388
  75.1 17.1 %copy-start.33 = (f32[32]{0:T(128)S(1)}, f32[32]{0:T(128)}, u32[]{:S(2)}) copy-start(f32[32]{0:T(128)} %copy-done.32) | copy-start | bytes 388
  75.1 17.1 %copy-start.34 = (f32[32]{0:T(128)S(1)}, f32[32]{0:T(128)}, u32[]{:S(2)}) copy-start(f32[32]{0:T(128)} %get-tuple-element.12) | copy-start | bytes 388
  76.4 18.2 %copy-start.10 = (bf16[128,2048]{0,1:T(8,128)(2,1)S(1)}, bf16[128,2048]{0,1:T(8,128)(2,1)}, u32[]{:S(2)}) copy-start(bf16[128,2048]{0,1:T(8,128)(2,1)} %copy.84) | copy-start | bytes 1572868
  76.4 18.2 %copy-start.17 = (f32[128,128]{0,1:T(8,128)S(1)}, f32[128,128]{0,1:T(8,128)}, u32[]{:S(2)}) copy-start(f32[128,128]{0,1:T(8,128)} %fusion.80) | copy-start | bytes 196612
  94.6 2.5 %copy-start.24 = (f32[128]{0:T(128)S(1)}, f32[128]{0:T(128)}, u32[]{:S(2)}) copy-start(f32[128]{0:T(128)} %copy-done.22) | copy-start | bytes 1540
  94.6 2.5 %copy-start.27 = (f32[1,128]{1,0:T(1,128)S(1)}, f32[1,128]{1,0:T(1,128)}, u32[]{:S(2)}) copy-start(f32[1,128]{1,0:T(1,128)} %copy-done.26) | copy-start | bytes 1540
  97.0 77.5 %copy-start.8 = (bf16[128,2048]{0,1:T(8,128)(2,1)S(1)}, bf16[128,2048]{0,1:T(8,128)(2,1)}, u32[]{:S(2)}) copy-start(bf16[128,2048]{0,1:T(8,128)(2,1)} %copy.69) | copy-start | bytes 1572868
  97.0 77.5 %copy-start.16 = (f32[128,128]{0,1:T(8,128)S(1)}, f32[128,128]{0,1:T(8,128)}, u32[]{:S(2)}) copy-start(f32[128,128]{0,1:T(8,128)} %copy-done.15) | copy-start | bytes 196612
  98.7 75.8 %all-reduce.2.cloned.1.call-start = ((), (), s32[]{:S(2)}) async-start(), calls=%async_computation.3 | async-start | bytes 294912 | tf_op jit(solution)/shard_map/psum | solution.py:126
  128.2 71.4 %all-gather.4.cloned.1.call-start = ((), (), s32[]{:S(2)}) async-start(), calls=%async_computation.4 | async-start | bytes 1327104 | tf_op jit(solution)/shard_map/all_gather | solution.py:127
  174.5 1.3 copy-start.29
Sparse Core Ops, SparseCore 0:
  39.3 52.8 all-gather.5
  98.8 29.3 reduce-scatter.1
  131.1 43.3 all-reduce.1
  176.1 23.5 all-gather.3

commit v3 on v2

--- a/solution.py
+++ b/solution.py
@@ -13,6 +13,41 @@
     causal = jnp.arange(row_count)[:, None] >= jnp.arange(row_count)[None, :]
     log_span = cum_decay.T[:, :, None] - cum_decay.T[:, None, :]
     return jnp.where(causal[None], jnp.exp(jnp.where(causal[None], log_span, -60.0)), 0.0)
+
+
+def axis_bits(axis):
+    size = lax.axis_size(axis)
+    assert size & (size - 1) == 0
+    return [1 << k for k in range(size.bit_length() - 1)]
+
+
+def exchange(value, axis, bit):
+    pairs = [(i, i ^ bit) for i in range(lax.axis_size(axis))]
+    return lax.ppermute(value, axis, pairs)
+
+
+def tree_psum(value):
+    steps = [("series", 1)] + [("tm", b) for b in axis_bits("tm")]
+    steps += [("series", b) for b in axis_bits("series") if b > 1]
+    done = []
+    for axis, bit in steps:
+        rows = value.shape[0]
+        if rows % 16 == 0:
+            upper = (lax.axis_index(axis) // bit) % 2
+            keep = lax.dynamic_slice_in_dim(value, upper * (rows // 2), rows // 2)
+            send = lax.dynamic_slice_in_dim(value, (1 - upper) * (rows // 2), rows // 2)
+            value = keep + exchange(send, axis, bit)
+            done.append((axis, bit, upper))
+        else:
+            value = value + exchange(value, axis, bit)
+    for axis, bit, upper in reversed(done):
+        other = exchange(value, axis, bit)
+        value = jnp.where(
+            upper == 1,
+            jnp.concatenate([other, value]),
+            jnp.concatenate([value, other]),
+        )
+    return value
 
 
 def on_device(codes, owner_slot, edges, w_in, w_dt, dt_bias, decay_rate, grad_out):
@@ -121,10 +156,8 @@
         ],
         axis=1,
     )
-    local_grad = jnp.einsum("tf,tw->fw", features, grad_rows, preferred_element_type=fl)
-    share_grad = lax.psum_scatter(local_grad, "series", scatter_dimension=1, tiled=True)
-    share_grad = lax.psum(share_grad, "tm")
-    total_grad = lax.all_gather(share_grad, "series", axis=1, tiled=True)
+    local_grad = jnp.einsum("tw,tf->wf", grad_rows, features, preferred_element_type=fl)
+    total_grad = tree_psum(local_grad).T
     grad_in = total_grad / math.sqrt(series_count * seq_len)
     return (ssd_output, grad_in)
 

time: 210 us -> 160 us (0.76)
  waiting for transfers between devices: 114 us -> 43.9 us
  starting transfers between devices: 6.9 us -> 28.1 us
    psum x1 -> x0, waiting for transfers between devices: 46 us -> none  [on_device(): share_grad = lax.psum(share_grad, 'tm')]
    reduce_scatter x1 -> x0, waiting for transfers between devices: 29.5 us -> none  [on_device(): lax.psum_scatter(local_grad, 'series', scatter_dimension=1, tiled=True)]
    ppermute x0 -> x10, waiting for transfers between devices: none -> 26.2 us  [exchange(): return lax.ppermute(value, axis, pairs)]
    ppermute x0 -> x10, starting transfers between devices: none -> 21.7 us  [exchange(): return lax.ppermute(value, axis, pairs)]
    all_gather x1 -> x0, waiting for transfers between devices: 20.4 us -> none  [on_device(): total_grad = lax.all_gather(share_grad, 'series', axis=1, tiled=True)]
    unnamed x79 -> x89, local copies, waits for them, and re-layouts: 6.36 us -> 6.4 us
  transfers between devices with their start and end apart: 5 -> 12, of which waited for: 5 -> 11; matrix products, arithmetic and copies ran while one was open for 20% -> 27% of each run, Pallas kernels for 0% -> 0%
where the time goes in v3:
time: 160 us; the launch traced here: 159 us
  waiting for transfers between devices  43.9 us (27%)
  starting transfers between devices  28.1 us (18%)
  matrix products  25.5 us (16%)
  local copies, waits for them, and re-layouts  25.4 us (16%)
  other arithmetic  15.5 us (10%)
  between operations  14.7 us (9%)
  blocking collectives  5.9 us (4%)
    ppermute x10, waiting for transfers between devices, exchange(): return lax.ppermute(value, axis, pairs)  26.2 us
    ppermute x10, starting transfers between devices, exchange(): return lax.ppermute(value, axis, pairs)  21.7 us
    all_gather x1, waiting for transfers between devices, on_device(): adjoint_all = lax.all_gather(adjoint_local, 'tm')  15.8 us
    unnamed x89, local copies, waits for them, and re-layouts  6.4 us
    all_to_all x1, starting transfers between devices, on_device(): lax.all_to_all(ordered, 'series', split_axis=0, concat_axis=1, tiled=True)  6.38 us
    all_gather x1, blocking collectives, on_device(): reading = lax.all_gather(own_block, 'tm', axis=1, tiled=True)[0]  5.9 us
    convert_element_type x1, local copies, waits for them, and re-layouts, on_device(): xw_all = (x_all * tail_all[..., None]).astype(half)  5.62 us
    dot_general x1, matrix products, on_device(): picked = jnp.dot(onehot, bin_table, precision=lax.Precision.HIGHEST)  4.14 us
  transfers between devices with their start and end apart: 12, of which 11 were waited for; matrix products, arithmetic and copies ran while one was open for 27% of the time, Pallas kernels for 0%

profile of v3, /device:TPU:1, one launch (start us, length us, event | category | flops | bytes accessed | tf_op | source)
XLA Modules:
  0.0 158.9 jit_solution(16817285643307575028)
XLA Ops:
  8.6 1.2 gather_fusion
  10.5 6.4 %all-to-all-start = ((f32[8,1,16]{2,1,0:T(1,128)}), f32[8,1,16]{2,1,0:T(1,128)S(1)}, u32[]{:S(2)}, u32[]{:S(2)}) async-start(f32[8,1,16]{2,1,0:T(1,128)} %bitcast.1), calls=%async_computation | async-start | bytes 8192 | tf_op jit(solution)/shard_map/all_to_all | solution.py:67
  18.5 1.3 copy.80
  19.8 1.9 %all-to-all-done = f32[8,1,16]{2,1,0:T(1,128)S(1)} async-done(((f32[8,1,16]{2,1,0:T(1,128)}), f32[8,1,16]{2,1,0:T(1,128)S(1)}, u32[]{:S(2)}, u32[]{:S(2)}) %all-to-all-start) | async-done | bytes 544 | tf_op jit(solution)/shard_map/all_to_all | solution.py:67
  22.9 5.9 %all_gather.9 = f32[1,512]{1,0:T(1,128)S(1)} all-gather(f32[1,128]{1,0:T(1,128)S(1)} %all_to_all.11), channel_id=1, replica_groups=mesh['tm'=4,'series'=8] {'tm'}, dimensions={1}, use_global_device_ids=true | all-gather | bytes 2560 | tf_op jit(solution)/shard_map/all_gather | solution.py:68
  28.8 1.4 convert_reduce_fusion
  30.9 4.1 %fusion = f32[512,4]{0,1:T(4,128)S(1)} fusion(f32[4096]{0:T(1024)S(1)} %get-tuple-element.11, f32[4096]{0:T(1024)S(1)} %convert_element_type.109, f32[512]{0:T(512)S(1)} %bitcast.191, f32[4096,1]{0,1:T(1,128)S(1)} %bitcast.192, f32[4096,1]{0,1:T(1,128)S(1)} %bitcast.186, f32[4096,1]{0,1:T(1,128)S(1)} %bitcast.185, f32[4096,1]{0,1:T(1,128)S(1)} %sub.79), kind=kOutput, calls=%fused_computation.3 | convolution fusion | flops 107003904 | bytes 108544 | tf_op jit(solution)/shard_map/dot_general | solution.py:77
  35.8 1.0 compare_select_fusion.1
  37.8 1.3 fusion.32
  41.3 1.1 compare_select_fusion
  44.3 1.6 %convolution_convert_fusion = bf16[512,2304]{1,0:T(8,128)(2,1)S(1)} fusion(bf16[128,2304]{1,0:T(8,128)(2,1)S(1)} %copy-done, f32[128]{0:T(128)S(1)} %copy-done.25, f32[512]{0:T(512)S(1)} %bitcast.195), kind=kOutput, calls=%fused_computation.4 | convolution fusion | flops 303300608 | bytes 2951680 | tf_op jit(solution)/shard_map/dot_general | solution.py:98
  45.9 2.5 %slice_convert_fusion = f32[4,128,2048]{2,1,0:T(8,128)} fusion(bf16[4,128,2304]{2,1,0:T(8,128)(2,1)S(1)} %bitcast.168), kind=kLoop, calls=%fused_computation.11 | loop fusion | flops 1048576 | bytes 6291456 | tf_op jit(solution)/shard_map/convert_element_type | solution.py:108
  48.5 5.6 %copy.76 = f32[4,128,2048]{1,2,0:T(8,128)} copy(f32[4,128,2048]{2,1,0:T(8,128)} %slice_convert_fusion) | data formatting | bytes 8388608 | tf_op jit(solution)/shard_map/convert_element_type | solution.py:108
  54.1 1.0 copy.69
  55.1 1.6 copy.72
  58.8 1.0 mul.275
  59.8 2.6 %copy.83 = f32[128,2048]{1,0:T(8,128)} copy(f32[128,2048]{0,1:T(8,128)} %bitcast.173) | data formatting | bytes 2097152 | tf_op jit(solution)/shard_map/mul | solution.py:140
  62.3 2.1 %multiply_convert_fusion.3 = bf16[128,2048]{1,0:T(8,128)(2,1)} fusion(f32[128,2048]{1,0:T(8,128)} %copy.83, bf16[128,2304]{1,0:T(8,128)(2,1)S(1)} %copy-done.3), kind=kLoop, calls=%fused_computation.53 | loop fusion | flops 786432 | bytes 2097152 | tf_op jit(solution)/shard_map/convert_element_type | solution.py:96
  64.5 2.0 %copy.84 = bf16[128,2048]{0,1:T(8,128)(2,1)} copy(bf16[128,2048]{1,0:T(8,128)(2,1)} %multiply_convert_fusion.3) | data formatting | bytes 1048576 | tf_op jit(solution)/shard_map/convert_element_type | solution.py:96
  66.5 1.4 multiply_bitcast_fusion
  67.9 2.9 %fusion.5 = bf16[128,128]{0,1:T(8,128)(2,1)S(1)} fusion(bf16[128,32,64]{0,2,1:T(8,128)(2,1)} %bitcast.178, bf16[128,32,64]{0,2,1:T(8,128)(2,1)} %bitcast.171, f32[32,128]{1,0:T(8,128)} %get-tuple-element.16, f32[32,128]{1,0:T(8,128)} %copy.72, pred[128,128]{0,1:T(8,128)(4,1)} %iota_compare_fusion), kind=kOutput, calls=%fused_computation.13 | convolution fusion | flops 70238208 | bytes 1130496 | tf_op jit(solution)/shard_map/thp,shp->hts/dot_general | solution.py:143
  73.8 1.0 copy-done.6
  74.9 1.3 convolution_bitcast_fusion
  76.2 15.8 %all-gather.3.cloned.1.call-done = f32[128,64,128]{2,1,0:T(8,128)} async-done(((f32[32,64,128]{2,1,0:T(8,128)}), f32[128,64,128]{2,1,0:T(8,128)}) %all-gather.3.cloned.1.call-update) | async-done | bytes 4194320 | tf_op jit(solution)/shard_map/all_gather | solution.py:119
  92.0 2.4 %fusion.10 = bf16[128,32,64]{0,2,1:T(8,128)(2,1)S(1)} fusion(f32[128,32,64]{0,2,1:T(8,128)S(1)} %convolution_bitcast_fusion, f32[128,64,128]{2,1,0:T(8,128)} %all-gather.3.cloned.1.call-done, f32[128,32]{0,1:T(8,128)S(1)} %copy-done.13, f32[32]{0:T(128)S(1)} %copy-done.38, f32[32]{0:T(128)S(1)} %copy-done.33, f32[32]{0:T(128)S(1)} %copy-done.36, ...), kind=kOutput, calls=%fused_computation.24 | convolution fusion | flops 70254592 | bytes 4769283 | tf_op jit(solution)/shard_map/sn,hpn->shp/dot_general | solution.py:140
  94.5 2.4 %fusion.15 = bf16[128,128]{0,1:T(8,128)(2,1)S(1)} fusion(f32[128,128]{0,1:T(8,128)S(1)} %copy-done.17, bf16[128,32,64]{0,2,1:T(8,128)(2,1)S(1)} %bitcast.181, f32[128,64,128]{2,1,0:T(8,128)} %all-gather.3.cloned.1.call-done, f32[32]{0:T(128)S(1)} %copy-done.38, f32[32]{0:T(128)S(1)} %copy-done.36, f32[32]{0:T(128)S(1)} %copy-done.33, pred[]{:T(512)S(6)} %lt.78, ...), kind=kOutput, calls=%fused_computation.33 | convolution fusion | flops 69500928 | bytes 3768707 | tf_op jit(solution)/shard_map/shp,hpn->sn/dot_general | solution.py:146
  98.3 1.6 %collective-permute-done = f32[1152,128]{1,0:T(8,128)S(1)} collective-permute-done((f32[1152,128]{1,0:T(8,128)S(1)}, f32[1152,128]{1,0:T(8,128)S(1)}, u32[]{:S(2)}, u32[]{:S(2)}) %collective-permute-start) | collective-permute-done | bytes 589856 | tf_op jit(solution)/shard_map/ppermute | solution.py:26
  100.0 1.3 collective-permute-start.1
  101.3 7.0 %collective-permute-done.1 = f32[576,128]{1,0:T(8,128)S(1)} collective-permute-done((f32[576,128]{1,0:T(8,128)S(1)}, f32[576,128]{1,0:T(8,128)S(1)}, u32[]{:S(2)}, u32[]{:S(2)}) %collective-permute-start.1) | collective-permute-done | bytes 294944 | tf_op jit(solution)/shard_map/ppermute | solution.py:26
  108.3 1.3 collective-permute-start.2
  109.6 2.8 %collective-permute-done.2 = f32[288,128]{1,0:T(8,128)S(1)} collective-permute-done((f32[288,128]{1,0:T(8,128)S(1)}, f32[288,128]{1,0:T(8,128)S(1)}, u32[]{:S(2)}, u32[]{:S(2)}) %collective-permute-start.2) | collective-permute-done | bytes 147488 | tf_op jit(solution)/shard_map/ppermute | solution.py:26
  112.4 1.3 collective-permute-start.3
  113.7 2.0 %collective-permute-done.3 = f32[144,128]{1,0:T(8,128)S(1)} collective-permute-done((f32[144,128]{1,0:T(8,128)S(1)}, f32[144,128]{1,0:T(8,128)S(1)}, u32[]{:S(2)}, u32[]{:S(2)}) %collective-permute-start.3) | collective-permute-done | bytes 73760 | tf_op jit(solution)/shard_map/ppermute | solution.py:26
  115.7 2.2 %collective-permute-start.4 = (f32[72,128]{1,0:T(8,128)S(1)}, f32[72,128]{1,0:T(8,128)S(1)}, u32[]{:S(2)}, u32[]{:S(2)}) collective-permute-start(f32[72,128]{1,0:T(8,128)S(1)} %constant_dynamic-slice_fusion), channel_id=1, source_target_pairs={{0,4},{1,5},{2,6},{3,7},{4,0},{5,1},{6,2},{7,3},{8,12},{9,13},{10,... | collective-permute-start | bytes 110600 | tf_op jit(solution)/shard_map/ppermute | solution.py:26
  117.9 1.6 collective-permute-done.4
  119.5 2.2 %collective-permute-start.5 = (f32[72,128]{1,0:T(8,128)S(1)}, f32[72,128]{1,0:T(8,128)S(1)}, u32[]{:S(2)}, u32[]{:S(2)}) collective-permute-start(f32[72,128]{1,0:T(8,128)S(1)} %dynamic-slice_add_fusion.4), channel_id=1, source_target_pairs={{0,4},{1,5},{2,6},{3,7},{4,0},{5,1},{6,2},{7,3},{8,12},{9,13},{10,... | collective-permute-start | bytes 110600 | tf_op jit(solution)/shard_map/ppermute | solution.py:26
  121.7 2.0 %collective-permute-done.5 = f32[72,128]{1,0:T(8,128)S(1)} collective-permute-done((f32[72,128]{1,0:T(8,128)S(1)}, f32[72,128]{1,0:T(8,128)S(1)}, u32[]{:S(2)}, u32[]{:S(2)}) %collective-permute-start.5) | collective-permute-done | bytes 36896 | tf_op jit(solution)/shard_map/ppermute | solution.py:26
  123.7 1.7 %collective-permute-start.6 = (f32[144,128]{1,0:T(8,128)S(1)}, f32[144,128]{1,0:T(8,128)S(1)}, u32[]{:S(2)}, u32[]{:S(2)}) collective-permute-start(f32[144,128]{1,0:T(8,128)S(1)} %maximum_select_fusion.4), channel_id=1, source_target_pairs={{0,2},{1,3},{2,0},{3,1},{4,6},{5,7},{6,4},{7,5},{8,10},{9,11},{10,... | collective-permute-start | bytes 221192 | tf_op jit(solution)/shard_map/ppermute | solution.py:26
  125.4 1.7 %collective-permute-done.6 = f32[144,128]{1,0:T(8,128)S(1)} collective-permute-done((f32[144,128]{1,0:T(8,128)S(1)}, f32[144,128]{1,0:T(8,128)S(1)}, u32[]{:S(2)}, u32[]{:S(2)}) %collective-permute-start.6) | collective-permute-done | bytes 73760 | tf_op jit(solution)/shard_map/ppermute | solution.py:26
  127.1 1.2 collective-permute-start.7
  128.4 2.8 %collective-permute-done.7 = f32[288,128]{1,0:T(8,128)S(1)} collective-permute-done((f32[288,128]{1,0:T(8,128)S(1)}, f32[288,128]{1,0:T(8,128)S(1)}, u32[]{:S(2)}, u32[]{:S(2)}) %collective-permute-start.7) | collective-permute-done | bytes 147488 | tf_op jit(solution)/shard_map/ppermute | solution.py:26
  131.2 1.2 collective-permute-start.8
  132.5 4.7 %collective-permute-done.8 = f32[576,128]{1,0:T(8,128)S(1)} collective-permute-done((f32[576,128]{1,0:T(8,128)S(1)}, f32[576,128]{1,0:T(8,128)S(1)}, u32[]{:S(2)}, u32[]{:S(2)}) %collective-permute-start.8) | collective-permute-done | bytes 294944 | tf_op jit(solution)/shard_map/ppermute | solution.py:26
  137.2 8.6 %collective-permute-start.9 = (f32[1152,128]{1,0:T(8,128)S(1)}, f32[1152,128]{1,0:T(8,128)S(1)}, u32[]{:S(2)}, u32[]{:S(2)}) collective-permute-start(f32[1152,128]{1,0:T(8,128)S(1)} %maximum_select_fusion.1), channel_id=1, source_target_pairs={{0,1},{1,0},{2,3},{3,2},{4,5},{5,4},{6,7},{7,6},{8,9},{9,8},{10,11... | collective-permute-start | bytes 1769480 | tf_op jit(solution)/shard_map/ppermute | solution.py:26
  145.9 1.3 convolution_bitcast_fusion.1
  147.2 2.4 %fusion.9 = bf16[128,32,64]{0,2,1:T(8,128)(2,1)S(1)} fusion(f32[128,32,64]{0,2,1:T(8,128)S(1)} %convolution_bitcast_fusion.1, f32[4,32,64,128]{3,2,1,0:T(8,128)} %copy-done.6, f32[128,32]{0,1:T(8,128)S(1)} %copy.79, f32[32]{0:T(128)S(1)} %copy-done.31, f32[32]{0:T(128)S(1)} %copy-done.34, f32[32]{0:T(128)S(1)} %copy-done.37, pred[]{:T(512)S(6)} %gt.24, ...), kind=kOutput, calls=%fused_computation.23 | convolution fusion | flops 70254592 | bytes 4769283 | tf_op jit(solution)/shard_map/tn,hpn->thp/dot_general | solution.py:133
  149.6 1.0 copy.86
  150.7 1.4 copy.87
  (149 shorter events, 18.0 us)
Async XLA Ops:
  7.2 28.0 %copy-start = (bf16[128,2304]{1,0:T(8,128)(2,1)S(1)}, bf16[128,2304]{1,0:T(8,128)(2,1)}, u32[]{:S(2)}) copy-start(bf16[128,2304]{1,0:T(8,128)(2,1)} %param.11) | copy-start | bytes 1769476
  10.5 11.2 %all-to-all-start = ((f32[8,1,16]{2,1,0:T(1,128)}), f32[8,1,16]{2,1,0:T(1,128)S(1)}, u32[]{:S(2)}, u32[]{:S(2)}) async-start(f32[8,1,16]{2,1,0:T(1,128)} %bitcast.1), calls=%async_computation | async-start | bytes 8192 | tf_op jit(solution)/shard_map/all_to_all | solution.py:67
  16.9 75.2 %all-gather.3.cloned.1.call-start = ((), (), s32[]{:S(2)}) async-start(), calls=%async_computation.1 | async-start | bytes 5242880 | tf_op jit(solution)/shard_map/all_gather | solution.py:119
  18.5 22.9 %copy-start.24 = (f32[128]{0:T(128)}, f32[128]{0:T(128)S(1)}, u32[]{:S(2)}) copy-start(f32[128]{0:T(128)S(1)} %add_multiply_fusion) | copy-start | bytes 1540
  19.8 19.9 %copy-start.4 = (bf16[1,128,2048]{1,2,0:T(8,128)(2,1)}, bf16[1,128,2048]{1,2,0:T(8,128)(2,1)S(1)}, u32[]{:S(2)}) copy-start(bf16[1,128,2048]{1,2,0:T(8,128)(2,1)S(1)} %copy.80) | copy-start | bytes 1572868
  30.9 4.9 %copy-start.39 = (bf16[128,32]{0,1:T(8,128)(2,1)S(1)}, bf16[128,32]{0,1:T(8,128)(2,1)}, u32[]{:S(2)}) copy-start(bf16[128,32]{0,1:T(8,128)(2,1)} %param.12) | copy-start | bytes 24580
  30.9 4.9 %copy-start.40 = (f32[32]{0:T(128)S(1)}, f32[32]{0:T(128)}, u32[]{:S(2)}) copy-start(f32[32]{0:T(128)} %param.13) | copy-start | bytes 388
  30.9 5.9 %copy-start.27 = (f32[32]{0:T(128)S(1)}, f32[32]{0:T(128)}, u32[]{:S(2)}) copy-start(f32[32]{0:T(128)} %param.14) | copy-start | bytes 388
  35.1 6.2 %copy-start.22 = (f32[512,1]{0,1:T(1,128)}, f32[512,1]{0,1:T(1,128)S(1)}, u32[]{:S(2)}) copy-start(f32[512,1]{0,1:T(1,128)S(1)} %fusion.94) | copy-start | bytes 6148
  35.8 4.0 %copy-start.2 = (bf16[128,2304]{1,0:T(8,128)(2,1)}, bf16[128,2304]{1,0:T(8,128)(2,1)S(1)}, u32[]{:S(2)}) copy-start(bf16[128,2304]{1,0:T(8,128)(2,1)S(1)} %convolution_convert_fusion.1) | copy-start | bytes 1769476
  37.7 3.0 %copy-start.7 = (f32[128,32]{1,0:T(8,128)}, f32[128,32]{1,0:T(8,128)S(1)}, u32[]{:S(2)}) copy-start(f32[128,32]{1,0:T(8,128)S(1)} %reduce_window_sum.46) | copy-start | bytes 49156
  42.4 1.8 %copy-start.23 = (f32[512,1]{0,1:T(1,128)S(1)}, f32[512,1]{0,1:T(1,128)}, u32[]{:S(2)}) copy-start(f32[512,1]{0,1:T(1,128)} %copy-done.22) | copy-start | bytes 6148
  42.4 1.8 %copy-start.25 = (f32[128]{0:T(128)S(1)}, f32[128]{0:T(128)}, u32[]{:S(2)}) copy-start(f32[128]{0:T(128)} %copy-done.24) | copy-start | bytes 1540
  48.4 5.6 %slice-start = ((bf16[128,2304]{1,0:T(8,128)(2,1)}), bf16[128,2048]{1,0:T(8,128)(2,1)S(1)}, s32[]{:S(2)}) async-start(bf16[128,2304]{1,0:T(8,128)(2,1)} %copy-done.2), calls=%async_computation.2 | async-start | bytes 1048576 | tf_op jit(solution)/shard_map/slice | solution.py:89
  55.1 7.3 %copy-start.3 = (bf16[128,2304]{1,0:T(8,128)(2,1)S(1)}, bf16[128,2304]{1,0:T(8,128)(2,1)}, u32[]{:S(2)}) copy-start(bf16[128,2304]{1,0:T(8,128)(2,1)} %copy-done.2) | copy-start | bytes 1769476
  67.9 4.9 %copy-start.30 = (f32[32]{0:T(128)}, f32[32]{0:T(128)S(1)}, u32[]{:S(2)}) copy-start(f32[32]{0:T(128)S(1)} %get-tuple-element.13) | copy-start | bytes 388
  67.9 4.9 %copy-start.32 = (f32[32]{0:T(128)}, f32[32]{0:T(128)S(1)}, u32[]{:S(2)}) copy-start(f32[32]{0:T(128)S(1)} %get-tuple-element.14) | copy-start | bytes 388
  67.9 4.9 %copy-start.35 = (f32[32]{0:T(128)}, f32[32]{0:T(128)S(1)}, u32[]{:S(2)}) copy-start(f32[32]{0:T(128)S(1)} %get-tuple-element.15) | copy-start | bytes 388
  67.9 4.2 %copy-start.1 = (f32[4,128,2048]{1,2,0:T(8,128)S(1)}, f32[4,128,2048]{1,2,0:T(8,128)}, u32[]{:S(2)}) copy-start(f32[4,128,2048]{1,2,0:T(8,128)} %copy.76) | copy-start | bytes 12582916
  67.9 4.2 %copy-start.11 = (f32[4,128,32]{1,2,0:T(8,128)S(1)}, f32[4,128,32]{1,2,0:T(8,128)}, u32[]{:S(2)}) copy-start(f32[4,128,32]{1,2,0:T(8,128)} %copy.78) | copy-start | bytes 196612
  72.1 1.7 %copy-start.15 = (f32[128,128]{0,1:T(8,128)}, f32[128,128]{0,1:T(8,128)S(1)}, u32[]{:S(2)}) copy-start(f32[128,128]{0,1:T(8,128)S(1)} %fusion.79) | copy-start | bytes 196612
  72.8 2.0 %copy-start.6 = (f32[4,32,64,128]{3,2,1,0:T(8,128)}, f32[4,32,64,128]{3,2,1,0:T(8,128)S(1)}, u32[]{:S(2)}) copy-start(f32[4,32,64,128]{3,2,1,0:T(8,128)S(1)} %fusion.4) | copy-start | bytes 12582916
  73.2 1.7 %copy-start.18 = (f32[32,128]{1,0:T(8,128)S(1)}, f32[32,128]{1,0:T(8,128)}, u32[]{:S(2)}) copy-start(f32[32,128]{1,0:T(8,128)} %copy.72) | copy-start | bytes 49156
  73.2 1.7 %copy-start.20 = (pred[128,128]{0,1:T(8,128)(4,1)S(1)}, pred[128,128]{0,1:T(8,128)(4,1)}, u32[]{:S(2)}) copy-start(pred[128,128]{0,1:T(8,128)(4,1)} %iota_compare_fusion) | copy-start | bytes 49156
  73.2 1.7 %copy-start.41 = (f32[32,128]{1,0:T(8,128)S(1)}, f32[32,128]{1,0:T(8,128)}, u32[]{:S(2)}) copy-start(f32[32,128]{1,0:T(8,128)} %get-tuple-element.16) | copy-start | bytes 49156
  74.9 17.2 %copy-start.13 = (f32[128,32]{0,1:T(8,128)S(1)}, f32[128,32]{0,1:T(8,128)}, u32[]{:S(2)}) copy-start(f32[128,32]{0,1:T(8,128)} %copy-done.12) | copy-start | bytes 49156
  74.9 17.2 %copy-start.33 = (f32[32]{0:T(128)S(1)}, f32[32]{0:T(128)}, u32[]{:S(2)}) copy-start(f32[32]{0:T(128)} %copy-done.32) | copy-start | bytes 388
  74.9 17.1 %copy-start.36 = (f32[32]{0:T(128)S(1)}, f32[32]{0:T(128)}, u32[]{:S(2)}) copy-start(f32[32]{0:T(128)} %copy-done.35) | copy-start | bytes 388
  74.9 17.1 %copy-start.38 = (f32[32]{0:T(128)S(1)}, f32[32]{0:T(128)}, u32[]{:S(2)}) copy-start(f32[32]{0:T(128)} %get-tuple-element.12) | copy-start | bytes 388
  76.2 18.2 %copy-start.10 = (bf16[128,2048]{0,1:T(8,128)(2,1)S(1)}, bf16[128,2048]{0,1:T(8,128)(2,1)}, u32[]{:S(2)}) copy-start(bf16[128,2048]{0,1:T(8,128)(2,1)} %copy.84) | copy-start | bytes 1572868
  76.2 18.2 %copy-start.17 = (f32[128,128]{0,1:T(8,128)S(1)}, f32[128,128]{0,1:T(8,128)}, u32[]{:S(2)}) copy-start(f32[128,128]{0,1:T(8,128)} %fusion.82) | copy-start | bytes 196612
  94.4 2.4 %copy-start.26 = (f32[128]{0:T(128)S(1)}, f32[128]{0:T(128)}, u32[]{:S(2)}) copy-start(f32[128]{0:T(128)} %copy-done.24) | copy-start | bytes 1540
  94.4 2.4 %copy-start.29 = (f32[1,128]{1,0:T(1,128)S(1)}, f32[1,128]{1,0:T(1,128)}, u32[]{:S(2)}) copy-start(f32[1,128]{1,0:T(1,128)} %copy-done.28) | copy-start | bytes 1540
  97.5 2.4 %collective-permute-start = (f32[1152,128]{1,0:T(8,128)S(1)}, f32[1152,128]{1,0:T(8,128)S(1)}, u32[]{:S(2)}, u32[]{:S(2)}) collective-permute-start(f32[1152,128]{1,0:T(8,128)S(1)} %constant_dynamic-slice_fusion.4), channel_id=1, source_target_pairs={{0,1},{1,0},{2,3},{3,2},{4,5},{5,4},{6,7},{7,6},{8,9},{9,8},{10,11... | collective-permute-start | bytes 1769480 | tf_op jit(solution)/shard_map/ppermute | solution.py:26
  100.0 8.3 %collective-permute-start.1 = (f32[576,128]{1,0:T(8,128)S(1)}, f32[576,128]{1,0:T(8,128)S(1)}, u32[]{:S(2)}, u32[]{:S(2)}) collective-permute-start(f32[576,128]{1,0:T(8,128)S(1)} %constant_dynamic-slice_fusion.3), channel_id=1, source_target_pairs={{0,8},{8,0},{16,24},{24,16},{1,9},{9,1},{17,25},{25,17},{2,10},{10... | collective-permute-start | bytes 884744 | tf_op jit(solution)/shard_map/ppermute | solution.py:26
  101.2 44.6 %copy-start.8 = (bf16[128,2048]{0,1:T(8,128)(2,1)S(1)}, bf16[128,2048]{0,1:T(8,128)(2,1)}, u32[]{:S(2)}) copy-start(bf16[128,2048]{0,1:T(8,128)(2,1)} %copy.69) | copy-start | bytes 1572868
  101.2 44.6 %copy-start.16 = (f32[128,128]{0,1:T(8,128)S(1)}, f32[128,128]{0,1:T(8,128)}, u32[]{:S(2)}) copy-start(f32[128,128]{0,1:T(8,128)} %copy-done.15) | copy-start | bytes 196612
  101.2 44.6 %copy-start.19 = (f32[32,128]{1,0:T(8,128)S(1)}, f32[32,128]{1,0:T(8,128)}, u32[]{:S(2)}) copy-start(f32[32,128]{1,0:T(8,128)} %copy.72) | copy-start | bytes 49156
  101.3 44.6 %copy-start.21 = (pred[128,128]{0,1:T(8,128)(4,1)S(1)}, pred[128,128]{0,1:T(8,128)(4,1)}, u32[]{:S(2)}) copy-start(pred[128,128]{0,1:T(8,128)(4,1)} %iota_compare_fusion) | copy-start | bytes 49156
  101.3 44.6 %copy-start.42 = (f32[32,128]{1,0:T(8,128)S(1)}, f32[32,128]{1,0:T(8,128)}, u32[]{:S(2)}) copy-start(f32[32,128]{1,0:T(8,128)} %get-tuple-element.16) | copy-start | bytes 49156
  108.3 4.1 %collective-permute-start.2 = (f32[288,128]{1,0:T(8,128)S(1)}, f32[288,128]{1,0:T(8,128)S(1)}, u32[]{:S(2)}, u32[]{:S(2)}) collective-permute-start(f32[288,128]{1,0:T(8,128)S(1)} %constant_dynamic-slice_fusion.2), channel_id=1, source_target_pairs={{0,16},{8,24},{16,0},{24,8},{1,17},{9,25},{17,1},{25,9},{2,18},{10... | collective-permute-start | bytes 442376 | tf_op jit(solution)/shard_map/ppermute | solution.py:26
  112.4 3.3 %collective-permute-start.3 = (f32[144,128]{1,0:T(8,128)S(1)}, f32[144,128]{1,0:T(8,128)S(1)}, u32[]{:S(2)}, u32[]{:S(2)}) collective-permute-start(f32[144,128]{1,0:T(8,128)S(1)} %constant_dynamic-slice_fusion.1), channel_id=1, source_target_pairs={{0,2},{1,3},{2,0},{3,1},{4,6},{5,7},{6,4},{7,5},{8,10},{9,11},{10,... | collective-permute-start | bytes 221192 | tf_op jit(solution)/shard_map/ppermute | solution.py:26
  115.7 3.8 %collective-permute-start.4 = (f32[72,128]{1,0:T(8,128)S(1)}, f32[72,128]{1,0:T(8,128)S(1)}, u32[]{:S(2)}, u32[]{:S(2)}) collective-permute-start(f32[72,128]{1,0:T(8,128)S(1)} %constant_dynamic-slice_fusion), channel_id=1, source_target_pairs={{0,4},{1,5},{2,6},{3,7},{4,0},{5,1},{6,2},{7,3},{8,12},{9,13},{10,... | collective-permute-start | bytes 110600 | tf_op jit(solution)/shard_map/ppermute | solution.py:26
  119.5 4.2 %collective-permute-start.5 = (f32[72,128]{1,0:T(8,128)S(1)}, f32[72,128]{1,0:T(8,128)S(1)}, u32[]{:S(2)}, u32[]{:S(2)}) collective-permute-start(f32[72,128]{1,0:T(8,128)S(1)} %dynamic-slice_add_fusion.4), channel_id=1, source_target_pairs={{0,4},{1,5},{2,6},{3,7},{4,0},{5,1},{6,2},{7,3},{8,12},{9,13},{10,... | collective-permute-start | bytes 110600 | tf_op jit(solution)/shard_map/ppermute | solution.py:26
  123.7 3.4 %collective-permute-start.6 = (f32[144,128]{1,0:T(8,128)S(1)}, f32[144,128]{1,0:T(8,128)S(1)}, u32[]{:S(2)}, u32[]{:S(2)}) collective-permute-start(f32[144,128]{1,0:T(8,128)S(1)} %maximum_select_fusion.4), channel_id=1, source_target_pairs={{0,2},{1,3},{2,0},{3,1},{4,6},{5,7},{6,4},{7,5},{8,10},{9,11},{10,... | collective-permute-start | bytes 221192 | tf_op jit(solution)/shard_map/ppermute | solution.py:26
  127.1 4.1 %collective-permute-start.7 = (f32[288,128]{1,0:T(8,128)S(1)}, f32[288,128]{1,0:T(8,128)S(1)}, u32[]{:S(2)}, u32[]{:S(2)}) collective-permute-start(f32[288,128]{1,0:T(8,128)S(1)} %maximum_select_fusion.3), channel_id=1, source_target_pairs={{0,16},{8,24},{16,0},{24,8},{1,17},{9,25},{17,1},{25,9},{2,18},{10... | collective-permute-start | bytes 442376 | tf_op jit(solution)/shard_map/ppermute | solution.py:26
  131.2 5.9 %collective-permute-start.8 = (f32[576,128]{1,0:T(8,128)S(1)}, f32[576,128]{1,0:T(8,128)S(1)}, u32[]{:S(2)}, u32[]{:S(2)}) collective-permute-start(f32[576,128]{1,0:T(8,128)S(1)} %maximum_select_fusion.2), channel_id=1, source_target_pairs={{0,8},{8,0},{16,24},{24,16},{1,9},{9,1},{17,25},{25,17},{2,10},{10... | collective-permute-start | bytes 884744 | tf_op jit(solution)/shard_map/ppermute | solution.py:26
  137.2 13.4 %collective-permute-start.9 = (f32[1152,128]{1,0:T(8,128)S(1)}, f32[1152,128]{1,0:T(8,128)S(1)}, u32[]{:S(2)}, u32[]{:S(2)}) collective-permute-start(f32[1152,128]{1,0:T(8,128)S(1)} %maximum_select_fusion.1), channel_id=1, source_target_pairs={{0,1},{1,0},{2,3},{3,2},{4,5},{5,4},{6,7},{7,6},{8,9},{9,8},{10,11... | collective-permute-start | bytes 1769480 | tf_op jit(solution)/shard_map/ppermute | solution.py:26
  (8 other events, 9.6 us)
Sparse Core Ops, SparseCore 0:
  39.2 52.7 all-gather.2

commit v4 on v3

--- a/solution.py
+++ b/solution.py
@@ -64,8 +64,8 @@
     my_block = lax.axis_index("tm")
 
     ordered = jnp.take(codes, owner_slot, axis=0).astype(fl)
-    own_block = lax.all_to_all(ordered, "series", split_axis=0, concat_axis=1, tiled=True)
-    reading = lax.all_gather(own_block, "tm", axis=1, tiled=True)[0]
+    outgoing = jnp.tile(ordered, (n_blocks, 1))
+    reading = lax.all_to_all(outgoing, ("tm", "series"), split_axis=0, concat_axis=1, tiled=True)[0]
     edge_float = edges.astype(fl)
     upper_edge = jnp.concatenate([edge_float[1:], jnp.full((1,), code_ceiling, fl)])
     onehot = (

time: 160 us -> 154 us (0.963)
  blocking collectives: 5.9 us -> 0 us
    all_gather x1 -> x0, blocking collectives: 5.9 us -> none  [on_device(): reading = lax.all_gather(own_block, 'tm', axis=1, tiled=True)[0]]
    all_gather x1, waiting for transfers between devices: 15.8 us -> 13.1 us  [on_device(): adjoint_all = lax.all_gather(adjoint_local, 'tm')]
    all_to_all x1, waiting for transfers between devices: 1.85 us -> 3.71 us  [on_device(): lax.all_to_all(outgoing, ('tm', 'series'), split_axis=0, concat_axis=1, t...]
  transfers between devices with their start and end apart: 12 -> 12, of which waited for: 11 -> 11; matrix products, arithmetic and copies ran while one was open for 27% -> 28% of each run, Pallas kernels for 0% -> 0%
where the time goes in v4:
time: 154 us; the launch traced here: 153 us
  waiting for transfers between devices  43 us (28%)
  starting transfers between devices  28.8 us (19%)
  local copies, waits for them, and re-layouts  26 us (17%)
  matrix products  25.4 us (16%)
  other arithmetic  14.9 us (10%)
  between operations  14.7 us (10%)
    ppermute x10, waiting for transfers between devices, exchange(): return lax.ppermute(value, axis, pairs)  26.3 us
    ppermute x10, starting transfers between devices, exchange(): return lax.ppermute(value, axis, pairs)  21.6 us
    all_gather x1, waiting for transfers between devices, on_device(): adjoint_all = lax.all_gather(adjoint_local, 'tm')  13.1 us
    all_to_all x1, starting transfers between devices, on_device(): lax.all_to_all(outgoing, ('tm', 'series'), split_axis=0, concat_axis=1, t...  7.1 us
    unnamed x89, local copies, waits for them, and re-layouts  6.4 us
    convert_element_type x1, local copies, waits for them, and re-layouts, on_device(): xw_all = (x_all * tail_all[..., None]).astype(half)  5.38 us
    dot_general x1, matrix products, on_device(): picked = jnp.dot(onehot, bin_table, precision=lax.Precision.HIGHEST)  4.14 us
    all_to_all x1, waiting for transfers between devices, on_device(): lax.all_to_all(outgoing, ('tm', 'series'), split_axis=0, concat_axis=1, t...  3.71 us
  transfers between devices with their start and end apart: 12, of which 11 were waited for; matrix products, arithmetic and copies ran while one was open for 28% of the time, Pallas kernels for 0%

profile of v4, /device:TPU:1, one launch (start us, length us, event | category | flops | bytes accessed | tf_op | source)
XLA Modules:
  0.0 152.9 jit_solution(13268687076017906681)
XLA Ops:
  8.6 1.2 gather_fusion
  10.5 7.1 %all-to-all-start = ((f32[32,1,16]{2,1,0:T(1,128)}), f32[32,1,16]{2,1,0:T(1,128)S(1)}, u32[]{:S(2)}, u32[]{:S(2)}) async-start(f32[32,1,16]{2,1,0:T(1,128)} %bitcast), calls=%async_computation | async-start | bytes 32768 | tf_op jit(solution)/shard_map/all_to_all | solution.py:68
  19.3 1.3 copy.78
  20.6 3.7 %all-to-all-done = f32[32,1,16]{2,1,0:T(1,128)S(1)} async-done(((f32[32,1,16]{2,1,0:T(1,128)}), f32[32,1,16]{2,1,0:T(1,128)S(1)}, u32[]{:S(2)}, u32[]{:S(2)}) %all-to-all-start) | async-done | bytes 2080 | tf_op jit(solution)/shard_map/all_to_all | solution.py:68
  25.6 1.5 convert_reduce_fusion
  27.8 4.1 %fusion = f32[512,4]{0,1:T(4,128)S(1)} fusion(f32[4096]{0:T(1024)S(1)} %get-tuple-element.11, f32[4096]{0:T(1024)S(1)} %convert_element_type.106, f32[512]{0:T(512)S(1)} %le.22, f32[4096,1]{0,1:T(1,128)S(1)} %bitcast.183, f32[4096,1]{0,1:T(1,128)S(1)} %bitcast.178, f32[4096,1]{0,1:T(1,128)S(1)} %bitcast.177, f32[4096,1]{0,1:T(1,128)S(1)} %sub.79), kind=kOutput, calls=%fused_computation.3 | convolution fusion | flops 107003904 | bytes 108544 | tf_op jit(solution)/shard_map/dot_general | solution.py:77
  32.7 1.0 compare_select_fusion.1
  34.6 1.3 fusion.32
  36.6 0.9 fusion.17
  38.2 1.1 compare_select_fusion
  41.1 1.6 %convolution_convert_fusion = bf16[512,2304]{1,0:T(8,128)(2,1)S(1)} fusion(bf16[128,2304]{1,0:T(8,128)(2,1)S(1)} %copy-done, f32[128]{0:T(128)S(1)} %copy-done.25, f32[512]{0:T(512)S(1)} %bitcast.186), kind=kOutput, calls=%fused_computation.4 | convolution fusion | flops 303300608 | bytes 2951680 | tf_op jit(solution)/shard_map/dot_general | solution.py:98
  42.8 2.5 %slice_convert_fusion = f32[4,128,2048]{2,1,0:T(8,128)} fusion(bf16[4,128,2304]{2,1,0:T(8,128)(2,1)S(1)} %bitcast.160), kind=kLoop, calls=%fused_computation.11 | loop fusion | flops 1048576 | bytes 6291456 | tf_op jit(solution)/shard_map/convert_element_type | solution.py:108
  45.3 5.4 %copy.74 = f32[4,128,2048]{1,2,0:T(8,128)} copy(f32[4,128,2048]{2,1,0:T(8,128)} %slice_convert_fusion) | data formatting | bytes 8388608 | tf_op jit(solution)/shard_map/convert_element_type | solution.py:108
  50.7 1.0 copy.67
  51.7 1.6 %copy.70 = f32[32,128]{1,0:T(8,128)} copy(f32[32,128]{0,1:T(8,128)} %bitcast.168) | data formatting | bytes 32768 | tf_op jit(solution)/shard_map/transpose | solution.py:14
  55.4 1.0 mul.275
  56.4 2.6 %copy.81 = f32[128,2048]{1,0:T(8,128)} copy(f32[128,2048]{0,1:T(8,128)} %bitcast.165) | data formatting | bytes 2097152 | tf_op jit(solution)/shard_map/mul | solution.py:140
  59.0 2.1 %multiply_convert_fusion.3 = bf16[128,2048]{1,0:T(8,128)(2,1)} fusion(f32[128,2048]{1,0:T(8,128)} %copy.81, bf16[128,2304]{1,0:T(8,128)(2,1)S(1)} %copy-done.3), kind=kLoop, calls=%fused_computation.53 | loop fusion | flops 786432 | bytes 2097152 | tf_op jit(solution)/shard_map/convert_element_type | solution.py:96
  61.1 2.2 %copy.82 = bf16[128,2048]{0,1:T(8,128)(2,1)} copy(bf16[128,2048]{1,0:T(8,128)(2,1)} %multiply_convert_fusion.3) | data formatting | bytes 1048576 | tf_op jit(solution)/shard_map/convert_element_type | solution.py:96
  63.3 1.4 multiply_bitcast_fusion
  64.7 2.8 %fusion.5 = bf16[128,128]{0,1:T(8,128)(2,1)S(1)} fusion(bf16[128,32,64]{0,2,1:T(8,128)(2,1)} %bitcast.170, bf16[128,32,64]{0,2,1:T(8,128)(2,1)} %bitcast.163, f32[32,128]{1,0:T(8,128)} %get-tuple-element.16, f32[32,128]{1,0:T(8,128)} %copy.70, pred[128,128]{0,1:T(8,128)(4,1)} %iota_compare_fusion), kind=kOutput, calls=%fused_computation.13 | convolution fusion | flops 70238208 | bytes 1130496 | tf_op jit(solution)/shard_map/thp,shp->hts/dot_general | solution.py:143
  70.5 1.1 copy-done.6
  71.6 1.3 convolution_bitcast_fusion
  72.9 13.1 %all-gather.3.cloned.1.call-done = f32[128,64,128]{2,1,0:T(8,128)} async-done(((f32[32,64,128]{2,1,0:T(8,128)}), f32[128,64,128]{2,1,0:T(8,128)}) %all-gather.3.cloned.1.call-update) | async-done | bytes 4194320 | tf_op jit(solution)/shard_map/all_gather | solution.py:119
  86.0 2.4 %fusion.10 = bf16[128,32,64]{0,2,1:T(8,128)(2,1)S(1)} fusion(f32[128,32,64]{0,2,1:T(8,128)S(1)} %convolution_bitcast_fusion, f32[128,64,128]{2,1,0:T(8,128)} %all-gather.3.cloned.1.call-done, f32[128,32]{0,1:T(8,128)S(1)} %copy-done.13, f32[32]{0:T(128)S(1)} %copy-done.38, f32[32]{0:T(128)S(1)} %copy-done.33, f32[32]{0:T(128)S(1)} %copy-done.36, ...), kind=kOutput, calls=%fused_computation.24 | convolution fusion | flops 70254592 | bytes 4769283 | tf_op jit(solution)/shard_map/sn,hpn->shp/dot_general | solution.py:140
  88.4 2.4 %fusion.15 = bf16[128,128]{0,1:T(8,128)(2,1)S(1)} fusion(f32[128,128]{0,1:T(8,128)S(1)} %copy-done.17, bf16[128,32,64]{0,2,1:T(8,128)(2,1)S(1)} %bitcast.173, f32[128,64,128]{2,1,0:T(8,128)} %all-gather.3.cloned.1.call-done, f32[32]{0:T(128)S(1)} %copy-done.38, f32[32]{0:T(128)S(1)} %copy-done.36, f32[32]{0:T(128)S(1)} %copy-done.33, pred[]{:T(512)S(6)} %lt.78, ...), kind=kOutput, calls=%fused_computation.33 | convolution fusion | flops 69500928 | bytes 3768707 | tf_op jit(solution)/shard_map/shp,hpn->sn/dot_general | solution.py:146
  92.2 1.6 %collective-permute-done = f32[1152,128]{1,0:T(8,128)S(1)} collective-permute-done((f32[1152,128]{1,0:T(8,128)S(1)}, f32[1152,128]{1,0:T(8,128)S(1)}, u32[]{:S(2)}, u32[]{:S(2)}) %collective-permute-start) | collective-permute-done | bytes 589856 | tf_op jit(solution)/shard_map/ppermute | solution.py:26
  93.9 1.3 collective-permute-start.1
  95.2 7.0 %collective-permute-done.1 = f32[576,128]{1,0:T(8,128)S(1)} collective-permute-done((f32[576,128]{1,0:T(8,128)S(1)}, f32[576,128]{1,0:T(8,128)S(1)}, u32[]{:S(2)}, u32[]{:S(2)}) %collective-permute-start.1) | collective-permute-done | bytes 294944 | tf_op jit(solution)/shard_map/ppermute | solution.py:26
  102.3 1.2 collective-permute-start.2
  103.5 2.8 %collective-permute-done.2 = f32[288,128]{1,0:T(8,128)S(1)} collective-permute-done((f32[288,128]{1,0:T(8,128)S(1)}, f32[288,128]{1,0:T(8,128)S(1)}, u32[]{:S(2)}, u32[]{:S(2)}) %collective-permute-start.2) | collective-permute-done | bytes 147488 | tf_op jit(solution)/shard_map/ppermute | solution.py:26
  106.4 1.3 collective-permute-start.3
  107.7 2.0 %collective-permute-done.3 = f32[144,128]{1,0:T(8,128)S(1)} collective-permute-done((f32[144,128]{1,0:T(8,128)S(1)}, f32[144,128]{1,0:T(8,128)S(1)}, u32[]{:S(2)}, u32[]{:S(2)}) %collective-permute-start.3) | collective-permute-done | bytes 73760 | tf_op jit(solution)/shard_map/ppermute | solution.py:26
  109.7 2.2 %collective-permute-start.4 = (f32[72,128]{1,0:T(8,128)S(1)}, f32[72,128]{1,0:T(8,128)S(1)}, u32[]{:S(2)}, u32[]{:S(2)}) collective-permute-start(f32[72,128]{1,0:T(8,128)S(1)} %constant_dynamic-slice_fusion), channel_id=1, source_target_pairs={{0,4},{1,5},{2,6},{3,7},{4,0},{5,1},{6,2},{7,3},{8,12},{9,13},{10,... | collective-permute-start | bytes 110600 | tf_op jit(solution)/shard_map/ppermute | solution.py:26
  111.9 1.6 %collective-permute-done.4 = f32[72,128]{1,0:T(8,128)S(1)} collective-permute-done((f32[72,128]{1,0:T(8,128)S(1)}, f32[72,128]{1,0:T(8,128)S(1)}, u32[]{:S(2)}, u32[]{:S(2)}) %collective-permute-start.4) | collective-permute-done | bytes 36896 | tf_op jit(solution)/shard_map/ppermute | solution.py:26
  113.5 2.2 %collective-permute-start.5 = (f32[72,128]{1,0:T(8,128)S(1)}, f32[72,128]{1,0:T(8,128)S(1)}, u32[]{:S(2)}, u32[]{:S(2)}) collective-permute-start(f32[72,128]{1,0:T(8,128)S(1)} %dynamic-slice_add_fusion.4), channel_id=1, source_target_pairs={{0,4},{1,5},{2,6},{3,7},{4,0},{5,1},{6,2},{7,3},{8,12},{9,13},{10,... | collective-permute-start | bytes 110600 | tf_op jit(solution)/shard_map/ppermute | solution.py:26
  115.6 2.0 %collective-permute-done.5 = f32[72,128]{1,0:T(8,128)S(1)} collective-permute-done((f32[72,128]{1,0:T(8,128)S(1)}, f32[72,128]{1,0:T(8,128)S(1)}, u32[]{:S(2)}, u32[]{:S(2)}) %collective-permute-start.5) | collective-permute-done | bytes 36896 | tf_op jit(solution)/shard_map/ppermute | solution.py:26
  117.6 1.7 %collective-permute-start.6 = (f32[144,128]{1,0:T(8,128)S(1)}, f32[144,128]{1,0:T(8,128)S(1)}, u32[]{:S(2)}, u32[]{:S(2)}) collective-permute-start(f32[144,128]{1,0:T(8,128)S(1)} %maximum_select_fusion.4), channel_id=1, source_target_pairs={{0,2},{1,3},{2,0},{3,1},{4,6},{5,7},{6,4},{7,5},{8,10},{9,11},{10,... | collective-permute-start | bytes 221192 | tf_op jit(solution)/shard_map/ppermute | solution.py:26
  119.3 1.7 %collective-permute-done.6 = f32[144,128]{1,0:T(8,128)S(1)} collective-permute-done((f32[144,128]{1,0:T(8,128)S(1)}, f32[144,128]{1,0:T(8,128)S(1)}, u32[]{:S(2)}, u32[]{:S(2)}) %collective-permute-start.6) | collective-permute-done | bytes 73760 | tf_op jit(solution)/shard_map/ppermute | solution.py:26
  121.1 1.3 collective-permute-start.7
  122.3 2.8 %collective-permute-done.7 = f32[288,128]{1,0:T(8,128)S(1)} collective-permute-done((f32[288,128]{1,0:T(8,128)S(1)}, f32[288,128]{1,0:T(8,128)S(1)}, u32[]{:S(2)}, u32[]{:S(2)}) %collective-permute-start.7) | collective-permute-done | bytes 147488 | tf_op jit(solution)/shard_map/ppermute | solution.py:26
  125.2 1.3 collective-permute-start.8
  126.4 4.7 %collective-permute-done.8 = f32[576,128]{1,0:T(8,128)S(1)} collective-permute-done((f32[576,128]{1,0:T(8,128)S(1)}, f32[576,128]{1,0:T(8,128)S(1)}, u32[]{:S(2)}, u32[]{:S(2)}) %collective-permute-start.8) | collective-permute-done | bytes 294944 | tf_op jit(solution)/shard_map/ppermute | solution.py:26
  131.2 8.6 %collective-permute-start.9 = (f32[1152,128]{1,0:T(8,128)S(1)}, f32[1152,128]{1,0:T(8,128)S(1)}, u32[]{:S(2)}, u32[]{:S(2)}) collective-permute-start(f32[1152,128]{1,0:T(8,128)S(1)} %maximum_select_fusion.1), channel_id=1, source_target_pairs={{0,1},{1,0},{2,3},{3,2},{4,5},{5,4},{6,7},{7,6},{8,9},{9,8},{10,11... | collective-permute-start | bytes 1769480 | tf_op jit(solution)/shard_map/ppermute | solution.py:26
  139.8 1.3 convolution_bitcast_fusion.1
  141.1 2.4 %fusion.9 = bf16[128,32,64]{0,2,1:T(8,128)(2,1)S(1)} fusion(f32[128,32,64]{0,2,1:T(8,128)S(1)} %convolution_bitcast_fusion.1, f32[4,32,64,128]{3,2,1,0:T(8,128)} %copy-done.6, f32[128,32]{0,1:T(8,128)S(1)} %copy.77, f32[32]{0:T(128)S(1)} %copy-done.31, f32[32]{0:T(128)S(1)} %copy-done.34, f32[32]{0:T(128)S(1)} %copy-done.37, pred[]{:T(512)S(6)} %gt.24, ...), kind=kOutput, calls=%fused_computation.23 | convolution fusion | flops 70254592 | bytes 4769283 | tf_op jit(solution)/shard_map/tn,hpn->thp/dot_general | solution.py:133
  143.5 1.0 copy.84
  144.6 1.4 copy.85
  (150 shorter events, 17.2 us)
Async XLA Ops:
  7.2 24.9 %copy-start = (bf16[128,2304]{1,0:T(8,128)(2,1)S(1)}, bf16[128,2304]{1,0:T(8,128)(2,1)}, u32[]{:S(2)}) copy-start(bf16[128,2304]{1,0:T(8,128)(2,1)} %param.11) | copy-start | bytes 1769476
  10.5 13.8 %all-to-all-start = ((f32[32,1,16]{2,1,0:T(1,128)}), f32[32,1,16]{2,1,0:T(1,128)S(1)}, u32[]{:S(2)}, u32[]{:S(2)}) async-start(f32[32,1,16]{2,1,0:T(1,128)} %bitcast), calls=%async_computation | async-start | bytes 32768 | tf_op jit(solution)/shard_map/all_to_all | solution.py:68
  17.6 68.4 %all-gather.3.cloned.1.call-start = ((), (), s32[]{:S(2)}) async-start(), calls=%async_computation.1 | async-start | bytes 5242880 | tf_op jit(solution)/shard_map/all_gather | solution.py:119
  19.3 18.9 %copy-start.24 = (f32[128]{0:T(128)}, f32[128]{0:T(128)S(1)}, u32[]{:S(2)}) copy-start(f32[128]{0:T(128)S(1)} %add_multiply_fusion) | copy-start | bytes 1540
  20.6 16.0 %copy-start.4 = (bf16[1,128,2048]{1,2,0:T(8,128)(2,1)}, bf16[1,128,2048]{1,2,0:T(8,128)(2,1)S(1)}, u32[]{:S(2)}) copy-start(bf16[1,128,2048]{1,2,0:T(8,128)(2,1)S(1)} %copy.78) | copy-start | bytes 1572868
  27.8 4.9 %copy-start.39 = (bf16[128,32]{0,1:T(8,128)(2,1)S(1)}, bf16[128,32]{0,1:T(8,128)(2,1)}, u32[]{:S(2)}) copy-start(bf16[128,32]{0,1:T(8,128)(2,1)} %param.12) | copy-start | bytes 24580
  27.8 4.9 %copy-start.40 = (f32[32]{0:T(128)S(1)}, f32[32]{0:T(128)}, u32[]{:S(2)}) copy-start(f32[32]{0:T(128)} %param.13) | copy-start | bytes 388
  27.8 5.9 %copy-start.27 = (f32[32]{0:T(128)S(1)}, f32[32]{0:T(128)}, u32[]{:S(2)}) copy-start(f32[32]{0:T(128)} %param.14) | copy-start | bytes 388
  32.0 6.2 %copy-start.22 = (f32[512,1]{0,1:T(1,128)}, f32[512,1]{0,1:T(1,128)S(1)}, u32[]{:S(2)}) copy-start(f32[512,1]{0,1:T(1,128)S(1)} %fusion.93) | copy-start | bytes 6148
  32.0 3.9 %copy-start.28 = (f32[1,128]{1,0:T(1,128)}, f32[1,128]{1,0:T(1,128)S(1)}, u32[]{:S(2)}) copy-start(f32[1,128]{1,0:T(1,128)S(1)} %constant_dynamic-slice_fusion.5) | copy-start | bytes 1540
  32.6 4.0 %copy-start.2 = (bf16[128,2304]{1,0:T(8,128)(2,1)}, bf16[128,2304]{1,0:T(8,128)(2,1)S(1)}, u32[]{:S(2)}) copy-start(bf16[128,2304]{1,0:T(8,128)(2,1)S(1)} %convolution_convert_fusion.1) | copy-start | bytes 1769476
  34.6 3.0 %copy-start.7 = (f32[128,32]{1,0:T(8,128)}, f32[128,32]{1,0:T(8,128)S(1)}, u32[]{:S(2)}) copy-start(f32[128,32]{1,0:T(8,128)S(1)} %reduce_window_sum.46) | copy-start | bytes 49156
  39.3 1.8 %copy-start.23 = (f32[512,1]{0,1:T(1,128)S(1)}, f32[512,1]{0,1:T(1,128)}, u32[]{:S(2)}) copy-start(f32[512,1]{0,1:T(1,128)} %copy-done.22) | copy-start | bytes 6148
  39.3 1.8 %copy-start.25 = (f32[128]{0:T(128)S(1)}, f32[128]{0:T(128)}, u32[]{:S(2)}) copy-start(f32[128]{0:T(128)} %copy-done.24) | copy-start | bytes 1540
  45.3 5.4 %slice-start = ((bf16[128,2304]{1,0:T(8,128)(2,1)}), bf16[128,2048]{1,0:T(8,128)(2,1)S(1)}, s32[]{:S(2)}) async-start(bf16[128,2304]{1,0:T(8,128)(2,1)} %copy-done.2), calls=%async_computation.2 | async-start | bytes 1048576 | tf_op jit(solution)/shard_map/slice | solution.py:89
  51.7 7.3 %copy-start.3 = (bf16[128,2304]{1,0:T(8,128)(2,1)S(1)}, bf16[128,2304]{1,0:T(8,128)(2,1)}, u32[]{:S(2)}) copy-start(bf16[128,2304]{1,0:T(8,128)(2,1)} %copy-done.2) | copy-start | bytes 1769476
  64.7 4.8 %copy-start.30 = (f32[32]{0:T(128)}, f32[32]{0:T(128)S(1)}, u32[]{:S(2)}) copy-start(f32[32]{0:T(128)S(1)} %get-tuple-element.13) | copy-start | bytes 388
  64.7 4.8 %copy-start.32 = (f32[32]{0:T(128)}, f32[32]{0:T(128)S(1)}, u32[]{:S(2)}) copy-start(f32[32]{0:T(128)S(1)} %get-tuple-element.14) | copy-start | bytes 388
  64.7 4.8 %copy-start.35 = (f32[32]{0:T(128)}, f32[32]{0:T(128)S(1)}, u32[]{:S(2)}) copy-start(f32[32]{0:T(128)S(1)} %get-tuple-element.15) | copy-start | bytes 388
  64.7 4.1 %copy-start.1 = (f32[4,128,2048]{1,2,0:T(8,128)S(1)}, f32[4,128,2048]{1,2,0:T(8,128)}, u32[]{:S(2)}) copy-start(f32[4,128,2048]{1,2,0:T(8,128)} %copy.74) | copy-start | bytes 12582916
  64.7 4.1 %copy-start.11 = (f32[4,128,32]{1,2,0:T(8,128)S(1)}, f32[4,128,32]{1,2,0:T(8,128)}, u32[]{:S(2)}) copy-start(f32[4,128,32]{1,2,0:T(8,128)} %copy.76) | copy-start | bytes 196612
  68.7 1.7 %copy-start.15 = (f32[128,128]{0,1:T(8,128)}, f32[128,128]{0,1:T(8,128)S(1)}, u32[]{:S(2)}) copy-start(f32[128,128]{0,1:T(8,128)S(1)} %fusion.79) | copy-start | bytes 196612
  69.5 2.0 %copy-start.6 = (f32[4,32,64,128]{3,2,1,0:T(8,128)}, f32[4,32,64,128]{3,2,1,0:T(8,128)S(1)}, u32[]{:S(2)}) copy-start(f32[4,32,64,128]{3,2,1,0:T(8,128)S(1)} %fusion.4) | copy-start | bytes 12582916
  69.9 1.7 %copy-start.20 = (pred[128,128]{0,1:T(8,128)(4,1)S(1)}, pred[128,128]{0,1:T(8,128)(4,1)}, u32[]{:S(2)}) copy-start(pred[128,128]{0,1:T(8,128)(4,1)} %iota_compare_fusion) | copy-start | bytes 49156
  69.9 1.7 %copy-start.41 = (f32[32,128]{1,0:T(8,128)S(1)}, f32[32,128]{1,0:T(8,128)}, u32[]{:S(2)}) copy-start(f32[32,128]{1,0:T(8,128)} %get-tuple-element.16) | copy-start | bytes 49156
  71.5 14.4 %copy-start.13 = (f32[128,32]{0,1:T(8,128)S(1)}, f32[128,32]{0,1:T(8,128)}, u32[]{:S(2)}) copy-start(f32[128,32]{0,1:T(8,128)} %copy-done.12) | copy-start | bytes 49156
  71.6 14.4 %copy-start.33 = (f32[32]{0:T(128)S(1)}, f32[32]{0:T(128)}, u32[]{:S(2)}) copy-start(f32[32]{0:T(128)} %copy-done.32) | copy-start | bytes 388
  71.6 14.4 %copy-start.36 = (f32[32]{0:T(128)S(1)}, f32[32]{0:T(128)}, u32[]{:S(2)}) copy-start(f32[32]{0:T(128)} %copy-done.35) | copy-start | bytes 388
  71.6 14.4 %copy-start.38 = (f32[32]{0:T(128)S(1)}, f32[32]{0:T(128)}, u32[]{:S(2)}) copy-start(f32[32]{0:T(128)} %get-tuple-element.12) | copy-start | bytes 388
  72.9 15.5 %copy-start.10 = (bf16[128,2048]{0,1:T(8,128)(2,1)S(1)}, bf16[128,2048]{0,1:T(8,128)(2,1)}, u32[]{:S(2)}) copy-start(bf16[128,2048]{0,1:T(8,128)(2,1)} %copy.82) | copy-start | bytes 1572868
  72.9 15.5 %copy-start.17 = (f32[128,128]{0,1:T(8,128)S(1)}, f32[128,128]{0,1:T(8,128)}, u32[]{:S(2)}) copy-start(f32[128,128]{0,1:T(8,128)} %fusion.82) | copy-start | bytes 196612
  88.4 2.4 %copy-start.26 = (f32[128]{0:T(128)S(1)}, f32[128]{0:T(128)}, u32[]{:S(2)}) copy-start(f32[128]{0:T(128)} %copy-done.24) | copy-start | bytes 1540
  88.4 2.4 %copy-start.29 = (f32[1,128]{1,0:T(1,128)S(1)}, f32[1,128]{1,0:T(1,128)}, u32[]{:S(2)}) copy-start(f32[1,128]{1,0:T(1,128)} %copy-done.28) | copy-start | bytes 1540
  91.5 2.4 %collective-permute-start = (f32[1152,128]{1,0:T(8,128)S(1)}, f32[1152,128]{1,0:T(8,128)S(1)}, u32[]{:S(2)}, u32[]{:S(2)}) collective-permute-start(f32[1152,128]{1,0:T(8,128)S(1)} %constant_dynamic-slice_fusion.4), channel_id=1, source_target_pairs={{0,1},{1,0},{2,3},{3,2},{4,5},{5,4},{6,7},{7,6},{8,9},{9,8},{10,11... | collective-permute-start | bytes 1769480 | tf_op jit(solution)/shard_map/ppermute | solution.py:26
  93.9 8.3 %collective-permute-start.1 = (f32[576,128]{1,0:T(8,128)S(1)}, f32[576,128]{1,0:T(8,128)S(1)}, u32[]{:S(2)}, u32[]{:S(2)}) collective-permute-start(f32[576,128]{1,0:T(8,128)S(1)} %constant_dynamic-slice_fusion.3), channel_id=1, source_target_pairs={{0,8},{8,0},{16,24},{24,16},{1,9},{9,1},{17,25},{25,17},{2,10},{10... | collective-permute-start | bytes 884744 | tf_op jit(solution)/shard_map/ppermute | solution.py:26
  95.2 44.5 %copy-start.8 = (bf16[128,2048]{0,1:T(8,128)(2,1)S(1)}, bf16[128,2048]{0,1:T(8,128)(2,1)}, u32[]{:S(2)}) copy-start(bf16[128,2048]{0,1:T(8,128)(2,1)} %copy.67) | copy-start | bytes 1572868
  95.2 44.5 %copy-start.16 = (f32[128,128]{0,1:T(8,128)S(1)}, f32[128,128]{0,1:T(8,128)}, u32[]{:S(2)}) copy-start(f32[128,128]{0,1:T(8,128)} %copy-done.15) | copy-start | bytes 196612
  95.2 44.5 %copy-start.19 = (f32[32,128]{1,0:T(8,128)S(1)}, f32[32,128]{1,0:T(8,128)}, u32[]{:S(2)}) copy-start(f32[32,128]{1,0:T(8,128)} %copy.70) | copy-start | bytes 49156
  95.2 44.5 %copy-start.21 = (pred[128,128]{0,1:T(8,128)(4,1)S(1)}, pred[128,128]{0,1:T(8,128)(4,1)}, u32[]{:S(2)}) copy-start(pred[128,128]{0,1:T(8,128)(4,1)} %iota_compare_fusion) | copy-start | bytes 49156
  95.2 44.5 %copy-start.42 = (f32[32,128]{1,0:T(8,128)S(1)}, f32[32,128]{1,0:T(8,128)}, u32[]{:S(2)}) copy-start(f32[32,128]{1,0:T(8,128)} %get-tuple-element.16) | copy-start | bytes 49156
  102.3 4.1 %collective-permute-start.2 = (f32[288,128]{1,0:T(8,128)S(1)}, f32[288,128]{1,0:T(8,128)S(1)}, u32[]{:S(2)}, u32[]{:S(2)}) collective-permute-start(f32[288,128]{1,0:T(8,128)S(1)} %constant_dynamic-slice_fusion.2), channel_id=1, source_target_pairs={{0,16},{8,24},{16,0},{24,8},{1,17},{9,25},{17,1},{25,9},{2,18},{10... | collective-permute-start | bytes 442376 | tf_op jit(solution)/shard_map/ppermute | solution.py:26
  106.4 3.3 %collective-permute-start.3 = (f32[144,128]{1,0:T(8,128)S(1)}, f32[144,128]{1,0:T(8,128)S(1)}, u32[]{:S(2)}, u32[]{:S(2)}) collective-permute-start(f32[144,128]{1,0:T(8,128)S(1)} %constant_dynamic-slice_fusion.1), channel_id=1, source_target_pairs={{0,2},{1,3},{2,0},{3,1},{4,6},{5,7},{6,4},{7,5},{8,10},{9,11},{10,... | collective-permute-start | bytes 221192 | tf_op jit(solution)/shard_map/ppermute | solution.py:26
  109.7 3.8 %collective-permute-start.4 = (f32[72,128]{1,0:T(8,128)S(1)}, f32[72,128]{1,0:T(8,128)S(1)}, u32[]{:S(2)}, u32[]{:S(2)}) collective-permute-start(f32[72,128]{1,0:T(8,128)S(1)} %constant_dynamic-slice_fusion), channel_id=1, source_target_pairs={{0,4},{1,5},{2,6},{3,7},{4,0},{5,1},{6,2},{7,3},{8,12},{9,13},{10,... | collective-permute-start | bytes 110600 | tf_op jit(solution)/shard_map/ppermute | solution.py:26
  113.5 4.2 %collective-permute-start.5 = (f32[72,128]{1,0:T(8,128)S(1)}, f32[72,128]{1,0:T(8,128)S(1)}, u32[]{:S(2)}, u32[]{:S(2)}) collective-permute-start(f32[72,128]{1,0:T(8,128)S(1)} %dynamic-slice_add_fusion.4), channel_id=1, source_target_pairs={{0,4},{1,5},{2,6},{3,7},{4,0},{5,1},{6,2},{7,3},{8,12},{9,13},{10,... | collective-permute-start | bytes 110600 | tf_op jit(solution)/shard_map/ppermute | solution.py:26
  117.6 3.4 %collective-permute-start.6 = (f32[144,128]{1,0:T(8,128)S(1)}, f32[144,128]{1,0:T(8,128)S(1)}, u32[]{:S(2)}, u32[]{:S(2)}) collective-permute-start(f32[144,128]{1,0:T(8,128)S(1)} %maximum_select_fusion.4), channel_id=1, source_target_pairs={{0,2},{1,3},{2,0},{3,1},{4,6},{5,7},{6,4},{7,5},{8,10},{9,11},{10,... | collective-permute-start | bytes 221192 | tf_op jit(solution)/shard_map/ppermute | solution.py:26
  121.1 4.1 %collective-permute-start.7 = (f32[288,128]{1,0:T(8,128)S(1)}, f32[288,128]{1,0:T(8,128)S(1)}, u32[]{:S(2)}, u32[]{:S(2)}) collective-permute-start(f32[288,128]{1,0:T(8,128)S(1)} %maximum_select_fusion.3), channel_id=1, source_target_pairs={{0,16},{8,24},{16,0},{24,8},{1,17},{9,25},{17,1},{25,9},{2,18},{10... | collective-permute-start | bytes 442376 | tf_op jit(solution)/shard_map/ppermute | solution.py:26
  125.2 5.9 %collective-permute-start.8 = (f32[576,128]{1,0:T(8,128)S(1)}, f32[576,128]{1,0:T(8,128)S(1)}, u32[]{:S(2)}, u32[]{:S(2)}) collective-permute-start(f32[576,128]{1,0:T(8,128)S(1)} %maximum_select_fusion.2), channel_id=1, source_target_pairs={{0,8},{8,0},{16,24},{24,16},{1,9},{9,1},{17,25},{25,17},{2,10},{10... | collective-permute-start | bytes 884744 | tf_op jit(solution)/shard_map/ppermute | solution.py:26
  131.2 13.4 %collective-permute-start.9 = (f32[1152,128]{1,0:T(8,128)S(1)}, f32[1152,128]{1,0:T(8,128)S(1)}, u32[]{:S(2)}, u32[]{:S(2)}) collective-permute-start(f32[1152,128]{1,0:T(8,128)S(1)} %maximum_select_fusion.1), channel_id=1, source_target_pairs={{0,1},{1,0},{2,3},{3,2},{4,5},{5,4},{6,7},{7,6},{8,9},{9,8},{10,11... | collective-permute-start | bytes 1769480 | tf_op jit(solution)/shard_map/ppermute | solution.py:26
  (8 other events, 9.6 us)
Sparse Core Ops, SparseCore 0:
  36.1 49.8 all-gather.2

commit v5 on v2

--- a/solution.py
+++ b/solution.py
@@ -15,6 +15,65 @@
     return jnp.where(causal[None], jnp.exp(jnp.where(causal[None], log_span, -60.0)), 0.0)
 
 
+def axis_bits(axis):
+    size = lax.axis_size(axis)
+    assert size & (size - 1) == 0
+    return [1 << k for k in range(size.bit_length() - 1)]
+
+
+def exchange(value, axis, flip):
+    pairs = [(i, i ^ flip) for i in range(lax.axis_size(axis))]
+    return lax.ppermute(value, axis, pairs)
+
+
+def bit_groups():
+    tm_bits, series_bits = axis_bits("tm"), axis_bits("series")
+    groups = [("series", series_bits[:1])] if series_bits else []
+    for axis, bits in (("tm", tm_bits), ("series", series_bits[1:])):
+        groups += [(axis, bits[i : i + 2]) for i in range(0, len(bits), 2)]
+    return groups
+
+
+def group_round(value, axis, bits, scatter):
+    index = lax.axis_index(axis)
+    coord = sum(((index // b) % 2) * (1 << j) for j, b in enumerate(bits))
+    size = 1 << len(bits)
+
+    def flip_of(m):
+        return sum(b for j, b in enumerate(bits) if (m >> j) & 1)
+
+    rows = value.shape[0]
+    if scatter:
+        part = rows // size
+        keep = lax.dynamic_slice_in_dim(value, coord * part, part)
+        got = [
+            exchange(lax.dynamic_slice_in_dim(value, (coord ^ m) * part, part), axis, flip_of(m))
+            for m in range(1, size)
+        ]
+        for piece in got:
+            keep = keep + piece
+        return keep
+    got = [value] + [exchange(value, axis, flip_of(m)) for m in range(1, size)]
+    stacked = jnp.stack(got)
+    return [lax.dynamic_index_in_dim(stacked, coord ^ q, 0, keepdims=False) for q in range(size)]
+
+
+def tree_psum(value):
+    done = []
+    for axis, bits in bit_groups():
+        if value.shape[0] % (8 << len(bits)) == 0:
+            value = group_round(value, axis, bits, True)
+            done.append((axis, bits))
+        else:
+            pieces = group_round(value, axis, bits, False)
+            value = pieces[0]
+            for piece in pieces[1:]:
+                value = value + piece
+    for axis, bits in reversed(done):
+        value = jnp.concatenate(group_round(value, axis, bits, False))
+    return value
+
+
 def on_device(codes, owner_slot, edges, w_in, w_dt, dt_bias, decay_rate, grad_out):
     fl = jnp.float32
     half = jnp.bfloat16
@@ -29,8 +88,8 @@
     my_block = lax.axis_index("tm")
 
     ordered = jnp.take(codes, owner_slot, axis=0).astype(fl)
-    own_block = lax.all_to_all(ordered, "series", split_axis=0, concat_axis=1, tiled=True)
-    reading = lax.all_gather(own_block, "tm", axis=1, tiled=True)[0]
+    outgoing = jnp.tile(ordered, (n_blocks, 1))
+    reading = lax.all_to_all(outgoing, ("tm", "series"), split_axis=0, concat_axis=1, tiled=True)[0]
     edge_float = edges.astype(fl)
     upper_edge = jnp.concatenate([edge_float[1:], jnp.full((1,), code_ceiling, fl)])
     onehot = (
@@ -121,10 +180,8 @@
         ],
         axis=1,
     )
-    local_grad = jnp.einsum("tf,tw->fw", features, grad_rows, preferred_element_type=fl)
-    share_grad = lax.psum_scatter(local_grad, "series", scatter_dimension=1, tiled=True)
-    share_grad = lax.psum(share_grad, "tm")
-    total_grad = lax.all_gather(share_grad, "series", axis=1, tiled=True)
+    local_grad = jnp.einsum("tw,tf->wf", grad_rows, features, preferred_element_type=fl)
+    total_grad = tree_psum(local_grad).T
     grad_in = total_grad / math.sqrt(series_count * seq_len)
     return (ssd_output, grad_in)
 

time: 210 us -> 145 us (0.69)
  waiting for transfers between devices: 114 us -> 35.5 us
  starting transfers between devices: 6.9 us -> 26.6 us
  blocking collectives: 5.9 us -> 0 us
    psum x1 -> x0, waiting for transfers between devices: 46 us -> none  [on_device(): share_grad = lax.psum(share_grad, 'tm')]
    reduce_scatter x1 -> x0, waiting for transfers between devices: 29.5 us -> none  [on_device(): lax.psum_scatter(local_grad, 'series', scatter_dimension=1, tiled=True)]
    all_gather x1 -> x0, waiting for transfers between devices: 20.4 us -> none  [on_device(): total_grad = lax.all_gather(share_grad, 'series', axis=1, tiled=True)]
    ppermute x0 -> x14, starting transfers between devices: none -> 19.4 us  [exchange(): return lax.ppermute(value, axis, pairs)]
    ppermute x0 -> x14, waiting for transfers between devices: none -> 18.4 us  [exchange(): return lax.ppermute(value, axis, pairs)]
    all_gather x1 -> x0, blocking collectives: 5.9 us -> none  [on_device(): reading = lax.all_gather(own_block, 'tm', axis=1, tiled=True)[0]]
    all_gather x1, waiting for transfers between devices: 15.7 us -> 13.3 us  [on_device(): adjoint_all = lax.all_gather(adjoint_local, 'tm')]
    unnamed x79 -> x75, local copies, waits for them, and re-layouts: 6.36 us -> 6.43 us
  transfers between devices with their start and end apart: 5 -> 16, of which waited for: 5 -> 13; matrix products, arithmetic and copies ran while one was open for 20% -> 30% of each run, Pallas kernels for 0% -> 0%
where the time goes in v5:
time: 145 us; the launch traced here: 144 us
  waiting for transfers between devices  35.5 us (24%)
  matrix products  26.8 us (18%)
  starting transfers between devices  26.6 us (18%)
  local copies, waits for them, and re-layouts  25.2 us (17%)
  other arithmetic  15.1 us (10%)
  between operations  14.7 us (10%)
    ppermute x14, starting transfers between devices, exchange(): return lax.ppermute(value, axis, pairs)  19.4 us
    ppermute x14, waiting for transfers between devices, exchange(): return lax.ppermute(value, axis, pairs)  18.4 us
    all_gather x1, waiting for transfers between devices, on_device(): adjoint_all = lax.all_gather(adjoint_local, 'tm')  13.3 us
    all_to_all x1, starting transfers between devices, on_device(): lax.all_to_all(outgoing, ('tm', 'series'), split_axis=0, concat_axis=1, t...  7.1 us
    unnamed x75, local copies, waits for them, and re-layouts  6.43 us
    convert_element_type x1, local copies, waits for them, and re-layouts, on_device(): xw_all = (x_all * tail_all[..., None]).astype(half)  5.34 us
    dot_general x1, matrix products, on_device(): picked = jnp.dot(onehot, bin_table, precision=lax.Precision.HIGHEST)  4.14 us
    all_to_all x1, waiting for transfers between devices, on_device(): lax.all_to_all(outgoing, ('tm', 'series'), split_axis=0, concat_axis=1, t...  3.71 us
  transfers between devices with their start and end apart: 16, of which 13 were waited for; matrix products, arithmetic and copies ran while one was open for 30% of the time, Pallas kernels for 0%

profile of v5, /device:TPU:1, one launch (start us, length us, event | category | flops | bytes accessed | tf_op | source)
XLA Modules:
  0.0 143.9 jit_solution(17921441672896526815)
XLA Ops:
  8.6 1.2 gather_fusion
  10.5 7.1 %all-to-all-start = ((f32[32,1,16]{2,1,0:T(1,128)}), f32[32,1,16]{2,1,0:T(1,128)S(1)}, u32[]{:S(2)}, u32[]{:S(2)}) async-start(f32[32,1,16]{2,1,0:T(1,128)} %bitcast), calls=%async_computation | async-start | bytes 32768 | tf_op jit(solution)/shard_map/all_to_all | solution.py:92
  19.3 1.3 copy.95
  20.6 3.7 %all-to-all-done = f32[32,1,16]{2,1,0:T(1,128)S(1)} async-done(((f32[32,1,16]{2,1,0:T(1,128)}), f32[32,1,16]{2,1,0:T(1,128)S(1)}, u32[]{:S(2)}, u32[]{:S(2)}) %all-to-all-start) | async-done | bytes 2080 | tf_op jit(solution)/shard_map/all_to_all | solution.py:92
  25.6 1.5 %convert_reduce_fusion = f32[4096]{0:T(1024)S(1)} fusion(f32[4096]{0:T(1024)S(1)} %get-tuple-element.33, f32[4096]{0:T(1024)S(1)} %convert_element_type.106, f32[512]{0:T(512)S(1)} %le.22), kind=kLoop, calls=%fused_computation.1 | loop fusion | flops 10481664 | bytes 51200 | tf_op jit(solution)/shard_map/reduce_sum | solution.py:98
  27.8 4.1 %fusion = f32[512,4]{0,1:T(4,128)S(1)} fusion(f32[4096]{0:T(1024)S(1)} %get-tuple-element.33, f32[4096]{0:T(1024)S(1)} %convert_element_type.106, f32[512]{0:T(512)S(1)} %le.22, f32[4096,1]{0,1:T(1,128)S(1)} %bitcast.223, f32[4096,1]{0,1:T(1,128)S(1)} %bitcast.215, f32[4096,1]{0,1:T(1,128)S(1)} %bitcast.214, f32[4096,1]{0,1:T(1,128)S(1)} %sub.69), kind=kOutput, calls=%fused_computation.3 | convolution fusion | flops 107003904 | bytes 108544 | tf_op jit(solution)/shard_map/dot_general | solution.py:101
  32.6 1.0 compare_select_fusion.1
  34.7 1.3 fusion.35
  36.7 0.9 fusion.16
  38.3 1.0 copy.84
  40.0 1.1 compare_select_fusion
  42.9 2.3 %convolution_convert_fusion = bf16[512,2304]{1,0:T(8,128)(2,1)S(1)} fusion(bf16[128,2304]{1,0:T(8,128)(2,1)S(1)} %copy-done, f32[128]{0:T(128)} %copy-done.19, f32[512]{0:T(512)} %bitcast.226), kind=kOutput, calls=%fused_computation.4 | convolution fusion | flops 303300608 | bytes 2951680 | tf_op jit(solution)/shard_map/dot_general | solution.py:122
  45.2 2.6 %slice_convert_fusion = f32[4,128,2048]{2,1,0:T(8,128)} fusion(bf16[4,128,2304]{2,1,0:T(8,128)(2,1)S(1)} %bitcast.192), kind=kLoop, calls=%fused_computation.11 | loop fusion | flops 1048576 | bytes 6291456 | tf_op jit(solution)/shard_map/convert_element_type | solution.py:132
  47.7 5.3 %copy.91 = f32[4,128,2048]{1,2,0:T(8,128)} copy(f32[4,128,2048]{2,1,0:T(8,128)} %slice_convert_fusion) | data formatting | bytes 8388608 | tf_op jit(solution)/shard_map/convert_element_type | solution.py:132
  55.2 1.0 mul.283
  56.2 2.5 %copy.98 = f32[128,2048]{1,0:T(8,128)} copy(f32[128,2048]{0,1:T(8,128)} %bitcast.197) | data formatting | bytes 2097152 | tf_op jit(solution)/shard_map/mul | solution.py:164
  58.8 2.1 %multiply_convert_fusion.3 = bf16[128,2048]{1,0:T(8,128)(2,1)} fusion(f32[128,2048]{1,0:T(8,128)} %copy.98, bf16[128,2304]{1,0:T(8,128)(2,1)S(1)} %convolution_convert_fusion.1), kind=kLoop, calls=%fused_computation.56 | loop fusion | flops 786432 | bytes 2097152 | tf_op jit(solution)/shard_map/convert_element_type | solution.py:120
  60.9 2.2 %copy.99 = bf16[128,2048]{0,1:T(8,128)(2,1)} copy(bf16[128,2048]{1,0:T(8,128)(2,1)} %multiply_convert_fusion.3) | data formatting | bytes 1048576 | tf_op jit(solution)/shard_map/convert_element_type | solution.py:120
  63.1 1.4 multiply_bitcast_fusion
  64.5 2.8 %fusion.5 = bf16[128,128]{0,1:T(8,128)(2,1)S(1)} fusion(bf16[128,32,64]{0,2,1:T(8,128)(2,1)} %bitcast.203, bf16[128,32,64]{0,2,1:T(8,128)(2,1)} %bitcast.195, f32[32,128]{1,0:T(8,128)} %get-tuple-element.38, f32[32,128]{1,0:T(8,128)} %copy.87, pred[128,128]{0,1:T(8,128)(4,1)} %iota_compare_fusion), kind=kOutput, calls=%fused_computation.13 | convolution fusion | flops 70238208 | bytes 1130496 | tf_op jit(solution)/shard_map/thp,shp->hts/dot_general | solution.py:167
  67.5 0.8 fusion.85
  70.2 1.1 copy-done.4
  71.4 1.3 convolution_bitcast_fusion
  72.7 13.3 %all-gather.3.cloned.1.call-done = f32[128,64,128]{2,1,0:T(8,128)} async-done(((f32[32,64,128]{2,1,0:T(8,128)}), f32[128,64,128]{2,1,0:T(8,128)}) %all-gather.3.cloned.1.call-update) | async-done | bytes 4194320 | tf_op jit(solution)/shard_map/all_gather | solution.py:143
  86.0 2.4 %fusion.10 = bf16[128,32,64]{0,2,1:T(8,128)(2,1)S(1)} fusion(f32[128,32,64]{0,2,1:T(8,128)S(1)} %convolution_bitcast_fusion, f32[128,64,128]{2,1,0:T(8,128)} %all-gather.3.cloned.1.call-done, f32[128,32]{0,1:T(8,128)S(1)} %copy-done.11, f32[32]{0:T(128)S(1)} %copy-done.32, f32[32]{0:T(128)S(1)} %copy-done.27, f32[32]{0:T(128)S(1)} %copy-done.30, ...), kind=kOutput, calls=%fused_computation.28 | convolution fusion | flops 70254592 | bytes 4769283 | tf_op jit(solution)/shard_map/sn,hpn->shp/dot_general | solution.py:164
  88.4 2.4 %fusion.14 = bf16[128,128]{0,1:T(8,128)(2,1)S(1)} fusion(f32[128,128]{0,1:T(8,128)S(1)} %copy-done.15, bf16[128,32,64]{0,2,1:T(8,128)(2,1)S(1)} %bitcast.206, f32[128,64,128]{2,1,0:T(8,128)} %all-gather.3.cloned.1.call-done, f32[32]{0:T(128)S(1)} %copy-done.32, f32[32]{0:T(128)S(1)} %copy-done.30, f32[32]{0:T(128)S(1)} %copy-done.27, pred[]{:T(512)S(6)} %lt.116, ...), kind=kOutput, calls=%fused_computation.36 | convolution fusion | flops 69500928 | bytes 3768707 | tf_op jit(solution)/shard_map/shp,hpn->sn/dot_general | solution.py:170
  92.3 1.6 %collective-permute-done = f32[1152,128]{1,0:T(8,128)S(1)} collective-permute-done((f32[1152,128]{1,0:T(8,128)S(1)}, f32[1152,128]{1,0:T(8,128)S(1)}, u32[]{:S(2)}, u32[]{:S(2)}) %collective-permute-start) | collective-permute-done | bytes 589856 | tf_op jit(solution)/shard_map/ppermute | solution.py:26
  94.0 1.2 collective-permute-start.1
  95.5 1.2 collective-permute-start.3
  96.7 2.4 %collective-permute-done.1 = f32[288,128]{1,0:T(8,128)S(1)} collective-permute-done((f32[288,128]{1,0:T(8,128)S(1)}, f32[288,128]{1,0:T(8,128)S(1)}, u32[]{:S(2)}, u32[]{:S(2)}) %collective-permute-start.1) | collective-permute-done | bytes 147488 | tf_op jit(solution)/shard_map/ppermute | solution.py:26
  99.1 0.9 collective-permute-done.2
  100.0 3.2 %collective-permute-done.3 = f32[288,128]{1,0:T(8,128)S(1)} collective-permute-done((f32[288,128]{1,0:T(8,128)S(1)}, f32[288,128]{1,0:T(8,128)S(1)}, u32[]{:S(2)}, u32[]{:S(2)}) %collective-permute-start.3) | collective-permute-done | bytes 147488 | tf_op jit(solution)/shard_map/ppermute | solution.py:26
  103.3 1.3 collective-permute-start.4
  104.6 2.1 %collective-permute-start.5 = (f32[72,128]{1,0:T(8,128)S(1)}, f32[72,128]{1,0:T(8,128)S(1)}, u32[]{:S(2)}, u32[]{:S(2)}) collective-permute-start(f32[72,128]{1,0:T(8,128)S(1)} %get-tuple-element.31), channel_id=1, source_target_pairs={{0,4},{1,5},{2,6},{3,7},{4,0},{5,1},{6,2},{7,3},{8,12},{9,13},{10,... | collective-permute-start | bytes 110600 | tf_op jit(solution)/shard_map/ppermute | solution.py:26
  106.9 1.8 %collective-permute-done.5 = f32[72,128]{1,0:T(8,128)S(1)} collective-permute-done((f32[72,128]{1,0:T(8,128)S(1)}, f32[72,128]{1,0:T(8,128)S(1)}, u32[]{:S(2)}, u32[]{:S(2)}) %collective-permute-start.5) | collective-permute-done | bytes 36896 | tf_op jit(solution)/shard_map/ppermute | solution.py:26
  108.7 2.6 %collective-permute-done.6 = f32[72,128]{1,0:T(8,128)S(1)} collective-permute-done((f32[72,128]{1,0:T(8,128)S(1)}, f32[72,128]{1,0:T(8,128)S(1)}, u32[]{:S(2)}, u32[]{:S(2)}) %collective-permute-start.6) | collective-permute-done | bytes 36896 | tf_op jit(solution)/shard_map/ppermute | solution.py:26
  111.4 0.8 collective-permute-start.8
  112.2 2.7 %collective-permute-start.9 = (f32[72,128]{1,0:T(8,128)S(1)}, f32[72,128]{1,0:T(8,128)S(1)}, u32[]{:S(2)}, u32[]{:S(2)}) collective-permute-start(f32[72,128]{1,0:T(8,128)S(1)} %add_add_fusion.1), channel_id=1, source_target_pairs={{0,6},{1,7},{2,4},{3,5},{4,2},{5,3},{6,0},{7,1},{8,14},{9,15},{10,... | collective-permute-start | bytes 110600 | tf_op jit(solution)/shard_map/ppermute | solution.py:26
  115.2 1.9 %collective-permute-done.9 = f32[72,128]{1,0:T(8,128)S(1)} collective-permute-done((f32[72,128]{1,0:T(8,128)S(1)}, f32[72,128]{1,0:T(8,128)S(1)}, u32[]{:S(2)}, u32[]{:S(2)}) %collective-permute-start.9) | collective-permute-done | bytes 36896 | tf_op jit(solution)/shard_map/ppermute | solution.py:26
  117.6 1.1 collective-permute-start.11
  118.7 1.2 collective-permute-start.12
  119.9 1.3 collective-permute-done.10
  121.6 2.0 %collective-permute-done.12 = f32[288,128]{1,0:T(8,128)S(1)} collective-permute-done((f32[288,128]{1,0:T(8,128)S(1)}, f32[288,128]{1,0:T(8,128)S(1)}, u32[]{:S(2)}, u32[]{:S(2)}) %collective-permute-start.12) | collective-permute-done | bytes 147488 | tf_op jit(solution)/shard_map/ppermute | solution.py:26
  123.8 6.0 %collective-permute-start.13 = (f32[1152,128]{1,0:T(8,128)S(1)}, f32[1152,128]{1,0:T(8,128)S(1)}, u32[]{:S(2)}, u32[]{:S(2)}) collective-permute-start(f32[1152,128]{1,0:T(8,128)S(1)} %get-tuple-element.14), channel_id=1, source_target_pairs={{0,1},{1,0},{2,3},{3,2},{4,5},{5,4},{6,7},{7,6},{8,9},{9,8},{10,11... | collective-permute-start | bytes 1769480 | tf_op jit(solution)/shard_map/ppermute | solution.py:26
  129.8 2.1 %convolution_bitcast_fusion.1 = f32[128,32,64]{0,2,1:T(8,128)S(1)} fusion(bf16[128,32,64]{0,2,1:T(8,128)(2,1)S(1)} %bitcast.204, f32[32,128]{1,0:T(8,128)} %get-tuple-element.38, f32[32,128]{1,0:T(8,128)} %copy.87, f32[128,128]{0,1:T(8,128)S(1)} %copy-done.14, pred[128,128]{0,1:T(8,128)(4,1)} %iota_compare_fusion), kind=kOutput, calls=%fused_computation.26 | convolution fusion | flops 70254592 | bytes 1687552 | tf_op jit(solution)/shard_map/hts,shp->thp/dot_general | solution.py:154
  132.0 2.4 %fusion.9 = bf16[128,32,64]{0,2,1:T(8,128)(2,1)S(1)} fusion(f32[128,32,64]{0,2,1:T(8,128)S(1)} %convolution_bitcast_fusion.1, f32[4,32,64,128]{3,2,1,0:T(8,128)} %copy-done.4, f32[128,32]{0,1:T(8,128)S(1)} %copy.94, f32[32]{0:T(128)S(1)} %copy-done.25, f32[32]{0:T(128)S(1)} %copy-done.28, f32[32]{0:T(128)S(1)} %copy-done.31, pred[]{:T(512)S(6)} %gt.24, ...), kind=kOutput, calls=%fused_computation.27 | convolution fusion | flops 70254592 | bytes 4769283 | tf_op jit(solution)/shard_map/tn,hpn->thp/dot_general | solution.py:157
  134.3 1.0 copy.101
  135.7 1.4 copy.102
  (142 shorter events, 19.0 us)
Async XLA Ops:
  7.2 24.9 %copy-start = (bf16[128,2304]{1,0:T(8,128)(2,1)S(1)}, bf16[128,2304]{1,0:T(8,128)(2,1)}, u32[]{:S(2)}) copy-start(bf16[128,2304]{1,0:T(8,128)(2,1)} %param.11) | copy-start | bytes 1769476
  10.5 13.8 %all-to-all-start = ((f32[32,1,16]{2,1,0:T(1,128)}), f32[32,1,16]{2,1,0:T(1,128)S(1)}, u32[]{:S(2)}, u32[]{:S(2)}) async-start(f32[32,1,16]{2,1,0:T(1,128)} %bitcast), calls=%async_computation | async-start | bytes 32768 | tf_op jit(solution)/shard_map/all_to_all | solution.py:92
  17.6 68.4 %all-gather.3.cloned.1.call-start = ((), (), s32[]{:S(2)}) async-start(), calls=%async_computation.1 | async-start | bytes 5242880 | tf_op jit(solution)/shard_map/all_gather | solution.py:143
  19.3 20.7 %copy-start.19 = (f32[128]{0:T(128)}, f32[128]{0:T(128)S(1)}, u32[]{:S(2)}) copy-start(f32[128]{0:T(128)S(1)} %add_multiply_fusion) | copy-start | bytes 1540
  20.6 16.1 %copy-start.2 = (bf16[1,128,2048]{1,2,0:T(8,128)(2,1)}, bf16[1,128,2048]{1,2,0:T(8,128)(2,1)S(1)}, u32[]{:S(2)}) copy-start(bf16[1,128,2048]{1,2,0:T(8,128)(2,1)S(1)} %copy.95) | copy-start | bytes 1572868
  27.8 4.9 %copy-start.33 = (bf16[128,32]{0,1:T(8,128)(2,1)S(1)}, bf16[128,32]{0,1:T(8,128)(2,1)}, u32[]{:S(2)}) copy-start(bf16[128,32]{0,1:T(8,128)(2,1)} %param.12) | copy-start | bytes 24580
  27.8 4.9 %copy-start.34 = (f32[32]{0:T(128)S(1)}, f32[32]{0:T(128)}, u32[]{:S(2)}) copy-start(f32[32]{0:T(128)} %param.13) | copy-start | bytes 388
  27.8 6.5 %copy-start.21 = (f32[32]{0:T(128)S(1)}, f32[32]{0:T(128)}, u32[]{:S(2)}) copy-start(f32[32]{0:T(128)} %param.14) | copy-start | bytes 388
  32.0 8.0 %copy-start.18 = (f32[512,1]{0,1:T(1,128)}, f32[512,1]{0,1:T(1,128)S(1)}, u32[]{:S(2)}) copy-start(f32[512,1]{0,1:T(1,128)S(1)} %fusion.96) | copy-start | bytes 6148
  34.6 4.7 %copy-start.5 = (f32[128,32]{1,0:T(8,128)}, f32[128,32]{1,0:T(8,128)S(1)}, u32[]{:S(2)}) copy-start(f32[128,32]{1,0:T(8,128)S(1)} %reduce_window_sum.46) | copy-start | bytes 49156
  64.5 4.8 %copy-start.24 = (f32[32]{0:T(128)}, f32[32]{0:T(128)S(1)}, u32[]{:S(2)}) copy-start(f32[32]{0:T(128)S(1)} %get-tuple-element.35) | copy-start | bytes 388
  64.5 4.8 %copy-start.26 = (f32[32]{0:T(128)}, f32[32]{0:T(128)S(1)}, u32[]{:S(2)}) copy-start(f32[32]{0:T(128)S(1)} %get-tuple-element.36) | copy-start | bytes 388
  64.5 4.8 %copy-start.29 = (f32[32]{0:T(128)}, f32[32]{0:T(128)S(1)}, u32[]{:S(2)}) copy-start(f32[32]{0:T(128)S(1)} %get-tuple-element.37) | copy-start | bytes 388
  64.5 4.0 %copy-start.1 = (f32[4,128,2048]{1,2,0:T(8,128)S(1)}, f32[4,128,2048]{1,2,0:T(8,128)}, u32[]{:S(2)}) copy-start(f32[4,128,2048]{1,2,0:T(8,128)} %copy.91) | copy-start | bytes 12582916
  64.5 4.1 %copy-start.9 = (f32[4,128,32]{1,2,0:T(8,128)S(1)}, f32[4,128,32]{1,2,0:T(8,128)}, u32[]{:S(2)}) copy-start(f32[4,128,32]{1,2,0:T(8,128)} %copy.93) | copy-start | bytes 196612
  68.5 1.7 %copy-start.13 = (f32[128,128]{0,1:T(8,128)}, f32[128,128]{0,1:T(8,128)S(1)}, u32[]{:S(2)}) copy-start(f32[128,128]{0,1:T(8,128)S(1)} %fusion.82) | copy-start | bytes 196612
  69.3 2.0 %copy-start.4 = (f32[4,32,64,128]{3,2,1,0:T(8,128)}, f32[4,32,64,128]{3,2,1,0:T(8,128)S(1)}, u32[]{:S(2)}) copy-start(f32[4,32,64,128]{3,2,1,0:T(8,128)S(1)} %fusion.4) | copy-start | bytes 12582916
  69.6 1.7 %copy-start.3 = (bf16[1,128,2048]{1,2,0:T(8,128)(2,1)S(1)}, bf16[1,128,2048]{1,2,0:T(8,128)(2,1)}, u32[]{:S(2)}) copy-start(bf16[1,128,2048]{1,2,0:T(8,128)(2,1)} %copy-done.2) | copy-start | bytes 1572868
  69.6 1.7 %copy-start.16 = (f32[32,128]{1,0:T(8,128)S(1)}, f32[32,128]{1,0:T(8,128)}, u32[]{:S(2)}) copy-start(f32[32,128]{1,0:T(8,128)} %copy.87) | copy-start | bytes 49156
  69.6 1.7 %copy-start.17 = (pred[128,128]{0,1:T(8,128)(4,1)S(1)}, pred[128,128]{0,1:T(8,128)(4,1)}, u32[]{:S(2)}) copy-start(pred[128,128]{0,1:T(8,128)(4,1)} %iota_compare_fusion) | copy-start | bytes 49156
  69.6 1.7 %copy-start.35 = (f32[32,128]{1,0:T(8,128)S(1)}, f32[32,128]{1,0:T(8,128)}, u32[]{:S(2)}) copy-start(f32[32,128]{1,0:T(8,128)} %get-tuple-element.38) | copy-start | bytes 49156
  71.3 14.7 %copy-start.11 = (f32[128,32]{0,1:T(8,128)S(1)}, f32[128,32]{0,1:T(8,128)}, u32[]{:S(2)}) copy-start(f32[128,32]{0,1:T(8,128)} %copy-done.10) | copy-start | bytes 49156
  71.3 14.7 %copy-start.27 = (f32[32]{0:T(128)S(1)}, f32[32]{0:T(128)}, u32[]{:S(2)}) copy-start(f32[32]{0:T(128)} %copy-done.26) | copy-start | bytes 388
  71.3 14.7 %copy-start.30 = (f32[32]{0:T(128)S(1)}, f32[32]{0:T(128)}, u32[]{:S(2)}) copy-start(f32[32]{0:T(128)} %copy-done.29) | copy-start | bytes 388
  71.3 14.7 %copy-start.32 = (f32[32]{0:T(128)S(1)}, f32[32]{0:T(128)}, u32[]{:S(2)}) copy-start(f32[32]{0:T(128)} %get-tuple-element.34) | copy-start | bytes 388
  72.7 15.7 %copy-start.8 = (bf16[128,2048]{0,1:T(8,128)(2,1)S(1)}, bf16[128,2048]{0,1:T(8,128)(2,1)}, u32[]{:S(2)}) copy-start(bf16[128,2048]{0,1:T(8,128)(2,1)} %copy.99) | copy-start | bytes 1572868
  72.7 15.7 %copy-start.15 = (f32[128,128]{0,1:T(8,128)S(1)}, f32[128,128]{0,1:T(8,128)}, u32[]{:S(2)}) copy-start(f32[128,128]{0,1:T(8,128)} %fusion.85) | copy-start | bytes 196612
  88.4 2.4 %copy-start.20 = (f32[128]{0:T(128)S(1)}, f32[128]{0:T(128)}, u32[]{:S(2)}) copy-start(f32[128]{0:T(128)} %copy-done.19) | copy-start | bytes 1540
  88.4 2.4 %copy-start.23 = (f32[1,128]{1,0:T(1,128)S(1)}, f32[1,128]{1,0:T(1,128)}, u32[]{:S(2)}) copy-start(f32[1,128]{1,0:T(1,128)} %copy-done.22) | copy-start | bytes 1540
  91.5 2.4 %collective-permute-start = (f32[1152,128]{1,0:T(8,128)S(1)}, f32[1152,128]{1,0:T(8,128)S(1)}, u32[]{:S(2)}, u32[]{:S(2)}) collective-permute-start(f32[1152,128]{1,0:T(8,128)S(1)} %constant_dynamic-slice_fusion.6), channel_id=1, source_target_pairs={{0,1},{1,0},{2,3},{3,2},{4,5},{5,4},{6,7},{7,6},{8,9},{9,8},{10,11... | collective-permute-start | bytes 1769480 | tf_op jit(solution)/shard_map/ppermute | solution.py:26
  94.0 5.1 %collective-permute-start.1 = (f32[288,128]{1,0:T(8,128)S(1)}, f32[288,128]{1,0:T(8,128)S(1)}, u32[]{:S(2)}, u32[]{:S(2)}) collective-permute-start(f32[288,128]{1,0:T(8,128)S(1)} %get-tuple-element.20), channel_id=1, source_target_pairs={{0,8},{8,0},{16,24},{24,16},{1,9},{9,1},{17,25},{25,17},{2,10},{10... | collective-permute-start | bytes 442376 | tf_op jit(solution)/shard_map/ppermute | solution.py:26
  95.2 4.7 %collective-permute-start.2 = (f32[288,128]{1,0:T(8,128)S(1)}, f32[288,128]{1,0:T(8,128)S(1)}, u32[]{:S(2)}, u32[]{:S(2)}) collective-permute-start(f32[288,128]{1,0:T(8,128)S(1)} %get-tuple-element.22), channel_id=1, source_target_pairs={{0,16},{8,24},{16,0},{24,8},{1,17},{9,25},{17,1},{25,9},{2,18},{10... | collective-permute-start | bytes 442376 | tf_op jit(solution)/shard_map/ppermute | solution.py:26
  95.5 7.7 %collective-permute-start.3 = (f32[288,128]{1,0:T(8,128)S(1)}, f32[288,128]{1,0:T(8,128)S(1)}, u32[]{:S(2)}, u32[]{:S(2)}) collective-permute-start(f32[288,128]{1,0:T(8,128)S(1)} %get-tuple-element.21), channel_id=1, source_target_pairs={{0,24},{8,16},{16,8},{24,0},{1,25},{9,17},{17,9},{25,1},{2,26},{10... | collective-permute-start | bytes 442376 | tf_op jit(solution)/shard_map/ppermute | solution.py:26
  103.3 3.6 %collective-permute-start.4 = (f32[72,128]{1,0:T(8,128)S(1)}, f32[72,128]{1,0:T(8,128)S(1)}, u32[]{:S(2)}, u32[]{:S(2)}) collective-permute-start(f32[72,128]{1,0:T(8,128)S(1)} %get-tuple-element.29), channel_id=1, source_target_pairs={{0,2},{1,3},{2,0},{3,1},{4,6},{5,7},{6,4},{7,5},{8,10},{9,11},{10,... | collective-permute-start | bytes 110600 | tf_op jit(solution)/shard_map/ppermute | solution.py:26
  104.6 4.1 %collective-permute-start.5 = (f32[72,128]{1,0:T(8,128)S(1)}, f32[72,128]{1,0:T(8,128)S(1)}, u32[]{:S(2)}, u32[]{:S(2)}) collective-permute-start(f32[72,128]{1,0:T(8,128)S(1)} %get-tuple-element.31), channel_id=1, source_target_pairs={{0,4},{1,5},{2,6},{3,7},{4,0},{5,1},{6,2},{7,3},{8,12},{9,13},{10,... | collective-permute-start | bytes 110600 | tf_op jit(solution)/shard_map/ppermute | solution.py:26
  106.7 4.6 %collective-permute-start.6 = (f32[72,128]{1,0:T(8,128)S(1)}, f32[72,128]{1,0:T(8,128)S(1)}, u32[]{:S(2)}, u32[]{:S(2)}) collective-permute-start(f32[72,128]{1,0:T(8,128)S(1)} %get-tuple-element.30), channel_id=1, source_target_pairs={{0,6},{1,7},{2,4},{3,5},{4,2},{5,3},{6,0},{7,1},{8,14},{9,15},{10,... | collective-permute-start | bytes 110600 | tf_op jit(solution)/shard_map/ppermute | solution.py:26
  111.3 3.6 %collective-permute-start.7 = (f32[72,128]{1,0:T(8,128)S(1)}, f32[72,128]{1,0:T(8,128)S(1)}, u32[]{:S(2)}, u32[]{:S(2)}) collective-permute-start(f32[72,128]{1,0:T(8,128)S(1)} %add_add_fusion.1), channel_id=1, source_target_pairs={{0,2},{1,3},{2,0},{3,1},{4,6},{5,7},{6,4},{7,5},{8,10},{9,11},{10,... | collective-permute-start | bytes 110600 | tf_op jit(solution)/shard_map/ppermute | solution.py:26
  111.4 3.8 %collective-permute-start.8 = (f32[72,128]{1,0:T(8,128)S(1)}, f32[72,128]{1,0:T(8,128)S(1)}, u32[]{:S(2)}, u32[]{:S(2)}) collective-permute-start(f32[72,128]{1,0:T(8,128)S(1)} %add_add_fusion.1), channel_id=1, source_target_pairs={{0,4},{1,5},{2,6},{3,7},{4,0},{5,1},{6,2},{7,3},{8,12},{9,13},{10,... | collective-permute-start | bytes 110600 | tf_op jit(solution)/shard_map/ppermute | solution.py:26
  112.2 4.8 %collective-permute-start.9 = (f32[72,128]{1,0:T(8,128)S(1)}, f32[72,128]{1,0:T(8,128)S(1)}, u32[]{:S(2)}, u32[]{:S(2)}) collective-permute-start(f32[72,128]{1,0:T(8,128)S(1)} %add_add_fusion.1), channel_id=1, source_target_pairs={{0,6},{1,7},{2,4},{3,5},{4,2},{5,3},{6,0},{7,1},{8,14},{9,15},{10,... | collective-permute-start | bytes 110600 | tf_op jit(solution)/shard_map/ppermute | solution.py:26
  117.1 12.7 %copy-start.6 = (bf16[128,2048]{0,1:T(8,128)(2,1)S(1)}, bf16[128,2048]{0,1:T(8,128)(2,1)}, u32[]{:S(2)}) copy-start(bf16[128,2048]{0,1:T(8,128)(2,1)} %copy.84) | copy-start | bytes 1572868
  117.1 12.7 %copy-start.14 = (f32[128,128]{0,1:T(8,128)S(1)}, f32[128,128]{0,1:T(8,128)}, u32[]{:S(2)}) copy-start(f32[128,128]{0,1:T(8,128)} %copy-done.13) | copy-start | bytes 196612
  117.2 4.1 %collective-permute-start.10 = (f32[288,128]{1,0:T(8,128)S(1)}, f32[288,128]{1,0:T(8,128)S(1)}, u32[]{:S(2)}, u32[]{:S(2)}) collective-permute-start(f32[288,128]{1,0:T(8,128)S(1)} %get-tuple-element.24), channel_id=1, source_target_pairs={{0,8},{8,0},{16,24},{24,16},{1,9},{9,1},{17,25},{25,17},{2,10},{10... | collective-permute-start | bytes 442376 | tf_op jit(solution)/shard_map/ppermute | solution.py:26
  117.6 4.0 %collective-permute-start.11 = (f32[288,128]{1,0:T(8,128)S(1)}, f32[288,128]{1,0:T(8,128)S(1)}, u32[]{:S(2)}, u32[]{:S(2)}) collective-permute-start(f32[288,128]{1,0:T(8,128)S(1)} %get-tuple-element.24), channel_id=1, source_target_pairs={{0,16},{8,24},{16,0},{24,8},{1,17},{9,25},{17,1},{25,9},{2,18},{10... | collective-permute-start | bytes 442376 | tf_op jit(solution)/shard_map/ppermute | solution.py:26
  118.7 4.9 %collective-permute-start.12 = (f32[288,128]{1,0:T(8,128)S(1)}, f32[288,128]{1,0:T(8,128)S(1)}, u32[]{:S(2)}, u32[]{:S(2)}) collective-permute-start(f32[288,128]{1,0:T(8,128)S(1)} %get-tuple-element.24), channel_id=1, source_target_pairs={{0,24},{8,16},{16,8},{24,0},{1,25},{9,17},{17,9},{25,1},{2,26},{10... | collective-permute-start | bytes 442376 | tf_op jit(solution)/shard_map/ppermute | solution.py:26
  123.8 11.6 %collective-permute-start.13 = (f32[1152,128]{1,0:T(8,128)S(1)}, f32[1152,128]{1,0:T(8,128)S(1)}, u32[]{:S(2)}, u32[]{:S(2)}) collective-permute-start(f32[1152,128]{1,0:T(8,128)S(1)} %get-tuple-element.14), channel_id=1, source_target_pairs={{0,1},{1,0},{2,3},{3,2},{4,5},{5,4},{6,7},{7,6},{8,9},{9,8},{10,11... | collective-permute-start | bytes 1769480 | tf_op jit(solution)/shard_map/ppermute | solution.py:26
  129.8 2.1 %copy-start.25 = (f32[32]{0:T(128)S(1)}, f32[32]{0:T(128)}, u32[]{:S(2)}) copy-start(f32[32]{0:T(128)} %copy-done.24) | copy-start | bytes 388
  129.8 2.1 %copy-start.28 = (f32[32]{0:T(128)S(1)}, f32[32]{0:T(128)}, u32[]{:S(2)}) copy-start(f32[32]{0:T(128)} %copy-done.26) | copy-start | bytes 388
  129.8 2.1 %copy-start.31 = (f32[32]{0:T(128)S(1)}, f32[32]{0:T(128)}, u32[]{:S(2)}) copy-start(f32[32]{0:T(128)} %copy-done.29) | copy-start | bytes 388
  (4 other events, 3.9 us)
Sparse Core Ops, SparseCore 0:
  36.1 49.8 all-gather.2

commit v6 on v5

--- a/solution.py
+++ b/solution.py
@@ -15,27 +15,23 @@
     return jnp.where(causal[None], jnp.exp(jnp.where(causal[None], log_span, -60.0)), 0.0)
 
 
-def axis_bits(axis):
-    size = lax.axis_size(axis)
-    assert size & (size - 1) == 0
-    return [1 << k for k in range(size.bit_length() - 1)]
+ALL = ("tm", "series")
 
 
-def exchange(value, axis, flip):
-    pairs = [(i, i ^ flip) for i in range(lax.axis_size(axis))]
-    return lax.ppermute(value, axis, pairs)
+def exchange(value, flip):
+    pairs = [(i, i ^ flip) for i in range(lax.axis_size(ALL))]
+    return lax.ppermute(value, ALL, pairs)
 
 
-def bit_groups():
-    tm_bits, series_bits = axis_bits("tm"), axis_bits("series")
-    groups = [("series", series_bits[:1])] if series_bits else []
-    for axis, bits in (("tm", tm_bits), ("series", series_bits[1:])):
-        groups += [(axis, bits[i : i + 2]) for i in range(0, len(bits), 2)]
-    return groups
+def bit_groups(widest):
+    size = lax.axis_size(ALL)
+    assert size & (size - 1) == 0
+    bits = [1 << k for k in range(size.bit_length() - 1)]
+    return [bits[:1]] + [bits[i : i + widest] for i in range(1, len(bits), widest)]
 
 
-def group_round(value, axis, bits, scatter):
-    index = lax.axis_index(axis)
+def group_round(value, bits, scatter):
+    index = lax.axis_index(ALL)
     coord = sum(((index // b) % 2) * (1 << j) for j, b in enumerate(bits))
     size = 1 << len(bits)
 
@@ -47,30 +43,30 @@
         part = rows // size
         keep = lax.dynamic_slice_in_dim(value, coord * part, part)
         got = [
-            exchange(lax.dynamic_slice_in_dim(value, (coord ^ m) * part, part), axis, flip_of(m))
+            exchange(lax.dynamic_slice_in_dim(value, (coord ^ m) * part, part), flip_of(m))
             for m in range(1, size)
         ]
         for piece in got:
             keep = keep + piece
         return keep
-    got = [value] + [exchange(value, axis, flip_of(m)) for m in range(1, size)]
+    got = [value] + [exchange(value, flip_of(m)) for m in range(1, size)]
     stacked = jnp.stack(got)
     return [lax.dynamic_index_in_dim(stacked, coord ^ q, 0, keepdims=False) for q in range(size)]
 
 
-def tree_psum(value):
+def tree_psum(value, widest):
     done = []
-    for axis, bits in bit_groups():
+    for bits in bit_groups(widest):
         if value.shape[0] % (8 << len(bits)) == 0:
-            value = group_round(value, axis, bits, True)
-            done.append((axis, bits))
+            value = group_round(value, bits, True)
+            done.append(bits)
         else:
-            pieces = group_round(value, axis, bits, False)
+            pieces = group_round(value, bits, False)
             value = pieces[0]
             for piece in pieces[1:]:
                 value = value + piece
-    for axis, bits in reversed(done):
-        value = jnp.concatenate(group_round(value, axis, bits, False))
+    for bits in reversed(done):
+        value = jnp.concatenate(group_round(value, bits, False))
     return value
 
 
@@ -181,7 +177,7 @@
         axis=1,
     )
     local_grad = jnp.einsum("tw,tf->wf", grad_rows, features, preferred_element_type=fl)
-    total_grad = tree_psum(local_grad).T
+    total_grad = tree_psum(local_grad, 4).T
     grad_in = total_grad / math.sqrt(series_count * seq_len)
     return (ssd_output, grad_in)
 

time: 145 us -> 171 us (1.18)
  starting transfers between devices: 26.6 us -> 61.5 us
  waiting for transfers between devices: 35.5 us -> 26.1 us
    ppermute x14 -> x32, starting transfers between devices: 19.4 us -> 54.3 us  [exchange(): return lax.ppermute(value, ALL, pairs)]
    ppermute x14 -> x32, waiting for transfers between devices: 18.4 us -> 9.05 us  [exchange(): return lax.ppermute(value, ALL, pairs)]
    unnamed x75 -> x103, local copies, waits for them, and re-layouts: 6.43 us -> 5.25 us
  transfers between devices with their start and end apart: 16 -> 34, of which waited for: 13 -> 9; matrix products, arithmetic and copies ran while one was open for 30% -> 25% of each run, Pallas kernels for 0% -> 0%
where the time goes in v6:
time: 171 us; the launch traced here: 170 us
  starting transfers between devices  61.5 us (36%)
  matrix products  26.8 us (16%)
  waiting for transfers between devices  26.1 us (15%)
  local copies, waits for them, and re-layouts  24.5 us (14%)
  other arithmetic  16 us (9%)
  between operations  15 us (9%)
    ppermute x32, starting transfers between devices, exchange(): return lax.ppermute(value, ALL, pairs)  54.3 us
    all_gather x1, waiting for transfers between devices, on_device(): adjoint_all = lax.all_gather(adjoint_local, 'tm')  13.4 us
    ppermute x32, waiting for transfers between devices, exchange(): return lax.ppermute(value, ALL, pairs)  9.05 us
    all_to_all x1, starting transfers between devices, on_device(): lax.all_to_all(outgoing, ('tm', 'series'), split_axis=0, concat_axis=1, t...  7.1 us
    convert_element_type x1, local copies, waits for them, and re-layouts, on_device(): xw_all = (x_all * tail_all[..., None]).astype(half)  5.36 us
    unnamed x103, local copies, waits for them, and re-layouts  5.25 us
    dot_general x1, matrix products, on_device(): picked = jnp.dot(onehot, bin_table, precision=lax.Precision.HIGHEST)  4.14 us
    all_to_all x1, waiting for transfers between devices, on_device(): lax.all_to_all(outgoing, ('tm', 'series'), split_axis=0, concat_axis=1, t...  3.71 us
  transfers between devices with their start and end apart: 34, of which 9 were waited for; matrix products, arithmetic and copies ran while one was open for 25% of the time, Pallas kernels for 0%

profile of v6, /device:TPU:1, one launch (start us, length us, event | category | flops | bytes accessed | tf_op | source)
XLA Modules:
  0.0 169.9 jit_solution(11964889406018404709)
XLA Ops:
  8.6 1.2 gather_fusion
  10.5 7.1 %all-to-all-start = ((f32[32,1,16]{2,1,0:T(1,128)}), f32[32,1,16]{2,1,0:T(1,128)S(1)}, u32[]{:S(2)}, u32[]{:S(2)}) async-start(f32[32,1,16]{2,1,0:T(1,128)} %bitcast), calls=%async_computation | async-start | bytes 32768 | tf_op jit(solution)/shard_map/all_to_all | solution.py:88
  19.3 1.3 copy.81
  20.6 3.7 %all-to-all-done = f32[32,1,16]{2,1,0:T(1,128)S(1)} async-done(((f32[32,1,16]{2,1,0:T(1,128)}), f32[32,1,16]{2,1,0:T(1,128)S(1)}, u32[]{:S(2)}, u32[]{:S(2)}) %all-to-all-start) | async-done | bytes 2080 | tf_op jit(solution)/shard_map/all_to_all | solution.py:88
  25.6 1.5 convert_reduce_fusion
  27.8 4.1 %fusion = f32[512,4]{0,1:T(4,128)S(1)} fusion(f32[4096]{0:T(1024)S(1)} %get-tuple-element.30, f32[4096]{0:T(1024)S(1)} %convert_element_type.106, f32[512]{0:T(512)S(1)} %le.22, f32[4096,1]{0,1:T(1,128)S(1)} %bitcast.255, f32[4096,1]{0,1:T(1,128)S(1)} %bitcast.250, f32[4096,1]{0,1:T(1,128)S(1)} %bitcast.249, f32[4096,1]{0,1:T(1,128)S(1)} %sub.71), kind=kOutput, calls=%fused_computation.3 | convolution fusion | flops 107003904 | bytes 108544 | tf_op jit(solution)/shard_map/dot_general | solution.py:97
  32.6 1.0 compare_select_fusion.1
  34.7 1.3 fusion.33
  40.0 1.1 compare_select_fusion
  42.9 2.3 %convolution_convert_fusion = bf16[512,2304]{1,0:T(8,128)(2,1)S(1)} fusion(bf16[128,2304]{1,0:T(8,128)(2,1)S(1)} %copy-done, f32[128]{0:T(128)} %copy-done.19, f32[512]{0:T(512)} %bitcast.258), kind=kOutput, calls=%fused_computation.4 | convolution fusion | flops 303300608 | bytes 2951680 | tf_op jit(solution)/shard_map/dot_general | solution.py:118
  45.2 2.6 %slice_convert_fusion = f32[4,128,2048]{2,1,0:T(8,128)} fusion(bf16[4,128,2304]{2,1,0:T(8,128)(2,1)S(1)} %bitcast.228), kind=kLoop, calls=%fused_computation.11 | loop fusion | flops 1048576 | bytes 6291456 | tf_op jit(solution)/shard_map/convert_element_type | solution.py:128
  47.8 5.4 %copy.77 = f32[4,128,2048]{1,2,0:T(8,128)} copy(f32[4,128,2048]{2,1,0:T(8,128)} %slice_convert_fusion) | data formatting | bytes 8388608 | tf_op jit(solution)/shard_map/convert_element_type | solution.py:128
  55.3 1.0 mul.317
  56.3 2.5 %copy.84 = f32[128,2048]{1,0:T(8,128)} copy(f32[128,2048]{0,1:T(8,128)} %bitcast.233) | data formatting | bytes 2097152 | tf_op jit(solution)/shard_map/mul | solution.py:160
  58.8 2.1 %multiply_convert_fusion.3 = bf16[128,2048]{1,0:T(8,128)(2,1)} fusion(f32[128,2048]{1,0:T(8,128)} %copy.84, bf16[128,2304]{1,0:T(8,128)(2,1)S(1)} %convolution_convert_fusion.1), kind=kLoop, calls=%fused_computation.56 | loop fusion | flops 786432 | bytes 2097152 | tf_op jit(solution)/shard_map/convert_element_type | solution.py:116
  60.9 2.2 %copy.85 = bf16[128,2048]{0,1:T(8,128)(2,1)} copy(bf16[128,2048]{1,0:T(8,128)(2,1)} %multiply_convert_fusion.3) | data formatting | bytes 1048576 | tf_op jit(solution)/shard_map/convert_element_type | solution.py:116
  63.1 1.3 multiply_bitcast_fusion
  64.5 2.8 %fusion.5 = bf16[128,128]{0,1:T(8,128)(2,1)S(1)} fusion(bf16[128,32,64]{0,2,1:T(8,128)(2,1)} %bitcast.242, bf16[128,32,64]{0,2,1:T(8,128)(2,1)} %bitcast.231, f32[32,128]{1,0:T(8,128)} %get-tuple-element.35, f32[32,128]{1,0:T(8,128)} %copy.73, pred[128,128]{0,1:T(8,128)(4,1)} %iota_compare_fusion), kind=kOutput, calls=%fused_computation.13 | convolution fusion | flops 70238208 | bytes 1130496 | tf_op jit(solution)/shard_map/thp,shp->hts/dot_general | solution.py:163
  70.3 1.0 copy-done.4
  71.3 1.3 convolution_bitcast_fusion
  72.7 13.4 %all-gather.3.cloned.1.call-done = f32[128,64,128]{2,1,0:T(8,128)} async-done(((f32[32,64,128]{2,1,0:T(8,128)}), f32[128,64,128]{2,1,0:T(8,128)}) %all-gather.3.cloned.1.call-update) | async-done | bytes 4194320 | tf_op jit(solution)/shard_map/all_gather | solution.py:139
  86.1 2.4 %fusion.10 = bf16[128,32,64]{0,2,1:T(8,128)(2,1)S(1)} fusion(f32[128,32,64]{0,2,1:T(8,128)S(1)} %convolution_bitcast_fusion, f32[128,64,128]{2,1,0:T(8,128)} %all-gather.3.cloned.1.call-done, f32[128,32]{0,1:T(8,128)S(1)} %copy-done.11, f32[32]{0:T(128)S(1)} %copy-done.32, f32[32]{0:T(128)S(1)} %copy-done.27, f32[32]{0:T(128)S(1)} %copy-done.30, ...), kind=kOutput, calls=%fused_computation.28 | convolution fusion | flops 70254592 | bytes 4769283 | tf_op jit(solution)/shard_map/sn,hpn->shp/dot_general | solution.py:160
  88.5 2.4 %fusion.14 = bf16[128,128]{0,1:T(8,128)(2,1)S(1)} fusion(f32[128,128]{0,1:T(8,128)S(1)} %copy-done.15, bf16[128,32,64]{0,2,1:T(8,128)(2,1)S(1)} %bitcast.245, f32[128,64,128]{2,1,0:T(8,128)} %all-gather.3.cloned.1.call-done, f32[32]{0:T(128)S(1)} %copy-done.32, f32[32]{0:T(128)S(1)} %copy-done.30, f32[32]{0:T(128)S(1)} %copy-done.27, pred[]{:T(512)S(6)} %lt.163, ...), kind=kOutput, calls=%fused_computation.36 | convolution fusion | flops 69500928 | bytes 3768707 | tf_op jit(solution)/shard_map/shp,hpn->sn/dot_general | solution.py:166
  92.3 1.6 collective-permute-done
  94.1 1.3 collective-permute-start.1
  95.4 3.0 %collective-permute-start.10 = (f32[72,128]{1,0:T(8,128)S(1)}, f32[72,128]{1,0:T(8,128)S(1)}, u32[]{:S(2)}, u32[]{:S(2)}) collective-permute-start(f32[72,128]{1,0:T(8,128)S(1)} %get-tuple-element.20), channel_id=1, source_target_pairs={{0,20},{1,21},{2,22},{3,23},{4,16},{5,17},{6,18},{7,19},{8,28},{9,... | collective-permute-start | bytes 110600 | tf_op jit(solution)/shard_map/ppermute | solution.py:23
  98.6 1.2 collective-permute-start.12
  99.8 1.2 collective-permute-start.13
  101.0 3.9 %collective-permute-start.14 = (f32[72,128]{1,0:T(8,128)S(1)}, f32[72,128]{1,0:T(8,128)S(1)}, u32[]{:S(2)}, u32[]{:S(2)}) collective-permute-start(f32[72,128]{1,0:T(8,128)S(1)} %get-tuple-element.16), channel_id=1, source_target_pairs={{0,28},{1,29},{2,30},{3,31},{4,24},{5,25},{6,26},{7,27},{8,20},{9,... | collective-permute-start | bytes 110600 | tf_op jit(solution)/shard_map/ppermute | solution.py:23
  104.9 1.1 collective-permute-start.15
  106.4 2.8 %collective-permute-start.3 = (f32[72,128]{1,0:T(8,128)S(1)}, f32[72,128]{1,0:T(8,128)S(1)}, u32[]{:S(2)}, u32[]{:S(2)}) collective-permute-start(f32[72,128]{1,0:T(8,128)S(1)} %get-tuple-element.27), channel_id=1, source_target_pairs={{0,6},{1,7},{2,4},{3,5},{4,2},{5,3},{6,0},{7,1},{8,14},{9,15},{10,... | collective-permute-start | bytes 110600 | tf_op jit(solution)/shard_map/ppermute | solution.py:23
  109.2 1.2 collective-permute-start.4
  112.0 2.8 %collective-permute-start.7 = (f32[72,128]{1,0:T(8,128)S(1)}, f32[72,128]{1,0:T(8,128)S(1)}, u32[]{:S(2)}, u32[]{:S(2)}) collective-permute-start(f32[72,128]{1,0:T(8,128)S(1)} %get-tuple-element.23), channel_id=1, source_target_pairs={{0,14},{1,15},{2,12},{3,13},{4,10},{5,11},{6,8},{7,9},{8,6},{9,7},... | collective-permute-start | bytes 110600 | tf_op jit(solution)/shard_map/ppermute | solution.py:23
  114.8 1.2 collective-permute-start.8
  117.9 2.3 %collective-permute-done.9 = f32[72,128]{1,0:T(8,128)S(1)} collective-permute-done((f32[72,128]{1,0:T(8,128)S(1)}, f32[72,128]{1,0:T(8,128)S(1)}, u32[]{:S(2)}, u32[]{:S(2)}) %collective-permute-start.9) | collective-permute-done | bytes 36896 | tf_op jit(solution)/shard_map/ppermute | solution.py:23
  121.0 3.0 %collective-permute-start.18 = (f32[72,128]{1,0:T(8,128)S(1)}, f32[72,128]{1,0:T(8,128)S(1)}, u32[]{:S(2)}, u32[]{:S(2)}) collective-permute-start(f32[72,128]{1,0:T(8,128)S(1)} %get-tuple-element.11), channel_id=1, source_target_pairs={{0,6},{1,7},{2,4},{3,5},{4,2},{5,3},{6,0},{7,1},{8,14},{9,15},{10,... | collective-permute-start | bytes 110600 | tf_op jit(solution)/shard_map/ppermute | solution.py:23
  124.4 1.6 collective-permute-start.21
  126.0 3.5 %collective-permute-start.22 = (f32[72,128]{1,0:T(8,128)S(1)}, f32[72,128]{1,0:T(8,128)S(1)}, u32[]{:S(2)}, u32[]{:S(2)}) collective-permute-start(f32[72,128]{1,0:T(8,128)S(1)} %get-tuple-element.11), channel_id=1, source_target_pairs={{0,14},{1,15},{2,12},{3,13},{4,10},{5,11},{6,8},{7,9},{8,6},{9,7},... | collective-permute-start | bytes 110600 | tf_op jit(solution)/shard_map/ppermute | solution.py:23
  129.7 2.0 %collective-permute-start.25 = (f32[72,128]{1,0:T(8,128)S(1)}, f32[72,128]{1,0:T(8,128)S(1)}, u32[]{:S(2)}, u32[]{:S(2)}) collective-permute-start(f32[72,128]{1,0:T(8,128)S(1)} %get-tuple-element.11), channel_id=1, source_target_pairs={{0,20},{1,21},{2,22},{3,23},{4,16},{5,17},{6,18},{7,19},{8,28},{9,... | collective-permute-start | bytes 110600 | tf_op jit(solution)/shard_map/ppermute | solution.py:23
  131.7 3.5 %collective-permute-start.26 = (f32[72,128]{1,0:T(8,128)S(1)}, f32[72,128]{1,0:T(8,128)S(1)}, u32[]{:S(2)}, u32[]{:S(2)}) collective-permute-start(f32[72,128]{1,0:T(8,128)S(1)} %get-tuple-element.11), channel_id=1, source_target_pairs={{0,22},{1,23},{2,20},{3,21},{4,18},{5,19},{6,16},{7,17},{8,30},{9,... | collective-permute-start | bytes 110600 | tf_op jit(solution)/shard_map/ppermute | solution.py:23
  135.2 1.2 collective-permute-start.27
  136.5 2.3 %collective-permute-start.29 = (f32[72,128]{1,0:T(8,128)S(1)}, f32[72,128]{1,0:T(8,128)S(1)}, u32[]{:S(2)}, u32[]{:S(2)}) collective-permute-start(f32[72,128]{1,0:T(8,128)S(1)} %get-tuple-element.11), channel_id=1, source_target_pairs={{0,28},{1,29},{2,30},{3,31},{4,24},{5,25},{6,26},{7,27},{8,20},{9,... | collective-permute-start | bytes 110600 | tf_op jit(solution)/shard_map/ppermute | solution.py:23
  138.8 3.8 %collective-permute-start.30 = (f32[72,128]{1,0:T(8,128)S(1)}, f32[72,128]{1,0:T(8,128)S(1)}, u32[]{:S(2)}, u32[]{:S(2)}) collective-permute-start(f32[72,128]{1,0:T(8,128)S(1)} %get-tuple-element.11), channel_id=1, source_target_pairs={{0,30},{1,31},{2,28},{3,29},{4,26},{5,27},{6,24},{7,25},{8,22},{9,... | collective-permute-start | bytes 110600 | tf_op jit(solution)/shard_map/ppermute | solution.py:23
  142.8 2.5 %collective-permute-done.30 = f32[72,128]{1,0:T(8,128)S(1)} collective-permute-done((f32[72,128]{1,0:T(8,128)S(1)}, f32[72,128]{1,0:T(8,128)S(1)}, u32[]{:S(2)}, u32[]{:S(2)}) %collective-permute-start.30) | collective-permute-done | bytes 36896 | tf_op jit(solution)/shard_map/ppermute | solution.py:23
  145.6 10.2 %collective-permute-start.31 = (f32[1152,128]{1,0:T(8,128)S(1)}, f32[1152,128]{1,0:T(8,128)S(1)}, u32[]{:S(2)}, u32[]{:S(2)}) collective-permute-start(f32[1152,128]{1,0:T(8,128)S(1)} %constant_dynamic-update-slice_fusion.16), channel_id=1, source_target_pairs={{0,1},{1,0},{2,3},{3,2},{4,5},{5,4},{6,7},{7,6},{8,9},{9,8},{10,11... | collective-permute-start | bytes 1769480 | tf_op jit(solution)/shard_map/ppermute | solution.py:23
  155.8 2.1 %convolution_bitcast_fusion.1 = f32[128,32,64]{0,2,1:T(8,128)S(1)} fusion(bf16[128,32,64]{0,2,1:T(8,128)(2,1)S(1)} %bitcast.243, f32[32,128]{1,0:T(8,128)} %get-tuple-element.35, f32[32,128]{1,0:T(8,128)} %copy.73, f32[128,128]{0,1:T(8,128)S(1)} %copy-done.14, pred[128,128]{0,1:T(8,128)(4,1)} %iota_compare_fusion), kind=kOutput, calls=%fused_computation.26 | convolution fusion | flops 70254592 | bytes 1687552 | tf_op jit(solution)/shard_map/hts,shp->thp/dot_general | solution.py:150
  157.9 2.4 %fusion.9 = bf16[128,32,64]{0,2,1:T(8,128)(2,1)S(1)} fusion(f32[128,32,64]{0,2,1:T(8,128)S(1)} %convolution_bitcast_fusion.1, f32[4,32,64,128]{3,2,1,0:T(8,128)} %copy-done.4, f32[128,32]{0,1:T(8,128)S(1)} %copy.80, f32[32]{0:T(128)S(1)} %copy-done.25, f32[32]{0:T(128)S(1)} %copy-done.28, f32[32]{0:T(128)S(1)} %copy-done.31, pred[]{:T(512)S(6)} %gt.24, ...), kind=kOutput, calls=%fused_computation.27 | convolution fusion | flops 70254592 | bytes 4769283 | tf_op jit(solution)/shard_map/tn,hpn->thp/dot_general | solution.py:153
  162.0 1.1 fusion.11
  (202 shorter events, 26.9 us)
Async XLA Ops:
  7.2 24.9 %copy-start = (bf16[128,2304]{1,0:T(8,128)(2,1)S(1)}, bf16[128,2304]{1,0:T(8,128)(2,1)}, u32[]{:S(2)}) copy-start(bf16[128,2304]{1,0:T(8,128)(2,1)} %param.11) | copy-start | bytes 1769476
  10.5 13.8 %all-to-all-start = ((f32[32,1,16]{2,1,0:T(1,128)}), f32[32,1,16]{2,1,0:T(1,128)S(1)}, u32[]{:S(2)}, u32[]{:S(2)}) async-start(f32[32,1,16]{2,1,0:T(1,128)} %bitcast), calls=%async_computation | async-start | bytes 32768 | tf_op jit(solution)/shard_map/all_to_all | solution.py:88
  17.6 68.4 %all-gather.3.cloned.1.call-start = ((), (), s32[]{:S(2)}) async-start(), calls=%async_computation.1 | async-start | bytes 5242880 | tf_op jit(solution)/shard_map/all_gather | solution.py:139
  19.3 20.7 %copy-start.19 = (f32[128]{0:T(128)}, f32[128]{0:T(128)S(1)}, u32[]{:S(2)}) copy-start(f32[128]{0:T(128)S(1)} %add_multiply_fusion) | copy-start | bytes 1540
  20.6 16.1 %copy-start.2 = (bf16[1,128,2048]{1,2,0:T(8,128)(2,1)}, bf16[1,128,2048]{1,2,0:T(8,128)(2,1)S(1)}, u32[]{:S(2)}) copy-start(bf16[1,128,2048]{1,2,0:T(8,128)(2,1)S(1)} %copy.81) | copy-start | bytes 1572868
  27.8 4.9 %copy-start.33 = (bf16[128,32]{0,1:T(8,128)(2,1)S(1)}, bf16[128,32]{0,1:T(8,128)(2,1)}, u32[]{:S(2)}) copy-start(bf16[128,32]{0,1:T(8,128)(2,1)} %param.12) | copy-start | bytes 24580
  27.8 6.5 %copy-start.21 = (f32[32]{0:T(128)S(1)}, f32[32]{0:T(128)}, u32[]{:S(2)}) copy-start(f32[32]{0:T(128)} %param.14) | copy-start | bytes 388
  32.0 8.0 %copy-start.18 = (f32[512,1]{0,1:T(1,128)}, f32[512,1]{0,1:T(1,128)S(1)}, u32[]{:S(2)}) copy-start(f32[512,1]{0,1:T(1,128)S(1)} %fusion.94) | copy-start | bytes 6148
  71.3 14.7 %copy-start.11 = (f32[128,32]{0,1:T(8,128)S(1)}, f32[128,32]{0,1:T(8,128)}, u32[]{:S(2)}) copy-start(f32[128,32]{0,1:T(8,128)} %copy-done.10) | copy-start | bytes 49156
  71.3 14.7 %copy-start.27 = (f32[32]{0:T(128)S(1)}, f32[32]{0:T(128)}, u32[]{:S(2)}) copy-start(f32[32]{0:T(128)} %copy-done.26) | copy-start | bytes 388
  71.3 14.7 %copy-start.30 = (f32[32]{0:T(128)S(1)}, f32[32]{0:T(128)}, u32[]{:S(2)}) copy-start(f32[32]{0:T(128)} %copy-done.29) | copy-start | bytes 388
  71.3 14.7 %copy-start.32 = (f32[32]{0:T(128)S(1)}, f32[32]{0:T(128)}, u32[]{:S(2)}) copy-start(f32[32]{0:T(128)} %get-tuple-element.31) | copy-start | bytes 388
  72.6 15.8 %copy-start.8 = (bf16[128,2048]{0,1:T(8,128)(2,1)S(1)}, bf16[128,2048]{0,1:T(8,128)(2,1)}, u32[]{:S(2)}) copy-start(bf16[128,2048]{0,1:T(8,128)(2,1)} %copy.85) | copy-start | bytes 1572868
  72.7 15.8 %copy-start.15 = (f32[128,128]{0,1:T(8,128)S(1)}, f32[128,128]{0,1:T(8,128)}, u32[]{:S(2)}) copy-start(f32[128,128]{0,1:T(8,128)} %fusion.83) | copy-start | bytes 196612
  91.5 2.4 %collective-permute-start = (f32[1152,128]{1,0:T(8,128)S(1)}, f32[1152,128]{1,0:T(8,128)S(1)}, u32[]{:S(2)}, u32[]{:S(2)}) collective-permute-start(f32[1152,128]{1,0:T(8,128)S(1)} %constant_dynamic-slice_fusion.15), channel_id=1, source_target_pairs={{0,1},{1,0},{2,3},{3,2},{4,5},{5,4},{6,7},{7,6},{8,9},{9,8},{10,11... | collective-permute-start | bytes 1769480 | tf_op jit(solution)/shard_map/ppermute | solution.py:23
  94.0 61.8 %copy-start.6 = (bf16[128,2048]{0,1:T(8,128)(2,1)S(1)}, bf16[128,2048]{0,1:T(8,128)(2,1)}, u32[]{:S(2)}) copy-start(bf16[128,2048]{0,1:T(8,128)(2,1)} %copy.70) | copy-start | bytes 1572868
  94.0 61.8 %copy-start.14 = (f32[128,128]{0,1:T(8,128)S(1)}, f32[128,128]{0,1:T(8,128)}, u32[]{:S(2)}) copy-start(f32[128,128]{0,1:T(8,128)} %copy-done.13) | copy-start | bytes 196612
  94.1 6.9 %collective-permute-start.1 = (f32[72,128]{1,0:T(8,128)S(1)}, f32[72,128]{1,0:T(8,128)S(1)}, u32[]{:S(2)}, u32[]{:S(2)}) collective-permute-start(f32[72,128]{1,0:T(8,128)S(1)} %get-tuple-element.14), channel_id=1, source_target_pairs={{0,2},{1,3},{2,0},{3,1},{4,6},{5,7},{6,4},{7,5},{8,10},{9,11},{10,... | collective-permute-start | bytes 110600 | tf_op jit(solution)/shard_map/ppermute | solution.py:23
  95.4 9.6 %collective-permute-start.10 = (f32[72,128]{1,0:T(8,128)S(1)}, f32[72,128]{1,0:T(8,128)S(1)}, u32[]{:S(2)}, u32[]{:S(2)}) collective-permute-start(f32[72,128]{1,0:T(8,128)S(1)} %get-tuple-element.20), channel_id=1, source_target_pairs={{0,20},{1,21},{2,22},{3,23},{4,16},{5,17},{6,18},{7,19},{8,28},{9,... | collective-permute-start | bytes 110600 | tf_op jit(solution)/shard_map/ppermute | solution.py:23
  98.4 7.6 %collective-permute-start.11 = (f32[72,128]{1,0:T(8,128)S(1)}, f32[72,128]{1,0:T(8,128)S(1)}, u32[]{:S(2)}, u32[]{:S(2)}) collective-permute-start(f32[72,128]{1,0:T(8,128)S(1)} %get-tuple-element.19), channel_id=1, source_target_pairs={{0,22},{1,23},{2,20},{3,21},{4,18},{5,19},{6,16},{7,17},{8,30},{9,... | collective-permute-start | bytes 110600 | tf_op jit(solution)/shard_map/ppermute | solution.py:23
  98.6 7.8 %collective-permute-start.12 = (f32[72,128]{1,0:T(8,128)S(1)}, f32[72,128]{1,0:T(8,128)S(1)}, u32[]{:S(2)}, u32[]{:S(2)}) collective-permute-start(f32[72,128]{1,0:T(8,128)S(1)} %get-tuple-element.18), channel_id=1, source_target_pairs={{0,24},{1,25},{2,26},{3,27},{4,28},{5,29},{6,30},{7,31},{8,16},{9,... | collective-permute-start | bytes 110600 | tf_op jit(solution)/shard_map/ppermute | solution.py:23
  99.8 9.4 %collective-permute-start.13 = (f32[72,128]{1,0:T(8,128)S(1)}, f32[72,128]{1,0:T(8,128)S(1)}, u32[]{:S(2)}, u32[]{:S(2)}) collective-permute-start(f32[72,128]{1,0:T(8,128)S(1)} %get-tuple-element.17), channel_id=1, source_target_pairs={{0,26},{1,27},{2,24},{3,25},{4,30},{5,31},{6,28},{7,29},{8,18},{9,... | collective-permute-start | bytes 110600 | tf_op jit(solution)/shard_map/ppermute | solution.py:23
  101.0 9.4 %collective-permute-start.14 = (f32[72,128]{1,0:T(8,128)S(1)}, f32[72,128]{1,0:T(8,128)S(1)}, u32[]{:S(2)}, u32[]{:S(2)}) collective-permute-start(f32[72,128]{1,0:T(8,128)S(1)} %get-tuple-element.16), channel_id=1, source_target_pairs={{0,28},{1,29},{2,30},{3,31},{4,24},{5,25},{6,26},{7,27},{8,20},{9,... | collective-permute-start | bytes 110600 | tf_op jit(solution)/shard_map/ppermute | solution.py:23
  104.9 6.5 %collective-permute-start.15 = (f32[72,128]{1,0:T(8,128)S(1)}, f32[72,128]{1,0:T(8,128)S(1)}, u32[]{:S(2)}, u32[]{:S(2)}) collective-permute-start(f32[72,128]{1,0:T(8,128)S(1)} %get-tuple-element.15), channel_id=1, source_target_pairs={{0,30},{1,31},{2,28},{3,29},{4,26},{5,27},{6,24},{7,25},{8,22},{9,... | collective-permute-start | bytes 110600 | tf_op jit(solution)/shard_map/ppermute | solution.py:23
  106.0 6.0 %collective-permute-start.2 = (f32[72,128]{1,0:T(8,128)S(1)}, f32[72,128]{1,0:T(8,128)S(1)}, u32[]{:S(2)}, u32[]{:S(2)}) collective-permute-start(f32[72,128]{1,0:T(8,128)S(1)} %get-tuple-element.28), channel_id=1, source_target_pairs={{0,4},{1,5},{2,6},{3,7},{4,0},{5,1},{6,2},{7,3},{8,12},{9,13},{10,... | collective-permute-start | bytes 110600 | tf_op jit(solution)/shard_map/ppermute | solution.py:23
  106.4 8.4 %collective-permute-start.3 = (f32[72,128]{1,0:T(8,128)S(1)}, f32[72,128]{1,0:T(8,128)S(1)}, u32[]{:S(2)}, u32[]{:S(2)}) collective-permute-start(f32[72,128]{1,0:T(8,128)S(1)} %get-tuple-element.27), channel_id=1, source_target_pairs={{0,6},{1,7},{2,4},{3,5},{4,2},{5,3},{6,0},{7,1},{8,14},{9,15},{10,... | collective-permute-start | bytes 110600 | tf_op jit(solution)/shard_map/ppermute | solution.py:23
  109.2 6.8 %collective-permute-start.4 = (f32[72,128]{1,0:T(8,128)S(1)}, f32[72,128]{1,0:T(8,128)S(1)}, u32[]{:S(2)}, u32[]{:S(2)}) collective-permute-start(f32[72,128]{1,0:T(8,128)S(1)} %get-tuple-element.26), channel_id=1, source_target_pairs={{0,8},{1,9},{2,10},{3,11},{4,12},{5,13},{6,14},{7,15},{8,0},{9,1},... | collective-permute-start | bytes 110600 | tf_op jit(solution)/shard_map/ppermute | solution.py:23
  110.4 5.8 %collective-permute-start.5 = (f32[72,128]{1,0:T(8,128)S(1)}, f32[72,128]{1,0:T(8,128)S(1)}, u32[]{:S(2)}, u32[]{:S(2)}) collective-permute-start(f32[72,128]{1,0:T(8,128)S(1)} %get-tuple-element.25), channel_id=1, source_target_pairs={{0,10},{1,11},{2,8},{3,9},{4,14},{5,15},{6,12},{7,13},{8,2},{9,3},... | collective-permute-start | bytes 110600 | tf_op jit(solution)/shard_map/ppermute | solution.py:23
  111.4 5.2 %collective-permute-start.6 = (f32[72,128]{1,0:T(8,128)S(1)}, f32[72,128]{1,0:T(8,128)S(1)}, u32[]{:S(2)}, u32[]{:S(2)}) collective-permute-start(f32[72,128]{1,0:T(8,128)S(1)} %get-tuple-element.24), channel_id=1, source_target_pairs={{0,12},{1,13},{2,14},{3,15},{4,8},{5,9},{6,10},{7,11},{8,4},{9,5},... | collective-permute-start | bytes 110600 | tf_op jit(solution)/shard_map/ppermute | solution.py:23
  112.0 5.6 %collective-permute-start.7 = (f32[72,128]{1,0:T(8,128)S(1)}, f32[72,128]{1,0:T(8,128)S(1)}, u32[]{:S(2)}, u32[]{:S(2)}) collective-permute-start(f32[72,128]{1,0:T(8,128)S(1)} %get-tuple-element.23), channel_id=1, source_target_pairs={{0,14},{1,15},{2,12},{3,13},{4,10},{5,11},{6,8},{7,9},{8,6},{9,7},... | collective-permute-start | bytes 110600 | tf_op jit(solution)/shard_map/ppermute | solution.py:23
  114.8 3.1 %collective-permute-start.8 = (f32[72,128]{1,0:T(8,128)S(1)}, f32[72,128]{1,0:T(8,128)S(1)}, u32[]{:S(2)}, u32[]{:S(2)}) collective-permute-start(f32[72,128]{1,0:T(8,128)S(1)} %get-tuple-element.22), channel_id=1, source_target_pairs={{0,16},{1,17},{2,18},{3,19},{4,20},{5,21},{6,22},{7,23},{8,24},{9,... | collective-permute-start | bytes 110600 | tf_op jit(solution)/shard_map/ppermute | solution.py:23
  116.0 4.3 %collective-permute-start.9 = (f32[72,128]{1,0:T(8,128)S(1)}, f32[72,128]{1,0:T(8,128)S(1)}, u32[]{:S(2)}, u32[]{:S(2)}) collective-permute-start(f32[72,128]{1,0:T(8,128)S(1)} %get-tuple-element.21), channel_id=1, source_target_pairs={{0,18},{1,19},{2,16},{3,17},{4,22},{5,23},{6,20},{7,21},{8,26},{9,... | collective-permute-start | bytes 110600 | tf_op jit(solution)/shard_map/ppermute | solution.py:23
  120.3 4.1 %collective-permute-start.16 = (f32[72,128]{1,0:T(8,128)S(1)}, f32[72,128]{1,0:T(8,128)S(1)}, u32[]{:S(2)}, u32[]{:S(2)}) collective-permute-start(f32[72,128]{1,0:T(8,128)S(1)} %get-tuple-element.11), channel_id=1, source_target_pairs={{0,2},{1,3},{2,0},{3,1},{4,6},{5,7},{6,4},{7,5},{8,10},{9,11},{10,... | collective-permute-start | bytes 110600 | tf_op jit(solution)/shard_map/ppermute | solution.py:23
  120.5 5.5 %collective-permute-start.17 = (f32[72,128]{1,0:T(8,128)S(1)}, f32[72,128]{1,0:T(8,128)S(1)}, u32[]{:S(2)}, u32[]{:S(2)}) collective-permute-start(f32[72,128]{1,0:T(8,128)S(1)} %get-tuple-element.11), channel_id=1, source_target_pairs={{0,4},{1,5},{2,6},{3,7},{4,0},{5,1},{6,2},{7,3},{8,12},{9,13},{10,... | collective-permute-start | bytes 110600 | tf_op jit(solution)/shard_map/ppermute | solution.py:23
  121.0 8.6 %collective-permute-start.18 = (f32[72,128]{1,0:T(8,128)S(1)}, f32[72,128]{1,0:T(8,128)S(1)}, u32[]{:S(2)}, u32[]{:S(2)}) collective-permute-start(f32[72,128]{1,0:T(8,128)S(1)} %get-tuple-element.11), channel_id=1, source_target_pairs={{0,6},{1,7},{2,4},{3,5},{4,2},{5,3},{6,0},{7,1},{8,14},{9,15},{10,... | collective-permute-start | bytes 110600 | tf_op jit(solution)/shard_map/ppermute | solution.py:23
  123.9 5.7 %collective-permute-start.19 = (f32[72,128]{1,0:T(8,128)S(1)}, f32[72,128]{1,0:T(8,128)S(1)}, u32[]{:S(2)}, u32[]{:S(2)}) collective-permute-start(f32[72,128]{1,0:T(8,128)S(1)} %get-tuple-element.11), channel_id=1, source_target_pairs={{0,8},{1,9},{2,10},{3,11},{4,12},{5,13},{6,14},{7,15},{8,0},{9,1},... | collective-permute-start | bytes 110600 | tf_op jit(solution)/shard_map/ppermute | solution.py:23
  123.9 5.8 %collective-permute-start.20 = (f32[72,128]{1,0:T(8,128)S(1)}, f32[72,128]{1,0:T(8,128)S(1)}, u32[]{:S(2)}, u32[]{:S(2)}) collective-permute-start(f32[72,128]{1,0:T(8,128)S(1)} %get-tuple-element.11), channel_id=1, source_target_pairs={{0,10},{1,11},{2,8},{3,9},{4,14},{5,15},{6,12},{7,13},{8,2},{9,3},... | collective-permute-start | bytes 110600 | tf_op jit(solution)/shard_map/ppermute | solution.py:23
  124.4 7.3 %collective-permute-start.21 = (f32[72,128]{1,0:T(8,128)S(1)}, f32[72,128]{1,0:T(8,128)S(1)}, u32[]{:S(2)}, u32[]{:S(2)}) collective-permute-start(f32[72,128]{1,0:T(8,128)S(1)} %get-tuple-element.11), channel_id=1, source_target_pairs={{0,12},{1,13},{2,14},{3,15},{4,8},{5,9},{6,10},{7,11},{8,4},{9,5},... | collective-permute-start | bytes 110600 | tf_op jit(solution)/shard_map/ppermute | solution.py:23
  126.0 9.2 %collective-permute-start.22 = (f32[72,128]{1,0:T(8,128)S(1)}, f32[72,128]{1,0:T(8,128)S(1)}, u32[]{:S(2)}, u32[]{:S(2)}) collective-permute-start(f32[72,128]{1,0:T(8,128)S(1)} %get-tuple-element.11), channel_id=1, source_target_pairs={{0,14},{1,15},{2,12},{3,13},{4,10},{5,11},{6,8},{7,9},{8,6},{9,7},... | collective-permute-start | bytes 110600 | tf_op jit(solution)/shard_map/ppermute | solution.py:23
  129.6 6.9 %collective-permute-start.23 = (f32[72,128]{1,0:T(8,128)S(1)}, f32[72,128]{1,0:T(8,128)S(1)}, u32[]{:S(2)}, u32[]{:S(2)}) collective-permute-start(f32[72,128]{1,0:T(8,128)S(1)} %get-tuple-element.11), channel_id=1, source_target_pairs={{0,16},{1,17},{2,18},{3,19},{4,20},{5,21},{6,22},{7,23},{8,24},{9,... | collective-permute-start | bytes 110600 | tf_op jit(solution)/shard_map/ppermute | solution.py:23
  129.6 6.9 %collective-permute-start.24 = (f32[72,128]{1,0:T(8,128)S(1)}, f32[72,128]{1,0:T(8,128)S(1)}, u32[]{:S(2)}, u32[]{:S(2)}) collective-permute-start(f32[72,128]{1,0:T(8,128)S(1)} %get-tuple-element.11), channel_id=1, source_target_pairs={{0,18},{1,19},{2,16},{3,17},{4,22},{5,23},{6,20},{7,21},{8,26},{9,... | collective-permute-start | bytes 110600 | tf_op jit(solution)/shard_map/ppermute | solution.py:23
  129.7 9.1 %collective-permute-start.25 = (f32[72,128]{1,0:T(8,128)S(1)}, f32[72,128]{1,0:T(8,128)S(1)}, u32[]{:S(2)}, u32[]{:S(2)}) collective-permute-start(f32[72,128]{1,0:T(8,128)S(1)} %get-tuple-element.11), channel_id=1, source_target_pairs={{0,20},{1,21},{2,22},{3,23},{4,16},{5,17},{6,18},{7,19},{8,28},{9,... | collective-permute-start | bytes 110600 | tf_op jit(solution)/shard_map/ppermute | solution.py:23
  131.7 11.0 %collective-permute-start.26 = (f32[72,128]{1,0:T(8,128)S(1)}, f32[72,128]{1,0:T(8,128)S(1)}, u32[]{:S(2)}, u32[]{:S(2)}) collective-permute-start(f32[72,128]{1,0:T(8,128)S(1)} %get-tuple-element.11), channel_id=1, source_target_pairs={{0,22},{1,23},{2,20},{3,21},{4,18},{5,19},{6,16},{7,17},{8,30},{9,... | collective-permute-start | bytes 110600 | tf_op jit(solution)/shard_map/ppermute | solution.py:23
  135.2 7.5 %collective-permute-start.27 = (f32[72,128]{1,0:T(8,128)S(1)}, f32[72,128]{1,0:T(8,128)S(1)}, u32[]{:S(2)}, u32[]{:S(2)}) collective-permute-start(f32[72,128]{1,0:T(8,128)S(1)} %get-tuple-element.11), channel_id=1, source_target_pairs={{0,24},{1,25},{2,26},{3,27},{4,28},{5,29},{6,30},{7,31},{8,16},{9,... | collective-permute-start | bytes 110600 | tf_op jit(solution)/shard_map/ppermute | solution.py:23
  136.5 6.3 %collective-permute-start.28 = (f32[72,128]{1,0:T(8,128)S(1)}, f32[72,128]{1,0:T(8,128)S(1)}, u32[]{:S(2)}, u32[]{:S(2)}) collective-permute-start(f32[72,128]{1,0:T(8,128)S(1)} %get-tuple-element.11), channel_id=1, source_target_pairs={{0,26},{1,27},{2,24},{3,25},{4,30},{5,31},{6,28},{7,29},{8,18},{9,... | collective-permute-start | bytes 110600 | tf_op jit(solution)/shard_map/ppermute | solution.py:23
  136.5 6.3 %collective-permute-start.29 = (f32[72,128]{1,0:T(8,128)S(1)}, f32[72,128]{1,0:T(8,128)S(1)}, u32[]{:S(2)}, u32[]{:S(2)}) collective-permute-start(f32[72,128]{1,0:T(8,128)S(1)} %get-tuple-element.11), channel_id=1, source_target_pairs={{0,28},{1,29},{2,30},{3,31},{4,24},{5,25},{6,26},{7,27},{8,20},{9,... | collective-permute-start | bytes 110600 | tf_op jit(solution)/shard_map/ppermute | solution.py:23
  138.8 6.4 %collective-permute-start.30 = (f32[72,128]{1,0:T(8,128)S(1)}, f32[72,128]{1,0:T(8,128)S(1)}, u32[]{:S(2)}, u32[]{:S(2)}) collective-permute-start(f32[72,128]{1,0:T(8,128)S(1)} %get-tuple-element.11), channel_id=1, source_target_pairs={{0,30},{1,31},{2,28},{3,29},{4,26},{5,27},{6,24},{7,25},{8,22},{9,... | collective-permute-start | bytes 110600 | tf_op jit(solution)/shard_map/ppermute | solution.py:23
  145.6 15.7 %collective-permute-start.31 = (f32[1152,128]{1,0:T(8,128)S(1)}, f32[1152,128]{1,0:T(8,128)S(1)}, u32[]{:S(2)}, u32[]{:S(2)}) collective-permute-start(f32[1152,128]{1,0:T(8,128)S(1)} %constant_dynamic-update-slice_fusion.16), channel_id=1, source_target_pairs={{0,1},{1,0},{2,3},{3,2},{4,5},{5,4},{6,7},{7,6},{8,9},{9,8},{10,11... | collective-permute-start | bytes 1769480 | tf_op jit(solution)/shard_map/ppermute | solution.py:23
  (22 other events, 57.6 us)
Sparse Core Ops, SparseCore 0:
  36.1 49.8 all-gather.2

commit v7 on v5

--- a/solution.py
+++ b/solution.py
@@ -140,11 +140,25 @@
     grad_heads = grad_out[0].reshape(tok_rows, head_count, head_dim)
     grad_weighted = (grad_heads * head_factor[:, :, None]).astype(half)
     adjoint_local = jnp.einsum("thp,tn->hpn", grad_weighted, c_proj, preferred_element_type=fl)
-    adjoint_all = lax.all_gather(adjoint_local, "tm")
     adjoint_in = jnp.zeros((head_count, head_dim, state_dim), fl)
-    for k in range(n_blocks - 1, 0, -1):
-        new = gate_all[k][:, None, None] * adjoint_in + adjoint_all[k]
-        adjoint_in = jnp.where(k > my_block, new, adjoint_in)
+    if n_blocks == 4:
+        first = lax.ppermute(adjoint_local, "tm", [(3, 2), (1, 0)])
+        second = lax.ppermute(adjoint_local, "tm", [(3, 1), (2, 0)])
+        third = lax.ppermute(second, "tm", [(0, 1)])
+        fourth = lax.ppermute(first, "tm", [(2, 0)])
+        seen = [
+            first,
+            jnp.where(my_block == 1, third, second),
+            jnp.where(my_block == 2, first, jnp.where(my_block == 1, second, fourth)),
+        ]
+        for k in range(n_blocks - 1, 0, -1):
+            new = gate_all[k][:, None, None] * adjoint_in + seen[k - 1]
+            adjoint_in = jnp.where(k > my_block, new, adjoint_in)
+    else:
+        adjoint_all = lax.all_gather(adjoint_local, "tm")
+        for k in range(n_blocks - 1, 0, -1):
+            new = gate_all[k][:, None, None] * adjoint_in + adjoint_all[k]
+            adjoint_in = jnp.where(k > my_block, new, adjoint_in)
 
     masked = decay_matrix(cum_decay) * step_size.T[:, None, :]
     scores = jnp.dot(c_proj, b_proj.T, preferred_element_type=fl)

time: 145 us -> 142 us (0.979)
  between operations: 14.7 us -> 1.38 us
  waiting for transfers between devices: 35.5 us -> 48.1 us
  starting transfers between devices: 26.6 us -> 37.7 us
  local copies, waits for them, and re-layouts: 25.2 us -> 15.2 us
  matrix products: 26.8 us -> 23.7 us
    ppermute x0 -> x4, waiting for transfers between devices: none -> 29.2 us  [the longest x1 20.1 us: on_device(): second = lax.ppermute(adjoint_local, 'tm', [(3, 1), (2, 0)])]
    all_gather x1 -> x0, waiting for transfers between devices: 13.3 us -> none  [on_device(): adjoint_all = lax.all_gather(adjoint_local, 'tm')]
    ppermute x0 -> x4, starting transfers between devices: none -> 9.65 us  [the longest x1 5.62 us: on_device(): third = lax.ppermute(second, 'tm', [(0, 1)])]
    mul x2 -> x0, local copies, waits for them, and re-layouts: 3.58 us -> none  [on_device(): jnp.einsum('sn,hpn->shp', b_proj, adjoint_half, preferred_element_type=fl)]
    ppermute x14, waiting for transfers between devices: 18.4 us -> 15.2 us  [exchange(): return lax.ppermute(value, axis, pairs)]
    dot_general x1, matrix products: 0.7 us -> 2.93 us  [on_device(): jnp.einsum('bthp,btn->bhpn', xw_all, b_all, preferred_element_type=fl)]
    convert_element_type x1 -> x0, local copies, waits for them, and re-layouts: 2.22 us -> none  [on_device(): x_weighted = (x_heads * tail_factor[:, :, None]).astype(half)]
    dot_general x1, matrix products: 2.42 us -> 0.36 us  [on_device(): jnp.einsum('shp,hpn->sn', x_weighted, adjoint_half, preferred_element_typ...]
  transfers between devices with their start and end apart: 16 -> 19, of which waited for: 13 -> 14; matrix products, arithmetic and copies ran while one was open for 30% -> 18% of each run, Pallas kernels for 0% -> 0%
where the time goes in v7:
time: 142 us; the launch traced here: 141 us
  waiting for transfers between devices  48.1 us (34%)
  starting transfers between devices  37.7 us (27%)
  matrix products  23.7 us (17%)
  local copies, waits for them, and re-layouts  15.2 us (11%)
  other arithmetic  15.1 us (11%)
    ppermute x14, starting transfers between devices, exchange(): return lax.ppermute(value, axis, pairs)  20.9 us
    ppermute x1, waiting for transfers between devices, on_device(): second = lax.ppermute(adjoint_local, 'tm', [(3, 1), (2, 0)])  20.1 us
    ppermute x14, waiting for transfers between devices, exchange(): return lax.ppermute(value, axis, pairs)  15.2 us
    all_to_all x1, starting transfers between devices, on_device(): lax.all_to_all(outgoing, ('tm', 'series'), split_axis=0, concat_axis=1, t...  7.1 us
    ppermute x1, starting transfers between devices, on_device(): third = lax.ppermute(second, 'tm', [(0, 1)])  5.62 us
    convert_element_type x1, local copies, waits for them, and re-layouts, on_device(): xw_all = (x_all * tail_all[..., None]).astype(half)  5.33 us
    unnamed x71, local copies, waits for them, and re-layouts  5.12 us
    ppermute x1, waiting for transfers between devices, on_device(): fourth = lax.ppermute(first, 'tm', [(2, 0)])  4.81 us
  transfers between devices with their start and end apart: 19, of which 14 were waited for; matrix products, arithmetic and copies ran while one was open for 18% of the time, Pallas kernels for 0%

profile of v7, /device:TPU:1, one launch (start us, length us, event | category | flops | bytes accessed | tf_op | source)
XLA Modules:
  0.0 141.2 jit_solution(4078318494694262687)
XLA Ops:
  2.0 1.2 gather_fusion
  4.0 7.1 %all-to-all-start = ((f32[32,1,16]{2,1,0:T(1,128)}), f32[32,1,16]{2,1,0:T(1,128)S(1)}, u32[]{:S(2)}, u32[]{:S(2)}) async-start(f32[32,1,16]{2,1,0:T(1,128)} %bitcast), calls=%async_computation | async-start | bytes 32768 | tf_op jit(solution)/shard_map/all_to_all | solution.py:92
  12.7 1.3 copy.89
  14.1 3.7 %all-to-all-done = f32[32,1,16]{2,1,0:T(1,128)S(1)} async-done(((f32[32,1,16]{2,1,0:T(1,128)}), f32[32,1,16]{2,1,0:T(1,128)S(1)}, u32[]{:S(2)}, u32[]{:S(2)}) %all-to-all-start) | async-done | bytes 2080 | tf_op jit(solution)/shard_map/all_to_all | solution.py:92
  19.1 1.5 %convert_reduce_fusion = f32[4096]{0:T(1024)S(1)} fusion(f32[4096]{0:T(1024)S(1)} %get-tuple-element.33, f32[4096]{0:T(1024)S(1)} %convert_element_type.97, f32[512]{0:T(512)S(1)} %le.22), kind=kLoop, calls=%fused_computation.1 | loop fusion | flops 10481664 | bytes 51200 | tf_op jit(solution)/shard_map/reduce_sum | solution.py:98
  21.2 4.1 %fusion = f32[512,4]{0,1:T(4,128)S(1)} fusion(f32[4096]{0:T(1024)S(1)} %get-tuple-element.33, f32[4096]{0:T(1024)S(1)} %convert_element_type.97, f32[512]{0:T(512)S(1)} %le.22, f32[4096,1]{0,1:T(1,128)S(1)} %bitcast.191, f32[4096,1]{0,1:T(1,128)S(1)} %bitcast.183, f32[4096,1]{0,1:T(1,128)S(1)} %bitcast.182, f32[4096,1]{0,1:T(1,128)S(1)} %sub.69), kind=kOutput, calls=%fused_computation.3 | convolution fusion | flops 107003904 | bytes 108544 | tf_op jit(solution)/shard_map/dot_general | solution.py:101
  27.4 1.1 compare_select_fusion
  30.4 1.6 %fusion.5 = bf16[128,128]{0,1:T(8,128)(2,1)S(1)} fusion(bf16[128,32,64]{0,2,1:T(8,128)(2,1)S(1)} %bitcast.171, bf16[128,32,64]{0,2,1:T(8,128)(2,1)S(1)} %bitcast.163, f32[32,128]{1,0:T(8,128)S(1)} %get-tuple-element.38, f32[32,128]{1,0:T(8,128)S(1)} %copy.81, pred[128,128]{0,1:T(8,128)(4,1)S(1)} %iota_compare_fusion), kind=kOutput, calls=%fused_computation.13 | convolution fusion | flops 70238208 | bytes 1130496 | tf_op jit(solution)/shard_map/thp,shp->hts/dot_general | solution.py:181
  32.0 0.9 fusion.67
  33.8 1.3 fusion.31
  35.1 1.3 collective-permute-start
  36.3 1.3 collective-permute-start.1
  38.4 1.6 %convolution_convert_fusion = bf16[512,2304]{1,0:T(8,128)(2,1)S(1)} fusion(bf16[128,2304]{1,0:T(8,128)(2,1)S(1)} %copy-done, f32[128]{0:T(128)S(1)} %add_multiply_fusion, f32[512]{0:T(512)S(1)} %bitcast.194), kind=kOutput, calls=%fused_computation.4 | convolution fusion | flops 303300608 | bytes 2951680 | tf_op jit(solution)/shard_map/dot_general | solution.py:122
  40.0 2.5 %slice_convert_fusion = f32[4,128,2048]{2,1,0:T(8,128)} fusion(bf16[4,128,2304]{2,1,0:T(8,128)(2,1)S(1)} %bitcast.161), kind=kLoop, calls=%fused_computation.11 | loop fusion | flops 1048576 | bytes 6291456 | tf_op jit(solution)/shard_map/convert_element_type | solution.py:132
  42.5 20.1 %collective-permute-done.1 = f32[32,64,128]{2,1,0:T(8,128)} collective-permute-done((f32[32,64,128]{2,1,0:T(8,128)}, f32[32,64,128]{2,1,0:T(8,128)}, u32[]{:S(2)}, u32[]{:S(2)}) %collective-permute-start.1) | collective-permute-done | bytes 1048608 | tf_op jit(solution)/shard_map/ppermute | solution.py:146
  62.6 5.6 %collective-permute-start.3 = (f32[32,64,128]{2,1,0:T(8,128)}, f32[32,64,128]{2,1,0:T(8,128)}, u32[]{:S(2)}, u32[]{:S(2)}) collective-permute-start(f32[32,64,128]{2,1,0:T(8,128)} %collective-permute-done.1), channel_id=1, source_target_pairs={{0,8},{1,9},{2,10},{3,11},{4,12},{5,13},{6,14},{7,15}} | collective-permute-start | bytes 3145736 | tf_op jit(solution)/shard_map/ppermute | solution.py:147
  68.3 1.5 %collective-permute-start.2 = (f32[32,64,128]{2,1,0:T(8,128)}, f32[32,64,128]{2,1,0:T(8,128)}, u32[]{:S(2)}, u32[]{:S(2)}) collective-permute-start(f32[32,64,128]{2,1,0:T(8,128)} %collective-permute-done), channel_id=1, source_target_pairs={{16,0},{17,1},{18,2},{19,3},{20,4},{21,5},{22,6},{23,7}} | collective-permute-start | bytes 3145736 | tf_op jit(solution)/shard_map/ppermute | solution.py:148
  70.3 0.9 fusion.16
  71.2 5.3 %copy.85 = f32[4,128,2048]{1,2,0:T(8,128)} copy(f32[4,128,2048]{2,1,0:T(8,128)} %slice_convert_fusion) | data formatting | bytes 8388608 | tf_op jit(solution)/shard_map/convert_element_type | solution.py:132
  76.6 1.0 copy.87
  77.6 2.9 %fusion.4 = f32[4,32,64,128]{3,2,1,0:T(8,128)S(1)} fusion(f32[4,128,32,64]{1,3,2,0:T(8,128)} %bitcast.160, f32[4,128,32]{1,2,0:T(8,128)S(1)} %copy.87, bf16[4,128,2304]{2,1,0:T(8,128)(2,1)S(1)} %bitcast.162), kind=kOutput, calls=%fused_computation.10 | convolution fusion | flops 270532608 | bytes 8585216 | tf_op jit(solution)/shard_map/bthp,btn->bhpn/dot_general | solution.py:133
  81.3 1.3 copy-done.1
  82.6 1.3 convolution_bitcast_fusion
  83.9 4.3 %collective-permute-done.3 = f32[32,64,128]{2,1,0:T(8,128)} collective-permute-done((f32[32,64,128]{2,1,0:T(8,128)}, f32[32,64,128]{2,1,0:T(8,128)}, u32[]{:S(2)}, u32[]{:S(2)}) %collective-permute-start.3) | collective-permute-done | bytes 1048608 | tf_op jit(solution)/shard_map/ppermute | solution.py:147
  88.2 4.8 %collective-permute-done.2 = f32[32,64,128]{2,1,0:T(8,128)} collective-permute-done((f32[32,64,128]{2,1,0:T(8,128)}, f32[32,64,128]{2,1,0:T(8,128)}, u32[]{:S(2)}, u32[]{:S(2)}) %collective-permute-start.2) | collective-permute-done | bytes 1048608 | tf_op jit(solution)/shard_map/ppermute | solution.py:148
  93.0 3.0 %select_convert_fusion.1 = bf16[32,64,128]{2,1,0:T(8,128)(2,1)S(1)} fusion(f32[32,64,128]{2,1,0:T(8,128)} %collective-permute-done, f32[32,64,128]{2,1,0:T(8,128)} %collective-permute-done.3, f32[32,64,128]{2,1,0:T(8,128)} %collective-permute-done.1, f32[32,64,128]{2,1,0:T(8,128)} %collective-permute-done.2, f32[32]{0:T(128)S(1)} %copy-done.26, ...), kind=kLoop, calls=%fused_computation.50 | loop fusion | flops 3145728 | bytes 4718981 | tf_op jit(solution)/shard_map/convert_element_type | solution.py:167
  96.4 1.1 fusion.10
  98.1 3.1 %collective-permute-start.4 = (f32[1152,128]{1,0:T(8,128)S(1)}, f32[1152,128]{1,0:T(8,128)S(1)}, u32[]{:S(2)}, u32[]{:S(2)}) collective-permute-start(f32[1152,128]{1,0:T(8,128)S(1)} %constant_dynamic-slice_fusion.6), channel_id=1, source_target_pairs={{0,1},{1,0},{2,3},{3,2},{4,5},{5,4},{6,7},{7,6},{8,9},{9,8},{10,11... | collective-permute-start | bytes 1769480 | tf_op jit(solution)/shard_map/ppermute | solution.py:26
  101.2 1.6 %collective-permute-done.4 = f32[1152,128]{1,0:T(8,128)S(1)} collective-permute-done((f32[1152,128]{1,0:T(8,128)S(1)}, f32[1152,128]{1,0:T(8,128)S(1)}, u32[]{:S(2)}, u32[]{:S(2)}) %collective-permute-start.4) | collective-permute-done | bytes 589856 | tf_op jit(solution)/shard_map/ppermute | solution.py:26
  103.1 2.6 %collective-permute-start.5 = (f32[288,128]{1,0:T(8,128)S(1)}, f32[288,128]{1,0:T(8,128)S(1)}, u32[]{:S(2)}, u32[]{:S(2)}) collective-permute-start(f32[288,128]{1,0:T(8,128)S(1)} %get-tuple-element.20), channel_id=1, source_target_pairs={{0,8},{8,0},{16,24},{24,16},{1,9},{9,1},{17,25},{25,17},{2,10},{10... | collective-permute-start | bytes 442376 | tf_op jit(solution)/shard_map/ppermute | solution.py:26
  105.7 3.4 %collective-permute-done.7 = f32[288,128]{1,0:T(8,128)S(1)} collective-permute-done((f32[288,128]{1,0:T(8,128)S(1)}, f32[288,128]{1,0:T(8,128)S(1)}, u32[]{:S(2)}, u32[]{:S(2)}) %collective-permute-start.7) | collective-permute-done | bytes 147488 | tf_op jit(solution)/shard_map/ppermute | solution.py:26
  109.0 2.3 %collective-permute-done.6 = f32[288,128]{1,0:T(8,128)S(1)} collective-permute-done((f32[288,128]{1,0:T(8,128)S(1)}, f32[288,128]{1,0:T(8,128)S(1)}, u32[]{:S(2)}, u32[]{:S(2)}) %collective-permute-start.6) | collective-permute-done | bytes 147488 | tf_op jit(solution)/shard_map/ppermute | solution.py:26
  111.5 1.3 collective-permute-start.9
  112.9 2.1 %collective-permute-start.8 = (f32[72,128]{1,0:T(8,128)S(1)}, f32[72,128]{1,0:T(8,128)S(1)}, u32[]{:S(2)}, u32[]{:S(2)}) collective-permute-start(f32[72,128]{1,0:T(8,128)S(1)} %get-tuple-element.29), channel_id=1, source_target_pairs={{0,2},{1,3},{2,0},{3,1},{4,6},{5,7},{6,4},{7,5},{8,10},{9,11},{10,... | collective-permute-start | bytes 110600 | tf_op jit(solution)/shard_map/ppermute | solution.py:26
  115.0 1.2 collective-permute-done.10
  116.6 1.9 %collective-permute-start.13 = (f32[72,128]{1,0:T(8,128)S(1)}, f32[72,128]{1,0:T(8,128)S(1)}, u32[]{:S(2)}, u32[]{:S(2)}) collective-permute-start(f32[72,128]{1,0:T(8,128)S(1)} %add_add_fusion.1), channel_id=1, source_target_pairs={{0,6},{1,7},{2,4},{3,5},{4,2},{5,3},{6,0},{7,1},{8,14},{9,15},{10,... | collective-permute-start | bytes 110600 | tf_op jit(solution)/shard_map/ppermute | solution.py:26
  118.5 1.1 collective-permute-start.12
  120.2 1.1 collective-permute-done.13
  121.3 1.0 collective-permute-done.12
  122.8 1.5 %collective-permute-start.16 = (f32[288,128]{1,0:T(8,128)S(1)}, f32[288,128]{1,0:T(8,128)S(1)}, u32[]{:S(2)}, u32[]{:S(2)}) collective-permute-start(f32[288,128]{1,0:T(8,128)S(1)} %get-tuple-element.24), channel_id=1, source_target_pairs={{0,24},{8,16},{16,8},{24,0},{1,25},{9,17},{17,9},{25,1},{2,26},{10... | collective-permute-start | bytes 442376 | tf_op jit(solution)/shard_map/ppermute | solution.py:26
  124.3 1.2 collective-permute-start.14
  125.5 2.3 %collective-permute-done.16 = f32[288,128]{1,0:T(8,128)S(1)} collective-permute-done((f32[288,128]{1,0:T(8,128)S(1)}, f32[288,128]{1,0:T(8,128)S(1)}, u32[]{:S(2)}, u32[]{:S(2)}) %collective-permute-start.16) | collective-permute-done | bytes 147488 | tf_op jit(solution)/shard_map/ppermute | solution.py:26
  127.9 1.5 %collective-permute-done.15 = f32[288,128]{1,0:T(8,128)S(1)} collective-permute-done((f32[288,128]{1,0:T(8,128)S(1)}, f32[288,128]{1,0:T(8,128)S(1)}, u32[]{:S(2)}, u32[]{:S(2)}) %collective-permute-start.15) | collective-permute-done | bytes 147488 | tf_op jit(solution)/shard_map/ppermute | solution.py:26
  129.5 5.2 %collective-permute-start.17 = (f32[1152,128]{1,0:T(8,128)S(1)}, f32[1152,128]{1,0:T(8,128)S(1)}, u32[]{:S(2)}, u32[]{:S(2)}) collective-permute-start(f32[1152,128]{1,0:T(8,128)S(1)} %get-tuple-element.14), channel_id=1, source_target_pairs={{0,1},{1,0},{2,3},{3,2},{4,5},{5,4},{6,7},{7,6},{8,9},{9,8},{10,11... | collective-permute-start | bytes 1769480 | tf_op jit(solution)/shard_map/ppermute | solution.py:26
  134.8 1.3 convolution_bitcast_fusion.1
  136.1 2.4 %fusion.9 = bf16[128,32,64]{0,2,1:T(8,128)(2,1)S(1)} fusion(f32[128,32,64]{0,2,1:T(8,128)S(1)} %convolution_bitcast_fusion.1, f32[4,32,64,128]{3,2,1,0:T(8,128)} %copy-done.1, f32[128,32]{0,1:T(8,128)S(1)} %copy.88, f32[32]{0:T(128)S(1)} %copy-done.28, f32[32]{0:T(128)S(1)} %copy-done.23, f32[32]{0:T(128)S(1)} %copy-done.25, pred[]{:T(512)S(6)} %gt.24, ...), kind=kOutput, calls=%fused_computation.27 | convolution fusion | flops 70254592 | bytes 4768131 | tf_op jit(solution)/shard_map/tn,hpn->thp/dot_general | solution.py:171
  138.5 1.0 copy.93
  139.8 1.4 copy.94
  (140 shorter events, 15.8 us)
Async XLA Ops:
  0.6 24.8 %copy-start = (bf16[128,2304]{1,0:T(8,128)(2,1)S(1)}, bf16[128,2304]{1,0:T(8,128)(2,1)}, u32[]{:S(2)}) copy-start(bf16[128,2304]{1,0:T(8,128)(2,1)} %param.11) | copy-start | bytes 1769476
  4.0 13.8 %all-to-all-start = ((f32[32,1,16]{2,1,0:T(1,128)}), f32[32,1,16]{2,1,0:T(1,128)S(1)}, u32[]{:S(2)}, u32[]{:S(2)}) async-start(f32[32,1,16]{2,1,0:T(1,128)} %bitcast), calls=%async_computation | async-start | bytes 32768 | tf_op jit(solution)/shard_map/all_to_all | solution.py:92
  11.1 19.3 %copy-start.14 = (pred[128,128]{0,1:T(8,128)(4,1)}, pred[128,128]{0,1:T(8,128)(4,1)S(1)}, u32[]{:S(2)}) copy-start(pred[128,128]{0,1:T(8,128)(4,1)S(1)} %iota_compare_fusion) | copy-start | bytes 49156
  12.7 25.7 %copy-start.17 = (f32[128]{0:T(128)}, f32[128]{0:T(128)S(1)}, u32[]{:S(2)}) copy-start(f32[128]{0:T(128)S(1)} %add_multiply_fusion) | copy-start | bytes 1540
  25.4 1.6 %copy-start.29 = (bf16[128,32]{0,1:T(8,128)(2,1)S(1)}, bf16[128,32]{0,1:T(8,128)(2,1)}, u32[]{:S(2)}) copy-start(bf16[128,32]{0,1:T(8,128)(2,1)} %param.12) | copy-start | bytes 24580
  25.4 1.6 %copy-start.30 = (f32[32]{0:T(128)S(1)}, f32[32]{0:T(128)}, u32[]{:S(2)}) copy-start(f32[32]{0:T(128)} %param.13) | copy-start | bytes 388
  25.4 3.2 %copy-start.19 = (f32[32]{0:T(128)S(1)}, f32[32]{0:T(128)}, u32[]{:S(2)}) copy-start(f32[32]{0:T(128)} %param.14) | copy-start | bytes 388
  25.5 3.4 %copy-start.20 = (f32[1,128]{1,0:T(1,128)}, f32[1,128]{1,0:T(1,128)S(1)}, u32[]{:S(2)}) copy-start(f32[1,128]{1,0:T(1,128)S(1)} %constant_dynamic-slice_fusion.7) | copy-start | bytes 1540
  26.0 7.7 %copy-start.2 = (bf16[128,2304]{1,0:T(8,128)(2,1)}, bf16[128,2304]{1,0:T(8,128)(2,1)S(1)}, u32[]{:S(2)}) copy-start(bf16[128,2304]{1,0:T(8,128)(2,1)S(1)} %convolution_convert_fusion.1) | copy-start | bytes 1769476
  27.4 4.6 %copy-start.31 = (f32[32,128]{1,0:T(8,128)}, f32[32,128]{1,0:T(8,128)S(1)}, u32[]{:S(2)}) copy-start(f32[32,128]{1,0:T(8,128)S(1)} %get-tuple-element.38) | copy-start | bytes 49156
  29.9 2.1 %copy-start.3 = (bf16[128,2048]{0,1:T(8,128)(2,1)}, bf16[128,2048]{0,1:T(8,128)(2,1)S(1)}, u32[]{:S(2)}) copy-start(bf16[128,2048]{0,1:T(8,128)(2,1)S(1)} %copy.78) | copy-start | bytes 1572868
  30.4 1.6 %copy-start.11 = (f32[32,128]{1,0:T(8,128)}, f32[32,128]{1,0:T(8,128)S(1)}, u32[]{:S(2)}) copy-start(f32[32,128]{1,0:T(8,128)S(1)} %copy.81) | copy-start | bytes 49156
  35.1 33.2 %collective-permute-start = (f32[32,64,128]{2,1,0:T(8,128)}, f32[32,64,128]{2,1,0:T(8,128)}, u32[]{:S(2)}, u32[]{:S(2)}) collective-permute-start(f32[32,64,128]{2,1,0:T(8,128)} %fusion.31), channel_id=1, source_target_pairs={{24,16},{8,0},{25,17},{9,1},{26,18},{10,2},{27,19},{11,3},{28,20},... | collective-permute-start | bytes 3145736 | tf_op jit(solution)/shard_map/ppermute | solution.py:145
  36.3 26.3 %collective-permute-start.1 = (f32[32,64,128]{2,1,0:T(8,128)}, f32[32,64,128]{2,1,0:T(8,128)}, u32[]{:S(2)}, u32[]{:S(2)}) collective-permute-start(f32[32,64,128]{2,1,0:T(8,128)} %fusion.31), channel_id=1, source_target_pairs={{24,8},{16,0},{25,9},{17,1},{26,10},{18,2},{27,11},{19,3},{28,12},... | collective-permute-start | bytes 3145736 | tf_op jit(solution)/shard_map/ppermute | solution.py:146
  62.6 25.6 %collective-permute-start.3 = (f32[32,64,128]{2,1,0:T(8,128)}, f32[32,64,128]{2,1,0:T(8,128)}, u32[]{:S(2)}, u32[]{:S(2)}) collective-permute-start(f32[32,64,128]{2,1,0:T(8,128)} %collective-permute-done.1), channel_id=1, source_target_pairs={{0,8},{1,9},{2,10},{3,11},{4,12},{5,13},{6,14},{7,15}} | collective-permute-start | bytes 3145736 | tf_op jit(solution)/shard_map/ppermute | solution.py:147
  68.3 24.8 %collective-permute-start.2 = (f32[32,64,128]{2,1,0:T(8,128)}, f32[32,64,128]{2,1,0:T(8,128)}, u32[]{:S(2)}, u32[]{:S(2)}) collective-permute-start(f32[32,64,128]{2,1,0:T(8,128)} %collective-permute-done), channel_id=1, source_target_pairs={{16,0},{17,1},{18,2},{19,3},{20,4},{21,5},{22,6},{23,7}} | collective-permute-start | bytes 3145736 | tf_op jit(solution)/shard_map/ppermute | solution.py:148
  77.6 3.0 %copy-start.5 = (bf16[1,128,2048]{1,2,0:T(8,128)(2,1)S(1)}, bf16[1,128,2048]{1,2,0:T(8,128)(2,1)}, u32[]{:S(2)}) copy-start(bf16[1,128,2048]{1,2,0:T(8,128)(2,1)} %fusion.16) | copy-start | bytes 1572868
  77.6 3.0 %copy-start.10 = (f32[128,128]{0,1:T(8,128)S(1)}, f32[128,128]{0,1:T(8,128)}, u32[]{:S(2)}) copy-start(f32[128,128]{0,1:T(8,128)} %fusion.67) | copy-start | bytes 196612
  77.6 3.0 %copy-start.22 = (f32[32]{0:T(128)S(1)}, f32[32]{0:T(128)}, u32[]{:S(2)}) copy-start(f32[32]{0:T(128)} %get-tuple-element.36) | copy-start | bytes 388
  77.6 3.0 %copy-start.24 = (f32[32]{0:T(128)S(1)}, f32[32]{0:T(128)}, u32[]{:S(2)}) copy-start(f32[32]{0:T(128)} %get-tuple-element.37) | copy-start | bytes 388
  77.6 3.0 %copy-start.27 = (f32[32]{0:T(128)S(1)}, f32[32]{0:T(128)}, u32[]{:S(2)}) copy-start(f32[32]{0:T(128)} %get-tuple-element.35) | copy-start | bytes 388
  80.6 2.0 %copy-start.1 = (f32[4,32,64,128]{3,2,1,0:T(8,128)}, f32[4,32,64,128]{3,2,1,0:T(8,128)S(1)}, u32[]{:S(2)}) copy-start(f32[4,32,64,128]{3,2,1,0:T(8,128)S(1)} %fusion.4) | copy-start | bytes 12582916
  80.6 1.9 %copy-start.7 = (f32[128,128]{0,1:T(8,128)S(1)}, f32[128,128]{0,1:T(8,128)}, u32[]{:S(2)}) copy-start(f32[128,128]{0,1:T(8,128)} %fusion.70) | copy-start | bytes 196612
  80.7 1.9 %copy-start.12 = (f32[32,128]{1,0:T(8,128)S(1)}, f32[32,128]{1,0:T(8,128)}, u32[]{:S(2)}) copy-start(f32[32,128]{1,0:T(8,128)} %copy-done.11) | copy-start | bytes 49156
  80.7 1.9 %copy-start.15 = (pred[128,128]{0,1:T(8,128)(4,1)S(1)}, pred[128,128]{0,1:T(8,128)(4,1)}, u32[]{:S(2)}) copy-start(pred[128,128]{0,1:T(8,128)(4,1)} %copy-done.14) | copy-start | bytes 49156
  80.7 1.9 %copy-start.32 = (f32[32,128]{1,0:T(8,128)S(1)}, f32[32,128]{1,0:T(8,128)}, u32[]{:S(2)}) copy-start(f32[32,128]{1,0:T(8,128)} %copy-done.31) | copy-start | bytes 49156
  82.6 10.4 %copy-start.26 = (f32[32]{0:T(128)S(1)}, f32[32]{0:T(128)}, u32[]{:S(2)}) copy-start(f32[32]{0:T(128)} %get-tuple-element.34) | copy-start | bytes 388
  93.0 3.0 %copy-start.4 = (bf16[128,2048]{0,1:T(8,128)(2,1)S(1)}, bf16[128,2048]{0,1:T(8,128)(2,1)}, u32[]{:S(2)}) copy-start(bf16[128,2048]{0,1:T(8,128)(2,1)} %copy-done.3) | copy-start | bytes 1572868
  93.0 3.0 %copy-start.6 = (f32[128,32]{0,1:T(8,128)S(1)}, f32[128,32]{0,1:T(8,128)}, u32[]{:S(2)}) copy-start(f32[128,32]{0,1:T(8,128)} %exponential_multiply_fusion.1) | copy-start | bytes 49156
  93.0 3.0 %copy-start.9 = (f32[128,128]{0,1:T(8,128)S(1)}, f32[128,128]{0,1:T(8,128)}, u32[]{:S(2)}) copy-start(f32[128,128]{0,1:T(8,128)} %fusion.73) | copy-start | bytes 196612
  98.1 4.7 %collective-permute-start.4 = (f32[1152,128]{1,0:T(8,128)S(1)}, f32[1152,128]{1,0:T(8,128)S(1)}, u32[]{:S(2)}, u32[]{:S(2)}) collective-permute-start(f32[1152,128]{1,0:T(8,128)S(1)} %constant_dynamic-slice_fusion.6), channel_id=1, source_target_pairs={{0,1},{1,0},{2,3},{3,2},{4,5},{5,4},{6,7},{7,6},{8,9},{9,8},{10,11... | collective-permute-start | bytes 1769480 | tf_op jit(solution)/shard_map/ppermute | solution.py:26
  102.9 6.1 %collective-permute-start.7 = (f32[288,128]{1,0:T(8,128)S(1)}, f32[288,128]{1,0:T(8,128)S(1)}, u32[]{:S(2)}, u32[]{:S(2)}) collective-permute-start(f32[288,128]{1,0:T(8,128)S(1)} %get-tuple-element.21), channel_id=1, source_target_pairs={{0,24},{8,16},{16,8},{24,0},{1,25},{9,17},{17,9},{25,1},{2,26},{10... | collective-permute-start | bytes 442376 | tf_op jit(solution)/shard_map/ppermute | solution.py:26
  103.0 8.3 %collective-permute-start.6 = (f32[288,128]{1,0:T(8,128)S(1)}, f32[288,128]{1,0:T(8,128)S(1)}, u32[]{:S(2)}, u32[]{:S(2)}) collective-permute-start(f32[288,128]{1,0:T(8,128)S(1)} %get-tuple-element.22), channel_id=1, source_target_pairs={{0,16},{8,24},{16,0},{24,8},{1,17},{9,25},{17,1},{25,9},{2,18},{10... | collective-permute-start | bytes 442376 | tf_op jit(solution)/shard_map/ppermute | solution.py:26
  103.1 8.2 %collective-permute-start.5 = (f32[288,128]{1,0:T(8,128)S(1)}, f32[288,128]{1,0:T(8,128)S(1)}, u32[]{:S(2)}, u32[]{:S(2)}) collective-permute-start(f32[288,128]{1,0:T(8,128)S(1)} %get-tuple-element.20), channel_id=1, source_target_pairs={{0,8},{8,0},{16,24},{24,16},{1,9},{9,1},{17,25},{25,17},{2,10},{10... | collective-permute-start | bytes 442376 | tf_op jit(solution)/shard_map/ppermute | solution.py:26
  111.4 4.8 %collective-permute-start.10 = (f32[72,128]{1,0:T(8,128)S(1)}, f32[72,128]{1,0:T(8,128)S(1)}, u32[]{:S(2)}, u32[]{:S(2)}) collective-permute-start(f32[72,128]{1,0:T(8,128)S(1)} %get-tuple-element.30), channel_id=1, source_target_pairs={{0,6},{1,7},{2,4},{3,5},{4,2},{5,3},{6,0},{7,1},{8,14},{9,15},{10,... | collective-permute-start | bytes 110600 | tf_op jit(solution)/shard_map/ppermute | solution.py:26
  111.5 4.6 %collective-permute-start.9 = (f32[72,128]{1,0:T(8,128)S(1)}, f32[72,128]{1,0:T(8,128)S(1)}, u32[]{:S(2)}, u32[]{:S(2)}) collective-permute-start(f32[72,128]{1,0:T(8,128)S(1)} %get-tuple-element.31), channel_id=1, source_target_pairs={{0,4},{1,5},{2,6},{3,7},{4,0},{5,1},{6,2},{7,3},{8,12},{9,13},{10,... | collective-permute-start | bytes 110600 | tf_op jit(solution)/shard_map/ppermute | solution.py:26
  112.9 3.7 %collective-permute-start.8 = (f32[72,128]{1,0:T(8,128)S(1)}, f32[72,128]{1,0:T(8,128)S(1)}, u32[]{:S(2)}, u32[]{:S(2)}) collective-permute-start(f32[72,128]{1,0:T(8,128)S(1)} %get-tuple-element.29), channel_id=1, source_target_pairs={{0,2},{1,3},{2,0},{3,1},{4,6},{5,7},{6,4},{7,5},{8,10},{9,11},{10,... | collective-permute-start | bytes 110600 | tf_op jit(solution)/shard_map/ppermute | solution.py:26
  116.6 4.7 %collective-permute-start.13 = (f32[72,128]{1,0:T(8,128)S(1)}, f32[72,128]{1,0:T(8,128)S(1)}, u32[]{:S(2)}, u32[]{:S(2)}) collective-permute-start(f32[72,128]{1,0:T(8,128)S(1)} %add_add_fusion.1), channel_id=1, source_target_pairs={{0,6},{1,7},{2,4},{3,5},{4,2},{5,3},{6,0},{7,1},{8,14},{9,15},{10,... | collective-permute-start | bytes 110600 | tf_op jit(solution)/shard_map/ppermute | solution.py:26
  118.5 3.8 %collective-permute-start.12 = (f32[72,128]{1,0:T(8,128)S(1)}, f32[72,128]{1,0:T(8,128)S(1)}, u32[]{:S(2)}, u32[]{:S(2)}) collective-permute-start(f32[72,128]{1,0:T(8,128)S(1)} %add_add_fusion.1), channel_id=1, source_target_pairs={{0,4},{1,5},{2,6},{3,7},{4,0},{5,1},{6,2},{7,3},{8,12},{9,13},{10,... | collective-permute-start | bytes 110600 | tf_op jit(solution)/shard_map/ppermute | solution.py:26
  119.6 3.1 %collective-permute-start.11 = (f32[72,128]{1,0:T(8,128)S(1)}, f32[72,128]{1,0:T(8,128)S(1)}, u32[]{:S(2)}, u32[]{:S(2)}) collective-permute-start(f32[72,128]{1,0:T(8,128)S(1)} %add_add_fusion.1), channel_id=1, source_target_pairs={{0,2},{1,3},{2,0},{3,1},{4,6},{5,7},{6,4},{7,5},{8,10},{9,11},{10,... | collective-permute-start | bytes 110600 | tf_op jit(solution)/shard_map/ppermute | solution.py:26
  122.8 12.0 %copy-start.8 = (f32[128,128]{0,1:T(8,128)S(1)}, f32[128,128]{0,1:T(8,128)}, u32[]{:S(2)}) copy-start(f32[128,128]{0,1:T(8,128)} %fusion.70) | copy-start | bytes 196612
  122.8 12.0 %copy-start.13 = (f32[32,128]{1,0:T(8,128)S(1)}, f32[32,128]{1,0:T(8,128)}, u32[]{:S(2)}) copy-start(f32[32,128]{1,0:T(8,128)} %copy-done.11) | copy-start | bytes 49156
  122.8 12.0 %copy-start.16 = (pred[128,128]{0,1:T(8,128)(4,1)S(1)}, pred[128,128]{0,1:T(8,128)(4,1)}, u32[]{:S(2)}) copy-start(pred[128,128]{0,1:T(8,128)(4,1)} %copy-done.14) | copy-start | bytes 49156
  122.8 11.9 %copy-start.33 = (f32[32,128]{1,0:T(8,128)S(1)}, f32[32,128]{1,0:T(8,128)}, u32[]{:S(2)}) copy-start(f32[32,128]{1,0:T(8,128)} %copy-done.31) | copy-start | bytes 49156
  122.8 5.1 %collective-permute-start.16 = (f32[288,128]{1,0:T(8,128)S(1)}, f32[288,128]{1,0:T(8,128)S(1)}, u32[]{:S(2)}, u32[]{:S(2)}) collective-permute-start(f32[288,128]{1,0:T(8,128)S(1)} %get-tuple-element.24), channel_id=1, source_target_pairs={{0,24},{8,16},{16,8},{24,0},{1,25},{9,17},{17,9},{25,1},{2,26},{10... | collective-permute-start | bytes 442376 | tf_op jit(solution)/shard_map/ppermute | solution.py:26
  124.3 5.1 %collective-permute-start.15 = (f32[288,128]{1,0:T(8,128)S(1)}, f32[288,128]{1,0:T(8,128)S(1)}, u32[]{:S(2)}, u32[]{:S(2)}) collective-permute-start(f32[288,128]{1,0:T(8,128)S(1)} %get-tuple-element.24), channel_id=1, source_target_pairs={{0,16},{8,24},{16,0},{24,8},{1,17},{9,25},{17,1},{25,9},{2,18},{10... | collective-permute-start | bytes 442376 | tf_op jit(solution)/shard_map/ppermute | solution.py:26
  124.3 5.1 %collective-permute-start.14 = (f32[288,128]{1,0:T(8,128)S(1)}, f32[288,128]{1,0:T(8,128)S(1)}, u32[]{:S(2)}, u32[]{:S(2)}) collective-permute-start(f32[288,128]{1,0:T(8,128)S(1)} %get-tuple-element.24), channel_id=1, source_target_pairs={{0,8},{8,0},{16,24},{24,16},{1,9},{9,1},{17,25},{25,17},{2,10},{10... | collective-permute-start | bytes 442376 | tf_op jit(solution)/shard_map/ppermute | solution.py:26
  129.5 10.0 %collective-permute-start.17 = (f32[1152,128]{1,0:T(8,128)S(1)}, f32[1152,128]{1,0:T(8,128)S(1)}, u32[]{:S(2)}, u32[]{:S(2)}) collective-permute-start(f32[1152,128]{1,0:T(8,128)S(1)} %get-tuple-element.14), channel_id=1, source_target_pairs={{0,1},{1,0},{2,3},{3,2},{4,5},{5,4},{6,7},{7,6},{8,9},{9,8},{10,11... | collective-permute-start | bytes 1769480 | tf_op jit(solution)/shard_map/ppermute | solution.py:26
  (5 other events, 6.9 us)

commit v8 on v7

--- a/solution.py
+++ b/solution.py
@@ -142,8 +142,9 @@
     adjoint_local = jnp.einsum("thp,tn->hpn", grad_weighted, c_proj, preferred_element_type=fl)
     adjoint_in = jnp.zeros((head_count, head_dim, state_dim), fl)
     if n_blocks == 4:
-        first = lax.ppermute(adjoint_local, "tm", [(3, 2), (1, 0)])
-        second = lax.ppermute(adjoint_local, "tm", [(3, 1), (2, 0)])
+        sent = grad_out[0].astype(fl)
+        first = lax.ppermute(sent, "tm", [(3, 2), (1, 0)])
+        second = lax.ppermute(sent, "tm", [(3, 1), (2, 0)])
         third = lax.ppermute(second, "tm", [(0, 1)])
         fourth = lax.ppermute(first, "tm", [(2, 0)])
         seen = [
@@ -151,8 +152,12 @@
             jnp.where(my_block == 1, third, second),
             jnp.where(my_block == 2, first, jnp.where(my_block == 1, second, fourth)),
         ]
+        c_all = projected_all[:, :, inner_width + state_dim :]
         for k in range(n_blocks - 1, 0, -1):
-            new = gate_all[k][:, None, None] * adjoint_in + seen[k - 1]
+            later = seen[k - 1].reshape(tok_rows, head_count, head_dim)
+            later_weighted = (later * jnp.exp(cum_all[k])[:, :, None]).astype(half)
+            later_local = jnp.einsum("thp,tn->hpn", later_weighted, c_all[k], preferred_element_type=fl)
+            new = gate_all[k][:, None, None] * adjoint_in + later_local
             adjoint_in = jnp.where(k > my_block, new, adjoint_in)
     else:
         adjoint_all = lax.all_gather(adjoint_local, "tm")

time: 142 us -> 136 us (0.958)
  waiting for transfers between devices: 48.1 us -> 33.9 us
  local copies, waits for them, and re-layouts: 15.2 us -> 21.5 us
  starting transfers between devices: 37.7 us -> 43 us
  other arithmetic: 15.1 us -> 11.9 us
    ppermute x2, waiting for transfers between devices: 20.1 us -> 0.01 us  [the longest x1 0.01 us: on_device(): first = lax.ppermute(sent, 'tm', [(3, 2), (1, 0)])]
    all_to_all x1, waiting for transfers between devices: 3.7 us -> 13.5 us  [on_device(): lax.all_to_all(outgoing, ('tm', 'series'), split_axis=0, concat_axis=1, t...]
    exp x0 -> x4, local copies, waits for them, and re-layouts: none -> 5.22 us  [on_device(): later_weighted = (later * jnp.exp(cum_all[k])[:, :, None]).astype(half)]
    ppermute x1, waiting for transfers between devices: 4.81 us -> 0.01 us  [on_device(): fourth = lax.ppermute(first, 'tm', [(2, 0)])]
    all_to_all x1, starting transfers between devices: 7.1 us -> 11.3 us  [on_device(): lax.all_to_all(outgoing, ('tm', 'series'), split_axis=0, concat_axis=1, t...]
    ppermute x14, waiting for transfers between devices: 15.2 us -> 18.5 us  [exchange(): return lax.ppermute(value, axis, pairs)]
    ppermute x1, waiting for transfers between devices: 4.3 us -> 1.89 us  [on_device(): third = lax.ppermute(second, 'tm', [(0, 1)])]
    exp x2, local copies, waits for them, and re-layouts: 0.07 us -> 1.54 us  [on_device(): head_factor = jnp.exp(cum_decay)]
  transfers between devices with their start and end apart: 19 -> 19, of which waited for: 14 -> 13; matrix products, arithmetic and copies ran while one was open for 18% -> 34% of each run, Pallas kernels for 0% -> 0%
where the time goes in v8:
time: 136 us; the launch traced here: 135 us
  starting transfers between devices  43 us (32%)
  waiting for transfers between devices  33.9 us (25%)
  matrix products  23.2 us (17%)
  local copies, waits for them, and re-layouts  21.5 us (16%)
  other arithmetic  11.9 us (9%)
  between operations  1.51 us (1%)
    ppermute x14, starting transfers between devices, exchange(): return lax.ppermute(value, axis, pairs)  21.7 us
    ppermute x14, waiting for transfers between devices, exchange(): return lax.ppermute(value, axis, pairs)  18.5 us
    all_to_all x1, waiting for transfers between devices, on_device(): lax.all_to_all(outgoing, ('tm', 'series'), split_axis=0, concat_axis=1, t...  13.5 us
    all_to_all x1, starting transfers between devices, on_device(): lax.all_to_all(outgoing, ('tm', 'series'), split_axis=0, concat_axis=1, t...  11.3 us
    ppermute x1, starting transfers between devices, on_device(): third = lax.ppermute(second, 'tm', [(0, 1)])  6.21 us
    convert_element_type x1, local copies, waits for them, and re-layouts, on_device(): xw_all = (x_all * tail_all[..., None]).astype(half)  5.38 us
    unnamed x81, local copies, waits for them, and re-layouts  5.32 us
    exp x4, local copies, waits for them, and re-layouts, on_device(): later_weighted = (later * jnp.exp(cum_all[k])[:, :, None]).astype(half)  5.22 us
  transfers between devices with their start and end apart: 19, of which 13 were waited for; matrix products, arithmetic and copies ran while one was open for 34% of the time, Pallas kernels for 0%

profile of v8, /device:TPU:1, one launch (start us, length us, event | category | flops | bytes accessed | tf_op | source)
XLA Modules:
  0.0 134.9 jit_solution(14328981587318109054)
XLA Ops:
  0.7 1.4 %copy.102 = bf16[1,128,2048]{1,2,0:T(8,128)(2,1)S(1)} copy(bf16[1,128,2048]{2,1,0:T(8,128)(2,1)} %param.15) | data formatting | bytes 1048576 | tf_op args[7]
  2.0 1.0 convert_bitcast_fusion
  3.1 1.3 collective-permute-start
  4.4 1.3 collective-permute-start.1
  7.0 11.3 %all-to-all-start = ((f32[32,1,16]{2,1,0:T(1,128)}), f32[32,1,16]{2,1,0:T(1,128)S(1)}, u32[]{:S(2)}, u32[]{:S(2)}) async-start(f32[32,1,16]{2,1,0:T(1,128)} %bitcast), calls=%async_computation | async-start | bytes 32768 | tf_op jit(solution)/shard_map/all_to_all | solution.py:92
  18.5 13.5 %all-to-all-done = f32[32,1,16]{2,1,0:T(1,128)S(1)} async-done(((f32[32,1,16]{2,1,0:T(1,128)}), f32[32,1,16]{2,1,0:T(1,128)S(1)}, u32[]{:S(2)}, u32[]{:S(2)}) %all-to-all-start) | async-done | bytes 2080 | tf_op jit(solution)/shard_map/all_to_all | solution.py:92
  33.3 1.5 %convert_reduce_fusion = f32[4096]{0:T(1024)S(1)} fusion(f32[4096]{0:T(1024)S(1)} %get-tuple-element.39, f32[4096]{0:T(1024)S(1)} %convert_element_type.117, f32[512]{0:T(512)S(1)} %le.22), kind=kLoop, calls=%fused_computation.1 | loop fusion | flops 10481664 | bytes 51200 | tf_op jit(solution)/shard_map/reduce_sum | solution.py:98
  35.5 4.1 %fusion = f32[512,4]{0,1:T(4,128)S(1)} fusion(f32[4096]{0:T(1024)S(1)} %get-tuple-element.39, f32[4096]{0:T(1024)S(1)} %convert_element_type.117, f32[512]{0:T(512)S(1)} %le.22, f32[4096,1]{0,1:T(1,128)S(1)} %bitcast.230, f32[4096,1]{0,1:T(1,128)S(1)} %bitcast.222, f32[4096,1]{0,1:T(1,128)S(1)} %bitcast.221, f32[4096,1]{0,1:T(1,128)S(1)} %sub.69), kind=kOutput, calls=%fused_computation.3 | convolution fusion | flops 107003904 | bytes 108544 | tf_op jit(solution)/shard_map/dot_general | solution.py:101
  39.7 1.1 compare_select_fusion
  44.7 1.6 %fusion.5 = bf16[128,128]{0,1:T(8,128)(2,1)S(1)} fusion(bf16[128,32,64]{0,2,1:T(8,128)(2,1)S(1)} %bitcast.210, bf16[128,32,64]{0,2,1:T(8,128)(2,1)S(1)} %bitcast.200, f32[32,128]{1,0:T(8,128)S(1)} %get-tuple-element.44, f32[32,128]{1,0:T(8,128)S(1)} %copy.94, pred[128,128]{0,1:T(8,128)(4,1)S(1)} %iota_compare_fusion), kind=kOutput, calls=%fused_computation.13 | convolution fusion | flops 70238208 | bytes 1130496 | tf_op jit(solution)/shard_map/thp,shp->hts/dot_general | solution.py:186
  49.4 1.6 %convolution_convert_fusion = bf16[512,2304]{1,0:T(8,128)(2,1)S(1)} fusion(bf16[128,2304]{1,0:T(8,128)(2,1)S(1)} %copy-done, f32[128]{0:T(128)S(1)} %add_multiply_fusion, f32[512]{0:T(512)S(1)} %bitcast.233), kind=kOutput, calls=%fused_computation.4 | convolution fusion | flops 303300608 | bytes 2951680 | tf_op jit(solution)/shard_map/dot_general | solution.py:122
  51.1 2.5 %slice_convert_fusion = f32[4,128,2048]{2,1,0:T(8,128)} fusion(bf16[4,128,2304]{2,1,0:T(8,128)(2,1)S(1)} %bitcast.195), kind=kLoop, calls=%fused_computation.11 | loop fusion | flops 1048576 | bytes 6291456 | tf_op jit(solution)/shard_map/convert_element_type | solution.py:132
  53.6 1.3 collective-permute-start.2
  54.9 6.2 %collective-permute-start.3 = (f32[128,2048]{0,1:T(8,128)}, f32[128,2048]{0,1:T(8,128)}, u32[]{:S(2)}, u32[]{:S(2)}) collective-permute-start(f32[128,2048]{0,1:T(8,128)} %collective-permute-done.1), channel_id=1, source_target_pairs={{0,8},{1,9},{2,10},{3,11},{4,12},{5,13},{6,14},{7,15}} | collective-permute-start | bytes 3145736 | tf_op jit(solution)/shard_map/ppermute | solution.py:148
  62.3 1.5 %copy.105 = f32[128,32]{0,1:T(8,128)} copy(f32[128,32]{1,0:T(8,128)} %get-tuple-element.28) | data formatting | bytes 32768 | tf_op jit(solution)/shard_map/exp | solution.py:158
  63.9 1.5 %copy.106 = f32[128,32]{0,1:T(8,128)} copy(f32[128,32]{1,0:T(8,128)} %get-tuple-element.27) | data formatting | bytes 32768 | tf_op jit(solution)/shard_map/exp | solution.py:158
  65.4 1.5 %copy.107 = f32[128,32]{0,1:T(8,128)} copy(f32[128,32]{1,0:T(8,128)} %get-tuple-element.26) | data formatting | bytes 32768 | tf_op jit(solution)/shard_map/exp | solution.py:158
  66.9 1.0 copy.100
  67.9 5.4 %copy.98 = f32[4,128,2048]{1,2,0:T(8,128)} copy(f32[4,128,2048]{2,1,0:T(8,128)} %slice_convert_fusion) | data formatting | bytes 8388608 | tf_op jit(solution)/shard_map/convert_element_type | solution.py:132
  73.3 0.9 copy.101
  74.4 2.9 %fusion.4 = f32[4,32,64,128]{3,2,1,0:T(8,128)S(1)} fusion(f32[4,128,32,64]{1,3,2,0:T(8,128)} %bitcast.194, f32[4,128,32]{1,2,0:T(8,128)S(1)} %copy.100, bf16[4,128,2304]{2,1,0:T(8,128)(2,1)S(1)} %bitcast.196), kind=kOutput, calls=%fused_computation.10 | convolution fusion | flops 270532608 | bytes 8585216 | tf_op jit(solution)/shard_map/bthp,btn->bhpn/dot_general | solution.py:133
  77.9 1.3 copy-done.1
  79.3 1.3 convolution_bitcast_fusion
  80.6 1.9 %collective-permute-done.3 = f32[128,2048]{0,1:T(8,128)} collective-permute-done((f32[128,2048]{0,1:T(8,128)}, f32[128,2048]{0,1:T(8,128)}, u32[]{:S(2)}, u32[]{:S(2)}) %collective-permute-start.3) | collective-permute-done | bytes 1048608 | tf_op jit(solution)/shard_map/ppermute | solution.py:148
  82.5 2.2 %fusion.21 = (bf16[128,2048]{0,1:T(8,128)(2,1)S(1)}, bf16[128,2048]{0,1:T(8,128)(2,1)S(1)}, bf16[128,2048]{0,1:T(8,128)(2,1)S(1)}) fusion(f32[128,2048]{0,1:T(8,128)} %collective-permute-done, f32[128,32]{0,1:T(8,128)S(1)} %copy-done.10, f32[128,32]{0,1:T(8,128)S(1)} %copy-done.8, f32[128,2048]{0,1:T(8,128)} %collective-permute-done.1, ...), kind=kLoop, calls=%fused_computation.50 | loop fusion | flops 2359296 | bytes 5816322 | tf_op jit(solution)/shard_map/convert_element_type | solution.py:158
  85.7 1.1 fusion.14
  87.8 1.3 collective-permute-start.4
  89.1 1.6 %collective-permute-done.4 = f32[1152,128]{1,0:T(8,128)S(1)} collective-permute-done((f32[1152,128]{1,0:T(8,128)S(1)}, f32[1152,128]{1,0:T(8,128)S(1)}, u32[]{:S(2)}, u32[]{:S(2)}) %collective-permute-start.4) | collective-permute-done | bytes 589856 | tf_op jit(solution)/shard_map/ppermute | solution.py:26
  90.9 2.3 %collective-permute-start.5 = (f32[288,128]{1,0:T(8,128)S(1)}, f32[288,128]{1,0:T(8,128)S(1)}, u32[]{:S(2)}, u32[]{:S(2)}) collective-permute-start(f32[288,128]{1,0:T(8,128)S(1)} %get-tuple-element.23), channel_id=1, source_target_pairs={{0,8},{8,0},{16,24},{24,16},{1,9},{9,1},{17,25},{25,17},{2,10},{10... | collective-permute-start | bytes 442376 | tf_op jit(solution)/shard_map/ppermute | solution.py:26
  93.1 1.3 collective-permute-start.7
  94.4 2.7 %collective-permute-done.5 = f32[288,128]{1,0:T(8,128)S(1)} collective-permute-done((f32[288,128]{1,0:T(8,128)S(1)}, f32[288,128]{1,0:T(8,128)S(1)}, u32[]{:S(2)}, u32[]{:S(2)}) %collective-permute-start.5) | collective-permute-done | bytes 147488 | tf_op jit(solution)/shard_map/ppermute | solution.py:26
  97.1 4.1 %collective-permute-done.6 = f32[288,128]{1,0:T(8,128)S(1)} collective-permute-done((f32[288,128]{1,0:T(8,128)S(1)}, f32[288,128]{1,0:T(8,128)S(1)}, u32[]{:S(2)}, u32[]{:S(2)}) %collective-permute-start.6) | collective-permute-done | bytes 147488 | tf_op jit(solution)/shard_map/ppermute | solution.py:26
  101.2 4.2 %collective-permute-start.10 = (f32[72,128]{1,0:T(8,128)S(1)}, f32[72,128]{1,0:T(8,128)S(1)}, u32[]{:S(2)}, u32[]{:S(2)}) collective-permute-start(f32[72,128]{1,0:T(8,128)S(1)} %get-tuple-element.36), channel_id=1, source_target_pairs={{0,6},{1,7},{2,4},{3,5},{4,2},{5,3},{6,0},{7,1},{8,14},{9,15},{10,... | collective-permute-start | bytes 110600 | tf_op jit(solution)/shard_map/ppermute | solution.py:26
  105.8 1.0 collective-permute-done.10
  106.8 1.9 %collective-permute-done.8 = f32[72,128]{1,0:T(8,128)S(1)} collective-permute-done((f32[72,128]{1,0:T(8,128)S(1)}, f32[72,128]{1,0:T(8,128)S(1)}, u32[]{:S(2)}, u32[]{:S(2)}) %collective-permute-start.8) | collective-permute-done | bytes 36896 | tf_op jit(solution)/shard_map/ppermute | solution.py:26
  109.2 1.5 %collective-permute-start.11 = (f32[72,128]{1,0:T(8,128)S(1)}, f32[72,128]{1,0:T(8,128)S(1)}, u32[]{:S(2)}, u32[]{:S(2)}) collective-permute-start(f32[72,128]{1,0:T(8,128)S(1)} %add_add_fusion.1), channel_id=1, source_target_pairs={{0,2},{1,3},{2,0},{3,1},{4,6},{5,7},{6,4},{7,5},{8,10},{9,11},{10,... | collective-permute-start | bytes 110600 | tf_op jit(solution)/shard_map/ppermute | solution.py:26
  111.5 1.3 collective-permute-start.13
  112.8 1.7 %collective-permute-done.12 = f32[72,128]{1,0:T(8,128)S(1)} collective-permute-done((f32[72,128]{1,0:T(8,128)S(1)}, f32[72,128]{1,0:T(8,128)S(1)}, u32[]{:S(2)}, u32[]{:S(2)}) %collective-permute-start.12) | collective-permute-done | bytes 36896 | tf_op jit(solution)/shard_map/ppermute | solution.py:26
  114.6 1.6 %collective-permute-done.13 = f32[72,128]{1,0:T(8,128)S(1)} collective-permute-done((f32[72,128]{1,0:T(8,128)S(1)}, f32[72,128]{1,0:T(8,128)S(1)}, u32[]{:S(2)}, u32[]{:S(2)}) %collective-permute-start.13) | collective-permute-done | bytes 36896 | tf_op jit(solution)/shard_map/ppermute | solution.py:26
  116.4 1.1 collective-permute-start.15
  117.5 1.5 %collective-permute-start.16 = (f32[288,128]{1,0:T(8,128)S(1)}, f32[288,128]{1,0:T(8,128)S(1)}, u32[]{:S(2)}, u32[]{:S(2)}) collective-permute-start(f32[288,128]{1,0:T(8,128)S(1)} %get-tuple-element.30), channel_id=1, source_target_pairs={{0,24},{8,16},{16,8},{24,0},{1,25},{9,17},{17,9},{25,1},{2,26},{10... | collective-permute-start | bytes 442376 | tf_op jit(solution)/shard_map/ppermute | solution.py:26
  119.0 1.3 collective-permute-done.14
  120.4 2.0 %collective-permute-done.16 = f32[288,128]{1,0:T(8,128)S(1)} collective-permute-done((f32[288,128]{1,0:T(8,128)S(1)}, f32[288,128]{1,0:T(8,128)S(1)}, u32[]{:S(2)}, u32[]{:S(2)}) %collective-permute-start.16) | collective-permute-done | bytes 147488 | tf_op jit(solution)/shard_map/ppermute | solution.py:26
  122.6 5.9 %collective-permute-start.17 = (f32[1152,128]{1,0:T(8,128)S(1)}, f32[1152,128]{1,0:T(8,128)S(1)}, u32[]{:S(2)}, u32[]{:S(2)}) collective-permute-start(f32[1152,128]{1,0:T(8,128)S(1)} %get-tuple-element.17), channel_id=1, source_target_pairs={{0,1},{1,0},{2,3},{3,2},{4,5},{5,4},{6,7},{7,6},{8,9},{9,8},{10,11... | collective-permute-start | bytes 1769480 | tf_op jit(solution)/shard_map/ppermute | solution.py:26
  128.5 1.3 convolution_bitcast_fusion.1
  129.8 2.4 %fusion.12 = bf16[128,32,64]{0,2,1:T(8,128)(2,1)S(1)} fusion(f32[128,32,64]{0,2,1:T(8,128)S(1)} %convolution_bitcast_fusion.1, f32[4,32,64,128]{3,2,1,0:T(8,128)} %copy-done.1, f32[128,32]{0,1:T(8,128)S(1)} %copy.101, f32[32]{0:T(128)S(1)} %copy-done.32, f32[32]{0:T(128)S(1)} %copy-done.30, f32[32]{0:T(128)S(1)} %copy-done.27, pred[]{:T(512)S(6)} %gt.24, ...), kind=kOutput, calls=%fused_computation.35 | convolution fusion | flops 70254592 | bytes 4768131 | tf_op jit(solution)/shard_map/tn,hpn->thp/dot_general | solution.py:176
  132.2 1.0 copy.109
  133.6 1.4 %copy.110 = f32[128,2304]{1,0:T(8,128)} copy(f32[128,2304]{0,1:T(8,128)S(1)} %fusion.15) | data formatting | bytes 2359296
  (157 shorter events, 17.1 us)
Async XLA Ops:
  0.6 42.2 %copy-start = (bf16[128,2304]{1,0:T(8,128)(2,1)S(1)}, bf16[128,2304]{1,0:T(8,128)(2,1)}, u32[]{:S(2)}) copy-start(bf16[128,2304]{1,0:T(8,128)(2,1)} %param.11) | copy-start | bytes 1769476
  0.6 5.0 %copy-start.34 = (s32[8]{0:T(128)S(1)}, s32[8]{0:T(128)}, u32[]{:S(2)}) copy-start(s32[8]{0:T(128)} %param.9) | copy-start | bytes 100
  0.7 5.1 %copy-start.6 = (s32[8,16]{1,0:T(8,128)S(1)}, s32[8,16]{1,0:T(8,128)}, u32[]{:S(2)}) copy-start(s32[8,16]{1,0:T(8,128)} %param.8) | copy-start | bytes 1540
  0.7 17.6 %copy-start.15 = (s32[4096]{0:T(1024)S(1)}, s32[4096]{0:T(1024)}, u32[]{:S(2)}) copy-start(s32[4096]{0:T(1024)} %param.10) | copy-start | bytes 49156
  3.1 50.5 %collective-permute-start = (f32[128,2048]{0,1:T(8,128)}, f32[128,2048]{0,1:T(8,128)}, u32[]{:S(2)}, u32[]{:S(2)}) collective-permute-start(f32[128,2048]{0,1:T(8,128)} %convert_bitcast_fusion), channel_id=1, source_target_pairs={{24,16},{8,0},{25,17},{9,1},{26,18},{10,2},{27,19},{11,3},{28,20},... | collective-permute-start | bytes 3145736 | tf_op jit(solution)/shard_map/ppermute | solution.py:146
  4.4 50.5 %collective-permute-start.1 = (f32[128,2048]{0,1:T(8,128)}, f32[128,2048]{0,1:T(8,128)}, u32[]{:S(2)}, u32[]{:S(2)}) collective-permute-start(f32[128,2048]{0,1:T(8,128)} %convert_bitcast_fusion), channel_id=1, source_target_pairs={{24,8},{16,0},{25,9},{17,1},{26,10},{18,2},{27,11},{19,3},{28,12},... | collective-permute-start | bytes 3145736 | tf_op jit(solution)/shard_map/ppermute | solution.py:147
  7.0 25.0 %all-to-all-start = ((f32[32,1,16]{2,1,0:T(1,128)}), f32[32,1,16]{2,1,0:T(1,128)S(1)}, u32[]{:S(2)}, u32[]{:S(2)}) async-start(f32[32,1,16]{2,1,0:T(1,128)} %bitcast), calls=%async_computation | async-start | bytes 32768 | tf_op jit(solution)/shard_map/all_to_all | solution.py:92
  18.3 26.4 %copy-start.18 = (pred[128,128]{0,1:T(8,128)(4,1)}, pred[128,128]{0,1:T(8,128)(4,1)S(1)}, u32[]{:S(2)}) copy-start(pred[128,128]{0,1:T(8,128)(4,1)S(1)} %iota_compare_fusion) | copy-start | bytes 49156
  18.5 31.0 %copy-start.21 = (f32[128]{0:T(128)}, f32[128]{0:T(128)S(1)}, u32[]{:S(2)}) copy-start(f32[128]{0:T(128)S(1)} %add_multiply_fusion) | copy-start | bytes 1540
  35.5 4.2 %copy-start.33 = (bf16[128,32]{0,1:T(8,128)(2,1)S(1)}, bf16[128,32]{0,1:T(8,128)(2,1)}, u32[]{:S(2)}) copy-start(bf16[128,32]{0,1:T(8,128)(2,1)} %param.12) | copy-start | bytes 24580
  35.5 4.2 %copy-start.35 = (f32[32]{0:T(128)S(1)}, f32[32]{0:T(128)}, u32[]{:S(2)}) copy-start(f32[32]{0:T(128)} %param.13) | copy-start | bytes 388
  35.5 5.5 %copy-start.23 = (f32[32]{0:T(128)S(1)}, f32[32]{0:T(128)}, u32[]{:S(2)}) copy-start(f32[32]{0:T(128)} %param.14) | copy-start | bytes 388
  42.0 2.4 %copy-start.24 = (f32[1,128]{1,0:T(1,128)}, f32[1,128]{1,0:T(1,128)S(1)}, u32[]{:S(2)}) copy-start(f32[1,128]{1,0:T(1,128)S(1)} %constant_dynamic-slice_fusion.7) | copy-start | bytes 1540
  42.4 3.9 %copy-start.36 = (f32[32,128]{1,0:T(8,128)}, f32[32,128]{1,0:T(8,128)S(1)}, u32[]{:S(2)}) copy-start(f32[32,128]{1,0:T(8,128)S(1)} %get-tuple-element.44) | copy-start | bytes 49156
  43.4 3.7 %copy-start.2 = (bf16[128,2304]{1,0:T(8,128)(2,1)}, bf16[128,2304]{1,0:T(8,128)(2,1)S(1)}, u32[]{:S(2)}) copy-start(bf16[128,2304]{1,0:T(8,128)(2,1)S(1)} %convolution_convert_fusion.1) | copy-start | bytes 1769476
  44.4 1.9 %copy-start.16 = (f32[32,128]{1,0:T(8,128)}, f32[32,128]{1,0:T(8,128)S(1)}, u32[]{:S(2)}) copy-start(f32[32,128]{1,0:T(8,128)S(1)} %copy.94) | copy-start | bytes 49156
  53.6 27.0 %collective-permute-start.2 = (f32[128,2048]{0,1:T(8,128)}, f32[128,2048]{0,1:T(8,128)}, u32[]{:S(2)}, u32[]{:S(2)}) collective-permute-start(f32[128,2048]{0,1:T(8,128)} %collective-permute-done), channel_id=1, source_target_pairs={{16,0},{17,1},{18,2},{19,3},{20,4},{21,5},{22,6},{23,7}} | collective-permute-start | bytes 3145736 | tf_op jit(solution)/shard_map/ppermute | solution.py:149
  54.9 27.6 %collective-permute-start.3 = (f32[128,2048]{0,1:T(8,128)}, f32[128,2048]{0,1:T(8,128)}, u32[]{:S(2)}, u32[]{:S(2)}) collective-permute-start(f32[128,2048]{0,1:T(8,128)} %collective-permute-done.1), channel_id=1, source_target_pairs={{0,8},{1,9},{2,10},{3,11},{4,12},{5,13},{6,14},{7,15}} | collective-permute-start | bytes 3145736 | tf_op jit(solution)/shard_map/ppermute | solution.py:148
  74.3 2.9 %copy-start.14 = (f32[128,128]{0,1:T(8,128)S(1)}, f32[128,128]{0,1:T(8,128)}, u32[]{:S(2)}) copy-start(f32[128,128]{0,1:T(8,128)} %fusion.74) | copy-start | bytes 196612
  74.3 2.9 %copy-start.26 = (f32[32]{0:T(128)S(1)}, f32[32]{0:T(128)}, u32[]{:S(2)}) copy-start(f32[32]{0:T(128)} %get-tuple-element.43) | copy-start | bytes 388
  74.3 2.9 %copy-start.29 = (f32[32]{0:T(128)S(1)}, f32[32]{0:T(128)}, u32[]{:S(2)}) copy-start(f32[32]{0:T(128)} %get-tuple-element.42) | copy-start | bytes 388
  74.4 2.9 %copy-start.31 = (f32[32]{0:T(128)S(1)}, f32[32]{0:T(128)}, u32[]{:S(2)}) copy-start(f32[32]{0:T(128)} %get-tuple-element.41) | copy-start | bytes 388
  77.2 2.0 %copy-start.1 = (f32[4,32,64,128]{3,2,1,0:T(8,128)}, f32[4,32,64,128]{3,2,1,0:T(8,128)S(1)}, u32[]{:S(2)}) copy-start(f32[4,32,64,128]{3,2,1,0:T(8,128)S(1)} %fusion.4) | copy-start | bytes 12582916
  77.3 1.9 %copy-start.11 = (f32[128,128]{0,1:T(8,128)S(1)}, f32[128,128]{0,1:T(8,128)}, u32[]{:S(2)}) copy-start(f32[128,128]{0,1:T(8,128)} %fusion.77) | copy-start | bytes 196612
  77.3 1.9 %copy-start.17 = (f32[32,128]{1,0:T(8,128)S(1)}, f32[32,128]{1,0:T(8,128)}, u32[]{:S(2)}) copy-start(f32[32,128]{1,0:T(8,128)} %copy-done.16) | copy-start | bytes 49156
  77.3 1.9 %copy-start.19 = (pred[128,128]{0,1:T(8,128)(4,1)S(1)}, pred[128,128]{0,1:T(8,128)(4,1)}, u32[]{:S(2)}) copy-start(pred[128,128]{0,1:T(8,128)(4,1)} %copy-done.18) | copy-start | bytes 49156
  79.2 3.3 %copy-start.8 = (f32[128,32]{0,1:T(8,128)S(1)}, f32[128,32]{0,1:T(8,128)}, u32[]{:S(2)}) copy-start(f32[128,32]{0,1:T(8,128)} %copy.105) | copy-start | bytes 49156
  79.2 3.3 %copy-start.9 = (f32[128,32]{0,1:T(8,128)S(1)}, f32[128,32]{0,1:T(8,128)}, u32[]{:S(2)}) copy-start(f32[128,32]{0,1:T(8,128)} %copy.106) | copy-start | bytes 49156
  79.2 3.2 %copy-start.10 = (f32[128,32]{0,1:T(8,128)S(1)}, f32[128,32]{0,1:T(8,128)}, u32[]{:S(2)}) copy-start(f32[128,32]{0,1:T(8,128)} %copy.107) | copy-start | bytes 49156
  80.6 4.1 %copy-start.28 = (f32[32]{0:T(128)S(1)}, f32[32]{0:T(128)}, u32[]{:S(2)}) copy-start(f32[32]{0:T(128)} %get-tuple-element.40) | copy-start | bytes 388
  87.8 2.9 %collective-permute-start.4 = (f32[1152,128]{1,0:T(8,128)S(1)}, f32[1152,128]{1,0:T(8,128)S(1)}, u32[]{:S(2)}, u32[]{:S(2)}) collective-permute-start(f32[1152,128]{1,0:T(8,128)S(1)} %constant_dynamic-slice_fusion.6), channel_id=1, source_target_pairs={{0,1},{1,0},{2,3},{3,2},{4,5},{5,4},{6,7},{7,6},{8,9},{9,8},{10,11... | collective-permute-start | bytes 1769480 | tf_op jit(solution)/shard_map/ppermute | solution.py:26
  90.9 6.2 %collective-permute-start.5 = (f32[288,128]{1,0:T(8,128)S(1)}, f32[288,128]{1,0:T(8,128)S(1)}, u32[]{:S(2)}, u32[]{:S(2)}) collective-permute-start(f32[288,128]{1,0:T(8,128)S(1)} %get-tuple-element.23), channel_id=1, source_target_pairs={{0,8},{8,0},{16,24},{24,16},{1,9},{9,1},{17,25},{25,17},{2,10},{10... | collective-permute-start | bytes 442376 | tf_op jit(solution)/shard_map/ppermute | solution.py:26
  93.1 8.0 %collective-permute-start.6 = (f32[288,128]{1,0:T(8,128)S(1)}, f32[288,128]{1,0:T(8,128)S(1)}, u32[]{:S(2)}, u32[]{:S(2)}) collective-permute-start(f32[288,128]{1,0:T(8,128)S(1)} %get-tuple-element.25), channel_id=1, source_target_pairs={{0,16},{8,24},{16,0},{24,8},{1,17},{9,25},{17,1},{25,9},{2,18},{10... | collective-permute-start | bytes 442376 | tf_op jit(solution)/shard_map/ppermute | solution.py:26
  93.1 8.0 %collective-permute-start.7 = (f32[288,128]{1,0:T(8,128)S(1)}, f32[288,128]{1,0:T(8,128)S(1)}, u32[]{:S(2)}, u32[]{:S(2)}) collective-permute-start(f32[288,128]{1,0:T(8,128)S(1)} %get-tuple-element.24), channel_id=1, source_target_pairs={{0,24},{8,16},{16,8},{24,0},{1,25},{9,17},{17,9},{25,1},{2,26},{10... | collective-permute-start | bytes 442376 | tf_op jit(solution)/shard_map/ppermute | solution.py:26
  101.2 5.6 %collective-permute-start.10 = (f32[72,128]{1,0:T(8,128)S(1)}, f32[72,128]{1,0:T(8,128)S(1)}, u32[]{:S(2)}, u32[]{:S(2)}) collective-permute-start(f32[72,128]{1,0:T(8,128)S(1)} %get-tuple-element.36), channel_id=1, source_target_pairs={{0,6},{1,7},{2,4},{3,5},{4,2},{5,3},{6,0},{7,1},{8,14},{9,15},{10,... | collective-permute-start | bytes 110600 | tf_op jit(solution)/shard_map/ppermute | solution.py:26
  105.4 3.2 %collective-permute-start.8 = (f32[72,128]{1,0:T(8,128)S(1)}, f32[72,128]{1,0:T(8,128)S(1)}, u32[]{:S(2)}, u32[]{:S(2)}) collective-permute-start(f32[72,128]{1,0:T(8,128)S(1)} %get-tuple-element.35), channel_id=1, source_target_pairs={{0,2},{1,3},{2,0},{3,1},{4,6},{5,7},{6,4},{7,5},{8,10},{9,11},{10,... | collective-permute-start | bytes 110600 | tf_op jit(solution)/shard_map/ppermute | solution.py:26
  105.4 3.7 %collective-permute-start.9 = (f32[72,128]{1,0:T(8,128)S(1)}, f32[72,128]{1,0:T(8,128)S(1)}, u32[]{:S(2)}, u32[]{:S(2)}) collective-permute-start(f32[72,128]{1,0:T(8,128)S(1)} %get-tuple-element.37), channel_id=1, source_target_pairs={{0,4},{1,5},{2,6},{3,7},{4,0},{5,1},{6,2},{7,3},{8,12},{9,13},{10,... | collective-permute-start | bytes 110600 | tf_op jit(solution)/shard_map/ppermute | solution.py:26
  109.2 3.7 %collective-permute-start.11 = (f32[72,128]{1,0:T(8,128)S(1)}, f32[72,128]{1,0:T(8,128)S(1)}, u32[]{:S(2)}, u32[]{:S(2)}) collective-permute-start(f32[72,128]{1,0:T(8,128)S(1)} %add_add_fusion.1), channel_id=1, source_target_pairs={{0,2},{1,3},{2,0},{3,1},{4,6},{5,7},{6,4},{7,5},{8,10},{9,11},{10,... | collective-permute-start | bytes 110600 | tf_op jit(solution)/shard_map/ppermute | solution.py:26
  110.7 3.9 %collective-permute-start.12 = (f32[72,128]{1,0:T(8,128)S(1)}, f32[72,128]{1,0:T(8,128)S(1)}, u32[]{:S(2)}, u32[]{:S(2)}) collective-permute-start(f32[72,128]{1,0:T(8,128)S(1)} %add_add_fusion.1), channel_id=1, source_target_pairs={{0,4},{1,5},{2,6},{3,7},{4,0},{5,1},{6,2},{7,3},{8,12},{9,13},{10,... | collective-permute-start | bytes 110600 | tf_op jit(solution)/shard_map/ppermute | solution.py:26
  111.5 4.6 %collective-permute-start.13 = (f32[72,128]{1,0:T(8,128)S(1)}, f32[72,128]{1,0:T(8,128)S(1)}, u32[]{:S(2)}, u32[]{:S(2)}) collective-permute-start(f32[72,128]{1,0:T(8,128)S(1)} %add_add_fusion.1), channel_id=1, source_target_pairs={{0,6},{1,7},{2,4},{3,5},{4,2},{5,3},{6,0},{7,1},{8,14},{9,15},{10,... | collective-permute-start | bytes 110600 | tf_op jit(solution)/shard_map/ppermute | solution.py:26
  116.2 12.2 %copy-start.5 = (bf16[128,2048]{0,1:T(8,128)(2,1)S(1)}, bf16[128,2048]{0,1:T(8,128)(2,1)}, u32[]{:S(2)}) copy-start(bf16[128,2048]{0,1:T(8,128)(2,1)} %copy-done.3) | copy-start | bytes 1572868
  116.2 12.2 %copy-start.12 = (f32[128,128]{0,1:T(8,128)S(1)}, f32[128,128]{0,1:T(8,128)}, u32[]{:S(2)}) copy-start(f32[128,128]{0,1:T(8,128)} %fusion.77) | copy-start | bytes 196612
  116.2 12.2 %copy-start.20 = (pred[128,128]{0,1:T(8,128)(4,1)S(1)}, pred[128,128]{0,1:T(8,128)(4,1)}, u32[]{:S(2)}) copy-start(pred[128,128]{0,1:T(8,128)(4,1)} %copy-done.18) | copy-start | bytes 49156
  116.3 12.2 %copy-start.38 = (f32[32,128]{1,0:T(8,128)S(1)}, f32[32,128]{1,0:T(8,128)}, u32[]{:S(2)}) copy-start(f32[32,128]{1,0:T(8,128)} %copy-done.36) | copy-start | bytes 49156
  116.3 4.1 %collective-permute-start.14 = (f32[288,128]{1,0:T(8,128)S(1)}, f32[288,128]{1,0:T(8,128)S(1)}, u32[]{:S(2)}, u32[]{:S(2)}) collective-permute-start(f32[288,128]{1,0:T(8,128)S(1)} %get-tuple-element.30), channel_id=1, source_target_pairs={{0,8},{8,0},{16,24},{24,16},{1,9},{9,1},{17,25},{25,17},{2,10},{10... | collective-permute-start | bytes 442376 | tf_op jit(solution)/shard_map/ppermute | solution.py:26
  116.4 4.0 %collective-permute-start.15 = (f32[288,128]{1,0:T(8,128)S(1)}, f32[288,128]{1,0:T(8,128)S(1)}, u32[]{:S(2)}, u32[]{:S(2)}) collective-permute-start(f32[288,128]{1,0:T(8,128)S(1)} %get-tuple-element.30), channel_id=1, source_target_pairs={{0,16},{8,24},{16,0},{24,8},{1,17},{9,25},{17,1},{25,9},{2,18},{10... | collective-permute-start | bytes 442376 | tf_op jit(solution)/shard_map/ppermute | solution.py:26
  117.5 4.9 %collective-permute-start.16 = (f32[288,128]{1,0:T(8,128)S(1)}, f32[288,128]{1,0:T(8,128)S(1)}, u32[]{:S(2)}, u32[]{:S(2)}) collective-permute-start(f32[288,128]{1,0:T(8,128)S(1)} %get-tuple-element.30), channel_id=1, source_target_pairs={{0,24},{8,16},{16,8},{24,0},{1,25},{9,17},{17,9},{25,1},{2,26},{10... | collective-permute-start | bytes 442376 | tf_op jit(solution)/shard_map/ppermute | solution.py:26
  122.6 10.6 %collective-permute-start.17 = (f32[1152,128]{1,0:T(8,128)S(1)}, f32[1152,128]{1,0:T(8,128)S(1)}, u32[]{:S(2)}, u32[]{:S(2)}) collective-permute-start(f32[1152,128]{1,0:T(8,128)S(1)} %get-tuple-element.17), channel_id=1, source_target_pairs={{0,1},{1,0},{2,3},{3,2},{4,5},{5,4},{6,7},{7,6},{8,9},{9,8},{10,11... | collective-permute-start | bytes 1769480 | tf_op jit(solution)/shard_map/ppermute | solution.py:26
  (10 other events, 14.1 us)

commit v9 on v8

--- a/solution.py
+++ b/solution.py
@@ -142,15 +142,17 @@
     adjoint_local = jnp.einsum("thp,tn->hpn", grad_weighted, c_proj, preferred_element_type=fl)
     adjoint_in = jnp.zeros((head_count, head_dim, state_dim), fl)
     if n_blocks == 4:
-        sent = grad_out[0].astype(fl)
-        first = lax.ppermute(sent, "tm", [(3, 2), (1, 0)])
+        sent, reading = lax.optimization_barrier((grad_out[0].astype(fl), reading))
+        half_rows = tok_rows // 2
+        first = lax.ppermute(sent, "tm", [(3, 2), (1, 0), (2, 3)])
         second = lax.ppermute(sent, "tm", [(3, 1), (2, 0)])
-        third = lax.ppermute(second, "tm", [(0, 1)])
-        fourth = lax.ppermute(first, "tm", [(2, 0)])
+        third = lax.ppermute(second[:half_rows], "tm", [(0, 1), (1, 0)])
+        fourth = lax.ppermute(first[half_rows:], "tm", [(3, 1), (2, 0)])
+        joined = jnp.concatenate([third, fourth])
         seen = [
             first,
-            jnp.where(my_block == 1, third, second),
-            jnp.where(my_block == 2, first, jnp.where(my_block == 1, second, fourth)),
+            jnp.where(my_block == 1, joined, second),
+            jnp.where(my_block == 2, first, jnp.where(my_block == 1, second, joined)),
         ]
         c_all = projected_all[:, :, inner_width + state_dim :]
         for k in range(n_blocks - 1, 0, -1):

time: 136 us -> 166 us (1.22)
  local copies, waits for them, and re-layouts: 21.5 us -> 39.3 us
  matrix products: 23.2 us -> 31.6 us
  other arithmetic: 11.9 us -> 16.4 us
  starting transfers between devices: 43 us -> 39.3 us
  waiting for transfers between devices: 33.9 us -> 37 us
    slice x1 -> x4, local copies, waits for them, and re-layouts: 0.08 us -> 7.35 us  [the longest x2 4.93 us: on_device(): fourth = lax.ppermute(first[half_rows:], 'tm', [(3, 1), (2, 0)])]
    ppermute x0 -> x2, local copies, waits for them, and re-layouts: none -> 4.72 us  [the longest x1 2.36 us: on_device(): third = lax.ppermute(second[:half_rows], 'tm', [(0, 1), (1, 0)])]
    slice x2, local copies, waits for them, and re-layouts: 0.33 us -> 3.93 us  [on_device(): x_heads = projected[:, :inner_width].reshape(tok_rows, head_count, head_dim)]
    ppermute x3, starting transfers between devices: 8.77 us -> 5.86 us  [the longest x1 3.11 us: on_device(): third = lax.ppermute(second[:half_rows], 'tm', [(0, 1), (1, 0)])]
    dot_general x1, matrix products: 0.6 us -> 3.23 us  [on_device(): jnp.einsum('thp,hpn->tn', grad_weighted, state_half, preferred_element_ty...]
    ppermute x3, waiting for transfers between devices: 1.9 us -> 4.1 us  [the longest x1 2.62 us: on_device(): fourth = lax.ppermute(first[half_rows:], 'tm', [(3, 1), (2, 0)])]
    unnamed x81 -> x79, local copies, waits for them, and re-layouts: 5.32 us -> 4.56 us
  transfers between devices with their start and end apart: 19 -> 19, of which waited for: 13 -> 14; matrix products, arithmetic and copies ran while one was open for 34% -> 45% of each run, Pallas kernels for 0% -> 0%
where the time goes in v9:
time: 166 us; the launch traced here: 165 us
  local copies, waits for them, and re-layouts  39.3 us (24%)
  starting transfers between devices  39.3 us (24%)
  waiting for transfers between devices  37 us (22%)
  matrix products  31.6 us (19%)
  other arithmetic  16.4 us (10%)
    ppermute x14, starting transfers between devices, exchange(): return lax.ppermute(value, axis, pairs)  20.9 us
    ppermute x14, waiting for transfers between devices, exchange(): return lax.ppermute(value, axis, pairs)  18.3 us
    all_to_all x1, waiting for transfers between devices, on_device(): lax.all_to_all(outgoing, ('tm', 'series'), split_axis=0, concat_axis=1, t...  14.7 us
    all_to_all x1, starting transfers between devices, on_device(): lax.all_to_all(outgoing, ('tm', 'series'), split_axis=0, concat_axis=1, t...  11.3 us
    convert_element_type x1, local copies, waits for them, and re-layouts, on_device(): xw_all = (x_all * tail_all[..., None]).astype(half)  5.33 us
    exp x4, local copies, waits for them, and re-layouts, on_device(): later_weighted = (later * jnp.exp(cum_all[k])[:, :, None]).astype(half)  5.29 us
    slice x2, local copies, waits for them, and re-layouts, on_device(): fourth = lax.ppermute(first[half_rows:], 'tm', [(3, 1), (2, 0)])  4.93 us
    unnamed x79, local copies, waits for them, and re-layouts  4.56 us
  transfers between devices with their start and end apart: 19, of which 14 were waited for; matrix products, arithmetic and copies ran while one was open for 45% of the time, Pallas kernels for 0%

profile of v9, /device:TPU:1, one launch (start us, length us, event | category | flops | bytes accessed | tf_op | source)
XLA Modules:
  0.0 164.9 jit_solution(8979256153117923339)
XLA Ops:
  0.7 1.4 copy.106
  7.0 11.3 %all-to-all-start = ((f32[32,1,16]{2,1,0:T(1,128)}), f32[32,1,16]{2,1,0:T(1,128)S(1)}, u32[]{:S(2)}, u32[]{:S(2)}) async-start(f32[32,1,16]{2,1,0:T(1,128)} %bitcast), calls=%async_computation | async-start | bytes 32768 | tf_op jit(solution)/shard_map/all_to_all | solution.py:92
  19.1 14.7 %all-to-all-done = f32[32,1,16]{2,1,0:T(1,128)S(1)} async-done(((f32[32,1,16]{2,1,0:T(1,128)}), f32[32,1,16]{2,1,0:T(1,128)S(1)}, u32[]{:S(2)}, u32[]{:S(2)}) %all-to-all-start) | async-done | bytes 2080 | tf_op jit(solution)/shard_map/all_to_all | solution.py:92
  35.0 1.5 convert_reduce_fusion
  37.2 4.1 %fusion = f32[512,4]{0,1:T(4,128)S(1)} fusion(f32[4096]{0:T(1024)S(1)} %get-tuple-element.39, f32[4096]{0:T(1024)S(1)} %convert_element_type.117, f32[512]{0:T(512)S(1)} %le.22, f32[4096,1]{0,1:T(1,128)S(1)} %bitcast.231, f32[4096,1]{0,1:T(1,128)S(1)} %bitcast.223, f32[4096,1]{0,1:T(1,128)S(1)} %bitcast.222, f32[4096,1]{0,1:T(1,128)S(1)} %sub.69), kind=kOutput, calls=%fused_computation.3 | convolution fusion | flops 107003904 | bytes 108544 | tf_op jit(solution)/shard_map/dot_general | solution.py:101
  43.8 1.6 convolution_convert_fusion
  46.5 1.4 convolution_convert_fusion.1
  50.9 1.6 fusion.77
  52.4 1.9 %slice.133 = bf16[128,2048]{1,0:T(8,128)(2,1)} slice(bf16[128,2304]{1,0:T(8,128)(2,1)} %convolution_convert_fusion.1), slice={[0:128], [0:2048]} | slice | bytes 1048576 | tf_op jit(solution)/shard_map/slice | solution.py:113
  54.9 1.8 %exponential_multiply_fusion = f32[4,128,32]{2,1,0:T(8,128)} fusion(f32[4,128,32]{2,1,0:T(8,128)} %bitcast.204, f32[4,128,32]{2,1,0:T(8,128)} %copy-done.3, f32[4,32]{1,0:T(4,128)S(1)} %bitcast.230), kind=kLoop, calls=%fused_computation.87 | loop fusion | flops 32768 | bytes 197120 | tf_op jit(solution)/shard_map/mul | solution.py:131
  57.3 1.5 copy.113
  58.8 1.5 copy.114
  60.3 1.5 copy.115
  62.5 2.0 %copy.95 = bf16[128,2048]{0,1:T(8,128)(2,1)} copy(bf16[128,2048]{1,0:T(8,128)(2,1)} %slice.133) | data formatting | bytes 1048576 | tf_op jit(solution)/shard_map/slice | solution.py:113
  65.6 2.6 %slice_convert_fusion = f32[4,128,2048]{2,1,0:T(8,128)} fusion(bf16[4,128,2304]{2,1,0:T(8,128)(2,1)S(1)} %bitcast.196), kind=kLoop, calls=%fused_computation.11 | loop fusion | flops 1048576 | bytes 6291456 | tf_op jit(solution)/shard_map/convert_element_type | solution.py:132
  68.2 5.3 %copy.102 = f32[4,128,2048]{1,2,0:T(8,128)} copy(f32[4,128,2048]{2,1,0:T(8,128)} %slice_convert_fusion) | data formatting | bytes 8388608 | tf_op jit(solution)/shard_map/convert_element_type | solution.py:132
  75.4 1.4 exponential_multiply_fusion.1
  76.8 2.7 %fusion.5 = bf16[128,128]{0,1:T(8,128)(2,1)S(1)} fusion(bf16[128,32,64]{0,2,1:T(8,128)(2,1)} %bitcast.211, bf16[128,32,64]{0,2,1:T(8,128)(2,1)S(1)} %bitcast.201, f32[32,128]{1,0:T(8,128)} %get-tuple-element.44, f32[32,128]{1,0:T(8,128)} %copy.98, pred[128,128]{0,1:T(8,128)(4,1)} %iota_compare_fusion), kind=kOutput, calls=%fused_computation.13 | convolution fusion | flops 70238208 | bytes 1130496 | tf_op jit(solution)/shard_map/thp,shp->hts/dot_general | solution.py:188
  80.1 1.6 fusion.79
  81.7 1.6 fusion.74
  83.3 2.7 %fusion.4 = f32[4,32,64,128]{3,2,1,0:T(8,128)} fusion(f32[4,128,32,64]{1,3,2,0:T(8,128)S(1)} %bitcast.195, f32[4,128,32]{1,2,0:T(8,128)S(1)} %copy.104, bf16[4,128,2304]{2,1,0:T(8,128)(2,1)S(1)} %bitcast.197), kind=kOutput, calls=%fused_computation.10 | convolution fusion | flops 270532608 | bytes 8585216 | tf_op jit(solution)/shard_map/bthp,btn->bhpn/dot_general | solution.py:133
  86.0 2.6 %slice.143 = f32[64,2048]{0,1:T(8,128)} slice(f32[128,2048]{0,1:T(8,128)} %collective-permute-done), slice={[64:128], [0:2048]} | slice | bytes 1048576 | tf_op jit(solution)/shard_map/slice | solution.py:150
  88.6 2.4 %copy.110 = f32[64,2048]{1,0:T(8,128)} copy(f32[64,2048]{0,1:T(8,128)} %slice.143) | data formatting | bytes 1048576 | tf_op jit(solution)/shard_map/slice | solution.py:150
  90.9 1.5 collective-permute-start.3
  92.4 2.3 %copy.109 = f32[64,2048]{1,0:T(8,128)} copy(f32[64,2048]{0,1:T(8,128)} %bitcast.194) | data formatting | bytes 1048576 | tf_op jit(solution)/shard_map/slice | solution.py:149
  94.7 3.1 %collective-permute-start.2 = (f32[64,2048]{1,0:T(8,128)}, f32[64,2048]{1,0:T(8,128)}, u32[]{:S(2)}, u32[]{:S(2)}) collective-permute-start(f32[64,2048]{1,0:T(8,128)} %copy.109), channel_id=1, source_target_pairs={{0,8},{8,0},{1,9},{9,1},{2,10},{10,2},{3,11},{11,3},{4,12},{12,4},... | collective-permute-start | bytes 1572872 | tf_op jit(solution)/shard_map/ppermute | solution.py:149
  97.9 3.2 %fusion.19 = bf16[128,128]{0,1:T(8,128)(2,1)} fusion(f32[128,128]{0,1:T(8,128)} %fusion.74, bf16[128,32,64]{0,2,1:T(8,128)(2,1)} %bitcast.214, f32[4,32,64,128]{3,2,1,0:T(8,128)} %fusion.4, f32[32]{0:T(128)} %get-tuple-element.41, f32[32]{0:T(128)} %get-tuple-element.42, f32[32]{0:T(128)} %get-tuple-element.43, pred[]{:T(512)S(6)} %gt.24, pred[]{:T(512)S(6)} %gt.23, ...), kind=kOutput, calls=%fused_computation.46 | convolution fusion | flops 69500928 | bytes 3769859 | tf_op jit(solution)/shard_map/thp,hpn->tn/dot_general | solution.py:193
  101.2 2.4 %convolution_bitcast_fusion = f32[128,32,64]{0,2,1:T(8,128)} fusion(bf16[128,32,64]{0,2,1:T(8,128)(2,1)S(1)} %bitcast.202, f32[32,128]{1,0:T(8,128)S(1)} %copy-done.36, f32[32,128]{1,0:T(8,128)S(1)} %copy-done.18, f32[128,128]{0,1:T(8,128)S(1)} %copy-done.13, pred[128,128]{0,1:T(8,128)(4,1)S(1)} %copy-done.20), kind=kOutput, calls=%fused_computation.29 | convolution fusion | flops 70254592 | bytes 1687552 | tf_op jit(solution)/shard_map/hts,thp->shp/dot_general | solution.py:182
  103.6 2.6 %collective-permute-done.3 = f32[64,2048]{1,0:T(8,128)} collective-permute-done((f32[64,2048]{1,0:T(8,128)}, f32[64,2048]{1,0:T(8,128)}, u32[]{:S(2)}, u32[]{:S(2)}) %collective-permute-start.3) | collective-permute-done | bytes 524320 | tf_op jit(solution)/shard_map/ppermute | solution.py:150
  106.2 2.4 %copy.112 = f32[64,2048]{0,1:T(8,128)} copy(f32[64,2048]{1,0:T(8,128)} %collective-permute-done.3) | data formatting | bytes 1048576 | tf_op jit(solution)/shard_map/ppermute | solution.py:150
  108.5 1.5 collective-permute-done.2
  110.0 2.4 %copy.111 = f32[64,2048]{0,1:T(8,128)} copy(f32[64,2048]{1,0:T(8,128)} %collective-permute-done.2) | data formatting | bytes 1048576 | tf_op jit(solution)/shard_map/ppermute | solution.py:149
  112.4 2.7 %fusion.22 = (bf16[128,2048]{0,1:T(8,128)(2,1)S(1)}, bf16[128,2048]{0,1:T(8,128)(2,1)S(1)}, bf16[128,2048]{0,1:T(8,128)(2,1)S(1)}) fusion(f32[128,2048]{0,1:T(8,128)} %collective-permute-done.1, f32[128,32]{0,1:T(8,128)S(1)} %copy-done.10, pred[]{:T(512)S(6)} %eq.19, f32[64,2048]{0,1:T(8,128)} %copy.112, f32[64,2048]{0,1:T(8,128)} %copy.111, ...), kind=kLoop, calls=%fused_computation.53 | loop fusion | flops 2621440 | bytes 4767746 | tf_op jit(solution)/shard_map/convert_element_type | solution.py:160
  118.7 1.4 collective-permute-start.4
  120.1 1.6 collective-permute-done.4
  123.1 1.4 collective-permute-start.7
  124.5 2.4 %collective-permute-done.5 = f32[288,128]{1,0:T(8,128)S(1)} collective-permute-done((f32[288,128]{1,0:T(8,128)S(1)}, f32[288,128]{1,0:T(8,128)S(1)}, u32[]{:S(2)}, u32[]{:S(2)}) %collective-permute-start.5) | collective-permute-done | bytes 147488 | tf_op jit(solution)/shard_map/ppermute | solution.py:26
  127.0 4.2 %collective-permute-done.6 = f32[288,128]{1,0:T(8,128)S(1)} collective-permute-done((f32[288,128]{1,0:T(8,128)S(1)}, f32[288,128]{1,0:T(8,128)S(1)}, u32[]{:S(2)}, u32[]{:S(2)}) %collective-permute-start.6) | collective-permute-done | bytes 147488 | tf_op jit(solution)/shard_map/ppermute | solution.py:26
  131.2 4.2 %collective-permute-start.10 = (f32[72,128]{1,0:T(8,128)S(1)}, f32[72,128]{1,0:T(8,128)S(1)}, u32[]{:S(2)}, u32[]{:S(2)}) collective-permute-start(f32[72,128]{1,0:T(8,128)S(1)} %get-tuple-element.36), channel_id=1, source_target_pairs={{0,6},{1,7},{2,4},{3,5},{4,2},{5,3},{6,0},{7,1},{8,14},{9,15},{10,... | collective-permute-start | bytes 110600 | tf_op jit(solution)/shard_map/ppermute | solution.py:26
  136.8 1.9 %collective-permute-done.8 = f32[72,128]{1,0:T(8,128)S(1)} collective-permute-done((f32[72,128]{1,0:T(8,128)S(1)}, f32[72,128]{1,0:T(8,128)S(1)}, u32[]{:S(2)}, u32[]{:S(2)}) %collective-permute-start.8) | collective-permute-done | bytes 36896 | tf_op jit(solution)/shard_map/ppermute | solution.py:26
  139.1 1.5 collective-permute-start.11
  142.8 1.7 %collective-permute-done.12 = f32[72,128]{1,0:T(8,128)S(1)} collective-permute-done((f32[72,128]{1,0:T(8,128)S(1)}, f32[72,128]{1,0:T(8,128)S(1)}, u32[]{:S(2)}, u32[]{:S(2)}) %collective-permute-start.12) | collective-permute-done | bytes 36896 | tf_op jit(solution)/shard_map/ppermute | solution.py:26
  144.6 1.6 collective-permute-done.13
  147.5 1.5 collective-permute-start.16
  150.4 2.0 %collective-permute-done.16 = f32[288,128]{1,0:T(8,128)S(1)} collective-permute-done((f32[288,128]{1,0:T(8,128)S(1)}, f32[288,128]{1,0:T(8,128)S(1)}, u32[]{:S(2)}, u32[]{:S(2)}) %collective-permute-start.16) | collective-permute-done | bytes 147488 | tf_op jit(solution)/shard_map/ppermute | solution.py:26
  152.6 5.9 %collective-permute-start.17 = (f32[1152,128]{1,0:T(8,128)S(1)}, f32[1152,128]{1,0:T(8,128)S(1)}, u32[]{:S(2)}, u32[]{:S(2)}) collective-permute-start(f32[1152,128]{1,0:T(8,128)S(1)} %get-tuple-element.17), channel_id=1, source_target_pairs={{0,1},{1,0},{2,3},{3,2},{4,5},{5,4},{6,7},{7,6},{8,9},{9,8},{10,11... | collective-permute-start | bytes 1769480 | tf_op jit(solution)/shard_map/ppermute | solution.py:26
  159.8 2.4 %fusion.12 = bf16[128,32,64]{0,2,1:T(8,128)(2,1)S(1)} fusion(f32[128,32,64]{0,2,1:T(8,128)S(1)} %convolution_bitcast_fusion.1, f32[4,32,64,128]{3,2,1,0:T(8,128)} %fusion.4, f32[128,32]{0,1:T(8,128)S(1)} %copy.105, f32[32]{0:T(128)S(1)} %copy-done.32, f32[32]{0:T(128)S(1)} %copy-done.31, f32[32]{0:T(128)S(1)} %copy-done.28, pred[]{:T(512)S(6)} %gt.24, ...), kind=kOutput, calls=%fused_computation.35 | convolution fusion | flops 70254592 | bytes 4768131 | tf_op jit(solution)/shard_map/tn,hpn->thp/dot_general | solution.py:178
  163.5 1.4 copy.118
  (160 shorter events, 34.0 us)
Async XLA Ops:
  0.6 43.2 %copy-start = (bf16[128,2304]{1,0:T(8,128)(2,1)S(1)}, bf16[128,2304]{1,0:T(8,128)(2,1)}, u32[]{:S(2)}) copy-start(bf16[128,2304]{1,0:T(8,128)(2,1)} %param.11) | copy-start | bytes 1769476
  0.6 5.0 %copy-start.34 = (s32[8]{0:T(128)S(1)}, s32[8]{0:T(128)}, u32[]{:S(2)}) copy-start(s32[8]{0:T(128)} %param.9) | copy-start | bytes 100
  0.7 5.1 %copy-start.7 = (s32[8,16]{1,0:T(8,128)S(1)}, s32[8,16]{1,0:T(8,128)}, u32[]{:S(2)}) copy-start(s32[8,16]{1,0:T(8,128)} %param.8) | copy-start | bytes 1540
  0.7 18.2 %copy-start.16 = (s32[4096]{0:T(1024)S(1)}, s32[4096]{0:T(1024)}, u32[]{:S(2)}) copy-start(s32[4096]{0:T(1024)} %param.10) | copy-start | bytes 49156
  3.1 82.9 %collective-permute-start = (f32[128,2048]{0,1:T(8,128)}, f32[128,2048]{0,1:T(8,128)}, u32[]{:S(2)}, u32[]{:S(2)}) collective-permute-start(f32[128,2048]{0,1:T(8,128)} %convert_bitcast_fusion), channel_id=1, source_target_pairs={{24,16},{8,0},{16,24},{25,17},{9,1},{17,25},{26,18},{10,2},{18,26}... | collective-permute-start | bytes 3145736 | tf_op jit(solution)/shard_map/ppermute | solution.py:147
  4.4 88.0 %collective-permute-start.1 = (f32[128,2048]{0,1:T(8,128)}, f32[128,2048]{0,1:T(8,128)}, u32[]{:S(2)}, u32[]{:S(2)}) collective-permute-start(f32[128,2048]{0,1:T(8,128)} %convert_bitcast_fusion), channel_id=1, source_target_pairs={{24,8},{16,0},{25,9},{17,1},{26,10},{18,2},{27,11},{19,3},{28,12},... | collective-permute-start | bytes 3145736 | tf_op jit(solution)/shard_map/ppermute | solution.py:148
  7.0 26.7 %all-to-all-start = ((f32[32,1,16]{2,1,0:T(1,128)}), f32[32,1,16]{2,1,0:T(1,128)S(1)}, u32[]{:S(2)}, u32[]{:S(2)}) async-start(f32[32,1,16]{2,1,0:T(1,128)} %bitcast), calls=%async_computation | async-start | bytes 32768 | tf_op jit(solution)/shard_map/all_to_all | solution.py:92
  19.1 27.4 %copy-start.23 = (f32[128]{0:T(128)}, f32[128]{0:T(128)S(1)}, u32[]{:S(2)}) copy-start(f32[128]{0:T(128)S(1)} %add_multiply_fusion) | copy-start | bytes 1540
  37.2 4.2 %copy-start.33 = (bf16[128,32]{0,1:T(8,128)(2,1)S(1)}, bf16[128,32]{0,1:T(8,128)(2,1)}, u32[]{:S(2)}) copy-start(bf16[128,32]{0,1:T(8,128)(2,1)} %param.12) | copy-start | bytes 24580
  37.2 4.2 %copy-start.35 = (f32[32]{0:T(128)S(1)}, f32[32]{0:T(128)}, u32[]{:S(2)}) copy-start(f32[32]{0:T(128)} %param.13) | copy-start | bytes 388
  37.2 5.5 %copy-start.25 = (f32[32]{0:T(128)S(1)}, f32[32]{0:T(128)}, u32[]{:S(2)}) copy-start(f32[32]{0:T(128)} %param.14) | copy-start | bytes 388
  45.4 2.4 %copy-start.26 = (f32[1,128]{1,0:T(1,128)}, f32[1,128]{1,0:T(1,128)S(1)}, u32[]{:S(2)}) copy-start(f32[1,128]{1,0:T(1,128)S(1)} %constant_dynamic-slice_fusion.7) | copy-start | bytes 1540
  76.8 2.7 %copy-start.22 = (f32[4,32]{1,0:T(4,128)S(1)}, f32[4,32]{1,0:T(4,128)}, u32[]{:S(2)}) copy-start(f32[4,32]{1,0:T(4,128)} %exp.68) | copy-start | bytes 1540
  76.8 6.5 %copy-start.1 = (f32[4,128,2048]{1,2,0:T(8,128)S(1)}, f32[4,128,2048]{1,2,0:T(8,128)}, u32[]{:S(2)}) copy-start(f32[4,128,2048]{1,2,0:T(8,128)} %copy.102) | copy-start | bytes 12582916
  90.9 15.3 %collective-permute-start.3 = (f32[64,2048]{1,0:T(8,128)}, f32[64,2048]{1,0:T(8,128)}, u32[]{:S(2)}, u32[]{:S(2)}) collective-permute-start(f32[64,2048]{1,0:T(8,128)} %copy.110), channel_id=1, source_target_pairs={{24,8},{16,0},{25,9},{17,1},{26,10},{18,2},{27,11},{19,3},{28,12},... | collective-permute-start | bytes 1572872 | tf_op jit(solution)/shard_map/ppermute | solution.py:150
  94.7 15.3 %collective-permute-start.2 = (f32[64,2048]{1,0:T(8,128)}, f32[64,2048]{1,0:T(8,128)}, u32[]{:S(2)}, u32[]{:S(2)}) collective-permute-start(f32[64,2048]{1,0:T(8,128)} %copy.109), channel_id=1, source_target_pairs={{0,8},{8,0},{1,9},{9,1},{2,10},{10,2},{3,11},{11,3},{4,12},{12,4},... | collective-permute-start | bytes 1572872 | tf_op jit(solution)/shard_map/ppermute | solution.py:149
  97.9 3.3 %copy-start.13 = (f32[128,128]{0,1:T(8,128)S(1)}, f32[128,128]{0,1:T(8,128)}, u32[]{:S(2)}) copy-start(f32[128,128]{0,1:T(8,128)} %fusion.77) | copy-start | bytes 196612
  97.9 3.3 %copy-start.18 = (f32[32,128]{1,0:T(8,128)S(1)}, f32[32,128]{1,0:T(8,128)}, u32[]{:S(2)}) copy-start(f32[32,128]{1,0:T(8,128)} %copy.98) | copy-start | bytes 49156
  97.9 3.3 %copy-start.20 = (pred[128,128]{0,1:T(8,128)(4,1)S(1)}, pred[128,128]{0,1:T(8,128)(4,1)}, u32[]{:S(2)}) copy-start(pred[128,128]{0,1:T(8,128)(4,1)} %iota_compare_fusion) | copy-start | bytes 49156
  97.9 3.3 %copy-start.36 = (f32[32,128]{1,0:T(8,128)S(1)}, f32[32,128]{1,0:T(8,128)}, u32[]{:S(2)}) copy-start(f32[32,128]{1,0:T(8,128)} %get-tuple-element.44) | copy-start | bytes 49156
  103.6 8.8 %copy-start.9 = (f32[128,32]{0,1:T(8,128)S(1)}, f32[128,32]{0,1:T(8,128)}, u32[]{:S(2)}) copy-start(f32[128,32]{0,1:T(8,128)} %copy.113) | copy-start | bytes 49156
  103.6 8.8 %copy-start.10 = (f32[128,32]{0,1:T(8,128)S(1)}, f32[128,32]{0,1:T(8,128)}, u32[]{:S(2)}) copy-start(f32[128,32]{0,1:T(8,128)} %copy.114) | copy-start | bytes 49156
  103.6 8.8 %copy-start.11 = (f32[128,32]{0,1:T(8,128)S(1)}, f32[128,32]{0,1:T(8,128)}, u32[]{:S(2)}) copy-start(f32[128,32]{0,1:T(8,128)} %copy.115) | copy-start | bytes 49156
  112.4 2.7 %copy-start.29 = (f32[32]{0:T(128)S(1)}, f32[32]{0:T(128)}, u32[]{:S(2)}) copy-start(f32[32]{0:T(128)} %get-tuple-element.40) | copy-start | bytes 388
  112.4 3.0 %copy-start.28 = (f32[32]{0:T(128)S(1)}, f32[32]{0:T(128)}, u32[]{:S(2)}) copy-start(f32[32]{0:T(128)} %get-tuple-element.43) | copy-start | bytes 388
  115.8 1.9 %copy-start.5 = (bf16[128,2048]{0,1:T(8,128)(2,1)S(1)}, bf16[128,2048]{0,1:T(8,128)(2,1)}, u32[]{:S(2)}) copy-start(bf16[128,2048]{0,1:T(8,128)(2,1)} %copy.95) | copy-start | bytes 1572868
  115.8 2.0 %copy-start.15 = (f32[128,128]{0,1:T(8,128)S(1)}, f32[128,128]{0,1:T(8,128)}, u32[]{:S(2)}) copy-start(f32[128,128]{0,1:T(8,128)} %fusion.79) | copy-start | bytes 196612
  116.6 1.5 copy-start.24
  116.6 1.5 copy-start.27
  118.7 3.0 %collective-permute-start.4 = (f32[1152,128]{1,0:T(8,128)S(1)}, f32[1152,128]{1,0:T(8,128)S(1)}, u32[]{:S(2)}, u32[]{:S(2)}) collective-permute-start(f32[1152,128]{1,0:T(8,128)S(1)} %constant_dynamic-slice_fusion.6), channel_id=1, source_target_pairs={{0,1},{1,0},{2,3},{3,2},{4,5},{5,4},{6,7},{7,6},{8,9},{9,8},{10,11... | collective-permute-start | bytes 1769480 | tf_op jit(solution)/shard_map/ppermute | solution.py:26
  121.8 5.1 %collective-permute-start.5 = (f32[288,128]{1,0:T(8,128)S(1)}, f32[288,128]{1,0:T(8,128)S(1)}, u32[]{:S(2)}, u32[]{:S(2)}) collective-permute-start(f32[288,128]{1,0:T(8,128)S(1)} %get-tuple-element.23), channel_id=1, source_target_pairs={{0,8},{8,0},{16,24},{24,16},{1,9},{9,1},{17,25},{25,17},{2,10},{10... | collective-permute-start | bytes 442376 | tf_op jit(solution)/shard_map/ppermute | solution.py:26
  123.1 8.0 %collective-permute-start.6 = (f32[288,128]{1,0:T(8,128)S(1)}, f32[288,128]{1,0:T(8,128)S(1)}, u32[]{:S(2)}, u32[]{:S(2)}) collective-permute-start(f32[288,128]{1,0:T(8,128)S(1)} %get-tuple-element.25), channel_id=1, source_target_pairs={{0,16},{8,24},{16,0},{24,8},{1,17},{9,25},{17,1},{25,9},{2,18},{10... | collective-permute-start | bytes 442376 | tf_op jit(solution)/shard_map/ppermute | solution.py:26
  123.1 8.0 %collective-permute-start.7 = (f32[288,128]{1,0:T(8,128)S(1)}, f32[288,128]{1,0:T(8,128)S(1)}, u32[]{:S(2)}, u32[]{:S(2)}) collective-permute-start(f32[288,128]{1,0:T(8,128)S(1)} %get-tuple-element.24), channel_id=1, source_target_pairs={{0,24},{8,16},{16,8},{24,0},{1,25},{9,17},{17,9},{25,1},{2,26},{10... | collective-permute-start | bytes 442376 | tf_op jit(solution)/shard_map/ppermute | solution.py:26
  131.2 5.6 %collective-permute-start.10 = (f32[72,128]{1,0:T(8,128)S(1)}, f32[72,128]{1,0:T(8,128)S(1)}, u32[]{:S(2)}, u32[]{:S(2)}) collective-permute-start(f32[72,128]{1,0:T(8,128)S(1)} %get-tuple-element.36), channel_id=1, source_target_pairs={{0,6},{1,7},{2,4},{3,5},{4,2},{5,3},{6,0},{7,1},{8,14},{9,15},{10,... | collective-permute-start | bytes 110600 | tf_op jit(solution)/shard_map/ppermute | solution.py:26
  135.4 3.2 %collective-permute-start.8 = (f32[72,128]{1,0:T(8,128)S(1)}, f32[72,128]{1,0:T(8,128)S(1)}, u32[]{:S(2)}, u32[]{:S(2)}) collective-permute-start(f32[72,128]{1,0:T(8,128)S(1)} %get-tuple-element.35), channel_id=1, source_target_pairs={{0,2},{1,3},{2,0},{3,1},{4,6},{5,7},{6,4},{7,5},{8,10},{9,11},{10,... | collective-permute-start | bytes 110600 | tf_op jit(solution)/shard_map/ppermute | solution.py:26
  135.4 3.7 %collective-permute-start.9 = (f32[72,128]{1,0:T(8,128)S(1)}, f32[72,128]{1,0:T(8,128)S(1)}, u32[]{:S(2)}, u32[]{:S(2)}) collective-permute-start(f32[72,128]{1,0:T(8,128)S(1)} %get-tuple-element.37), channel_id=1, source_target_pairs={{0,4},{1,5},{2,6},{3,7},{4,0},{5,1},{6,2},{7,3},{8,12},{9,13},{10,... | collective-permute-start | bytes 110600 | tf_op jit(solution)/shard_map/ppermute | solution.py:26
  139.1 3.7 %collective-permute-start.11 = (f32[72,128]{1,0:T(8,128)S(1)}, f32[72,128]{1,0:T(8,128)S(1)}, u32[]{:S(2)}, u32[]{:S(2)}) collective-permute-start(f32[72,128]{1,0:T(8,128)S(1)} %add_add_fusion.1), channel_id=1, source_target_pairs={{0,2},{1,3},{2,0},{3,1},{4,6},{5,7},{6,4},{7,5},{8,10},{9,11},{10,... | collective-permute-start | bytes 110600 | tf_op jit(solution)/shard_map/ppermute | solution.py:26
  140.7 3.9 %collective-permute-start.12 = (f32[72,128]{1,0:T(8,128)S(1)}, f32[72,128]{1,0:T(8,128)S(1)}, u32[]{:S(2)}, u32[]{:S(2)}) collective-permute-start(f32[72,128]{1,0:T(8,128)S(1)} %add_add_fusion.1), channel_id=1, source_target_pairs={{0,4},{1,5},{2,6},{3,7},{4,0},{5,1},{6,2},{7,3},{8,12},{9,13},{10,... | collective-permute-start | bytes 110600 | tf_op jit(solution)/shard_map/ppermute | solution.py:26
  141.5 4.6 %collective-permute-start.13 = (f32[72,128]{1,0:T(8,128)S(1)}, f32[72,128]{1,0:T(8,128)S(1)}, u32[]{:S(2)}, u32[]{:S(2)}) collective-permute-start(f32[72,128]{1,0:T(8,128)S(1)} %add_add_fusion.1), channel_id=1, source_target_pairs={{0,6},{1,7},{2,4},{3,5},{4,2},{5,3},{6,0},{7,1},{8,14},{9,15},{10,... | collective-permute-start | bytes 110600 | tf_op jit(solution)/shard_map/ppermute | solution.py:26
  146.2 12.2 %copy-start.6 = (bf16[128,2048]{0,1:T(8,128)(2,1)S(1)}, bf16[128,2048]{0,1:T(8,128)(2,1)}, u32[]{:S(2)}) copy-start(bf16[128,2048]{0,1:T(8,128)(2,1)} %copy.95) | copy-start | bytes 1572868
  146.2 12.2 %copy-start.14 = (f32[128,128]{0,1:T(8,128)S(1)}, f32[128,128]{0,1:T(8,128)}, u32[]{:S(2)}) copy-start(f32[128,128]{0,1:T(8,128)} %fusion.77) | copy-start | bytes 196612
  146.2 12.2 %copy-start.19 = (f32[32,128]{1,0:T(8,128)S(1)}, f32[32,128]{1,0:T(8,128)}, u32[]{:S(2)}) copy-start(f32[32,128]{1,0:T(8,128)} %copy.98) | copy-start | bytes 49156
  146.2 12.2 %copy-start.21 = (pred[128,128]{0,1:T(8,128)(4,1)S(1)}, pred[128,128]{0,1:T(8,128)(4,1)}, u32[]{:S(2)}) copy-start(pred[128,128]{0,1:T(8,128)(4,1)} %iota_compare_fusion) | copy-start | bytes 49156
  146.2 12.2 %copy-start.37 = (f32[32,128]{1,0:T(8,128)S(1)}, f32[32,128]{1,0:T(8,128)}, u32[]{:S(2)}) copy-start(f32[32,128]{1,0:T(8,128)} %get-tuple-element.44) | copy-start | bytes 49156
  146.3 4.1 %collective-permute-start.14 = (f32[288,128]{1,0:T(8,128)S(1)}, f32[288,128]{1,0:T(8,128)S(1)}, u32[]{:S(2)}, u32[]{:S(2)}) collective-permute-start(f32[288,128]{1,0:T(8,128)S(1)} %get-tuple-element.30), channel_id=1, source_target_pairs={{0,8},{8,0},{16,24},{24,16},{1,9},{9,1},{17,25},{25,17},{2,10},{10... | collective-permute-start | bytes 442376 | tf_op jit(solution)/shard_map/ppermute | solution.py:26
  146.4 4.0 %collective-permute-start.15 = (f32[288,128]{1,0:T(8,128)S(1)}, f32[288,128]{1,0:T(8,128)S(1)}, u32[]{:S(2)}, u32[]{:S(2)}) collective-permute-start(f32[288,128]{1,0:T(8,128)S(1)} %get-tuple-element.30), channel_id=1, source_target_pairs={{0,16},{8,24},{16,0},{24,8},{1,17},{9,25},{17,1},{25,9},{2,18},{10... | collective-permute-start | bytes 442376 | tf_op jit(solution)/shard_map/ppermute | solution.py:26
  147.5 4.9 %collective-permute-start.16 = (f32[288,128]{1,0:T(8,128)S(1)}, f32[288,128]{1,0:T(8,128)S(1)}, u32[]{:S(2)}, u32[]{:S(2)}) collective-permute-start(f32[288,128]{1,0:T(8,128)S(1)} %get-tuple-element.30), channel_id=1, source_target_pairs={{0,24},{8,16},{16,8},{24,0},{1,25},{9,17},{17,9},{25,1},{2,26},{10... | collective-permute-start | bytes 442376 | tf_op jit(solution)/shard_map/ppermute | solution.py:26
  152.6 10.6 %collective-permute-start.17 = (f32[1152,128]{1,0:T(8,128)S(1)}, f32[1152,128]{1,0:T(8,128)S(1)}, u32[]{:S(2)}, u32[]{:S(2)}) collective-permute-start(f32[1152,128]{1,0:T(8,128)S(1)} %get-tuple-element.17), channel_id=1, source_target_pairs={{0,1},{1,0},{2,3},{3,2},{4,5},{5,4},{6,7},{7,6},{8,9},{9,8},{10,11... | collective-permute-start | bytes 1769480 | tf_op jit(solution)/shard_map/ppermute | solution.py:26
  (9 other events, 10.4 us)

commit v10 on v8

--- a/solution.py
+++ b/solution.py
@@ -129,13 +129,18 @@
     cum_all = jnp.cumsum(-step_all * decay_rate, axis=1)
     gate_all = jnp.exp(cum_all[:, -1])
     tail_all = jnp.exp(cum_all[:, -1:, :] - cum_all) * step_all
-    xw_all = (x_all * tail_all[..., None]).astype(half)
-    state_local_all = jnp.einsum("bthp,btn->bhpn", xw_all, b_all, preferred_element_type=fl)
-
-    state_in = jnp.zeros((head_count, head_dim, state_dim), fl)
-    for k in range(n_blocks - 1):
-        new = gate_all[k][:, None, None] * state_in + state_local_all[k]
-        state_in = jnp.where(k < my_block, new, state_in)
+    head_all = jnp.exp(cum_all)
+    earlier = n_blocks - 1
+    xw_all = (x_all[:earlier] * tail_all[:earlier, :, :, None]).astype(half)
+    xw_all = xw_all.reshape(earlier, tok_rows, inner_width)
+    state_local_t = jnp.einsum("btn,btk->bnk", b_all[:earlier], xw_all, preferred_element_type=fl)
+
+    state_t = jnp.zeros((state_dim, inner_width), fl)
+    for k in range(earlier):
+        gate_row = jnp.repeat(gate_all[k], head_dim)[None, :]
+        new = gate_row * state_t + state_local_t[k]
+        state_t = jnp.where(k < my_block, new, state_t)
+    state_in = state_t.reshape(state_dim, head_count, head_dim).transpose(1, 2, 0)
 
     grad_heads = grad_out[0].reshape(tok_rows, head_count, head_dim)
     grad_weighted = (grad_heads * head_factor[:, :, None]).astype(half)
@@ -152,13 +157,17 @@
             jnp.where(my_block == 1, third, second),
             jnp.where(my_block == 2, first, jnp.where(my_block == 1, second, fourth)),
         ]
-        c_all = projected_all[:, :, inner_width + state_dim :]
+        c_all = projected_all[1:, :, inner_width + state_dim :]
+        later = jnp.stack(seen).reshape(n_blocks - 1, tok_rows, head_count, head_dim)
+        later_weighted = (later * head_all[1:, :, :, None]).astype(half)
+        later_weighted = later_weighted.reshape(n_blocks - 1, tok_rows, inner_width)
+        later_local_t = jnp.einsum("btn,btk->bnk", c_all, later_weighted, preferred_element_type=fl)
+        adjoint_t = jnp.zeros((state_dim, inner_width), fl)
         for k in range(n_blocks - 1, 0, -1):
-            later = seen[k - 1].reshape(tok_rows, head_count, head_dim)
-            later_weighted = (later * jnp.exp(cum_all[k])[:, :, None]).astype(half)
-            later_local = jnp.einsum("thp,tn->hpn", later_weighted, c_all[k], preferred_element_type=fl)
-            new = gate_all[k][:, None, None] * adjoint_in + later_local
-            adjoint_in = jnp.where(k > my_block, new, adjoint_in)
+            gate_row = jnp.repeat(gate_all[k], head_dim)[None, :]
+            new = gate_row * adjoint_t + later_local_t[k - 1]
+            adjoint_t = jnp.where(k > my_block, new, adjoint_t)
+        adjoint_in = adjoint_t.reshape(state_dim, head_count, head_dim).transpose(1, 2, 0)
     else:
         adjoint_all = lax.all_gather(adjoint_local, "tm")
         for k in range(n_blocks - 1, 0, -1):

time: 136 us -> 165 us (1.21)
  local copies, waits for them, and re-layouts: 21.5 us -> 41 us
  other arithmetic: 11.9 us -> 22.5 us
    slice x1 -> x12, local copies, waits for them, and re-layouts: 0.08 us -> 22.3 us  [the longest x4 9.53 us: on_device(): new = gate_row * state_t + state_local_t[k]]
    convert_element_type x1 -> x0, local copies, waits for them, and re-layouts: 5.38 us -> none  [on_device(): xw_all = (x_all * tail_all[..., None]).astype(half)]
    exp x4 -> x0, local copies, waits for them, and re-layouts: 5.22 us -> none  [on_device(): later_weighted = (later * jnp.exp(cum_all[k])[:, :, None]).astype(half)]
    dot_general x4 -> x2, matrix products: 3.74 us -> 1.23 us  [the longest x1 0.62 us: on_device(): jnp.einsum('btn,btk->bnk', c_all, later_weighted, preferred_element_type=fl)]
    dot_general x1, matrix products: 2.39 us -> 0.29 us  [on_device(): jnp.einsum('tn,hpn->thp', c_proj, state_half, preferred_element_type=fl)]
    unnamed x81 -> x92, local copies, waits for them, and re-layouts: 5.32 us -> 7.4 us
    dot_general x1, matrix products: 1.29 us -> 3.33 us  [on_device(): jnp.einsum('hts,shp->thp', weights, x_heads, preferred_element_type=fl)]
    exp x0 -> x1, other arithmetic: none -> 1.91 us  [on_device(): head_all = jnp.exp(cum_all)]
  transfers between devices with their start and end apart: 19 -> 19, of which waited for: 13 -> 13; matrix products, arithmetic and copies ran while one was open for 34% -> 39% of each run, Pallas kernels for 0% -> 0%
where the time goes in v10:
time: 165 us; the launch traced here: 164 us
  starting transfers between devices  43 us (26%)
  local copies, waits for them, and re-layouts  41 us (25%)
  waiting for transfers between devices  32.6 us (20%)
  matrix products  23.1 us (14%)
  other arithmetic  22.5 us (14%)
    ppermute x14, starting transfers between devices, exchange(): return lax.ppermute(value, axis, pairs)  21.7 us
    ppermute x14, waiting for transfers between devices, exchange(): return lax.ppermute(value, axis, pairs)  18.5 us
    all_to_all x1, waiting for transfers between devices, on_device(): lax.all_to_all(outgoing, ('tm', 'series'), split_axis=0, concat_axis=1, t...  12.9 us
    all_to_all x1, starting transfers between devices, on_device(): lax.all_to_all(outgoing, ('tm', 'series'), split_axis=0, concat_axis=1, t...  11.3 us
    slice x4, local copies, waits for them, and re-layouts, on_device(): new = gate_row * state_t + state_local_t[k]  9.53 us
    slice x4, local copies, waits for them, and re-layouts, on_device(): new = gate_row * adjoint_t + later_local_t[k - 1]  8.04 us
    unnamed x92, local copies, waits for them, and re-layouts  7.4 us
    ppermute x1, starting transfers between devices, on_device(): third = lax.ppermute(second, 'tm', [(0, 1)])  6.18 us
  transfers between devices with their start and end apart: 19, of which 13 were waited for; matrix products, arithmetic and copies ran while one was open for 39% of the time, Pallas kernels for 0%

profile of v10, /device:TPU:1, one launch (start us, length us, event | category | flops | bytes accessed | tf_op | source)
XLA Modules:
  0.0 163.7 jit_solution(14272860561133382814)
XLA Ops:
  0.7 1.4 copy.132
  7.1 11.3 %all-to-all-start = ((f32[32,1,16]{2,1,0:T(1,128)}), f32[32,1,16]{2,1,0:T(1,128)S(1)}, u32[]{:S(2)}, u32[]{:S(2)}) async-start(f32[32,1,16]{2,1,0:T(1,128)} %bitcast), calls=%async_computation | async-start | bytes 32768 | tf_op jit(solution)/shard_map/all_to_all | solution.py:92
  19.2 12.9 %all-to-all-done = f32[32,1,16]{2,1,0:T(1,128)S(1)} async-done(((f32[32,1,16]{2,1,0:T(1,128)}), f32[32,1,16]{2,1,0:T(1,128)S(1)}, u32[]{:S(2)}, u32[]{:S(2)}) %all-to-all-start) | async-done | bytes 2080 | tf_op jit(solution)/shard_map/all_to_all | solution.py:92
  33.4 1.5 convert_reduce_fusion
  35.5 4.1 %fusion = f32[512,4]{0,1:T(4,128)S(1)} fusion(f32[4096]{0:T(1024)S(1)} %get-tuple-element.43, f32[4096]{0:T(1024)S(1)} %convert_element_type.99, f32[512]{0:T(512)S(1)} %le.22, f32[4096,1]{0,1:T(1,128)S(1)} %bitcast.186, f32[4096,1]{0,1:T(1,128)S(1)} %bitcast.178, f32[4096,1]{0,1:T(1,128)S(1)} %bitcast.177, f32[4096,1]{0,1:T(1,128)S(1)} %sub.65), kind=kOutput, calls=%fused_computation.3 | convolution fusion | flops 107003904 | bytes 108544 | tf_op jit(solution)/shard_map/dot_general | solution.py:101
  39.8 1.6 convolution_convert_fusion
  41.4 1.7 %compare_select_fusion = f32[512,32]{0,1:T(8,128)} fusion(bf16[128,32]{0,1:T(8,128)(2,1)S(1)} %copy-done.39, f32[128]{0:T(128)S(1)} %add_multiply_fusion, f32[512]{0:T(512)S(1)} %bitcast.188, f32[32]{0:T(128)S(1)} %copy-done.41), kind=kOutput, calls=%fused_computation.69 | convolution fusion | flops 4440064 | bytes 76416 | tf_op jit(solution)/shard_map/dot_general | solution.py:127
  45.6 1.6 reduce_window_sum.46
  49.4 1.7 %copy.149 = f32[512,32]{1,0:T(8,128)} copy(f32[512,32]{0,1:T(8,128)} %compare_select_fusion) | data formatting | bytes 131072 | tf_op jit(solution)/shard_map/reshape | solution.py:128
  51.1 1.7 %negate_multiply_fusion = f32[4,128,32]{2,1,0:T(8,128)} fusion(f32[4,128,32]{2,1,0:T(8,128)} %bitcast.165, f32[32]{0:T(128)} %param.14), kind=kLoop, calls=%fused_computation.63 | loop fusion | flops 32768 | bytes 131200 | tf_op jit(solution)/shard_map/mul | solution.py:129
  52.7 1.9 %reduce_window_sum.47 = f32[4,128,32]{2,1,0:T(8,128)} reduce-window(f32[4,128,32]{2,1,0:T(8,128)} %negate_multiply_fusion, f32[]{:T(128)} %constant.170.clone.1), window={size=1x128x1 pad=0_0x127_0x0_0}, to_apply=%region_4.5 | reduce-window | flops 2080768 | bytes 131076 | tf_op jit(solution)/shard_map/jit(cumsum)/reduce_window_sum | solution.py:129
  55.9 1.9 %slice_exponential_fusion = (f32[3,128,32]{2,1,0:T(8,128)}, f32[3,128,32]{2,1,0:T(8,128)}) fusion(f32[4,128,32]{2,1,0:T(8,128)} %reduce_window_sum.47, f32[4,128,32]{2,1,0:T(8,128)} %bitcast.166, f32[3,32]{1,0:T(4,128)S(1)} %bitcast.185), kind=kLoop, calls=%fused_computation.65 | loop fusion | flops 24576 | bytes 246144 | tf_op jit(solution)/shard_map/exp | solution.py:132
  57.8 1.7 %copy.126 = f32[3,128,32]{1,2,0:T(8,128)} copy(f32[3,128,32]{2,1,0:T(8,128)} %get-tuple-element.32) | data formatting | bytes 98304 | tf_op jit(solution)/shard_map/slice | solution.py:134
  59.5 1.3 slice.131
  60.8 2.6 %copy.151 = bf16[3,128,2048]{1,2,0:T(8,128)(2,1)} copy(bf16[3,128,2048]{2,1,0:T(8,128)(2,1)} %slice.131) | data formatting | bytes 3145728
  64.2 1.7 %fusion.5 = bf16[3,128,2048]{1,2,0:T(8,128)(2,1)S(1)} fusion(bf16[3,128,2048]{1,2,0:T(8,128)(2,1)} %copy.151, f32[3,128,32]{1,2,0:T(8,128)} %copy.126), kind=kLoop, calls=%fused_computation.12 | loop fusion | flops 2359296 | bytes 3194880 | tf_op jit(solution)/shard_map/convert_element_type | solution.py:134
  67.2 1.8 %fusion.84 = (f32[1,128,2048]{2,1,0:T(8,128)}, f32[1,128,2048]{2,1,0:T(8,128)}, f32[1,128,2048]{2,1,0:T(8,128)}) fusion(f32[3,128,2048]{2,1,0:T(8,128)S(1)} %fusion.37), kind=kLoop, calls=%fused_computation.165 | loop fusion | bytes 6291456 | tf_op jit(solution)/shard_map/slice | solution.py:141
  70.3 6.2 %collective-permute-start.2 = (f32[128,2048]{0,1:T(8,128)}, f32[128,2048]{0,1:T(8,128)}, u32[]{:S(2)}, u32[]{:S(2)}) collective-permute-start(f32[128,2048]{0,1:T(8,128)} %collective-permute-done.1), channel_id=1, source_target_pairs={{0,8},{1,9},{2,10},{3,11},{4,12},{5,13},{6,14},{7,15}} | collective-permute-start | bytes 3145736 | tf_op jit(solution)/shard_map/ppermute | solution.py:153
  77.8 1.6 %copy.136 = f32[3,128,32]{1,2,0:T(8,128)} copy(f32[3,128,32]{2,1,0:T(8,128)} %get-tuple-element.31) | data formatting | bytes 98304 | tf_op jit(solution)/shard_map/slice | solution.py:162
  79.4 2.6 %copy.128 = f32[1,128,2048]{1,2,0:T(8,128)} copy(f32[1,128,2048]{2,1,0:T(8,128)} %get-tuple-element.15) | data formatting | bytes 2097152 | tf_op jit(solution)/shard_map/slice | solution.py:141
  82.0 2.6 %copy.129 = f32[1,128,2048]{1,2,0:T(8,128)} copy(f32[1,128,2048]{2,1,0:T(8,128)} %get-tuple-element.17) | data formatting | bytes 2097152 | tf_op jit(solution)/shard_map/slice | solution.py:141
  84.6 2.6 %copy.130 = f32[1,128,2048]{1,2,0:T(8,128)} copy(f32[1,128,2048]{2,1,0:T(8,128)} %get-tuple-element.16) | data formatting | bytes 2097152 | tf_op jit(solution)/shard_map/slice | solution.py:141
  89.8 2.8 %fusion.6 = bf16[128,128]{0,1:T(8,128)(2,1)S(1)} fusion(bf16[128,32,64]{0,2,1:T(8,128)(2,1)} %bitcast.168, bf16[128,32,64]{0,2,1:T(8,128)(2,1)} %bitcast.160, f32[32,128]{1,0:T(8,128)} %get-tuple-element.50, f32[32,128]{1,0:T(8,128)} %copy.119, pred[128,128]{0,1:T(8,128)(4,1)} %iota_compare_fusion), kind=kOutput, calls=%fused_computation.14 | convolution fusion | flops 70238208 | bytes 1130496 | tf_op jit(solution)/shard_map/thp,shp->hts/dot_general | solution.py:195
  94.2 2.4 %convolution_bitcast_fusion = f32[128,32,64]{0,2,1:T(8,128)} fusion(bf16[128,32,64]{0,2,1:T(8,128)(2,1)S(1)} %bitcast.161, f32[32,128]{1,0:T(8,128)S(1)} %copy-done.42, f32[32,128]{1,0:T(8,128)S(1)} %copy-done.24, f32[128,128]{0,1:T(8,128)S(1)} %copy-done.19, pred[128,128]{0,1:T(8,128)(4,1)S(1)} %copy-done.26), kind=kOutput, calls=%fused_computation.23 | convolution fusion | flops 70254592 | bytes 1687552 | tf_op jit(solution)/shard_map/hts,thp->shp/dot_general | solution.py:189
  97.9 1.7 %select_bitcast_fusion.1 = (f32[1,128,2048]{1,2,0:T(8,128)S(1)}, f32[1,128,2048]{1,2,0:T(8,128)S(1)}) fusion(f32[128,2048]{0,1:T(8,128)} %collective-permute-done.2, f32[128,2048]{0,1:T(8,128)} %collective-permute-done.1, pred[]{:T(512)S(6)} %eq.18, f32[128,2048]{0,1:T(8,128)} %collective-permute-done, f32[128,2048]{0,1:T(8,128)} %collective-permute-done.3, ...), kind=kLoop, calls=%fused_computation.43 | loop fusion | flops 786432 | bytes 6291458 | tf_op jit(solution)/shard_map/stack | solution.py:161
  99.7 1.6 fusion.4
  101.9 1.5 fusion.83
  103.4 1.3 copy.138
  104.7 2.7 %copy.139 = f32[1,128,2048]{1,2,0:T(8,128)} copy(f32[1,128,2048]{2,1,0:T(8,128)} %get-tuple-element.14) | data formatting | bytes 2097152 | tf_op jit(solution)/shard_map/slice | solution.py:168
  107.4 2.5 %copy.140 = f32[1,128,2048]{1,2,0:T(8,128)} copy(f32[1,128,2048]{2,1,0:T(8,128)} %get-tuple-element.13) | data formatting | bytes 2097152 | tf_op jit(solution)/shard_map/slice | solution.py:168
  110.0 3.0 %fusion.27 = (bf16[32,64,128]{2,1,0:T(8,128)(2,1)S(1)}, bf16[32,64,128]{2,1,0:T(8,128)(2,1)S(1)}) fusion(f32[128,32,64]{0,2,1:T(8,128)} %bitcast.159, f32[128,32,64]{0,2,1:T(8,128)} %bitcast.158, f32[128,32,64]{0,2,1:T(8,128)} %bitcast.157, f32[32]{0:T(128)S(1)} %copy-done.34, f32[32]{0:T(128)S(1)} %copy-done.36, f32[32]{0:T(128)S(1)} %copy-done.37, ...), kind=kLoop, calls=%fused_computation.59 | loop fusion | flops 4718592 | bytes 7340550 | tf_op jit(solution)/shard_map/convert_element_type | solution.py:181
  115.6 1.3 collective-permute-start.4
  117.0 1.6 collective-permute-done.4
  118.7 2.3 %collective-permute-start.5 = (f32[288,128]{1,0:T(8,128)S(1)}, f32[288,128]{1,0:T(8,128)S(1)}, u32[]{:S(2)}, u32[]{:S(2)}) collective-permute-start(f32[288,128]{1,0:T(8,128)S(1)} %get-tuple-element.28), channel_id=1, source_target_pairs={{0,8},{8,0},{16,24},{24,16},{1,9},{9,1},{17,25},{25,17},{2,10},{10... | collective-permute-start | bytes 442376 | tf_op jit(solution)/shard_map/ppermute | solution.py:26
  122.2 2.7 %collective-permute-done.5 = f32[288,128]{1,0:T(8,128)S(1)} collective-permute-done((f32[288,128]{1,0:T(8,128)S(1)}, f32[288,128]{1,0:T(8,128)S(1)}, u32[]{:S(2)}, u32[]{:S(2)}) %collective-permute-start.5) | collective-permute-done | bytes 147488 | tf_op jit(solution)/shard_map/ppermute | solution.py:26
  124.9 4.1 %collective-permute-done.6 = f32[288,128]{1,0:T(8,128)S(1)} collective-permute-done((f32[288,128]{1,0:T(8,128)S(1)}, f32[288,128]{1,0:T(8,128)S(1)}, u32[]{:S(2)}, u32[]{:S(2)}) %collective-permute-start.6) | collective-permute-done | bytes 147488 | tf_op jit(solution)/shard_map/ppermute | solution.py:26
  129.0 4.2 %collective-permute-start.10 = (f32[72,128]{1,0:T(8,128)S(1)}, f32[72,128]{1,0:T(8,128)S(1)}, u32[]{:S(2)}, u32[]{:S(2)}) collective-permute-start(f32[72,128]{1,0:T(8,128)S(1)} %get-tuple-element.40), channel_id=1, source_target_pairs={{0,6},{1,7},{2,4},{3,5},{4,2},{5,3},{6,0},{7,1},{8,14},{9,15},{10,... | collective-permute-start | bytes 110600 | tf_op jit(solution)/shard_map/ppermute | solution.py:26
  134.6 1.9 %collective-permute-done.8 = f32[72,128]{1,0:T(8,128)S(1)} collective-permute-done((f32[72,128]{1,0:T(8,128)S(1)}, f32[72,128]{1,0:T(8,128)S(1)}, u32[]{:S(2)}, u32[]{:S(2)}) %collective-permute-start.8) | collective-permute-done | bytes 36896 | tf_op jit(solution)/shard_map/ppermute | solution.py:26
  137.0 1.5 collective-permute-start.11
  139.4 1.3 collective-permute-start.13
  140.7 1.7 %collective-permute-done.12 = f32[72,128]{1,0:T(8,128)S(1)} collective-permute-done((f32[72,128]{1,0:T(8,128)S(1)}, f32[72,128]{1,0:T(8,128)S(1)}, u32[]{:S(2)}, u32[]{:S(2)}) %collective-permute-start.12) | collective-permute-done | bytes 36896 | tf_op jit(solution)/shard_map/ppermute | solution.py:26
  142.4 1.6 collective-permute-done.13
  145.4 1.5 collective-permute-start.16
  146.8 1.3 collective-permute-done.14
  148.3 2.0 %collective-permute-done.16 = f32[288,128]{1,0:T(8,128)S(1)} collective-permute-done((f32[288,128]{1,0:T(8,128)S(1)}, f32[288,128]{1,0:T(8,128)S(1)}, u32[]{:S(2)}, u32[]{:S(2)}) %collective-permute-start.16) | collective-permute-done | bytes 147488 | tf_op jit(solution)/shard_map/ppermute | solution.py:26
  150.4 5.9 %collective-permute-start.17 = (f32[1152,128]{1,0:T(8,128)S(1)}, f32[1152,128]{1,0:T(8,128)}, u32[]{:S(2)}, u32[]{:S(2)}) collective-permute-start(f32[1152,128]{1,0:T(8,128)S(1)} %get-tuple-element.22), channel_id=1, source_target_pairs={{0,1},{1,0},{2,3},{3,2},{4,5},{5,4},{6,7},{7,6},{8,9},{9,8},{10,11... | collective-permute-start | bytes 1769480 | tf_op jit(solution)/shard_map/ppermute | solution.py:26
  156.3 3.3 %convolution_bitcast_fusion.1 = f32[128,32,64]{0,2,1:T(8,128)S(1)} fusion(bf16[128,32,64]{0,2,1:T(8,128)(2,1)} %bitcast.169, f32[32,128]{1,0:T(8,128)S(1)} %copy-done.43, f32[32,128]{1,0:T(8,128)S(1)} %copy-done.25, f32[128,128]{0,1:T(8,128)S(1)} %copy-done.20, pred[128,128]{0,1:T(8,128)(4,1)S(1)} %copy-done.27), kind=kOutput, calls=%fused_computation.26 | convolution fusion | flops 70254592 | bytes 1687552 | tf_op jit(solution)/shard_map/hts,shp->thp/dot_general | solution.py:182
  162.3 1.4 copy.143
  (173 shorter events, 35.2 us)
Async XLA Ops:
  0.6 39.1 %copy-start = (bf16[128,2304]{1,0:T(8,128)(2,1)S(1)}, bf16[128,2304]{1,0:T(8,128)(2,1)}, u32[]{:S(2)}) copy-start(bf16[128,2304]{1,0:T(8,128)(2,1)} %param.11) | copy-start | bytes 1769476
  0.6 5.1 %copy-start.40 = (s32[8]{0:T(128)S(1)}, s32[8]{0:T(128)}, u32[]{:S(2)}) copy-start(s32[8]{0:T(128)} %param.9) | copy-start | bytes 100
  0.7 5.1 %copy-start.14 = (s32[8,16]{1,0:T(8,128)S(1)}, s32[8,16]{1,0:T(8,128)}, u32[]{:S(2)}) copy-start(s32[8,16]{1,0:T(8,128)} %param.8) | copy-start | bytes 1540
  0.7 18.3 %copy-start.23 = (s32[4096]{0:T(1024)S(1)}, s32[4096]{0:T(1024)}, u32[]{:S(2)}) copy-start(s32[4096]{0:T(1024)} %param.10) | copy-start | bytes 49156
  2.0 37.6 %copy-start.5 = (bf16[1,128,2048]{1,2,0:T(8,128)(2,1)}, bf16[1,128,2048]{1,2,0:T(8,128)(2,1)S(1)}, u32[]{:S(2)}) copy-start(bf16[1,128,2048]{1,2,0:T(8,128)(2,1)S(1)} %copy.132) | copy-start | bytes 1572868
  3.2 65.9 %collective-permute-start = (f32[128,2048]{0,1:T(8,128)}, f32[128,2048]{0,1:T(8,128)}, u32[]{:S(2)}, u32[]{:S(2)}) collective-permute-start(f32[128,2048]{0,1:T(8,128)} %bitcast_convert_fusion), channel_id=1, source_target_pairs={{24,16},{8,0},{25,17},{9,1},{26,18},{10,2},{27,19},{11,3},{28,20},... | collective-permute-start | bytes 3145736 | tf_op jit(solution)/shard_map/ppermute | solution.py:151
  4.5 65.9 %collective-permute-start.1 = (f32[128,2048]{0,1:T(8,128)}, f32[128,2048]{0,1:T(8,128)}, u32[]{:S(2)}, u32[]{:S(2)}) collective-permute-start(f32[128,2048]{0,1:T(8,128)} %bitcast_convert_fusion), channel_id=1, source_target_pairs={{24,8},{16,0},{25,9},{17,1},{26,10},{18,2},{27,11},{19,3},{28,12},... | collective-permute-start | bytes 3145736 | tf_op jit(solution)/shard_map/ppermute | solution.py:152
  7.1 25.0 %all-to-all-start = ((f32[32,1,16]{2,1,0:T(1,128)}), f32[32,1,16]{2,1,0:T(1,128)S(1)}, u32[]{:S(2)}, u32[]{:S(2)}) async-start(f32[32,1,16]{2,1,0:T(1,128)} %bitcast), calls=%async_computation | async-start | bytes 32768 | tf_op jit(solution)/shard_map/all_to_all | solution.py:92
  19.1 25.0 %copy-start.29 = (f32[128]{0:T(128)}, f32[128]{0:T(128)S(1)}, u32[]{:S(2)}) copy-start(f32[128]{0:T(128)S(1)} %add_multiply_fusion) | copy-start | bytes 1540
  39.7 5.0 %copy-start.31 = (f32[32]{0:T(128)S(1)}, f32[32]{0:T(128)}, u32[]{:S(2)}) copy-start(f32[32]{0:T(128)} %param.14) | copy-start | bytes 388
  44.7 32.4 %copy-start.3 = (bf16[128,2304]{1,0:T(8,128)(2,1)}, bf16[128,2304]{1,0:T(8,128)(2,1)S(1)}, u32[]{:S(2)}) copy-start(bf16[128,2304]{1,0:T(8,128)(2,1)S(1)} %convolution_convert_fusion.1) | copy-start | bytes 1769476
  67.2 9.3 %copy-start.28 = (f32[4,32]{1,0:T(4,128)S(1)}, f32[4,32]{1,0:T(4,128)}, u32[]{:S(2)}) copy-start(f32[4,32]{1,0:T(4,128)} %exp.37) | copy-start | bytes 1540
  67.2 9.9 %copy-start.10 = (f32[128,32]{1,0:T(8,128)S(1)}, f32[128,32]{1,0:T(8,128)}, u32[]{:S(2)}) copy-start(f32[128,32]{1,0:T(8,128)} %reduce_window_sum.46) | copy-start | bytes 49156
  69.0 27.6 %collective-permute-start.3 = (f32[128,2048]{0,1:T(8,128)}, f32[128,2048]{0,1:T(8,128)}, u32[]{:S(2)}, u32[]{:S(2)}) collective-permute-start(f32[128,2048]{0,1:T(8,128)} %collective-permute-done), channel_id=1, source_target_pairs={{16,0},{17,1},{18,2},{19,3},{20,4},{21,5},{22,6},{23,7}} | collective-permute-start | bytes 3145736 | tf_op jit(solution)/shard_map/ppermute | solution.py:154
  70.3 27.6 %collective-permute-start.2 = (f32[128,2048]{0,1:T(8,128)}, f32[128,2048]{0,1:T(8,128)}, u32[]{:S(2)}, u32[]{:S(2)}) collective-permute-start(f32[128,2048]{0,1:T(8,128)} %collective-permute-done.1), channel_id=1, source_target_pairs={{0,8},{1,9},{2,10},{3,11},{4,12},{5,13},{6,14},{7,15}} | collective-permute-start | bytes 3145736 | tf_op jit(solution)/shard_map/ppermute | solution.py:153
  82.0 5.2 %copy-start.11 = (f32[128,32]{1,0:T(8,128)S(1)}, f32[128,32]{1,0:T(8,128)}, u32[]{:S(2)}) copy-start(f32[128,32]{1,0:T(8,128)} %reduce_window_sum.46) | copy-start | bytes 49156
  82.0 5.8 %slice-start = ((bf16[128,2304]{1,0:T(8,128)(2,1)}), bf16[128,2048]{1,0:T(8,128)(2,1)S(1)}, s32[]{:S(2)}) async-start(bf16[128,2304]{1,0:T(8,128)(2,1)} %copy-done.3), calls=%async_computation.1 | async-start | bytes 1048576 | tf_op jit(solution)/shard_map/slice | solution.py:113
  89.7 4.5 %copy-start.6 = (bf16[1,128,2048]{1,2,0:T(8,128)(2,1)S(1)}, bf16[1,128,2048]{1,2,0:T(8,128)(2,1)}, u32[]{:S(2)}) copy-start(bf16[1,128,2048]{1,2,0:T(8,128)(2,1)} %copy-done.5) | copy-start | bytes 1572868
  89.7 4.5 %copy-start.19 = (f32[128,128]{0,1:T(8,128)S(1)}, f32[128,128]{0,1:T(8,128)}, u32[]{:S(2)}) copy-start(f32[128,128]{0,1:T(8,128)} %fusion.61) | copy-start | bytes 196612
  89.7 4.5 %copy-start.24 = (f32[32,128]{1,0:T(8,128)S(1)}, f32[32,128]{1,0:T(8,128)}, u32[]{:S(2)}) copy-start(f32[32,128]{1,0:T(8,128)} %copy.119) | copy-start | bytes 49156
  89.7 4.5 %copy-start.26 = (pred[128,128]{0,1:T(8,128)(4,1)S(1)}, pred[128,128]{0,1:T(8,128)(4,1)}, u32[]{:S(2)}) copy-start(pred[128,128]{0,1:T(8,128)(4,1)} %iota_compare_fusion) | copy-start | bytes 49156
  89.7 4.5 %copy-start.42 = (f32[32,128]{1,0:T(8,128)S(1)}, f32[32,128]{1,0:T(8,128)}, u32[]{:S(2)}) copy-start(f32[32,128]{1,0:T(8,128)} %get-tuple-element.50) | copy-start | bytes 49156
  104.7 5.2 %copy-start.1 = (f32[1,128,2048]{1,2,0:T(8,128)S(1)}, f32[1,128,2048]{1,2,0:T(8,128)}, u32[]{:S(2)}) copy-start(f32[1,128,2048]{1,2,0:T(8,128)} %copy.128) | copy-start | bytes 3145732
  104.7 5.2 %copy-start.2 = (f32[1,128,2048]{1,2,0:T(8,128)S(1)}, f32[1,128,2048]{1,2,0:T(8,128)}, u32[]{:S(2)}) copy-start(f32[1,128,2048]{1,2,0:T(8,128)} %copy.129) | copy-start | bytes 3145732
  104.7 5.2 %copy-start.34 = (f32[32]{0:T(128)S(1)}, f32[32]{0:T(128)}, u32[]{:S(2)}) copy-start(f32[32]{0:T(128)} %get-tuple-element.44) | copy-start | bytes 388
  104.7 5.2 %copy-start.35 = (f32[32]{0:T(128)S(1)}, f32[32]{0:T(128)}, u32[]{:S(2)}) copy-start(f32[32]{0:T(128)} %get-tuple-element.45) | copy-start | bytes 388
  104.7 5.3 %copy-start.36 = (f32[32]{0:T(128)S(1)}, f32[32]{0:T(128)}, u32[]{:S(2)}) copy-start(f32[32]{0:T(128)} %get-tuple-element.46) | copy-start | bytes 388
  104.7 5.3 %copy-start.37 = (f32[32]{0:T(128)S(1)}, f32[32]{0:T(128)}, u32[]{:S(2)}) copy-start(f32[32]{0:T(128)} %get-tuple-element.47) | copy-start | bytes 388
  110.0 3.1 %copy-start.12 = (f32[128,32,64]{0,2,1:T(8,128)S(1)}, f32[128,32,64]{0,2,1:T(8,128)}, u32[]{:S(2)}) copy-start(f32[128,32,64]{0,2,1:T(8,128)} %convolution_bitcast_fusion) | copy-start | bytes 3145732
  115.6 2.9 %collective-permute-start.4 = (f32[1152,128]{1,0:T(8,128)S(1)}, f32[1152,128]{1,0:T(8,128)S(1)}, u32[]{:S(2)}, u32[]{:S(2)}) collective-permute-start(f32[1152,128]{1,0:T(8,128)S(1)} %constant_dynamic-slice_fusion.6), channel_id=1, source_target_pairs={{0,1},{1,0},{2,3},{3,2},{4,5},{5,4},{6,7},{7,6},{8,9},{9,8},{10,11... | collective-permute-start | bytes 1769480 | tf_op jit(solution)/shard_map/ppermute | solution.py:26
  118.7 6.2 %collective-permute-start.5 = (f32[288,128]{1,0:T(8,128)S(1)}, f32[288,128]{1,0:T(8,128)S(1)}, u32[]{:S(2)}, u32[]{:S(2)}) collective-permute-start(f32[288,128]{1,0:T(8,128)S(1)} %get-tuple-element.28), channel_id=1, source_target_pairs={{0,8},{8,0},{16,24},{24,16},{1,9},{9,1},{17,25},{25,17},{2,10},{10... | collective-permute-start | bytes 442376 | tf_op jit(solution)/shard_map/ppermute | solution.py:26
  121.0 8.0 %collective-permute-start.6 = (f32[288,128]{1,0:T(8,128)S(1)}, f32[288,128]{1,0:T(8,128)S(1)}, u32[]{:S(2)}, u32[]{:S(2)}) collective-permute-start(f32[288,128]{1,0:T(8,128)S(1)} %get-tuple-element.30), channel_id=1, source_target_pairs={{0,16},{8,24},{16,0},{24,8},{1,17},{9,25},{17,1},{25,9},{2,18},{10... | collective-permute-start | bytes 442376 | tf_op jit(solution)/shard_map/ppermute | solution.py:26
  121.0 8.0 %collective-permute-start.7 = (f32[288,128]{1,0:T(8,128)S(1)}, f32[288,128]{1,0:T(8,128)S(1)}, u32[]{:S(2)}, u32[]{:S(2)}) collective-permute-start(f32[288,128]{1,0:T(8,128)S(1)} %get-tuple-element.29), channel_id=1, source_target_pairs={{0,24},{8,16},{16,8},{24,0},{1,25},{9,17},{17,9},{25,1},{2,26},{10... | collective-permute-start | bytes 442376 | tf_op jit(solution)/shard_map/ppermute | solution.py:26
  129.0 5.6 %collective-permute-start.10 = (f32[72,128]{1,0:T(8,128)S(1)}, f32[72,128]{1,0:T(8,128)S(1)}, u32[]{:S(2)}, u32[]{:S(2)}) collective-permute-start(f32[72,128]{1,0:T(8,128)S(1)} %get-tuple-element.40), channel_id=1, source_target_pairs={{0,6},{1,7},{2,4},{3,5},{4,2},{5,3},{6,0},{7,1},{8,14},{9,15},{10,... | collective-permute-start | bytes 110600 | tf_op jit(solution)/shard_map/ppermute | solution.py:26
  133.3 3.2 %collective-permute-start.8 = (f32[72,128]{1,0:T(8,128)S(1)}, f32[72,128]{1,0:T(8,128)S(1)}, u32[]{:S(2)}, u32[]{:S(2)}) collective-permute-start(f32[72,128]{1,0:T(8,128)S(1)} %get-tuple-element.39), channel_id=1, source_target_pairs={{0,2},{1,3},{2,0},{3,1},{4,6},{5,7},{6,4},{7,5},{8,10},{9,11},{10,... | collective-permute-start | bytes 110600 | tf_op jit(solution)/shard_map/ppermute | solution.py:26
  133.3 3.7 %collective-permute-start.9 = (f32[72,128]{1,0:T(8,128)S(1)}, f32[72,128]{1,0:T(8,128)S(1)}, u32[]{:S(2)}, u32[]{:S(2)}) collective-permute-start(f32[72,128]{1,0:T(8,128)S(1)} %get-tuple-element.41), channel_id=1, source_target_pairs={{0,4},{1,5},{2,6},{3,7},{4,0},{5,1},{6,2},{7,3},{8,12},{9,13},{10,... | collective-permute-start | bytes 110600 | tf_op jit(solution)/shard_map/ppermute | solution.py:26
  137.0 3.7 %collective-permute-start.11 = (f32[72,128]{1,0:T(8,128)S(1)}, f32[72,128]{1,0:T(8,128)S(1)}, u32[]{:S(2)}, u32[]{:S(2)}) collective-permute-start(f32[72,128]{1,0:T(8,128)S(1)} %add_add_fusion.1), channel_id=1, source_target_pairs={{0,2},{1,3},{2,0},{3,1},{4,6},{5,7},{6,4},{7,5},{8,10},{9,11},{10,... | collective-permute-start | bytes 110600 | tf_op jit(solution)/shard_map/ppermute | solution.py:26
  138.5 3.9 %collective-permute-start.12 = (f32[72,128]{1,0:T(8,128)S(1)}, f32[72,128]{1,0:T(8,128)S(1)}, u32[]{:S(2)}, u32[]{:S(2)}) collective-permute-start(f32[72,128]{1,0:T(8,128)S(1)} %add_add_fusion.1), channel_id=1, source_target_pairs={{0,4},{1,5},{2,6},{3,7},{4,0},{5,1},{6,2},{7,3},{8,12},{9,13},{10,... | collective-permute-start | bytes 110600 | tf_op jit(solution)/shard_map/ppermute | solution.py:26
  139.4 4.6 %collective-permute-start.13 = (f32[72,128]{1,0:T(8,128)S(1)}, f32[72,128]{1,0:T(8,128)S(1)}, u32[]{:S(2)}, u32[]{:S(2)}) collective-permute-start(f32[72,128]{1,0:T(8,128)S(1)} %add_add_fusion.1), channel_id=1, source_target_pairs={{0,6},{1,7},{2,4},{3,5},{4,2},{5,3},{6,0},{7,1},{8,14},{9,15},{10,... | collective-permute-start | bytes 110600 | tf_op jit(solution)/shard_map/ppermute | solution.py:26
  144.1 12.2 %copy-start.20 = (f32[128,128]{0,1:T(8,128)S(1)}, f32[128,128]{0,1:T(8,128)}, u32[]{:S(2)}) copy-start(f32[128,128]{0,1:T(8,128)} %fusion.61) | copy-start | bytes 196612
  144.1 12.2 %copy-start.25 = (f32[32,128]{1,0:T(8,128)S(1)}, f32[32,128]{1,0:T(8,128)}, u32[]{:S(2)}) copy-start(f32[32,128]{1,0:T(8,128)} %copy.119) | copy-start | bytes 49156
  144.1 12.2 %copy-start.27 = (pred[128,128]{0,1:T(8,128)(4,1)S(1)}, pred[128,128]{0,1:T(8,128)(4,1)}, u32[]{:S(2)}) copy-start(pred[128,128]{0,1:T(8,128)(4,1)} %iota_compare_fusion) | copy-start | bytes 49156
  144.1 12.2 %copy-start.43 = (f32[32,128]{1,0:T(8,128)S(1)}, f32[32,128]{1,0:T(8,128)}, u32[]{:S(2)}) copy-start(f32[32,128]{1,0:T(8,128)} %get-tuple-element.50) | copy-start | bytes 49156
  144.1 4.1 %collective-permute-start.14 = (f32[288,128]{1,0:T(8,128)S(1)}, f32[288,128]{1,0:T(8,128)S(1)}, u32[]{:S(2)}, u32[]{:S(2)}) collective-permute-start(f32[288,128]{1,0:T(8,128)S(1)} %get-tuple-element.34), channel_id=1, source_target_pairs={{0,8},{8,0},{16,24},{24,16},{1,9},{9,1},{17,25},{25,17},{2,10},{10... | collective-permute-start | bytes 442376 | tf_op jit(solution)/shard_map/ppermute | solution.py:26
  144.3 4.0 %collective-permute-start.15 = (f32[288,128]{1,0:T(8,128)S(1)}, f32[288,128]{1,0:T(8,128)S(1)}, u32[]{:S(2)}, u32[]{:S(2)}) collective-permute-start(f32[288,128]{1,0:T(8,128)S(1)} %get-tuple-element.34), channel_id=1, source_target_pairs={{0,16},{8,24},{16,0},{24,8},{1,17},{9,25},{17,1},{25,9},{2,18},{10... | collective-permute-start | bytes 442376 | tf_op jit(solution)/shard_map/ppermute | solution.py:26
  145.4 4.9 %collective-permute-start.16 = (f32[288,128]{1,0:T(8,128)S(1)}, f32[288,128]{1,0:T(8,128)S(1)}, u32[]{:S(2)}, u32[]{:S(2)}) collective-permute-start(f32[288,128]{1,0:T(8,128)S(1)} %get-tuple-element.34), channel_id=1, source_target_pairs={{0,24},{8,16},{16,8},{24,0},{1,25},{9,17},{17,9},{25,1},{2,26},{10... | collective-permute-start | bytes 442376 | tf_op jit(solution)/shard_map/ppermute | solution.py:26
  150.4 10.5 %collective-permute-start.17 = (f32[1152,128]{1,0:T(8,128)S(1)}, f32[1152,128]{1,0:T(8,128)}, u32[]{:S(2)}, u32[]{:S(2)}) collective-permute-start(f32[1152,128]{1,0:T(8,128)S(1)} %get-tuple-element.22), channel_id=1, source_target_pairs={{0,1},{1,0},{2,3},{3,2},{4,5},{5,4},{6,7},{7,6},{8,9},{9,8},{10,11... | collective-permute-start | bytes 1769480 | tf_op jit(solution)/shard_map/ppermute | solution.py:26
  156.3 3.3 %copy-start.9 = (bf16[32,64,128]{2,1,0:T(8,128)(2,1)S(1)}, bf16[32,64,128]{2,1,0:T(8,128)(2,1)}, u32[]{:S(2)}) copy-start(bf16[32,64,128]{2,1,0:T(8,128)(2,1)} %copy-done.8) | copy-start | bytes 1572868
  (16 other events, 31.0 us)

commit v11 on v8

--- a/solution.py
+++ b/solution.py
@@ -143,14 +143,13 @@
     adjoint_in = jnp.zeros((head_count, head_dim, state_dim), fl)
     if n_blocks == 4:
         sent = grad_out[0].astype(fl)
-        first = lax.ppermute(sent, "tm", [(3, 2), (1, 0)])
-        second = lax.ppermute(sent, "tm", [(3, 1), (2, 0)])
-        third = lax.ppermute(second, "tm", [(0, 1)])
-        fourth = lax.ppermute(first, "tm", [(2, 0)])
+        along_x = lax.ppermute(sent, "tm", [(3, 2), (1, 0)])
+        along_y = lax.ppermute(sent, "tm", [(3, 1), (2, 0)])
+        diagonal = lax.ppermute(sent, "tm", [(2, 1), (3, 0)])
         seen = [
-            first,
-            jnp.where(my_block == 1, third, second),
-            jnp.where(my_block == 2, first, jnp.where(my_block == 1, second, fourth)),
+            along_x,
+            jnp.where(my_block == 1, diagonal, along_y),
+            jnp.where(my_block == 2, along_x, jnp.where(my_block == 1, along_y, diagonal)),
         ]
         c_all = projected_all[:, :, inner_width + state_dim :]
         for k in range(n_blocks - 1, 0, -1):

time: 136 us -> 160 us (1.18)
  waiting for transfers between devices: 33.9 us -> 52.1 us
  local copies, waits for them, and re-layouts: 21.5 us -> 27.5 us
  starting transfers between devices: 43 us -> 37.2 us
  matrix products: 23.2 us -> 28 us
    all_to_all x1, waiting for transfers between devices: 13.5 us -> 33.5 us  [on_device(): lax.all_to_all(outgoing, ('tm', 'series'), split_axis=0, concat_axis=1, t...]
    ppermute x4 -> x3, starting transfers between devices: 10.1 us -> 3.86 us  [the longest x1 1.29 us: on_device(): along_y = lax.ppermute(sent, 'tm', [(3, 1), (2, 0)])]
    slice x2, local copies, waits for them, and re-layouts: 0.33 us -> 3.98 us  [on_device(): x_heads = projected[:, :inner_width].reshape(tok_rows, head_count, head_dim)]
    ppermute x4 -> x3, waiting for transfers between devices: 1.9 us -> 0.01 us  [the longest x1 0.01 us: on_device(): diagonal = lax.ppermute(sent, 'tm', [(2, 1), (3, 0)])]
    unnamed x81 -> x87, local copies, waits for them, and re-layouts: 5.32 us -> 5.32 us
  transfers between devices with their start and end apart: 19 -> 18, of which waited for: 13 -> 11; matrix products, arithmetic and copies ran while one was open for 34% -> 36% of each run, Pallas kernels for 0% -> 0%
where the time goes in v11:
time: 160 us; the launch traced here: 159 us
  waiting for transfers between devices  52.1 us (33%)
  starting transfers between devices  37.2 us (23%)
  matrix products  28 us (18%)
  local copies, waits for them, and re-layouts  27.5 us (17%)
  other arithmetic  13.2 us (8%)
    all_to_all x1, waiting for transfers between devices, on_device(): lax.all_to_all(outgoing, ('tm', 'series'), split_axis=0, concat_axis=1, t...  33.5 us
    ppermute x14, starting transfers between devices, exchange(): return lax.ppermute(value, axis, pairs)  21.1 us
    ppermute x14, waiting for transfers between devices, exchange(): return lax.ppermute(value, axis, pairs)  18.6 us
    all_to_all x1, starting transfers between devices, on_device(): lax.all_to_all(outgoing, ('tm', 'series'), split_axis=0, concat_axis=1, t...  12.2 us
    convert_element_type x1, local copies, waits for them, and re-layouts, on_device(): xw_all = (x_all * tail_all[..., None]).astype(half)  5.41 us
    unnamed x87, local copies, waits for them, and re-layouts  5.32 us
    exp x4, local copies, waits for them, and re-layouts, on_device(): later_weighted = (later * jnp.exp(cum_all[k])[:, :, None]).astype(half)  5.28 us
    dot_general x1, matrix products, on_device(): picked = jnp.dot(onehot, bin_table, precision=lax.Precision.HIGHEST)  4.14 us
  transfers between devices with their start and end apart: 18, of which 11 were waited for; matrix products, arithmetic and copies ran while one was open for 36% of the time, Pallas kernels for 0%

profile of v11, /device:TPU:1, one launch (start us, length us, event | category | flops | bytes accessed | tf_op | source)
XLA Modules:
  0.0 159.5 jit_solution(4956691590731969142)
XLA Ops:
  0.7 1.4 copy.102
  2.0 1.0 convert_bitcast_fusion
  3.1 1.3 collective-permute-start
  4.4 1.3 collective-permute-start.1
  5.7 1.3 collective-permute-start.2
  8.3 12.2 %all-to-all-start = ((f32[32,1,16]{2,1,0:T(1,128)}), f32[32,1,16]{2,1,0:T(1,128)S(1)}, u32[]{:S(2)}, u32[]{:S(2)}) async-start(f32[32,1,16]{2,1,0:T(1,128)} %bitcast), calls=%async_computation | async-start | bytes 32768 | tf_op jit(solution)/shard_map/all_to_all | solution.py:92
  21.3 33.5 %all-to-all-done = f32[32,1,16]{2,1,0:T(1,128)S(1)} async-done(((f32[32,1,16]{2,1,0:T(1,128)}), f32[32,1,16]{2,1,0:T(1,128)S(1)}, u32[]{:S(2)}, u32[]{:S(2)}) %all-to-all-start) | async-done | bytes 2080 | tf_op jit(solution)/shard_map/all_to_all | solution.py:92
  56.1 1.5 convert_reduce_fusion
  58.4 4.1 %fusion = f32[512,4]{0,1:T(4,128)S(1)} fusion(f32[4096]{0:T(1024)S(1)} %get-tuple-element.39, f32[4096]{0:T(1024)S(1)} %convert_element_type.117, f32[512]{0:T(512)S(1)} %le.22, f32[4096,1]{0,1:T(1,128)S(1)} %bitcast.230, f32[4096,1]{0,1:T(1,128)S(1)} %bitcast.222, f32[4096,1]{0,1:T(1,128)S(1)} %bitcast.221, f32[4096,1]{0,1:T(1,128)S(1)} %sub.69), kind=kOutput, calls=%fused_computation.3 | convolution fusion | flops 107003904 | bytes 108544 | tf_op jit(solution)/shard_map/dot_general | solution.py:101
  62.6 1.1 compare_select_fusion
  65.5 1.6 %convolution_convert_fusion = bf16[512,2304]{1,0:T(8,128)(2,1)S(1)} fusion(bf16[128,2304]{1,0:T(8,128)(2,1)S(1)} %copy-done, f32[128]{0:T(128)S(1)} %add_multiply_fusion, f32[512]{0:T(512)S(1)} %bitcast.232), kind=kOutput, calls=%fused_computation.4 | convolution fusion | flops 303300608 | bytes 2951680 | tf_op jit(solution)/shard_map/dot_general | solution.py:122
  68.1 1.4 convolution_convert_fusion.1
  71.9 1.5 fusion.77
  73.5 1.9 %slice.125 = bf16[128,2048]{1,0:T(8,128)(2,1)} slice(bf16[128,2304]{1,0:T(8,128)(2,1)} %convolution_convert_fusion.1), slice={[0:128], [0:2048]} | slice | bytes 1048576 | tf_op jit(solution)/shard_map/slice | solution.py:113
  76.0 2.1 %copy.91 = bf16[128,2048]{0,1:T(8,128)(2,1)} copy(bf16[128,2048]{1,0:T(8,128)(2,1)} %slice.125) | data formatting | bytes 1048576 | tf_op jit(solution)/shard_map/slice | solution.py:113
  78.1 2.6 %fusion.5 = bf16[128,128]{0,1:T(8,128)(2,1)S(1)} fusion(bf16[128,32,64]{0,2,1:T(8,128)(2,1)} %bitcast.210, bf16[128,32,64]{0,2,1:T(8,128)(2,1)S(1)} %bitcast.200, f32[32,128]{1,0:T(8,128)} %get-tuple-element.44, f32[32,128]{1,0:T(8,128)} %copy.94, pred[128,128]{0,1:T(8,128)(4,1)} %iota_compare_fusion), kind=kOutput, calls=%fused_computation.13 | convolution fusion | flops 70238208 | bytes 1130496 | tf_op jit(solution)/shard_map/thp,shp->hts/dot_general | solution.py:185
  80.8 1.6 %fusion.79 = f32[128,128]{0,1:T(8,128)} fusion(bf16[128,2304]{1,0:T(8,128)(2,1)} %convolution_convert_fusion.1, bf16[128,128]{0,1:T(8,128)(2,1)S(1)} %fusion.5), kind=kOutput, calls=%fused_computation.141 | convolution fusion | flops 4194304 | bytes 131072 | tf_op jit(solution)/shard_map/dot_general | solution.py:187
  82.4 1.6 fusion.74
  84.7 2.5 %slice_convert_fusion = f32[4,128,2048]{2,1,0:T(8,128)} fusion(bf16[4,128,2304]{2,1,0:T(8,128)(2,1)S(1)} %bitcast.195), kind=kLoop, calls=%fused_computation.11 | loop fusion | flops 1048576 | bytes 6291456 | tf_op jit(solution)/shard_map/convert_element_type | solution.py:132
  89.1 1.5 copy.105
  90.7 1.5 copy.106
  92.2 1.5 copy.107
  93.7 1.0 copy.100
  94.7 5.4 %copy.98 = f32[4,128,2048]{1,2,0:T(8,128)} copy(f32[4,128,2048]{2,1,0:T(8,128)} %slice_convert_fusion) | data formatting | bytes 8388608 | tf_op jit(solution)/shard_map/convert_element_type | solution.py:132
  101.2 2.9 %fusion.4 = f32[4,32,64,128]{3,2,1,0:T(8,128)S(1)} fusion(f32[4,128,32,64]{1,3,2,0:T(8,128)} %bitcast.194, f32[4,128,32]{1,2,0:T(8,128)S(1)} %copy.100, bf16[4,128,2304]{2,1,0:T(8,128)(2,1)S(1)} %bitcast.196), kind=kOutput, calls=%fused_computation.10 | convolution fusion | flops 270532608 | bytes 8585216 | tf_op jit(solution)/shard_map/bthp,btn->bhpn/dot_general | solution.py:133
  104.8 1.3 copy-done.1
  106.1 1.3 convolution_bitcast_fusion
  107.5 2.2 %fusion.22 = (bf16[128,2048]{0,1:T(8,128)(2,1)S(1)}, bf16[128,2048]{0,1:T(8,128)(2,1)S(1)}, bf16[128,2048]{0,1:T(8,128)(2,1)S(1)}) fusion(f32[128,2048]{0,1:T(8,128)} %collective-permute-done.2, f32[128,2048]{0,1:T(8,128)} %collective-permute-done.1, f32[128,32]{0,1:T(8,128)S(1)} %copy-done.11, pred[]{:T(512)S(6)} %eq.19, f32[128,32]{0,1:T(8,128)S(1)} %copy-done.10, ...), kind=kLoop, calls=%fused_computation.52 | loop fusion | flops 2359296 | bytes 4767746 | tf_op jit(solution)/shard_map/convert_element_type | solution.py:157
  110.7 1.1 fusion.14
  113.3 1.6 %collective-permute-done.3 = f32[1152,128]{1,0:T(8,128)S(1)} collective-permute-done((f32[1152,128]{1,0:T(8,128)S(1)}, f32[1152,128]{1,0:T(8,128)S(1)}, u32[]{:S(2)}, u32[]{:S(2)}) %collective-permute-start.3) | collective-permute-done | bytes 589856 | tf_op jit(solution)/shard_map/ppermute | solution.py:26
  115.0 2.6 %collective-permute-start.4 = (f32[288,128]{1,0:T(8,128)S(1)}, f32[288,128]{1,0:T(8,128)S(1)}, u32[]{:S(2)}, u32[]{:S(2)}) collective-permute-start(f32[288,128]{1,0:T(8,128)S(1)} %get-tuple-element.23), channel_id=1, source_target_pairs={{0,8},{8,0},{16,24},{24,16},{1,9},{9,1},{17,25},{25,17},{2,10},{10... | collective-permute-start | bytes 442376 | tf_op jit(solution)/shard_map/ppermute | solution.py:26
  117.7 1.3 collective-permute-start.6
  118.9 2.7 %collective-permute-done.4 = f32[288,128]{1,0:T(8,128)S(1)} collective-permute-done((f32[288,128]{1,0:T(8,128)S(1)}, f32[288,128]{1,0:T(8,128)S(1)}, u32[]{:S(2)}, u32[]{:S(2)}) %collective-permute-start.4) | collective-permute-done | bytes 147488 | tf_op jit(solution)/shard_map/ppermute | solution.py:26
  121.6 4.1 %collective-permute-done.5 = f32[288,128]{1,0:T(8,128)S(1)} collective-permute-done((f32[288,128]{1,0:T(8,128)S(1)}, f32[288,128]{1,0:T(8,128)S(1)}, u32[]{:S(2)}, u32[]{:S(2)}) %collective-permute-start.5) | collective-permute-done | bytes 147488 | tf_op jit(solution)/shard_map/ppermute | solution.py:26
  125.7 2.2 %collective-permute-start.7 = (f32[72,128]{1,0:T(8,128)S(1)}, f32[72,128]{1,0:T(8,128)S(1)}, u32[]{:S(2)}, u32[]{:S(2)}) collective-permute-start(f32[72,128]{1,0:T(8,128)S(1)} %get-tuple-element.35), channel_id=1, source_target_pairs={{0,2},{1,3},{2,0},{3,1},{4,6},{5,7},{6,4},{7,5},{8,10},{9,11},{10,... | collective-permute-start | bytes 110600 | tf_op jit(solution)/shard_map/ppermute | solution.py:26
  127.9 2.3 %collective-permute-start.8 = (f32[72,128]{1,0:T(8,128)S(1)}, f32[72,128]{1,0:T(8,128)S(1)}, u32[]{:S(2)}, u32[]{:S(2)}) collective-permute-start(f32[72,128]{1,0:T(8,128)S(1)} %get-tuple-element.37), channel_id=1, source_target_pairs={{0,4},{1,5},{2,6},{3,7},{4,0},{5,1},{6,2},{7,3},{8,12},{9,13},{10,... | collective-permute-start | bytes 110600 | tf_op jit(solution)/shard_map/ppermute | solution.py:26
  130.2 1.8 %collective-permute-done.8 = f32[72,128]{1,0:T(8,128)S(1)} collective-permute-done((f32[72,128]{1,0:T(8,128)S(1)}, f32[72,128]{1,0:T(8,128)S(1)}, u32[]{:S(2)}, u32[]{:S(2)}) %collective-permute-start.8) | collective-permute-done | bytes 36896 | tf_op jit(solution)/shard_map/ppermute | solution.py:26
  132.0 2.8 %collective-permute-done.9 = f32[72,128]{1,0:T(8,128)S(1)} collective-permute-done((f32[72,128]{1,0:T(8,128)S(1)}, f32[72,128]{1,0:T(8,128)S(1)}, u32[]{:S(2)}, u32[]{:S(2)}) %collective-permute-start.9) | collective-permute-done | bytes 36896 | tf_op jit(solution)/shard_map/ppermute | solution.py:26
  135.6 2.9 %collective-permute-start.12 = (f32[72,128]{1,0:T(8,128)S(1)}, f32[72,128]{1,0:T(8,128)S(1)}, u32[]{:S(2)}, u32[]{:S(2)}) collective-permute-start(f32[72,128]{1,0:T(8,128)S(1)} %add_add_fusion.1), channel_id=1, source_target_pairs={{0,6},{1,7},{2,4},{3,5},{4,2},{5,3},{6,0},{7,1},{8,14},{9,15},{10,... | collective-permute-start | bytes 110600 | tf_op jit(solution)/shard_map/ppermute | solution.py:26
  138.7 1.9 %collective-permute-done.12 = f32[72,128]{1,0:T(8,128)S(1)} collective-permute-done((f32[72,128]{1,0:T(8,128)S(1)}, f32[72,128]{1,0:T(8,128)S(1)}, u32[]{:S(2)}, u32[]{:S(2)}) %collective-permute-start.12) | collective-permute-done | bytes 36896 | tf_op jit(solution)/shard_map/ppermute | solution.py:26
  140.9 1.1 collective-permute-start.14
  142.0 1.4 collective-permute-start.15
  143.4 1.3 collective-permute-done.13
  144.9 2.0 %collective-permute-done.15 = f32[288,128]{1,0:T(8,128)S(1)} collective-permute-done((f32[288,128]{1,0:T(8,128)S(1)}, f32[288,128]{1,0:T(8,128)S(1)}, u32[]{:S(2)}, u32[]{:S(2)}) %collective-permute-start.15) | collective-permute-done | bytes 147488 | tf_op jit(solution)/shard_map/ppermute | solution.py:26
  147.1 5.9 %collective-permute-start.16 = (f32[1152,128]{1,0:T(8,128)S(1)}, f32[1152,128]{1,0:T(8,128)S(1)}, u32[]{:S(2)}, u32[]{:S(2)}) collective-permute-start(f32[1152,128]{1,0:T(8,128)S(1)} %get-tuple-element.17), channel_id=1, source_target_pairs={{0,1},{1,0},{2,3},{3,2},{4,5},{5,4},{6,7},{7,6},{8,9},{9,8},{10,11... | collective-permute-start | bytes 1769480 | tf_op jit(solution)/shard_map/ppermute | solution.py:26
  153.0 1.3 convolution_bitcast_fusion.1
  154.3 2.4 %fusion.12 = bf16[128,32,64]{0,2,1:T(8,128)(2,1)S(1)} fusion(f32[128,32,64]{0,2,1:T(8,128)S(1)} %convolution_bitcast_fusion.1, f32[4,32,64,128]{3,2,1,0:T(8,128)} %copy-done.1, f32[128,32]{0,1:T(8,128)S(1)} %copy.101, f32[32]{0:T(128)S(1)} %copy-done.36, f32[32]{0:T(128)S(1)} %copy-done.33, f32[32]{0:T(128)S(1)} %copy-done.30, pred[]{:T(512)S(6)} %gt.24, ...), kind=kOutput, calls=%fused_computation.35 | convolution fusion | flops 70254592 | bytes 4768131 | tf_op jit(solution)/shard_map/tn,hpn->thp/dot_general | solution.py:175
  158.1 1.4 copy.110
  (161 shorter events, 19.8 us)
Async XLA Ops:
  0.6 64.8 %copy-start = (bf16[128,2304]{1,0:T(8,128)(2,1)S(1)}, bf16[128,2304]{1,0:T(8,128)(2,1)}, u32[]{:S(2)}) copy-start(bf16[128,2304]{1,0:T(8,128)(2,1)} %param.11) | copy-start | bytes 1769476
  0.6 6.3 %copy-start.38 = (s32[8]{0:T(128)S(1)}, s32[8]{0:T(128)}, u32[]{:S(2)}) copy-start(s32[8]{0:T(128)} %param.9) | copy-start | bytes 100
  0.7 6.4 %copy-start.8 = (s32[8,16]{1,0:T(8,128)S(1)}, s32[8,16]{1,0:T(8,128)}, u32[]{:S(2)}) copy-start(s32[8,16]{1,0:T(8,128)} %param.8) | copy-start | bytes 1540
  0.7 20.5 %copy-start.19 = (s32[4096]{0:T(1024)S(1)}, s32[4096]{0:T(1024)}, u32[]{:S(2)}) copy-start(s32[4096]{0:T(1024)} %param.10) | copy-start | bytes 49156
  3.1 104.3 %collective-permute-start = (f32[128,2048]{0,1:T(8,128)}, f32[128,2048]{0,1:T(8,128)}, u32[]{:S(2)}, u32[]{:S(2)}) collective-permute-start(f32[128,2048]{0,1:T(8,128)} %convert_bitcast_fusion), channel_id=1, source_target_pairs={{24,16},{8,0},{25,17},{9,1},{26,18},{10,2},{27,19},{11,3},{28,20},... | collective-permute-start | bytes 3145736 | tf_op jit(solution)/shard_map/ppermute | solution.py:146
  4.4 103.0 %collective-permute-start.1 = (f32[128,2048]{0,1:T(8,128)}, f32[128,2048]{0,1:T(8,128)}, u32[]{:S(2)}, u32[]{:S(2)}) collective-permute-start(f32[128,2048]{0,1:T(8,128)} %convert_bitcast_fusion), channel_id=1, source_target_pairs={{24,8},{16,0},{25,9},{17,1},{26,10},{18,2},{27,11},{19,3},{28,12},... | collective-permute-start | bytes 3145736 | tf_op jit(solution)/shard_map/ppermute | solution.py:147
  5.7 101.8 %collective-permute-start.2 = (f32[128,2048]{0,1:T(8,128)}, f32[128,2048]{0,1:T(8,128)}, u32[]{:S(2)}, u32[]{:S(2)}) collective-permute-start(f32[128,2048]{0,1:T(8,128)} %convert_bitcast_fusion), channel_id=1, source_target_pairs={{16,8},{24,0},{17,9},{25,1},{18,10},{26,2},{19,11},{27,3},{20,12},... | collective-permute-start | bytes 3145736 | tf_op jit(solution)/shard_map/ppermute | solution.py:148
  8.3 46.6 %all-to-all-start = ((f32[32,1,16]{2,1,0:T(1,128)}), f32[32,1,16]{2,1,0:T(1,128)S(1)}, u32[]{:S(2)}, u32[]{:S(2)}) async-start(f32[32,1,16]{2,1,0:T(1,128)} %bitcast), calls=%async_computation | async-start | bytes 32768 | tf_op jit(solution)/shard_map/all_to_all | solution.py:92
  21.3 46.8 %copy-start.24 = (f32[128]{0:T(128)}, f32[128]{0:T(128)S(1)}, u32[]{:S(2)}) copy-start(f32[128]{0:T(128)S(1)} %add_multiply_fusion) | copy-start | bytes 1540
  58.3 4.2 %copy-start.37 = (bf16[128,32]{0,1:T(8,128)(2,1)S(1)}, bf16[128,32]{0,1:T(8,128)(2,1)}, u32[]{:S(2)}) copy-start(bf16[128,32]{0,1:T(8,128)(2,1)} %param.12) | copy-start | bytes 24580
  58.3 4.2 %copy-start.39 = (f32[32]{0:T(128)S(1)}, f32[32]{0:T(128)}, u32[]{:S(2)}) copy-start(f32[32]{0:T(128)} %param.13) | copy-start | bytes 388
  58.4 5.5 %copy-start.26 = (f32[32]{0:T(128)S(1)}, f32[32]{0:T(128)}, u32[]{:S(2)}) copy-start(f32[32]{0:T(128)} %param.14) | copy-start | bytes 388
  67.1 2.5 %copy-start.27 = (f32[1,128]{1,0:T(1,128)}, f32[1,128]{1,0:T(1,128)S(1)}, u32[]{:S(2)}) copy-start(f32[1,128]{1,0:T(1,128)S(1)} %constant_dynamic-slice_fusion.7) | copy-start | bytes 1540
  78.1 5.8 %copy-start.20 = (f32[4,1,32]{2,1,0:T(1,128)S(1)}, f32[4,1,32]{2,1,0:T(1,128)}, u32[]{:S(2)}) copy-start(f32[4,1,32]{2,1,0:T(1,128)} %slice.128) | copy-start | bytes 1540
  78.1 5.8 %copy-start.3 = (f32[512,32]{1,0:T(8,128)S(1)}, f32[512,32]{1,0:T(8,128)}, u32[]{:S(2)}) copy-start(f32[512,32]{1,0:T(8,128)} %copy-done.2) | copy-start | bytes 196612
  78.1 5.8 %copy-start.5 = (f32[4,128,32]{2,1,0:T(8,128)S(1)}, f32[4,128,32]{2,1,0:T(8,128)}, u32[]{:S(2)}) copy-start(f32[4,128,32]{2,1,0:T(8,128)} %copy-done.4) | copy-start | bytes 196612
  84.7 2.5 %copy-start.14 = (f32[128,32]{0,1:T(8,128)S(1)}, f32[128,32]{0,1:T(8,128)}, u32[]{:S(2)}) copy-start(f32[128,32]{0,1:T(8,128)} %copy-done.13) | copy-start | bytes 49156
  84.7 2.5 %copy-start.34 = (f32[32]{0:T(128)S(1)}, f32[32]{0:T(128)}, u32[]{:S(2)}) copy-start(f32[32]{0:T(128)} %slice_bitcast_fusion.8) | copy-start | bytes 388
  101.2 2.9 %copy-start.18 = (f32[128,128]{0,1:T(8,128)S(1)}, f32[128,128]{0,1:T(8,128)}, u32[]{:S(2)}) copy-start(f32[128,128]{0,1:T(8,128)} %fusion.74) | copy-start | bytes 196612
  101.2 2.9 %copy-start.29 = (f32[32]{0:T(128)S(1)}, f32[32]{0:T(128)}, u32[]{:S(2)}) copy-start(f32[32]{0:T(128)} %get-tuple-element.43) | copy-start | bytes 388
  101.2 2.9 %copy-start.32 = (f32[32]{0:T(128)S(1)}, f32[32]{0:T(128)}, u32[]{:S(2)}) copy-start(f32[32]{0:T(128)} %get-tuple-element.42) | copy-start | bytes 388
  101.2 2.9 %copy-start.35 = (f32[32]{0:T(128)S(1)}, f32[32]{0:T(128)}, u32[]{:S(2)}) copy-start(f32[32]{0:T(128)} %get-tuple-element.41) | copy-start | bytes 388
  104.1 2.0 %copy-start.1 = (f32[4,32,64,128]{3,2,1,0:T(8,128)}, f32[4,32,64,128]{3,2,1,0:T(8,128)S(1)}, u32[]{:S(2)}) copy-start(f32[4,32,64,128]{3,2,1,0:T(8,128)S(1)} %fusion.4) | copy-start | bytes 12582916
  104.1 1.9 %copy-start.15 = (f32[128,128]{0,1:T(8,128)S(1)}, f32[128,128]{0,1:T(8,128)}, u32[]{:S(2)}) copy-start(f32[128,128]{0,1:T(8,128)} %fusion.77) | copy-start | bytes 196612
  104.2 1.9 %copy-start.21 = (f32[32,128]{1,0:T(8,128)S(1)}, f32[32,128]{1,0:T(8,128)}, u32[]{:S(2)}) copy-start(f32[32,128]{1,0:T(8,128)} %copy.94) | copy-start | bytes 49156
  104.2 1.9 %copy-start.22 = (pred[128,128]{0,1:T(8,128)(4,1)S(1)}, pred[128,128]{0,1:T(8,128)(4,1)}, u32[]{:S(2)}) copy-start(pred[128,128]{0,1:T(8,128)(4,1)} %iota_compare_fusion) | copy-start | bytes 49156
  104.2 1.9 %copy-start.40 = (f32[32,128]{1,0:T(8,128)S(1)}, f32[32,128]{1,0:T(8,128)}, u32[]{:S(2)}) copy-start(f32[32,128]{1,0:T(8,128)} %get-tuple-element.44) | copy-start | bytes 49156
  107.4 2.3 %copy-start.31 = (f32[32]{0:T(128)S(1)}, f32[32]{0:T(128)}, u32[]{:S(2)}) copy-start(f32[32]{0:T(128)} %get-tuple-element.40) | copy-start | bytes 388
  110.3 1.5 copy-start.6
  110.3 1.5 copy-start.17
  112.8 2.1 %collective-permute-start.3 = (f32[1152,128]{1,0:T(8,128)S(1)}, f32[1152,128]{1,0:T(8,128)S(1)}, u32[]{:S(2)}, u32[]{:S(2)}) collective-permute-start(f32[1152,128]{1,0:T(8,128)S(1)} %constant_dynamic-slice_fusion.6), channel_id=1, source_target_pairs={{0,1},{1,0},{2,3},{3,2},{4,5},{5,4},{6,7},{7,6},{8,9},{9,8},{10,11... | collective-permute-start | bytes 1769480 | tf_op jit(solution)/shard_map/ppermute | solution.py:26
  115.0 6.6 %collective-permute-start.4 = (f32[288,128]{1,0:T(8,128)S(1)}, f32[288,128]{1,0:T(8,128)S(1)}, u32[]{:S(2)}, u32[]{:S(2)}) collective-permute-start(f32[288,128]{1,0:T(8,128)S(1)} %get-tuple-element.23), channel_id=1, source_target_pairs={{0,8},{8,0},{16,24},{24,16},{1,9},{9,1},{17,25},{25,17},{2,10},{10... | collective-permute-start | bytes 442376 | tf_op jit(solution)/shard_map/ppermute | solution.py:26
  117.7 8.0 %collective-permute-start.5 = (f32[288,128]{1,0:T(8,128)S(1)}, f32[288,128]{1,0:T(8,128)S(1)}, u32[]{:S(2)}, u32[]{:S(2)}) collective-permute-start(f32[288,128]{1,0:T(8,128)S(1)} %get-tuple-element.25), channel_id=1, source_target_pairs={{0,16},{8,24},{16,0},{24,8},{1,17},{9,25},{17,1},{25,9},{2,18},{10... | collective-permute-start | bytes 442376 | tf_op jit(solution)/shard_map/ppermute | solution.py:26
  117.7 8.0 %collective-permute-start.6 = (f32[288,128]{1,0:T(8,128)S(1)}, f32[288,128]{1,0:T(8,128)S(1)}, u32[]{:S(2)}, u32[]{:S(2)}) collective-permute-start(f32[288,128]{1,0:T(8,128)S(1)} %get-tuple-element.24), channel_id=1, source_target_pairs={{0,24},{8,16},{16,8},{24,0},{1,25},{9,17},{17,9},{25,1},{2,26},{10... | collective-permute-start | bytes 442376 | tf_op jit(solution)/shard_map/ppermute | solution.py:26
  125.7 4.5 %collective-permute-start.7 = (f32[72,128]{1,0:T(8,128)S(1)}, f32[72,128]{1,0:T(8,128)S(1)}, u32[]{:S(2)}, u32[]{:S(2)}) collective-permute-start(f32[72,128]{1,0:T(8,128)S(1)} %get-tuple-element.35), channel_id=1, source_target_pairs={{0,2},{1,3},{2,0},{3,1},{4,6},{5,7},{6,4},{7,5},{8,10},{9,11},{10,... | collective-permute-start | bytes 110600 | tf_op jit(solution)/shard_map/ppermute | solution.py:26
  127.9 4.1 %collective-permute-start.8 = (f32[72,128]{1,0:T(8,128)S(1)}, f32[72,128]{1,0:T(8,128)S(1)}, u32[]{:S(2)}, u32[]{:S(2)}) collective-permute-start(f32[72,128]{1,0:T(8,128)S(1)} %get-tuple-element.37), channel_id=1, source_target_pairs={{0,4},{1,5},{2,6},{3,7},{4,0},{5,1},{6,2},{7,3},{8,12},{9,13},{10,... | collective-permute-start | bytes 110600 | tf_op jit(solution)/shard_map/ppermute | solution.py:26
  130.2 4.6 %collective-permute-start.9 = (f32[72,128]{1,0:T(8,128)S(1)}, f32[72,128]{1,0:T(8,128)S(1)}, u32[]{:S(2)}, u32[]{:S(2)}) collective-permute-start(f32[72,128]{1,0:T(8,128)S(1)} %get-tuple-element.36), channel_id=1, source_target_pairs={{0,6},{1,7},{2,4},{3,5},{4,2},{5,3},{6,0},{7,1},{8,14},{9,15},{10,... | collective-permute-start | bytes 110600 | tf_op jit(solution)/shard_map/ppermute | solution.py:26
  134.9 3.6 %collective-permute-start.10 = (f32[72,128]{1,0:T(8,128)S(1)}, f32[72,128]{1,0:T(8,128)S(1)}, u32[]{:S(2)}, u32[]{:S(2)}) collective-permute-start(f32[72,128]{1,0:T(8,128)S(1)} %add_add_fusion.1), channel_id=1, source_target_pairs={{0,2},{1,3},{2,0},{3,1},{4,6},{5,7},{6,4},{7,5},{8,10},{9,11},{10,... | collective-permute-start | bytes 110600 | tf_op jit(solution)/shard_map/ppermute | solution.py:26
  134.9 3.8 %collective-permute-start.11 = (f32[72,128]{1,0:T(8,128)S(1)}, f32[72,128]{1,0:T(8,128)S(1)}, u32[]{:S(2)}, u32[]{:S(2)}) collective-permute-start(f32[72,128]{1,0:T(8,128)S(1)} %add_add_fusion.1), channel_id=1, source_target_pairs={{0,4},{1,5},{2,6},{3,7},{4,0},{5,1},{6,2},{7,3},{8,12},{9,13},{10,... | collective-permute-start | bytes 110600 | tf_op jit(solution)/shard_map/ppermute | solution.py:26
  135.6 5.0 %collective-permute-start.12 = (f32[72,128]{1,0:T(8,128)S(1)}, f32[72,128]{1,0:T(8,128)S(1)}, u32[]{:S(2)}, u32[]{:S(2)}) collective-permute-start(f32[72,128]{1,0:T(8,128)S(1)} %add_add_fusion.1), channel_id=1, source_target_pairs={{0,6},{1,7},{2,4},{3,5},{4,2},{5,3},{6,0},{7,1},{8,14},{9,15},{10,... | collective-permute-start | bytes 110600 | tf_op jit(solution)/shard_map/ppermute | solution.py:26
  140.7 12.3 %copy-start.7 = (bf16[128,2048]{0,1:T(8,128)(2,1)S(1)}, bf16[128,2048]{0,1:T(8,128)(2,1)}, u32[]{:S(2)}) copy-start(bf16[128,2048]{0,1:T(8,128)(2,1)} %copy.91) | copy-start | bytes 1572868
  140.7 12.3 %copy-start.16 = (f32[128,128]{0,1:T(8,128)S(1)}, f32[128,128]{0,1:T(8,128)}, u32[]{:S(2)}) copy-start(f32[128,128]{0,1:T(8,128)} %fusion.77) | copy-start | bytes 196612
  140.7 12.3 %copy-start.23 = (pred[128,128]{0,1:T(8,128)(4,1)S(1)}, pred[128,128]{0,1:T(8,128)(4,1)}, u32[]{:S(2)}) copy-start(pred[128,128]{0,1:T(8,128)(4,1)} %iota_compare_fusion) | copy-start | bytes 49156
  140.7 12.3 %copy-start.41 = (f32[32,128]{1,0:T(8,128)S(1)}, f32[32,128]{1,0:T(8,128)}, u32[]{:S(2)}) copy-start(f32[32,128]{1,0:T(8,128)} %get-tuple-element.44) | copy-start | bytes 49156
  140.7 4.1 %collective-permute-start.13 = (f32[288,128]{1,0:T(8,128)S(1)}, f32[288,128]{1,0:T(8,128)S(1)}, u32[]{:S(2)}, u32[]{:S(2)}) collective-permute-start(f32[288,128]{1,0:T(8,128)S(1)} %get-tuple-element.30), channel_id=1, source_target_pairs={{0,8},{8,0},{16,24},{24,16},{1,9},{9,1},{17,25},{25,17},{2,10},{10... | collective-permute-start | bytes 442376 | tf_op jit(solution)/shard_map/ppermute | solution.py:26
  140.9 4.0 %collective-permute-start.14 = (f32[288,128]{1,0:T(8,128)S(1)}, f32[288,128]{1,0:T(8,128)S(1)}, u32[]{:S(2)}, u32[]{:S(2)}) collective-permute-start(f32[288,128]{1,0:T(8,128)S(1)} %get-tuple-element.30), channel_id=1, source_target_pairs={{0,16},{8,24},{16,0},{24,8},{1,17},{9,25},{17,1},{25,9},{2,18},{10... | collective-permute-start | bytes 442376 | tf_op jit(solution)/shard_map/ppermute | solution.py:26
  142.0 4.9 %collective-permute-start.15 = (f32[288,128]{1,0:T(8,128)S(1)}, f32[288,128]{1,0:T(8,128)S(1)}, u32[]{:S(2)}, u32[]{:S(2)}) collective-permute-start(f32[288,128]{1,0:T(8,128)S(1)} %get-tuple-element.30), channel_id=1, source_target_pairs={{0,24},{8,16},{16,8},{24,0},{1,25},{9,17},{17,9},{25,1},{2,26},{10... | collective-permute-start | bytes 442376 | tf_op jit(solution)/shard_map/ppermute | solution.py:26
  147.1 10.7 %collective-permute-start.16 = (f32[1152,128]{1,0:T(8,128)S(1)}, f32[1152,128]{1,0:T(8,128)S(1)}, u32[]{:S(2)}, u32[]{:S(2)}) collective-permute-start(f32[1152,128]{1,0:T(8,128)S(1)} %get-tuple-element.17), channel_id=1, source_target_pairs={{0,1},{1,0},{2,3},{3,2},{4,5},{5,4},{6,7},{7,6},{8,9},{9,8},{10,11... | collective-permute-start | bytes 1769480 | tf_op jit(solution)/shard_map/ppermute | solution.py:26
  (12 other events, 15.0 us)

commit v12 on v11

--- a/solution.py
+++ b/solution.py
@@ -90,6 +90,7 @@
     ordered = jnp.take(codes, owner_slot, axis=0).astype(fl)
     outgoing = jnp.tile(ordered, (n_blocks, 1))
     reading = lax.all_to_all(outgoing, ("tm", "series"), split_axis=0, concat_axis=1, tiled=True)[0]
+    sent, reading = lax.optimization_barrier((grad_out[0].astype(fl), reading))
     edge_float = edges.astype(fl)
     upper_edge = jnp.concatenate([edge_float[1:], jnp.full((1,), code_ceiling, fl)])
     onehot = (
@@ -142,7 +143,6 @@
     adjoint_local = jnp.einsum("thp,tn->hpn", grad_weighted, c_proj, preferred_element_type=fl)
     adjoint_in = jnp.zeros((head_count, head_dim, state_dim), fl)
     if n_blocks == 4:
-        sent = grad_out[0].astype(fl)
         along_x = lax.ppermute(sent, "tm", [(3, 2), (1, 0)])
         along_y = lax.ppermute(sent, "tm", [(3, 1), (2, 0)])
         diagonal = lax.ppermute(sent, "tm", [(2, 1), (3, 0)])

time: 160 us -> 133 us (0.83)
  waiting for transfers between devices: 52.1 us -> 22 us
  other arithmetic: 13.2 us -> 15.6 us
  local copies, waits for them, and re-layouts: 27.5 us -> 29.4 us
  starting transfers between devices: 37.2 us -> 35.4 us
    all_to_all x1, waiting for transfers between devices: 33.5 us -> 3.52 us  [on_device(): lax.all_to_all(outgoing, ('tm', 'series'), split_axis=0, concat_axis=1, t...]
    all_to_all x1, starting transfers between devices: 12.2 us -> 7.1 us  [on_device(): lax.all_to_all(outgoing, ('tm', 'series'), split_axis=0, concat_axis=1, t...]
    ppermute x14, starting transfers between devices: 21.1 us -> 24.5 us  [exchange(): return lax.ppermute(value, axis, pairs)]
    unnamed x87 -> x79, local copies, waits for them, and re-layouts: 5.32 us -> 5.28 us
  transfers between devices with their start and end apart: 18 -> 18, of which waited for: 11 -> 11; matrix products, arithmetic and copies ran while one was open for 36% -> 45% of each run, Pallas kernels for 0% -> 0%
where the time goes in v12:
time: 133 us; the launch traced here: 132 us
  starting transfers between devices  35.4 us (27%)
  local copies, waits for them, and re-layouts  29.4 us (22%)
  matrix products  28.1 us (21%)
  waiting for transfers between devices  22 us (17%)
  other arithmetic  15.6 us (12%)
  between operations  1.39 us (1%)
    ppermute x14, starting transfers between devices, exchange(): return lax.ppermute(value, axis, pairs)  24.5 us
    ppermute x14, waiting for transfers between devices, exchange(): return lax.ppermute(value, axis, pairs)  18.5 us
    all_to_all x1, starting transfers between devices, on_device(): lax.all_to_all(outgoing, ('tm', 'series'), split_axis=0, concat_axis=1, t...  7.1 us
    convert_element_type x1, local copies, waits for them, and re-layouts, on_device(): xw_all = (x_all * tail_all[..., None]).astype(half)  5.36 us
    exp x4, local copies, waits for them, and re-layouts, on_device(): later_weighted = (later * jnp.exp(cum_all[k])[:, :, None]).astype(half)  5.3 us
    unnamed x79, local copies, waits for them, and re-layouts  5.28 us
    dot_general x1, matrix products, on_device(): picked = jnp.dot(onehot, bin_table, precision=lax.Precision.HIGHEST)  4.14 us
    slice x2, local copies, waits for them, and re-layouts, on_device(): x_heads = projected[:, :inner_width].reshape(tok_rows, head_count, head_dim)  3.96 us
  transfers between devices with their start and end apart: 18, of which 11 were waited for; matrix products, arithmetic and copies ran while one was open for 45% of the time, Pallas kernels for 0%

profile of v12, /device:TPU:1, one launch (start us, length us, event | category | flops | bytes accessed | tf_op | source)
XLA Modules:
  0.0 132.0 jit_solution(18083709884846465283)
XLA Ops:
  2.0 1.2 gather_fusion
  4.0 7.1 %all-to-all-start = ((f32[32,1,16]{2,1,0:T(1,128)}), f32[32,1,16]{2,1,0:T(1,128)S(1)}, u32[]{:S(2)}, u32[]{:S(2)}) async-start(f32[32,1,16]{2,1,0:T(1,128)} %bitcast.1), calls=%async_computation | async-start | bytes 32768 | tf_op jit(solution)/shard_map/all_to_all | solution.py:92
  11.7 1.3 copy.91
  13.0 1.0 convert_bitcast_fusion
  14.3 3.5 %all-to-all-done = f32[32,1,16]{2,1,0:T(1,128)S(1)} async-done(((f32[32,1,16]{2,1,0:T(1,128)}), f32[32,1,16]{2,1,0:T(1,128)S(1)}, u32[]{:S(2)}, u32[]{:S(2)}) %all-to-all-start) | async-done | bytes 2080 | tf_op jit(solution)/shard_map/all_to_all | solution.py:92
  19.1 1.3 collective-permute-start
  20.4 1.3 collective-permute-start.1
  21.7 1.3 collective-permute-start.2
  23.0 1.4 %convert_reduce_fusion = f32[4096]{0:T(1024)S(1)} fusion(f32[4096]{0:T(1024)S(1)} %get-tuple-element.43, f32[4096]{0:T(1024)S(1)} %convert_element_type.117, f32[512]{0:T(512)S(1)} %squeeze.77), kind=kLoop, calls=%fused_computation.1 | loop fusion | flops 10481664 | bytes 51200 | tf_op jit(solution)/shard_map/reduce_sum | solution.py:99
  25.1 4.1 %fusion = f32[512,4]{0,1:T(4,128)S(1)} fusion(f32[4096]{0:T(1024)S(1)} %get-tuple-element.43, f32[4096]{0:T(1024)S(1)} %convert_element_type.117, f32[512]{0:T(512)S(1)} %squeeze.77, f32[4096,1]{0,1:T(1,128)S(1)} %bitcast.231, f32[4096,1]{0,1:T(1,128)S(1)} %bitcast.224, f32[4096,1]{0,1:T(1,128)S(1)} %bitcast.223, f32[4096,1]{0,1:T(1,128)S(1)} %sub.68), kind=kOutput, calls=%fused_computation.3 | convolution fusion | flops 107003904 | bytes 108544 | tf_op jit(solution)/shard_map/dot_general | solution.py:102
  29.3 1.1 compare_select_fusion
  32.3 1.6 %convolution_convert_fusion = bf16[512,2304]{1,0:T(8,128)(2,1)S(1)} fusion(bf16[128,2304]{1,0:T(8,128)(2,1)S(1)} %copy-done, f32[128]{0:T(128)S(1)} %add_multiply_fusion.1, f32[512]{0:T(512)S(1)} %add_multiply_fusion), kind=kOutput, calls=%fused_computation.4 | convolution fusion | flops 303300608 | bytes 2951680 | tf_op jit(solution)/shard_map/dot_general | solution.py:123
  35.0 1.4 %convolution_convert_fusion.1 = bf16[128,2304]{1,0:T(8,128)(2,1)} fusion(bf16[128,2304]{1,0:T(8,128)(2,1)S(1)} %copy-done, f32[128]{0:T(128)S(1)} %add_multiply_fusion.1, f32[1,128]{1,0:T(1,128)S(1)} %constant_dynamic-slice_fusion.7), kind=kOutput, calls=%fused_computation.9 | convolution fusion | flops 75825152 | bytes 1180672 | tf_op jit(solution)/shard_map/dot_general | solution.py:113
  38.8 1.6 %fusion.77 = f32[128,128]{0,1:T(8,128)} fusion(bf16[128,2304]{1,0:T(8,128)(2,1)} %convolution_convert_fusion.1), kind=kOutput, calls=%fused_computation.139 | convolution fusion | flops 4194304 | bytes 131072 | tf_op jit(solution)/shard_map/dot_general | solution.py:168
  40.4 1.9 %slice.125 = bf16[128,2048]{1,0:T(8,128)(2,1)} slice(bf16[128,2304]{1,0:T(8,128)(2,1)} %convolution_convert_fusion.1), slice={[0:128], [0:2048]} | slice | bytes 1048576 | tf_op jit(solution)/shard_map/slice | solution.py:114
  42.2 1.2 exp.68
  43.5 1.8 %exponential_multiply_fusion = f32[4,128,32]{2,1,0:T(8,128)} fusion(f32[4,128,32]{2,1,0:T(8,128)} %bitcast.205, f32[4,128,32]{2,1,0:T(8,128)} %copy-done.3, f32[4,32]{1,0:T(4,128)} %bitcast.230), kind=kLoop, calls=%fused_computation.86 | loop fusion | flops 32768 | bytes 197120 | tf_op jit(solution)/shard_map/mul | solution.py:132
  45.9 2.1 %copy.92 = bf16[128,2048]{0,1:T(8,128)(2,1)} copy(bf16[128,2048]{1,0:T(8,128)(2,1)} %slice.125) | data formatting | bytes 1048576 | tf_op jit(solution)/shard_map/slice | solution.py:114
  48.0 2.8 %fusion.5 = bf16[128,128]{0,1:T(8,128)(2,1)S(1)} fusion(bf16[128,32,64]{0,2,1:T(8,128)(2,1)} %bitcast.212, bf16[128,32,64]{0,2,1:T(8,128)(2,1)S(1)} %bitcast.202, f32[32,128]{1,0:T(8,128)} %get-tuple-element.52, f32[32,128]{1,0:T(8,128)} %copy.95, pred[128,128]{0,1:T(8,128)(4,1)} %iota_compare_fusion), kind=kOutput, calls=%fused_computation.13 | convolution fusion | flops 70238208 | bytes 1130496 | tf_op jit(solution)/shard_map/thp,shp->hts/dot_general | solution.py:185
  50.8 1.6 %fusion.79 = f32[128,128]{0,1:T(8,128)} fusion(bf16[128,2304]{1,0:T(8,128)(2,1)} %convolution_convert_fusion.1, bf16[128,128]{0,1:T(8,128)(2,1)S(1)} %fusion.5), kind=kOutput, calls=%fused_computation.141 | convolution fusion | flops 4194304 | bytes 131072 | tf_op jit(solution)/shard_map/dot_general | solution.py:187
  52.4 1.6 %fusion.74 = f32[128,128]{0,1:T(8,128)} fusion(bf16[128,2304]{1,0:T(8,128)(2,1)} %convolution_convert_fusion.1, bf16[128,128]{0,1:T(8,128)(2,1)S(1)} %fusion.5), kind=kOutput, calls=%fused_computation.136 | convolution fusion | flops 4194304 | bytes 131072 | tf_op jit(solution)/shard_map/dot_general | solution.py:189
  54.0 2.5 %slice_convert_fusion = f32[4,128,2048]{2,1,0:T(8,128)} fusion(bf16[4,128,2304]{2,1,0:T(8,128)(2,1)S(1)} %bitcast.197), kind=kLoop, calls=%fused_computation.11 | loop fusion | flops 1048576 | bytes 6291456 | tf_op jit(solution)/shard_map/convert_element_type | solution.py:133
  58.4 1.5 %copy.105 = f32[128,32]{0,1:T(8,128)} copy(f32[128,32]{1,0:T(8,128)} %get-tuple-element.32) | data formatting | bytes 32768 | tf_op jit(solution)/shard_map/exp | solution.py:157
  60.0 1.5 %copy.106 = f32[128,32]{0,1:T(8,128)} copy(f32[128,32]{1,0:T(8,128)} %get-tuple-element.31) | data formatting | bytes 32768 | tf_op jit(solution)/shard_map/exp | solution.py:157
  61.5 1.5 %copy.107 = f32[128,32]{0,1:T(8,128)} copy(f32[128,32]{1,0:T(8,128)} %get-tuple-element.30) | data formatting | bytes 32768 | tf_op jit(solution)/shard_map/exp | solution.py:157
  63.0 1.0 copy.101
  64.0 5.4 %copy.99 = f32[4,128,2048]{1,2,0:T(8,128)} copy(f32[4,128,2048]{2,1,0:T(8,128)} %slice_convert_fusion) | data formatting | bytes 8388608 | tf_op jit(solution)/shard_map/convert_element_type | solution.py:133
  70.5 2.9 %fusion.4 = f32[4,32,64,128]{3,2,1,0:T(8,128)S(1)} fusion(f32[4,128,32,64]{1,3,2,0:T(8,128)} %bitcast.196, f32[4,128,32]{1,2,0:T(8,128)S(1)} %copy.101, bf16[4,128,2304]{2,1,0:T(8,128)(2,1)S(1)} %bitcast.198), kind=kOutput, calls=%fused_computation.10 | convolution fusion | flops 270532608 | bytes 8585216 | tf_op jit(solution)/shard_map/bthp,btn->bhpn/dot_general | solution.py:134
  74.1 1.3 copy-done.1
  75.4 1.3 convolution_bitcast_fusion
  76.7 2.2 %fusion.22 = (bf16[128,2048]{0,1:T(8,128)(2,1)S(1)}, bf16[128,2048]{0,1:T(8,128)(2,1)S(1)}, bf16[128,2048]{0,1:T(8,128)(2,1)S(1)}) fusion(f32[128,2048]{0,1:T(8,128)} %collective-permute-done.2, f32[128,2048]{0,1:T(8,128)} %collective-permute-done.1, f32[128,32]{0,1:T(8,128)S(1)} %copy-done.8, pred[]{:T(512)S(6)} %eq.19, f32[128,32]{0,1:T(8,128)S(1)} %copy-done.7, ...), kind=kLoop, calls=%fused_computation.52 | loop fusion | flops 2359296 | bytes 4767746 | tf_op jit(solution)/shard_map/convert_element_type | solution.py:157
  80.0 1.1 fusion.14
  82.7 1.6 %collective-permute-done.3 = f32[1152,128]{1,0:T(8,128)S(1)} collective-permute-done((f32[1152,128]{1,0:T(8,128)S(1)}, f32[1152,128]{1,0:T(8,128)S(1)}, u32[]{:S(2)}, u32[]{:S(2)}) %collective-permute-start.3) | collective-permute-done | bytes 589856 | tf_op jit(solution)/shard_map/ppermute | solution.py:26
  84.5 3.4 %collective-permute-start.4 = (f32[288,128]{1,0:T(8,128)S(1)}, f32[288,128]{1,0:T(8,128)S(1)}, u32[]{:S(2)}, u32[]{:S(2)}) collective-permute-start(f32[288,128]{1,0:T(8,128)S(1)} %get-tuple-element.27), channel_id=1, source_target_pairs={{0,8},{8,0},{16,24},{24,16},{1,9},{9,1},{17,25},{25,17},{2,10},{10... | collective-permute-start | bytes 442376 | tf_op jit(solution)/shard_map/ppermute | solution.py:26
  87.9 4.3 %collective-permute-start.5 = (f32[288,128]{1,0:T(8,128)S(1)}, f32[288,128]{1,0:T(8,128)S(1)}, u32[]{:S(2)}, u32[]{:S(2)}) collective-permute-start(f32[288,128]{1,0:T(8,128)S(1)} %get-tuple-element.29), channel_id=1, source_target_pairs={{0,16},{8,24},{16,0},{24,8},{1,17},{9,25},{17,1},{25,9},{2,18},{10... | collective-permute-start | bytes 442376 | tf_op jit(solution)/shard_map/ppermute | solution.py:26
  92.2 5.8 %collective-permute-done.5 = f32[288,128]{1,0:T(8,128)S(1)} collective-permute-done((f32[288,128]{1,0:T(8,128)S(1)}, f32[288,128]{1,0:T(8,128)S(1)}, u32[]{:S(2)}, u32[]{:S(2)}) %collective-permute-start.5) | collective-permute-done | bytes 147488 | tf_op jit(solution)/shard_map/ppermute | solution.py:26
  99.7 3.0 %collective-permute-start.9 = (f32[72,128]{1,0:T(8,128)S(1)}, f32[72,128]{1,0:T(8,128)S(1)}, u32[]{:S(2)}, u32[]{:S(2)}) collective-permute-start(f32[72,128]{1,0:T(8,128)S(1)} %get-tuple-element.40), channel_id=1, source_target_pairs={{0,6},{1,7},{2,4},{3,5},{4,2},{5,3},{6,0},{7,1},{8,14},{9,15},{10,... | collective-permute-start | bytes 110600 | tf_op jit(solution)/shard_map/ppermute | solution.py:26
  103.1 1.3 collective-permute-done.9
  104.5 3.1 %collective-permute-start.11 = (f32[72,128]{1,0:T(8,128)S(1)}, f32[72,128]{1,0:T(8,128)S(1)}, u32[]{:S(2)}, u32[]{:S(2)}) collective-permute-start(f32[72,128]{1,0:T(8,128)S(1)} %add_add_fusion.1), channel_id=1, source_target_pairs={{0,4},{1,5},{2,6},{3,7},{4,0},{5,1},{6,2},{7,3},{8,12},{9,13},{10,... | collective-permute-start | bytes 110600 | tf_op jit(solution)/shard_map/ppermute | solution.py:26
  108.9 3.3 %collective-permute-done.12 = f32[72,128]{1,0:T(8,128)S(1)} collective-permute-done((f32[72,128]{1,0:T(8,128)S(1)}, f32[72,128]{1,0:T(8,128)S(1)}, u32[]{:S(2)}, u32[]{:S(2)}) %collective-permute-start.12) | collective-permute-done | bytes 36896 | tf_op jit(solution)/shard_map/ppermute | solution.py:26
  112.3 1.2 collective-permute-start.13
  115.1 1.4 %collective-permute-done.13 = f32[288,128]{1,0:T(8,128)S(1)} collective-permute-done((f32[288,128]{1,0:T(8,128)S(1)}, f32[288,128]{1,0:T(8,128)S(1)}, u32[]{:S(2)}, u32[]{:S(2)}) %collective-permute-start.13) | collective-permute-done | bytes 147488 | tf_op jit(solution)/shard_map/ppermute | solution.py:26
  116.4 1.1 collective-permute-done.14
  117.6 1.6 %collective-permute-done.15 = f32[288,128]{1,0:T(8,128)S(1)} collective-permute-done((f32[288,128]{1,0:T(8,128)S(1)}, f32[288,128]{1,0:T(8,128)S(1)}, u32[]{:S(2)}, u32[]{:S(2)}) %collective-permute-start.15) | collective-permute-done | bytes 147488 | tf_op jit(solution)/shard_map/ppermute | solution.py:26
  119.3 6.2 %collective-permute-start.16 = (f32[1152,128]{1,0:T(8,128)S(1)}, f32[1152,128]{1,0:T(8,128)S(1)}, u32[]{:S(2)}, u32[]{:S(2)}) collective-permute-start(f32[1152,128]{1,0:T(8,128)S(1)} %get-tuple-element.21), channel_id=1, source_target_pairs={{0,1},{1,0},{2,3},{3,2},{4,5},{5,4},{6,7},{7,6},{8,9},{9,8},{10,11... | collective-permute-start | bytes 1769480 | tf_op jit(solution)/shard_map/ppermute | solution.py:26
  125.6 1.3 convolution_bitcast_fusion.1
  126.9 2.4 %fusion.12 = bf16[128,32,64]{0,2,1:T(8,128)(2,1)S(1)} fusion(f32[128,32,64]{0,2,1:T(8,128)S(1)} %convolution_bitcast_fusion.1, f32[4,32,64,128]{3,2,1,0:T(8,128)} %copy-done.1, f32[128,32]{0,1:T(8,128)S(1)} %copy.102, f32[32]{0:T(128)S(1)} %copy-done.33, f32[32]{0:T(128)S(1)} %copy-done.30, f32[32]{0:T(128)S(1)} %copy-done.27, pred[]{:T(512)S(6)} %gt.24, ...), kind=kOutput, calls=%fused_computation.35 | convolution fusion | flops 70254592 | bytes 4768131 | tf_op jit(solution)/shard_map/tn,hpn->thp/dot_general | solution.py:175
  130.6 1.4 %copy.110 = f32[128,2304]{1,0:T(8,128)} copy(f32[128,2304]{0,1:T(8,128)S(1)} %fusion.15) | data formatting | bytes 2359296
  (153 shorter events, 23.8 us)
Async XLA Ops:
  0.6 31.7 %copy-start = (bf16[128,2304]{1,0:T(8,128)(2,1)S(1)}, bf16[128,2304]{1,0:T(8,128)(2,1)}, u32[]{:S(2)}) copy-start(bf16[128,2304]{1,0:T(8,128)(2,1)} %param.11) | copy-start | bytes 1769476
  0.6 13.4 %copy-start.16 = (s32[4096]{0:T(1024)S(1)}, s32[4096]{0:T(1024)}, u32[]{:S(2)}) copy-start(s32[4096]{0:T(1024)} %param.10) | copy-start | bytes 49156
  4.0 13.8 %all-to-all-start = ((f32[32,1,16]{2,1,0:T(1,128)}), f32[32,1,16]{2,1,0:T(1,128)S(1)}, u32[]{:S(2)}, u32[]{:S(2)}) async-start(f32[32,1,16]{2,1,0:T(1,128)} %bitcast.1), calls=%async_computation | async-start | bytes 32768 | tf_op jit(solution)/shard_map/all_to_all | solution.py:92
  14.2 20.7 %copy-start.21 = (f32[128]{0:T(128)}, f32[128]{0:T(128)S(1)}, u32[]{:S(2)}) copy-start(f32[128]{0:T(128)S(1)} %add_multiply_fusion.1) | copy-start | bytes 1540
  19.1 57.6 %collective-permute-start = (f32[128,2048]{0,1:T(8,128)}, f32[128,2048]{0,1:T(8,128)}, u32[]{:S(2)}, u32[]{:S(2)}) collective-permute-start(f32[128,2048]{0,1:T(8,128)} %convert_bitcast_fusion), channel_id=1, source_target_pairs={{24,16},{8,0},{25,17},{9,1},{26,18},{10,2},{27,19},{11,3},{28,20},... | collective-permute-start | bytes 3145736 | tf_op jit(solution)/shard_map/ppermute | solution.py:146
  20.4 56.3 %collective-permute-start.1 = (f32[128,2048]{0,1:T(8,128)}, f32[128,2048]{0,1:T(8,128)}, u32[]{:S(2)}, u32[]{:S(2)}) collective-permute-start(f32[128,2048]{0,1:T(8,128)} %convert_bitcast_fusion), channel_id=1, source_target_pairs={{24,8},{16,0},{25,9},{17,1},{26,10},{18,2},{27,11},{19,3},{28,12},... | collective-permute-start | bytes 3145736 | tf_op jit(solution)/shard_map/ppermute | solution.py:147
  21.7 55.0 %collective-permute-start.2 = (f32[128,2048]{0,1:T(8,128)}, f32[128,2048]{0,1:T(8,128)}, u32[]{:S(2)}, u32[]{:S(2)}) collective-permute-start(f32[128,2048]{0,1:T(8,128)} %convert_bitcast_fusion), channel_id=1, source_target_pairs={{16,8},{24,0},{17,9},{25,1},{18,10},{26,2},{19,11},{27,3},{20,12},... | collective-permute-start | bytes 3145736 | tf_op jit(solution)/shard_map/ppermute | solution.py:148
  25.1 4.2 %copy-start.34 = (bf16[128,32]{0,1:T(8,128)(2,1)S(1)}, bf16[128,32]{0,1:T(8,128)(2,1)}, u32[]{:S(2)}) copy-start(bf16[128,32]{0,1:T(8,128)(2,1)} %param.12) | copy-start | bytes 24580
  25.1 4.2 %copy-start.35 = (f32[32]{0:T(128)S(1)}, f32[32]{0:T(128)}, u32[]{:S(2)}) copy-start(f32[32]{0:T(128)} %param.13) | copy-start | bytes 388
  25.1 5.5 %copy-start.23 = (f32[32]{0:T(128)S(1)}, f32[32]{0:T(128)}, u32[]{:S(2)}) copy-start(f32[32]{0:T(128)} %param.14) | copy-start | bytes 388
  33.9 2.4 %copy-start.24 = (f32[1,128]{1,0:T(1,128)}, f32[1,128]{1,0:T(1,128)S(1)}, u32[]{:S(2)}) copy-start(f32[1,128]{1,0:T(1,128)S(1)} %constant_dynamic-slice_fusion.7) | copy-start | bytes 1540
  35.0 1.4 %copy-start.10 = (f32[128,32]{0,1:T(8,128)}, f32[128,32]{0,1:T(8,128)S(1)}, u32[]{:S(2)}) copy-start(f32[128,32]{0,1:T(8,128)S(1)} %get-tuple-element.53) | copy-start | bytes 49156
  54.0 2.5 %copy-start.11 = (f32[128,32]{0,1:T(8,128)S(1)}, f32[128,32]{0,1:T(8,128)}, u32[]{:S(2)}) copy-start(f32[128,32]{0,1:T(8,128)} %copy-done.10) | copy-start | bytes 49156
  54.0 2.5 %copy-start.31 = (f32[32]{0:T(128)S(1)}, f32[32]{0:T(128)}, u32[]{:S(2)}) copy-start(f32[32]{0:T(128)} %slice_bitcast_fusion.8) | copy-start | bytes 388
  54.0 3.2 %copy-start.20 = (f32[4,32]{1,0:T(4,128)S(1)}, f32[4,32]{1,0:T(4,128)}, u32[]{:S(2)}) copy-start(f32[4,32]{1,0:T(4,128)} %exp.68) | copy-start | bytes 1540
  70.4 2.9 %copy-start.15 = (f32[128,128]{0,1:T(8,128)S(1)}, f32[128,128]{0,1:T(8,128)}, u32[]{:S(2)}) copy-start(f32[128,128]{0,1:T(8,128)} %fusion.74) | copy-start | bytes 196612
  70.4 2.9 %copy-start.26 = (f32[32]{0:T(128)S(1)}, f32[32]{0:T(128)}, u32[]{:S(2)}) copy-start(f32[32]{0:T(128)} %get-tuple-element.51) | copy-start | bytes 388
  70.4 2.9 %copy-start.29 = (f32[32]{0:T(128)S(1)}, f32[32]{0:T(128)}, u32[]{:S(2)}) copy-start(f32[32]{0:T(128)} %get-tuple-element.50) | copy-start | bytes 388
  70.4 2.9 %copy-start.32 = (f32[32]{0:T(128)S(1)}, f32[32]{0:T(128)}, u32[]{:S(2)}) copy-start(f32[32]{0:T(128)} %get-tuple-element.49) | copy-start | bytes 388
  73.4 2.0 %copy-start.1 = (f32[4,32,64,128]{3,2,1,0:T(8,128)}, f32[4,32,64,128]{3,2,1,0:T(8,128)S(1)}, u32[]{:S(2)}) copy-start(f32[4,32,64,128]{3,2,1,0:T(8,128)S(1)} %fusion.4) | copy-start | bytes 12582916
  73.4 1.9 %copy-start.12 = (f32[128,128]{0,1:T(8,128)S(1)}, f32[128,128]{0,1:T(8,128)}, u32[]{:S(2)}) copy-start(f32[128,128]{0,1:T(8,128)} %fusion.77) | copy-start | bytes 196612
  73.4 1.9 %copy-start.17 = (f32[32,128]{1,0:T(8,128)S(1)}, f32[32,128]{1,0:T(8,128)}, u32[]{:S(2)}) copy-start(f32[32,128]{1,0:T(8,128)} %copy.95) | copy-start | bytes 49156
  73.4 1.9 %copy-start.18 = (pred[128,128]{0,1:T(8,128)(4,1)S(1)}, pred[128,128]{0,1:T(8,128)(4,1)}, u32[]{:S(2)}) copy-start(pred[128,128]{0,1:T(8,128)(4,1)} %iota_compare_fusion) | copy-start | bytes 49156
  73.4 1.9 %copy-start.36 = (f32[32,128]{1,0:T(8,128)S(1)}, f32[32,128]{1,0:T(8,128)}, u32[]{:S(2)}) copy-start(f32[32,128]{1,0:T(8,128)} %get-tuple-element.52) | copy-start | bytes 49156
  75.3 1.4 %copy-start.7 = (f32[128,32]{0,1:T(8,128)S(1)}, f32[128,32]{0,1:T(8,128)}, u32[]{:S(2)}) copy-start(f32[128,32]{0,1:T(8,128)} %copy.105) | copy-start | bytes 49156
  76.7 2.3 %copy-start.28 = (f32[32]{0:T(128)S(1)}, f32[32]{0:T(128)}, u32[]{:S(2)}) copy-start(f32[32]{0:T(128)} %get-tuple-element.48) | copy-start | bytes 388
  79.5 1.5 %copy-start.4 = (bf16[128,2048]{0,1:T(8,128)(2,1)S(1)}, bf16[128,2048]{0,1:T(8,128)(2,1)}, u32[]{:S(2)}) copy-start(bf16[128,2048]{0,1:T(8,128)(2,1)} %copy.92) | copy-start | bytes 1572868
  79.5 1.5 %copy-start.14 = (f32[128,128]{0,1:T(8,128)S(1)}, f32[128,128]{0,1:T(8,128)}, u32[]{:S(2)}) copy-start(f32[128,128]{0,1:T(8,128)} %fusion.79) | copy-start | bytes 196612
  80.0 1.5 %copy-start.22 = (f32[128]{0:T(128)S(1)}, f32[128]{0:T(128)}, u32[]{:S(2)}) copy-start(f32[128]{0:T(128)} %copy-done.21) | copy-start | bytes 1540
  80.0 1.5 %copy-start.25 = (f32[1,128]{1,0:T(1,128)S(1)}, f32[1,128]{1,0:T(1,128)}, u32[]{:S(2)}) copy-start(f32[1,128]{1,0:T(1,128)} %copy-done.24) | copy-start | bytes 1540
  82.1 2.3 %collective-permute-start.3 = (f32[1152,128]{1,0:T(8,128)S(1)}, f32[1152,128]{1,0:T(8,128)S(1)}, u32[]{:S(2)}, u32[]{:S(2)}) collective-permute-start(f32[1152,128]{1,0:T(8,128)S(1)} %constant_dynamic-slice_fusion.6), channel_id=1, source_target_pairs={{0,1},{1,0},{2,3},{3,2},{4,5},{5,4},{6,7},{7,6},{8,9},{9,8},{10,11... | collective-permute-start | bytes 1769480 | tf_op jit(solution)/shard_map/ppermute | solution.py:26
  84.5 7.7 %collective-permute-start.4 = (f32[288,128]{1,0:T(8,128)S(1)}, f32[288,128]{1,0:T(8,128)S(1)}, u32[]{:S(2)}, u32[]{:S(2)}) collective-permute-start(f32[288,128]{1,0:T(8,128)S(1)} %get-tuple-element.27), channel_id=1, source_target_pairs={{0,8},{8,0},{16,24},{24,16},{1,9},{9,1},{17,25},{25,17},{2,10},{10... | collective-permute-start | bytes 442376 | tf_op jit(solution)/shard_map/ppermute | solution.py:26
  87.9 10.1 %collective-permute-start.5 = (f32[288,128]{1,0:T(8,128)S(1)}, f32[288,128]{1,0:T(8,128)S(1)}, u32[]{:S(2)}, u32[]{:S(2)}) collective-permute-start(f32[288,128]{1,0:T(8,128)S(1)} %get-tuple-element.29), channel_id=1, source_target_pairs={{0,16},{8,24},{16,0},{24,8},{1,17},{9,25},{17,1},{25,9},{2,18},{10... | collective-permute-start | bytes 442376 | tf_op jit(solution)/shard_map/ppermute | solution.py:26
  92.2 6.8 %collective-permute-start.6 = (f32[288,128]{1,0:T(8,128)S(1)}, f32[288,128]{1,0:T(8,128)S(1)}, u32[]{:S(2)}, u32[]{:S(2)}) collective-permute-start(f32[288,128]{1,0:T(8,128)S(1)} %get-tuple-element.28), channel_id=1, source_target_pairs={{0,24},{8,16},{16,8},{24,0},{1,25},{9,17},{17,9},{25,1},{2,26},{10... | collective-permute-start | bytes 442376 | tf_op jit(solution)/shard_map/ppermute | solution.py:26
  99.0 3.6 %collective-permute-start.7 = (f32[72,128]{1,0:T(8,128)S(1)}, f32[72,128]{1,0:T(8,128)S(1)}, u32[]{:S(2)}, u32[]{:S(2)}) collective-permute-start(f32[72,128]{1,0:T(8,128)S(1)} %get-tuple-element.39), channel_id=1, source_target_pairs={{0,2},{1,3},{2,0},{3,1},{4,6},{5,7},{6,4},{7,5},{8,10},{9,11},{10,... | collective-permute-start | bytes 110600 | tf_op jit(solution)/shard_map/ppermute | solution.py:26
  99.4 3.7 %collective-permute-start.8 = (f32[72,128]{1,0:T(8,128)S(1)}, f32[72,128]{1,0:T(8,128)S(1)}, u32[]{:S(2)}, u32[]{:S(2)}) collective-permute-start(f32[72,128]{1,0:T(8,128)S(1)} %get-tuple-element.41), channel_id=1, source_target_pairs={{0,4},{1,5},{2,6},{3,7},{4,0},{5,1},{6,2},{7,3},{8,12},{9,13},{10,... | collective-permute-start | bytes 110600 | tf_op jit(solution)/shard_map/ppermute | solution.py:26
  99.7 4.7 %collective-permute-start.9 = (f32[72,128]{1,0:T(8,128)S(1)}, f32[72,128]{1,0:T(8,128)S(1)}, u32[]{:S(2)}, u32[]{:S(2)}) collective-permute-start(f32[72,128]{1,0:T(8,128)S(1)} %get-tuple-element.40), channel_id=1, source_target_pairs={{0,6},{1,7},{2,4},{3,5},{4,2},{5,3},{6,0},{7,1},{8,14},{9,15},{10,... | collective-permute-start | bytes 110600 | tf_op jit(solution)/shard_map/ppermute | solution.py:26
  104.4 3.6 %collective-permute-start.10 = (f32[72,128]{1,0:T(8,128)S(1)}, f32[72,128]{1,0:T(8,128)S(1)}, u32[]{:S(2)}, u32[]{:S(2)}) collective-permute-start(f32[72,128]{1,0:T(8,128)S(1)} %add_add_fusion.1), channel_id=1, source_target_pairs={{0,2},{1,3},{2,0},{3,1},{4,6},{5,7},{6,4},{7,5},{8,10},{9,11},{10,... | collective-permute-start | bytes 110600 | tf_op jit(solution)/shard_map/ppermute | solution.py:26
  104.5 4.5 %collective-permute-start.11 = (f32[72,128]{1,0:T(8,128)S(1)}, f32[72,128]{1,0:T(8,128)S(1)}, u32[]{:S(2)}, u32[]{:S(2)}) collective-permute-start(f32[72,128]{1,0:T(8,128)S(1)} %add_add_fusion.1), channel_id=1, source_target_pairs={{0,4},{1,5},{2,6},{3,7},{4,0},{5,1},{6,2},{7,3},{8,12},{9,13},{10,... | collective-permute-start | bytes 110600 | tf_op jit(solution)/shard_map/ppermute | solution.py:26
  107.6 4.6 %collective-permute-start.12 = (f32[72,128]{1,0:T(8,128)S(1)}, f32[72,128]{1,0:T(8,128)S(1)}, u32[]{:S(2)}, u32[]{:S(2)}) collective-permute-start(f32[72,128]{1,0:T(8,128)S(1)} %add_add_fusion.1), channel_id=1, source_target_pairs={{0,6},{1,7},{2,4},{3,5},{4,2},{5,3},{6,0},{7,1},{8,14},{9,15},{10,... | collective-permute-start | bytes 110600 | tf_op jit(solution)/shard_map/ppermute | solution.py:26
  112.3 13.2 %copy-start.5 = (bf16[128,2048]{0,1:T(8,128)(2,1)S(1)}, bf16[128,2048]{0,1:T(8,128)(2,1)}, u32[]{:S(2)}) copy-start(bf16[128,2048]{0,1:T(8,128)(2,1)} %copy.92) | copy-start | bytes 1572868
  112.3 13.2 %copy-start.13 = (f32[128,128]{0,1:T(8,128)S(1)}, f32[128,128]{0,1:T(8,128)}, u32[]{:S(2)}) copy-start(f32[128,128]{0,1:T(8,128)} %fusion.77) | copy-start | bytes 196612
  112.3 13.2 %copy-start.19 = (pred[128,128]{0,1:T(8,128)(4,1)S(1)}, pred[128,128]{0,1:T(8,128)(4,1)}, u32[]{:S(2)}) copy-start(pred[128,128]{0,1:T(8,128)(4,1)} %iota_compare_fusion) | copy-start | bytes 49156
  112.3 13.2 %copy-start.37 = (f32[32,128]{1,0:T(8,128)S(1)}, f32[32,128]{1,0:T(8,128)}, u32[]{:S(2)}) copy-start(f32[32,128]{1,0:T(8,128)} %get-tuple-element.52) | copy-start | bytes 49156
  112.3 4.1 %collective-permute-start.13 = (f32[288,128]{1,0:T(8,128)S(1)}, f32[288,128]{1,0:T(8,128)S(1)}, u32[]{:S(2)}, u32[]{:S(2)}) collective-permute-start(f32[288,128]{1,0:T(8,128)S(1)} %get-tuple-element.34), channel_id=1, source_target_pairs={{0,8},{8,0},{16,24},{24,16},{1,9},{9,1},{17,25},{25,17},{2,10},{10... | collective-permute-start | bytes 442376 | tf_op jit(solution)/shard_map/ppermute | solution.py:26
  113.6 4.0 %collective-permute-start.14 = (f32[288,128]{1,0:T(8,128)S(1)}, f32[288,128]{1,0:T(8,128)S(1)}, u32[]{:S(2)}, u32[]{:S(2)}) collective-permute-start(f32[288,128]{1,0:T(8,128)S(1)} %get-tuple-element.34), channel_id=1, source_target_pairs={{0,16},{8,24},{16,0},{24,8},{1,17},{9,25},{17,1},{25,9},{2,18},{10... | collective-permute-start | bytes 442376 | tf_op jit(solution)/shard_map/ppermute | solution.py:26
  114.1 5.1 %collective-permute-start.15 = (f32[288,128]{1,0:T(8,128)S(1)}, f32[288,128]{1,0:T(8,128)S(1)}, u32[]{:S(2)}, u32[]{:S(2)}) collective-permute-start(f32[288,128]{1,0:T(8,128)S(1)} %get-tuple-element.34), channel_id=1, source_target_pairs={{0,24},{8,16},{16,8},{24,0},{1,25},{9,17},{17,9},{25,1},{2,26},{10... | collective-permute-start | bytes 442376 | tf_op jit(solution)/shard_map/ppermute | solution.py:26
  119.3 11.0 %collective-permute-start.16 = (f32[1152,128]{1,0:T(8,128)S(1)}, f32[1152,128]{1,0:T(8,128)S(1)}, u32[]{:S(2)}, u32[]{:S(2)}) collective-permute-start(f32[1152,128]{1,0:T(8,128)S(1)} %get-tuple-element.21), channel_id=1, source_target_pairs={{0,1},{1,0},{2,3},{3,2},{4,5},{5,4},{6,7},{7,6},{8,9},{9,8},{10,11... | collective-permute-start | bytes 1769480 | tf_op jit(solution)/shard_map/ppermute | solution.py:26
  (8 other events, 9.3 us)

commit v13 on v12

--- a/solution.py
+++ b/solution.py
@@ -130,13 +130,17 @@
     cum_all = jnp.cumsum(-step_all * decay_rate, axis=1)
     gate_all = jnp.exp(cum_all[:, -1])
     tail_all = jnp.exp(cum_all[:, -1:, :] - cum_all) * step_all
-    xw_all = (x_all * tail_all[..., None]).astype(half)
-    state_local_all = jnp.einsum("bthp,btn->bhpn", xw_all, b_all, preferred_element_type=fl)
-
-    state_in = jnp.zeros((head_count, head_dim, state_dim), fl)
-    for k in range(n_blocks - 1):
-        new = gate_all[k][:, None, None] * state_in + state_local_all[k]
-        state_in = jnp.where(k < my_block, new, state_in)
+    earlier = n_blocks - 1
+    xw_all = (x_all[:earlier] * tail_all[:earlier, :, :, None]).astype(half)
+    xw_all = xw_all.reshape(earlier, tok_rows, inner_width)
+    state_local_t = jnp.einsum("btn,btk->bnk", b_all[:earlier], xw_all, preferred_element_type=fl)
+
+    state_t = jnp.zeros((state_dim, inner_width), fl)
+    for k in range(earlier):
+        gate_row = jnp.repeat(gate_all[k], head_dim)[None, :]
+        new = gate_row * state_t + state_local_t[k]
+        state_t = jnp.where(k < my_block, new, state_t)
+    state_in = state_t.reshape(state_dim, head_count, head_dim).transpose(1, 2, 0)
 
     grad_heads = grad_out[0].reshape(tok_rows, head_count, head_dim)
     grad_weighted = (grad_heads * head_factor[:, :, None]).astype(half)

time: 133 us -> 142 us (1.068)
  local copies, waits for them, and re-layouts: 29.4 us -> 40.4 us
  matrix products: 28.1 us -> 23.5 us
  other arithmetic: 15.6 us -> 18.5 us
    slice x1 -> x6, local copies, waits for them, and re-layouts: 0.08 us -> 11.1 us  [the longest x4 9.39 us: on_device(): new = gate_row * state_t + state_local_t[k]]
    convert_element_type x1 -> x0, local copies, waits for them, and re-layouts: 5.36 us -> none  [on_device(): xw_all = (x_all * tail_all[..., None]).astype(half)]
    mul x1 -> x2, local copies, waits for them, and re-layouts: 1.05 us -> 6.22 us  [on_device(): xw_all = (x_all[:earlier] * tail_all[:earlier, :, :, None]).astype(half)]
    dot_general x1, matrix products: 2.39 us -> 0.3 us  [on_device(): jnp.einsum('tn,hpn->thp', c_proj, state_half, preferred_element_type=fl)]
    dot_general x1, matrix products: 1.29 us -> 3.33 us  [on_device(): jnp.einsum('hts,shp->thp', weights, x_heads, preferred_element_type=fl)]
    another operation x1, local copies, waits for them, and re-layouts: 0.05 us -> 1.51 us  [on_device(): cum_decay = jnp.cumsum(-step_size * decay_rate, axis=0)]
    unnamed x79 -> x69, local copies, waits for them, and re-layouts: 5.28 us -> 4.27 us
  transfers between devices with their start and end apart: 18 -> 18, of which waited for: 11 -> 11; matrix products, arithmetic and copies ran while one was open for 45% -> 50% of each run, Pallas kernels for 0% -> 0%
where the time goes in v13:
time: 142 us; the launch traced here: 140 us
  local copies, waits for them, and re-layouts  40.4 us (28%)
  starting transfers between devices  35.5 us (25%)
  matrix products  23.5 us (17%)
  waiting for transfers between devices  21.2 us (15%)
  other arithmetic  18.5 us (13%)
    ppermute x14, starting transfers between devices, exchange(): return lax.ppermute(value, axis, pairs)  24.5 us
    ppermute x14, waiting for transfers between devices, exchange(): return lax.ppermute(value, axis, pairs)  18.5 us
    slice x4, local copies, waits for them, and re-layouts, on_device(): new = gate_row * state_t + state_local_t[k]  9.39 us
    all_to_all x1, starting transfers between devices, on_device(): lax.all_to_all(outgoing, ('tm', 'series'), split_axis=0, concat_axis=1, t...  7.1 us
    mul x2, local copies, waits for them, and re-layouts, on_device(): xw_all = (x_all[:earlier] * tail_all[:earlier, :, :, None]).astype(half)  6.22 us
    exp x4, local copies, waits for them, and re-layouts, on_device(): later_weighted = (later * jnp.exp(cum_all[k])[:, :, None]).astype(half)  5.27 us
    unnamed x69, local copies, waits for them, and re-layouts  4.27 us
    dot_general x1, matrix products, on_device(): picked = jnp.dot(onehot, bin_table, precision=lax.Precision.HIGHEST)  4.14 us
  transfers between devices with their start and end apart: 18, of which 11 were waited for; matrix products, arithmetic and copies ran while one was open for 50% of the time, Pallas kernels for 0%

profile of v13, /device:TPU:1, one launch (start us, length us, event | category | flops | bytes accessed | tf_op | source)
XLA Modules:
  0.0 140.4 jit_solution(3233488795026965473)
XLA Ops:
  2.1 1.2 gather_fusion
  4.0 7.1 %all-to-all-start = ((f32[32,1,16]{2,1,0:T(1,128)}), f32[32,1,16]{2,1,0:T(1,128)S(1)}, u32[]{:S(2)}, u32[]{:S(2)}) async-start(f32[32,1,16]{2,1,0:T(1,128)} %bitcast.1), calls=%async_computation | async-start | bytes 32768 | tf_op jit(solution)/shard_map/all_to_all | solution.py:92
  12.5 1.3 copy.103
  13.8 1.1 bitcast_convert_fusion
  15.1 2.7 %all-to-all-done = f32[32,1,16]{2,1,0:T(1,128)S(1)} async-done(((f32[32,1,16]{2,1,0:T(1,128)}), f32[32,1,16]{2,1,0:T(1,128)S(1)}, u32[]{:S(2)}, u32[]{:S(2)}) %all-to-all-start) | async-done | bytes 2080 | tf_op jit(solution)/shard_map/all_to_all | solution.py:92
  19.1 1.3 collective-permute-start
  20.4 1.3 collective-permute-start.1
  21.7 1.3 collective-permute-start.2
  23.0 1.4 %convert_reduce_fusion = f32[4096]{0:T(1024)S(1)} fusion(f32[4096]{0:T(1024)S(1)} %get-tuple-element.46, f32[4096]{0:T(1024)S(1)} %convert_element_type.110, f32[512]{0:T(512)S(1)} %squeeze.84), kind=kLoop, calls=%fused_computation.1 | loop fusion | flops 10481664 | bytes 51200 | tf_op jit(solution)/shard_map/reduce_sum | solution.py:99
  25.1 4.1 %fusion = f32[512,4]{0,1:T(4,128)S(1)} fusion(f32[4096]{0:T(1024)S(1)} %get-tuple-element.46, f32[4096]{0:T(1024)S(1)} %convert_element_type.110, f32[512]{0:T(512)S(1)} %squeeze.84, f32[4096,1]{0,1:T(1,128)S(1)} %bitcast.208, f32[4096,1]{0,1:T(1,128)S(1)} %bitcast.201, f32[4096,1]{0,1:T(1,128)S(1)} %bitcast.200, f32[4096,1]{0,1:T(1,128)S(1)} %sub.64), kind=kOutput, calls=%fused_computation.3 | convolution fusion | flops 107003904 | bytes 108544 | tf_op jit(solution)/shard_map/dot_general | solution.py:102
  32.2 1.6 %convolution_convert_fusion = bf16[512,2304]{1,0:T(8,128)(2,1)S(1)} fusion(bf16[128,2304]{1,0:T(8,128)(2,1)S(1)} %copy-done, f32[128]{0:T(128)S(1)} %add_multiply_fusion.1, f32[512]{0:T(512)S(1)} %add_multiply_fusion), kind=kOutput, calls=%fused_computation.4 | convolution fusion | flops 303300608 | bytes 2951680 | tf_op jit(solution)/shard_map/dot_general | solution.py:123
  36.3 1.6 %reduce_window_sum.46 = f32[128,32]{1,0:T(8,128)} reduce-window(f32[128,32]{1,0:T(8,128)} %copy.106, f32[]{:T(128)} %constant.171.clone.1), window={size=128x1 pad=127_0x0_0}, to_apply=%region_3.4 | reduce-window | flops 520192 | bytes 32772 | tf_op jit(solution)/shard_map/jit(cumsum)/reduce_window_sum | solution.py:118
  37.9 1.5 %copy.124 = f32[128,32]{0,1:T(8,128)} copy(f32[128,32]{1,0:T(8,128)} %reduce_window_sum.46) | data formatting | bytes 32768 | tf_op jit(solution)/shard_map/jit(cumsum)/reduce_window_sum | solution.py:118
  39.4 1.2 slice_bitcast_fusion.6
  42.2 1.5 %copy.107 = f32[32,128]{1,0:T(8,128)} copy(f32[32,128]{0,1:T(8,128)} %bitcast.190) | data formatting | bytes 32768 | tf_op jit(solution)/shard_map/transpose | solution.py:14
  43.7 2.0 %copy.104 = bf16[128,2048]{0,1:T(8,128)(2,1)} copy(bf16[128,2048]{1,0:T(8,128)(2,1)} %slice.134) | data formatting | bytes 1048576 | tf_op jit(solution)/shard_map/slice | solution.py:114
  45.8 2.7 %fusion.4 = bf16[128,128]{0,1:T(8,128)(2,1)S(1)} fusion(bf16[128,32,64]{0,2,1:T(8,128)(2,1)} %bitcast.191, bf16[128,32,64]{0,2,1:T(8,128)(2,1)} %bitcast.180, f32[32,128]{1,0:T(8,128)} %get-tuple-element.55, f32[32,128]{1,0:T(8,128)} %copy.107, pred[128,128]{0,1:T(8,128)(4,1)} %iota_compare_fusion), kind=kOutput, calls=%fused_computation.11 | convolution fusion | flops 70238208 | bytes 1130496 | tf_op jit(solution)/shard_map/thp,shp->hts/dot_general | solution.py:189
  50.8 1.5 %copy.121 = f32[128,32]{0,1:T(8,128)} copy(f32[128,32]{1,0:T(8,128)} %get-tuple-element.35) | data formatting | bytes 32768 | tf_op jit(solution)/shard_map/exp | solution.py:161
  52.3 1.5 %copy.122 = f32[128,32]{0,1:T(8,128)} copy(f32[128,32]{1,0:T(8,128)} %get-tuple-element.34) | data formatting | bytes 32768 | tf_op jit(solution)/shard_map/exp | solution.py:161
  53.8 1.5 %copy.123 = f32[128,32]{0,1:T(8,128)} copy(f32[128,32]{1,0:T(8,128)} %get-tuple-element.33) | data formatting | bytes 32768 | tf_op jit(solution)/shard_map/exp | solution.py:161
  56.0 1.7 %slice_multiply_fusion = f32[3,128,32]{2,1,0:T(8,128)} fusion(f32[4,128,32]{2,1,0:T(8,128)} %bitcast.189, f32[4,128,32]{2,1,0:T(8,128)} %copy-done.6, f32[3,32]{1,0:T(4,128)S(1)} %bitcast.207), kind=kLoop, calls=%fused_computation.73 | loop fusion | flops 24576 | bytes 147840 | tf_op jit(solution)/shard_map/mul | solution.py:132
  57.7 1.7 %copy.113 = f32[3,128,32]{1,2,0:T(8,128)} copy(f32[3,128,32]{2,1,0:T(8,128)} %slice_multiply_fusion) | data formatting | bytes 98304 | tf_op jit(solution)/shard_map/slice | solution.py:134
  59.3 2.6 %mul.272 = f32[3,128,32,64]{1,3,2,0:T(8,128)} broadcast(f32[3,128,32]{1,2,0:T(8,128)} %copy.113), dimensions={0,1,2} | broadcast | bytes 3194880 | tf_op jit(solution)/shard_map/mul | solution.py:134
  62.0 3.6 %copy.114 = f32[3,128,2048]{2,1,0:T(8,128)} copy(f32[3,128,2048]{1,2,0:T(8,128)} %bitcast.172) | data formatting | bytes 6291456 | tf_op jit(solution)/shard_map/mul | solution.py:134
  65.6 2.5 %fusion.5 = f32[3,128,2048]{2,1,0:T(8,128)S(1)} fusion(f32[3,128,2048]{2,1,0:T(8,128)} %copy.114, bf16[4,128,2304]{2,1,0:T(8,128)(2,1)S(1)} %bitcast.173), kind=kOutput, calls=%fused_computation.14 | convolution fusion | flops 203685888 | bytes 7962624 | tf_op jit(solution)/shard_map/btn,btk->bnk/dot_general | solution.py:136
  68.1 1.8 %fusion.87 = (f32[1,128,2048]{2,1,0:T(8,128)}, f32[1,128,2048]{2,1,0:T(8,128)}, f32[1,128,2048]{2,1,0:T(8,128)}) fusion(f32[3,128,2048]{2,1,0:T(8,128)S(1)} %fusion.5), kind=kLoop, calls=%fused_computation.173 | loop fusion | bytes 6291456 | tf_op jit(solution)/shard_map/slice | solution.py:141
  69.8 2.5 %copy.115 = f32[1,128,2048]{1,2,0:T(8,128)} copy(f32[1,128,2048]{2,1,0:T(8,128)} %get-tuple-element.16) | data formatting | bytes 2097152 | tf_op jit(solution)/shard_map/slice | solution.py:141
  72.4 2.6 %copy.116 = f32[1,128,2048]{1,2,0:T(8,128)} copy(f32[1,128,2048]{2,1,0:T(8,128)} %get-tuple-element.18) | data formatting | bytes 2097152 | tf_op jit(solution)/shard_map/slice | solution.py:141
  74.9 2.5 %copy.117 = f32[1,128,2048]{1,2,0:T(8,128)} copy(f32[1,128,2048]{2,1,0:T(8,128)} %get-tuple-element.17) | data formatting | bytes 2097152 | tf_op jit(solution)/shard_map/slice | solution.py:141
  80.1 2.7 %fusion.33 = bf16[32,64,128]{2,1,0:T(8,128)(2,1)S(1)} fusion(f32[128,32,64]{0,2,1:T(8,128)} %bitcast.179, f32[128,32,64]{0,2,1:T(8,128)} %bitcast.178, f32[128,32,64]{0,2,1:T(8,128)} %bitcast.177, f32[32]{0:T(128)S(1)} %get-tuple-element.52, f32[32]{0:T(128)S(1)} %get-tuple-element.53, f32[32]{0:T(128)S(1)} %get-tuple-element.54, pred[]{:T(512)S(6)} %gt.24, ...), kind=kLoop, calls=%fused_computation.67 | loop fusion | flops 2359296 | bytes 3670403 | tf_op jit(solution)/shard_map/convert_element_type | solution.py:174
  83.3 1.3 convolution_bitcast_fusion
  84.7 2.2 %fusion.21 = (bf16[128,2048]{0,1:T(8,128)(2,1)S(1)}, bf16[128,2048]{0,1:T(8,128)(2,1)S(1)}, bf16[128,2048]{0,1:T(8,128)(2,1)S(1)}) fusion(f32[128,2048]{0,1:T(8,128)} %collective-permute-done.2, f32[128,2048]{0,1:T(8,128)} %collective-permute-done.1, f32[128,32]{0,1:T(8,128)S(1)} %copy-done.10, pred[]{:T(512)S(6)} %eq.19, f32[128,32]{0,1:T(8,128)S(1)} %copy-done.9, ...), kind=kLoop, calls=%fused_computation.48 | loop fusion | flops 2359296 | bytes 4767746 | tf_op jit(solution)/shard_map/convert_element_type | solution.py:161
  90.2 1.6 %collective-permute-done.3 = f32[1152,128]{1,0:T(8,128)S(1)} collective-permute-done((f32[1152,128]{1,0:T(8,128)S(1)}, f32[1152,128]{1,0:T(8,128)S(1)}, u32[]{:S(2)}, u32[]{:S(2)}) %collective-permute-start.3) | collective-permute-done | bytes 589856 | tf_op jit(solution)/shard_map/ppermute | solution.py:26
  92.0 3.4 %collective-permute-start.4 = (f32[288,128]{1,0:T(8,128)S(1)}, f32[288,128]{1,0:T(8,128)S(1)}, u32[]{:S(2)}, u32[]{:S(2)}) collective-permute-start(f32[288,128]{1,0:T(8,128)S(1)} %get-tuple-element.30), channel_id=1, source_target_pairs={{0,8},{8,0},{16,24},{24,16},{1,9},{9,1},{17,25},{25,17},{2,10},{10... | collective-permute-start | bytes 442376 | tf_op jit(solution)/shard_map/ppermute | solution.py:26
  95.4 4.4 %collective-permute-start.5 = (f32[288,128]{1,0:T(8,128)S(1)}, f32[288,128]{1,0:T(8,128)S(1)}, u32[]{:S(2)}, u32[]{:S(2)}) collective-permute-start(f32[288,128]{1,0:T(8,128)S(1)} %get-tuple-element.32), channel_id=1, source_target_pairs={{0,16},{8,24},{16,0},{24,8},{1,17},{9,25},{17,1},{25,9},{2,18},{10... | collective-permute-start | bytes 442376 | tf_op jit(solution)/shard_map/ppermute | solution.py:26
  99.8 5.8 %collective-permute-done.5 = f32[288,128]{1,0:T(8,128)S(1)} collective-permute-done((f32[288,128]{1,0:T(8,128)S(1)}, f32[288,128]{1,0:T(8,128)S(1)}, u32[]{:S(2)}, u32[]{:S(2)}) %collective-permute-start.5) | collective-permute-done | bytes 147488 | tf_op jit(solution)/shard_map/ppermute | solution.py:26
  107.1 3.0 %collective-permute-start.9 = (f32[72,128]{1,0:T(8,128)S(1)}, f32[72,128]{1,0:T(8,128)S(1)}, u32[]{:S(2)}, u32[]{:S(2)}) collective-permute-start(f32[72,128]{1,0:T(8,128)S(1)} %get-tuple-element.43), channel_id=1, source_target_pairs={{0,6},{1,7},{2,4},{3,5},{4,2},{5,3},{6,0},{7,1},{8,14},{9,15},{10,... | collective-permute-start | bytes 110600 | tf_op jit(solution)/shard_map/ppermute | solution.py:26
  110.5 1.4 collective-permute-done.9
  112.0 3.1 %collective-permute-start.11 = (f32[72,128]{1,0:T(8,128)S(1)}, f32[72,128]{1,0:T(8,128)S(1)}, u32[]{:S(2)}, u32[]{:S(2)}) collective-permute-start(f32[72,128]{1,0:T(8,128)S(1)} %add_add_fusion.1), channel_id=1, source_target_pairs={{0,4},{1,5},{2,6},{3,7},{4,0},{5,1},{6,2},{7,3},{8,12},{9,13},{10,... | collective-permute-start | bytes 110600 | tf_op jit(solution)/shard_map/ppermute | solution.py:26
  116.4 3.4 %collective-permute-done.12 = f32[72,128]{1,0:T(8,128)S(1)} collective-permute-done((f32[72,128]{1,0:T(8,128)S(1)}, f32[72,128]{1,0:T(8,128)S(1)}, u32[]{:S(2)}, u32[]{:S(2)}) %collective-permute-start.12) | collective-permute-done | bytes 36896 | tf_op jit(solution)/shard_map/ppermute | solution.py:26
  119.9 1.3 collective-permute-start.13
  122.6 1.4 %collective-permute-done.13 = f32[288,128]{1,0:T(8,128)S(1)} collective-permute-done((f32[288,128]{1,0:T(8,128)S(1)}, f32[288,128]{1,0:T(8,128)S(1)}, u32[]{:S(2)}, u32[]{:S(2)}) %collective-permute-start.13) | collective-permute-done | bytes 147488 | tf_op jit(solution)/shard_map/ppermute | solution.py:26
  124.0 1.2 collective-permute-done.14
  125.2 1.6 %collective-permute-done.15 = f32[288,128]{1,0:T(8,128)S(1)} collective-permute-done((f32[288,128]{1,0:T(8,128)S(1)}, f32[288,128]{1,0:T(8,128)S(1)}, u32[]{:S(2)}, u32[]{:S(2)}) %collective-permute-start.15) | collective-permute-done | bytes 147488 | tf_op jit(solution)/shard_map/ppermute | solution.py:26
  126.9 6.1 %collective-permute-start.16 = (f32[1152,128]{1,0:T(8,128)S(1)}, f32[1152,128]{1,0:T(8,128)}, u32[]{:S(2)}, u32[]{:S(2)}) collective-permute-start(f32[1152,128]{1,0:T(8,128)S(1)} %get-tuple-element.24), channel_id=1, source_target_pairs={{0,1},{1,0},{2,3},{3,2},{4,5},{5,4},{6,7},{7,6},{8,9},{9,8},{10,11... | collective-permute-start | bytes 1769480 | tf_op jit(solution)/shard_map/ppermute | solution.py:26
  133.1 3.3 %convolution_bitcast_fusion.1 = f32[128,32,64]{0,2,1:T(8,128)S(1)} fusion(bf16[128,32,64]{0,2,1:T(8,128)(2,1)} %bitcast.192, f32[32,128]{1,0:T(8,128)S(1)} %copy-done.32, f32[32,128]{1,0:T(8,128)S(1)} %copy-done.20, f32[128,128]{0,1:T(8,128)S(1)} %copy-done.14, pred[128,128]{0,1:T(8,128)(4,1)S(1)} %copy-done.22), kind=kOutput, calls=%fused_computation.31 | convolution fusion | flops 70254592 | bytes 1687552 | tf_op jit(solution)/shard_map/hts,shp->thp/dot_general | solution.py:176
  137.7 1.2 fusion.26
  139.0 1.4 copy.126
  (147 shorter events, 28.2 us)
Async XLA Ops:
  0.6 31.6 %copy-start = (bf16[128,2304]{1,0:T(8,128)(2,1)S(1)}, bf16[128,2304]{1,0:T(8,128)(2,1)}, u32[]{:S(2)}) copy-start(bf16[128,2304]{1,0:T(8,128)(2,1)} %param.11) | copy-start | bytes 1769476
  0.6 14.3 %copy-start.17 = (s32[4096]{0:T(1024)S(1)}, s32[4096]{0:T(1024)}, u32[]{:S(2)}) copy-start(s32[4096]{0:T(1024)} %param.10) | copy-start | bytes 49156
  4.0 13.8 %all-to-all-start = ((f32[32,1,16]{2,1,0:T(1,128)}), f32[32,1,16]{2,1,0:T(1,128)S(1)}, u32[]{:S(2)}, u32[]{:S(2)}) async-start(f32[32,1,16]{2,1,0:T(1,128)} %bitcast.1), calls=%async_computation | async-start | bytes 32768 | tf_op jit(solution)/shard_map/all_to_all | solution.py:92
  13.8 15.4 %copy-start.1 = (bf16[1,128,2048]{1,2,0:T(8,128)(2,1)}, bf16[1,128,2048]{1,2,0:T(8,128)(2,1)S(1)}, u32[]{:S(2)}) copy-start(bf16[1,128,2048]{1,2,0:T(8,128)(2,1)S(1)} %copy.103) | copy-start | bytes 1572868
  15.0 19.9 %copy-start.23 = (f32[128]{0:T(128)}, f32[128]{0:T(128)S(1)}, u32[]{:S(2)}) copy-start(f32[128]{0:T(128)S(1)} %add_multiply_fusion.1) | copy-start | bytes 1540
  19.1 65.6 %collective-permute-start = (f32[128,2048]{0,1:T(8,128)}, f32[128,2048]{0,1:T(8,128)}, u32[]{:S(2)}, u32[]{:S(2)}) collective-permute-start(f32[128,2048]{0,1:T(8,128)} %bitcast_convert_fusion), channel_id=1, source_target_pairs={{24,16},{8,0},{25,17},{9,1},{26,18},{10,2},{27,19},{11,3},{28,20},... | collective-permute-start | bytes 3145736 | tf_op jit(solution)/shard_map/ppermute | solution.py:150
  20.4 64.3 %collective-permute-start.1 = (f32[128,2048]{0,1:T(8,128)}, f32[128,2048]{0,1:T(8,128)}, u32[]{:S(2)}, u32[]{:S(2)}) collective-permute-start(f32[128,2048]{0,1:T(8,128)} %bitcast_convert_fusion), channel_id=1, source_target_pairs={{24,8},{16,0},{25,9},{17,1},{26,10},{18,2},{27,11},{19,3},{28,12},... | collective-permute-start | bytes 3145736 | tf_op jit(solution)/shard_map/ppermute | solution.py:151
  21.7 63.0 %collective-permute-start.2 = (f32[128,2048]{0,1:T(8,128)}, f32[128,2048]{0,1:T(8,128)}, u32[]{:S(2)}, u32[]{:S(2)}) collective-permute-start(f32[128,2048]{0,1:T(8,128)} %bitcast_convert_fusion), channel_id=1, source_target_pairs={{16,8},{24,0},{17,9},{25,1},{18,10},{26,2},{19,11},{27,3},{20,12},... | collective-permute-start | bytes 3145736 | tf_op jit(solution)/shard_map/ppermute | solution.py:152
  25.1 4.2 %copy-start.29 = (bf16[128,32]{0,1:T(8,128)(2,1)S(1)}, bf16[128,32]{0,1:T(8,128)(2,1)}, u32[]{:S(2)}) copy-start(bf16[128,32]{0,1:T(8,128)(2,1)} %param.12) | copy-start | bytes 24580
  25.1 4.2 %copy-start.30 = (f32[32]{0:T(128)S(1)}, f32[32]{0:T(128)}, u32[]{:S(2)}) copy-start(f32[32]{0:T(128)} %param.13) | copy-start | bytes 388
  25.1 5.5 %copy-start.25 = (f32[32]{0:T(128)S(1)}, f32[32]{0:T(128)}, u32[]{:S(2)}) copy-start(f32[32]{0:T(128)} %param.14) | copy-start | bytes 388
  30.6 1.1 copy-start.5
  32.2 3.3 %copy-start.26 = (f32[32]{0:T(128)S(1)}, f32[32]{0:T(128)}, u32[]{:S(2)}) copy-start(f32[32]{0:T(128)} %param.14) | copy-start | bytes 388
  33.9 1.6 %copy-start.27 = (f32[1,128]{1,0:T(1,128)}, f32[1,128]{1,0:T(1,128)S(1)}, u32[]{:S(2)}) copy-start(f32[1,128]{1,0:T(1,128)S(1)} %constant_dynamic-slice_fusion.7) | copy-start | bytes 1540
  45.8 4.4 %copy-start.7 = (f32[128,32]{1,0:T(8,128)S(1)}, f32[128,32]{1,0:T(8,128)}, u32[]{:S(2)}) copy-start(f32[128,32]{1,0:T(8,128)} %reduce_window_sum.46) | copy-start | bytes 49156
  45.8 9.6 %copy-start.18 = (f32[4,1,32]{2,1,0:T(1,128)S(1)}, f32[4,1,32]{2,1,0:T(1,128)}, u32[]{:S(2)}) copy-start(f32[4,1,32]{2,1,0:T(1,128)} %slice.137) | copy-start | bytes 1540
  78.4 4.5 %copy-start.2 = (bf16[1,128,2048]{1,2,0:T(8,128)(2,1)S(1)}, bf16[1,128,2048]{1,2,0:T(8,128)(2,1)}, u32[]{:S(2)}) copy-start(bf16[1,128,2048]{1,2,0:T(8,128)(2,1)} %copy-done.1) | copy-start | bytes 1572868
  78.4 4.5 %copy-start.16 = (f32[128,128]{0,1:T(8,128)S(1)}, f32[128,128]{0,1:T(8,128)}, u32[]{:S(2)}) copy-start(f32[128,128]{0,1:T(8,128)} %fusion.64) | copy-start | bytes 196612
  80.1 3.1 %copy-start.13 = (f32[128,128]{0,1:T(8,128)S(1)}, f32[128,128]{0,1:T(8,128)}, u32[]{:S(2)}) copy-start(f32[128,128]{0,1:T(8,128)} %fusion.67) | copy-start | bytes 196612
  80.1 3.2 %copy-start.19 = (f32[32,128]{1,0:T(8,128)S(1)}, f32[32,128]{1,0:T(8,128)}, u32[]{:S(2)}) copy-start(f32[32,128]{1,0:T(8,128)} %copy.107) | copy-start | bytes 49156
  80.1 3.2 %copy-start.21 = (pred[128,128]{0,1:T(8,128)(4,1)S(1)}, pred[128,128]{0,1:T(8,128)(4,1)}, u32[]{:S(2)}) copy-start(pred[128,128]{0,1:T(8,128)(4,1)} %iota_compare_fusion) | copy-start | bytes 49156
  80.1 3.2 %copy-start.31 = (f32[32,128]{1,0:T(8,128)S(1)}, f32[32,128]{1,0:T(8,128)}, u32[]{:S(2)}) copy-start(f32[32,128]{1,0:T(8,128)} %get-tuple-element.55) | copy-start | bytes 49156
  82.9 1.8 %copy-start.3 = (bf16[32,64,128]{2,1,0:T(8,128)(2,1)}, bf16[32,64,128]{2,1,0:T(8,128)(2,1)S(1)}, u32[]{:S(2)}) copy-start(bf16[32,64,128]{2,1,0:T(8,128)(2,1)S(1)} %fusion.33) | copy-start | bytes 1572868
  83.3 1.4 copy-start.9
  83.3 1.4 copy-start.10
  83.3 1.4 copy-start.11
  87.5 1.0 copy-start.8
  87.8 1.1 copy-start.24
  87.8 1.1 copy-start.28
  89.5 2.3 %collective-permute-start.3 = (f32[1152,128]{1,0:T(8,128)S(1)}, f32[1152,128]{1,0:T(8,128)S(1)}, u32[]{:S(2)}, u32[]{:S(2)}) collective-permute-start(f32[1152,128]{1,0:T(8,128)S(1)} %constant_dynamic-slice_fusion.6), channel_id=1, source_target_pairs={{0,1},{1,0},{2,3},{3,2},{4,5},{5,4},{6,7},{7,6},{8,9},{9,8},{10,11... | collective-permute-start | bytes 1769480 | tf_op jit(solution)/shard_map/ppermute | solution.py:26
  92.0 7.8 %collective-permute-start.4 = (f32[288,128]{1,0:T(8,128)S(1)}, f32[288,128]{1,0:T(8,128)S(1)}, u32[]{:S(2)}, u32[]{:S(2)}) collective-permute-start(f32[288,128]{1,0:T(8,128)S(1)} %get-tuple-element.30), channel_id=1, source_target_pairs={{0,8},{8,0},{16,24},{24,16},{1,9},{9,1},{17,25},{25,17},{2,10},{10... | collective-permute-start | bytes 442376 | tf_op jit(solution)/shard_map/ppermute | solution.py:26
  95.4 10.2 %collective-permute-start.5 = (f32[288,128]{1,0:T(8,128)S(1)}, f32[288,128]{1,0:T(8,128)S(1)}, u32[]{:S(2)}, u32[]{:S(2)}) collective-permute-start(f32[288,128]{1,0:T(8,128)S(1)} %get-tuple-element.32), channel_id=1, source_target_pairs={{0,16},{8,24},{16,0},{24,8},{1,17},{9,25},{17,1},{25,9},{2,18},{10... | collective-permute-start | bytes 442376 | tf_op jit(solution)/shard_map/ppermute | solution.py:26
  99.8 6.6 %collective-permute-start.6 = (f32[288,128]{1,0:T(8,128)S(1)}, f32[288,128]{1,0:T(8,128)S(1)}, u32[]{:S(2)}, u32[]{:S(2)}) collective-permute-start(f32[288,128]{1,0:T(8,128)S(1)} %get-tuple-element.31), channel_id=1, source_target_pairs={{0,24},{8,16},{16,8},{24,0},{1,25},{9,17},{17,9},{25,1},{2,26},{10... | collective-permute-start | bytes 442376 | tf_op jit(solution)/shard_map/ppermute | solution.py:26
  106.5 3.6 %collective-permute-start.7 = (f32[72,128]{1,0:T(8,128)S(1)}, f32[72,128]{1,0:T(8,128)S(1)}, u32[]{:S(2)}, u32[]{:S(2)}) collective-permute-start(f32[72,128]{1,0:T(8,128)S(1)} %get-tuple-element.42), channel_id=1, source_target_pairs={{0,2},{1,3},{2,0},{3,1},{4,6},{5,7},{6,4},{7,5},{8,10},{9,11},{10,... | collective-permute-start | bytes 110600 | tf_op jit(solution)/shard_map/ppermute | solution.py:26
  106.8 3.7 %collective-permute-start.8 = (f32[72,128]{1,0:T(8,128)S(1)}, f32[72,128]{1,0:T(8,128)S(1)}, u32[]{:S(2)}, u32[]{:S(2)}) collective-permute-start(f32[72,128]{1,0:T(8,128)S(1)} %get-tuple-element.44), channel_id=1, source_target_pairs={{0,4},{1,5},{2,6},{3,7},{4,0},{5,1},{6,2},{7,3},{8,12},{9,13},{10,... | collective-permute-start | bytes 110600 | tf_op jit(solution)/shard_map/ppermute | solution.py:26
  107.1 4.8 %collective-permute-start.9 = (f32[72,128]{1,0:T(8,128)S(1)}, f32[72,128]{1,0:T(8,128)S(1)}, u32[]{:S(2)}, u32[]{:S(2)}) collective-permute-start(f32[72,128]{1,0:T(8,128)S(1)} %get-tuple-element.43), channel_id=1, source_target_pairs={{0,6},{1,7},{2,4},{3,5},{4,2},{5,3},{6,0},{7,1},{8,14},{9,15},{10,... | collective-permute-start | bytes 110600 | tf_op jit(solution)/shard_map/ppermute | solution.py:26
  111.9 3.6 %collective-permute-start.10 = (f32[72,128]{1,0:T(8,128)S(1)}, f32[72,128]{1,0:T(8,128)S(1)}, u32[]{:S(2)}, u32[]{:S(2)}) collective-permute-start(f32[72,128]{1,0:T(8,128)S(1)} %add_add_fusion.1), channel_id=1, source_target_pairs={{0,2},{1,3},{2,0},{3,1},{4,6},{5,7},{6,4},{7,5},{8,10},{9,11},{10,... | collective-permute-start | bytes 110600 | tf_op jit(solution)/shard_map/ppermute | solution.py:26
  112.0 4.4 %collective-permute-start.11 = (f32[72,128]{1,0:T(8,128)S(1)}, f32[72,128]{1,0:T(8,128)S(1)}, u32[]{:S(2)}, u32[]{:S(2)}) collective-permute-start(f32[72,128]{1,0:T(8,128)S(1)} %add_add_fusion.1), channel_id=1, source_target_pairs={{0,4},{1,5},{2,6},{3,7},{4,0},{5,1},{6,2},{7,3},{8,12},{9,13},{10,... | collective-permute-start | bytes 110600 | tf_op jit(solution)/shard_map/ppermute | solution.py:26
  115.0 4.7 %collective-permute-start.12 = (f32[72,128]{1,0:T(8,128)S(1)}, f32[72,128]{1,0:T(8,128)S(1)}, u32[]{:S(2)}, u32[]{:S(2)}) collective-permute-start(f32[72,128]{1,0:T(8,128)S(1)} %add_add_fusion.1), channel_id=1, source_target_pairs={{0,6},{1,7},{2,4},{3,5},{4,2},{5,3},{6,0},{7,1},{8,14},{9,15},{10,... | collective-permute-start | bytes 110600 | tf_op jit(solution)/shard_map/ppermute | solution.py:26
  119.8 13.2 %copy-start.14 = (f32[128,128]{0,1:T(8,128)S(1)}, f32[128,128]{0,1:T(8,128)}, u32[]{:S(2)}) copy-start(f32[128,128]{0,1:T(8,128)} %fusion.67) | copy-start | bytes 196612
  119.9 13.2 %copy-start.20 = (f32[32,128]{1,0:T(8,128)S(1)}, f32[32,128]{1,0:T(8,128)}, u32[]{:S(2)}) copy-start(f32[32,128]{1,0:T(8,128)} %copy.107) | copy-start | bytes 49156
  119.9 13.2 %copy-start.22 = (pred[128,128]{0,1:T(8,128)(4,1)S(1)}, pred[128,128]{0,1:T(8,128)(4,1)}, u32[]{:S(2)}) copy-start(pred[128,128]{0,1:T(8,128)(4,1)} %iota_compare_fusion) | copy-start | bytes 49156
  119.9 13.2 %copy-start.32 = (f32[32,128]{1,0:T(8,128)S(1)}, f32[32,128]{1,0:T(8,128)}, u32[]{:S(2)}) copy-start(f32[32,128]{1,0:T(8,128)} %get-tuple-element.55) | copy-start | bytes 49156
  119.9 4.1 %collective-permute-start.13 = (f32[288,128]{1,0:T(8,128)S(1)}, f32[288,128]{1,0:T(8,128)S(1)}, u32[]{:S(2)}, u32[]{:S(2)}) collective-permute-start(f32[288,128]{1,0:T(8,128)S(1)} %get-tuple-element.37), channel_id=1, source_target_pairs={{0,8},{8,0},{16,24},{24,16},{1,9},{9,1},{17,25},{25,17},{2,10},{10... | collective-permute-start | bytes 442376 | tf_op jit(solution)/shard_map/ppermute | solution.py:26
  121.2 4.0 %collective-permute-start.14 = (f32[288,128]{1,0:T(8,128)S(1)}, f32[288,128]{1,0:T(8,128)S(1)}, u32[]{:S(2)}, u32[]{:S(2)}) collective-permute-start(f32[288,128]{1,0:T(8,128)S(1)} %get-tuple-element.37), channel_id=1, source_target_pairs={{0,16},{8,24},{16,0},{24,8},{1,17},{9,25},{17,1},{25,9},{2,18},{10... | collective-permute-start | bytes 442376 | tf_op jit(solution)/shard_map/ppermute | solution.py:26
  121.6 5.2 %collective-permute-start.15 = (f32[288,128]{1,0:T(8,128)S(1)}, f32[288,128]{1,0:T(8,128)S(1)}, u32[]{:S(2)}, u32[]{:S(2)}) collective-permute-start(f32[288,128]{1,0:T(8,128)S(1)} %get-tuple-element.37), channel_id=1, source_target_pairs={{0,24},{8,16},{16,8},{24,0},{1,25},{9,17},{17,9},{25,1},{2,26},{10... | collective-permute-start | bytes 442376 | tf_op jit(solution)/shard_map/ppermute | solution.py:26
  126.9 10.8 %collective-permute-start.16 = (f32[1152,128]{1,0:T(8,128)S(1)}, f32[1152,128]{1,0:T(8,128)}, u32[]{:S(2)}, u32[]{:S(2)}) collective-permute-start(f32[1152,128]{1,0:T(8,128)S(1)} %get-tuple-element.24), channel_id=1, source_target_pairs={{0,1},{1,0},{2,3},{3,2},{4,5},{5,4},{6,7},{7,6},{8,9},{9,8},{10,11... | collective-permute-start | bytes 1769480 | tf_op jit(solution)/shard_map/ppermute | solution.py:26
  133.1 3.3 %copy-start.4 = (bf16[32,64,128]{2,1,0:T(8,128)(2,1)S(1)}, bf16[32,64,128]{2,1,0:T(8,128)(2,1)}, u32[]{:S(2)}) copy-start(bf16[32,64,128]{2,1,0:T(8,128)(2,1)} %copy-done.3) | copy-start | bytes 1572868
  (3 other events, 2.4 us)

commit v14 on v12

--- a/solution.py
+++ b/solution.py
@@ -130,8 +130,12 @@
     cum_all = jnp.cumsum(-step_all * decay_rate, axis=1)
     gate_all = jnp.exp(cum_all[:, -1])
     tail_all = jnp.exp(cum_all[:, -1:, :] - cum_all) * step_all
-    xw_all = (x_all * tail_all[..., None]).astype(half)
-    state_local_all = jnp.einsum("bthp,btn->bhpn", xw_all, b_all, preferred_element_type=fl)
+    head_all = jnp.exp(cum_all)
+    earlier = n_blocks - 1
+    xw_all = (x_all[:earlier] * tail_all[:earlier, :, :, None]).astype(half)
+    state_local_all = jnp.einsum(
+        "bthp,btn->bhpn", xw_all, b_all[:earlier], preferred_element_type=fl
+    )
 
     state_in = jnp.zeros((head_count, head_dim, state_dim), fl)
     for k in range(n_blocks - 1):
@@ -154,7 +158,7 @@
         c_all = projected_all[:, :, inner_width + state_dim :]
         for k in range(n_blocks - 1, 0, -1):
             later = seen[k - 1].reshape(tok_rows, head_count, head_dim)
-            later_weighted = (later * jnp.exp(cum_all[k])[:, :, None]).astype(half)
+            later_weighted = (later * head_all[k][:, :, None]).astype(half)
             later_local = jnp.einsum("thp,tn->hpn", later_weighted, c_all[k], preferred_element_type=fl)
             new = gate_all[k][:, None, None] * adjoint_in + later_local
             adjoint_in = jnp.where(k > my_block, new, adjoint_in)

time: 133 us -> 130 us (0.977)
  local copies, waits for them, and re-layouts: 29.4 us -> 26.8 us
    exp x4 -> x1, local copies, waits for them, and re-layouts: 5.3 us -> 0.81 us  [on_device(): head_all = jnp.exp(cum_all)]
    mul x1 -> x4, local copies, waits for them, and re-layouts: 1.05 us -> 4.34 us  [on_device(): later_weighted = (later * head_all[k][:, :, None]).astype(half)]
    convert_element_type x1, local copies, waits for them, and re-layouts: 5.36 us -> 3.56 us  [on_device(): xw_all = (x_all[:earlier] * tail_all[:earlier, :, :, None]).astype(half)]
    slice x1 -> x2, local copies, waits for them, and re-layouts: 0.08 us -> 1.73 us  [the longest x1 1.65 us: on_device(): xw_all = (x_all[:earlier] * tail_all[:earlier, :, :, None]).astype(half)]
    unnamed x79 -> x73, local copies, waits for them, and re-layouts: 5.28 us -> 5.52 us
  transfers between devices with their start and end apart: 18 -> 18, of which waited for: 11 -> 11; matrix products, arithmetic and copies ran while one was open for 45% -> 44% of each run, Pallas kernels for 0% -> 0%
where the time goes in v14:
time: 130 us; the launch traced here: 129 us
  starting transfers between devices  35.5 us (27%)
  matrix products  27.7 us (21%)
  local copies, waits for them, and re-layouts  26.8 us (21%)
  waiting for transfers between devices  22 us (17%)
  other arithmetic  15.5 us (12%)
  between operations  1.37 us (1%)
    ppermute x14, starting transfers between devices, exchange(): return lax.ppermute(value, axis, pairs)  24.5 us
    ppermute x14, waiting for transfers between devices, exchange(): return lax.ppermute(value, axis, pairs)  18.5 us
    all_to_all x1, starting transfers between devices, on_device(): lax.all_to_all(outgoing, ('tm', 'series'), split_axis=0, concat_axis=1, t...  7.1 us
    unnamed x73, local copies, waits for them, and re-layouts  5.52 us
    mul x4, local copies, waits for them, and re-layouts, on_device(): later_weighted = (later * head_all[k][:, :, None]).astype(half)  4.34 us
    dot_general x1, matrix products, on_device(): picked = jnp.dot(onehot, bin_table, precision=lax.Precision.HIGHEST)  4.14 us
    slice x2, local copies, waits for them, and re-layouts, on_device(): x_heads = projected[:, :inner_width].reshape(tok_rows, head_count, head_dim)  3.92 us
    convert_element_type x1, local copies, waits for them, and re-layouts, on_device(): xw_all = (x_all[:earlier] * tail_all[:earlier, :, :, None]).astype(half)  3.56 us
  transfers between devices with their start and end apart: 18, of which 11 were waited for; matrix products, arithmetic and copies ran while one was open for 44% of the time, Pallas kernels for 0%

profile of v14, /device:TPU:1, one launch (start us, length us, event | category | flops | bytes accessed | tf_op | source)
XLA Modules:
  0.0 128.9 jit_solution(17387321181965002899)
XLA Ops:
  2.0 1.2 gather_fusion
  4.0 7.1 %all-to-all-start = ((f32[32,1,16]{2,1,0:T(1,128)}), f32[32,1,16]{2,1,0:T(1,128)S(1)}, u32[]{:S(2)}, u32[]{:S(2)}) async-start(f32[32,1,16]{2,1,0:T(1,128)} %bitcast.1), calls=%async_computation | async-start | bytes 32768 | tf_op jit(solution)/shard_map/all_to_all | solution.py:92
  11.7 1.3 %copy.91 = bf16[1,128,2048]{1,2,0:T(8,128)(2,1)S(1)} copy(bf16[1,128,2048]{2,1,0:T(8,128)(2,1)} %param.15) | data formatting | bytes 1048576 | tf_op args[7]
  13.0 1.0 convert_bitcast_fusion
  14.2 3.5 %all-to-all-done = f32[32,1,16]{2,1,0:T(1,128)S(1)} async-done(((f32[32,1,16]{2,1,0:T(1,128)}), f32[32,1,16]{2,1,0:T(1,128)S(1)}, u32[]{:S(2)}, u32[]{:S(2)}) %all-to-all-start) | async-done | bytes 2080 | tf_op jit(solution)/shard_map/all_to_all | solution.py:92
  19.1 1.3 collective-permute-start
  20.4 1.3 %collective-permute-start.1 = (f32[128,2048]{0,1:T(8,128)}, f32[128,2048]{0,1:T(8,128)}, u32[]{:S(2)}, u32[]{:S(2)}) collective-permute-start(f32[128,2048]{0,1:T(8,128)} %convert_bitcast_fusion), channel_id=1, source_target_pairs={{24,8},{16,0},{25,9},{17,1},{26,10},{18,2},{27,11},{19,3},{28,12},... | collective-permute-start | bytes 3145736 | tf_op jit(solution)/shard_map/ppermute | solution.py:151
  21.7 1.3 %collective-permute-start.2 = (f32[128,2048]{0,1:T(8,128)}, f32[128,2048]{0,1:T(8,128)}, u32[]{:S(2)}, u32[]{:S(2)}) collective-permute-start(f32[128,2048]{0,1:T(8,128)} %convert_bitcast_fusion), channel_id=1, source_target_pairs={{16,8},{24,0},{17,9},{25,1},{18,10},{26,2},{19,11},{27,3},{20,12},... | collective-permute-start | bytes 3145736 | tf_op jit(solution)/shard_map/ppermute | solution.py:152
  23.0 1.4 %convert_reduce_fusion = f32[4096]{0:T(1024)S(1)} fusion(f32[4096]{0:T(1024)S(1)} %get-tuple-element.43, f32[4096]{0:T(1024)S(1)} %convert_element_type.117, f32[512]{0:T(512)S(1)} %squeeze.74), kind=kLoop, calls=%fused_computation.1 | loop fusion | flops 10481664 | bytes 51200 | tf_op jit(solution)/shard_map/reduce_sum | solution.py:99
  25.1 4.1 %fusion = f32[512,4]{0,1:T(4,128)S(1)} fusion(f32[4096]{0:T(1024)S(1)} %get-tuple-element.43, f32[4096]{0:T(1024)S(1)} %convert_element_type.117, f32[512]{0:T(512)S(1)} %squeeze.74, f32[4096,1]{0,1:T(1,128)S(1)} %bitcast.232, f32[4096,1]{0,1:T(1,128)S(1)} %bitcast.225, f32[4096,1]{0,1:T(1,128)S(1)} %bitcast.224, f32[4096,1]{0,1:T(1,128)S(1)} %sub.64), kind=kOutput, calls=%fused_computation.3 | convolution fusion | flops 107003904 | bytes 108544 | tf_op jit(solution)/shard_map/dot_general | solution.py:102
  29.3 1.1 compare_select_fusion
  32.4 1.6 %convolution_convert_fusion = bf16[512,2304]{1,0:T(8,128)(2,1)S(1)} fusion(bf16[128,2304]{1,0:T(8,128)(2,1)S(1)} %copy-done, f32[128]{0:T(128)S(1)} %add_multiply_fusion.1, f32[512]{0:T(512)S(1)} %add_multiply_fusion), kind=kOutput, calls=%fused_computation.4 | convolution fusion | flops 303300608 | bytes 2951680 | tf_op jit(solution)/shard_map/dot_general | solution.py:123
  34.0 1.0 compare_select_fusion.1
  35.1 1.4 %convolution_convert_fusion.1 = bf16[128,2304]{1,0:T(8,128)(2,1)} fusion(bf16[128,2304]{1,0:T(8,128)(2,1)S(1)} %copy-done, f32[128]{0:T(128)S(1)} %add_multiply_fusion.1, f32[1,128]{1,0:T(1,128)S(1)} %constant_dynamic-slice_fusion.7), kind=kOutput, calls=%fused_computation.8 | convolution fusion | flops 75825152 | bytes 1180672 | tf_op jit(solution)/shard_map/dot_general | solution.py:113
  37.3 1.0 reduce_window_sum.46
  39.5 1.5 %fusion.75 = f32[128,128]{0,1:T(8,128)} fusion(bf16[128,2304]{1,0:T(8,128)(2,1)} %convolution_convert_fusion.1), kind=kOutput, calls=%fused_computation.138 | convolution fusion | flops 4194304 | bytes 131072 | tf_op jit(solution)/shard_map/dot_general | solution.py:172
  41.1 1.9 %slice.134 = bf16[128,2048]{1,0:T(8,128)(2,1)} slice(bf16[128,2304]{1,0:T(8,128)(2,1)} %convolution_convert_fusion.1), slice={[0:128], [0:2048]} | slice | bytes 1048576 | tf_op jit(solution)/shard_map/slice | solution.py:114
  43.6 2.0 %copy.92 = bf16[128,2048]{0,1:T(8,128)(2,1)} copy(bf16[128,2048]{1,0:T(8,128)(2,1)} %slice.134) | data formatting | bytes 1048576 | tf_op jit(solution)/shard_map/slice | solution.py:114
  45.7 2.8 %fusion.4 = bf16[128,128]{0,1:T(8,128)(2,1)S(1)} fusion(bf16[128,32,64]{0,2,1:T(8,128)(2,1)} %bitcast.213, bf16[128,32,64]{0,2,1:T(8,128)(2,1)S(1)} %bitcast.203, f32[32,128]{1,0:T(8,128)} %get-tuple-element.52, f32[32,128]{1,0:T(8,128)} %copy.95, pred[128,128]{0,1:T(8,128)(4,1)} %iota_compare_fusion), kind=kOutput, calls=%fused_computation.11 | convolution fusion | flops 70238208 | bytes 1130496 | tf_op jit(solution)/shard_map/thp,shp->hts/dot_general | solution.py:189
  48.4 1.6 %fusion.77 = f32[128,128]{0,1:T(8,128)} fusion(bf16[128,2304]{1,0:T(8,128)(2,1)} %convolution_convert_fusion.1, bf16[128,128]{0,1:T(8,128)(2,1)S(1)} %fusion.4), kind=kOutput, calls=%fused_computation.140 | convolution fusion | flops 4194304 | bytes 131072 | tf_op jit(solution)/shard_map/dot_general | solution.py:191
  50.0 1.6 %fusion.72 = f32[128,128]{0,1:T(8,128)} fusion(bf16[128,2304]{1,0:T(8,128)(2,1)} %convolution_convert_fusion.1, bf16[128,128]{0,1:T(8,128)(2,1)S(1)} %fusion.4), kind=kOutput, calls=%fused_computation.135 | convolution fusion | flops 4194304 | bytes 131072 | tf_op jit(solution)/shard_map/dot_general | solution.py:193
  52.9 1.5 %copy.105 = f32[128,32]{0,1:T(8,128)} copy(f32[128,32]{1,0:T(8,128)} %get-tuple-element.32) | data formatting | bytes 32768 | tf_op jit(solution)/shard_map/mul | solution.py:161
  54.4 1.5 %copy.106 = f32[128,32]{0,1:T(8,128)} copy(f32[128,32]{1,0:T(8,128)} %get-tuple-element.31) | data formatting | bytes 32768 | tf_op jit(solution)/shard_map/mul | solution.py:161
  57.2 1.7 %slice_multiply_fusion = f32[3,128,32]{2,1,0:T(8,128)} fusion(f32[4,128,32]{2,1,0:T(8,128)} %bitcast.210, f32[4,128,32]{2,1,0:T(8,128)} %copy-done.2, f32[3,32]{1,0:T(4,128)S(1)} %bitcast.231), kind=kLoop, calls=%fused_computation.88 | loop fusion | flops 24576 | bytes 147840 | tf_op jit(solution)/shard_map/mul | solution.py:132
  58.9 1.7 %copy.101 = f32[3,128,32]{1,2,0:T(8,128)} copy(f32[3,128,32]{2,1,0:T(8,128)} %slice_multiply_fusion) | data formatting | bytes 98304 | tf_op jit(solution)/shard_map/slice | solution.py:135
  60.6 2.1 %slice_convert_fusion = f32[3,128,2048]{2,1,0:T(8,128)} fusion(bf16[4,128,2304]{2,1,0:T(8,128)(2,1)S(1)} %bitcast.198), kind=kLoop, calls=%fused_computation.15 | loop fusion | flops 786432 | bytes 4718592 | tf_op jit(solution)/shard_map/convert_element_type | solution.py:135
  62.7 3.6 %copy.99 = f32[3,128,2048]{1,2,0:T(8,128)} copy(f32[3,128,2048]{2,1,0:T(8,128)} %slice_convert_fusion) | data formatting | bytes 6291456 | tf_op jit(solution)/shard_map/convert_element_type | solution.py:135
  68.1 2.5 %fusion.5 = f32[3,32,64,128]{3,2,1,0:T(8,128)S(1)} fusion(f32[3,128,32,64]{1,3,2,0:T(8,128)} %bitcast.197, f32[3,128,32]{1,2,0:T(8,128)} %copy.101, bf16[4,128,2304]{2,1,0:T(8,128)(2,1)S(1)} %bitcast.199), kind=kOutput, calls=%fused_computation.14 | convolution fusion | flops 202899456 | bytes 6438912 | tf_op jit(solution)/shard_map/bthp,btn->bhpn/dot_general | solution.py:136
  72.3 1.3 %convolution_bitcast_fusion = f32[128,32,64]{0,2,1:T(8,128)S(1)} fusion(bf16[128,32,64]{0,2,1:T(8,128)(2,1)S(1)} %bitcast.204, f32[32,128]{1,0:T(8,128)S(1)} %copy-done.33, f32[32,128]{1,0:T(8,128)S(1)} %copy-done.17, f32[128,128]{0,1:T(8,128)S(1)} %copy-done.12, pred[128,128]{0,1:T(8,128)(4,1)S(1)} %copy-done.18), kind=kOutput, calls=%fused_computation.29 | convolution fusion | flops 70254592 | bytes 1687552 | tf_op jit(solution)/shard_map/hts,thp->shp/dot_general | solution.py:183
  73.6 2.2 %fusion.22 = (bf16[128,2048]{0,1:T(8,128)(2,1)S(1)}, bf16[128,2048]{0,1:T(8,128)(2,1)S(1)}, bf16[128,2048]{0,1:T(8,128)(2,1)S(1)}) fusion(f32[128,2048]{0,1:T(8,128)} %collective-permute-done.2, f32[128,2048]{0,1:T(8,128)} %collective-permute-done.1, f32[128,32]{0,1:T(8,128)S(1)} %copy-done.9, pred[]{:T(512)S(6)} %eq.19, f32[128,32]{0,1:T(8,128)S(1)} %copy-done.8, ...), kind=kLoop, calls=%fused_computation.52 | loop fusion | flops 2359296 | bytes 4767746 | tf_op jit(solution)/shard_map/convert_element_type | solution.py:161
  76.8 1.1 fusion.14
  79.6 1.6 %collective-permute-done.3 = f32[1152,128]{1,0:T(8,128)S(1)} collective-permute-done((f32[1152,128]{1,0:T(8,128)S(1)}, f32[1152,128]{1,0:T(8,128)S(1)}, u32[]{:S(2)}, u32[]{:S(2)}) %collective-permute-start.3) | collective-permute-done | bytes 589856 | tf_op jit(solution)/shard_map/ppermute | solution.py:26
  81.3 3.4 %collective-permute-start.4 = (f32[288,128]{1,0:T(8,128)S(1)}, f32[288,128]{1,0:T(8,128)S(1)}, u32[]{:S(2)}, u32[]{:S(2)}) collective-permute-start(f32[288,128]{1,0:T(8,128)S(1)} %get-tuple-element.27), channel_id=1, source_target_pairs={{0,8},{8,0},{16,24},{24,16},{1,9},{9,1},{17,25},{25,17},{2,10},{10... | collective-permute-start | bytes 442376 | tf_op jit(solution)/shard_map/ppermute | solution.py:26
  84.7 4.4 %collective-permute-start.5 = (f32[288,128]{1,0:T(8,128)S(1)}, f32[288,128]{1,0:T(8,128)S(1)}, u32[]{:S(2)}, u32[]{:S(2)}) collective-permute-start(f32[288,128]{1,0:T(8,128)S(1)} %get-tuple-element.29), channel_id=1, source_target_pairs={{0,16},{8,24},{16,0},{24,8},{1,17},{9,25},{17,1},{25,9},{2,18},{10... | collective-permute-start | bytes 442376 | tf_op jit(solution)/shard_map/ppermute | solution.py:26
  89.1 5.8 %collective-permute-done.5 = f32[288,128]{1,0:T(8,128)S(1)} collective-permute-done((f32[288,128]{1,0:T(8,128)S(1)}, f32[288,128]{1,0:T(8,128)S(1)}, u32[]{:S(2)}, u32[]{:S(2)}) %collective-permute-start.5) | collective-permute-done | bytes 147488 | tf_op jit(solution)/shard_map/ppermute | solution.py:26
  96.4 3.0 %collective-permute-start.9 = (f32[72,128]{1,0:T(8,128)S(1)}, f32[72,128]{1,0:T(8,128)S(1)}, u32[]{:S(2)}, u32[]{:S(2)}) collective-permute-start(f32[72,128]{1,0:T(8,128)S(1)} %get-tuple-element.40), channel_id=1, source_target_pairs={{0,6},{1,7},{2,4},{3,5},{4,2},{5,3},{6,0},{7,1},{8,14},{9,15},{10,... | collective-permute-start | bytes 110600 | tf_op jit(solution)/shard_map/ppermute | solution.py:26
  99.8 1.4 %collective-permute-done.9 = f32[72,128]{1,0:T(8,128)S(1)} collective-permute-done((f32[72,128]{1,0:T(8,128)S(1)}, f32[72,128]{1,0:T(8,128)S(1)}, u32[]{:S(2)}, u32[]{:S(2)}) %collective-permute-start.9) | collective-permute-done | bytes 36896 | tf_op jit(solution)/shard_map/ppermute | solution.py:26
  101.3 3.1 %collective-permute-start.11 = (f32[72,128]{1,0:T(8,128)S(1)}, f32[72,128]{1,0:T(8,128)S(1)}, u32[]{:S(2)}, u32[]{:S(2)}) collective-permute-start(f32[72,128]{1,0:T(8,128)S(1)} %add_add_fusion.1), channel_id=1, source_target_pairs={{0,4},{1,5},{2,6},{3,7},{4,0},{5,1},{6,2},{7,3},{8,12},{9,13},{10,... | collective-permute-start | bytes 110600 | tf_op jit(solution)/shard_map/ppermute | solution.py:26
  105.7 3.4 %collective-permute-done.12 = f32[72,128]{1,0:T(8,128)S(1)} collective-permute-done((f32[72,128]{1,0:T(8,128)S(1)}, f32[72,128]{1,0:T(8,128)S(1)}, u32[]{:S(2)}, u32[]{:S(2)}) %collective-permute-start.12) | collective-permute-done | bytes 36896 | tf_op jit(solution)/shard_map/ppermute | solution.py:26
  109.2 1.3 %collective-permute-start.13 = (f32[288,128]{1,0:T(8,128)S(1)}, f32[288,128]{1,0:T(8,128)S(1)}, u32[]{:S(2)}, u32[]{:S(2)}) collective-permute-start(f32[288,128]{1,0:T(8,128)S(1)} %get-tuple-element.34), channel_id=1, source_target_pairs={{0,8},{8,0},{16,24},{24,16},{1,9},{9,1},{17,25},{25,17},{2,10},{10... | collective-permute-start | bytes 442376 | tf_op jit(solution)/shard_map/ppermute | solution.py:26
  111.9 1.4 %collective-permute-done.13 = f32[288,128]{1,0:T(8,128)S(1)} collective-permute-done((f32[288,128]{1,0:T(8,128)S(1)}, f32[288,128]{1,0:T(8,128)S(1)}, u32[]{:S(2)}, u32[]{:S(2)}) %collective-permute-start.13) | collective-permute-done | bytes 147488 | tf_op jit(solution)/shard_map/ppermute | solution.py:26
  113.4 1.2 collective-permute-done.14
  114.5 1.6 %collective-permute-done.15 = f32[288,128]{1,0:T(8,128)S(1)} collective-permute-done((f32[288,128]{1,0:T(8,128)S(1)}, f32[288,128]{1,0:T(8,128)S(1)}, u32[]{:S(2)}, u32[]{:S(2)}) %collective-permute-start.15) | collective-permute-done | bytes 147488 | tf_op jit(solution)/shard_map/ppermute | solution.py:26
  116.3 6.1 %collective-permute-start.16 = (f32[1152,128]{1,0:T(8,128)S(1)}, f32[1152,128]{1,0:T(8,128)S(1)}, u32[]{:S(2)}, u32[]{:S(2)}) collective-permute-start(f32[1152,128]{1,0:T(8,128)S(1)} %get-tuple-element.21), channel_id=1, source_target_pairs={{0,1},{1,0},{2,3},{3,2},{4,5},{5,4},{6,7},{7,6},{8,9},{9,8},{10,11... | collective-permute-start | bytes 1769480 | tf_op jit(solution)/shard_map/ppermute | solution.py:26
  122.4 1.3 convolution_bitcast_fusion.1
  123.7 2.4 %fusion.12 = bf16[128,32,64]{0,2,1:T(8,128)(2,1)S(1)} fusion(f32[128,32,64]{0,2,1:T(8,128)S(1)} %convolution_bitcast_fusion.1, f32[3,32,64,128]{3,2,1,0:T(8,128)} %copy-done.1, f32[128,32]{0,1:T(8,128)S(1)} %copy.102, f32[32]{0:T(128)S(1)} %copy-done.30, f32[32]{0:T(128)S(1)} %copy-done.28, f32[32]{0:T(128)S(1)} %copy-done.26, pred[]{:T(512)S(6)} %gt.24, ...), kind=kOutput, calls=%fused_computation.35 | convolution fusion | flops 70254592 | bytes 4768131 | tf_op jit(solution)/shard_map/tn,hpn->thp/dot_general | solution.py:179
  126.1 1.0 copy.109
  127.5 1.4 %copy.110 = f32[128,2304]{1,0:T(8,128)} copy(f32[128,2304]{0,1:T(8,128)S(1)} %fusion.15) | data formatting | bytes 2359296
  (148 shorter events, 23.5 us)
Async XLA Ops:
  0.6 31.7 %copy-start = (bf16[128,2304]{1,0:T(8,128)(2,1)S(1)}, bf16[128,2304]{1,0:T(8,128)(2,1)}, u32[]{:S(2)}) copy-start(bf16[128,2304]{1,0:T(8,128)(2,1)} %param.11) | copy-start | bytes 1769476
  0.6 13.4 %copy-start.16 = (s32[4096]{0:T(1024)S(1)}, s32[4096]{0:T(1024)}, u32[]{:S(2)}) copy-start(s32[4096]{0:T(1024)} %param.10) | copy-start | bytes 49156
  4.0 13.8 %all-to-all-start = ((f32[32,1,16]{2,1,0:T(1,128)}), f32[32,1,16]{2,1,0:T(1,128)S(1)}, u32[]{:S(2)}, u32[]{:S(2)}) async-start(f32[32,1,16]{2,1,0:T(1,128)} %bitcast.1), calls=%async_computation | async-start | bytes 32768 | tf_op jit(solution)/shard_map/all_to_all | solution.py:92
  14.2 20.8 %copy-start.20 = (f32[128]{0:T(128)}, f32[128]{0:T(128)S(1)}, u32[]{:S(2)}) copy-start(f32[128]{0:T(128)S(1)} %add_multiply_fusion.1) | copy-start | bytes 1540
  19.1 54.5 %collective-permute-start = (f32[128,2048]{0,1:T(8,128)}, f32[128,2048]{0,1:T(8,128)}, u32[]{:S(2)}, u32[]{:S(2)}) collective-permute-start(f32[128,2048]{0,1:T(8,128)} %convert_bitcast_fusion), channel_id=1, source_target_pairs={{24,16},{8,0},{25,17},{9,1},{26,18},{10,2},{27,19},{11,3},{28,20},... | collective-permute-start | bytes 3145736 | tf_op jit(solution)/shard_map/ppermute | solution.py:150
  20.4 53.2 %collective-permute-start.1 = (f32[128,2048]{0,1:T(8,128)}, f32[128,2048]{0,1:T(8,128)}, u32[]{:S(2)}, u32[]{:S(2)}) collective-permute-start(f32[128,2048]{0,1:T(8,128)} %convert_bitcast_fusion), channel_id=1, source_target_pairs={{24,8},{16,0},{25,9},{17,1},{26,10},{18,2},{27,11},{19,3},{28,12},... | collective-permute-start | bytes 3145736 | tf_op jit(solution)/shard_map/ppermute | solution.py:151
  21.7 51.9 %collective-permute-start.2 = (f32[128,2048]{0,1:T(8,128)}, f32[128,2048]{0,1:T(8,128)}, u32[]{:S(2)}, u32[]{:S(2)}) collective-permute-start(f32[128,2048]{0,1:T(8,128)} %convert_bitcast_fusion), channel_id=1, source_target_pairs={{16,8},{24,0},{17,9},{25,1},{18,10},{26,2},{19,11},{27,3},{20,12},... | collective-permute-start | bytes 3145736 | tf_op jit(solution)/shard_map/ppermute | solution.py:152
  25.1 4.2 %copy-start.31 = (bf16[128,32]{0,1:T(8,128)(2,1)S(1)}, bf16[128,32]{0,1:T(8,128)(2,1)}, u32[]{:S(2)}) copy-start(bf16[128,32]{0,1:T(8,128)(2,1)} %param.12) | copy-start | bytes 24580
  25.1 4.2 %copy-start.32 = (f32[32]{0:T(128)S(1)}, f32[32]{0:T(128)}, u32[]{:S(2)}) copy-start(f32[32]{0:T(128)} %param.13) | copy-start | bytes 388
  25.1 6.2 %copy-start.22 = (f32[32]{0:T(128)S(1)}, f32[32]{0:T(128)}, u32[]{:S(2)}) copy-start(f32[32]{0:T(128)} %param.14) | copy-start | bytes 388
  34.0 2.4 %copy-start.23 = (f32[1,128]{1,0:T(1,128)}, f32[1,128]{1,0:T(1,128)S(1)}, u32[]{:S(2)}) copy-start(f32[1,128]{1,0:T(1,128)S(1)} %constant_dynamic-slice_fusion.7) | copy-start | bytes 1540
  35.1 1.4 %copy-start.11 = (f32[128,32]{0,1:T(8,128)}, f32[128,32]{0,1:T(8,128)S(1)}, u32[]{:S(2)}) copy-start(f32[128,32]{0,1:T(8,128)S(1)} %get-tuple-element.53) | copy-start | bytes 49156
  45.6 6.6 %copy-start.4 = (f32[4,128,32]{2,1,0:T(8,128)S(1)}, f32[4,128,32]{2,1,0:T(8,128)}, u32[]{:S(2)}) copy-start(f32[4,128,32]{2,1,0:T(8,128)} %exp.40) | copy-start | bytes 196612
  62.7 3.6 %copy-start.7 = (f32[128,32]{1,0:T(8,128)S(1)}, f32[128,32]{1,0:T(8,128)}, u32[]{:S(2)}) copy-start(f32[128,32]{1,0:T(8,128)} %exp.39) | copy-start | bytes 49156
  68.1 2.5 %copy-start.29 = (f32[32]{0:T(128)}, f32[32]{0:T(128)S(1)}, u32[]{:S(2)}) copy-start(f32[32]{0:T(128)S(1)} %get-tuple-element.49) | copy-start | bytes 388
  68.1 8.1 %copy-start.25 = (f32[32]{0:T(128)}, f32[32]{0:T(128)S(1)}, u32[]{:S(2)}) copy-start(f32[32]{0:T(128)S(1)} %get-tuple-element.51) | copy-start | bytes 388
  68.1 8.4 %copy-start.27 = (f32[32]{0:T(128)}, f32[32]{0:T(128)S(1)}, u32[]{:S(2)}) copy-start(f32[32]{0:T(128)S(1)} %get-tuple-element.50) | copy-start | bytes 388
  68.1 2.5 %copy-start.15 = (f32[128,128]{0,1:T(8,128)S(1)}, f32[128,128]{0,1:T(8,128)}, u32[]{:S(2)}) copy-start(f32[128,128]{0,1:T(8,128)} %fusion.72) | copy-start | bytes 196612
  70.6 1.6 %copy-start.1 = (f32[3,32,64,128]{3,2,1,0:T(8,128)}, f32[3,32,64,128]{3,2,1,0:T(8,128)S(1)}, u32[]{:S(2)}) copy-start(f32[3,32,64,128]{3,2,1,0:T(8,128)S(1)} %fusion.5) | copy-start | bytes 9437188
  70.6 1.6 %copy-start.12 = (f32[128,128]{0,1:T(8,128)S(1)}, f32[128,128]{0,1:T(8,128)}, u32[]{:S(2)}) copy-start(f32[128,128]{0,1:T(8,128)} %fusion.75) | copy-start | bytes 196612
  70.6 1.6 %copy-start.17 = (f32[32,128]{1,0:T(8,128)S(1)}, f32[32,128]{1,0:T(8,128)}, u32[]{:S(2)}) copy-start(f32[32,128]{1,0:T(8,128)} %copy.95) | copy-start | bytes 49156
  70.6 1.6 %copy-start.18 = (pred[128,128]{0,1:T(8,128)(4,1)S(1)}, pred[128,128]{0,1:T(8,128)(4,1)}, u32[]{:S(2)}) copy-start(pred[128,128]{0,1:T(8,128)(4,1)} %iota_compare_fusion) | copy-start | bytes 49156
  70.6 1.6 %copy-start.33 = (f32[32,128]{1,0:T(8,128)S(1)}, f32[32,128]{1,0:T(8,128)}, u32[]{:S(2)}) copy-start(f32[32,128]{1,0:T(8,128)} %get-tuple-element.52) | copy-start | bytes 49156
  72.2 1.4 %copy-start.8 = (f32[128,32]{0,1:T(8,128)S(1)}, f32[128,32]{0,1:T(8,128)}, u32[]{:S(2)}) copy-start(f32[128,32]{0,1:T(8,128)} %copy.105) | copy-start | bytes 49156
  72.2 1.4 %copy-start.9 = (f32[128,32]{0,1:T(8,128)S(1)}, f32[128,32]{0,1:T(8,128)}, u32[]{:S(2)}) copy-start(f32[128,32]{0,1:T(8,128)} %copy.106) | copy-start | bytes 49156
  72.3 1.4 %copy-start.10 = (f32[128,32]{0,1:T(8,128)S(1)}, f32[128,32]{0,1:T(8,128)}, u32[]{:S(2)}) copy-start(f32[128,32]{0,1:T(8,128)} %copy.107) | copy-start | bytes 49156
  76.5 1.4 %copy-start.5 = (bf16[128,2048]{0,1:T(8,128)(2,1)S(1)}, bf16[128,2048]{0,1:T(8,128)(2,1)}, u32[]{:S(2)}) copy-start(bf16[128,2048]{0,1:T(8,128)(2,1)} %copy.92) | copy-start | bytes 1572868
  76.5 1.4 %copy-start.14 = (f32[128,128]{0,1:T(8,128)S(1)}, f32[128,128]{0,1:T(8,128)}, u32[]{:S(2)}) copy-start(f32[128,128]{0,1:T(8,128)} %fusion.77) | copy-start | bytes 196612
  76.8 1.5 %copy-start.21 = (f32[128]{0:T(128)S(1)}, f32[128]{0:T(128)}, u32[]{:S(2)}) copy-start(f32[128]{0:T(128)} %copy-done.20) | copy-start | bytes 1540
  76.8 1.5 %copy-start.24 = (f32[1,128]{1,0:T(1,128)S(1)}, f32[1,128]{1,0:T(1,128)}, u32[]{:S(2)}) copy-start(f32[1,128]{1,0:T(1,128)} %copy-done.23) | copy-start | bytes 1540
  78.9 2.3 %collective-permute-start.3 = (f32[1152,128]{1,0:T(8,128)S(1)}, f32[1152,128]{1,0:T(8,128)S(1)}, u32[]{:S(2)}, u32[]{:S(2)}) collective-permute-start(f32[1152,128]{1,0:T(8,128)S(1)} %constant_dynamic-slice_fusion.6), channel_id=1, source_target_pairs={{0,1},{1,0},{2,3},{3,2},{4,5},{5,4},{6,7},{7,6},{8,9},{9,8},{10,11... | collective-permute-start | bytes 1769480 | tf_op jit(solution)/shard_map/ppermute | solution.py:26
  81.3 7.8 %collective-permute-start.4 = (f32[288,128]{1,0:T(8,128)S(1)}, f32[288,128]{1,0:T(8,128)S(1)}, u32[]{:S(2)}, u32[]{:S(2)}) collective-permute-start(f32[288,128]{1,0:T(8,128)S(1)} %get-tuple-element.27), channel_id=1, source_target_pairs={{0,8},{8,0},{16,24},{24,16},{1,9},{9,1},{17,25},{25,17},{2,10},{10... | collective-permute-start | bytes 442376 | tf_op jit(solution)/shard_map/ppermute | solution.py:26
  84.7 10.2 %collective-permute-start.5 = (f32[288,128]{1,0:T(8,128)S(1)}, f32[288,128]{1,0:T(8,128)S(1)}, u32[]{:S(2)}, u32[]{:S(2)}) collective-permute-start(f32[288,128]{1,0:T(8,128)S(1)} %get-tuple-element.29), channel_id=1, source_target_pairs={{0,16},{8,24},{16,0},{24,8},{1,17},{9,25},{17,1},{25,9},{2,18},{10... | collective-permute-start | bytes 442376 | tf_op jit(solution)/shard_map/ppermute | solution.py:26
  89.1 6.6 %collective-permute-start.6 = (f32[288,128]{1,0:T(8,128)S(1)}, f32[288,128]{1,0:T(8,128)S(1)}, u32[]{:S(2)}, u32[]{:S(2)}) collective-permute-start(f32[288,128]{1,0:T(8,128)S(1)} %get-tuple-element.28), channel_id=1, source_target_pairs={{0,24},{8,16},{16,8},{24,0},{1,25},{9,17},{17,9},{25,1},{2,26},{10... | collective-permute-start | bytes 442376 | tf_op jit(solution)/shard_map/ppermute | solution.py:26
  95.8 3.6 %collective-permute-start.7 = (f32[72,128]{1,0:T(8,128)S(1)}, f32[72,128]{1,0:T(8,128)S(1)}, u32[]{:S(2)}, u32[]{:S(2)}) collective-permute-start(f32[72,128]{1,0:T(8,128)S(1)} %get-tuple-element.39), channel_id=1, source_target_pairs={{0,2},{1,3},{2,0},{3,1},{4,6},{5,7},{6,4},{7,5},{8,10},{9,11},{10,... | collective-permute-start | bytes 110600 | tf_op jit(solution)/shard_map/ppermute | solution.py:26
  96.1 3.7 %collective-permute-start.8 = (f32[72,128]{1,0:T(8,128)S(1)}, f32[72,128]{1,0:T(8,128)S(1)}, u32[]{:S(2)}, u32[]{:S(2)}) collective-permute-start(f32[72,128]{1,0:T(8,128)S(1)} %get-tuple-element.41), channel_id=1, source_target_pairs={{0,4},{1,5},{2,6},{3,7},{4,0},{5,1},{6,2},{7,3},{8,12},{9,13},{10,... | collective-permute-start | bytes 110600 | tf_op jit(solution)/shard_map/ppermute | solution.py:26
  96.4 4.7 %collective-permute-start.9 = (f32[72,128]{1,0:T(8,128)S(1)}, f32[72,128]{1,0:T(8,128)S(1)}, u32[]{:S(2)}, u32[]{:S(2)}) collective-permute-start(f32[72,128]{1,0:T(8,128)S(1)} %get-tuple-element.40), channel_id=1, source_target_pairs={{0,6},{1,7},{2,4},{3,5},{4,2},{5,3},{6,0},{7,1},{8,14},{9,15},{10,... | collective-permute-start | bytes 110600 | tf_op jit(solution)/shard_map/ppermute | solution.py:26
  101.2 3.6 %collective-permute-start.10 = (f32[72,128]{1,0:T(8,128)S(1)}, f32[72,128]{1,0:T(8,128)S(1)}, u32[]{:S(2)}, u32[]{:S(2)}) collective-permute-start(f32[72,128]{1,0:T(8,128)S(1)} %add_add_fusion.1), channel_id=1, source_target_pairs={{0,2},{1,3},{2,0},{3,1},{4,6},{5,7},{6,4},{7,5},{8,10},{9,11},{10,... | collective-permute-start | bytes 110600 | tf_op jit(solution)/shard_map/ppermute | solution.py:26
  101.3 4.4 %collective-permute-start.11 = (f32[72,128]{1,0:T(8,128)S(1)}, f32[72,128]{1,0:T(8,128)S(1)}, u32[]{:S(2)}, u32[]{:S(2)}) collective-permute-start(f32[72,128]{1,0:T(8,128)S(1)} %add_add_fusion.1), channel_id=1, source_target_pairs={{0,4},{1,5},{2,6},{3,7},{4,0},{5,1},{6,2},{7,3},{8,12},{9,13},{10,... | collective-permute-start | bytes 110600 | tf_op jit(solution)/shard_map/ppermute | solution.py:26
  104.4 4.7 %collective-permute-start.12 = (f32[72,128]{1,0:T(8,128)S(1)}, f32[72,128]{1,0:T(8,128)S(1)}, u32[]{:S(2)}, u32[]{:S(2)}) collective-permute-start(f32[72,128]{1,0:T(8,128)S(1)} %add_add_fusion.1), channel_id=1, source_target_pairs={{0,6},{1,7},{2,4},{3,5},{4,2},{5,3},{6,0},{7,1},{8,14},{9,15},{10,... | collective-permute-start | bytes 110600 | tf_op jit(solution)/shard_map/ppermute | solution.py:26
  109.2 13.2 %copy-start.6 = (bf16[128,2048]{0,1:T(8,128)(2,1)S(1)}, bf16[128,2048]{0,1:T(8,128)(2,1)}, u32[]{:S(2)}) copy-start(bf16[128,2048]{0,1:T(8,128)(2,1)} %copy.92) | copy-start | bytes 1572868
  109.2 13.2 %copy-start.13 = (f32[128,128]{0,1:T(8,128)S(1)}, f32[128,128]{0,1:T(8,128)}, u32[]{:S(2)}) copy-start(f32[128,128]{0,1:T(8,128)} %fusion.75) | copy-start | bytes 196612
  109.2 13.2 %copy-start.19 = (pred[128,128]{0,1:T(8,128)(4,1)S(1)}, pred[128,128]{0,1:T(8,128)(4,1)}, u32[]{:S(2)}) copy-start(pred[128,128]{0,1:T(8,128)(4,1)} %iota_compare_fusion) | copy-start | bytes 49156
  109.2 13.2 %copy-start.34 = (f32[32,128]{1,0:T(8,128)S(1)}, f32[32,128]{1,0:T(8,128)}, u32[]{:S(2)}) copy-start(f32[32,128]{1,0:T(8,128)} %get-tuple-element.52) | copy-start | bytes 49156
  109.2 4.1 %collective-permute-start.13 = (f32[288,128]{1,0:T(8,128)S(1)}, f32[288,128]{1,0:T(8,128)S(1)}, u32[]{:S(2)}, u32[]{:S(2)}) collective-permute-start(f32[288,128]{1,0:T(8,128)S(1)} %get-tuple-element.34), channel_id=1, source_target_pairs={{0,8},{8,0},{16,24},{24,16},{1,9},{9,1},{17,25},{25,17},{2,10},{10... | collective-permute-start | bytes 442376 | tf_op jit(solution)/shard_map/ppermute | solution.py:26
  110.5 4.0 %collective-permute-start.14 = (f32[288,128]{1,0:T(8,128)S(1)}, f32[288,128]{1,0:T(8,128)S(1)}, u32[]{:S(2)}, u32[]{:S(2)}) collective-permute-start(f32[288,128]{1,0:T(8,128)S(1)} %get-tuple-element.34), channel_id=1, source_target_pairs={{0,16},{8,24},{16,0},{24,8},{1,17},{9,25},{17,1},{25,9},{2,18},{10... | collective-permute-start | bytes 442376 | tf_op jit(solution)/shard_map/ppermute | solution.py:26
  110.9 5.1 %collective-permute-start.15 = (f32[288,128]{1,0:T(8,128)S(1)}, f32[288,128]{1,0:T(8,128)S(1)}, u32[]{:S(2)}, u32[]{:S(2)}) collective-permute-start(f32[288,128]{1,0:T(8,128)S(1)} %get-tuple-element.34), channel_id=1, source_target_pairs={{0,24},{8,16},{16,8},{24,0},{1,25},{9,17},{17,9},{25,1},{2,26},{10... | collective-permute-start | bytes 442376 | tf_op jit(solution)/shard_map/ppermute | solution.py:26
  116.3 10.9 %collective-permute-start.16 = (f32[1152,128]{1,0:T(8,128)S(1)}, f32[1152,128]{1,0:T(8,128)S(1)}, u32[]{:S(2)}, u32[]{:S(2)}) collective-permute-start(f32[1152,128]{1,0:T(8,128)S(1)} %get-tuple-element.21), channel_id=1, source_target_pairs={{0,1},{1,0},{2,3},{3,2},{4,5},{5,4},{6,7},{7,6},{8,9},{9,8},{10,11... | collective-permute-start | bytes 1769480 | tf_op jit(solution)/shard_map/ppermute | solution.py:26
  (5 other events, 5.5 us)

commit v15 on v14

--- a/solution.py
+++ b/solution.py
@@ -99,7 +99,13 @@
     counts = jnp.sum(onehot, axis=0)
     before = jnp.cumsum(counts) - counts
     bin_table = jnp.stack([before, counts, edge_float, upper_edge - edge_float], axis=1)
-    picked = jnp.dot(onehot, bin_table, precision=lax.Precision.HIGHEST)
+    high = jnp.floor(bin_table / 65536.0) * 65536.0
+    middle = jnp.floor((bin_table - high) / 256.0) * 256.0
+    low = bin_table - high - middle
+    pieces = jnp.concatenate([high, middle, low], axis=1).astype(half)
+    picked3 = jnp.dot(onehot.astype(half), pieces, preferred_element_type=fl)
+    width = bin_table.shape[1]
+    picked = picked3[:, :width] + picked3[:, width : 2 * width] + picked3[:, 2 * width :]
     within_bin = (reading - picked[:, 2]) / picked[:, 3]
     quantile = (picked[:, 0] + picked[:, 1] * within_bin) / seq_len
     frequency = (jnp.arange(w_in.shape[0], dtype=fl) + 0.5) * math.pi

time: 130 us -> 135 us (1.038)
  waiting for transfers between devices: 22 us -> 42.6 us
  matrix products: 27.7 us -> 20 us
  starting transfers between devices: 35.5 us -> 29.5 us
  local copies, waits for them, and re-layouts: 26.8 us -> 24.6 us
    ppermute x1, waiting for transfers between devices: 0.01 us -> 21.3 us  [on_device(): along_y = lax.ppermute(sent, 'tm', [(3, 1), (2, 0)])]
    ppermute x14, starting transfers between devices: 24.5 us -> 18.4 us  [exchange(): return lax.ppermute(value, axis, pairs)]
    slice x2, local copies, waits for them, and re-layouts: 3.92 us -> 0.33 us  [on_device(): x_heads = projected[:, :inner_width].reshape(tok_rows, head_count, head_dim)]
    dot_general x1, matrix products: 4.14 us -> 1.26 us  [on_device(): picked3 = jnp.dot(onehot.astype(half), pieces, preferred_element_type=fl)]
    unnamed x73 -> x83, local copies, waits for them, and re-layouts: 5.52 us -> 6.63 us
  transfers between devices with their start and end apart: 18 -> 18, of which waited for: 11 -> 14; matrix products, arithmetic and copies ran while one was open for 44% -> 24% of each run, Pallas kernels for 0% -> 0%
where the time goes in v15:
time: 135 us; the launch traced here: 134 us
  waiting for transfers between devices  42.6 us (32%)
  starting transfers between devices  29.5 us (22%)
  local copies, waits for them, and re-layouts  24.6 us (18%)
  matrix products  20 us (15%)
  other arithmetic  15.7 us (12%)
  between operations  1.45 us (1%)
    ppermute x1, waiting for transfers between devices, on_device(): along_y = lax.ppermute(sent, 'tm', [(3, 1), (2, 0)])  21.3 us
    ppermute x14, starting transfers between devices, exchange(): return lax.ppermute(value, axis, pairs)  18.4 us
    ppermute x14, waiting for transfers between devices, exchange(): return lax.ppermute(value, axis, pairs)  17.9 us
    all_to_all x1, starting transfers between devices, on_device(): lax.all_to_all(outgoing, ('tm', 'series'), split_axis=0, concat_axis=1, t...  7.1 us
    unnamed x83, local copies, waits for them, and re-layouts  6.63 us
    mul x4, local copies, waits for them, and re-layouts, on_device(): later_weighted = (later * head_all[k][:, :, None]).astype(half)  5.26 us
    convert_element_type x1, local copies, waits for them, and re-layouts, on_device(): xw_all = (x_all[:earlier] * tail_all[:earlier, :, :, None]).astype(half)  3.54 us
    all_to_all x1, waiting for transfers between devices, on_device(): lax.all_to_all(outgoing, ('tm', 'series'), split_axis=0, concat_axis=1, t...  3.4 us
  transfers between devices with their start and end apart: 18, of which 14 were waited for; matrix products, arithmetic and copies ran while one was open for 24% of the time, Pallas kernels for 0%

profile of v15, /device:TPU:1, one launch (start us, length us, event | category | flops | bytes accessed | tf_op | source)
XLA Modules:
  0.0 133.8 jit_solution(9544065960437560551)
XLA Ops:
  2.1 1.2 gather_fusion
  4.0 7.1 %all-to-all-start = ((f32[32,1,16]{2,1,0:T(1,128)}), f32[32,1,16]{2,1,0:T(1,128)S(1)}, u32[]{:S(2)}, u32[]{:S(2)}) async-start(f32[32,1,16]{2,1,0:T(1,128)} %bitcast.1), calls=%async_computation | async-start | bytes 32768 | tf_op jit(solution)/shard_map/all_to_all | solution.py:92
  11.9 1.3 copy.91
  13.2 1.0 convert_bitcast_fusion
  14.4 3.4 %all-to-all-done = f32[32,1,16]{2,1,0:T(1,128)S(1)} async-done(((f32[32,1,16]{2,1,0:T(1,128)}), f32[32,1,16]{2,1,0:T(1,128)S(1)}, u32[]{:S(2)}, u32[]{:S(2)}) %all-to-all-start) | async-done | bytes 2080 | tf_op jit(solution)/shard_map/all_to_all | solution.py:92
  19.1 1.5 %convert_reduce_fusion = f32[4096]{0:T(1024)S(1)} fusion(f32[4096]{0:T(1024)S(1)} %get-tuple-element.46, f32[4096]{0:T(1024)S(1)} %convert_element_type.121, f32[512]{0:T(512)S(1)} %squeeze.74), kind=kLoop, calls=%fused_computation.1 | loop fusion | flops 10481664 | bytes 51200 | tf_op jit(solution)/shard_map/reduce_sum | solution.py:99
  21.3 1.3 fusion
  25.3 1.1 compare_select_fusion
  30.9 1.6 %fusion.2 = bf16[128,128]{0,1:T(8,128)(2,1)S(1)} fusion(bf16[128,32,64]{0,2,1:T(8,128)(2,1)S(1)} %bitcast.213, bf16[128,32,64]{0,2,1:T(8,128)(2,1)S(1)} %bitcast.203, f32[32,128]{1,0:T(8,128)S(1)} %get-tuple-element.55, f32[32,128]{1,0:T(8,128)S(1)} %copy.95, pred[128,128]{0,1:T(8,128)(4,1)S(1)} %iota_compare_fusion), kind=kOutput, calls=%fused_computation.10 | convolution fusion | flops 70238208 | bytes 1130496 | tf_op jit(solution)/shard_map/thp,shp->hts/dot_general | solution.py:195
  34.2 1.3 collective-permute-start.2
  35.5 1.3 collective-permute-start.1
  36.8 1.5 %collective-permute-start = (f32[128,2048]{0,1:T(8,128)}, f32[128,2048]{0,1:T(8,128)}, u32[]{:S(2)}, u32[]{:S(2)}) collective-permute-start(f32[128,2048]{0,1:T(8,128)} %convert_bitcast_fusion), channel_id=1, source_target_pairs={{24,16},{8,0},{25,17},{9,1},{26,18},{10,2},{27,19},{11,3},{28,20},... | collective-permute-start | bytes 3145736 | tf_op jit(solution)/shard_map/ppermute | solution.py:156
  38.3 1.6 %convolution_convert_fusion = bf16[512,2304]{1,0:T(8,128)(2,1)S(1)} fusion(bf16[128,2304]{1,0:T(8,128)(2,1)S(1)} %copy-done, f32[128]{0:T(128)S(1)} %add_multiply_fusion.1, f32[512]{0:T(512)S(1)} %add_multiply_fusion), kind=kOutput, calls=%fused_computation.4 | convolution fusion | flops 303300608 | bytes 2951680 | tf_op jit(solution)/shard_map/dot_general | solution.py:129
  40.0 1.3 exp.37
  41.2 1.7 %slice_multiply_fusion = f32[3,128,32]{2,1,0:T(8,128)} fusion(f32[4,128,32]{2,1,0:T(8,128)} %bitcast.210, f32[4,128,32]{2,1,0:T(8,128)} %copy-done.3, f32[3,32]{1,0:T(4,128)} %bitcast.232), kind=kLoop, calls=%fused_computation.87 | loop fusion | flops 24576 | bytes 147840 | tf_op jit(solution)/shard_map/mul | solution.py:138
  43.0 1.7 %copy.101 = f32[3,128,32]{1,2,0:T(8,128)} copy(f32[3,128,32]{2,1,0:T(8,128)} %slice_multiply_fusion) | data formatting | bytes 98304 | tf_op jit(solution)/shard_map/slice | solution.py:141
  44.6 1.6 %slice_bitcast_fusion.2 = (f32[128,32]{1,0:T(8,128)}, f32[128,32]{1,0:T(8,128)}, f32[128,32]{1,0:T(8,128)S(1)}) fusion(f32[4,128,32]{2,1,0:T(8,128)} %exp.40), kind=kLoop, calls=%fused_computation.108 | loop fusion | bytes 98304 | tf_op jit(solution)/shard_map/mul | solution.py:167
  46.2 1.5 %copy.107 = f32[128,32]{0,1:T(8,128)} copy(f32[128,32]{1,0:T(8,128)} %get-tuple-element.30) | data formatting | bytes 32768 | tf_op jit(solution)/shard_map/mul | solution.py:167
  47.7 1.5 %copy.106 = f32[128,32]{0,1:T(8,128)} copy(f32[128,32]{1,0:T(8,128)} %get-tuple-element.31) | data formatting | bytes 32768 | tf_op jit(solution)/shard_map/mul | solution.py:167
  50.8 2.1 %slice_convert_fusion = f32[3,128,2048]{2,1,0:T(8,128)} fusion(bf16[4,128,2304]{2,1,0:T(8,128)(2,1)S(1)} %bitcast.198), kind=kLoop, calls=%fused_computation.14 | loop fusion | flops 786432 | bytes 4718592 | tf_op jit(solution)/shard_map/convert_element_type | solution.py:141
  52.8 3.5 %copy.99 = f32[3,128,2048]{1,2,0:T(8,128)} copy(f32[3,128,2048]{2,1,0:T(8,128)} %slice_convert_fusion) | data formatting | bytes 6291456 | tf_op jit(solution)/shard_map/convert_element_type | solution.py:141
  58.1 2.5 %fusion.3 = f32[3,32,64,128]{3,2,1,0:T(8,128)S(1)} fusion(f32[3,128,32,64]{1,3,2,0:T(8,128)} %bitcast.197, f32[3,128,32]{1,2,0:T(8,128)S(1)} %copy-done.9, bf16[4,128,2304]{2,1,0:T(8,128)(2,1)S(1)} %bitcast.199), kind=kOutput, calls=%fused_computation.13 | convolution fusion | flops 202899456 | bytes 6438912 | tf_op jit(solution)/shard_map/bthp,btn->bhpn/dot_general | solution.py:142
  62.3 1.3 convolution_bitcast_fusion
  63.6 21.3 %collective-permute-done.1 = f32[128,2048]{0,1:T(8,128)} collective-permute-done((f32[128,2048]{0,1:T(8,128)}, f32[128,2048]{0,1:T(8,128)}, u32[]{:S(2)}, u32[]{:S(2)}) %collective-permute-start.1) | collective-permute-done | bytes 1048608 | tf_op jit(solution)/shard_map/ppermute | solution.py:157
  84.9 2.2 %fusion.20 = (bf16[128,2048]{0,1:T(8,128)(2,1)S(1)}, bf16[128,2048]{0,1:T(8,128)(2,1)S(1)}, bf16[128,2048]{0,1:T(8,128)(2,1)S(1)}) fusion(f32[128,2048]{0,1:T(8,128)} %collective-permute-done.2, f32[128,2048]{0,1:T(8,128)} %collective-permute-done.1, f32[128,32]{0,1:T(8,128)S(1)} %copy-done.11, pred[]{:T(512)S(6)} %eq.19, f32[128,32]{0,1:T(8,128)S(1)} %copy-done.12, ...), kind=kLoop, calls=%fused_computation.51 | loop fusion | flops 2359296 | bytes 4767746 | tf_op jit(solution)/shard_map/convert_element_type | solution.py:167
  88.8 1.1 fusion.12
  91.1 1.6 %collective-permute-done.3 = f32[1152,128]{1,0:T(8,128)S(1)} collective-permute-done((f32[1152,128]{1,0:T(8,128)S(1)}, f32[1152,128]{1,0:T(8,128)S(1)}, u32[]{:S(2)}, u32[]{:S(2)}) %collective-permute-start.3) | collective-permute-done | bytes 589856 | tf_op jit(solution)/shard_map/ppermute | solution.py:26
  93.0 1.3 collective-permute-start.6
  94.4 1.1 collective-permute-start.5
  95.5 2.4 %collective-permute-done.4 = f32[288,128]{1,0:T(8,128)S(1)} collective-permute-done((f32[288,128]{1,0:T(8,128)S(1)}, f32[288,128]{1,0:T(8,128)S(1)}, u32[]{:S(2)}, u32[]{:S(2)}) %collective-permute-start.4) | collective-permute-done | bytes 147488 | tf_op jit(solution)/shard_map/ppermute | solution.py:26
  97.9 3.2 %collective-permute-done.6 = f32[288,128]{1,0:T(8,128)S(1)} collective-permute-done((f32[288,128]{1,0:T(8,128)S(1)}, f32[288,128]{1,0:T(8,128)S(1)}, u32[]{:S(2)}, u32[]{:S(2)}) %collective-permute-start.6) | collective-permute-done | bytes 147488 | tf_op jit(solution)/shard_map/ppermute | solution.py:26
  101.2 1.0 collective-permute-done.5
  102.6 1.1 collective-permute-start.9
  103.7 1.3 collective-permute-start.8
  105.1 2.6 %collective-permute-done.9 = f32[72,128]{1,0:T(8,128)S(1)} collective-permute-done((f32[72,128]{1,0:T(8,128)S(1)}, f32[72,128]{1,0:T(8,128)S(1)}, u32[]{:S(2)}, u32[]{:S(2)}) %collective-permute-start.9) | collective-permute-done | bytes 36896 | tf_op jit(solution)/shard_map/ppermute | solution.py:26
  108.1 2.0 %collective-permute-start.12 = (f32[72,128]{1,0:T(8,128)S(1)}, f32[72,128]{1,0:T(8,128)S(1)}, u32[]{:S(2)}, u32[]{:S(2)}) collective-permute-start(f32[72,128]{1,0:T(8,128)S(1)} %add_add_fusion.1), channel_id=1, source_target_pairs={{0,6},{1,7},{2,4},{3,5},{4,2},{5,3},{6,0},{7,1},{8,14},{9,15},{10,... | collective-permute-start | bytes 110600 | tf_op jit(solution)/shard_map/ppermute | solution.py:26
  110.1 1.6 %collective-permute-start.10 = (f32[72,128]{1,0:T(8,128)S(1)}, f32[72,128]{1,0:T(8,128)S(1)}, u32[]{:S(2)}, u32[]{:S(2)}) collective-permute-start(f32[72,128]{1,0:T(8,128)S(1)} %add_add_fusion.1), channel_id=1, source_target_pairs={{0,2},{1,3},{2,0},{3,1},{4,6},{5,7},{6,4},{7,5},{8,10},{9,11},{10,... | collective-permute-start | bytes 110600 | tf_op jit(solution)/shard_map/ppermute | solution.py:26
  111.7 1.1 collective-permute-done.12
  112.8 1.3 collective-permute-done.11
  114.2 1.2 collective-permute-start.14
  117.0 1.4 %collective-permute-done.14 = f32[288,128]{1,0:T(8,128)S(1)} collective-permute-done((f32[288,128]{1,0:T(8,128)S(1)}, f32[288,128]{1,0:T(8,128)S(1)}, u32[]{:S(2)}, u32[]{:S(2)}) %collective-permute-start.14) | collective-permute-done | bytes 147488 | tf_op jit(solution)/shard_map/ppermute | solution.py:26
  118.3 1.1 collective-permute-done.13
  119.4 1.6 %collective-permute-done.15 = f32[288,128]{1,0:T(8,128)S(1)} collective-permute-done((f32[288,128]{1,0:T(8,128)S(1)}, f32[288,128]{1,0:T(8,128)S(1)}, u32[]{:S(2)}, u32[]{:S(2)}) %collective-permute-start.15) | collective-permute-done | bytes 147488 | tf_op jit(solution)/shard_map/ppermute | solution.py:26
  121.3 6.1 %collective-permute-start.16 = (f32[1152,128]{1,0:T(8,128)S(1)}, f32[1152,128]{1,0:T(8,128)S(1)}, u32[]{:S(2)}, u32[]{:S(2)}) collective-permute-start(f32[1152,128]{1,0:T(8,128)S(1)} %get-tuple-element.21), channel_id=1, source_target_pairs={{0,1},{1,0},{2,3},{3,2},{4,5},{5,4},{6,7},{7,6},{8,9},{9,8},{10,11... | collective-permute-start | bytes 1769480 | tf_op jit(solution)/shard_map/ppermute | solution.py:26
  127.4 1.3 convolution_bitcast_fusion.1
  128.7 2.4 %fusion.10 = bf16[128,32,64]{0,2,1:T(8,128)(2,1)S(1)} fusion(f32[128,32,64]{0,2,1:T(8,128)S(1)} %convolution_bitcast_fusion.1, f32[3,32,64,128]{3,2,1,0:T(8,128)} %copy-done.1, f32[128,32]{0,1:T(8,128)S(1)} %copy.102, f32[32]{0:T(128)S(1)} %copy-done.34, f32[32]{0:T(128)S(1)} %copy-done.32, f32[32]{0:T(128)S(1)} %copy-done.30, pred[]{:T(512)S(6)} %gt.24, ...), kind=kOutput, calls=%fused_computation.34 | convolution fusion | flops 70254592 | bytes 4768131 | tf_op jit(solution)/shard_map/tn,hpn->thp/dot_general | solution.py:185
  131.1 1.0 copy.109
  132.4 1.4 %copy.110 = f32[128,2304]{1,0:T(8,128)} copy(f32[128,2304]{0,1:T(8,128)S(1)} %fusion.13) | data formatting | bytes 2359296
  (160 shorter events, 24.8 us)
Async XLA Ops:
  0.6 28.4 %copy-start = (bf16[128,2304]{1,0:T(8,128)(2,1)S(1)}, bf16[128,2304]{1,0:T(8,128)(2,1)}, u32[]{:S(2)}) copy-start(bf16[128,2304]{1,0:T(8,128)(2,1)} %param.11) | copy-start | bytes 1769476
  0.6 13.6 %copy-start.18 = (s32[4096]{0:T(1024)S(1)}, s32[4096]{0:T(1024)}, u32[]{:S(2)}) copy-start(s32[4096]{0:T(1024)} %param.10) | copy-start | bytes 49156
  4.0 13.8 %all-to-all-start = ((f32[32,1,16]{2,1,0:T(1,128)}), f32[32,1,16]{2,1,0:T(1,128)S(1)}, u32[]{:S(2)}, u32[]{:S(2)}) async-start(f32[32,1,16]{2,1,0:T(1,128)} %bitcast.1), calls=%async_computation | async-start | bytes 32768 | tf_op jit(solution)/shard_map/all_to_all | solution.py:92
  11.1 19.8 %copy-start.21 = (pred[128,128]{0,1:T(8,128)(4,1)}, pred[128,128]{0,1:T(8,128)(4,1)S(1)}, u32[]{:S(2)}) copy-start(pred[128,128]{0,1:T(8,128)(4,1)S(1)} %iota_compare_fusion) | copy-start | bytes 49156
  14.4 23.9 %copy-start.24 = (f32[128]{0:T(128)}, f32[128]{0:T(128)S(1)}, u32[]{:S(2)}) copy-start(f32[128]{0:T(128)S(1)} %add_multiply_fusion.1) | copy-start | bytes 1540
  21.3 2.4 %copy-start.26 = (f32[32]{0:T(128)S(1)}, f32[32]{0:T(128)}, u32[]{:S(2)}) copy-start(f32[32]{0:T(128)} %param.14) | copy-start | bytes 388
  22.7 7.9 %copy-start.27 = (f32[1,128]{1,0:T(1,128)}, f32[1,128]{1,0:T(1,128)S(1)}, u32[]{:S(2)}) copy-start(f32[1,128]{1,0:T(1,128)S(1)} %constant_dynamic-slice_fusion.7) | copy-start | bytes 1540
  23.1 7.8 %copy-start.37 = (f32[32,128]{1,0:T(8,128)}, f32[32,128]{1,0:T(8,128)S(1)}, u32[]{:S(2)}) copy-start(f32[32,128]{1,0:T(8,128)S(1)} %get-tuple-element.55) | copy-start | bytes 49156
  29.6 3.8 %copy-start.2 = (bf16[128,2304]{1,0:T(8,128)(2,1)}, bf16[128,2304]{1,0:T(8,128)(2,1)S(1)}, u32[]{:S(2)}) copy-start(bf16[128,2304]{1,0:T(8,128)(2,1)S(1)} %convolution_convert_fusion.1) | copy-start | bytes 1769476
  30.6 1.9 %copy-start.19 = (f32[32,128]{1,0:T(8,128)}, f32[32,128]{1,0:T(8,128)S(1)}, u32[]{:S(2)}) copy-start(f32[32,128]{1,0:T(8,128)S(1)} %copy.95) | copy-start | bytes 49156
  30.9 1.6 %copy-start.5 = (bf16[128,2048]{0,1:T(8,128)(2,1)}, bf16[128,2048]{0,1:T(8,128)(2,1)S(1)}, u32[]{:S(2)}) copy-start(bf16[128,2048]{0,1:T(8,128)(2,1)S(1)} %copy.92) | copy-start | bytes 1572868
  34.2 29.4 %collective-permute-start.2 = (f32[128,2048]{0,1:T(8,128)}, f32[128,2048]{0,1:T(8,128)}, u32[]{:S(2)}, u32[]{:S(2)}) collective-permute-start(f32[128,2048]{0,1:T(8,128)} %convert_bitcast_fusion), channel_id=1, source_target_pairs={{16,8},{24,0},{17,9},{25,1},{18,10},{26,2},{19,11},{27,3},{20,12},... | collective-permute-start | bytes 3145736 | tf_op jit(solution)/shard_map/ppermute | solution.py:158
  35.5 49.4 %collective-permute-start.1 = (f32[128,2048]{0,1:T(8,128)}, f32[128,2048]{0,1:T(8,128)}, u32[]{:S(2)}, u32[]{:S(2)}) collective-permute-start(f32[128,2048]{0,1:T(8,128)} %convert_bitcast_fusion), channel_id=1, source_target_pairs={{24,8},{16,0},{25,9},{17,1},{26,10},{18,2},{27,11},{19,3},{28,12},... | collective-permute-start | bytes 3145736 | tf_op jit(solution)/shard_map/ppermute | solution.py:157
  36.8 48.1 %collective-permute-start = (f32[128,2048]{0,1:T(8,128)}, f32[128,2048]{0,1:T(8,128)}, u32[]{:S(2)}, u32[]{:S(2)}) collective-permute-start(f32[128,2048]{0,1:T(8,128)} %convert_bitcast_fusion), channel_id=1, source_target_pairs={{24,16},{8,0},{25,17},{9,1},{26,18},{10,2},{27,19},{11,3},{28,20},... | collective-permute-start | bytes 3145736 | tf_op jit(solution)/shard_map/ppermute | solution.py:156
  52.8 5.2 %copy-start.9 = (f32[3,128,32]{1,2,0:T(8,128)S(1)}, f32[3,128,32]{1,2,0:T(8,128)}, u32[]{:S(2)}) copy-start(f32[3,128,32]{1,2,0:T(8,128)} %copy.101) | copy-start | bytes 147460
  58.0 2.6 %copy-start.33 = (f32[32]{0:T(128)}, f32[32]{0:T(128)S(1)}, u32[]{:S(2)}) copy-start(f32[32]{0:T(128)S(1)} %get-tuple-element.52) | copy-start | bytes 388
  58.0 29.4 %copy-start.29 = (f32[32]{0:T(128)}, f32[32]{0:T(128)S(1)}, u32[]{:S(2)}) copy-start(f32[32]{0:T(128)S(1)} %get-tuple-element.54) | copy-start | bytes 388
  58.0 29.7 %copy-start.31 = (f32[32]{0:T(128)}, f32[32]{0:T(128)S(1)}, u32[]{:S(2)}) copy-start(f32[32]{0:T(128)S(1)} %get-tuple-element.53) | copy-start | bytes 388
  58.0 2.5 %copy-start.8 = (bf16[1,128,2048]{1,2,0:T(8,128)(2,1)S(1)}, bf16[1,128,2048]{1,2,0:T(8,128)(2,1)}, u32[]{:S(2)}) copy-start(bf16[1,128,2048]{1,2,0:T(8,128)(2,1)} %fusion.18) | copy-start | bytes 1572868
  58.1 2.5 %copy-start.17 = (f32[128,128]{0,1:T(8,128)S(1)}, f32[128,128]{0,1:T(8,128)}, u32[]{:S(2)}) copy-start(f32[128,128]{0,1:T(8,128)} %fusion.71) | copy-start | bytes 196612
  60.6 1.6 %copy-start.1 = (f32[3,32,64,128]{3,2,1,0:T(8,128)}, f32[3,32,64,128]{3,2,1,0:T(8,128)S(1)}, u32[]{:S(2)}) copy-start(f32[3,32,64,128]{3,2,1,0:T(8,128)S(1)} %fusion.3) | copy-start | bytes 9437188
  60.6 1.6 %copy-start.14 = (f32[128,128]{0,1:T(8,128)S(1)}, f32[128,128]{0,1:T(8,128)}, u32[]{:S(2)}) copy-start(f32[128,128]{0,1:T(8,128)} %fusion.74) | copy-start | bytes 196612
  60.6 1.6 %copy-start.20 = (f32[32,128]{1,0:T(8,128)S(1)}, f32[32,128]{1,0:T(8,128)}, u32[]{:S(2)}) copy-start(f32[32,128]{1,0:T(8,128)} %copy-done.19) | copy-start | bytes 49156
  60.6 1.6 %copy-start.22 = (pred[128,128]{0,1:T(8,128)(4,1)S(1)}, pred[128,128]{0,1:T(8,128)(4,1)}, u32[]{:S(2)}) copy-start(pred[128,128]{0,1:T(8,128)(4,1)} %copy-done.21) | copy-start | bytes 49156
  60.6 1.6 %copy-start.38 = (f32[32,128]{1,0:T(8,128)S(1)}, f32[32,128]{1,0:T(8,128)}, u32[]{:S(2)}) copy-start(f32[32,128]{1,0:T(8,128)} %copy-done.37) | copy-start | bytes 49156
  62.2 22.6 %copy-start.10 = (f32[128,32]{0,1:T(8,128)S(1)}, f32[128,32]{0,1:T(8,128)}, u32[]{:S(2)}) copy-start(f32[128,32]{0,1:T(8,128)} %copy.107) | copy-start | bytes 49156
  62.2 22.6 %copy-start.11 = (f32[128,32]{0,1:T(8,128)S(1)}, f32[128,32]{0,1:T(8,128)}, u32[]{:S(2)}) copy-start(f32[128,32]{0,1:T(8,128)} %copy.106) | copy-start | bytes 49156
  62.2 22.6 %copy-start.12 = (f32[128,32]{0,1:T(8,128)S(1)}, f32[128,32]{0,1:T(8,128)}, u32[]{:S(2)}) copy-start(f32[128,32]{0,1:T(8,128)} %copy.105) | copy-start | bytes 49156
  88.4 1.4 %copy-start.25 = (f32[128]{0:T(128)S(1)}, f32[128]{0:T(128)}, u32[]{:S(2)}) copy-start(f32[128]{0:T(128)} %copy-done.24) | copy-start | bytes 1540
  88.4 1.4 %copy-start.28 = (f32[1,128]{1,0:T(1,128)S(1)}, f32[1,128]{1,0:T(1,128)}, u32[]{:S(2)}) copy-start(f32[1,128]{1,0:T(1,128)} %copy-done.27) | copy-start | bytes 1540
  90.5 2.2 %collective-permute-start.3 = (f32[1152,128]{1,0:T(8,128)S(1)}, f32[1152,128]{1,0:T(8,128)S(1)}, u32[]{:S(2)}, u32[]{:S(2)}) collective-permute-start(f32[1152,128]{1,0:T(8,128)S(1)} %constant_dynamic-slice_fusion.6), channel_id=1, source_target_pairs={{0,1},{1,0},{2,3},{3,2},{4,5},{5,4},{6,7},{7,6},{8,9},{9,8},{10,11... | collective-permute-start | bytes 1769480 | tf_op jit(solution)/shard_map/ppermute | solution.py:26
  92.8 5.1 %collective-permute-start.4 = (f32[288,128]{1,0:T(8,128)S(1)}, f32[288,128]{1,0:T(8,128)S(1)}, u32[]{:S(2)}, u32[]{:S(2)}) collective-permute-start(f32[288,128]{1,0:T(8,128)S(1)} %get-tuple-element.27), channel_id=1, source_target_pairs={{0,8},{8,0},{16,24},{24,16},{1,9},{9,1},{17,25},{25,17},{2,10},{10... | collective-permute-start | bytes 442376 | tf_op jit(solution)/shard_map/ppermute | solution.py:26
  93.0 8.1 %collective-permute-start.6 = (f32[288,128]{1,0:T(8,128)S(1)}, f32[288,128]{1,0:T(8,128)S(1)}, u32[]{:S(2)}, u32[]{:S(2)}) collective-permute-start(f32[288,128]{1,0:T(8,128)S(1)} %get-tuple-element.28), channel_id=1, source_target_pairs={{0,24},{8,16},{16,8},{24,0},{1,25},{9,17},{17,9},{25,1},{2,26},{10... | collective-permute-start | bytes 442376 | tf_op jit(solution)/shard_map/ppermute | solution.py:26
  94.4 7.8 %collective-permute-start.5 = (f32[288,128]{1,0:T(8,128)S(1)}, f32[288,128]{1,0:T(8,128)S(1)}, u32[]{:S(2)}, u32[]{:S(2)}) collective-permute-start(f32[288,128]{1,0:T(8,128)S(1)} %get-tuple-element.29), channel_id=1, source_target_pairs={{0,16},{8,24},{16,0},{24,8},{1,17},{9,25},{17,1},{25,9},{2,18},{10... | collective-permute-start | bytes 442376 | tf_op jit(solution)/shard_map/ppermute | solution.py:26
  102.3 2.9 %collective-permute-start.7 = (f32[72,128]{1,0:T(8,128)S(1)}, f32[72,128]{1,0:T(8,128)S(1)}, u32[]{:S(2)}, u32[]{:S(2)}) collective-permute-start(f32[72,128]{1,0:T(8,128)S(1)} %get-tuple-element.39), channel_id=1, source_target_pairs={{0,2},{1,3},{2,0},{3,1},{4,6},{5,7},{6,4},{7,5},{8,10},{9,11},{10,... | collective-permute-start | bytes 110600 | tf_op jit(solution)/shard_map/ppermute | solution.py:26
  102.6 5.1 %collective-permute-start.9 = (f32[72,128]{1,0:T(8,128)S(1)}, f32[72,128]{1,0:T(8,128)S(1)}, u32[]{:S(2)}, u32[]{:S(2)}) collective-permute-start(f32[72,128]{1,0:T(8,128)S(1)} %get-tuple-element.40), channel_id=1, source_target_pairs={{0,6},{1,7},{2,4},{3,5},{4,2},{5,3},{6,0},{7,1},{8,14},{9,15},{10,... | collective-permute-start | bytes 110600 | tf_op jit(solution)/shard_map/ppermute | solution.py:26
  103.7 4.4 %collective-permute-start.8 = (f32[72,128]{1,0:T(8,128)S(1)}, f32[72,128]{1,0:T(8,128)S(1)}, u32[]{:S(2)}, u32[]{:S(2)}) collective-permute-start(f32[72,128]{1,0:T(8,128)S(1)} %get-tuple-element.41), channel_id=1, source_target_pairs={{0,4},{1,5},{2,6},{3,7},{4,0},{5,1},{6,2},{7,3},{8,12},{9,13},{10,... | collective-permute-start | bytes 110600 | tf_op jit(solution)/shard_map/ppermute | solution.py:26
  108.1 4.7 %collective-permute-start.12 = (f32[72,128]{1,0:T(8,128)S(1)}, f32[72,128]{1,0:T(8,128)S(1)}, u32[]{:S(2)}, u32[]{:S(2)}) collective-permute-start(f32[72,128]{1,0:T(8,128)S(1)} %add_add_fusion.1), channel_id=1, source_target_pairs={{0,6},{1,7},{2,4},{3,5},{4,2},{5,3},{6,0},{7,1},{8,14},{9,15},{10,... | collective-permute-start | bytes 110600 | tf_op jit(solution)/shard_map/ppermute | solution.py:26
  110.1 4.0 %collective-permute-start.11 = (f32[72,128]{1,0:T(8,128)S(1)}, f32[72,128]{1,0:T(8,128)S(1)}, u32[]{:S(2)}, u32[]{:S(2)}) collective-permute-start(f32[72,128]{1,0:T(8,128)S(1)} %add_add_fusion.1), channel_id=1, source_target_pairs={{0,4},{1,5},{2,6},{3,7},{4,0},{5,1},{6,2},{7,3},{8,12},{9,13},{10,... | collective-permute-start | bytes 110600 | tf_op jit(solution)/shard_map/ppermute | solution.py:26
  110.1 4.0 %collective-permute-start.10 = (f32[72,128]{1,0:T(8,128)S(1)}, f32[72,128]{1,0:T(8,128)S(1)}, u32[]{:S(2)}, u32[]{:S(2)}) collective-permute-start(f32[72,128]{1,0:T(8,128)S(1)} %add_add_fusion.1), channel_id=1, source_target_pairs={{0,2},{1,3},{2,0},{3,1},{4,6},{5,7},{6,4},{7,5},{8,10},{9,11},{10,... | collective-permute-start | bytes 110600 | tf_op jit(solution)/shard_map/ppermute | solution.py:26
  114.2 13.1 %copy-start.7 = (bf16[128,2048]{0,1:T(8,128)(2,1)S(1)}, bf16[128,2048]{0,1:T(8,128)(2,1)}, u32[]{:S(2)}) copy-start(bf16[128,2048]{0,1:T(8,128)(2,1)} %copy-done.5) | copy-start | bytes 1572868
  114.2 13.1 %copy-start.15 = (f32[128,128]{0,1:T(8,128)S(1)}, f32[128,128]{0,1:T(8,128)}, u32[]{:S(2)}) copy-start(f32[128,128]{0,1:T(8,128)} %fusion.74) | copy-start | bytes 196612
  114.2 13.1 %copy-start.23 = (pred[128,128]{0,1:T(8,128)(4,1)S(1)}, pred[128,128]{0,1:T(8,128)(4,1)}, u32[]{:S(2)}) copy-start(pred[128,128]{0,1:T(8,128)(4,1)} %copy-done.21) | copy-start | bytes 49156
  114.2 13.1 %copy-start.39 = (f32[32,128]{1,0:T(8,128)S(1)}, f32[32,128]{1,0:T(8,128)}, u32[]{:S(2)}) copy-start(f32[32,128]{1,0:T(8,128)} %copy-done.37) | copy-start | bytes 49156
  114.2 4.1 %collective-permute-start.14 = (f32[288,128]{1,0:T(8,128)S(1)}, f32[288,128]{1,0:T(8,128)S(1)}, u32[]{:S(2)}, u32[]{:S(2)}) collective-permute-start(f32[288,128]{1,0:T(8,128)S(1)} %get-tuple-element.34), channel_id=1, source_target_pairs={{0,16},{8,24},{16,0},{24,8},{1,17},{9,25},{17,1},{25,9},{2,18},{10... | collective-permute-start | bytes 442376 | tf_op jit(solution)/shard_map/ppermute | solution.py:26
  115.5 4.0 %collective-permute-start.13 = (f32[288,128]{1,0:T(8,128)S(1)}, f32[288,128]{1,0:T(8,128)S(1)}, u32[]{:S(2)}, u32[]{:S(2)}) collective-permute-start(f32[288,128]{1,0:T(8,128)S(1)} %get-tuple-element.34), channel_id=1, source_target_pairs={{0,8},{8,0},{16,24},{24,16},{1,9},{9,1},{17,25},{25,17},{2,10},{10... | collective-permute-start | bytes 442376 | tf_op jit(solution)/shard_map/ppermute | solution.py:26
  116.0 5.1 %collective-permute-start.15 = (f32[288,128]{1,0:T(8,128)S(1)}, f32[288,128]{1,0:T(8,128)S(1)}, u32[]{:S(2)}, u32[]{:S(2)}) collective-permute-start(f32[288,128]{1,0:T(8,128)S(1)} %get-tuple-element.34), channel_id=1, source_target_pairs={{0,24},{8,16},{16,8},{24,0},{1,25},{9,17},{17,9},{25,1},{2,26},{10... | collective-permute-start | bytes 442376 | tf_op jit(solution)/shard_map/ppermute | solution.py:26
  121.3 10.9 %collective-permute-start.16 = (f32[1152,128]{1,0:T(8,128)S(1)}, f32[1152,128]{1,0:T(8,128)S(1)}, u32[]{:S(2)}, u32[]{:S(2)}) collective-permute-start(f32[1152,128]{1,0:T(8,128)S(1)} %get-tuple-element.21), channel_id=1, source_target_pairs={{0,1},{1,0},{2,3},{3,2},{4,5},{5,4},{6,7},{7,6},{8,9},{9,8},{10,11... | collective-permute-start | bytes 1769480 | tf_op jit(solution)/shard_map/ppermute | solution.py:26
  (10 other events, 10.8 us)

commit v16 on v14

--- a/solution.py
+++ b/solution.py
@@ -133,6 +133,7 @@
     head_all = jnp.exp(cum_all)
     earlier = n_blocks - 1
     xw_all = (x_all[:earlier] * tail_all[:earlier, :, :, None]).astype(half)
+    xw_all = lax.optimization_barrier(xw_all)
     state_local_all = jnp.einsum(
         "bthp,btn->bhpn", xw_all, b_all[:earlier], preferred_element_type=fl
     )

time: 130 us -> 133 us (1.023)
  other arithmetic: 15.5 us -> 19.1 us
    convert_element_type x1 -> x2, other arithmetic: 2.09 us -> 5.67 us  [on_device(): xw_all = (x_all[:earlier] * tail_all[:earlier, :, :, None]).astype(half)]
    unnamed x73 -> x75, local copies, waits for them, and re-layouts: 5.52 us -> 5.51 us
  transfers between devices with their start and end apart: 18 -> 18, of which waited for: 11 -> 11; matrix products, arithmetic and copies ran while one was open for 44% -> 45% of each run, Pallas kernels for 0% -> 0%
where the time goes in v16:
time: 133 us; the launch traced here: 132 us
  starting transfers between devices  35.5 us (27%)
  matrix products  27.2 us (20%)
  local copies, waits for them, and re-layouts  26.8 us (20%)
  waiting for transfers between devices  22 us (17%)
  other arithmetic  19.1 us (14%)
  between operations  1.39 us (1%)
    ppermute x14, starting transfers between devices, exchange(): return lax.ppermute(value, axis, pairs)  24.5 us
    ppermute x14, waiting for transfers between devices, exchange(): return lax.ppermute(value, axis, pairs)  18.5 us
    all_to_all x1, starting transfers between devices, on_device(): lax.all_to_all(outgoing, ('tm', 'series'), split_axis=0, concat_axis=1, t...  7.1 us
    convert_element_type x2, other arithmetic, on_device(): xw_all = (x_all[:earlier] * tail_all[:earlier, :, :, None]).astype(half)  5.67 us
    unnamed x75, local copies, waits for them, and re-layouts  5.51 us
    mul x4, local copies, waits for them, and re-layouts, on_device(): later_weighted = (later * head_all[k][:, :, None]).astype(half)  4.35 us
    dot_general x1, matrix products, on_device(): picked = jnp.dot(onehot, bin_table, precision=lax.Precision.HIGHEST)  4.14 us
    slice x2, local copies, waits for them, and re-layouts, on_device(): x_heads = projected[:, :inner_width].reshape(tok_rows, head_count, head_dim)  3.92 us
  transfers between devices with their start and end apart: 18, of which 11 were waited for; matrix products, arithmetic and copies ran while one was open for 45% of the time, Pallas kernels for 0%

profile of v16, /device:TPU:1, one launch (start us, length us, event | category | flops | bytes accessed | tf_op | source)
XLA Modules:
  0.0 132.0 jit_solution(961180472103760709)
XLA Ops:
  2.0 1.2 gather_fusion
  4.0 7.1 %all-to-all-start = ((f32[32,1,16]{2,1,0:T(1,128)}), f32[32,1,16]{2,1,0:T(1,128)S(1)}, u32[]{:S(2)}, u32[]{:S(2)}) async-start(f32[32,1,16]{2,1,0:T(1,128)} %bitcast.1), calls=%async_computation | async-start | bytes 32768 | tf_op jit(solution)/shard_map/all_to_all | solution.py:92
  11.7 1.3 copy.91
  13.0 1.0 convert_bitcast_fusion
  14.3 3.5 %all-to-all-done = f32[32,1,16]{2,1,0:T(1,128)S(1)} async-done(((f32[32,1,16]{2,1,0:T(1,128)}), f32[32,1,16]{2,1,0:T(1,128)S(1)}, u32[]{:S(2)}, u32[]{:S(2)}) %all-to-all-start) | async-done | bytes 2080 | tf_op jit(solution)/shard_map/all_to_all | solution.py:92
  19.1 1.3 collective-permute-start
  20.4 1.3 collective-permute-start.1
  21.7 1.3 collective-permute-start.2
  23.0 1.4 %convert_reduce_fusion = f32[4096]{0:T(1024)S(1)} fusion(f32[4096]{0:T(1024)S(1)} %get-tuple-element.43, f32[4096]{0:T(1024)S(1)} %convert_element_type.117, f32[512]{0:T(512)S(1)} %squeeze.74), kind=kLoop, calls=%fused_computation.1 | loop fusion | flops 10481664 | bytes 51200 | tf_op jit(solution)/shard_map/reduce_sum | solution.py:99
  25.1 4.1 %fusion = f32[512,4]{0,1:T(4,128)S(1)} fusion(f32[4096]{0:T(1024)S(1)} %get-tuple-element.43, f32[4096]{0:T(1024)S(1)} %convert_element_type.117, f32[512]{0:T(512)S(1)} %squeeze.74, f32[4096,1]{0,1:T(1,128)S(1)} %bitcast.233, f32[4096,1]{0,1:T(1,128)S(1)} %bitcast.226, f32[4096,1]{0,1:T(1,128)S(1)} %bitcast.225, f32[4096,1]{0,1:T(1,128)S(1)} %sub.64), kind=kOutput, calls=%fused_computation.3 | convolution fusion | flops 107003904 | bytes 108544 | tf_op jit(solution)/shard_map/dot_general | solution.py:102
  29.3 1.1 compare_select_fusion
  32.4 1.6 %convolution_convert_fusion = bf16[512,2304]{1,0:T(8,128)(2,1)S(1)} fusion(bf16[128,2304]{1,0:T(8,128)(2,1)S(1)} %copy-done, f32[128]{0:T(128)S(1)} %add_multiply_fusion.1, f32[512]{0:T(512)S(1)} %add_multiply_fusion), kind=kOutput, calls=%fused_computation.4 | convolution fusion | flops 303300608 | bytes 2951680 | tf_op jit(solution)/shard_map/dot_general | solution.py:123
  34.0 1.0 compare_select_fusion.1
  35.1 1.4 %convolution_convert_fusion.1 = bf16[128,2304]{1,0:T(8,128)(2,1)} fusion(bf16[128,2304]{1,0:T(8,128)(2,1)S(1)} %copy-done, f32[128]{0:T(128)S(1)} %add_multiply_fusion.1, f32[1,128]{1,0:T(1,128)S(1)} %constant_dynamic-slice_fusion.7), kind=kOutput, calls=%fused_computation.8 | convolution fusion | flops 75825152 | bytes 1180672 | tf_op jit(solution)/shard_map/dot_general | solution.py:113
  37.3 1.0 reduce_window_sum.46
  39.6 1.5 %fusion.74 = f32[128,128]{0,1:T(8,128)} fusion(bf16[128,2304]{1,0:T(8,128)(2,1)} %convolution_convert_fusion.1), kind=kOutput, calls=%fused_computation.137 | convolution fusion | flops 4194304 | bytes 131072 | tf_op jit(solution)/shard_map/dot_general | solution.py:173
  41.1 1.9 %slice.134 = bf16[128,2048]{1,0:T(8,128)(2,1)} slice(bf16[128,2304]{1,0:T(8,128)(2,1)} %convolution_convert_fusion.1), slice={[0:128], [0:2048]} | slice | bytes 1048576 | tf_op jit(solution)/shard_map/slice | solution.py:114
  43.7 2.0 %copy.92 = bf16[128,2048]{0,1:T(8,128)(2,1)} copy(bf16[128,2048]{1,0:T(8,128)(2,1)} %slice.134) | data formatting | bytes 1048576 | tf_op jit(solution)/shard_map/slice | solution.py:114
  45.7 2.8 %fusion.4 = bf16[128,128]{0,1:T(8,128)(2,1)S(1)} fusion(bf16[128,32,64]{0,2,1:T(8,128)(2,1)} %bitcast.214, bf16[128,32,64]{0,2,1:T(8,128)(2,1)S(1)} %bitcast.204, f32[32,128]{1,0:T(8,128)} %get-tuple-element.52, f32[32,128]{1,0:T(8,128)} %copy.95, pred[128,128]{0,1:T(8,128)(4,1)} %iota_compare_fusion), kind=kOutput, calls=%fused_computation.11 | convolution fusion | flops 70238208 | bytes 1130496 | tf_op jit(solution)/shard_map/thp,shp->hts/dot_general | solution.py:190
  48.5 1.6 %fusion.76 = f32[128,128]{0,1:T(8,128)} fusion(bf16[128,2304]{1,0:T(8,128)(2,1)} %convolution_convert_fusion.1, bf16[128,128]{0,1:T(8,128)(2,1)S(1)} %fusion.4), kind=kOutput, calls=%fused_computation.139 | convolution fusion | flops 4194304 | bytes 131072 | tf_op jit(solution)/shard_map/dot_general | solution.py:192
  50.1 1.6 %fusion.71 = f32[128,128]{0,1:T(8,128)} fusion(bf16[128,2304]{1,0:T(8,128)(2,1)} %convolution_convert_fusion.1, bf16[128,128]{0,1:T(8,128)(2,1)S(1)} %fusion.4), kind=kOutput, calls=%fused_computation.134 | convolution fusion | flops 4194304 | bytes 131072 | tf_op jit(solution)/shard_map/dot_general | solution.py:194
  53.0 1.5 %copy.105 = f32[128,32]{0,1:T(8,128)} copy(f32[128,32]{1,0:T(8,128)} %get-tuple-element.32) | data formatting | bytes 32768 | tf_op jit(solution)/shard_map/mul | solution.py:162
  54.5 1.5 %copy.106 = f32[128,32]{0,1:T(8,128)} copy(f32[128,32]{1,0:T(8,128)} %get-tuple-element.31) | data formatting | bytes 32768 | tf_op jit(solution)/shard_map/mul | solution.py:162
  57.3 1.7 %slice_multiply_fusion = f32[3,128,32]{2,1,0:T(8,128)} fusion(f32[4,128,32]{2,1,0:T(8,128)} %bitcast.211, f32[4,128,32]{2,1,0:T(8,128)} %copy-done.2, f32[3,32]{1,0:T(4,128)S(1)} %bitcast.232), kind=kLoop, calls=%fused_computation.86 | loop fusion | flops 24576 | bytes 147840 | tf_op jit(solution)/shard_map/mul | solution.py:132
  59.0 1.6 %copy.101 = f32[3,128,32]{1,2,0:T(8,128)} copy(f32[3,128,32]{2,1,0:T(8,128)} %slice_multiply_fusion) | data formatting | bytes 98304 | tf_op jit(solution)/shard_map/slice | solution.py:135
  60.6 2.1 %slice_convert_fusion = f32[3,128,2048]{2,1,0:T(8,128)} fusion(bf16[4,128,2304]{2,1,0:T(8,128)(2,1)S(1)} %bitcast.199), kind=kLoop, calls=%fused_computation.14 | loop fusion | flops 786432 | bytes 4718592 | tf_op jit(solution)/shard_map/convert_element_type | solution.py:135
  62.7 3.5 %copy.99 = f32[3,128,2048]{1,2,0:T(8,128)} copy(f32[3,128,2048]{2,1,0:T(8,128)} %slice_convert_fusion) | data formatting | bytes 6291456 | tf_op jit(solution)/shard_map/convert_element_type | solution.py:135
  66.3 3.6 %multiply_convert_fusion = bf16[3,128,32,64]{1,3,2,0:T(8,128)(2,1)} fusion(f32[3,128,32,64]{1,3,2,0:T(8,128)} %bitcast.198, f32[3,128,32]{1,2,0:T(8,128)} %copy.101), kind=kLoop, calls=%fused_computation.9 | loop fusion | flops 1572864 | bytes 4767744 | tf_op jit(solution)/shard_map/convert_element_type | solution.py:135
  71.7 2.0 %fusion.51 = f32[3,32,64,128]{3,2,1,0:T(8,128)S(1)} fusion(bf16[3,128,32,64]{1,3,2,0:T(8,128)(2,1)} %multiply_convert_fusion, bf16[4,128,2304]{2,1,0:T(8,128)(2,1)S(1)} %bitcast.200), kind=kOutput, calls=%fused_computation.102 | convolution fusion | flops 201326592 | bytes 4816896 | tf_op jit(solution)/shard_map/bthp,btn->bhpn/dot_general | solution.py:137
  75.4 1.3 convolution_bitcast_fusion
  76.8 2.2 %fusion.20 = (bf16[128,2048]{0,1:T(8,128)(2,1)S(1)}, bf16[128,2048]{0,1:T(8,128)(2,1)S(1)}, bf16[128,2048]{0,1:T(8,128)(2,1)S(1)}) fusion(f32[128,2048]{0,1:T(8,128)} %collective-permute-done.2, f32[128,2048]{0,1:T(8,128)} %collective-permute-done.1, f32[128,32]{0,1:T(8,128)S(1)} %copy-done.9, pred[]{:T(512)S(6)} %eq.19, f32[128,32]{0,1:T(8,128)S(1)} %copy-done.8, ...), kind=kLoop, calls=%fused_computation.50 | loop fusion | flops 2359296 | bytes 4767746 | tf_op jit(solution)/shard_map/convert_element_type | solution.py:162
  79.9 1.1 fusion.12
  82.7 1.6 %collective-permute-done.3 = f32[1152,128]{1,0:T(8,128)S(1)} collective-permute-done((f32[1152,128]{1,0:T(8,128)S(1)}, f32[1152,128]{1,0:T(8,128)S(1)}, u32[]{:S(2)}, u32[]{:S(2)}) %collective-permute-start.3) | collective-permute-done | bytes 589856 | tf_op jit(solution)/shard_map/ppermute | solution.py:26
  84.4 3.4 %collective-permute-start.4 = (f32[288,128]{1,0:T(8,128)S(1)}, f32[288,128]{1,0:T(8,128)S(1)}, u32[]{:S(2)}, u32[]{:S(2)}) collective-permute-start(f32[288,128]{1,0:T(8,128)S(1)} %get-tuple-element.27), channel_id=1, source_target_pairs={{0,8},{8,0},{16,24},{24,16},{1,9},{9,1},{17,25},{25,17},{2,10},{10... | collective-permute-start | bytes 442376 | tf_op jit(solution)/shard_map/ppermute | solution.py:26
  87.8 4.4 %collective-permute-start.5 = (f32[288,128]{1,0:T(8,128)S(1)}, f32[288,128]{1,0:T(8,128)S(1)}, u32[]{:S(2)}, u32[]{:S(2)}) collective-permute-start(f32[288,128]{1,0:T(8,128)S(1)} %get-tuple-element.29), channel_id=1, source_target_pairs={{0,16},{8,24},{16,0},{24,8},{1,17},{9,25},{17,1},{25,9},{2,18},{10... | collective-permute-start | bytes 442376 | tf_op jit(solution)/shard_map/ppermute | solution.py:26
  92.2 5.8 %collective-permute-done.5 = f32[288,128]{1,0:T(8,128)S(1)} collective-permute-done((f32[288,128]{1,0:T(8,128)S(1)}, f32[288,128]{1,0:T(8,128)S(1)}, u32[]{:S(2)}, u32[]{:S(2)}) %collective-permute-start.5) | collective-permute-done | bytes 147488 | tf_op jit(solution)/shard_map/ppermute | solution.py:26
  99.6 3.0 %collective-permute-start.9 = (f32[72,128]{1,0:T(8,128)S(1)}, f32[72,128]{1,0:T(8,128)S(1)}, u32[]{:S(2)}, u32[]{:S(2)}) collective-permute-start(f32[72,128]{1,0:T(8,128)S(1)} %get-tuple-element.40), channel_id=1, source_target_pairs={{0,6},{1,7},{2,4},{3,5},{4,2},{5,3},{6,0},{7,1},{8,14},{9,15},{10,... | collective-permute-start | bytes 110600 | tf_op jit(solution)/shard_map/ppermute | solution.py:26
  103.0 1.3 %collective-permute-done.9 = f32[72,128]{1,0:T(8,128)S(1)} collective-permute-done((f32[72,128]{1,0:T(8,128)S(1)}, f32[72,128]{1,0:T(8,128)S(1)}, u32[]{:S(2)}, u32[]{:S(2)}) %collective-permute-start.9) | collective-permute-done | bytes 36896 | tf_op jit(solution)/shard_map/ppermute | solution.py:26
  104.4 3.1 %collective-permute-start.11 = (f32[72,128]{1,0:T(8,128)S(1)}, f32[72,128]{1,0:T(8,128)S(1)}, u32[]{:S(2)}, u32[]{:S(2)}) collective-permute-start(f32[72,128]{1,0:T(8,128)S(1)} %add_add_fusion.1), channel_id=1, source_target_pairs={{0,4},{1,5},{2,6},{3,7},{4,0},{5,1},{6,2},{7,3},{8,12},{9,13},{10,... | collective-permute-start | bytes 110600 | tf_op jit(solution)/shard_map/ppermute | solution.py:26
  108.9 3.3 %collective-permute-done.12 = f32[72,128]{1,0:T(8,128)S(1)} collective-permute-done((f32[72,128]{1,0:T(8,128)S(1)}, f32[72,128]{1,0:T(8,128)S(1)}, u32[]{:S(2)}, u32[]{:S(2)}) %collective-permute-start.12) | collective-permute-done | bytes 36896 | tf_op jit(solution)/shard_map/ppermute | solution.py:26
  112.3 1.3 collective-permute-start.13
  115.0 1.4 %collective-permute-done.13 = f32[288,128]{1,0:T(8,128)S(1)} collective-permute-done((f32[288,128]{1,0:T(8,128)S(1)}, f32[288,128]{1,0:T(8,128)S(1)}, u32[]{:S(2)}, u32[]{:S(2)}) %collective-permute-start.13) | collective-permute-done | bytes 147488 | tf_op jit(solution)/shard_map/ppermute | solution.py:26
  116.5 1.2 collective-permute-done.14
  117.6 1.6 %collective-permute-done.15 = f32[288,128]{1,0:T(8,128)S(1)} collective-permute-done((f32[288,128]{1,0:T(8,128)S(1)}, f32[288,128]{1,0:T(8,128)S(1)}, u32[]{:S(2)}, u32[]{:S(2)}) %collective-permute-start.15) | collective-permute-done | bytes 147488 | tf_op jit(solution)/shard_map/ppermute | solution.py:26
  119.4 6.1 %collective-permute-start.16 = (f32[1152,128]{1,0:T(8,128)S(1)}, f32[1152,128]{1,0:T(8,128)S(1)}, u32[]{:S(2)}, u32[]{:S(2)}) collective-permute-start(f32[1152,128]{1,0:T(8,128)S(1)} %get-tuple-element.21), channel_id=1, source_target_pairs={{0,1},{1,0},{2,3},{3,2},{4,5},{5,4},{6,7},{7,6},{8,9},{9,8},{10,11... | collective-permute-start | bytes 1769480 | tf_op jit(solution)/shard_map/ppermute | solution.py:26
  125.6 1.3 convolution_bitcast_fusion.1
  126.9 2.4 %fusion.10 = bf16[128,32,64]{0,2,1:T(8,128)(2,1)S(1)} fusion(f32[128,32,64]{0,2,1:T(8,128)S(1)} %convolution_bitcast_fusion.1, f32[3,32,64,128]{3,2,1,0:T(8,128)} %copy-done.1, f32[128,32]{0,1:T(8,128)S(1)} %copy.102, f32[32]{0:T(128)S(1)} %copy-done.31, f32[32]{0:T(128)S(1)} %copy-done.29, f32[32]{0:T(128)S(1)} %copy-done.27, pred[]{:T(512)S(6)} %gt.24, ...), kind=kOutput, calls=%fused_computation.33 | convolution fusion | flops 70254592 | bytes 4768131 | tf_op jit(solution)/shard_map/tn,hpn->thp/dot_general | solution.py:180
  130.6 1.4 %copy.110 = f32[128,2304]{1,0:T(8,128)} copy(f32[128,2304]{0,1:T(8,128)S(1)} %fusion.13) | data formatting | bytes 2359296
  (151 shorter events, 24.6 us)
Async XLA Ops:
  0.6 31.7 %copy-start = (bf16[128,2304]{1,0:T(8,128)(2,1)S(1)}, bf16[128,2304]{1,0:T(8,128)(2,1)}, u32[]{:S(2)}) copy-start(bf16[128,2304]{1,0:T(8,128)(2,1)} %param.11) | copy-start | bytes 1769476
  0.6 13.4 %copy-start.16 = (s32[4096]{0:T(1024)S(1)}, s32[4096]{0:T(1024)}, u32[]{:S(2)}) copy-start(s32[4096]{0:T(1024)} %param.10) | copy-start | bytes 49156
  4.0 13.8 %all-to-all-start = ((f32[32,1,16]{2,1,0:T(1,128)}), f32[32,1,16]{2,1,0:T(1,128)S(1)}, u32[]{:S(2)}, u32[]{:S(2)}) async-start(f32[32,1,16]{2,1,0:T(1,128)} %bitcast.1), calls=%async_computation | async-start | bytes 32768 | tf_op jit(solution)/shard_map/all_to_all | solution.py:92
  14.2 20.8 %copy-start.21 = (f32[128]{0:T(128)}, f32[128]{0:T(128)S(1)}, u32[]{:S(2)}) copy-start(f32[128]{0:T(128)S(1)} %add_multiply_fusion.1) | copy-start | bytes 1540
  19.1 57.6 %collective-permute-start = (f32[128,2048]{0,1:T(8,128)}, f32[128,2048]{0,1:T(8,128)}, u32[]{:S(2)}, u32[]{:S(2)}) collective-permute-start(f32[128,2048]{0,1:T(8,128)} %convert_bitcast_fusion), channel_id=1, source_target_pairs={{24,16},{8,0},{25,17},{9,1},{26,18},{10,2},{27,19},{11,3},{28,20},... | collective-permute-start | bytes 3145736 | tf_op jit(solution)/shard_map/ppermute | solution.py:151
  20.4 56.4 %collective-permute-start.1 = (f32[128,2048]{0,1:T(8,128)}, f32[128,2048]{0,1:T(8,128)}, u32[]{:S(2)}, u32[]{:S(2)}) collective-permute-start(f32[128,2048]{0,1:T(8,128)} %convert_bitcast_fusion), channel_id=1, source_target_pairs={{24,8},{16,0},{25,9},{17,1},{26,10},{18,2},{27,11},{19,3},{28,12},... | collective-permute-start | bytes 3145736 | tf_op jit(solution)/shard_map/ppermute | solution.py:152
  21.7 55.1 %collective-permute-start.2 = (f32[128,2048]{0,1:T(8,128)}, f32[128,2048]{0,1:T(8,128)}, u32[]{:S(2)}, u32[]{:S(2)}) collective-permute-start(f32[128,2048]{0,1:T(8,128)} %convert_bitcast_fusion), channel_id=1, source_target_pairs={{16,8},{24,0},{17,9},{25,1},{18,10},{26,2},{19,11},{27,3},{20,12},... | collective-permute-start | bytes 3145736 | tf_op jit(solution)/shard_map/ppermute | solution.py:153
  25.1 4.2 %copy-start.32 = (bf16[128,32]{0,1:T(8,128)(2,1)S(1)}, bf16[128,32]{0,1:T(8,128)(2,1)}, u32[]{:S(2)}) copy-start(bf16[128,32]{0,1:T(8,128)(2,1)} %param.12) | copy-start | bytes 24580
  25.1 4.2 %copy-start.33 = (f32[32]{0:T(128)S(1)}, f32[32]{0:T(128)}, u32[]{:S(2)}) copy-start(f32[32]{0:T(128)} %param.13) | copy-start | bytes 388
  25.1 6.2 %copy-start.23 = (f32[32]{0:T(128)S(1)}, f32[32]{0:T(128)}, u32[]{:S(2)}) copy-start(f32[32]{0:T(128)} %param.14) | copy-start | bytes 388
  34.0 2.5 %copy-start.24 = (f32[1,128]{1,0:T(1,128)}, f32[1,128]{1,0:T(1,128)S(1)}, u32[]{:S(2)}) copy-start(f32[1,128]{1,0:T(1,128)S(1)} %constant_dynamic-slice_fusion.7) | copy-start | bytes 1540
  35.1 1.4 %copy-start.11 = (f32[128,32]{0,1:T(8,128)}, f32[128,32]{0,1:T(8,128)S(1)}, u32[]{:S(2)}) copy-start(f32[128,32]{0,1:T(8,128)S(1)} %get-tuple-element.53) | copy-start | bytes 49156
  45.7 6.6 %copy-start.4 = (f32[4,128,32]{2,1,0:T(8,128)S(1)}, f32[4,128,32]{2,1,0:T(8,128)}, u32[]{:S(2)}) copy-start(f32[4,128,32]{2,1,0:T(8,128)} %exp.40) | copy-start | bytes 196612
  66.3 3.6 %copy-start.7 = (f32[128,32]{1,0:T(8,128)S(1)}, f32[128,32]{1,0:T(8,128)}, u32[]{:S(2)}) copy-start(f32[128,32]{1,0:T(8,128)} %exp.39) | copy-start | bytes 49156
  71.7 2.0 %copy-start.30 = (f32[32]{0:T(128)}, f32[32]{0:T(128)S(1)}, u32[]{:S(2)}) copy-start(f32[32]{0:T(128)S(1)} %get-tuple-element.49) | copy-start | bytes 388
  71.7 7.6 %copy-start.26 = (f32[32]{0:T(128)}, f32[32]{0:T(128)S(1)}, u32[]{:S(2)}) copy-start(f32[32]{0:T(128)S(1)} %get-tuple-element.51) | copy-start | bytes 388
  71.7 7.9 %copy-start.28 = (f32[32]{0:T(128)}, f32[32]{0:T(128)S(1)}, u32[]{:S(2)}) copy-start(f32[32]{0:T(128)S(1)} %get-tuple-element.50) | copy-start | bytes 388
  71.7 2.0 %copy-start.15 = (f32[128,128]{0,1:T(8,128)S(1)}, f32[128,128]{0,1:T(8,128)}, u32[]{:S(2)}) copy-start(f32[128,128]{0,1:T(8,128)} %fusion.71) | copy-start | bytes 196612
  73.7 1.6 %copy-start.1 = (f32[3,32,64,128]{3,2,1,0:T(8,128)}, f32[3,32,64,128]{3,2,1,0:T(8,128)S(1)}, u32[]{:S(2)}) copy-start(f32[3,32,64,128]{3,2,1,0:T(8,128)S(1)} %fusion.51) | copy-start | bytes 9437188
  73.7 1.6 %copy-start.12 = (f32[128,128]{0,1:T(8,128)S(1)}, f32[128,128]{0,1:T(8,128)}, u32[]{:S(2)}) copy-start(f32[128,128]{0,1:T(8,128)} %fusion.74) | copy-start | bytes 196612
  73.7 1.6 %copy-start.17 = (f32[32,128]{1,0:T(8,128)S(1)}, f32[32,128]{1,0:T(8,128)}, u32[]{:S(2)}) copy-start(f32[32,128]{1,0:T(8,128)} %copy.95) | copy-start | bytes 49156
  73.8 1.6 %copy-start.19 = (pred[128,128]{0,1:T(8,128)(4,1)S(1)}, pred[128,128]{0,1:T(8,128)(4,1)}, u32[]{:S(2)}) copy-start(pred[128,128]{0,1:T(8,128)(4,1)} %iota_compare_fusion) | copy-start | bytes 49156
  73.8 1.6 %copy-start.34 = (f32[32,128]{1,0:T(8,128)S(1)}, f32[32,128]{1,0:T(8,128)}, u32[]{:S(2)}) copy-start(f32[32,128]{1,0:T(8,128)} %get-tuple-element.52) | copy-start | bytes 49156
  75.4 1.4 %copy-start.8 = (f32[128,32]{0,1:T(8,128)S(1)}, f32[128,32]{0,1:T(8,128)}, u32[]{:S(2)}) copy-start(f32[128,32]{0,1:T(8,128)} %copy.105) | copy-start | bytes 49156
  75.4 1.4 %copy-start.9 = (f32[128,32]{0,1:T(8,128)S(1)}, f32[128,32]{0,1:T(8,128)}, u32[]{:S(2)}) copy-start(f32[128,32]{0,1:T(8,128)} %copy.106) | copy-start | bytes 49156
  79.6 1.4 %copy-start.5 = (bf16[128,2048]{0,1:T(8,128)(2,1)S(1)}, bf16[128,2048]{0,1:T(8,128)(2,1)}, u32[]{:S(2)}) copy-start(bf16[128,2048]{0,1:T(8,128)(2,1)} %copy.92) | copy-start | bytes 1572868
  79.6 1.4 %copy-start.14 = (f32[128,128]{0,1:T(8,128)S(1)}, f32[128,128]{0,1:T(8,128)}, u32[]{:S(2)}) copy-start(f32[128,128]{0,1:T(8,128)} %fusion.76) | copy-start | bytes 196612
  79.9 1.5 %copy-start.22 = (f32[128]{0:T(128)S(1)}, f32[128]{0:T(128)}, u32[]{:S(2)}) copy-start(f32[128]{0:T(128)} %copy-done.21) | copy-start | bytes 1540
  79.9 1.5 %copy-start.25 = (f32[1,128]{1,0:T(1,128)S(1)}, f32[1,128]{1,0:T(1,128)}, u32[]{:S(2)}) copy-start(f32[1,128]{1,0:T(1,128)} %copy-done.24) | copy-start | bytes 1540
  82.0 2.3 %collective-permute-start.3 = (f32[1152,128]{1,0:T(8,128)S(1)}, f32[1152,128]{1,0:T(8,128)S(1)}, u32[]{:S(2)}, u32[]{:S(2)}) collective-permute-start(f32[1152,128]{1,0:T(8,128)S(1)} %constant_dynamic-slice_fusion.6), channel_id=1, source_target_pairs={{0,1},{1,0},{2,3},{3,2},{4,5},{5,4},{6,7},{7,6},{8,9},{9,8},{10,11... | collective-permute-start | bytes 1769480 | tf_op jit(solution)/shard_map/ppermute | solution.py:26
  84.4 7.8 %collective-permute-start.4 = (f32[288,128]{1,0:T(8,128)S(1)}, f32[288,128]{1,0:T(8,128)S(1)}, u32[]{:S(2)}, u32[]{:S(2)}) collective-permute-start(f32[288,128]{1,0:T(8,128)S(1)} %get-tuple-element.27), channel_id=1, source_target_pairs={{0,8},{8,0},{16,24},{24,16},{1,9},{9,1},{17,25},{25,17},{2,10},{10... | collective-permute-start | bytes 442376 | tf_op jit(solution)/shard_map/ppermute | solution.py:26
  87.8 10.2 %collective-permute-start.5 = (f32[288,128]{1,0:T(8,128)S(1)}, f32[288,128]{1,0:T(8,128)S(1)}, u32[]{:S(2)}, u32[]{:S(2)}) collective-permute-start(f32[288,128]{1,0:T(8,128)S(1)} %get-tuple-element.29), channel_id=1, source_target_pairs={{0,16},{8,24},{16,0},{24,8},{1,17},{9,25},{17,1},{25,9},{2,18},{10... | collective-permute-start | bytes 442376 | tf_op jit(solution)/shard_map/ppermute | solution.py:26
  92.2 6.7 %collective-permute-start.6 = (f32[288,128]{1,0:T(8,128)S(1)}, f32[288,128]{1,0:T(8,128)S(1)}, u32[]{:S(2)}, u32[]{:S(2)}) collective-permute-start(f32[288,128]{1,0:T(8,128)S(1)} %get-tuple-element.28), channel_id=1, source_target_pairs={{0,24},{8,16},{16,8},{24,0},{1,25},{9,17},{17,9},{25,1},{2,26},{10... | collective-permute-start | bytes 442376 | tf_op jit(solution)/shard_map/ppermute | solution.py:26
  98.9 3.6 %collective-permute-start.7 = (f32[72,128]{1,0:T(8,128)S(1)}, f32[72,128]{1,0:T(8,128)S(1)}, u32[]{:S(2)}, u32[]{:S(2)}) collective-permute-start(f32[72,128]{1,0:T(8,128)S(1)} %get-tuple-element.39), channel_id=1, source_target_pairs={{0,2},{1,3},{2,0},{3,1},{4,6},{5,7},{6,4},{7,5},{8,10},{9,11},{10,... | collective-permute-start | bytes 110600 | tf_op jit(solution)/shard_map/ppermute | solution.py:26
  99.3 3.7 %collective-permute-start.8 = (f32[72,128]{1,0:T(8,128)S(1)}, f32[72,128]{1,0:T(8,128)S(1)}, u32[]{:S(2)}, u32[]{:S(2)}) collective-permute-start(f32[72,128]{1,0:T(8,128)S(1)} %get-tuple-element.41), channel_id=1, source_target_pairs={{0,4},{1,5},{2,6},{3,7},{4,0},{5,1},{6,2},{7,3},{8,12},{9,13},{10,... | collective-permute-start | bytes 110600 | tf_op jit(solution)/shard_map/ppermute | solution.py:26
  99.6 4.7 %collective-permute-start.9 = (f32[72,128]{1,0:T(8,128)S(1)}, f32[72,128]{1,0:T(8,128)S(1)}, u32[]{:S(2)}, u32[]{:S(2)}) collective-permute-start(f32[72,128]{1,0:T(8,128)S(1)} %get-tuple-element.40), channel_id=1, source_target_pairs={{0,6},{1,7},{2,4},{3,5},{4,2},{5,3},{6,0},{7,1},{8,14},{9,15},{10,... | collective-permute-start | bytes 110600 | tf_op jit(solution)/shard_map/ppermute | solution.py:26
  104.3 3.6 %collective-permute-start.10 = (f32[72,128]{1,0:T(8,128)S(1)}, f32[72,128]{1,0:T(8,128)S(1)}, u32[]{:S(2)}, u32[]{:S(2)}) collective-permute-start(f32[72,128]{1,0:T(8,128)S(1)} %add_add_fusion.1), channel_id=1, source_target_pairs={{0,2},{1,3},{2,0},{3,1},{4,6},{5,7},{6,4},{7,5},{8,10},{9,11},{10,... | collective-permute-start | bytes 110600 | tf_op jit(solution)/shard_map/ppermute | solution.py:26
  104.4 4.5 %collective-permute-start.11 = (f32[72,128]{1,0:T(8,128)S(1)}, f32[72,128]{1,0:T(8,128)S(1)}, u32[]{:S(2)}, u32[]{:S(2)}) collective-permute-start(f32[72,128]{1,0:T(8,128)S(1)} %add_add_fusion.1), channel_id=1, source_target_pairs={{0,4},{1,5},{2,6},{3,7},{4,0},{5,1},{6,2},{7,3},{8,12},{9,13},{10,... | collective-permute-start | bytes 110600 | tf_op jit(solution)/shard_map/ppermute | solution.py:26
  107.5 4.7 %collective-permute-start.12 = (f32[72,128]{1,0:T(8,128)S(1)}, f32[72,128]{1,0:T(8,128)S(1)}, u32[]{:S(2)}, u32[]{:S(2)}) collective-permute-start(f32[72,128]{1,0:T(8,128)S(1)} %add_add_fusion.1), channel_id=1, source_target_pairs={{0,6},{1,7},{2,4},{3,5},{4,2},{5,3},{6,0},{7,1},{8,14},{9,15},{10,... | collective-permute-start | bytes 110600 | tf_op jit(solution)/shard_map/ppermute | solution.py:26
  112.3 13.2 %copy-start.6 = (bf16[128,2048]{0,1:T(8,128)(2,1)S(1)}, bf16[128,2048]{0,1:T(8,128)(2,1)}, u32[]{:S(2)}) copy-start(bf16[128,2048]{0,1:T(8,128)(2,1)} %copy.92) | copy-start | bytes 1572868
  112.3 13.2 %copy-start.13 = (f32[128,128]{0,1:T(8,128)S(1)}, f32[128,128]{0,1:T(8,128)}, u32[]{:S(2)}) copy-start(f32[128,128]{0,1:T(8,128)} %fusion.74) | copy-start | bytes 196612
  112.3 13.2 %copy-start.18 = (f32[32,128]{1,0:T(8,128)S(1)}, f32[32,128]{1,0:T(8,128)}, u32[]{:S(2)}) copy-start(f32[32,128]{1,0:T(8,128)} %copy.95) | copy-start | bytes 49156
  112.3 13.2 %copy-start.20 = (pred[128,128]{0,1:T(8,128)(4,1)S(1)}, pred[128,128]{0,1:T(8,128)(4,1)}, u32[]{:S(2)}) copy-start(pred[128,128]{0,1:T(8,128)(4,1)} %iota_compare_fusion) | copy-start | bytes 49156
  112.3 13.2 %copy-start.35 = (f32[32,128]{1,0:T(8,128)S(1)}, f32[32,128]{1,0:T(8,128)}, u32[]{:S(2)}) copy-start(f32[32,128]{1,0:T(8,128)} %get-tuple-element.52) | copy-start | bytes 49156
  112.3 4.1 %collective-permute-start.13 = (f32[288,128]{1,0:T(8,128)S(1)}, f32[288,128]{1,0:T(8,128)S(1)}, u32[]{:S(2)}, u32[]{:S(2)}) collective-permute-start(f32[288,128]{1,0:T(8,128)S(1)} %get-tuple-element.34), channel_id=1, source_target_pairs={{0,8},{8,0},{16,24},{24,16},{1,9},{9,1},{17,25},{25,17},{2,10},{10... | collective-permute-start | bytes 442376 | tf_op jit(solution)/shard_map/ppermute | solution.py:26
  113.6 4.0 %collective-permute-start.14 = (f32[288,128]{1,0:T(8,128)S(1)}, f32[288,128]{1,0:T(8,128)S(1)}, u32[]{:S(2)}, u32[]{:S(2)}) collective-permute-start(f32[288,128]{1,0:T(8,128)S(1)} %get-tuple-element.34), channel_id=1, source_target_pairs={{0,16},{8,24},{16,0},{24,8},{1,17},{9,25},{17,1},{25,9},{2,18},{10... | collective-permute-start | bytes 442376 | tf_op jit(solution)/shard_map/ppermute | solution.py:26
  114.1 5.1 %collective-permute-start.15 = (f32[288,128]{1,0:T(8,128)S(1)}, f32[288,128]{1,0:T(8,128)S(1)}, u32[]{:S(2)}, u32[]{:S(2)}) collective-permute-start(f32[288,128]{1,0:T(8,128)S(1)} %get-tuple-element.34), channel_id=1, source_target_pairs={{0,24},{8,16},{16,8},{24,0},{1,25},{9,17},{17,9},{25,1},{2,26},{10... | collective-permute-start | bytes 442376 | tf_op jit(solution)/shard_map/ppermute | solution.py:26
  119.4 10.9 %collective-permute-start.16 = (f32[1152,128]{1,0:T(8,128)S(1)}, f32[1152,128]{1,0:T(8,128)S(1)}, u32[]{:S(2)}, u32[]{:S(2)}) collective-permute-start(f32[1152,128]{1,0:T(8,128)S(1)} %get-tuple-element.21), channel_id=1, source_target_pairs={{0,1},{1,0},{2,3},{3,2},{4,5},{5,4},{6,7},{7,6},{8,9},{9,8},{10,11... | collective-permute-start | bytes 1769480 | tf_op jit(solution)/shard_map/ppermute | solution.py:26
  (6 other events, 6.9 us)

commit v17 on v14

--- a/solution.py
+++ b/solution.py
@@ -29,7 +29,7 @@
 def bit_groups():
     tm_bits, series_bits = axis_bits("tm"), axis_bits("series")
     groups = [("series", series_bits[:1])] if series_bits else []
-    for axis, bits in (("tm", tm_bits), ("series", series_bits[1:])):
+    for axis, bits in (("series", series_bits[1:]), ("tm", tm_bits)):
         groups += [(axis, bits[i : i + 2]) for i in range(0, len(bits), 2)]
     return groups
 

time: 130 us -> 136 us (1.046)
  waiting for transfers between devices: 22 us -> 25 us
  starting transfers between devices: 35.5 us -> 38.4 us
    ppermute x14, waiting for transfers between devices: 18.5 us -> 21.4 us  [exchange(): return lax.ppermute(value, axis, pairs)]
    ppermute x14, starting transfers between devices: 24.5 us -> 27.5 us  [exchange(): return lax.ppermute(value, axis, pairs)]
  transfers between devices with their start and end apart: 18 -> 18, of which waited for: 11 -> 11; matrix products, arithmetic and copies ran while one was open for 44% -> 42% of each run, Pallas kernels for 0% -> 0%
where the time goes in v17:
time: 136 us; the launch traced here: 135 us
  starting transfers between devices  38.4 us (28%)
  matrix products  27.7 us (20%)
  local copies, waits for them, and re-layouts  26.8 us (20%)
  waiting for transfers between devices  25 us (18%)
  other arithmetic  15.5 us (11%)
  between operations  1.36 us (1%)
    ppermute x14, starting transfers between devices, exchange(): return lax.ppermute(value, axis, pairs)  27.5 us
    ppermute x14, waiting for transfers between devices, exchange(): return lax.ppermute(value, axis, pairs)  21.4 us
    all_to_all x1, starting transfers between devices, on_device(): lax.all_to_all(outgoing, ('tm', 'series'), split_axis=0, concat_axis=1, t...  7.1 us
    unnamed x73, local copies, waits for them, and re-layouts  5.52 us
    mul x4, local copies, waits for them, and re-layouts, on_device(): later_weighted = (later * head_all[k][:, :, None]).astype(half)  4.34 us
    dot_general x1, matrix products, on_device(): picked = jnp.dot(onehot, bin_table, precision=lax.Precision.HIGHEST)  4.14 us
    slice x2, local copies, waits for them, and re-layouts, on_device(): x_heads = projected[:, :inner_width].reshape(tok_rows, head_count, head_dim)  3.92 us
    convert_element_type x1, local copies, waits for them, and re-layouts, on_device(): xw_all = (x_all[:earlier] * tail_all[:earlier, :, :, None]).astype(half)  3.56 us
  transfers between devices with their start and end apart: 18, of which 11 were waited for; matrix products, arithmetic and copies ran while one was open for 42% of the time, Pallas kernels for 0%

profile of v17, /device:TPU:1, one launch (start us, length us, event | category | flops | bytes accessed | tf_op | source)
XLA Modules:
  0.0 134.8 jit_solution(17006288896589365984)
XLA Ops:
  2.0 1.2 gather_fusion
  4.0 7.1 %all-to-all-start = ((f32[32,1,16]{2,1,0:T(1,128)}), f32[32,1,16]{2,1,0:T(1,128)S(1)}, u32[]{:S(2)}, u32[]{:S(2)}) async-start(f32[32,1,16]{2,1,0:T(1,128)} %bitcast.1), calls=%async_computation | async-start | bytes 32768 | tf_op jit(solution)/shard_map/all_to_all | solution.py:92
  11.7 1.3 copy.91
  13.0 1.0 convert_bitcast_fusion
  14.2 3.5 %all-to-all-done = f32[32,1,16]{2,1,0:T(1,128)S(1)} async-done(((f32[32,1,16]{2,1,0:T(1,128)}), f32[32,1,16]{2,1,0:T(1,128)S(1)}, u32[]{:S(2)}, u32[]{:S(2)}) %all-to-all-start) | async-done | bytes 2080 | tf_op jit(solution)/shard_map/all_to_all | solution.py:92
  19.1 1.3 collective-permute-start
  20.4 1.3 collective-permute-start.1
  21.7 1.3 collective-permute-start.2
  23.0 1.4 %convert_reduce_fusion = f32[4096]{0:T(1024)S(1)} fusion(f32[4096]{0:T(1024)S(1)} %get-tuple-element.43, f32[4096]{0:T(1024)S(1)} %convert_element_type.117, f32[512]{0:T(512)S(1)} %squeeze.74), kind=kLoop, calls=%fused_computation.1 | loop fusion | flops 10481664 | bytes 51200 | tf_op jit(solution)/shard_map/reduce_sum | solution.py:99
  25.1 4.1 %fusion = f32[512,4]{0,1:T(4,128)S(1)} fusion(f32[4096]{0:T(1024)S(1)} %get-tuple-element.43, f32[4096]{0:T(1024)S(1)} %convert_element_type.117, f32[512]{0:T(512)S(1)} %squeeze.74, f32[4096,1]{0,1:T(1,128)S(1)} %bitcast.232, f32[4096,1]{0,1:T(1,128)S(1)} %bitcast.225, f32[4096,1]{0,1:T(1,128)S(1)} %bitcast.224, f32[4096,1]{0,1:T(1,128)S(1)} %sub.64), kind=kOutput, calls=%fused_computation.3 | convolution fusion | flops 107003904 | bytes 108544 | tf_op jit(solution)/shard_map/dot_general | solution.py:102
  29.3 1.1 compare_select_fusion
  32.4 1.6 %convolution_convert_fusion = bf16[512,2304]{1,0:T(8,128)(2,1)S(1)} fusion(bf16[128,2304]{1,0:T(8,128)(2,1)S(1)} %copy-done, f32[128]{0:T(128)S(1)} %add_multiply_fusion.1, f32[512]{0:T(512)S(1)} %add_multiply_fusion), kind=kOutput, calls=%fused_computation.4 | convolution fusion | flops 303300608 | bytes 2951680 | tf_op jit(solution)/shard_map/dot_general | solution.py:123
  34.0 1.0 compare_select_fusion.1
  35.1 1.4 %convolution_convert_fusion.1 = bf16[128,2304]{1,0:T(8,128)(2,1)} fusion(bf16[128,2304]{1,0:T(8,128)(2,1)S(1)} %copy-done, f32[128]{0:T(128)S(1)} %add_multiply_fusion.1, f32[1,128]{1,0:T(1,128)S(1)} %constant_dynamic-slice_fusion.7), kind=kOutput, calls=%fused_computation.8 | convolution fusion | flops 75825152 | bytes 1180672 | tf_op jit(solution)/shard_map/dot_general | solution.py:113
  37.3 1.0 reduce_window_sum.46
  39.5 1.5 %fusion.75 = f32[128,128]{0,1:T(8,128)} fusion(bf16[128,2304]{1,0:T(8,128)(2,1)} %convolution_convert_fusion.1), kind=kOutput, calls=%fused_computation.138 | convolution fusion | flops 4194304 | bytes 131072 | tf_op jit(solution)/shard_map/dot_general | solution.py:172
  41.1 1.9 %slice.134 = bf16[128,2048]{1,0:T(8,128)(2,1)} slice(bf16[128,2304]{1,0:T(8,128)(2,1)} %convolution_convert_fusion.1), slice={[0:128], [0:2048]} | slice | bytes 1048576 | tf_op jit(solution)/shard_map/slice | solution.py:114
  43.6 2.0 %copy.92 = bf16[128,2048]{0,1:T(8,128)(2,1)} copy(bf16[128,2048]{1,0:T(8,128)(2,1)} %slice.134) | data formatting | bytes 1048576 | tf_op jit(solution)/shard_map/slice | solution.py:114
  45.7 2.8 %fusion.4 = bf16[128,128]{0,1:T(8,128)(2,1)S(1)} fusion(bf16[128,32,64]{0,2,1:T(8,128)(2,1)} %bitcast.213, bf16[128,32,64]{0,2,1:T(8,128)(2,1)S(1)} %bitcast.203, f32[32,128]{1,0:T(8,128)} %get-tuple-element.52, f32[32,128]{1,0:T(8,128)} %copy.95, pred[128,128]{0,1:T(8,128)(4,1)} %iota_compare_fusion), kind=kOutput, calls=%fused_computation.11 | convolution fusion | flops 70238208 | bytes 1130496 | tf_op jit(solution)/shard_map/thp,shp->hts/dot_general | solution.py:189
  48.4 1.6 %fusion.77 = f32[128,128]{0,1:T(8,128)} fusion(bf16[128,2304]{1,0:T(8,128)(2,1)} %convolution_convert_fusion.1, bf16[128,128]{0,1:T(8,128)(2,1)S(1)} %fusion.4), kind=kOutput, calls=%fused_computation.140 | convolution fusion | flops 4194304 | bytes 131072 | tf_op jit(solution)/shard_map/dot_general | solution.py:191
  50.0 1.6 %fusion.72 = f32[128,128]{0,1:T(8,128)} fusion(bf16[128,2304]{1,0:T(8,128)(2,1)} %convolution_convert_fusion.1, bf16[128,128]{0,1:T(8,128)(2,1)S(1)} %fusion.4), kind=kOutput, calls=%fused_computation.135 | convolution fusion | flops 4194304 | bytes 131072 | tf_op jit(solution)/shard_map/dot_general | solution.py:193
  52.9 1.5 %copy.105 = f32[128,32]{0,1:T(8,128)} copy(f32[128,32]{1,0:T(8,128)} %get-tuple-element.32) | data formatting | bytes 32768 | tf_op jit(solution)/shard_map/mul | solution.py:161
  54.4 1.5 %copy.106 = f32[128,32]{0,1:T(8,128)} copy(f32[128,32]{1,0:T(8,128)} %get-tuple-element.31) | data formatting | bytes 32768 | tf_op jit(solution)/shard_map/mul | solution.py:161
  57.2 1.7 %slice_multiply_fusion = f32[3,128,32]{2,1,0:T(8,128)} fusion(f32[4,128,32]{2,1,0:T(8,128)} %bitcast.210, f32[4,128,32]{2,1,0:T(8,128)} %copy-done.2, f32[3,32]{1,0:T(4,128)S(1)} %bitcast.231), kind=kLoop, calls=%fused_computation.88 | loop fusion | flops 24576 | bytes 147840 | tf_op jit(solution)/shard_map/mul | solution.py:132
  58.9 1.7 %copy.101 = f32[3,128,32]{1,2,0:T(8,128)} copy(f32[3,128,32]{2,1,0:T(8,128)} %slice_multiply_fusion) | data formatting | bytes 98304 | tf_op jit(solution)/shard_map/slice | solution.py:135
  60.6 2.1 %slice_convert_fusion = f32[3,128,2048]{2,1,0:T(8,128)} fusion(bf16[4,128,2304]{2,1,0:T(8,128)(2,1)S(1)} %bitcast.198), kind=kLoop, calls=%fused_computation.15 | loop fusion | flops 786432 | bytes 4718592 | tf_op jit(solution)/shard_map/convert_element_type | solution.py:135
  62.7 3.6 %copy.99 = f32[3,128,2048]{1,2,0:T(8,128)} copy(f32[3,128,2048]{2,1,0:T(8,128)} %slice_convert_fusion) | data formatting | bytes 6291456 | tf_op jit(solution)/shard_map/convert_element_type | solution.py:135
  68.1 2.5 %fusion.5 = f32[3,32,64,128]{3,2,1,0:T(8,128)S(1)} fusion(f32[3,128,32,64]{1,3,2,0:T(8,128)} %bitcast.197, f32[3,128,32]{1,2,0:T(8,128)} %copy.101, bf16[4,128,2304]{2,1,0:T(8,128)(2,1)S(1)} %bitcast.199), kind=kOutput, calls=%fused_computation.14 | convolution fusion | flops 202899456 | bytes 6438912 | tf_op jit(solution)/shard_map/bthp,btn->bhpn/dot_general | solution.py:136
  72.3 1.3 convolution_bitcast_fusion
  73.6 2.2 %fusion.22 = (bf16[128,2048]{0,1:T(8,128)(2,1)S(1)}, bf16[128,2048]{0,1:T(8,128)(2,1)S(1)}, bf16[128,2048]{0,1:T(8,128)(2,1)S(1)}) fusion(f32[128,2048]{0,1:T(8,128)} %collective-permute-done.2, f32[128,2048]{0,1:T(8,128)} %collective-permute-done.1, f32[128,32]{0,1:T(8,128)S(1)} %copy-done.9, pred[]{:T(512)S(6)} %eq.19, f32[128,32]{0,1:T(8,128)S(1)} %copy-done.8, ...), kind=kLoop, calls=%fused_computation.52 | loop fusion | flops 2359296 | bytes 4767746 | tf_op jit(solution)/shard_map/convert_element_type | solution.py:161
  76.8 1.1 fusion.14
  79.6 1.6 %collective-permute-done.3 = f32[1152,128]{1,0:T(8,128)S(1)} collective-permute-done((f32[1152,128]{1,0:T(8,128)S(1)}, f32[1152,128]{1,0:T(8,128)S(1)}, u32[]{:S(2)}, u32[]{:S(2)}) %collective-permute-start.3) | collective-permute-done | bytes 589856 | tf_op jit(solution)/shard_map/ppermute | solution.py:26
  82.0 3.0 %collective-permute-start.6 = (f32[288,128]{1,0:T(8,128)S(1)}, f32[288,128]{1,0:T(8,128)S(1)}, u32[]{:S(2)}, u32[]{:S(2)}) collective-permute-start(f32[288,128]{1,0:T(8,128)S(1)} %get-tuple-element.28), channel_id=1, source_target_pairs={{0,6},{1,7},{2,4},{3,5},{4,2},{5,3},{6,0},{7,1},{8,14},{9,15},{10,... | collective-permute-start | bytes 442376 | tf_op jit(solution)/shard_map/ppermute | solution.py:26
  84.9 3.5 %collective-permute-done.4 = f32[288,128]{1,0:T(8,128)S(1)} collective-permute-done((f32[288,128]{1,0:T(8,128)S(1)}, f32[288,128]{1,0:T(8,128)S(1)}, u32[]{:S(2)}, u32[]{:S(2)}) %collective-permute-start.4) | collective-permute-done | bytes 147488 | tf_op jit(solution)/shard_map/ppermute | solution.py:26
  88.5 5.2 %collective-permute-done.5 = f32[288,128]{1,0:T(8,128)S(1)} collective-permute-done((f32[288,128]{1,0:T(8,128)S(1)}, f32[288,128]{1,0:T(8,128)S(1)}, u32[]{:S(2)}, u32[]{:S(2)}) %collective-permute-start.5) | collective-permute-done | bytes 147488 | tf_op jit(solution)/shard_map/ppermute | solution.py:26
  93.8 3.4 %collective-permute-start.7 = (f32[72,128]{1,0:T(8,128)S(1)}, f32[72,128]{1,0:T(8,128)S(1)}, u32[]{:S(2)}, u32[]{:S(2)}) collective-permute-start(f32[72,128]{1,0:T(8,128)S(1)} %get-tuple-element.39), channel_id=1, source_target_pairs={{0,8},{8,0},{16,24},{24,16},{1,9},{9,1},{17,25},{25,17},{2,10},{10... | collective-permute-start | bytes 110600 | tf_op jit(solution)/shard_map/ppermute | solution.py:26
  97.2 4.4 %collective-permute-start.8 = (f32[72,128]{1,0:T(8,128)S(1)}, f32[72,128]{1,0:T(8,128)S(1)}, u32[]{:S(2)}, u32[]{:S(2)}) collective-permute-start(f32[72,128]{1,0:T(8,128)S(1)} %get-tuple-element.41), channel_id=1, source_target_pairs={{0,16},{8,24},{16,0},{24,8},{1,17},{9,25},{17,1},{25,9},{2,18},{10... | collective-permute-start | bytes 110600 | tf_op jit(solution)/shard_map/ppermute | solution.py:26
  101.6 1.3 collective-permute-done.8
  102.9 2.4 %collective-permute-done.9 = f32[72,128]{1,0:T(8,128)S(1)} collective-permute-done((f32[72,128]{1,0:T(8,128)S(1)}, f32[72,128]{1,0:T(8,128)S(1)}, u32[]{:S(2)}, u32[]{:S(2)}) %collective-permute-start.9) | collective-permute-done | bytes 36896 | tf_op jit(solution)/shard_map/ppermute | solution.py:26
  105.6 2.4 %collective-permute-start.12 = (f32[72,128]{1,0:T(8,128)S(1)}, f32[72,128]{1,0:T(8,128)S(1)}, u32[]{:S(2)}, u32[]{:S(2)}) collective-permute-start(f32[72,128]{1,0:T(8,128)S(1)} %add_add_fusion.1), channel_id=1, source_target_pairs={{0,24},{8,16},{16,8},{24,0},{1,25},{9,17},{17,9},{25,1},{2,26},{10... | collective-permute-start | bytes 110600 | tf_op jit(solution)/shard_map/ppermute | solution.py:26
  108.3 1.1 collective-permute-done.12
  109.5 3.5 %collective-permute-start.13 = (f32[288,128]{1,0:T(8,128)S(1)}, f32[288,128]{1,0:T(8,128)S(1)}, u32[]{:S(2)}, u32[]{:S(2)}) collective-permute-start(f32[288,128]{1,0:T(8,128)S(1)} %get-tuple-element.34), channel_id=1, source_target_pairs={{0,2},{1,3},{2,0},{3,1},{4,6},{5,7},{6,4},{7,5},{8,10},{9,11},{10,... | collective-permute-start | bytes 442376 | tf_op jit(solution)/shard_map/ppermute | solution.py:26
  113.0 2.1 %collective-permute-start.15 = (f32[288,128]{1,0:T(8,128)S(1)}, f32[288,128]{1,0:T(8,128)S(1)}, u32[]{:S(2)}, u32[]{:S(2)}) collective-permute-start(f32[288,128]{1,0:T(8,128)S(1)} %get-tuple-element.34), channel_id=1, source_target_pairs={{0,6},{1,7},{2,4},{3,5},{4,2},{5,3},{6,0},{7,1},{8,14},{9,15},{10,... | collective-permute-start | bytes 442376 | tf_op jit(solution)/shard_map/ppermute | solution.py:26
  115.5 5.6 %collective-permute-done.14 = f32[288,128]{1,0:T(8,128)S(1)} collective-permute-done((f32[288,128]{1,0:T(8,128)S(1)}, f32[288,128]{1,0:T(8,128)S(1)}, u32[]{:S(2)}, u32[]{:S(2)}) %collective-permute-start.14) | collective-permute-done | bytes 147488 | tf_op jit(solution)/shard_map/ppermute | solution.py:26
  121.3 7.0 %collective-permute-start.16 = (f32[1152,128]{1,0:T(8,128)S(1)}, f32[1152,128]{1,0:T(8,128)S(1)}, u32[]{:S(2)}, u32[]{:S(2)}) collective-permute-start(f32[1152,128]{1,0:T(8,128)S(1)} %get-tuple-element.21), channel_id=1, source_target_pairs={{0,1},{1,0},{2,3},{3,2},{4,5},{5,4},{6,7},{7,6},{8,9},{9,8},{10,11... | collective-permute-start | bytes 1769480 | tf_op jit(solution)/shard_map/ppermute | solution.py:26
  128.4 1.3 convolution_bitcast_fusion.1
  129.7 2.4 %fusion.12 = bf16[128,32,64]{0,2,1:T(8,128)(2,1)S(1)} fusion(f32[128,32,64]{0,2,1:T(8,128)S(1)} %convolution_bitcast_fusion.1, f32[3,32,64,128]{3,2,1,0:T(8,128)} %copy-done.1, f32[128,32]{0,1:T(8,128)S(1)} %copy.102, f32[32]{0:T(128)S(1)} %copy-done.30, f32[32]{0:T(128)S(1)} %copy-done.28, f32[32]{0:T(128)S(1)} %copy-done.26, pred[]{:T(512)S(6)} %gt.24, ...), kind=kOutput, calls=%fused_computation.35 | convolution fusion | flops 70254592 | bytes 4768131 | tf_op jit(solution)/shard_map/tn,hpn->thp/dot_general | solution.py:179
  133.4 1.4 %copy.110 = f32[128,2304]{1,0:T(8,128)} copy(f32[128,2304]{0,1:T(8,128)S(1)} %fusion.15) | data formatting | bytes 2359296
  (148 shorter events, 21.5 us)
Async XLA Ops:
  0.6 31.7 %copy-start = (bf16[128,2304]{1,0:T(8,128)(2,1)S(1)}, bf16[128,2304]{1,0:T(8,128)(2,1)}, u32[]{:S(2)}) copy-start(bf16[128,2304]{1,0:T(8,128)(2,1)} %param.11) | copy-start | bytes 1769476
  0.6 13.4 %copy-start.16 = (s32[4096]{0:T(1024)S(1)}, s32[4096]{0:T(1024)}, u32[]{:S(2)}) copy-start(s32[4096]{0:T(1024)} %param.10) | copy-start | bytes 49156
  4.0 13.8 %all-to-all-start = ((f32[32,1,16]{2,1,0:T(1,128)}), f32[32,1,16]{2,1,0:T(1,128)S(1)}, u32[]{:S(2)}, u32[]{:S(2)}) async-start(f32[32,1,16]{2,1,0:T(1,128)} %bitcast.1), calls=%async_computation | async-start | bytes 32768 | tf_op jit(solution)/shard_map/all_to_all | solution.py:92
  14.2 20.8 %copy-start.20 = (f32[128]{0:T(128)}, f32[128]{0:T(128)S(1)}, u32[]{:S(2)}) copy-start(f32[128]{0:T(128)S(1)} %add_multiply_fusion.1) | copy-start | bytes 1540
  19.1 54.5 %collective-permute-start = (f32[128,2048]{0,1:T(8,128)}, f32[128,2048]{0,1:T(8,128)}, u32[]{:S(2)}, u32[]{:S(2)}) collective-permute-start(f32[128,2048]{0,1:T(8,128)} %convert_bitcast_fusion), channel_id=1, source_target_pairs={{24,16},{8,0},{25,17},{9,1},{26,18},{10,2},{27,19},{11,3},{28,20},... | collective-permute-start | bytes 3145736 | tf_op jit(solution)/shard_map/ppermute | solution.py:150
  20.4 53.2 %collective-permute-start.1 = (f32[128,2048]{0,1:T(8,128)}, f32[128,2048]{0,1:T(8,128)}, u32[]{:S(2)}, u32[]{:S(2)}) collective-permute-start(f32[128,2048]{0,1:T(8,128)} %convert_bitcast_fusion), channel_id=1, source_target_pairs={{24,8},{16,0},{25,9},{17,1},{26,10},{18,2},{27,11},{19,3},{28,12},... | collective-permute-start | bytes 3145736 | tf_op jit(solution)/shard_map/ppermute | solution.py:151
  21.7 51.9 %collective-permute-start.2 = (f32[128,2048]{0,1:T(8,128)}, f32[128,2048]{0,1:T(8,128)}, u32[]{:S(2)}, u32[]{:S(2)}) collective-permute-start(f32[128,2048]{0,1:T(8,128)} %convert_bitcast_fusion), channel_id=1, source_target_pairs={{16,8},{24,0},{17,9},{25,1},{18,10},{26,2},{19,11},{27,3},{20,12},... | collective-permute-start | bytes 3145736 | tf_op jit(solution)/shard_map/ppermute | solution.py:152
  25.1 4.2 %copy-start.31 = (bf16[128,32]{0,1:T(8,128)(2,1)S(1)}, bf16[128,32]{0,1:T(8,128)(2,1)}, u32[]{:S(2)}) copy-start(bf16[128,32]{0,1:T(8,128)(2,1)} %param.12) | copy-start | bytes 24580
  25.1 4.2 %copy-start.32 = (f32[32]{0:T(128)S(1)}, f32[32]{0:T(128)}, u32[]{:S(2)}) copy-start(f32[32]{0:T(128)} %param.13) | copy-start | bytes 388
  25.1 6.2 %copy-start.22 = (f32[32]{0:T(128)S(1)}, f32[32]{0:T(128)}, u32[]{:S(2)}) copy-start(f32[32]{0:T(128)} %param.14) | copy-start | bytes 388
  34.0 2.4 %copy-start.23 = (f32[1,128]{1,0:T(1,128)}, f32[1,128]{1,0:T(1,128)S(1)}, u32[]{:S(2)}) copy-start(f32[1,128]{1,0:T(1,128)S(1)} %constant_dynamic-slice_fusion.7) | copy-start | bytes 1540
  35.1 1.4 %copy-start.11 = (f32[128,32]{0,1:T(8,128)}, f32[128,32]{0,1:T(8,128)S(1)}, u32[]{:S(2)}) copy-start(f32[128,32]{0,1:T(8,128)S(1)} %get-tuple-element.53) | copy-start | bytes 49156
  45.6 6.6 %copy-start.4 = (f32[4,128,32]{2,1,0:T(8,128)S(1)}, f32[4,128,32]{2,1,0:T(8,128)}, u32[]{:S(2)}) copy-start(f32[4,128,32]{2,1,0:T(8,128)} %exp.40) | copy-start | bytes 196612
  62.7 3.6 %copy-start.7 = (f32[128,32]{1,0:T(8,128)S(1)}, f32[128,32]{1,0:T(8,128)}, u32[]{:S(2)}) copy-start(f32[128,32]{1,0:T(8,128)} %exp.39) | copy-start | bytes 49156
  68.1 2.5 %copy-start.29 = (f32[32]{0:T(128)}, f32[32]{0:T(128)S(1)}, u32[]{:S(2)}) copy-start(f32[32]{0:T(128)S(1)} %get-tuple-element.49) | copy-start | bytes 388
  68.1 8.1 %copy-start.25 = (f32[32]{0:T(128)}, f32[32]{0:T(128)S(1)}, u32[]{:S(2)}) copy-start(f32[32]{0:T(128)S(1)} %get-tuple-element.51) | copy-start | bytes 388
  68.1 8.4 %copy-start.27 = (f32[32]{0:T(128)}, f32[32]{0:T(128)S(1)}, u32[]{:S(2)}) copy-start(f32[32]{0:T(128)S(1)} %get-tuple-element.50) | copy-start | bytes 388
  68.1 2.5 %copy-start.15 = (f32[128,128]{0,1:T(8,128)S(1)}, f32[128,128]{0,1:T(8,128)}, u32[]{:S(2)}) copy-start(f32[128,128]{0,1:T(8,128)} %fusion.72) | copy-start | bytes 196612
  70.6 1.6 %copy-start.1 = (f32[3,32,64,128]{3,2,1,0:T(8,128)}, f32[3,32,64,128]{3,2,1,0:T(8,128)S(1)}, u32[]{:S(2)}) copy-start(f32[3,32,64,128]{3,2,1,0:T(8,128)S(1)} %fusion.5) | copy-start | bytes 9437188
  70.6 1.6 %copy-start.12 = (f32[128,128]{0,1:T(8,128)S(1)}, f32[128,128]{0,1:T(8,128)}, u32[]{:S(2)}) copy-start(f32[128,128]{0,1:T(8,128)} %fusion.75) | copy-start | bytes 196612
  70.6 1.6 %copy-start.17 = (f32[32,128]{1,0:T(8,128)S(1)}, f32[32,128]{1,0:T(8,128)}, u32[]{:S(2)}) copy-start(f32[32,128]{1,0:T(8,128)} %copy.95) | copy-start | bytes 49156
  70.6 1.6 %copy-start.18 = (pred[128,128]{0,1:T(8,128)(4,1)S(1)}, pred[128,128]{0,1:T(8,128)(4,1)}, u32[]{:S(2)}) copy-start(pred[128,128]{0,1:T(8,128)(4,1)} %iota_compare_fusion) | copy-start | bytes 49156
  70.6 1.6 %copy-start.33 = (f32[32,128]{1,0:T(8,128)S(1)}, f32[32,128]{1,0:T(8,128)}, u32[]{:S(2)}) copy-start(f32[32,128]{1,0:T(8,128)} %get-tuple-element.52) | copy-start | bytes 49156
  72.2 1.4 %copy-start.8 = (f32[128,32]{0,1:T(8,128)S(1)}, f32[128,32]{0,1:T(8,128)}, u32[]{:S(2)}) copy-start(f32[128,32]{0,1:T(8,128)} %copy.105) | copy-start | bytes 49156
  72.2 1.4 %copy-start.9 = (f32[128,32]{0,1:T(8,128)S(1)}, f32[128,32]{0,1:T(8,128)}, u32[]{:S(2)}) copy-start(f32[128,32]{0,1:T(8,128)} %copy.106) | copy-start | bytes 49156
  72.3 1.4 %copy-start.10 = (f32[128,32]{0,1:T(8,128)S(1)}, f32[128,32]{0,1:T(8,128)}, u32[]{:S(2)}) copy-start(f32[128,32]{0,1:T(8,128)} %copy.107) | copy-start | bytes 49156
  76.5 1.4 %copy-start.5 = (bf16[128,2048]{0,1:T(8,128)(2,1)S(1)}, bf16[128,2048]{0,1:T(8,128)(2,1)}, u32[]{:S(2)}) copy-start(bf16[128,2048]{0,1:T(8,128)(2,1)} %copy.92) | copy-start | bytes 1572868
  76.5 1.4 %copy-start.14 = (f32[128,128]{0,1:T(8,128)S(1)}, f32[128,128]{0,1:T(8,128)}, u32[]{:S(2)}) copy-start(f32[128,128]{0,1:T(8,128)} %fusion.77) | copy-start | bytes 196612
  76.8 1.5 %copy-start.21 = (f32[128]{0:T(128)S(1)}, f32[128]{0:T(128)}, u32[]{:S(2)}) copy-start(f32[128]{0:T(128)} %copy-done.20) | copy-start | bytes 1540
  76.8 1.5 %copy-start.24 = (f32[1,128]{1,0:T(1,128)S(1)}, f32[1,128]{1,0:T(1,128)}, u32[]{:S(2)}) copy-start(f32[1,128]{1,0:T(1,128)} %copy-done.23) | copy-start | bytes 1540
  78.9 2.3 %collective-permute-start.3 = (f32[1152,128]{1,0:T(8,128)S(1)}, f32[1152,128]{1,0:T(8,128)S(1)}, u32[]{:S(2)}, u32[]{:S(2)}) collective-permute-start(f32[1152,128]{1,0:T(8,128)S(1)} %constant_dynamic-slice_fusion.6), channel_id=1, source_target_pairs={{0,1},{1,0},{2,3},{3,2},{4,5},{5,4},{6,7},{7,6},{8,9},{9,8},{10,11... | collective-permute-start | bytes 1769480 | tf_op jit(solution)/shard_map/ppermute | solution.py:26
  81.3 7.1 %collective-permute-start.4 = (f32[288,128]{1,0:T(8,128)S(1)}, f32[288,128]{1,0:T(8,128)S(1)}, u32[]{:S(2)}, u32[]{:S(2)}) collective-permute-start(f32[288,128]{1,0:T(8,128)S(1)} %get-tuple-element.27), channel_id=1, source_target_pairs={{0,2},{1,3},{2,0},{3,1},{4,6},{5,7},{6,4},{7,5},{8,10},{9,11},{10,... | collective-permute-start | bytes 442376 | tf_op jit(solution)/shard_map/ppermute | solution.py:26
  81.7 12.1 %collective-permute-start.5 = (f32[288,128]{1,0:T(8,128)S(1)}, f32[288,128]{1,0:T(8,128)S(1)}, u32[]{:S(2)}, u32[]{:S(2)}) collective-permute-start(f32[288,128]{1,0:T(8,128)S(1)} %get-tuple-element.29), channel_id=1, source_target_pairs={{0,4},{1,5},{2,6},{3,7},{4,0},{5,1},{6,2},{7,3},{8,12},{9,13},{10,... | collective-permute-start | bytes 442376 | tf_op jit(solution)/shard_map/ppermute | solution.py:26
  82.0 11.7 %collective-permute-start.6 = (f32[288,128]{1,0:T(8,128)S(1)}, f32[288,128]{1,0:T(8,128)S(1)}, u32[]{:S(2)}, u32[]{:S(2)}) collective-permute-start(f32[288,128]{1,0:T(8,128)S(1)} %get-tuple-element.28), channel_id=1, source_target_pairs={{0,6},{1,7},{2,4},{3,5},{4,2},{5,3},{6,0},{7,1},{8,14},{9,15},{10,... | collective-permute-start | bytes 442376 | tf_op jit(solution)/shard_map/ppermute | solution.py:26
  93.8 7.8 %collective-permute-start.7 = (f32[72,128]{1,0:T(8,128)S(1)}, f32[72,128]{1,0:T(8,128)S(1)}, u32[]{:S(2)}, u32[]{:S(2)}) collective-permute-start(f32[72,128]{1,0:T(8,128)S(1)} %get-tuple-element.39), channel_id=1, source_target_pairs={{0,8},{8,0},{16,24},{24,16},{1,9},{9,1},{17,25},{25,17},{2,10},{10... | collective-permute-start | bytes 110600 | tf_op jit(solution)/shard_map/ppermute | solution.py:26
  97.2 5.7 %collective-permute-start.8 = (f32[72,128]{1,0:T(8,128)S(1)}, f32[72,128]{1,0:T(8,128)S(1)}, u32[]{:S(2)}, u32[]{:S(2)}) collective-permute-start(f32[72,128]{1,0:T(8,128)S(1)} %get-tuple-element.41), channel_id=1, source_target_pairs={{0,16},{8,24},{16,0},{24,8},{1,17},{9,25},{17,1},{25,9},{2,18},{10... | collective-permute-start | bytes 110600 | tf_op jit(solution)/shard_map/ppermute | solution.py:26
  101.5 3.7 %collective-permute-start.9 = (f32[72,128]{1,0:T(8,128)S(1)}, f32[72,128]{1,0:T(8,128)S(1)}, u32[]{:S(2)}, u32[]{:S(2)}) collective-permute-start(f32[72,128]{1,0:T(8,128)S(1)} %get-tuple-element.40), channel_id=1, source_target_pairs={{0,24},{8,16},{16,8},{24,0},{1,25},{9,17},{17,9},{25,1},{2,26},{10... | collective-permute-start | bytes 110600 | tf_op jit(solution)/shard_map/ppermute | solution.py:26
  105.3 2.9 %collective-permute-start.10 = (f32[72,128]{1,0:T(8,128)S(1)}, f32[72,128]{1,0:T(8,128)S(1)}, u32[]{:S(2)}, u32[]{:S(2)}) collective-permute-start(f32[72,128]{1,0:T(8,128)S(1)} %add_add_fusion.1), channel_id=1, source_target_pairs={{0,8},{8,0},{16,24},{24,16},{1,9},{9,1},{17,25},{25,17},{2,10},{10... | collective-permute-start | bytes 110600 | tf_op jit(solution)/shard_map/ppermute | solution.py:26
  105.5 2.8 %collective-permute-start.11 = (f32[72,128]{1,0:T(8,128)S(1)}, f32[72,128]{1,0:T(8,128)S(1)}, u32[]{:S(2)}, u32[]{:S(2)}) collective-permute-start(f32[72,128]{1,0:T(8,128)S(1)} %add_add_fusion.1), channel_id=1, source_target_pairs={{0,16},{8,24},{16,0},{24,8},{1,17},{9,25},{17,1},{25,9},{2,18},{10... | collective-permute-start | bytes 110600 | tf_op jit(solution)/shard_map/ppermute | solution.py:26
  105.6 3.7 %collective-permute-start.12 = (f32[72,128]{1,0:T(8,128)S(1)}, f32[72,128]{1,0:T(8,128)S(1)}, u32[]{:S(2)}, u32[]{:S(2)}) collective-permute-start(f32[72,128]{1,0:T(8,128)S(1)} %add_add_fusion.1), channel_id=1, source_target_pairs={{0,24},{8,16},{16,8},{24,0},{1,25},{9,17},{17,9},{25,1},{2,26},{10... | collective-permute-start | bytes 110600 | tf_op jit(solution)/shard_map/ppermute | solution.py:26
  109.4 18.9 %copy-start.6 = (bf16[128,2048]{0,1:T(8,128)(2,1)S(1)}, bf16[128,2048]{0,1:T(8,128)(2,1)}, u32[]{:S(2)}) copy-start(bf16[128,2048]{0,1:T(8,128)(2,1)} %copy.92) | copy-start | bytes 1572868
  109.4 18.9 %copy-start.13 = (f32[128,128]{0,1:T(8,128)S(1)}, f32[128,128]{0,1:T(8,128)}, u32[]{:S(2)}) copy-start(f32[128,128]{0,1:T(8,128)} %fusion.75) | copy-start | bytes 196612
  109.4 18.9 %copy-start.19 = (pred[128,128]{0,1:T(8,128)(4,1)S(1)}, pred[128,128]{0,1:T(8,128)(4,1)}, u32[]{:S(2)}) copy-start(pred[128,128]{0,1:T(8,128)(4,1)} %iota_compare_fusion) | copy-start | bytes 49156
  109.4 18.9 %copy-start.34 = (f32[32,128]{1,0:T(8,128)S(1)}, f32[32,128]{1,0:T(8,128)}, u32[]{:S(2)}) copy-start(f32[32,128]{1,0:T(8,128)} %get-tuple-element.52) | copy-start | bytes 49156
  109.5 6.0 %collective-permute-start.13 = (f32[288,128]{1,0:T(8,128)S(1)}, f32[288,128]{1,0:T(8,128)S(1)}, u32[]{:S(2)}, u32[]{:S(2)}) collective-permute-start(f32[288,128]{1,0:T(8,128)S(1)} %get-tuple-element.34), channel_id=1, source_target_pairs={{0,2},{1,3},{2,0},{3,1},{4,6},{5,7},{6,4},{7,5},{8,10},{9,11},{10,... | collective-permute-start | bytes 442376 | tf_op jit(solution)/shard_map/ppermute | solution.py:26
  113.0 8.2 %collective-permute-start.14 = (f32[288,128]{1,0:T(8,128)S(1)}, f32[288,128]{1,0:T(8,128)S(1)}, u32[]{:S(2)}, u32[]{:S(2)}) collective-permute-start(f32[288,128]{1,0:T(8,128)S(1)} %get-tuple-element.34), channel_id=1, source_target_pairs={{0,4},{1,5},{2,6},{3,7},{4,0},{5,1},{6,2},{7,3},{8,12},{9,13},{10,... | collective-permute-start | bytes 442376 | tf_op jit(solution)/shard_map/ppermute | solution.py:26
  113.0 8.1 %collective-permute-start.15 = (f32[288,128]{1,0:T(8,128)S(1)}, f32[288,128]{1,0:T(8,128)S(1)}, u32[]{:S(2)}, u32[]{:S(2)}) collective-permute-start(f32[288,128]{1,0:T(8,128)S(1)} %get-tuple-element.34), channel_id=1, source_target_pairs={{0,6},{1,7},{2,4},{3,5},{4,2},{5,3},{6,0},{7,1},{8,14},{9,15},{10,... | collective-permute-start | bytes 442376 | tf_op jit(solution)/shard_map/ppermute | solution.py:26
  121.3 11.8 %collective-permute-start.16 = (f32[1152,128]{1,0:T(8,128)S(1)}, f32[1152,128]{1,0:T(8,128)S(1)}, u32[]{:S(2)}, u32[]{:S(2)}) collective-permute-start(f32[1152,128]{1,0:T(8,128)S(1)} %get-tuple-element.21), channel_id=1, source_target_pairs={{0,1},{1,0},{2,3},{3,2},{4,5},{5,4},{6,7},{7,6},{8,9},{9,8},{10,11... | collective-permute-start | bytes 1769480 | tf_op jit(solution)/shard_map/ppermute | solution.py:26
  (5 other events, 5.5 us)

commit v18 on v15

--- a/solution.py
+++ b/solution.py
@@ -90,13 +90,13 @@
     ordered = jnp.take(codes, owner_slot, axis=0).astype(fl)
     outgoing = jnp.tile(ordered, (n_blocks, 1))
     reading = lax.all_to_all(outgoing, ("tm", "series"), split_axis=0, concat_axis=1, tiled=True)[0]
-    sent, reading = lax.optimization_barrier((grad_out[0].astype(fl), reading))
     edge_float = edges.astype(fl)
     upper_edge = jnp.concatenate([edge_float[1:], jnp.full((1,), code_ceiling, fl)])
     onehot = (
         (edge_float[None, :] <= reading[:, None]) & (upper_edge[None, :] > reading[:, None])
     ).astype(fl)
     counts = jnp.sum(onehot, axis=0)
+    sent, counts = lax.optimization_barrier((grad_out[0].astype(fl), counts))
     before = jnp.cumsum(counts) - counts
     bin_table = jnp.stack([before, counts, edge_float, upper_edge - edge_float], axis=1)
     high = jnp.floor(bin_table / 65536.0) * 65536.0

time: 135 us -> 127 us (0.941)
  waiting for transfers between devices: 42.6 us -> 21.3 us
  starting transfers between devices: 29.5 us -> 35.5 us
  matrix products: 20 us -> 24.8 us
  local copies, waits for them, and re-layouts: 24.6 us -> 26.8 us
    ppermute x1, waiting for transfers between devices: 21.3 us -> 0.01 us  [on_device(): along_y = lax.ppermute(sent, 'tm', [(3, 1), (2, 0)])]
    ppermute x14, starting transfers between devices: 18.4 us -> 24.5 us  [exchange(): return lax.ppermute(value, axis, pairs)]
    slice x2, local copies, waits for them, and re-layouts: 0.33 us -> 3.92 us  [on_device(): x_heads = projected[:, :inner_width].reshape(tok_rows, head_count, head_dim)]
    unnamed x83 -> x73, local copies, waits for them, and re-layouts: 6.63 us -> 5.53 us
  transfers between devices with their start and end apart: 18 -> 18, of which waited for: 14 -> 11; matrix products, arithmetic and copies ran while one was open for 24% -> 42% of each run, Pallas kernels for 0% -> 0%
where the time goes in v18:
time: 127 us; the launch traced here: 126 us
  starting transfers between devices  35.5 us (28%)
  local copies, waits for them, and re-layouts  26.8 us (21%)
  matrix products  24.8 us (20%)
  waiting for transfers between devices  21.3 us (17%)
  other arithmetic  16.4 us (13%)
  between operations  1.37 us (1%)
    ppermute x14, starting transfers between devices, exchange(): return lax.ppermute(value, axis, pairs)  24.5 us
    ppermute x14, waiting for transfers between devices, exchange(): return lax.ppermute(value, axis, pairs)  18.5 us
    all_to_all x1, starting transfers between devices, on_device(): lax.all_to_all(outgoing, ('tm', 'series'), split_axis=0, concat_axis=1, t...  7.1 us
    unnamed x73, local copies, waits for them, and re-layouts  5.53 us
    mul x4, local copies, waits for them, and re-layouts, on_device(): later_weighted = (later * head_all[k][:, :, None]).astype(half)  4.34 us
    slice x2, local copies, waits for them, and re-layouts, on_device(): x_heads = projected[:, :inner_width].reshape(tok_rows, head_count, head_dim)  3.92 us
    convert_element_type x1, local copies, waits for them, and re-layouts, on_device(): xw_all = (x_all[:earlier] * tail_all[:earlier, :, :, None]).astype(half)  3.56 us
    all_to_all x1, waiting for transfers between devices, on_device(): lax.all_to_all(outgoing, ('tm', 'series'), split_axis=0, concat_axis=1, t...  2.82 us
  transfers between devices with their start and end apart: 18, of which 11 were waited for; matrix products, arithmetic and copies ran while one was open for 42% of the time, Pallas kernels for 0%

profile of v18, /device:TPU:1, one launch (start us, length us, event | category | flops | bytes accessed | tf_op | source)
XLA Modules:
  0.0 126.1 jit_solution(2450364868659103316)
XLA Ops:
  2.1 1.2 gather_fusion
  4.0 7.1 %all-to-all-start = ((f32[32,1,16]{2,1,0:T(1,128)}), f32[32,1,16]{2,1,0:T(1,128)S(1)}, u32[]{:S(2)}, u32[]{:S(2)}) async-start(f32[32,1,16]{2,1,0:T(1,128)} %bitcast), calls=%async_computation | async-start | bytes 32768 | tf_op jit(solution)/shard_map/all_to_all | solution.py:92
  12.5 1.3 %copy.91 = bf16[1,128,2048]{1,2,0:T(8,128)(2,1)S(1)} copy(bf16[1,128,2048]{2,1,0:T(8,128)(2,1)} %param.15) | data formatting | bytes 1048576 | tf_op args[7]
  13.8 1.0 convert_bitcast_fusion
  15.0 2.8 %all-to-all-done = f32[32,1,16]{2,1,0:T(1,128)S(1)} async-done(((f32[32,1,16]{2,1,0:T(1,128)}), f32[32,1,16]{2,1,0:T(1,128)S(1)}, u32[]{:S(2)}, u32[]{:S(2)}) %all-to-all-start) | async-done | bytes 2080 | tf_op jit(solution)/shard_map/all_to_all | solution.py:92
  19.1 1.5 %convert_reduce_fusion = f32[4096]{0:T(1024)S(1)} fusion(f32[4096]{0:T(1024)S(1)} %get-tuple-element.46, f32[4096]{0:T(1024)S(1)} %convert_element_type.121, f32[512]{0:T(512)S(1)} %le.22), kind=kLoop, calls=%fused_computation.1 | loop fusion | flops 10481664 | bytes 51200 | tf_op jit(solution)/shard_map/reduce_sum | solution.py:98
  20.5 1.3 %collective-permute-start = (f32[128,2048]{0,1:T(8,128)}, f32[128,2048]{0,1:T(8,128)}, u32[]{:S(2)}, u32[]{:S(2)}) collective-permute-start(f32[128,2048]{0,1:T(8,128)} %convert_bitcast_fusion), channel_id=1, source_target_pairs={{24,16},{8,0},{25,17},{9,1},{26,18},{10,2},{27,19},{11,3},{28,20},... | collective-permute-start | bytes 3145736 | tf_op jit(solution)/shard_map/ppermute | solution.py:156
  21.8 1.3 %collective-permute-start.1 = (f32[128,2048]{0,1:T(8,128)}, f32[128,2048]{0,1:T(8,128)}, u32[]{:S(2)}, u32[]{:S(2)}) collective-permute-start(f32[128,2048]{0,1:T(8,128)} %convert_bitcast_fusion), channel_id=1, source_target_pairs={{24,8},{16,0},{25,9},{17,1},{26,10},{18,2},{27,11},{19,3},{28,12},... | collective-permute-start | bytes 3145736 | tf_op jit(solution)/shard_map/ppermute | solution.py:157
  23.1 1.3 %collective-permute-start.2 = (f32[128,2048]{0,1:T(8,128)}, f32[128,2048]{0,1:T(8,128)}, u32[]{:S(2)}, u32[]{:S(2)}) collective-permute-start(f32[128,2048]{0,1:T(8,128)} %convert_bitcast_fusion), channel_id=1, source_target_pairs={{16,8},{24,0},{17,9},{25,1},{18,10},{26,2},{19,11},{27,3},{20,12},... | collective-permute-start | bytes 3145736 | tf_op jit(solution)/shard_map/ppermute | solution.py:158
  25.2 1.3 %fusion = f32[512,12]{0,1:T(8,128)S(1)} fusion(f32[4096]{0:T(1024)S(1)} %get-tuple-element.46, f32[4096]{0:T(1024)S(1)} %convert_element_type.121, f32[512]{0:T(512)S(1)} %le.22, bf16[4096,4]{0,1:T(4,128)(2,1)S(1)} %get-tuple-element.44, bf16[4096,4]{0,1:T(4,128)(2,1)S(1)} %get-tuple-element.43, bf16[4096,4]{0,1:T(4,128)(2,1)S(1)} %get-tuple-element.42), kind=kOutput, calls=%fused_computation.5 | convolution fusion | flops 61112320 | bytes 157696 | tf_op jit(solution)/shard_map/dot_general | solution.py:106
  26.6 1.1 compare_select_fusion
  29.7 1.6 %convolution_convert_fusion = bf16[512,2304]{1,0:T(8,128)(2,1)S(1)} fusion(bf16[128,2304]{1,0:T(8,128)(2,1)S(1)} %copy-done, f32[128]{0:T(128)S(1)} %add_multiply_fusion, f32[512]{0:T(512)S(1)} %bitcast.234), kind=kOutput, calls=%fused_computation.4 | convolution fusion | flops 303300608 | bytes 2951680 | tf_op jit(solution)/shard_map/dot_general | solution.py:129
  31.3 1.0 compare_select_fusion.1
  32.3 1.4 %convolution_convert_fusion.1 = bf16[128,2304]{1,0:T(8,128)(2,1)} fusion(bf16[128,2304]{1,0:T(8,128)(2,1)S(1)} %copy-done, f32[128]{0:T(128)S(1)} %add_multiply_fusion, f32[1,128]{1,0:T(1,128)S(1)} %constant_dynamic-slice_fusion.7), kind=kOutput, calls=%fused_computation.7 | convolution fusion | flops 75825152 | bytes 1180672 | tf_op jit(solution)/shard_map/dot_general | solution.py:119
  34.6 1.0 reduce_window_sum.39
  36.8 1.5 %fusion.74 = f32[128,128]{0,1:T(8,128)} fusion(bf16[128,2304]{1,0:T(8,128)(2,1)} %convolution_convert_fusion.1), kind=kOutput, calls=%fused_computation.142 | convolution fusion | flops 4194304 | bytes 131072 | tf_op jit(solution)/shard_map/dot_general | solution.py:178
  38.3 1.9 %slice.149 = bf16[128,2048]{1,0:T(8,128)(2,1)} slice(bf16[128,2304]{1,0:T(8,128)(2,1)} %convolution_convert_fusion.1), slice={[0:128], [0:2048]} | slice | bytes 1048576 | tf_op jit(solution)/shard_map/slice | solution.py:120
  40.9 2.0 %copy.92 = bf16[128,2048]{0,1:T(8,128)(2,1)} copy(bf16[128,2048]{1,0:T(8,128)(2,1)} %slice.149) | data formatting | bytes 1048576 | tf_op jit(solution)/shard_map/slice | solution.py:120
  42.9 2.8 %fusion.2 = bf16[128,128]{0,1:T(8,128)(2,1)S(1)} fusion(bf16[128,32,64]{0,2,1:T(8,128)(2,1)} %bitcast.213, bf16[128,32,64]{0,2,1:T(8,128)(2,1)S(1)} %bitcast.203, f32[32,128]{1,0:T(8,128)} %get-tuple-element.51, f32[32,128]{1,0:T(8,128)} %copy.95, pred[128,128]{0,1:T(8,128)(4,1)} %iota_compare_fusion), kind=kOutput, calls=%fused_computation.10 | convolution fusion | flops 70238208 | bytes 1130496 | tf_op jit(solution)/shard_map/thp,shp->hts/dot_general | solution.py:195
  45.7 1.6 %fusion.76 = f32[128,128]{0,1:T(8,128)} fusion(bf16[128,2304]{1,0:T(8,128)(2,1)} %convolution_convert_fusion.1, bf16[128,128]{0,1:T(8,128)(2,1)S(1)} %fusion.2), kind=kOutput, calls=%fused_computation.144 | convolution fusion | flops 4194304 | bytes 131072 | tf_op jit(solution)/shard_map/dot_general | solution.py:197
  47.3 1.6 %fusion.71 = f32[128,128]{0,1:T(8,128)} fusion(bf16[128,2304]{1,0:T(8,128)(2,1)} %convolution_convert_fusion.1, bf16[128,128]{0,1:T(8,128)(2,1)S(1)} %fusion.2), kind=kOutput, calls=%fused_computation.139 | convolution fusion | flops 4194304 | bytes 131072 | tf_op jit(solution)/shard_map/dot_general | solution.py:199
  50.2 1.5 %copy.105 = f32[128,32]{0,1:T(8,128)} copy(f32[128,32]{1,0:T(8,128)} %get-tuple-element.32) | data formatting | bytes 32768 | tf_op jit(solution)/shard_map/mul | solution.py:167
  51.7 1.5 %copy.106 = f32[128,32]{0,1:T(8,128)} copy(f32[128,32]{1,0:T(8,128)} %get-tuple-element.31) | data formatting | bytes 32768 | tf_op jit(solution)/shard_map/mul | solution.py:167
  54.5 1.7 %slice_multiply_fusion = f32[3,128,32]{2,1,0:T(8,128)} fusion(f32[4,128,32]{2,1,0:T(8,128)} %bitcast.210, f32[4,128,32]{2,1,0:T(8,128)} %copy-done.2, f32[3,32]{1,0:T(4,128)S(1)} %bitcast.232), kind=kLoop, calls=%fused_computation.87 | loop fusion | flops 24576 | bytes 147840 | tf_op jit(solution)/shard_map/mul | solution.py:138
  56.2 1.7 %copy.101 = f32[3,128,32]{1,2,0:T(8,128)} copy(f32[3,128,32]{2,1,0:T(8,128)} %slice_multiply_fusion) | data formatting | bytes 98304 | tf_op jit(solution)/shard_map/slice | solution.py:141
  57.9 2.1 %slice_convert_fusion = f32[3,128,2048]{2,1,0:T(8,128)} fusion(bf16[4,128,2304]{2,1,0:T(8,128)(2,1)S(1)} %bitcast.198), kind=kLoop, calls=%fused_computation.14 | loop fusion | flops 786432 | bytes 4718592 | tf_op jit(solution)/shard_map/convert_element_type | solution.py:141
  59.9 3.6 %copy.99 = f32[3,128,2048]{1,2,0:T(8,128)} copy(f32[3,128,2048]{2,1,0:T(8,128)} %slice_convert_fusion) | data formatting | bytes 6291456 | tf_op jit(solution)/shard_map/convert_element_type | solution.py:141
  65.4 2.5 %fusion.3 = f32[3,32,64,128]{3,2,1,0:T(8,128)S(1)} fusion(f32[3,128,32,64]{1,3,2,0:T(8,128)} %bitcast.197, f32[3,128,32]{1,2,0:T(8,128)} %copy.101, bf16[4,128,2304]{2,1,0:T(8,128)(2,1)S(1)} %bitcast.199), kind=kOutput, calls=%fused_computation.13 | convolution fusion | flops 202899456 | bytes 6438912 | tf_op jit(solution)/shard_map/bthp,btn->bhpn/dot_general | solution.py:142
  69.6 1.3 %convolution_bitcast_fusion = f32[128,32,64]{0,2,1:T(8,128)S(1)} fusion(bf16[128,32,64]{0,2,1:T(8,128)(2,1)S(1)} %bitcast.204, f32[32,128]{1,0:T(8,128)S(1)} %copy-done.33, f32[32,128]{1,0:T(8,128)S(1)} %copy-done.17, f32[128,128]{0,1:T(8,128)S(1)} %copy-done.12, pred[128,128]{0,1:T(8,128)(4,1)S(1)} %copy-done.18), kind=kOutput, calls=%fused_computation.28 | convolution fusion | flops 70254592 | bytes 1687552 | tf_op jit(solution)/shard_map/hts,thp->shp/dot_general | solution.py:189
  70.9 2.2 %fusion.20 = (bf16[128,2048]{0,1:T(8,128)(2,1)S(1)}, bf16[128,2048]{0,1:T(8,128)(2,1)S(1)}, bf16[128,2048]{0,1:T(8,128)(2,1)S(1)}) fusion(f32[128,2048]{0,1:T(8,128)} %collective-permute-done.2, f32[128,2048]{0,1:T(8,128)} %collective-permute-done.1, f32[128,32]{0,1:T(8,128)S(1)} %copy-done.9, pred[]{:T(512)S(6)} %eq.19, f32[128,32]{0,1:T(8,128)S(1)} %copy-done.8, ...), kind=kLoop, calls=%fused_computation.51 | loop fusion | flops 2359296 | bytes 4767746 | tf_op jit(solution)/shard_map/convert_element_type | solution.py:167
  74.1 1.1 fusion.12
  76.2 1.2 collective-permute-start.3
  77.4 1.6 %collective-permute-done.3 = f32[1152,128]{1,0:T(8,128)S(1)} collective-permute-done((f32[1152,128]{1,0:T(8,128)S(1)}, f32[1152,128]{1,0:T(8,128)S(1)}, u32[]{:S(2)}, u32[]{:S(2)}) %collective-permute-start.3) | collective-permute-done | bytes 589856 | tf_op jit(solution)/shard_map/ppermute | solution.py:26
  79.2 3.1 %collective-permute-start.4 = (f32[288,128]{1,0:T(8,128)S(1)}, f32[288,128]{1,0:T(8,128)S(1)}, u32[]{:S(2)}, u32[]{:S(2)}) collective-permute-start(f32[288,128]{1,0:T(8,128)S(1)} %get-tuple-element.27), channel_id=1, source_target_pairs={{0,8},{8,0},{16,24},{24,16},{1,9},{9,1},{17,25},{25,17},{2,10},{10... | collective-permute-start | bytes 442376 | tf_op jit(solution)/shard_map/ppermute | solution.py:26
  82.3 4.1 %collective-permute-start.5 = (f32[288,128]{1,0:T(8,128)S(1)}, f32[288,128]{1,0:T(8,128)S(1)}, u32[]{:S(2)}, u32[]{:S(2)}) collective-permute-start(f32[288,128]{1,0:T(8,128)S(1)} %get-tuple-element.29), channel_id=1, source_target_pairs={{0,16},{8,24},{16,0},{24,8},{1,17},{9,25},{17,1},{25,9},{2,18},{10... | collective-permute-start | bytes 442376 | tf_op jit(solution)/shard_map/ppermute | solution.py:26
  86.4 5.8 %collective-permute-done.5 = f32[288,128]{1,0:T(8,128)S(1)} collective-permute-done((f32[288,128]{1,0:T(8,128)S(1)}, f32[288,128]{1,0:T(8,128)S(1)}, u32[]{:S(2)}, u32[]{:S(2)}) %collective-permute-start.5) | collective-permute-done | bytes 147488 | tf_op jit(solution)/shard_map/ppermute | solution.py:26
  93.7 3.0 %collective-permute-start.9 = (f32[72,128]{1,0:T(8,128)S(1)}, f32[72,128]{1,0:T(8,128)S(1)}, u32[]{:S(2)}, u32[]{:S(2)}) collective-permute-start(f32[72,128]{1,0:T(8,128)S(1)} %get-tuple-element.40), channel_id=1, source_target_pairs={{0,6},{1,7},{2,4},{3,5},{4,2},{5,3},{6,0},{7,1},{8,14},{9,15},{10,... | collective-permute-start | bytes 110600 | tf_op jit(solution)/shard_map/ppermute | solution.py:26
  97.1 1.4 %collective-permute-done.9 = f32[72,128]{1,0:T(8,128)S(1)} collective-permute-done((f32[72,128]{1,0:T(8,128)S(1)}, f32[72,128]{1,0:T(8,128)S(1)}, u32[]{:S(2)}, u32[]{:S(2)}) %collective-permute-start.9) | collective-permute-done | bytes 36896 | tf_op jit(solution)/shard_map/ppermute | solution.py:26
  98.6 3.1 %collective-permute-start.11 = (f32[72,128]{1,0:T(8,128)S(1)}, f32[72,128]{1,0:T(8,128)S(1)}, u32[]{:S(2)}, u32[]{:S(2)}) collective-permute-start(f32[72,128]{1,0:T(8,128)S(1)} %add_add_fusion.1), channel_id=1, source_target_pairs={{0,4},{1,5},{2,6},{3,7},{4,0},{5,1},{6,2},{7,3},{8,12},{9,13},{10,... | collective-permute-start | bytes 110600 | tf_op jit(solution)/shard_map/ppermute | solution.py:26
  103.0 3.4 %collective-permute-done.12 = f32[72,128]{1,0:T(8,128)S(1)} collective-permute-done((f32[72,128]{1,0:T(8,128)S(1)}, f32[72,128]{1,0:T(8,128)S(1)}, u32[]{:S(2)}, u32[]{:S(2)}) %collective-permute-start.12) | collective-permute-done | bytes 36896 | tf_op jit(solution)/shard_map/ppermute | solution.py:26
  106.5 1.3 %collective-permute-start.13 = (f32[288,128]{1,0:T(8,128)S(1)}, f32[288,128]{1,0:T(8,128)S(1)}, u32[]{:S(2)}, u32[]{:S(2)}) collective-permute-start(f32[288,128]{1,0:T(8,128)S(1)} %get-tuple-element.34), channel_id=1, source_target_pairs={{0,8},{8,0},{16,24},{24,16},{1,9},{9,1},{17,25},{25,17},{2,10},{10... | collective-permute-start | bytes 442376 | tf_op jit(solution)/shard_map/ppermute | solution.py:26
  109.2 1.4 %collective-permute-done.13 = f32[288,128]{1,0:T(8,128)S(1)} collective-permute-done((f32[288,128]{1,0:T(8,128)S(1)}, f32[288,128]{1,0:T(8,128)S(1)}, u32[]{:S(2)}, u32[]{:S(2)}) %collective-permute-start.13) | collective-permute-done | bytes 147488 | tf_op jit(solution)/shard_map/ppermute | solution.py:26
  110.6 1.2 collective-permute-done.14
  111.8 1.6 %collective-permute-done.15 = f32[288,128]{1,0:T(8,128)S(1)} collective-permute-done((f32[288,128]{1,0:T(8,128)S(1)}, f32[288,128]{1,0:T(8,128)S(1)}, u32[]{:S(2)}, u32[]{:S(2)}) %collective-permute-start.15) | collective-permute-done | bytes 147488 | tf_op jit(solution)/shard_map/ppermute | solution.py:26
  113.6 6.1 %collective-permute-start.16 = (f32[1152,128]{1,0:T(8,128)S(1)}, f32[1152,128]{1,0:T(8,128)S(1)}, u32[]{:S(2)}, u32[]{:S(2)}) collective-permute-start(f32[1152,128]{1,0:T(8,128)S(1)} %get-tuple-element.21), channel_id=1, source_target_pairs={{0,1},{1,0},{2,3},{3,2},{4,5},{5,4},{6,7},{7,6},{8,9},{9,8},{10,11... | collective-permute-start | bytes 1769480 | tf_op jit(solution)/shard_map/ppermute | solution.py:26
  119.7 1.3 %convolution_bitcast_fusion.1 = f32[128,32,64]{0,2,1:T(8,128)S(1)} fusion(bf16[128,32,64]{0,2,1:T(8,128)(2,1)S(1)} %bitcast.215, f32[32,128]{1,0:T(8,128)S(1)} %copy-done.34, f32[32,128]{1,0:T(8,128)S(1)} %copy-done.17, f32[128,128]{0,1:T(8,128)S(1)} %copy-done.13, pred[128,128]{0,1:T(8,128)(4,1)S(1)} %copy-done.19), kind=kOutput, calls=%fused_computation.31 | convolution fusion | flops 70254592 | bytes 1687552 | tf_op jit(solution)/shard_map/hts,shp->thp/dot_general | solution.py:182
  121.0 2.4 %fusion.10 = bf16[128,32,64]{0,2,1:T(8,128)(2,1)S(1)} fusion(f32[128,32,64]{0,2,1:T(8,128)S(1)} %convolution_bitcast_fusion.1, f32[3,32,64,128]{3,2,1,0:T(8,128)} %copy-done.1, f32[128,32]{0,1:T(8,128)S(1)} %copy.102, f32[32]{0:T(128)S(1)} %copy-done.30, f32[32]{0:T(128)S(1)} %copy-done.28, f32[32]{0:T(128)S(1)} %copy-done.26, pred[]{:T(512)S(6)} %gt.24, ...), kind=kOutput, calls=%fused_computation.34 | convolution fusion | flops 70254592 | bytes 4768131 | tf_op jit(solution)/shard_map/tn,hpn->thp/dot_general | solution.py:185
  124.8 1.4 %copy.110 = f32[128,2304]{1,0:T(8,128)} copy(f32[128,2304]{0,1:T(8,128)S(1)} %fusion.13) | data formatting | bytes 2359296
  (149 shorter events, 24.7 us)
Async XLA Ops:
  0.6 29.0 %copy-start = (bf16[128,2304]{1,0:T(8,128)(2,1)S(1)}, bf16[128,2304]{1,0:T(8,128)(2,1)}, u32[]{:S(2)}) copy-start(bf16[128,2304]{1,0:T(8,128)(2,1)} %param.11) | copy-start | bytes 1769476
  0.6 14.2 %copy-start.16 = (s32[4096]{0:T(1024)S(1)}, s32[4096]{0:T(1024)}, u32[]{:S(2)}) copy-start(s32[4096]{0:T(1024)} %param.10) | copy-start | bytes 49156
  4.0 13.8 %all-to-all-start = ((f32[32,1,16]{2,1,0:T(1,128)}), f32[32,1,16]{2,1,0:T(1,128)S(1)}, u32[]{:S(2)}, u32[]{:S(2)}) async-start(f32[32,1,16]{2,1,0:T(1,128)} %bitcast), calls=%async_computation | async-start | bytes 32768 | tf_op jit(solution)/shard_map/all_to_all | solution.py:92
  14.9 17.4 %copy-start.20 = (f32[128]{0:T(128)}, f32[128]{0:T(128)S(1)}, u32[]{:S(2)}) copy-start(f32[128]{0:T(128)S(1)} %add_multiply_fusion) | copy-start | bytes 1540
  20.5 50.3 %collective-permute-start = (f32[128,2048]{0,1:T(8,128)}, f32[128,2048]{0,1:T(8,128)}, u32[]{:S(2)}, u32[]{:S(2)}) collective-permute-start(f32[128,2048]{0,1:T(8,128)} %convert_bitcast_fusion), channel_id=1, source_target_pairs={{24,16},{8,0},{25,17},{9,1},{26,18},{10,2},{27,19},{11,3},{28,20},... | collective-permute-start | bytes 3145736 | tf_op jit(solution)/shard_map/ppermute | solution.py:156
  21.8 49.0 %collective-permute-start.1 = (f32[128,2048]{0,1:T(8,128)}, f32[128,2048]{0,1:T(8,128)}, u32[]{:S(2)}, u32[]{:S(2)}) collective-permute-start(f32[128,2048]{0,1:T(8,128)} %convert_bitcast_fusion), channel_id=1, source_target_pairs={{24,8},{16,0},{25,9},{17,1},{26,10},{18,2},{27,11},{19,3},{28,12},... | collective-permute-start | bytes 3145736 | tf_op jit(solution)/shard_map/ppermute | solution.py:157
  23.1 47.8 %collective-permute-start.2 = (f32[128,2048]{0,1:T(8,128)}, f32[128,2048]{0,1:T(8,128)}, u32[]{:S(2)}, u32[]{:S(2)}) collective-permute-start(f32[128,2048]{0,1:T(8,128)} %convert_bitcast_fusion), channel_id=1, source_target_pairs={{16,8},{24,0},{17,9},{25,1},{18,10},{26,2},{19,11},{27,3},{20,12},... | collective-permute-start | bytes 3145736 | tf_op jit(solution)/shard_map/ppermute | solution.py:158
  25.2 1.4 %copy-start.31 = (bf16[128,32]{0,1:T(8,128)(2,1)S(1)}, bf16[128,32]{0,1:T(8,128)(2,1)}, u32[]{:S(2)}) copy-start(bf16[128,32]{0,1:T(8,128)(2,1)} %param.12) | copy-start | bytes 24580
  25.2 1.4 %copy-start.32 = (f32[32]{0:T(128)S(1)}, f32[32]{0:T(128)}, u32[]{:S(2)}) copy-start(f32[32]{0:T(128)} %param.13) | copy-start | bytes 388
  25.2 3.4 %copy-start.22 = (f32[32]{0:T(128)S(1)}, f32[32]{0:T(128)}, u32[]{:S(2)}) copy-start(f32[32]{0:T(128)} %param.14) | copy-start | bytes 388
  31.3 2.4 %copy-start.23 = (f32[1,128]{1,0:T(1,128)}, f32[1,128]{1,0:T(1,128)S(1)}, u32[]{:S(2)}) copy-start(f32[1,128]{1,0:T(1,128)S(1)} %constant_dynamic-slice_fusion.7) | copy-start | bytes 1540
  32.3 1.4 %copy-start.11 = (f32[128,32]{0,1:T(8,128)}, f32[128,32]{0,1:T(8,128)S(1)}, u32[]{:S(2)}) copy-start(f32[128,32]{0,1:T(8,128)S(1)} %get-tuple-element.52) | copy-start | bytes 49156
  42.9 6.6 %copy-start.4 = (f32[4,128,32]{2,1,0:T(8,128)S(1)}, f32[4,128,32]{2,1,0:T(8,128)}, u32[]{:S(2)}) copy-start(f32[4,128,32]{2,1,0:T(8,128)} %exp.40) | copy-start | bytes 196612
  59.9 3.6 %copy-start.7 = (f32[128,32]{1,0:T(8,128)S(1)}, f32[128,32]{1,0:T(8,128)}, u32[]{:S(2)}) copy-start(f32[128,32]{1,0:T(8,128)} %exp.39) | copy-start | bytes 49156
  65.4 2.5 %copy-start.29 = (f32[32]{0:T(128)}, f32[32]{0:T(128)S(1)}, u32[]{:S(2)}) copy-start(f32[32]{0:T(128)S(1)} %get-tuple-element.48) | copy-start | bytes 388
  65.4 8.1 %copy-start.25 = (f32[32]{0:T(128)}, f32[32]{0:T(128)S(1)}, u32[]{:S(2)}) copy-start(f32[32]{0:T(128)S(1)} %get-tuple-element.50) | copy-start | bytes 388
  65.4 8.4 %copy-start.27 = (f32[32]{0:T(128)}, f32[32]{0:T(128)S(1)}, u32[]{:S(2)}) copy-start(f32[32]{0:T(128)S(1)} %get-tuple-element.49) | copy-start | bytes 388
  65.4 2.5 %copy-start.15 = (f32[128,128]{0,1:T(8,128)S(1)}, f32[128,128]{0,1:T(8,128)}, u32[]{:S(2)}) copy-start(f32[128,128]{0,1:T(8,128)} %fusion.71) | copy-start | bytes 196612
  67.9 1.6 %copy-start.1 = (f32[3,32,64,128]{3,2,1,0:T(8,128)}, f32[3,32,64,128]{3,2,1,0:T(8,128)S(1)}, u32[]{:S(2)}) copy-start(f32[3,32,64,128]{3,2,1,0:T(8,128)S(1)} %fusion.3) | copy-start | bytes 9437188
  67.9 1.6 %copy-start.12 = (f32[128,128]{0,1:T(8,128)S(1)}, f32[128,128]{0,1:T(8,128)}, u32[]{:S(2)}) copy-start(f32[128,128]{0,1:T(8,128)} %fusion.74) | copy-start | bytes 196612
  67.9 1.6 %copy-start.17 = (f32[32,128]{1,0:T(8,128)S(1)}, f32[32,128]{1,0:T(8,128)}, u32[]{:S(2)}) copy-start(f32[32,128]{1,0:T(8,128)} %copy.95) | copy-start | bytes 49156
  67.9 1.6 %copy-start.18 = (pred[128,128]{0,1:T(8,128)(4,1)S(1)}, pred[128,128]{0,1:T(8,128)(4,1)}, u32[]{:S(2)}) copy-start(pred[128,128]{0,1:T(8,128)(4,1)} %iota_compare_fusion) | copy-start | bytes 49156
  67.9 1.6 %copy-start.33 = (f32[32,128]{1,0:T(8,128)S(1)}, f32[32,128]{1,0:T(8,128)}, u32[]{:S(2)}) copy-start(f32[32,128]{1,0:T(8,128)} %get-tuple-element.51) | copy-start | bytes 49156
  69.5 1.4 %copy-start.8 = (f32[128,32]{0,1:T(8,128)S(1)}, f32[128,32]{0,1:T(8,128)}, u32[]{:S(2)}) copy-start(f32[128,32]{0,1:T(8,128)} %copy.105) | copy-start | bytes 49156
  69.5 1.4 %copy-start.9 = (f32[128,32]{0,1:T(8,128)S(1)}, f32[128,32]{0,1:T(8,128)}, u32[]{:S(2)}) copy-start(f32[128,32]{0,1:T(8,128)} %copy.106) | copy-start | bytes 49156
  69.5 1.4 %copy-start.10 = (f32[128,32]{0,1:T(8,128)S(1)}, f32[128,32]{0,1:T(8,128)}, u32[]{:S(2)}) copy-start(f32[128,32]{0,1:T(8,128)} %copy.107) | copy-start | bytes 49156
  73.7 1.4 %copy-start.5 = (bf16[128,2048]{0,1:T(8,128)(2,1)S(1)}, bf16[128,2048]{0,1:T(8,128)(2,1)}, u32[]{:S(2)}) copy-start(bf16[128,2048]{0,1:T(8,128)(2,1)} %copy.92) | copy-start | bytes 1572868
  73.8 1.4 %copy-start.14 = (f32[128,128]{0,1:T(8,128)S(1)}, f32[128,128]{0,1:T(8,128)}, u32[]{:S(2)}) copy-start(f32[128,128]{0,1:T(8,128)} %fusion.76) | copy-start | bytes 196612
  74.1 1.5 %copy-start.21 = (f32[128]{0:T(128)S(1)}, f32[128]{0:T(128)}, u32[]{:S(2)}) copy-start(f32[128]{0:T(128)} %copy-done.20) | copy-start | bytes 1540
  74.1 1.5 %copy-start.24 = (f32[1,128]{1,0:T(1,128)S(1)}, f32[1,128]{1,0:T(1,128)}, u32[]{:S(2)}) copy-start(f32[1,128]{1,0:T(1,128)} %copy-done.23) | copy-start | bytes 1540
  76.2 2.9 %collective-permute-start.3 = (f32[1152,128]{1,0:T(8,128)S(1)}, f32[1152,128]{1,0:T(8,128)S(1)}, u32[]{:S(2)}, u32[]{:S(2)}) collective-permute-start(f32[1152,128]{1,0:T(8,128)S(1)} %constant_dynamic-slice_fusion.6), channel_id=1, source_target_pairs={{0,1},{1,0},{2,3},{3,2},{4,5},{5,4},{6,7},{7,6},{8,9},{9,8},{10,11... | collective-permute-start | bytes 1769480 | tf_op jit(solution)/shard_map/ppermute | solution.py:26
  79.2 7.2 %collective-permute-start.4 = (f32[288,128]{1,0:T(8,128)S(1)}, f32[288,128]{1,0:T(8,128)S(1)}, u32[]{:S(2)}, u32[]{:S(2)}) collective-permute-start(f32[288,128]{1,0:T(8,128)S(1)} %get-tuple-element.27), channel_id=1, source_target_pairs={{0,8},{8,0},{16,24},{24,16},{1,9},{9,1},{17,25},{25,17},{2,10},{10... | collective-permute-start | bytes 442376 | tf_op jit(solution)/shard_map/ppermute | solution.py:26
  82.3 9.9 %collective-permute-start.5 = (f32[288,128]{1,0:T(8,128)S(1)}, f32[288,128]{1,0:T(8,128)S(1)}, u32[]{:S(2)}, u32[]{:S(2)}) collective-permute-start(f32[288,128]{1,0:T(8,128)S(1)} %get-tuple-element.29), channel_id=1, source_target_pairs={{0,16},{8,24},{16,0},{24,8},{1,17},{9,25},{17,1},{25,9},{2,18},{10... | collective-permute-start | bytes 442376 | tf_op jit(solution)/shard_map/ppermute | solution.py:26
  86.4 6.6 %collective-permute-start.6 = (f32[288,128]{1,0:T(8,128)S(1)}, f32[288,128]{1,0:T(8,128)S(1)}, u32[]{:S(2)}, u32[]{:S(2)}) collective-permute-start(f32[288,128]{1,0:T(8,128)S(1)} %get-tuple-element.28), channel_id=1, source_target_pairs={{0,24},{8,16},{16,8},{24,0},{1,25},{9,17},{17,9},{25,1},{2,26},{10... | collective-permute-start | bytes 442376 | tf_op jit(solution)/shard_map/ppermute | solution.py:26
  93.1 3.6 %collective-permute-start.7 = (f32[72,128]{1,0:T(8,128)S(1)}, f32[72,128]{1,0:T(8,128)S(1)}, u32[]{:S(2)}, u32[]{:S(2)}) collective-permute-start(f32[72,128]{1,0:T(8,128)S(1)} %get-tuple-element.39), channel_id=1, source_target_pairs={{0,2},{1,3},{2,0},{3,1},{4,6},{5,7},{6,4},{7,5},{8,10},{9,11},{10,... | collective-permute-start | bytes 110600 | tf_op jit(solution)/shard_map/ppermute | solution.py:26
  93.4 3.7 %collective-permute-start.8 = (f32[72,128]{1,0:T(8,128)S(1)}, f32[72,128]{1,0:T(8,128)S(1)}, u32[]{:S(2)}, u32[]{:S(2)}) collective-permute-start(f32[72,128]{1,0:T(8,128)S(1)} %get-tuple-element.41), channel_id=1, source_target_pairs={{0,4},{1,5},{2,6},{3,7},{4,0},{5,1},{6,2},{7,3},{8,12},{9,13},{10,... | collective-permute-start | bytes 110600 | tf_op jit(solution)/shard_map/ppermute | solution.py:26
  93.7 4.7 %collective-permute-start.9 = (f32[72,128]{1,0:T(8,128)S(1)}, f32[72,128]{1,0:T(8,128)S(1)}, u32[]{:S(2)}, u32[]{:S(2)}) collective-permute-start(f32[72,128]{1,0:T(8,128)S(1)} %get-tuple-element.40), channel_id=1, source_target_pairs={{0,6},{1,7},{2,4},{3,5},{4,2},{5,3},{6,0},{7,1},{8,14},{9,15},{10,... | collective-permute-start | bytes 110600 | tf_op jit(solution)/shard_map/ppermute | solution.py:26
  98.5 3.6 %collective-permute-start.10 = (f32[72,128]{1,0:T(8,128)S(1)}, f32[72,128]{1,0:T(8,128)S(1)}, u32[]{:S(2)}, u32[]{:S(2)}) collective-permute-start(f32[72,128]{1,0:T(8,128)S(1)} %add_add_fusion.1), channel_id=1, source_target_pairs={{0,2},{1,3},{2,0},{3,1},{4,6},{5,7},{6,4},{7,5},{8,10},{9,11},{10,... | collective-permute-start | bytes 110600 | tf_op jit(solution)/shard_map/ppermute | solution.py:26
  98.6 4.4 %collective-permute-start.11 = (f32[72,128]{1,0:T(8,128)S(1)}, f32[72,128]{1,0:T(8,128)S(1)}, u32[]{:S(2)}, u32[]{:S(2)}) collective-permute-start(f32[72,128]{1,0:T(8,128)S(1)} %add_add_fusion.1), channel_id=1, source_target_pairs={{0,4},{1,5},{2,6},{3,7},{4,0},{5,1},{6,2},{7,3},{8,12},{9,13},{10,... | collective-permute-start | bytes 110600 | tf_op jit(solution)/shard_map/ppermute | solution.py:26
  101.7 4.7 %collective-permute-start.12 = (f32[72,128]{1,0:T(8,128)S(1)}, f32[72,128]{1,0:T(8,128)S(1)}, u32[]{:S(2)}, u32[]{:S(2)}) collective-permute-start(f32[72,128]{1,0:T(8,128)S(1)} %add_add_fusion.1), channel_id=1, source_target_pairs={{0,6},{1,7},{2,4},{3,5},{4,2},{5,3},{6,0},{7,1},{8,14},{9,15},{10,... | collective-permute-start | bytes 110600 | tf_op jit(solution)/shard_map/ppermute | solution.py:26
  106.5 13.2 %copy-start.6 = (bf16[128,2048]{0,1:T(8,128)(2,1)S(1)}, bf16[128,2048]{0,1:T(8,128)(2,1)}, u32[]{:S(2)}) copy-start(bf16[128,2048]{0,1:T(8,128)(2,1)} %copy.92) | copy-start | bytes 1572868
  106.5 13.2 %copy-start.13 = (f32[128,128]{0,1:T(8,128)S(1)}, f32[128,128]{0,1:T(8,128)}, u32[]{:S(2)}) copy-start(f32[128,128]{0,1:T(8,128)} %fusion.74) | copy-start | bytes 196612
  106.5 13.2 %copy-start.19 = (pred[128,128]{0,1:T(8,128)(4,1)S(1)}, pred[128,128]{0,1:T(8,128)(4,1)}, u32[]{:S(2)}) copy-start(pred[128,128]{0,1:T(8,128)(4,1)} %iota_compare_fusion) | copy-start | bytes 49156
  106.5 13.2 %copy-start.34 = (f32[32,128]{1,0:T(8,128)S(1)}, f32[32,128]{1,0:T(8,128)}, u32[]{:S(2)}) copy-start(f32[32,128]{1,0:T(8,128)} %get-tuple-element.51) | copy-start | bytes 49156
  106.5 4.1 %collective-permute-start.13 = (f32[288,128]{1,0:T(8,128)S(1)}, f32[288,128]{1,0:T(8,128)S(1)}, u32[]{:S(2)}, u32[]{:S(2)}) collective-permute-start(f32[288,128]{1,0:T(8,128)S(1)} %get-tuple-element.34), channel_id=1, source_target_pairs={{0,8},{8,0},{16,24},{24,16},{1,9},{9,1},{17,25},{25,17},{2,10},{10... | collective-permute-start | bytes 442376 | tf_op jit(solution)/shard_map/ppermute | solution.py:26
  107.8 4.0 %collective-permute-start.14 = (f32[288,128]{1,0:T(8,128)S(1)}, f32[288,128]{1,0:T(8,128)S(1)}, u32[]{:S(2)}, u32[]{:S(2)}) collective-permute-start(f32[288,128]{1,0:T(8,128)S(1)} %get-tuple-element.34), channel_id=1, source_target_pairs={{0,16},{8,24},{16,0},{24,8},{1,17},{9,25},{17,1},{25,9},{2,18},{10... | collective-permute-start | bytes 442376 | tf_op jit(solution)/shard_map/ppermute | solution.py:26
  108.2 5.1 %collective-permute-start.15 = (f32[288,128]{1,0:T(8,128)S(1)}, f32[288,128]{1,0:T(8,128)S(1)}, u32[]{:S(2)}, u32[]{:S(2)}) collective-permute-start(f32[288,128]{1,0:T(8,128)S(1)} %get-tuple-element.34), channel_id=1, source_target_pairs={{0,24},{8,16},{16,8},{24,0},{1,25},{9,17},{17,9},{25,1},{2,26},{10... | collective-permute-start | bytes 442376 | tf_op jit(solution)/shard_map/ppermute | solution.py:26
  113.6 10.9 %collective-permute-start.16 = (f32[1152,128]{1,0:T(8,128)S(1)}, f32[1152,128]{1,0:T(8,128)S(1)}, u32[]{:S(2)}, u32[]{:S(2)}) collective-permute-start(f32[1152,128]{1,0:T(8,128)S(1)} %get-tuple-element.21), channel_id=1, source_target_pairs={{0,1},{1,0},{2,3},{3,2},{4,5},{5,4},{6,7},{7,6},{8,9},{9,8},{10,11... | collective-permute-start | bytes 1769480 | tf_op jit(solution)/shard_map/ppermute | solution.py:26
  (5 other events, 5.5 us)

commit v19 on v18

--- a/solution.py
+++ b/solution.py
@@ -29,8 +29,9 @@
 def bit_groups():
     tm_bits, series_bits = axis_bits("tm"), axis_bits("series")
     groups = [("series", series_bits[:1])] if series_bits else []
-    for axis, bits in (("tm", tm_bits), ("series", series_bits[1:])):
-        groups += [(axis, bits[i : i + 2]) for i in range(0, len(bits), 2)]
+    groups += [("tm", [b]) for b in tm_bits]
+    rest = series_bits[1:]
+    groups += [("series", rest[i : i + 2]) for i in range(0, len(rest), 2)]
     return groups
 
 

time: 127 us -> 135 us (1.063)
  waiting for transfers between devices: 21.3 us -> 28.5 us
    ppermute x14 -> x12, waiting for transfers between devices: 18.5 us -> 25.7 us  [exchange(): return lax.ppermute(value, axis, pairs)]
    unnamed x73 -> x72, local copies, waits for them, and re-layouts: 5.53 us -> 4.14 us
    ppermute x14 -> x12, starting transfers between devices: 24.5 us -> 24.8 us  [exchange(): return lax.ppermute(value, axis, pairs)]
  transfers between devices with their start and end apart: 18 -> 16, of which waited for: 11 -> 10; matrix products, arithmetic and copies ran while one was open for 42% -> 40% of each run, Pallas kernels for 0% -> 0%
where the time goes in v19:
time: 135 us; the launch traced here: 134 us
  starting transfers between devices  35.8 us (27%)
  waiting for transfers between devices  28.5 us (21%)
  local copies, waits for them, and re-layouts  25.9 us (19%)
  matrix products  24.8 us (18%)
  other arithmetic  17.6 us (13%)
  between operations  1.35 us (1%)
    ppermute x12, waiting for transfers between devices, exchange(): return lax.ppermute(value, axis, pairs)  25.7 us
    ppermute x12, starting transfers between devices, exchange(): return lax.ppermute(value, axis, pairs)  24.8 us
    all_to_all x1, starting transfers between devices, on_device(): lax.all_to_all(outgoing, ('tm', 'series'), split_axis=0, concat_axis=1, t...  7.1 us
    mul x4, local copies, waits for them, and re-layouts, on_device(): later_weighted = (later * head_all[k][:, :, None]).astype(half)  4.36 us
    unnamed x72, local copies, waits for them, and re-layouts  4.14 us
    slice x2, local copies, waits for them, and re-layouts, on_device(): x_heads = projected[:, :inner_width].reshape(tok_rows, head_count, head_dim)  3.92 us
    convert_element_type x1, local copies, waits for them, and re-layouts, on_device(): xw_all = (x_all[:earlier] * tail_all[:earlier, :, :, None]).astype(half)  3.56 us
    all_to_all x1, waiting for transfers between devices, on_device(): lax.all_to_all(outgoing, ('tm', 'series'), split_axis=0, concat_axis=1, t...  2.82 us
  transfers between devices with their start and end apart: 16, of which 10 were waited for; matrix products, arithmetic and copies ran while one was open for 40% of the time, Pallas kernels for 0%

profile of v19, /device:TPU:1, one launch (start us, length us, event | category | flops | bytes accessed | tf_op | source)
XLA Modules:
  0.0 133.9 jit_solution(131820587587662737)
XLA Ops:
  2.1 1.2 gather_fusion
  4.0 7.1 %all-to-all-start = ((f32[32,1,16]{2,1,0:T(1,128)}), f32[32,1,16]{2,1,0:T(1,128)S(1)}, u32[]{:S(2)}, u32[]{:S(2)}) async-start(f32[32,1,16]{2,1,0:T(1,128)} %bitcast), calls=%async_computation | async-start | bytes 32768 | tf_op jit(solution)/shard_map/all_to_all | solution.py:93
  12.5 1.3 copy.74
  13.8 1.0 convert_bitcast_fusion
  15.0 2.8 %all-to-all-done = f32[32,1,16]{2,1,0:T(1,128)S(1)} async-done(((f32[32,1,16]{2,1,0:T(1,128)}), f32[32,1,16]{2,1,0:T(1,128)S(1)}, u32[]{:S(2)}, u32[]{:S(2)}) %all-to-all-start) | async-done | bytes 2080 | tf_op jit(solution)/shard_map/all_to_all | solution.py:93
  19.1 1.5 %convert_reduce_fusion = f32[4096]{0:T(1024)S(1)} fusion(f32[4096]{0:T(1024)S(1)} %get-tuple-element.43, f32[4096]{0:T(1024)S(1)} %convert_element_type.121, f32[512]{0:T(512)S(1)} %le.22), kind=kLoop, calls=%fused_computation.1 | loop fusion | flops 10481664 | bytes 51200 | tf_op jit(solution)/shard_map/reduce_sum | solution.py:99
  20.5 1.3 collective-permute-start
  21.8 1.3 collective-permute-start.1
  23.1 1.3 collective-permute-start.2
  25.2 1.3 fusion
  26.6 1.1 compare_select_fusion
  29.7 1.6 %convolution_convert_fusion = bf16[512,2304]{1,0:T(8,128)(2,1)S(1)} fusion(bf16[128,2304]{1,0:T(8,128)(2,1)S(1)} %copy-done, f32[128]{0:T(128)S(1)} %add_multiply_fusion, f32[512]{0:T(512)S(1)} %bitcast.234), kind=kOutput, calls=%fused_computation.4 | convolution fusion | flops 303300608 | bytes 2951680 | tf_op jit(solution)/shard_map/dot_general | solution.py:130
  31.3 1.0 compare_select_fusion.1
  32.3 1.4 %convolution_convert_fusion.1 = bf16[128,2304]{1,0:T(8,128)(2,1)} fusion(bf16[128,2304]{1,0:T(8,128)(2,1)S(1)} %copy-done, f32[128]{0:T(128)S(1)} %add_multiply_fusion, f32[1,128]{1,0:T(1,128)S(1)} %constant_dynamic-slice_fusion.6), kind=kOutput, calls=%fused_computation.7 | convolution fusion | flops 75825152 | bytes 1180672 | tf_op jit(solution)/shard_map/dot_general | solution.py:120
  34.5 1.0 reduce_window_sum.39
  36.8 1.6 %fusion.80 = f32[128,128]{0,1:T(8,128)} fusion(bf16[128,2304]{1,0:T(8,128)(2,1)} %convolution_convert_fusion.1), kind=kOutput, calls=%fused_computation.153 | convolution fusion | flops 4194304 | bytes 131072 | tf_op jit(solution)/shard_map/dot_general | solution.py:179
  38.3 1.9 %slice.149 = bf16[128,2048]{1,0:T(8,128)(2,1)} slice(bf16[128,2304]{1,0:T(8,128)(2,1)} %convolution_convert_fusion.1), slice={[0:128], [0:2048]} | slice | bytes 1048576 | tf_op jit(solution)/shard_map/slice | solution.py:121
  40.9 2.0 %copy.75 = bf16[128,2048]{0,1:T(8,128)(2,1)} copy(bf16[128,2048]{1,0:T(8,128)(2,1)} %slice.149) | data formatting | bytes 1048576 | tf_op jit(solution)/shard_map/slice | solution.py:121
  42.9 2.8 %fusion.2 = bf16[128,128]{0,1:T(8,128)(2,1)S(1)} fusion(bf16[128,32,64]{0,2,1:T(8,128)(2,1)} %bitcast.214, bf16[128,32,64]{0,2,1:T(8,128)(2,1)S(1)} %bitcast.202, f32[32,128]{1,0:T(8,128)} %get-tuple-element.48, f32[32,128]{1,0:T(8,128)} %copy.78, pred[128,128]{0,1:T(8,128)(4,1)} %iota_compare_fusion), kind=kOutput, calls=%fused_computation.10 | convolution fusion | flops 70238208 | bytes 1130496 | tf_op jit(solution)/shard_map/thp,shp->hts/dot_general | solution.py:196
  45.7 1.6 %fusion.82 = f32[128,128]{0,1:T(8,128)} fusion(bf16[128,2304]{1,0:T(8,128)(2,1)} %convolution_convert_fusion.1, bf16[128,128]{0,1:T(8,128)(2,1)S(1)} %fusion.2), kind=kOutput, calls=%fused_computation.155 | convolution fusion | flops 4194304 | bytes 131072 | tf_op jit(solution)/shard_map/dot_general | solution.py:198
  47.3 1.6 %fusion.77 = f32[128,128]{0,1:T(8,128)} fusion(bf16[128,2304]{1,0:T(8,128)(2,1)} %convolution_convert_fusion.1, bf16[128,128]{0,1:T(8,128)(2,1)S(1)} %fusion.2), kind=kOutput, calls=%fused_computation.150 | convolution fusion | flops 4194304 | bytes 131072 | tf_op jit(solution)/shard_map/dot_general | solution.py:200
  50.2 1.5 %copy.88 = f32[128,32]{0,1:T(8,128)} copy(f32[128,32]{1,0:T(8,128)} %get-tuple-element.29) | data formatting | bytes 32768 | tf_op jit(solution)/shard_map/mul | solution.py:168
  51.7 1.5 %copy.89 = f32[128,32]{0,1:T(8,128)} copy(f32[128,32]{1,0:T(8,128)} %get-tuple-element.28) | data formatting | bytes 32768 | tf_op jit(solution)/shard_map/mul | solution.py:168
  54.5 1.7 %slice_multiply_fusion = f32[3,128,32]{2,1,0:T(8,128)} fusion(f32[4,128,32]{2,1,0:T(8,128)} %bitcast.211, f32[4,128,32]{2,1,0:T(8,128)} %copy-done.2, f32[3,32]{1,0:T(4,128)S(1)} %bitcast.232), kind=kLoop, calls=%fused_computation.98 | loop fusion | flops 24576 | bytes 147840 | tf_op jit(solution)/shard_map/mul | solution.py:139
  56.2 1.6 %copy.84 = f32[3,128,32]{1,2,0:T(8,128)} copy(f32[3,128,32]{2,1,0:T(8,128)} %slice_multiply_fusion) | data formatting | bytes 98304 | tf_op jit(solution)/shard_map/slice | solution.py:142
  57.9 2.1 %slice_convert_fusion = f32[3,128,2048]{2,1,0:T(8,128)} fusion(bf16[4,128,2304]{2,1,0:T(8,128)(2,1)S(1)} %bitcast.197), kind=kLoop, calls=%fused_computation.14 | loop fusion | flops 786432 | bytes 4718592 | tf_op jit(solution)/shard_map/convert_element_type | solution.py:142
  59.9 3.6 %copy.82 = f32[3,128,2048]{1,2,0:T(8,128)} copy(f32[3,128,2048]{2,1,0:T(8,128)} %slice_convert_fusion) | data formatting | bytes 6291456 | tf_op jit(solution)/shard_map/convert_element_type | solution.py:142
  65.4 2.5 %fusion.3 = f32[3,32,64,128]{3,2,1,0:T(8,128)S(1)} fusion(f32[3,128,32,64]{1,3,2,0:T(8,128)} %bitcast.196, f32[3,128,32]{1,2,0:T(8,128)} %copy.84, bf16[4,128,2304]{2,1,0:T(8,128)(2,1)S(1)} %bitcast.198), kind=kOutput, calls=%fused_computation.13 | convolution fusion | flops 202899456 | bytes 6438912 | tf_op jit(solution)/shard_map/bthp,btn->bhpn/dot_general | solution.py:143
  69.5 1.3 convolution_bitcast_fusion
  70.9 2.2 %fusion.20 = (bf16[128,2048]{0,1:T(8,128)(2,1)S(1)}, bf16[128,2048]{0,1:T(8,128)(2,1)S(1)}, bf16[128,2048]{0,1:T(8,128)(2,1)S(1)}) fusion(f32[128,2048]{0,1:T(8,128)} %collective-permute-done.2, f32[128,2048]{0,1:T(8,128)} %collective-permute-done.1, f32[128,32]{0,1:T(8,128)S(1)} %copy-done.9, pred[]{:T(512)S(6)} %eq.19, f32[128,32]{0,1:T(8,128)S(1)} %copy-done.8, ...), kind=kLoop, calls=%fused_computation.51 | loop fusion | flops 2359296 | bytes 4767746 | tf_op jit(solution)/shard_map/convert_element_type | solution.py:168
  74.1 1.1 fusion.12
  76.2 1.3 collective-permute-start.3
  77.4 1.6 %collective-permute-done.3 = f32[1152,128]{1,0:T(8,128)S(1)} collective-permute-done((f32[1152,128]{1,0:T(8,128)S(1)}, f32[1152,128]{1,0:T(8,128)S(1)}, u32[]{:S(2)}, u32[]{:S(2)}) %collective-permute-start.3) | collective-permute-done | bytes 589856 | tf_op jit(solution)/shard_map/ppermute | solution.py:26
  79.2 3.1 %collective-permute-start.4 = (f32[576,128]{1,0:T(8,128)S(1)}, f32[576,128]{1,0:T(8,128)S(1)}, u32[]{:S(2)}, u32[]{:S(2)}) collective-permute-start(f32[576,128]{1,0:T(8,128)S(1)} %constant_dynamic-slice_fusion.4), channel_id=1, source_target_pairs={{0,8},{8,0},{16,24},{24,16},{1,9},{9,1},{17,25},{25,17},{2,10},{10... | collective-permute-start | bytes 884744 | tf_op jit(solution)/shard_map/ppermute | solution.py:26
  82.3 7.1 %collective-permute-done.4 = f32[576,128]{1,0:T(8,128)S(1)} collective-permute-done((f32[576,128]{1,0:T(8,128)S(1)}, f32[576,128]{1,0:T(8,128)S(1)}, u32[]{:S(2)}, u32[]{:S(2)}) %collective-permute-start.4) | collective-permute-done | bytes 294944 | tf_op jit(solution)/shard_map/ppermute | solution.py:26
  89.4 4.0 %collective-permute-start.5 = (f32[288,128]{1,0:T(8,128)S(1)}, f32[288,128]{1,0:T(8,128)S(1)}, u32[]{:S(2)}, u32[]{:S(2)}) collective-permute-start(f32[288,128]{1,0:T(8,128)S(1)} %constant_dynamic-slice_fusion.3), channel_id=1, source_target_pairs={{0,16},{8,24},{16,0},{24,8},{1,17},{9,25},{17,1},{25,9},{2,18},{10... | collective-permute-start | bytes 442376 | tf_op jit(solution)/shard_map/ppermute | solution.py:26
  93.4 3.0 %collective-permute-done.5 = f32[288,128]{1,0:T(8,128)S(1)} collective-permute-done((f32[288,128]{1,0:T(8,128)S(1)}, f32[288,128]{1,0:T(8,128)S(1)}, u32[]{:S(2)}, u32[]{:S(2)}) %collective-permute-start.5) | collective-permute-done | bytes 147488 | tf_op jit(solution)/shard_map/ppermute | solution.py:26
  97.1 2.9 %collective-permute-start.8 = (f32[72,128]{1,0:T(8,128)S(1)}, f32[72,128]{1,0:T(8,128)S(1)}, u32[]{:S(2)}, u32[]{:S(2)}) collective-permute-start(f32[72,128]{1,0:T(8,128)S(1)} %get-tuple-element.37), channel_id=1, source_target_pairs={{0,6},{1,7},{2,4},{3,5},{4,2},{5,3},{6,0},{7,1},{8,14},{9,15},{10,... | collective-permute-start | bytes 110600 | tf_op jit(solution)/shard_map/ppermute | solution.py:26
  100.4 1.7 %collective-permute-done.8 = f32[72,128]{1,0:T(8,128)S(1)} collective-permute-done((f32[72,128]{1,0:T(8,128)S(1)}, f32[72,128]{1,0:T(8,128)S(1)}, u32[]{:S(2)}, u32[]{:S(2)}) %collective-permute-start.8) | collective-permute-done | bytes 36896 | tf_op jit(solution)/shard_map/ppermute | solution.py:26
  102.2 2.9 %collective-permute-start.10 = (f32[72,128]{1,0:T(8,128)S(1)}, f32[72,128]{1,0:T(8,128)S(1)}, u32[]{:S(2)}, u32[]{:S(2)}) collective-permute-start(f32[72,128]{1,0:T(8,128)S(1)} %add_add_fusion), channel_id=1, source_target_pairs={{0,4},{1,5},{2,6},{3,7},{4,0},{5,1},{6,2},{7,3},{8,12},{9,13},{10,... | collective-permute-start | bytes 110600 | tf_op jit(solution)/shard_map/ppermute | solution.py:26
  106.4 3.6 %collective-permute-done.11 = f32[72,128]{1,0:T(8,128)S(1)} collective-permute-done((f32[72,128]{1,0:T(8,128)S(1)}, f32[72,128]{1,0:T(8,128)S(1)}, u32[]{:S(2)}, u32[]{:S(2)}) %collective-permute-start.11) | collective-permute-done | bytes 36896 | tf_op jit(solution)/shard_map/ppermute | solution.py:26
  111.1 3.4 %collective-permute-done.12 = f32[288,128]{1,0:T(8,128)S(1)} collective-permute-done((f32[288,128]{1,0:T(8,128)S(1)}, f32[288,128]{1,0:T(8,128)S(1)}, u32[]{:S(2)}, u32[]{:S(2)}) %collective-permute-start.12) | collective-permute-done | bytes 147488 | tf_op jit(solution)/shard_map/ppermute | solution.py:26
  114.6 1.4 %collective-permute-start.13 = (f32[576,128]{1,0:T(8,128)S(1)}, f32[576,128]{1,0:T(8,128)S(1)}, u32[]{:S(2)}, u32[]{:S(2)}) collective-permute-start(f32[576,128]{1,0:T(8,128)S(1)} %get-tuple-element.23), channel_id=1, source_target_pairs={{0,8},{8,0},{16,24},{24,16},{1,9},{9,1},{17,25},{25,17},{2,10},{10... | collective-permute-start | bytes 884744 | tf_op jit(solution)/shard_map/ppermute | solution.py:26
  116.0 4.3 %collective-permute-done.13 = f32[576,128]{1,0:T(8,128)S(1)} collective-permute-done((f32[576,128]{1,0:T(8,128)S(1)}, f32[576,128]{1,0:T(8,128)S(1)}, u32[]{:S(2)}, u32[]{:S(2)}) %collective-permute-start.13) | collective-permute-done | bytes 294944 | tf_op jit(solution)/shard_map/ppermute | solution.py:26
  120.4 6.9 %collective-permute-start.14 = (f32[1152,128]{1,0:T(8,128)S(1)}, f32[1152,128]{1,0:T(8,128)S(1)}, u32[]{:S(2)}, u32[]{:S(2)}) collective-permute-start(f32[1152,128]{1,0:T(8,128)S(1)} %get-tuple-element.19), channel_id=1, source_target_pairs={{0,1},{1,0},{2,3},{3,2},{4,5},{5,4},{6,7},{7,6},{8,9},{9,8},{10,11... | collective-permute-start | bytes 1769480 | tf_op jit(solution)/shard_map/ppermute | solution.py:26
  127.4 1.3 convolution_bitcast_fusion.1
  128.7 2.4 %fusion.10 = bf16[128,32,64]{0,2,1:T(8,128)(2,1)S(1)} fusion(f32[128,32,64]{0,2,1:T(8,128)S(1)} %convolution_bitcast_fusion.1, f32[3,32,64,128]{3,2,1,0:T(8,128)} %copy-done.1, f32[128,32]{0,1:T(8,128)S(1)} %copy.85, f32[32]{0:T(128)S(1)} %copy-done.30, f32[32]{0:T(128)S(1)} %copy-done.28, f32[32]{0:T(128)S(1)} %copy-done.26, pred[]{:T(512)S(6)} %gt.24, ...), kind=kOutput, calls=%fused_computation.34 | convolution fusion | flops 70254592 | bytes 4768131 | tf_op jit(solution)/shard_map/tn,hpn->thp/dot_general | solution.py:186
  132.8 1.1 fusion.13
  (149 shorter events, 24.0 us)
Async XLA Ops:
  0.6 29.0 %copy-start = (bf16[128,2304]{1,0:T(8,128)(2,1)S(1)}, bf16[128,2304]{1,0:T(8,128)(2,1)}, u32[]{:S(2)}) copy-start(bf16[128,2304]{1,0:T(8,128)(2,1)} %param.11) | copy-start | bytes 1769476
  0.6 14.2 %copy-start.16 = (s32[4096]{0:T(1024)S(1)}, s32[4096]{0:T(1024)}, u32[]{:S(2)}) copy-start(s32[4096]{0:T(1024)} %param.10) | copy-start | bytes 49156
  4.0 13.8 %all-to-all-start = ((f32[32,1,16]{2,1,0:T(1,128)}), f32[32,1,16]{2,1,0:T(1,128)S(1)}, u32[]{:S(2)}, u32[]{:S(2)}) async-start(f32[32,1,16]{2,1,0:T(1,128)} %bitcast), calls=%async_computation | async-start | bytes 32768 | tf_op jit(solution)/shard_map/all_to_all | solution.py:93
  14.9 17.4 %copy-start.20 = (f32[128]{0:T(128)}, f32[128]{0:T(128)S(1)}, u32[]{:S(2)}) copy-start(f32[128]{0:T(128)S(1)} %add_multiply_fusion) | copy-start | bytes 1540
  20.5 50.3 %collective-permute-start = (f32[128,2048]{0,1:T(8,128)}, f32[128,2048]{0,1:T(8,128)}, u32[]{:S(2)}, u32[]{:S(2)}) collective-permute-start(f32[128,2048]{0,1:T(8,128)} %convert_bitcast_fusion), channel_id=1, source_target_pairs={{24,16},{8,0},{25,17},{9,1},{26,18},{10,2},{27,19},{11,3},{28,20},... | collective-permute-start | bytes 3145736 | tf_op jit(solution)/shard_map/ppermute | solution.py:157
  21.8 49.0 %collective-permute-start.1 = (f32[128,2048]{0,1:T(8,128)}, f32[128,2048]{0,1:T(8,128)}, u32[]{:S(2)}, u32[]{:S(2)}) collective-permute-start(f32[128,2048]{0,1:T(8,128)} %convert_bitcast_fusion), channel_id=1, source_target_pairs={{24,8},{16,0},{25,9},{17,1},{26,10},{18,2},{27,11},{19,3},{28,12},... | collective-permute-start | bytes 3145736 | tf_op jit(solution)/shard_map/ppermute | solution.py:158
  23.1 47.7 %collective-permute-start.2 = (f32[128,2048]{0,1:T(8,128)}, f32[128,2048]{0,1:T(8,128)}, u32[]{:S(2)}, u32[]{:S(2)}) collective-permute-start(f32[128,2048]{0,1:T(8,128)} %convert_bitcast_fusion), channel_id=1, source_target_pairs={{16,8},{24,0},{17,9},{25,1},{18,10},{26,2},{19,11},{27,3},{20,12},... | collective-permute-start | bytes 3145736 | tf_op jit(solution)/shard_map/ppermute | solution.py:159
  25.2 1.4 %copy-start.31 = (bf16[128,32]{0,1:T(8,128)(2,1)S(1)}, bf16[128,32]{0,1:T(8,128)(2,1)}, u32[]{:S(2)}) copy-start(bf16[128,32]{0,1:T(8,128)(2,1)} %param.12) | copy-start | bytes 24580
  25.2 1.4 %copy-start.32 = (f32[32]{0:T(128)S(1)}, f32[32]{0:T(128)}, u32[]{:S(2)}) copy-start(f32[32]{0:T(128)} %param.13) | copy-start | bytes 388
  25.2 3.4 %copy-start.22 = (f32[32]{0:T(128)S(1)}, f32[32]{0:T(128)}, u32[]{:S(2)}) copy-start(f32[32]{0:T(128)} %param.14) | copy-start | bytes 388
  31.3 2.4 %copy-start.23 = (f32[1,128]{1,0:T(1,128)}, f32[1,128]{1,0:T(1,128)S(1)}, u32[]{:S(2)}) copy-start(f32[1,128]{1,0:T(1,128)S(1)} %constant_dynamic-slice_fusion.6) | copy-start | bytes 1540
  32.3 1.4 %copy-start.11 = (f32[128,32]{0,1:T(8,128)}, f32[128,32]{0,1:T(8,128)S(1)}, u32[]{:S(2)}) copy-start(f32[128,32]{0,1:T(8,128)S(1)} %get-tuple-element.49) | copy-start | bytes 49156
  42.9 6.6 %copy-start.4 = (f32[4,128,32]{2,1,0:T(8,128)S(1)}, f32[4,128,32]{2,1,0:T(8,128)}, u32[]{:S(2)}) copy-start(f32[4,128,32]{2,1,0:T(8,128)} %exp.40) | copy-start | bytes 196612
  59.9 3.6 %copy-start.7 = (f32[128,32]{1,0:T(8,128)S(1)}, f32[128,32]{1,0:T(8,128)}, u32[]{:S(2)}) copy-start(f32[128,32]{1,0:T(8,128)} %exp.39) | copy-start | bytes 49156
  65.3 2.5 %copy-start.29 = (f32[32]{0:T(128)}, f32[32]{0:T(128)S(1)}, u32[]{:S(2)}) copy-start(f32[32]{0:T(128)S(1)} %get-tuple-element.45) | copy-start | bytes 388
  65.3 8.1 %copy-start.25 = (f32[32]{0:T(128)}, f32[32]{0:T(128)S(1)}, u32[]{:S(2)}) copy-start(f32[32]{0:T(128)S(1)} %get-tuple-element.47) | copy-start | bytes 388
  65.3 8.4 %copy-start.27 = (f32[32]{0:T(128)}, f32[32]{0:T(128)S(1)}, u32[]{:S(2)}) copy-start(f32[32]{0:T(128)S(1)} %get-tuple-element.46) | copy-start | bytes 388
  65.3 2.5 %copy-start.15 = (f32[128,128]{0,1:T(8,128)S(1)}, f32[128,128]{0,1:T(8,128)}, u32[]{:S(2)}) copy-start(f32[128,128]{0,1:T(8,128)} %fusion.77) | copy-start | bytes 196612
  67.8 1.7 %copy-start.1 = (f32[3,32,64,128]{3,2,1,0:T(8,128)}, f32[3,32,64,128]{3,2,1,0:T(8,128)S(1)}, u32[]{:S(2)}) copy-start(f32[3,32,64,128]{3,2,1,0:T(8,128)S(1)} %fusion.3) | copy-start | bytes 9437188
  67.9 1.6 %copy-start.12 = (f32[128,128]{0,1:T(8,128)S(1)}, f32[128,128]{0,1:T(8,128)}, u32[]{:S(2)}) copy-start(f32[128,128]{0,1:T(8,128)} %fusion.80) | copy-start | bytes 196612
  67.9 1.6 %copy-start.17 = (f32[32,128]{1,0:T(8,128)S(1)}, f32[32,128]{1,0:T(8,128)}, u32[]{:S(2)}) copy-start(f32[32,128]{1,0:T(8,128)} %copy.78) | copy-start | bytes 49156
  67.9 1.6 %copy-start.18 = (pred[128,128]{0,1:T(8,128)(4,1)S(1)}, pred[128,128]{0,1:T(8,128)(4,1)}, u32[]{:S(2)}) copy-start(pred[128,128]{0,1:T(8,128)(4,1)} %iota_compare_fusion) | copy-start | bytes 49156
  67.9 1.6 %copy-start.33 = (f32[32,128]{1,0:T(8,128)S(1)}, f32[32,128]{1,0:T(8,128)}, u32[]{:S(2)}) copy-start(f32[32,128]{1,0:T(8,128)} %get-tuple-element.48) | copy-start | bytes 49156
  69.5 1.4 %copy-start.8 = (f32[128,32]{0,1:T(8,128)S(1)}, f32[128,32]{0,1:T(8,128)}, u32[]{:S(2)}) copy-start(f32[128,32]{0,1:T(8,128)} %copy.88) | copy-start | bytes 49156
  69.5 1.4 %copy-start.9 = (f32[128,32]{0,1:T(8,128)S(1)}, f32[128,32]{0,1:T(8,128)}, u32[]{:S(2)}) copy-start(f32[128,32]{0,1:T(8,128)} %copy.89) | copy-start | bytes 49156
  69.5 1.4 %copy-start.10 = (f32[128,32]{0,1:T(8,128)S(1)}, f32[128,32]{0,1:T(8,128)}, u32[]{:S(2)}) copy-start(f32[128,32]{0,1:T(8,128)} %copy.90) | copy-start | bytes 49156
  73.7 1.4 %copy-start.5 = (bf16[128,2048]{0,1:T(8,128)(2,1)S(1)}, bf16[128,2048]{0,1:T(8,128)(2,1)}, u32[]{:S(2)}) copy-start(bf16[128,2048]{0,1:T(8,128)(2,1)} %copy.75) | copy-start | bytes 1572868
  73.7 1.4 %copy-start.14 = (f32[128,128]{0,1:T(8,128)S(1)}, f32[128,128]{0,1:T(8,128)}, u32[]{:S(2)}) copy-start(f32[128,128]{0,1:T(8,128)} %fusion.82) | copy-start | bytes 196612
  74.0 1.5 %copy-start.21 = (f32[128]{0:T(128)S(1)}, f32[128]{0:T(128)}, u32[]{:S(2)}) copy-start(f32[128]{0:T(128)} %copy-done.20) | copy-start | bytes 1540
  74.1 1.5 %copy-start.24 = (f32[1,128]{1,0:T(1,128)S(1)}, f32[1,128]{1,0:T(1,128)}, u32[]{:S(2)}) copy-start(f32[1,128]{1,0:T(1,128)} %copy-done.23) | copy-start | bytes 1540
  76.2 2.9 %collective-permute-start.3 = (f32[1152,128]{1,0:T(8,128)S(1)}, f32[1152,128]{1,0:T(8,128)S(1)}, u32[]{:S(2)}, u32[]{:S(2)}) collective-permute-start(f32[1152,128]{1,0:T(8,128)S(1)} %constant_dynamic-slice_fusion.5), channel_id=1, source_target_pairs={{0,1},{1,0},{2,3},{3,2},{4,5},{5,4},{6,7},{7,6},{8,9},{9,8},{10,11... | collective-permute-start | bytes 1769480 | tf_op jit(solution)/shard_map/ppermute | solution.py:26
  79.2 10.2 %collective-permute-start.4 = (f32[576,128]{1,0:T(8,128)S(1)}, f32[576,128]{1,0:T(8,128)S(1)}, u32[]{:S(2)}, u32[]{:S(2)}) collective-permute-start(f32[576,128]{1,0:T(8,128)S(1)} %constant_dynamic-slice_fusion.4), channel_id=1, source_target_pairs={{0,8},{8,0},{16,24},{24,16},{1,9},{9,1},{17,25},{25,17},{2,10},{10... | collective-permute-start | bytes 884744 | tf_op jit(solution)/shard_map/ppermute | solution.py:26
  89.4 6.9 %collective-permute-start.5 = (f32[288,128]{1,0:T(8,128)S(1)}, f32[288,128]{1,0:T(8,128)S(1)}, u32[]{:S(2)}, u32[]{:S(2)}) collective-permute-start(f32[288,128]{1,0:T(8,128)S(1)} %constant_dynamic-slice_fusion.3), channel_id=1, source_target_pairs={{0,16},{8,24},{16,0},{24,8},{1,17},{9,25},{17,1},{25,9},{2,18},{10... | collective-permute-start | bytes 442376 | tf_op jit(solution)/shard_map/ppermute | solution.py:26
  96.4 3.6 %collective-permute-start.6 = (f32[72,128]{1,0:T(8,128)S(1)}, f32[72,128]{1,0:T(8,128)S(1)}, u32[]{:S(2)}, u32[]{:S(2)}) collective-permute-start(f32[72,128]{1,0:T(8,128)S(1)} %get-tuple-element.36), channel_id=1, source_target_pairs={{0,2},{1,3},{2,0},{3,1},{4,6},{5,7},{6,4},{7,5},{8,10},{9,11},{10,... | collective-permute-start | bytes 110600 | tf_op jit(solution)/shard_map/ppermute | solution.py:26
  96.7 3.7 %collective-permute-start.7 = (f32[72,128]{1,0:T(8,128)S(1)}, f32[72,128]{1,0:T(8,128)S(1)}, u32[]{:S(2)}, u32[]{:S(2)}) collective-permute-start(f32[72,128]{1,0:T(8,128)S(1)} %get-tuple-element.38), channel_id=1, source_target_pairs={{0,4},{1,5},{2,6},{3,7},{4,0},{5,1},{6,2},{7,3},{8,12},{9,13},{10,... | collective-permute-start | bytes 110600 | tf_op jit(solution)/shard_map/ppermute | solution.py:26
  97.1 5.1 %collective-permute-start.8 = (f32[72,128]{1,0:T(8,128)S(1)}, f32[72,128]{1,0:T(8,128)S(1)}, u32[]{:S(2)}, u32[]{:S(2)}) collective-permute-start(f32[72,128]{1,0:T(8,128)S(1)} %get-tuple-element.37), channel_id=1, source_target_pairs={{0,6},{1,7},{2,4},{3,5},{4,2},{5,3},{6,0},{7,1},{8,14},{9,15},{10,... | collective-permute-start | bytes 110600 | tf_op jit(solution)/shard_map/ppermute | solution.py:26
  102.2 3.6 %collective-permute-start.9 = (f32[72,128]{1,0:T(8,128)S(1)}, f32[72,128]{1,0:T(8,128)S(1)}, u32[]{:S(2)}, u32[]{:S(2)}) collective-permute-start(f32[72,128]{1,0:T(8,128)S(1)} %add_add_fusion), channel_id=1, source_target_pairs={{0,2},{1,3},{2,0},{3,1},{4,6},{5,7},{6,4},{7,5},{8,10},{9,11},{10,... | collective-permute-start | bytes 110600 | tf_op jit(solution)/shard_map/ppermute | solution.py:26
  102.2 4.2 %collective-permute-start.10 = (f32[72,128]{1,0:T(8,128)S(1)}, f32[72,128]{1,0:T(8,128)S(1)}, u32[]{:S(2)}, u32[]{:S(2)}) collective-permute-start(f32[72,128]{1,0:T(8,128)S(1)} %add_add_fusion), channel_id=1, source_target_pairs={{0,4},{1,5},{2,6},{3,7},{4,0},{5,1},{6,2},{7,3},{8,12},{9,13},{10,... | collective-permute-start | bytes 110600 | tf_op jit(solution)/shard_map/ppermute | solution.py:26
  105.1 4.9 %collective-permute-start.11 = (f32[72,128]{1,0:T(8,128)S(1)}, f32[72,128]{1,0:T(8,128)S(1)}, u32[]{:S(2)}, u32[]{:S(2)}) collective-permute-start(f32[72,128]{1,0:T(8,128)S(1)} %add_add_fusion), channel_id=1, source_target_pairs={{0,6},{1,7},{2,4},{3,5},{4,2},{5,3},{6,0},{7,1},{8,14},{9,15},{10,... | collective-permute-start | bytes 110600 | tf_op jit(solution)/shard_map/ppermute | solution.py:26
  110.1 4.4 %collective-permute-start.12 = (f32[288,128]{1,0:T(8,128)S(1)}, f32[288,128]{1,0:T(8,128)S(1)}, u32[]{:S(2)}, u32[]{:S(2)}) collective-permute-start(f32[288,128]{1,0:T(8,128)S(1)} %get-tuple-element.30), channel_id=1, source_target_pairs={{0,16},{8,24},{16,0},{24,8},{1,17},{9,25},{17,1},{25,9},{2,18},{10... | collective-permute-start | bytes 442376 | tf_op jit(solution)/shard_map/ppermute | solution.py:26
  114.5 12.9 %copy-start.6 = (bf16[128,2048]{0,1:T(8,128)(2,1)S(1)}, bf16[128,2048]{0,1:T(8,128)(2,1)}, u32[]{:S(2)}) copy-start(bf16[128,2048]{0,1:T(8,128)(2,1)} %copy.75) | copy-start | bytes 1572868
  114.5 12.9 %copy-start.13 = (f32[128,128]{0,1:T(8,128)S(1)}, f32[128,128]{0,1:T(8,128)}, u32[]{:S(2)}) copy-start(f32[128,128]{0,1:T(8,128)} %fusion.80) | copy-start | bytes 196612
  114.5 12.9 %copy-start.19 = (pred[128,128]{0,1:T(8,128)(4,1)S(1)}, pred[128,128]{0,1:T(8,128)(4,1)}, u32[]{:S(2)}) copy-start(pred[128,128]{0,1:T(8,128)(4,1)} %iota_compare_fusion) | copy-start | bytes 49156
  114.5 12.9 %copy-start.34 = (f32[32,128]{1,0:T(8,128)S(1)}, f32[32,128]{1,0:T(8,128)}, u32[]{:S(2)}) copy-start(f32[32,128]{1,0:T(8,128)} %get-tuple-element.48) | copy-start | bytes 49156
  114.6 5.6 %collective-permute-start.13 = (f32[576,128]{1,0:T(8,128)S(1)}, f32[576,128]{1,0:T(8,128)S(1)}, u32[]{:S(2)}, u32[]{:S(2)}) collective-permute-start(f32[576,128]{1,0:T(8,128)S(1)} %get-tuple-element.23), channel_id=1, source_target_pairs={{0,8},{8,0},{16,24},{24,16},{1,9},{9,1},{17,25},{25,17},{2,10},{10... | collective-permute-start | bytes 884744 | tf_op jit(solution)/shard_map/ppermute | solution.py:26
  120.4 11.7 %collective-permute-start.14 = (f32[1152,128]{1,0:T(8,128)S(1)}, f32[1152,128]{1,0:T(8,128)S(1)}, u32[]{:S(2)}, u32[]{:S(2)}) collective-permute-start(f32[1152,128]{1,0:T(8,128)S(1)} %get-tuple-element.19), channel_id=1, source_target_pairs={{0,1},{1,0},{2,3},{3,2},{4,5},{5,4},{6,7},{7,6},{8,9},{9,8},{10,11... | collective-permute-start | bytes 1769480 | tf_op jit(solution)/shard_map/ppermute | solution.py:26
  127.4 1.3 copy-start.26
  127.4 1.3 copy-start.28
  (3 other events, 2.8 us)

commit v20 on v18

--- a/solution.py
+++ b/solution.py
@@ -87,8 +87,7 @@
     series_count = lax.axis_size("series")
     my_block = lax.axis_index("tm")
 
-    ordered = jnp.take(codes, owner_slot, axis=0).astype(fl)
-    outgoing = jnp.tile(ordered, (n_blocks, 1))
+    outgoing = jnp.take(codes, jnp.tile(owner_slot, n_blocks), axis=0).astype(fl)
     reading = lax.all_to_all(outgoing, ("tm", "series"), split_axis=0, concat_axis=1, tiled=True)[0]
     edge_float = edges.astype(fl)
     upper_edge = jnp.concatenate([edge_float[1:], jnp.full((1,), code_ceiling, fl)])

time: 127 us -> 127 us (level)
  other arithmetic: 16.4 us -> 14.9 us
where the time goes in v20:
time: 127 us; the launch traced here: 126 us
  starting transfers between devices  35.5 us (28%)
  local copies, waits for them, and re-layouts  27.9 us (22%)
  matrix products  24.8 us (20%)
  waiting for transfers between devices  21.3 us (17%)
  other arithmetic  14.9 us (12%)
  between operations  1.37 us (1%)
    ppermute x14, starting transfers between devices, exchange(): return lax.ppermute(value, axis, pairs)  24.5 us
    ppermute x14, waiting for transfers between devices, exchange(): return lax.ppermute(value, axis, pairs)  18.5 us
    all_to_all x1, starting transfers between devices, on_device(): lax.all_to_all(outgoing, ('tm', 'series'), split_axis=0, concat_axis=1, t...  7.1 us
    unnamed x73, local copies, waits for them, and re-layouts  5.53 us
    mul x4, local copies, waits for them, and re-layouts, on_device(): later_weighted = (later * head_all[k][:, :, None]).astype(half)  4.34 us
    slice x2, local copies, waits for them, and re-layouts, on_device(): x_heads = projected[:, :inner_width].reshape(tok_rows, head_count, head_dim)  3.92 us
    convert_element_type x1, local copies, waits for them, and re-layouts, on_device(): xw_all = (x_all[:earlier] * tail_all[:earlier, :, :, None]).astype(half)  3.56 us
    all_to_all x1, waiting for transfers between devices, on_device(): lax.all_to_all(outgoing, ('tm', 'series'), split_axis=0, concat_axis=1, t...  2.82 us
  transfers between devices with their start and end apart: 18, of which 11 were waited for; matrix products, arithmetic and copies ran while one was open for 42% of the time, Pallas kernels for 0%

profile of v20, /device:TPU:1, one launch (start us, length us, event | category | flops | bytes accessed | tf_op | source)
XLA Modules:
  0.0 125.8 jit_solution(17091871378148190611)
XLA Ops:
  1.6 1.3 %gather_fusion = s32[32,16]{1,0:T(8,128)S(1)} fusion(s32[8,16]{1,0:T(8,128)} %param.8, s32[1024]{0:T(1024)S(1)} %pad_clamp_fusion), kind=kCustom, calls=%fused_computation | custom fusion | bytes 4224 | tf_op jit(solution)/shard_map/jit(_take)/gather | solution.py:90
  3.6 7.1 %all-to-all-start = ((f32[32,1,16]{2,1,0:T(1,128)}), f32[32,1,16]{2,1,0:T(1,128)S(1)}, u32[]{:S(2)}, u32[]{:S(2)}) async-start(f32[32,1,16]{2,1,0:T(1,128)} %copy.114), calls=%async_computation | async-start | bytes 32768 | tf_op jit(solution)/shard_map/all_to_all | solution.py:91
  12.1 1.3 %copy.115 = bf16[1,128,2048]{1,2,0:T(8,128)(2,1)S(1)} copy(bf16[1,128,2048]{2,1,0:T(8,128)(2,1)} %param.15) | data formatting | bytes 1048576 | tf_op args[7]
  13.4 1.0 convert_bitcast_fusion
  14.6 2.8 %all-to-all-done = f32[32,1,16]{2,1,0:T(1,128)S(1)} async-done(((f32[32,1,16]{2,1,0:T(1,128)}), f32[32,1,16]{2,1,0:T(1,128)S(1)}, u32[]{:S(2)}, u32[]{:S(2)}) %all-to-all-start) | async-done | bytes 2080 | tf_op jit(solution)/shard_map/all_to_all | solution.py:91
  18.7 1.5 %convert_reduce_fusion = f32[4096]{0:T(1024)S(1)} fusion(f32[4096]{0:T(1024)S(1)} %get-tuple-element.48, f32[4096]{0:T(1024)S(1)} %convert_element_type.124, f32[512]{0:T(512)S(1)} %le.29), kind=kLoop, calls=%fused_computation.1 | loop fusion | flops 10481664 | bytes 51200 | tf_op jit(solution)/shard_map/reduce_sum | solution.py:97
  20.1 1.3 %collective-permute-start = (f32[128,2048]{0,1:T(8,128)}, f32[128,2048]{0,1:T(8,128)}, u32[]{:S(2)}, u32[]{:S(2)}) collective-permute-start(f32[128,2048]{0,1:T(8,128)} %convert_bitcast_fusion), channel_id=1, source_target_pairs={{24,16},{8,0},{25,17},{9,1},{26,18},{10,2},{27,19},{11,3},{28,20},... | collective-permute-start | bytes 3145736 | tf_op jit(solution)/shard_map/ppermute | solution.py:155
  21.4 1.3 %collective-permute-start.1 = (f32[128,2048]{0,1:T(8,128)}, f32[128,2048]{0,1:T(8,128)}, u32[]{:S(2)}, u32[]{:S(2)}) collective-permute-start(f32[128,2048]{0,1:T(8,128)} %convert_bitcast_fusion), channel_id=1, source_target_pairs={{24,8},{16,0},{25,9},{17,1},{26,10},{18,2},{27,11},{19,3},{28,12},... | collective-permute-start | bytes 3145736 | tf_op jit(solution)/shard_map/ppermute | solution.py:156
  22.7 1.3 %collective-permute-start.2 = (f32[128,2048]{0,1:T(8,128)}, f32[128,2048]{0,1:T(8,128)}, u32[]{:S(2)}, u32[]{:S(2)}) collective-permute-start(f32[128,2048]{0,1:T(8,128)} %convert_bitcast_fusion), channel_id=1, source_target_pairs={{16,8},{24,0},{17,9},{25,1},{18,10},{26,2},{19,11},{27,3},{20,12},... | collective-permute-start | bytes 3145736 | tf_op jit(solution)/shard_map/ppermute | solution.py:157
  24.8 1.3 %fusion = f32[512,12]{0,1:T(8,128)S(1)} fusion(f32[4096]{0:T(1024)S(1)} %get-tuple-element.48, f32[4096]{0:T(1024)S(1)} %convert_element_type.124, f32[512]{0:T(512)S(1)} %le.29, bf16[4096,4]{0,1:T(4,128)(2,1)S(1)} %get-tuple-element.46, bf16[4096,4]{0,1:T(4,128)(2,1)S(1)} %get-tuple-element.45, bf16[4096,4]{0,1:T(4,128)(2,1)S(1)} %get-tuple-element.44), kind=kOutput, calls=%fused_computation.5 | convolution fusion | flops 61112320 | bytes 157696 | tf_op jit(solution)/shard_map/dot_general | solution.py:105
  26.2 1.1 compare_select_fusion
  29.3 1.6 %convolution_convert_fusion = bf16[512,2304]{1,0:T(8,128)(2,1)S(1)} fusion(bf16[128,2304]{1,0:T(8,128)(2,1)S(1)} %copy-done, f32[128]{0:T(128)S(1)} %add_multiply_fusion, f32[512]{0:T(512)S(1)} %bitcast.239), kind=kOutput, calls=%fused_computation.4 | convolution fusion | flops 303300608 | bytes 2951680 | tf_op jit(solution)/shard_map/dot_general | solution.py:128
  30.9 1.0 compare_select_fusion.1
  32.0 1.4 %convolution_convert_fusion.1 = bf16[128,2304]{1,0:T(8,128)(2,1)} fusion(bf16[128,2304]{1,0:T(8,128)(2,1)S(1)} %copy-done, f32[128]{0:T(128)S(1)} %add_multiply_fusion, f32[1,128]{1,0:T(1,128)S(1)} %constant_dynamic-slice_fusion.7), kind=kOutput, calls=%fused_computation.7 | convolution fusion | flops 75825152 | bytes 1180672 | tf_op jit(solution)/shard_map/dot_general | solution.py:118
  36.4 1.5 %fusion.74 = f32[128,128]{0,1:T(8,128)} fusion(bf16[128,2304]{1,0:T(8,128)(2,1)} %convolution_convert_fusion.1), kind=kOutput, calls=%fused_computation.142 | convolution fusion | flops 4194304 | bytes 131072 | tf_op jit(solution)/shard_map/dot_general | solution.py:177
  38.0 1.9 %slice.149 = bf16[128,2048]{1,0:T(8,128)(2,1)} slice(bf16[128,2304]{1,0:T(8,128)(2,1)} %convolution_convert_fusion.1), slice={[0:128], [0:2048]} | slice | bytes 1048576 | tf_op jit(solution)/shard_map/slice | solution.py:119
  40.5 2.0 %copy.116 = bf16[128,2048]{0,1:T(8,128)(2,1)} copy(bf16[128,2048]{1,0:T(8,128)(2,1)} %slice.149) | data formatting | bytes 1048576 | tf_op jit(solution)/shard_map/slice | solution.py:119
  42.6 2.8 %fusion.2 = bf16[128,128]{0,1:T(8,128)(2,1)S(1)} fusion(bf16[128,32,64]{0,2,1:T(8,128)(2,1)} %bitcast.218, bf16[128,32,64]{0,2,1:T(8,128)(2,1)S(1)} %bitcast.208, f32[32,128]{1,0:T(8,128)} %get-tuple-element.53, f32[32,128]{1,0:T(8,128)} %copy.119, pred[128,128]{0,1:T(8,128)(4,1)} %iota_compare_fusion), kind=kOutput, calls=%fused_computation.10 | convolution fusion | flops 70238208 | bytes 1130496 | tf_op jit(solution)/shard_map/thp,shp->hts/dot_general | solution.py:194
  45.3 1.6 %fusion.76 = f32[128,128]{0,1:T(8,128)} fusion(bf16[128,2304]{1,0:T(8,128)(2,1)} %convolution_convert_fusion.1, bf16[128,128]{0,1:T(8,128)(2,1)S(1)} %fusion.2), kind=kOutput, calls=%fused_computation.144 | convolution fusion | flops 4194304 | bytes 131072 | tf_op jit(solution)/shard_map/dot_general | solution.py:196
  46.9 1.6 %fusion.71 = f32[128,128]{0,1:T(8,128)} fusion(bf16[128,2304]{1,0:T(8,128)(2,1)} %convolution_convert_fusion.1, bf16[128,128]{0,1:T(8,128)(2,1)S(1)} %fusion.2), kind=kOutput, calls=%fused_computation.139 | convolution fusion | flops 4194304 | bytes 131072 | tf_op jit(solution)/shard_map/dot_general | solution.py:198
  49.8 1.5 %copy.129 = f32[128,32]{0,1:T(8,128)} copy(f32[128,32]{1,0:T(8,128)} %get-tuple-element.34) | data formatting | bytes 32768 | tf_op jit(solution)/shard_map/mul | solution.py:166
  51.3 1.5 %copy.130 = f32[128,32]{0,1:T(8,128)} copy(f32[128,32]{1,0:T(8,128)} %get-tuple-element.33) | data formatting | bytes 32768 | tf_op jit(solution)/shard_map/mul | solution.py:166
  54.1 1.7 %slice_multiply_fusion = f32[3,128,32]{2,1,0:T(8,128)} fusion(f32[4,128,32]{2,1,0:T(8,128)} %bitcast.215, f32[4,128,32]{2,1,0:T(8,128)} %copy-done.2, f32[3,32]{1,0:T(4,128)S(1)} %bitcast.237), kind=kLoop, calls=%fused_computation.87 | loop fusion | flops 24576 | bytes 147840 | tf_op jit(solution)/shard_map/mul | solution.py:137
  55.8 1.7 %copy.125 = f32[3,128,32]{1,2,0:T(8,128)} copy(f32[3,128,32]{2,1,0:T(8,128)} %slice_multiply_fusion) | data formatting | bytes 98304 | tf_op jit(solution)/shard_map/slice | solution.py:140
  57.5 2.1 %slice_convert_fusion = f32[3,128,2048]{2,1,0:T(8,128)} fusion(bf16[4,128,2304]{2,1,0:T(8,128)(2,1)S(1)} %bitcast.203), kind=kLoop, calls=%fused_computation.14 | loop fusion | flops 786432 | bytes 4718592 | tf_op jit(solution)/shard_map/convert_element_type | solution.py:140
  59.6 3.6 %copy.123 = f32[3,128,2048]{1,2,0:T(8,128)} copy(f32[3,128,2048]{2,1,0:T(8,128)} %slice_convert_fusion) | data formatting | bytes 6291456 | tf_op jit(solution)/shard_map/convert_element_type | solution.py:140
  65.0 2.5 %fusion.3 = f32[3,32,64,128]{3,2,1,0:T(8,128)S(1)} fusion(f32[3,128,32,64]{1,3,2,0:T(8,128)} %bitcast.202, f32[3,128,32]{1,2,0:T(8,128)} %copy.125, bf16[4,128,2304]{2,1,0:T(8,128)(2,1)S(1)} %bitcast.204), kind=kOutput, calls=%fused_computation.13 | convolution fusion | flops 202899456 | bytes 6438912 | tf_op jit(solution)/shard_map/bthp,btn->bhpn/dot_general | solution.py:141
  69.2 1.3 %convolution_bitcast_fusion = f32[128,32,64]{0,2,1:T(8,128)S(1)} fusion(bf16[128,32,64]{0,2,1:T(8,128)(2,1)S(1)} %bitcast.209, f32[32,128]{1,0:T(8,128)S(1)} %copy-done.33, f32[32,128]{1,0:T(8,128)S(1)} %copy-done.17, f32[128,128]{0,1:T(8,128)S(1)} %copy-done.12, pred[128,128]{0,1:T(8,128)(4,1)S(1)} %copy-done.18), kind=kOutput, calls=%fused_computation.28 | convolution fusion | flops 70254592 | bytes 1687552 | tf_op jit(solution)/shard_map/hts,thp->shp/dot_general | solution.py:188
  70.5 2.2 %fusion.20 = (bf16[128,2048]{0,1:T(8,128)(2,1)S(1)}, bf16[128,2048]{0,1:T(8,128)(2,1)S(1)}, bf16[128,2048]{0,1:T(8,128)(2,1)S(1)}) fusion(f32[128,2048]{0,1:T(8,128)} %collective-permute-done.2, f32[128,2048]{0,1:T(8,128)} %collective-permute-done.1, f32[128,32]{0,1:T(8,128)S(1)} %copy-done.9, pred[]{:T(512)S(6)} %eq.19, f32[128,32]{0,1:T(8,128)S(1)} %copy-done.8, ...), kind=kLoop, calls=%fused_computation.51 | loop fusion | flops 2359296 | bytes 4767746 | tf_op jit(solution)/shard_map/convert_element_type | solution.py:166
  73.7 1.1 fusion.12
  75.8 1.2 collective-permute-start.3
  77.0 1.6 %collective-permute-done.3 = f32[1152,128]{1,0:T(8,128)S(1)} collective-permute-done((f32[1152,128]{1,0:T(8,128)S(1)}, f32[1152,128]{1,0:T(8,128)S(1)}, u32[]{:S(2)}, u32[]{:S(2)}) %collective-permute-start.3) | collective-permute-done | bytes 589856 | tf_op jit(solution)/shard_map/ppermute | solution.py:26
  78.8 3.1 %collective-permute-start.4 = (f32[288,128]{1,0:T(8,128)S(1)}, f32[288,128]{1,0:T(8,128)S(1)}, u32[]{:S(2)}, u32[]{:S(2)}) collective-permute-start(f32[288,128]{1,0:T(8,128)S(1)} %get-tuple-element.29), channel_id=1, source_target_pairs={{0,8},{8,0},{16,24},{24,16},{1,9},{9,1},{17,25},{25,17},{2,10},{10... | collective-permute-start | bytes 442376 | tf_op jit(solution)/shard_map/ppermute | solution.py:26
  81.9 4.1 %collective-permute-start.5 = (f32[288,128]{1,0:T(8,128)S(1)}, f32[288,128]{1,0:T(8,128)S(1)}, u32[]{:S(2)}, u32[]{:S(2)}) collective-permute-start(f32[288,128]{1,0:T(8,128)S(1)} %get-tuple-element.31), channel_id=1, source_target_pairs={{0,16},{8,24},{16,0},{24,8},{1,17},{9,25},{17,1},{25,9},{2,18},{10... | collective-permute-start | bytes 442376 | tf_op jit(solution)/shard_map/ppermute | solution.py:26
  86.0 5.8 %collective-permute-done.5 = f32[288,128]{1,0:T(8,128)S(1)} collective-permute-done((f32[288,128]{1,0:T(8,128)S(1)}, f32[288,128]{1,0:T(8,128)S(1)}, u32[]{:S(2)}, u32[]{:S(2)}) %collective-permute-start.5) | collective-permute-done | bytes 147488 | tf_op jit(solution)/shard_map/ppermute | solution.py:26
  93.3 3.0 %collective-permute-start.9 = (f32[72,128]{1,0:T(8,128)S(1)}, f32[72,128]{1,0:T(8,128)S(1)}, u32[]{:S(2)}, u32[]{:S(2)}) collective-permute-start(f32[72,128]{1,0:T(8,128)S(1)} %get-tuple-element.42), channel_id=1, source_target_pairs={{0,6},{1,7},{2,4},{3,5},{4,2},{5,3},{6,0},{7,1},{8,14},{9,15},{10,... | collective-permute-start | bytes 110600 | tf_op jit(solution)/shard_map/ppermute | solution.py:26
  96.7 1.4 %collective-permute-done.9 = f32[72,128]{1,0:T(8,128)S(1)} collective-permute-done((f32[72,128]{1,0:T(8,128)S(1)}, f32[72,128]{1,0:T(8,128)S(1)}, u32[]{:S(2)}, u32[]{:S(2)}) %collective-permute-start.9) | collective-permute-done | bytes 36896 | tf_op jit(solution)/shard_map/ppermute | solution.py:26
  98.2 3.1 %collective-permute-start.11 = (f32[72,128]{1,0:T(8,128)S(1)}, f32[72,128]{1,0:T(8,128)S(1)}, u32[]{:S(2)}, u32[]{:S(2)}) collective-permute-start(f32[72,128]{1,0:T(8,128)S(1)} %add_add_fusion.1), channel_id=1, source_target_pairs={{0,4},{1,5},{2,6},{3,7},{4,0},{5,1},{6,2},{7,3},{8,12},{9,13},{10,... | collective-permute-start | bytes 110600 | tf_op jit(solution)/shard_map/ppermute | solution.py:26
  102.6 3.4 %collective-permute-done.12 = f32[72,128]{1,0:T(8,128)S(1)} collective-permute-done((f32[72,128]{1,0:T(8,128)S(1)}, f32[72,128]{1,0:T(8,128)S(1)}, u32[]{:S(2)}, u32[]{:S(2)}) %collective-permute-start.12) | collective-permute-done | bytes 36896 | tf_op jit(solution)/shard_map/ppermute | solution.py:26
  106.1 1.3 %collective-permute-start.13 = (f32[288,128]{1,0:T(8,128)S(1)}, f32[288,128]{1,0:T(8,128)S(1)}, u32[]{:S(2)}, u32[]{:S(2)}) collective-permute-start(f32[288,128]{1,0:T(8,128)S(1)} %get-tuple-element.36), channel_id=1, source_target_pairs={{0,8},{8,0},{16,24},{24,16},{1,9},{9,1},{17,25},{25,17},{2,10},{10... | collective-permute-start | bytes 442376 | tf_op jit(solution)/shard_map/ppermute | solution.py:26
  108.8 1.4 %collective-permute-done.13 = f32[288,128]{1,0:T(8,128)S(1)} collective-permute-done((f32[288,128]{1,0:T(8,128)S(1)}, f32[288,128]{1,0:T(8,128)S(1)}, u32[]{:S(2)}, u32[]{:S(2)}) %collective-permute-start.13) | collective-permute-done | bytes 147488 | tf_op jit(solution)/shard_map/ppermute | solution.py:26
  110.3 1.2 collective-permute-done.14
  111.4 1.6 %collective-permute-done.15 = f32[288,128]{1,0:T(8,128)S(1)} collective-permute-done((f32[288,128]{1,0:T(8,128)S(1)}, f32[288,128]{1,0:T(8,128)S(1)}, u32[]{:S(2)}, u32[]{:S(2)}) %collective-permute-start.15) | collective-permute-done | bytes 147488 | tf_op jit(solution)/shard_map/ppermute | solution.py:26
  113.2 6.1 %collective-permute-start.16 = (f32[1152,128]{1,0:T(8,128)S(1)}, f32[1152,128]{1,0:T(8,128)S(1)}, u32[]{:S(2)}, u32[]{:S(2)}) collective-permute-start(f32[1152,128]{1,0:T(8,128)S(1)} %get-tuple-element.23), channel_id=1, source_target_pairs={{0,1},{1,0},{2,3},{3,2},{4,5},{5,4},{6,7},{7,6},{8,9},{9,8},{10,11... | collective-permute-start | bytes 1769480 | tf_op jit(solution)/shard_map/ppermute | solution.py:26
  119.3 1.3 %convolution_bitcast_fusion.1 = f32[128,32,64]{0,2,1:T(8,128)S(1)} fusion(bf16[128,32,64]{0,2,1:T(8,128)(2,1)S(1)} %bitcast.220, f32[32,128]{1,0:T(8,128)S(1)} %copy-done.34, f32[32,128]{1,0:T(8,128)S(1)} %copy-done.17, f32[128,128]{0,1:T(8,128)S(1)} %copy-done.13, pred[128,128]{0,1:T(8,128)(4,1)S(1)} %copy-done.19), kind=kOutput, calls=%fused_computation.31 | convolution fusion | flops 70254592 | bytes 1687552 | tf_op jit(solution)/shard_map/hts,shp->thp/dot_general | solution.py:181
  120.6 2.4 %fusion.10 = bf16[128,32,64]{0,2,1:T(8,128)(2,1)S(1)} fusion(f32[128,32,64]{0,2,1:T(8,128)S(1)} %convolution_bitcast_fusion.1, f32[3,32,64,128]{3,2,1,0:T(8,128)} %copy-done.1, f32[128,32]{0,1:T(8,128)S(1)} %copy.126, f32[32]{0:T(128)S(1)} %copy-done.30, f32[32]{0:T(128)S(1)} %copy-done.28, f32[32]{0:T(128)S(1)} %copy-done.26, pred[]{:T(512)S(6)} %gt.24, ...), kind=kOutput, calls=%fused_computation.34 | convolution fusion | flops 70254592 | bytes 4768131 | tf_op jit(solution)/shard_map/tn,hpn->thp/dot_general | solution.py:184
  123.0 1.0 copy.133
  124.4 1.4 %copy.134 = f32[128,2304]{1,0:T(8,128)} copy(f32[128,2304]{0,1:T(8,128)S(1)} %fusion.13) | data formatting | bytes 2359296
  (153 shorter events, 24.3 us)
Async XLA Ops:
  0.6 28.6 %copy-start = (bf16[128,2304]{1,0:T(8,128)(2,1)S(1)}, bf16[128,2304]{1,0:T(8,128)(2,1)}, u32[]{:S(2)}) copy-start(bf16[128,2304]{1,0:T(8,128)(2,1)} %param.11) | copy-start | bytes 1769476
  0.6 13.8 %copy-start.16 = (s32[4096]{0:T(1024)S(1)}, s32[4096]{0:T(1024)}, u32[]{:S(2)}) copy-start(s32[4096]{0:T(1024)} %param.10) | copy-start | bytes 49156
  3.6 13.8 %all-to-all-start = ((f32[32,1,16]{2,1,0:T(1,128)}), f32[32,1,16]{2,1,0:T(1,128)S(1)}, u32[]{:S(2)}, u32[]{:S(2)}) async-start(f32[32,1,16]{2,1,0:T(1,128)} %copy.114), calls=%async_computation | async-start | bytes 32768 | tf_op jit(solution)/shard_map/all_to_all | solution.py:91
  14.6 17.4 %copy-start.20 = (f32[128]{0:T(128)}, f32[128]{0:T(128)S(1)}, u32[]{:S(2)}) copy-start(f32[128]{0:T(128)S(1)} %add_multiply_fusion) | copy-start | bytes 1540
  20.1 50.3 %collective-permute-start = (f32[128,2048]{0,1:T(8,128)}, f32[128,2048]{0,1:T(8,128)}, u32[]{:S(2)}, u32[]{:S(2)}) collective-permute-start(f32[128,2048]{0,1:T(8,128)} %convert_bitcast_fusion), channel_id=1, source_target_pairs={{24,16},{8,0},{25,17},{9,1},{26,18},{10,2},{27,19},{11,3},{28,20},... | collective-permute-start | bytes 3145736 | tf_op jit(solution)/shard_map/ppermute | solution.py:155
  21.4 49.1 %collective-permute-start.1 = (f32[128,2048]{0,1:T(8,128)}, f32[128,2048]{0,1:T(8,128)}, u32[]{:S(2)}, u32[]{:S(2)}) collective-permute-start(f32[128,2048]{0,1:T(8,128)} %convert_bitcast_fusion), channel_id=1, source_target_pairs={{24,8},{16,0},{25,9},{17,1},{26,10},{18,2},{27,11},{19,3},{28,12},... | collective-permute-start | bytes 3145736 | tf_op jit(solution)/shard_map/ppermute | solution.py:156
  22.7 47.8 %collective-permute-start.2 = (f32[128,2048]{0,1:T(8,128)}, f32[128,2048]{0,1:T(8,128)}, u32[]{:S(2)}, u32[]{:S(2)}) collective-permute-start(f32[128,2048]{0,1:T(8,128)} %convert_bitcast_fusion), channel_id=1, source_target_pairs={{16,8},{24,0},{17,9},{25,1},{18,10},{26,2},{19,11},{27,3},{20,12},... | collective-permute-start | bytes 3145736 | tf_op jit(solution)/shard_map/ppermute | solution.py:157
  24.8 1.4 %copy-start.31 = (bf16[128,32]{0,1:T(8,128)(2,1)S(1)}, bf16[128,32]{0,1:T(8,128)(2,1)}, u32[]{:S(2)}) copy-start(bf16[128,32]{0,1:T(8,128)(2,1)} %param.12) | copy-start | bytes 24580
  24.8 1.4 %copy-start.32 = (f32[32]{0:T(128)S(1)}, f32[32]{0:T(128)}, u32[]{:S(2)}) copy-start(f32[32]{0:T(128)} %param.13) | copy-start | bytes 388
  24.8 3.4 %copy-start.22 = (f32[32]{0:T(128)S(1)}, f32[32]{0:T(128)}, u32[]{:S(2)}) copy-start(f32[32]{0:T(128)} %param.14) | copy-start | bytes 388
  30.9 2.4 %copy-start.23 = (f32[1,128]{1,0:T(1,128)}, f32[1,128]{1,0:T(1,128)S(1)}, u32[]{:S(2)}) copy-start(f32[1,128]{1,0:T(1,128)S(1)} %constant_dynamic-slice_fusion.7) | copy-start | bytes 1540
  32.0 1.4 %copy-start.11 = (f32[128,32]{0,1:T(8,128)}, f32[128,32]{0,1:T(8,128)S(1)}, u32[]{:S(2)}) copy-start(f32[128,32]{0,1:T(8,128)S(1)} %get-tuple-element.54) | copy-start | bytes 49156
  42.6 6.6 %copy-start.4 = (f32[4,128,32]{2,1,0:T(8,128)S(1)}, f32[4,128,32]{2,1,0:T(8,128)}, u32[]{:S(2)}) copy-start(f32[4,128,32]{2,1,0:T(8,128)} %exp.40) | copy-start | bytes 196612
  59.6 3.6 %copy-start.7 = (f32[128,32]{1,0:T(8,128)S(1)}, f32[128,32]{1,0:T(8,128)}, u32[]{:S(2)}) copy-start(f32[128,32]{1,0:T(8,128)} %exp.39) | copy-start | bytes 49156
  65.0 2.5 %copy-start.29 = (f32[32]{0:T(128)}, f32[32]{0:T(128)S(1)}, u32[]{:S(2)}) copy-start(f32[32]{0:T(128)S(1)} %get-tuple-element.50) | copy-start | bytes 388
  65.0 8.1 %copy-start.25 = (f32[32]{0:T(128)}, f32[32]{0:T(128)S(1)}, u32[]{:S(2)}) copy-start(f32[32]{0:T(128)S(1)} %get-tuple-element.52) | copy-start | bytes 388
  65.0 8.4 %copy-start.27 = (f32[32]{0:T(128)}, f32[32]{0:T(128)S(1)}, u32[]{:S(2)}) copy-start(f32[32]{0:T(128)S(1)} %get-tuple-element.51) | copy-start | bytes 388
  65.0 2.5 %copy-start.15 = (f32[128,128]{0,1:T(8,128)S(1)}, f32[128,128]{0,1:T(8,128)}, u32[]{:S(2)}) copy-start(f32[128,128]{0,1:T(8,128)} %fusion.71) | copy-start | bytes 196612
  67.5 1.6 %copy-start.1 = (f32[3,32,64,128]{3,2,1,0:T(8,128)}, f32[3,32,64,128]{3,2,1,0:T(8,128)S(1)}, u32[]{:S(2)}) copy-start(f32[3,32,64,128]{3,2,1,0:T(8,128)S(1)} %fusion.3) | copy-start | bytes 9437188
  67.5 1.6 %copy-start.12 = (f32[128,128]{0,1:T(8,128)S(1)}, f32[128,128]{0,1:T(8,128)}, u32[]{:S(2)}) copy-start(f32[128,128]{0,1:T(8,128)} %fusion.74) | copy-start | bytes 196612
  67.5 1.6 %copy-start.17 = (f32[32,128]{1,0:T(8,128)S(1)}, f32[32,128]{1,0:T(8,128)}, u32[]{:S(2)}) copy-start(f32[32,128]{1,0:T(8,128)} %copy.119) | copy-start | bytes 49156
  67.5 1.6 %copy-start.18 = (pred[128,128]{0,1:T(8,128)(4,1)S(1)}, pred[128,128]{0,1:T(8,128)(4,1)}, u32[]{:S(2)}) copy-start(pred[128,128]{0,1:T(8,128)(4,1)} %iota_compare_fusion) | copy-start | bytes 49156
  67.5 1.6 %copy-start.33 = (f32[32,128]{1,0:T(8,128)S(1)}, f32[32,128]{1,0:T(8,128)}, u32[]{:S(2)}) copy-start(f32[32,128]{1,0:T(8,128)} %get-tuple-element.53) | copy-start | bytes 49156
  69.1 1.4 %copy-start.8 = (f32[128,32]{0,1:T(8,128)S(1)}, f32[128,32]{0,1:T(8,128)}, u32[]{:S(2)}) copy-start(f32[128,32]{0,1:T(8,128)} %copy.129) | copy-start | bytes 49156
  69.2 1.4 %copy-start.9 = (f32[128,32]{0,1:T(8,128)S(1)}, f32[128,32]{0,1:T(8,128)}, u32[]{:S(2)}) copy-start(f32[128,32]{0,1:T(8,128)} %copy.130) | copy-start | bytes 49156
  69.2 1.4 %copy-start.10 = (f32[128,32]{0,1:T(8,128)S(1)}, f32[128,32]{0,1:T(8,128)}, u32[]{:S(2)}) copy-start(f32[128,32]{0,1:T(8,128)} %copy.131) | copy-start | bytes 49156
  73.4 1.4 %copy-start.5 = (bf16[128,2048]{0,1:T(8,128)(2,1)S(1)}, bf16[128,2048]{0,1:T(8,128)(2,1)}, u32[]{:S(2)}) copy-start(bf16[128,2048]{0,1:T(8,128)(2,1)} %copy.116) | copy-start | bytes 1572868
  73.4 1.4 %copy-start.14 = (f32[128,128]{0,1:T(8,128)S(1)}, f32[128,128]{0,1:T(8,128)}, u32[]{:S(2)}) copy-start(f32[128,128]{0,1:T(8,128)} %fusion.76) | copy-start | bytes 196612
  73.7 1.5 %copy-start.21 = (f32[128]{0:T(128)S(1)}, f32[128]{0:T(128)}, u32[]{:S(2)}) copy-start(f32[128]{0:T(128)} %copy-done.20) | copy-start | bytes 1540
  73.7 1.5 %copy-start.24 = (f32[1,128]{1,0:T(1,128)S(1)}, f32[1,128]{1,0:T(1,128)}, u32[]{:S(2)}) copy-start(f32[1,128]{1,0:T(1,128)} %copy-done.23) | copy-start | bytes 1540
  75.8 2.9 %collective-permute-start.3 = (f32[1152,128]{1,0:T(8,128)S(1)}, f32[1152,128]{1,0:T(8,128)S(1)}, u32[]{:S(2)}, u32[]{:S(2)}) collective-permute-start(f32[1152,128]{1,0:T(8,128)S(1)} %constant_dynamic-slice_fusion.6), channel_id=1, source_target_pairs={{0,1},{1,0},{2,3},{3,2},{4,5},{5,4},{6,7},{7,6},{8,9},{9,8},{10,11... | collective-permute-start | bytes 1769480 | tf_op jit(solution)/shard_map/ppermute | solution.py:26
  78.8 7.3 %collective-permute-start.4 = (f32[288,128]{1,0:T(8,128)S(1)}, f32[288,128]{1,0:T(8,128)S(1)}, u32[]{:S(2)}, u32[]{:S(2)}) collective-permute-start(f32[288,128]{1,0:T(8,128)S(1)} %get-tuple-element.29), channel_id=1, source_target_pairs={{0,8},{8,0},{16,24},{24,16},{1,9},{9,1},{17,25},{25,17},{2,10},{10... | collective-permute-start | bytes 442376 | tf_op jit(solution)/shard_map/ppermute | solution.py:26
  81.9 10.0 %collective-permute-start.5 = (f32[288,128]{1,0:T(8,128)S(1)}, f32[288,128]{1,0:T(8,128)S(1)}, u32[]{:S(2)}, u32[]{:S(2)}) collective-permute-start(f32[288,128]{1,0:T(8,128)S(1)} %get-tuple-element.31), channel_id=1, source_target_pairs={{0,16},{8,24},{16,0},{24,8},{1,17},{9,25},{17,1},{25,9},{2,18},{10... | collective-permute-start | bytes 442376 | tf_op jit(solution)/shard_map/ppermute | solution.py:26
  86.0 6.6 %collective-permute-start.6 = (f32[288,128]{1,0:T(8,128)S(1)}, f32[288,128]{1,0:T(8,128)S(1)}, u32[]{:S(2)}, u32[]{:S(2)}) collective-permute-start(f32[288,128]{1,0:T(8,128)S(1)} %get-tuple-element.30), channel_id=1, source_target_pairs={{0,24},{8,16},{16,8},{24,0},{1,25},{9,17},{17,9},{25,1},{2,26},{10... | collective-permute-start | bytes 442376 | tf_op jit(solution)/shard_map/ppermute | solution.py:26
  92.7 3.6 %collective-permute-start.7 = (f32[72,128]{1,0:T(8,128)S(1)}, f32[72,128]{1,0:T(8,128)S(1)}, u32[]{:S(2)}, u32[]{:S(2)}) collective-permute-start(f32[72,128]{1,0:T(8,128)S(1)} %get-tuple-element.41), channel_id=1, source_target_pairs={{0,2},{1,3},{2,0},{3,1},{4,6},{5,7},{6,4},{7,5},{8,10},{9,11},{10,... | collective-permute-start | bytes 110600 | tf_op jit(solution)/shard_map/ppermute | solution.py:26
  93.0 3.7 %collective-permute-start.8 = (f32[72,128]{1,0:T(8,128)S(1)}, f32[72,128]{1,0:T(8,128)S(1)}, u32[]{:S(2)}, u32[]{:S(2)}) collective-permute-start(f32[72,128]{1,0:T(8,128)S(1)} %get-tuple-element.43), channel_id=1, source_target_pairs={{0,4},{1,5},{2,6},{3,7},{4,0},{5,1},{6,2},{7,3},{8,12},{9,13},{10,... | collective-permute-start | bytes 110600 | tf_op jit(solution)/shard_map/ppermute | solution.py:26
  93.3 4.8 %collective-permute-start.9 = (f32[72,128]{1,0:T(8,128)S(1)}, f32[72,128]{1,0:T(8,128)S(1)}, u32[]{:S(2)}, u32[]{:S(2)}) collective-permute-start(f32[72,128]{1,0:T(8,128)S(1)} %get-tuple-element.42), channel_id=1, source_target_pairs={{0,6},{1,7},{2,4},{3,5},{4,2},{5,3},{6,0},{7,1},{8,14},{9,15},{10,... | collective-permute-start | bytes 110600 | tf_op jit(solution)/shard_map/ppermute | solution.py:26
  98.1 3.6 %collective-permute-start.10 = (f32[72,128]{1,0:T(8,128)S(1)}, f32[72,128]{1,0:T(8,128)S(1)}, u32[]{:S(2)}, u32[]{:S(2)}) collective-permute-start(f32[72,128]{1,0:T(8,128)S(1)} %add_add_fusion.1), channel_id=1, source_target_pairs={{0,2},{1,3},{2,0},{3,1},{4,6},{5,7},{6,4},{7,5},{8,10},{9,11},{10,... | collective-permute-start | bytes 110600 | tf_op jit(solution)/shard_map/ppermute | solution.py:26
  98.2 4.4 %collective-permute-start.11 = (f32[72,128]{1,0:T(8,128)S(1)}, f32[72,128]{1,0:T(8,128)S(1)}, u32[]{:S(2)}, u32[]{:S(2)}) collective-permute-start(f32[72,128]{1,0:T(8,128)S(1)} %add_add_fusion.1), channel_id=1, source_target_pairs={{0,4},{1,5},{2,6},{3,7},{4,0},{5,1},{6,2},{7,3},{8,12},{9,13},{10,... | collective-permute-start | bytes 110600 | tf_op jit(solution)/shard_map/ppermute | solution.py:26
  101.3 4.7 %collective-permute-start.12 = (f32[72,128]{1,0:T(8,128)S(1)}, f32[72,128]{1,0:T(8,128)S(1)}, u32[]{:S(2)}, u32[]{:S(2)}) collective-permute-start(f32[72,128]{1,0:T(8,128)S(1)} %add_add_fusion.1), channel_id=1, source_target_pairs={{0,6},{1,7},{2,4},{3,5},{4,2},{5,3},{6,0},{7,1},{8,14},{9,15},{10,... | collective-permute-start | bytes 110600 | tf_op jit(solution)/shard_map/ppermute | solution.py:26
  106.1 13.2 %copy-start.6 = (bf16[128,2048]{0,1:T(8,128)(2,1)S(1)}, bf16[128,2048]{0,1:T(8,128)(2,1)}, u32[]{:S(2)}) copy-start(bf16[128,2048]{0,1:T(8,128)(2,1)} %copy.116) | copy-start | bytes 1572868
  106.1 13.2 %copy-start.13 = (f32[128,128]{0,1:T(8,128)S(1)}, f32[128,128]{0,1:T(8,128)}, u32[]{:S(2)}) copy-start(f32[128,128]{0,1:T(8,128)} %fusion.74) | copy-start | bytes 196612
  106.1 13.2 %copy-start.19 = (pred[128,128]{0,1:T(8,128)(4,1)S(1)}, pred[128,128]{0,1:T(8,128)(4,1)}, u32[]{:S(2)}) copy-start(pred[128,128]{0,1:T(8,128)(4,1)} %iota_compare_fusion) | copy-start | bytes 49156
  106.1 13.2 %copy-start.34 = (f32[32,128]{1,0:T(8,128)S(1)}, f32[32,128]{1,0:T(8,128)}, u32[]{:S(2)}) copy-start(f32[32,128]{1,0:T(8,128)} %get-tuple-element.53) | copy-start | bytes 49156
  106.1 4.1 %collective-permute-start.13 = (f32[288,128]{1,0:T(8,128)S(1)}, f32[288,128]{1,0:T(8,128)S(1)}, u32[]{:S(2)}, u32[]{:S(2)}) collective-permute-start(f32[288,128]{1,0:T(8,128)S(1)} %get-tuple-element.36), channel_id=1, source_target_pairs={{0,8},{8,0},{16,24},{24,16},{1,9},{9,1},{17,25},{25,17},{2,10},{10... | collective-permute-start | bytes 442376 | tf_op jit(solution)/shard_map/ppermute | solution.py:26
  107.4 4.0 %collective-permute-start.14 = (f32[288,128]{1,0:T(8,128)S(1)}, f32[288,128]{1,0:T(8,128)S(1)}, u32[]{:S(2)}, u32[]{:S(2)}) collective-permute-start(f32[288,128]{1,0:T(8,128)S(1)} %get-tuple-element.36), channel_id=1, source_target_pairs={{0,16},{8,24},{16,0},{24,8},{1,17},{9,25},{17,1},{25,9},{2,18},{10... | collective-permute-start | bytes 442376 | tf_op jit(solution)/shard_map/ppermute | solution.py:26
  107.8 5.1 %collective-permute-start.15 = (f32[288,128]{1,0:T(8,128)S(1)}, f32[288,128]{1,0:T(8,128)S(1)}, u32[]{:S(2)}, u32[]{:S(2)}) collective-permute-start(f32[288,128]{1,0:T(8,128)S(1)} %get-tuple-element.36), channel_id=1, source_target_pairs={{0,24},{8,16},{16,8},{24,0},{1,25},{9,17},{17,9},{25,1},{2,26},{10... | collective-permute-start | bytes 442376 | tf_op jit(solution)/shard_map/ppermute | solution.py:26
  113.2 10.9 %collective-permute-start.16 = (f32[1152,128]{1,0:T(8,128)S(1)}, f32[1152,128]{1,0:T(8,128)S(1)}, u32[]{:S(2)}, u32[]{:S(2)}) collective-permute-start(f32[1152,128]{1,0:T(8,128)S(1)} %get-tuple-element.23), channel_id=1, source_target_pairs={{0,1},{1,0},{2,3},{3,2},{4,5},{5,4},{6,7},{7,6},{8,9},{9,8},{10,11... | collective-permute-start | bytes 1769480 | tf_op jit(solution)/shard_map/ppermute | solution.py:26
  (5 other events, 5.5 us)

commit v21 on v20

--- a/solution.py
+++ b/solution.py
@@ -138,6 +138,7 @@
     head_all = jnp.exp(cum_all)
     earlier = n_blocks - 1
     xw_all = (x_all[:earlier] * tail_all[:earlier, :, :, None]).astype(half)
+    xw_all = lax.optimization_barrier(xw_all)
     state_local_all = jnp.einsum(
         "bthp,btn->bhpn", xw_all, b_all[:earlier], preferred_element_type=fl
     )

time: 127 us -> 130 us (1.024)
  other arithmetic: 14.9 us -> 18.5 us
    convert_element_type x1 -> x2, other arithmetic: 2.09 us -> 5.67 us  [on_device(): xw_all = (x_all[:earlier] * tail_all[:earlier, :, :, None]).astype(half)]
    unnamed x73 -> x75, local copies, waits for them, and re-layouts: 5.53 us -> 5.52 us
  transfers between devices with their start and end apart: 18 -> 18, of which waited for: 11 -> 11; matrix products, arithmetic and copies ran while one was open for 42% -> 44% of each run, Pallas kernels for 0% -> 0%
where the time goes in v21:
time: 130 us; the launch traced here: 129 us
  starting transfers between devices  35.5 us (27%)
  local copies, waits for them, and re-layouts  27.9 us (21%)
  matrix products  24.3 us (19%)
  waiting for transfers between devices  21.3 us (16%)
  other arithmetic  18.5 us (14%)
  between operations  1.39 us (1%)
    ppermute x14, starting transfers between devices, exchange(): return lax.ppermute(value, axis, pairs)  24.5 us
    ppermute x14, waiting for transfers between devices, exchange(): return lax.ppermute(value, axis, pairs)  18.5 us
    all_to_all x1, starting transfers between devices, on_device(): lax.all_to_all(outgoing, ('tm', 'series'), split_axis=0, concat_axis=1, t...  7.1 us
    convert_element_type x2, other arithmetic, on_device(): xw_all = (x_all[:earlier] * tail_all[:earlier, :, :, None]).astype(half)  5.67 us
    unnamed x75, local copies, waits for them, and re-layouts  5.52 us
    mul x4, local copies, waits for them, and re-layouts, on_device(): later_weighted = (later * head_all[k][:, :, None]).astype(half)  4.35 us
    slice x2, local copies, waits for them, and re-layouts, on_device(): x_heads = projected[:, :inner_width].reshape(tok_rows, head_count, head_dim)  3.92 us
    convert_element_type x1, local copies, waits for them, and re-layouts, on_device(): xw_all = (x_all[:earlier] * tail_all[:earlier, :, :, None]).astype(half)  3.53 us
  transfers between devices with their start and end apart: 18, of which 11 were waited for; matrix products, arithmetic and copies ran while one was open for 44% of the time, Pallas kernels for 0%

profile of v21, /device:TPU:1, one launch (start us, length us, event | category | flops | bytes accessed | tf_op | source)
XLA Modules:
  0.0 128.9 jit_solution(10854340312728997405)
XLA Ops:
  1.6 1.3 gather_fusion
  3.6 7.1 %all-to-all-start = ((f32[32,1,16]{2,1,0:T(1,128)}), f32[32,1,16]{2,1,0:T(1,128)S(1)}, u32[]{:S(2)}, u32[]{:S(2)}) async-start(f32[32,1,16]{2,1,0:T(1,128)} %copy.114), calls=%async_computation | async-start | bytes 32768 | tf_op jit(solution)/shard_map/all_to_all | solution.py:91
  12.1 1.3 %copy.115 = bf16[1,128,2048]{1,2,0:T(8,128)(2,1)S(1)} copy(bf16[1,128,2048]{2,1,0:T(8,128)(2,1)} %param.15) | data formatting | bytes 1048576 | tf_op args[7]
  13.4 1.0 convert_bitcast_fusion
  14.6 2.8 %all-to-all-done = f32[32,1,16]{2,1,0:T(1,128)S(1)} async-done(((f32[32,1,16]{2,1,0:T(1,128)}), f32[32,1,16]{2,1,0:T(1,128)S(1)}, u32[]{:S(2)}, u32[]{:S(2)}) %all-to-all-start) | async-done | bytes 2080 | tf_op jit(solution)/shard_map/all_to_all | solution.py:91
  18.7 1.5 %convert_reduce_fusion = f32[4096]{0:T(1024)S(1)} fusion(f32[4096]{0:T(1024)S(1)} %get-tuple-element.48, f32[4096]{0:T(1024)S(1)} %convert_element_type.124, f32[512]{0:T(512)S(1)} %le.29), kind=kLoop, calls=%fused_computation.1 | loop fusion | flops 10481664 | bytes 51200 | tf_op jit(solution)/shard_map/reduce_sum | solution.py:97
  20.1 1.3 %collective-permute-start = (f32[128,2048]{0,1:T(8,128)}, f32[128,2048]{0,1:T(8,128)}, u32[]{:S(2)}, u32[]{:S(2)}) collective-permute-start(f32[128,2048]{0,1:T(8,128)} %convert_bitcast_fusion), channel_id=1, source_target_pairs={{24,16},{8,0},{25,17},{9,1},{26,18},{10,2},{27,19},{11,3},{28,20},... | collective-permute-start | bytes 3145736 | tf_op jit(solution)/shard_map/ppermute | solution.py:156
  21.4 1.3 %collective-permute-start.1 = (f32[128,2048]{0,1:T(8,128)}, f32[128,2048]{0,1:T(8,128)}, u32[]{:S(2)}, u32[]{:S(2)}) collective-permute-start(f32[128,2048]{0,1:T(8,128)} %convert_bitcast_fusion), channel_id=1, source_target_pairs={{24,8},{16,0},{25,9},{17,1},{26,10},{18,2},{27,11},{19,3},{28,12},... | collective-permute-start | bytes 3145736 | tf_op jit(solution)/shard_map/ppermute | solution.py:157
  22.7 1.3 %collective-permute-start.2 = (f32[128,2048]{0,1:T(8,128)}, f32[128,2048]{0,1:T(8,128)}, u32[]{:S(2)}, u32[]{:S(2)}) collective-permute-start(f32[128,2048]{0,1:T(8,128)} %convert_bitcast_fusion), channel_id=1, source_target_pairs={{16,8},{24,0},{17,9},{25,1},{18,10},{26,2},{19,11},{27,3},{20,12},... | collective-permute-start | bytes 3145736 | tf_op jit(solution)/shard_map/ppermute | solution.py:158
  24.8 1.3 fusion
  26.2 1.1 compare_select_fusion
  29.3 1.6 %convolution_convert_fusion = bf16[512,2304]{1,0:T(8,128)(2,1)S(1)} fusion(bf16[128,2304]{1,0:T(8,128)(2,1)S(1)} %copy-done, f32[128]{0:T(128)S(1)} %add_multiply_fusion, f32[512]{0:T(512)S(1)} %bitcast.240), kind=kOutput, calls=%fused_computation.4 | convolution fusion | flops 303300608 | bytes 2951680 | tf_op jit(solution)/shard_map/dot_general | solution.py:128
  30.9 1.0 compare_select_fusion.1
  32.0 1.4 %convolution_convert_fusion.1 = bf16[128,2304]{1,0:T(8,128)(2,1)} fusion(bf16[128,2304]{1,0:T(8,128)(2,1)S(1)} %copy-done, f32[128]{0:T(128)S(1)} %add_multiply_fusion, f32[1,128]{1,0:T(1,128)S(1)} %constant_dynamic-slice_fusion.7), kind=kOutput, calls=%fused_computation.7 | convolution fusion | flops 75825152 | bytes 1180672 | tf_op jit(solution)/shard_map/dot_general | solution.py:118
  34.2 1.0 reduce_window_sum.39
  36.5 1.5 %fusion.73 = f32[128,128]{0,1:T(8,128)} fusion(bf16[128,2304]{1,0:T(8,128)(2,1)} %convolution_convert_fusion.1), kind=kOutput, calls=%fused_computation.141 | convolution fusion | flops 4194304 | bytes 131072 | tf_op jit(solution)/shard_map/dot_general | solution.py:178
  38.0 1.9 %slice.149 = bf16[128,2048]{1,0:T(8,128)(2,1)} slice(bf16[128,2304]{1,0:T(8,128)(2,1)} %convolution_convert_fusion.1), slice={[0:128], [0:2048]} | slice | bytes 1048576 | tf_op jit(solution)/shard_map/slice | solution.py:119
  40.6 2.0 %copy.116 = bf16[128,2048]{0,1:T(8,128)(2,1)} copy(bf16[128,2048]{1,0:T(8,128)(2,1)} %slice.149) | data formatting | bytes 1048576 | tf_op jit(solution)/shard_map/slice | solution.py:119
  42.6 2.8 %fusion.2 = bf16[128,128]{0,1:T(8,128)(2,1)S(1)} fusion(bf16[128,32,64]{0,2,1:T(8,128)(2,1)} %bitcast.219, bf16[128,32,64]{0,2,1:T(8,128)(2,1)S(1)} %bitcast.209, f32[32,128]{1,0:T(8,128)} %get-tuple-element.53, f32[32,128]{1,0:T(8,128)} %copy.119, pred[128,128]{0,1:T(8,128)(4,1)} %iota_compare_fusion), kind=kOutput, calls=%fused_computation.10 | convolution fusion | flops 70238208 | bytes 1130496 | tf_op jit(solution)/shard_map/thp,shp->hts/dot_general | solution.py:195
  45.4 1.6 %fusion.75 = f32[128,128]{0,1:T(8,128)} fusion(bf16[128,2304]{1,0:T(8,128)(2,1)} %convolution_convert_fusion.1, bf16[128,128]{0,1:T(8,128)(2,1)S(1)} %fusion.2), kind=kOutput, calls=%fused_computation.143 | convolution fusion | flops 4194304 | bytes 131072 | tf_op jit(solution)/shard_map/dot_general | solution.py:197
  47.0 1.6 %fusion.70 = f32[128,128]{0,1:T(8,128)} fusion(bf16[128,2304]{1,0:T(8,128)(2,1)} %convolution_convert_fusion.1, bf16[128,128]{0,1:T(8,128)(2,1)S(1)} %fusion.2), kind=kOutput, calls=%fused_computation.138 | convolution fusion | flops 4194304 | bytes 131072 | tf_op jit(solution)/shard_map/dot_general | solution.py:199
  49.9 1.5 %copy.129 = f32[128,32]{0,1:T(8,128)} copy(f32[128,32]{1,0:T(8,128)} %get-tuple-element.34) | data formatting | bytes 32768 | tf_op jit(solution)/shard_map/mul | solution.py:167
  51.4 1.5 %copy.130 = f32[128,32]{0,1:T(8,128)} copy(f32[128,32]{1,0:T(8,128)} %get-tuple-element.33) | data formatting | bytes 32768 | tf_op jit(solution)/shard_map/mul | solution.py:167
  54.2 1.7 %slice_multiply_fusion = f32[3,128,32]{2,1,0:T(8,128)} fusion(f32[4,128,32]{2,1,0:T(8,128)} %bitcast.216, f32[4,128,32]{2,1,0:T(8,128)} %copy-done.2, f32[3,32]{1,0:T(4,128)S(1)} %bitcast.238), kind=kLoop, calls=%fused_computation.85 | loop fusion | flops 24576 | bytes 147840 | tf_op jit(solution)/shard_map/mul | solution.py:137
  55.9 1.6 %copy.125 = f32[3,128,32]{1,2,0:T(8,128)} copy(f32[3,128,32]{2,1,0:T(8,128)} %slice_multiply_fusion) | data formatting | bytes 98304 | tf_op jit(solution)/shard_map/slice | solution.py:140
  57.5 2.1 %slice_convert_fusion = f32[3,128,2048]{2,1,0:T(8,128)} fusion(bf16[4,128,2304]{2,1,0:T(8,128)(2,1)S(1)} %bitcast.204), kind=kLoop, calls=%fused_computation.13 | loop fusion | flops 786432 | bytes 4718592 | tf_op jit(solution)/shard_map/convert_element_type | solution.py:140
  59.6 3.5 %copy.123 = f32[3,128,2048]{1,2,0:T(8,128)} copy(f32[3,128,2048]{2,1,0:T(8,128)} %slice_convert_fusion) | data formatting | bytes 6291456 | tf_op jit(solution)/shard_map/convert_element_type | solution.py:140
  63.2 3.6 %multiply_convert_fusion = bf16[3,128,32,64]{1,3,2,0:T(8,128)(2,1)} fusion(f32[3,128,32,64]{1,3,2,0:T(8,128)} %bitcast.203, f32[3,128,32]{1,2,0:T(8,128)} %copy.125), kind=kLoop, calls=%fused_computation.8 | loop fusion | flops 1572864 | bytes 4767744 | tf_op jit(solution)/shard_map/convert_element_type | solution.py:140
  68.6 2.0 %fusion.54 = f32[3,32,64,128]{3,2,1,0:T(8,128)S(1)} fusion(bf16[3,128,32,64]{1,3,2,0:T(8,128)(2,1)} %multiply_convert_fusion, bf16[4,128,2304]{2,1,0:T(8,128)(2,1)S(1)} %bitcast.205), kind=kOutput, calls=%fused_computation.106 | convolution fusion | flops 201326592 | bytes 4816896 | tf_op jit(solution)/shard_map/bthp,btn->bhpn/dot_general | solution.py:142
  72.3 1.3 %convolution_bitcast_fusion = f32[128,32,64]{0,2,1:T(8,128)S(1)} fusion(bf16[128,32,64]{0,2,1:T(8,128)(2,1)S(1)} %bitcast.210, f32[32,128]{1,0:T(8,128)S(1)} %copy-done.34, f32[32,128]{1,0:T(8,128)S(1)} %copy-done.17, f32[128,128]{0,1:T(8,128)S(1)} %copy-done.12, pred[128,128]{0,1:T(8,128)(4,1)S(1)} %copy-done.19), kind=kOutput, calls=%fused_computation.26 | convolution fusion | flops 70254592 | bytes 1687552 | tf_op jit(solution)/shard_map/hts,thp->shp/dot_general | solution.py:189
  73.7 2.2 %fusion.18 = (bf16[128,2048]{0,1:T(8,128)(2,1)S(1)}, bf16[128,2048]{0,1:T(8,128)(2,1)S(1)}, bf16[128,2048]{0,1:T(8,128)(2,1)S(1)}) fusion(f32[128,2048]{0,1:T(8,128)} %collective-permute-done.2, f32[128,2048]{0,1:T(8,128)} %collective-permute-done.1, f32[128,32]{0,1:T(8,128)S(1)} %copy-done.9, pred[]{:T(512)S(6)} %eq.19, f32[128,32]{0,1:T(8,128)S(1)} %copy-done.8, ...), kind=kLoop, calls=%fused_computation.49 | loop fusion | flops 2359296 | bytes 4767746 | tf_op jit(solution)/shard_map/convert_element_type | solution.py:167
  76.8 1.1 fusion.10
  79.6 1.6 %collective-permute-done.3 = f32[1152,128]{1,0:T(8,128)S(1)} collective-permute-done((f32[1152,128]{1,0:T(8,128)S(1)}, f32[1152,128]{1,0:T(8,128)S(1)}, u32[]{:S(2)}, u32[]{:S(2)}) %collective-permute-start.3) | collective-permute-done | bytes 589856 | tf_op jit(solution)/shard_map/ppermute | solution.py:26
  81.3 3.4 %collective-permute-start.4 = (f32[288,128]{1,0:T(8,128)S(1)}, f32[288,128]{1,0:T(8,128)S(1)}, u32[]{:S(2)}, u32[]{:S(2)}) collective-permute-start(f32[288,128]{1,0:T(8,128)S(1)} %get-tuple-element.29), channel_id=1, source_target_pairs={{0,8},{8,0},{16,24},{24,16},{1,9},{9,1},{17,25},{25,17},{2,10},{10... | collective-permute-start | bytes 442376 | tf_op jit(solution)/shard_map/ppermute | solution.py:26
  84.7 4.4 %collective-permute-start.5 = (f32[288,128]{1,0:T(8,128)S(1)}, f32[288,128]{1,0:T(8,128)S(1)}, u32[]{:S(2)}, u32[]{:S(2)}) collective-permute-start(f32[288,128]{1,0:T(8,128)S(1)} %get-tuple-element.31), channel_id=1, source_target_pairs={{0,16},{8,24},{16,0},{24,8},{1,17},{9,25},{17,1},{25,9},{2,18},{10... | collective-permute-start | bytes 442376 | tf_op jit(solution)/shard_map/ppermute | solution.py:26
  89.1 5.8 %collective-permute-done.5 = f32[288,128]{1,0:T(8,128)S(1)} collective-permute-done((f32[288,128]{1,0:T(8,128)S(1)}, f32[288,128]{1,0:T(8,128)S(1)}, u32[]{:S(2)}, u32[]{:S(2)}) %collective-permute-start.5) | collective-permute-done | bytes 147488 | tf_op jit(solution)/shard_map/ppermute | solution.py:26
  96.5 3.0 %collective-permute-start.9 = (f32[72,128]{1,0:T(8,128)S(1)}, f32[72,128]{1,0:T(8,128)S(1)}, u32[]{:S(2)}, u32[]{:S(2)}) collective-permute-start(f32[72,128]{1,0:T(8,128)S(1)} %get-tuple-element.42), channel_id=1, source_target_pairs={{0,6},{1,7},{2,4},{3,5},{4,2},{5,3},{6,0},{7,1},{8,14},{9,15},{10,... | collective-permute-start | bytes 110600 | tf_op jit(solution)/shard_map/ppermute | solution.py:26
  99.9 1.3 %collective-permute-done.9 = f32[72,128]{1,0:T(8,128)S(1)} collective-permute-done((f32[72,128]{1,0:T(8,128)S(1)}, f32[72,128]{1,0:T(8,128)S(1)}, u32[]{:S(2)}, u32[]{:S(2)}) %collective-permute-start.9) | collective-permute-done | bytes 36896 | tf_op jit(solution)/shard_map/ppermute | solution.py:26
  101.3 3.1 %collective-permute-start.11 = (f32[72,128]{1,0:T(8,128)S(1)}, f32[72,128]{1,0:T(8,128)S(1)}, u32[]{:S(2)}, u32[]{:S(2)}) collective-permute-start(f32[72,128]{1,0:T(8,128)S(1)} %add_add_fusion.1), channel_id=1, source_target_pairs={{0,4},{1,5},{2,6},{3,7},{4,0},{5,1},{6,2},{7,3},{8,12},{9,13},{10,... | collective-permute-start | bytes 110600 | tf_op jit(solution)/shard_map/ppermute | solution.py:26
  105.8 3.3 %collective-permute-done.12 = f32[72,128]{1,0:T(8,128)S(1)} collective-permute-done((f32[72,128]{1,0:T(8,128)S(1)}, f32[72,128]{1,0:T(8,128)S(1)}, u32[]{:S(2)}, u32[]{:S(2)}) %collective-permute-start.12) | collective-permute-done | bytes 36896 | tf_op jit(solution)/shard_map/ppermute | solution.py:26
  109.2 1.3 %collective-permute-start.13 = (f32[288,128]{1,0:T(8,128)S(1)}, f32[288,128]{1,0:T(8,128)S(1)}, u32[]{:S(2)}, u32[]{:S(2)}) collective-permute-start(f32[288,128]{1,0:T(8,128)S(1)} %get-tuple-element.36), channel_id=1, source_target_pairs={{0,8},{8,0},{16,24},{24,16},{1,9},{9,1},{17,25},{25,17},{2,10},{10... | collective-permute-start | bytes 442376 | tf_op jit(solution)/shard_map/ppermute | solution.py:26
  111.9 1.4 %collective-permute-done.13 = f32[288,128]{1,0:T(8,128)S(1)} collective-permute-done((f32[288,128]{1,0:T(8,128)S(1)}, f32[288,128]{1,0:T(8,128)S(1)}, u32[]{:S(2)}, u32[]{:S(2)}) %collective-permute-start.13) | collective-permute-done | bytes 147488 | tf_op jit(solution)/shard_map/ppermute | solution.py:26
  113.4 1.2 collective-permute-done.14
  114.5 1.6 %collective-permute-done.15 = f32[288,128]{1,0:T(8,128)S(1)} collective-permute-done((f32[288,128]{1,0:T(8,128)S(1)}, f32[288,128]{1,0:T(8,128)S(1)}, u32[]{:S(2)}, u32[]{:S(2)}) %collective-permute-start.15) | collective-permute-done | bytes 147488 | tf_op jit(solution)/shard_map/ppermute | solution.py:26
  116.3 6.1 %collective-permute-start.16 = (f32[1152,128]{1,0:T(8,128)S(1)}, f32[1152,128]{1,0:T(8,128)S(1)}, u32[]{:S(2)}, u32[]{:S(2)}) collective-permute-start(f32[1152,128]{1,0:T(8,128)S(1)} %get-tuple-element.23), channel_id=1, source_target_pairs={{0,1},{1,0},{2,3},{3,2},{4,5},{5,4},{6,7},{7,6},{8,9},{9,8},{10,11... | collective-permute-start | bytes 1769480 | tf_op jit(solution)/shard_map/ppermute | solution.py:26
  122.5 1.3 convolution_bitcast_fusion.1
  123.8 2.4 %fusion.8 = bf16[128,32,64]{0,2,1:T(8,128)(2,1)S(1)} fusion(f32[128,32,64]{0,2,1:T(8,128)S(1)} %convolution_bitcast_fusion.1, f32[3,32,64,128]{3,2,1,0:T(8,128)} %copy-done.1, f32[128,32]{0,1:T(8,128)S(1)} %copy.126, f32[32]{0:T(128)S(1)} %copy-done.31, f32[32]{0:T(128)S(1)} %copy-done.29, f32[32]{0:T(128)S(1)} %copy-done.27, pred[]{:T(512)S(6)} %gt.24, ...), kind=kOutput, calls=%fused_computation.32 | convolution fusion | flops 70254592 | bytes 4768131 | tf_op jit(solution)/shard_map/tn,hpn->thp/dot_general | solution.py:185
  127.5 1.4 %copy.134 = f32[128,2304]{1,0:T(8,128)} copy(f32[128,2304]{0,1:T(8,128)S(1)} %fusion.11) | data formatting | bytes 2359296
  (156 shorter events, 25.0 us)
Async XLA Ops:
  0.6 28.6 %copy-start = (bf16[128,2304]{1,0:T(8,128)(2,1)S(1)}, bf16[128,2304]{1,0:T(8,128)(2,1)}, u32[]{:S(2)}) copy-start(bf16[128,2304]{1,0:T(8,128)(2,1)} %param.11) | copy-start | bytes 1769476
  0.6 13.8 %copy-start.16 = (s32[4096]{0:T(1024)S(1)}, s32[4096]{0:T(1024)}, u32[]{:S(2)}) copy-start(s32[4096]{0:T(1024)} %param.10) | copy-start | bytes 49156
  3.6 13.8 %all-to-all-start = ((f32[32,1,16]{2,1,0:T(1,128)}), f32[32,1,16]{2,1,0:T(1,128)S(1)}, u32[]{:S(2)}, u32[]{:S(2)}) async-start(f32[32,1,16]{2,1,0:T(1,128)} %copy.114), calls=%async_computation | async-start | bytes 32768 | tf_op jit(solution)/shard_map/all_to_all | solution.py:91
  14.6 17.4 %copy-start.21 = (f32[128]{0:T(128)}, f32[128]{0:T(128)S(1)}, u32[]{:S(2)}) copy-start(f32[128]{0:T(128)S(1)} %add_multiply_fusion) | copy-start | bytes 1540
  20.1 53.5 %collective-permute-start = (f32[128,2048]{0,1:T(8,128)}, f32[128,2048]{0,1:T(8,128)}, u32[]{:S(2)}, u32[]{:S(2)}) collective-permute-start(f32[128,2048]{0,1:T(8,128)} %convert_bitcast_fusion), channel_id=1, source_target_pairs={{24,16},{8,0},{25,17},{9,1},{26,18},{10,2},{27,19},{11,3},{28,20},... | collective-permute-start | bytes 3145736 | tf_op jit(solution)/shard_map/ppermute | solution.py:156
  21.4 52.2 %collective-permute-start.1 = (f32[128,2048]{0,1:T(8,128)}, f32[128,2048]{0,1:T(8,128)}, u32[]{:S(2)}, u32[]{:S(2)}) collective-permute-start(f32[128,2048]{0,1:T(8,128)} %convert_bitcast_fusion), channel_id=1, source_target_pairs={{24,8},{16,0},{25,9},{17,1},{26,10},{18,2},{27,11},{19,3},{28,12},... | collective-permute-start | bytes 3145736 | tf_op jit(solution)/shard_map/ppermute | solution.py:157
  22.7 50.9 %collective-permute-start.2 = (f32[128,2048]{0,1:T(8,128)}, f32[128,2048]{0,1:T(8,128)}, u32[]{:S(2)}, u32[]{:S(2)}) collective-permute-start(f32[128,2048]{0,1:T(8,128)} %convert_bitcast_fusion), channel_id=1, source_target_pairs={{16,8},{24,0},{17,9},{25,1},{18,10},{26,2},{19,11},{27,3},{20,12},... | collective-permute-start | bytes 3145736 | tf_op jit(solution)/shard_map/ppermute | solution.py:158
  24.8 1.4 %copy-start.32 = (bf16[128,32]{0,1:T(8,128)(2,1)S(1)}, bf16[128,32]{0,1:T(8,128)(2,1)}, u32[]{:S(2)}) copy-start(bf16[128,32]{0,1:T(8,128)(2,1)} %param.12) | copy-start | bytes 24580
  24.8 1.4 %copy-start.33 = (f32[32]{0:T(128)S(1)}, f32[32]{0:T(128)}, u32[]{:S(2)}) copy-start(f32[32]{0:T(128)} %param.13) | copy-start | bytes 388
  24.8 3.4 %copy-start.23 = (f32[32]{0:T(128)S(1)}, f32[32]{0:T(128)}, u32[]{:S(2)}) copy-start(f32[32]{0:T(128)} %param.14) | copy-start | bytes 388
  30.9 2.5 %copy-start.24 = (f32[1,128]{1,0:T(1,128)}, f32[1,128]{1,0:T(1,128)S(1)}, u32[]{:S(2)}) copy-start(f32[1,128]{1,0:T(1,128)S(1)} %constant_dynamic-slice_fusion.7) | copy-start | bytes 1540
  32.0 1.4 %copy-start.11 = (f32[128,32]{0,1:T(8,128)}, f32[128,32]{0,1:T(8,128)S(1)}, u32[]{:S(2)}) copy-start(f32[128,32]{0,1:T(8,128)S(1)} %get-tuple-element.54) | copy-start | bytes 49156
  42.6 6.6 %copy-start.4 = (f32[4,128,32]{2,1,0:T(8,128)S(1)}, f32[4,128,32]{2,1,0:T(8,128)}, u32[]{:S(2)}) copy-start(f32[4,128,32]{2,1,0:T(8,128)} %exp.40) | copy-start | bytes 196612
  63.2 3.6 %copy-start.7 = (f32[128,32]{1,0:T(8,128)S(1)}, f32[128,32]{1,0:T(8,128)}, u32[]{:S(2)}) copy-start(f32[128,32]{1,0:T(8,128)} %exp.39) | copy-start | bytes 49156
  68.6 2.0 %copy-start.30 = (f32[32]{0:T(128)}, f32[32]{0:T(128)S(1)}, u32[]{:S(2)}) copy-start(f32[32]{0:T(128)S(1)} %get-tuple-element.50) | copy-start | bytes 388
  68.6 7.6 %copy-start.26 = (f32[32]{0:T(128)}, f32[32]{0:T(128)S(1)}, u32[]{:S(2)}) copy-start(f32[32]{0:T(128)S(1)} %get-tuple-element.52) | copy-start | bytes 388
  68.6 7.9 %copy-start.28 = (f32[32]{0:T(128)}, f32[32]{0:T(128)S(1)}, u32[]{:S(2)}) copy-start(f32[32]{0:T(128)S(1)} %get-tuple-element.51) | copy-start | bytes 388
  68.6 2.0 %copy-start.15 = (f32[128,128]{0,1:T(8,128)S(1)}, f32[128,128]{0,1:T(8,128)}, u32[]{:S(2)}) copy-start(f32[128,128]{0,1:T(8,128)} %fusion.70) | copy-start | bytes 196612
  70.6 1.6 %copy-start.1 = (f32[3,32,64,128]{3,2,1,0:T(8,128)}, f32[3,32,64,128]{3,2,1,0:T(8,128)S(1)}, u32[]{:S(2)}) copy-start(f32[3,32,64,128]{3,2,1,0:T(8,128)S(1)} %fusion.54) | copy-start | bytes 9437188
  70.6 1.6 %copy-start.12 = (f32[128,128]{0,1:T(8,128)S(1)}, f32[128,128]{0,1:T(8,128)}, u32[]{:S(2)}) copy-start(f32[128,128]{0,1:T(8,128)} %fusion.73) | copy-start | bytes 196612
  70.7 1.6 %copy-start.17 = (f32[32,128]{1,0:T(8,128)S(1)}, f32[32,128]{1,0:T(8,128)}, u32[]{:S(2)}) copy-start(f32[32,128]{1,0:T(8,128)} %copy.119) | copy-start | bytes 49156
  70.7 1.6 %copy-start.19 = (pred[128,128]{0,1:T(8,128)(4,1)S(1)}, pred[128,128]{0,1:T(8,128)(4,1)}, u32[]{:S(2)}) copy-start(pred[128,128]{0,1:T(8,128)(4,1)} %iota_compare_fusion) | copy-start | bytes 49156
  70.7 1.6 %copy-start.34 = (f32[32,128]{1,0:T(8,128)S(1)}, f32[32,128]{1,0:T(8,128)}, u32[]{:S(2)}) copy-start(f32[32,128]{1,0:T(8,128)} %get-tuple-element.53) | copy-start | bytes 49156
  72.3 1.4 %copy-start.8 = (f32[128,32]{0,1:T(8,128)S(1)}, f32[128,32]{0,1:T(8,128)}, u32[]{:S(2)}) copy-start(f32[128,32]{0,1:T(8,128)} %copy.129) | copy-start | bytes 49156
  72.3 1.4 %copy-start.9 = (f32[128,32]{0,1:T(8,128)S(1)}, f32[128,32]{0,1:T(8,128)}, u32[]{:S(2)}) copy-start(f32[128,32]{0,1:T(8,128)} %copy.130) | copy-start | bytes 49156
  76.5 1.4 %copy-start.5 = (bf16[128,2048]{0,1:T(8,128)(2,1)S(1)}, bf16[128,2048]{0,1:T(8,128)(2,1)}, u32[]{:S(2)}) copy-start(bf16[128,2048]{0,1:T(8,128)(2,1)} %copy.116) | copy-start | bytes 1572868
  76.5 1.4 %copy-start.14 = (f32[128,128]{0,1:T(8,128)S(1)}, f32[128,128]{0,1:T(8,128)}, u32[]{:S(2)}) copy-start(f32[128,128]{0,1:T(8,128)} %fusion.75) | copy-start | bytes 196612
  76.8 1.5 %copy-start.22 = (f32[128]{0:T(128)S(1)}, f32[128]{0:T(128)}, u32[]{:S(2)}) copy-start(f32[128]{0:T(128)} %copy-done.21) | copy-start | bytes 1540
  76.8 1.5 %copy-start.25 = (f32[1,128]{1,0:T(1,128)S(1)}, f32[1,128]{1,0:T(1,128)}, u32[]{:S(2)}) copy-start(f32[1,128]{1,0:T(1,128)} %copy-done.24) | copy-start | bytes 1540
  78.9 2.3 %collective-permute-start.3 = (f32[1152,128]{1,0:T(8,128)S(1)}, f32[1152,128]{1,0:T(8,128)S(1)}, u32[]{:S(2)}, u32[]{:S(2)}) collective-permute-start(f32[1152,128]{1,0:T(8,128)S(1)} %constant_dynamic-slice_fusion.6), channel_id=1, source_target_pairs={{0,1},{1,0},{2,3},{3,2},{4,5},{5,4},{6,7},{7,6},{8,9},{9,8},{10,11... | collective-permute-start | bytes 1769480 | tf_op jit(solution)/shard_map/ppermute | solution.py:26
  81.3 7.8 %collective-permute-start.4 = (f32[288,128]{1,0:T(8,128)S(1)}, f32[288,128]{1,0:T(8,128)S(1)}, u32[]{:S(2)}, u32[]{:S(2)}) collective-permute-start(f32[288,128]{1,0:T(8,128)S(1)} %get-tuple-element.29), channel_id=1, source_target_pairs={{0,8},{8,0},{16,24},{24,16},{1,9},{9,1},{17,25},{25,17},{2,10},{10... | collective-permute-start | bytes 442376 | tf_op jit(solution)/shard_map/ppermute | solution.py:26
  84.7 10.2 %collective-permute-start.5 = (f32[288,128]{1,0:T(8,128)S(1)}, f32[288,128]{1,0:T(8,128)S(1)}, u32[]{:S(2)}, u32[]{:S(2)}) collective-permute-start(f32[288,128]{1,0:T(8,128)S(1)} %get-tuple-element.31), channel_id=1, source_target_pairs={{0,16},{8,24},{16,0},{24,8},{1,17},{9,25},{17,1},{25,9},{2,18},{10... | collective-permute-start | bytes 442376 | tf_op jit(solution)/shard_map/ppermute | solution.py:26
  89.1 6.7 %collective-permute-start.6 = (f32[288,128]{1,0:T(8,128)S(1)}, f32[288,128]{1,0:T(8,128)S(1)}, u32[]{:S(2)}, u32[]{:S(2)}) collective-permute-start(f32[288,128]{1,0:T(8,128)S(1)} %get-tuple-element.30), channel_id=1, source_target_pairs={{0,24},{8,16},{16,8},{24,0},{1,25},{9,17},{17,9},{25,1},{2,26},{10... | collective-permute-start | bytes 442376 | tf_op jit(solution)/shard_map/ppermute | solution.py:26
  95.9 3.6 %collective-permute-start.7 = (f32[72,128]{1,0:T(8,128)S(1)}, f32[72,128]{1,0:T(8,128)S(1)}, u32[]{:S(2)}, u32[]{:S(2)}) collective-permute-start(f32[72,128]{1,0:T(8,128)S(1)} %get-tuple-element.41), channel_id=1, source_target_pairs={{0,2},{1,3},{2,0},{3,1},{4,6},{5,7},{6,4},{7,5},{8,10},{9,11},{10,... | collective-permute-start | bytes 110600 | tf_op jit(solution)/shard_map/ppermute | solution.py:26
  96.2 3.7 %collective-permute-start.8 = (f32[72,128]{1,0:T(8,128)S(1)}, f32[72,128]{1,0:T(8,128)S(1)}, u32[]{:S(2)}, u32[]{:S(2)}) collective-permute-start(f32[72,128]{1,0:T(8,128)S(1)} %get-tuple-element.43), channel_id=1, source_target_pairs={{0,4},{1,5},{2,6},{3,7},{4,0},{5,1},{6,2},{7,3},{8,12},{9,13},{10,... | collective-permute-start | bytes 110600 | tf_op jit(solution)/shard_map/ppermute | solution.py:26
  96.5 4.7 %collective-permute-start.9 = (f32[72,128]{1,0:T(8,128)S(1)}, f32[72,128]{1,0:T(8,128)S(1)}, u32[]{:S(2)}, u32[]{:S(2)}) collective-permute-start(f32[72,128]{1,0:T(8,128)S(1)} %get-tuple-element.42), channel_id=1, source_target_pairs={{0,6},{1,7},{2,4},{3,5},{4,2},{5,3},{6,0},{7,1},{8,14},{9,15},{10,... | collective-permute-start | bytes 110600 | tf_op jit(solution)/shard_map/ppermute | solution.py:26
  101.2 3.6 %collective-permute-start.10 = (f32[72,128]{1,0:T(8,128)S(1)}, f32[72,128]{1,0:T(8,128)S(1)}, u32[]{:S(2)}, u32[]{:S(2)}) collective-permute-start(f32[72,128]{1,0:T(8,128)S(1)} %add_add_fusion.1), channel_id=1, source_target_pairs={{0,2},{1,3},{2,0},{3,1},{4,6},{5,7},{6,4},{7,5},{8,10},{9,11},{10,... | collective-permute-start | bytes 110600 | tf_op jit(solution)/shard_map/ppermute | solution.py:26
  101.3 4.5 %collective-permute-start.11 = (f32[72,128]{1,0:T(8,128)S(1)}, f32[72,128]{1,0:T(8,128)S(1)}, u32[]{:S(2)}, u32[]{:S(2)}) collective-permute-start(f32[72,128]{1,0:T(8,128)S(1)} %add_add_fusion.1), channel_id=1, source_target_pairs={{0,4},{1,5},{2,6},{3,7},{4,0},{5,1},{6,2},{7,3},{8,12},{9,13},{10,... | collective-permute-start | bytes 110600 | tf_op jit(solution)/shard_map/ppermute | solution.py:26
  104.4 4.7 %collective-permute-start.12 = (f32[72,128]{1,0:T(8,128)S(1)}, f32[72,128]{1,0:T(8,128)S(1)}, u32[]{:S(2)}, u32[]{:S(2)}) collective-permute-start(f32[72,128]{1,0:T(8,128)S(1)} %add_add_fusion.1), channel_id=1, source_target_pairs={{0,6},{1,7},{2,4},{3,5},{4,2},{5,3},{6,0},{7,1},{8,14},{9,15},{10,... | collective-permute-start | bytes 110600 | tf_op jit(solution)/shard_map/ppermute | solution.py:26
  109.2 13.2 %copy-start.6 = (bf16[128,2048]{0,1:T(8,128)(2,1)S(1)}, bf16[128,2048]{0,1:T(8,128)(2,1)}, u32[]{:S(2)}) copy-start(bf16[128,2048]{0,1:T(8,128)(2,1)} %copy.116) | copy-start | bytes 1572868
  109.2 13.2 %copy-start.13 = (f32[128,128]{0,1:T(8,128)S(1)}, f32[128,128]{0,1:T(8,128)}, u32[]{:S(2)}) copy-start(f32[128,128]{0,1:T(8,128)} %fusion.73) | copy-start | bytes 196612
  109.2 13.2 %copy-start.18 = (f32[32,128]{1,0:T(8,128)S(1)}, f32[32,128]{1,0:T(8,128)}, u32[]{:S(2)}) copy-start(f32[32,128]{1,0:T(8,128)} %copy.119) | copy-start | bytes 49156
  109.2 13.2 %copy-start.20 = (pred[128,128]{0,1:T(8,128)(4,1)S(1)}, pred[128,128]{0,1:T(8,128)(4,1)}, u32[]{:S(2)}) copy-start(pred[128,128]{0,1:T(8,128)(4,1)} %iota_compare_fusion) | copy-start | bytes 49156
  109.2 13.2 %copy-start.35 = (f32[32,128]{1,0:T(8,128)S(1)}, f32[32,128]{1,0:T(8,128)}, u32[]{:S(2)}) copy-start(f32[32,128]{1,0:T(8,128)} %get-tuple-element.53) | copy-start | bytes 49156
  109.2 4.1 %collective-permute-start.13 = (f32[288,128]{1,0:T(8,128)S(1)}, f32[288,128]{1,0:T(8,128)S(1)}, u32[]{:S(2)}, u32[]{:S(2)}) collective-permute-start(f32[288,128]{1,0:T(8,128)S(1)} %get-tuple-element.36), channel_id=1, source_target_pairs={{0,8},{8,0},{16,24},{24,16},{1,9},{9,1},{17,25},{25,17},{2,10},{10... | collective-permute-start | bytes 442376 | tf_op jit(solution)/shard_map/ppermute | solution.py:26
  110.5 4.0 %collective-permute-start.14 = (f32[288,128]{1,0:T(8,128)S(1)}, f32[288,128]{1,0:T(8,128)S(1)}, u32[]{:S(2)}, u32[]{:S(2)}) collective-permute-start(f32[288,128]{1,0:T(8,128)S(1)} %get-tuple-element.36), channel_id=1, source_target_pairs={{0,16},{8,24},{16,0},{24,8},{1,17},{9,25},{17,1},{25,9},{2,18},{10... | collective-permute-start | bytes 442376 | tf_op jit(solution)/shard_map/ppermute | solution.py:26
  111.0 5.1 %collective-permute-start.15 = (f32[288,128]{1,0:T(8,128)S(1)}, f32[288,128]{1,0:T(8,128)S(1)}, u32[]{:S(2)}, u32[]{:S(2)}) collective-permute-start(f32[288,128]{1,0:T(8,128)S(1)} %get-tuple-element.36), channel_id=1, source_target_pairs={{0,24},{8,16},{16,8},{24,0},{1,25},{9,17},{17,9},{25,1},{2,26},{10... | collective-permute-start | bytes 442376 | tf_op jit(solution)/shard_map/ppermute | solution.py:26
  116.3 10.9 %collective-permute-start.16 = (f32[1152,128]{1,0:T(8,128)S(1)}, f32[1152,128]{1,0:T(8,128)S(1)}, u32[]{:S(2)}, u32[]{:S(2)}) collective-permute-start(f32[1152,128]{1,0:T(8,128)S(1)} %get-tuple-element.23), channel_id=1, source_target_pairs={{0,1},{1,0},{2,3},{3,2},{4,5},{5,4},{6,7},{7,6},{8,9},{9,8},{10,11... | collective-permute-start | bytes 1769480 | tf_op jit(solution)/shard_map/ppermute | solution.py:26
  (6 other events, 6.9 us)

commit v22 on v20

--- a/solution.py
+++ b/solution.py
@@ -154,7 +154,11 @@
     if n_blocks == 4:
         along_x = lax.ppermute(sent, "tm", [(3, 2), (1, 0)])
         along_y = lax.ppermute(sent, "tm", [(3, 1), (2, 0)])
-        diagonal = lax.ppermute(sent, "tm", [(2, 1), (3, 0)])
+        half_rows = tok_rows // 2
+        direct = lax.ppermute(sent[:half_rows], "tm", [(2, 1), (3, 0)])
+        held, state_in = lax.optimization_barrier((along_y[half_rows:], state_in))
+        relayed = lax.ppermute(held, "tm", [(1, 0), (0, 1)])
+        diagonal = jnp.concatenate([direct, relayed])
         seen = [
             along_x,
             jnp.where(my_block == 1, diagonal, along_y),

time: 127 us -> 147 us (1.16)
  local copies, waits for them, and re-layouts: 27.9 us -> 43.8 us
  other arithmetic: 14.9 us -> 19.9 us
  matrix products: 24.8 us -> 23.3 us
  starting transfers between devices: 35.5 us -> 37 us
    ppermute x1 -> x2, starting transfers between devices: 1.29 us -> 6.35 us  [the longest x1 5.07 us: on_device(): relayed = lax.ppermute(held, 'tm', [(1, 0), (0, 1)])]
    slice x1 -> x3, local copies, waits for them, and re-layouts: 0.08 us -> 4.99 us  [the longest x1 2.58 us: on_device(): held, state_in = lax.optimization_barrier((along_y[half_rows:], state_in))]
    ppermute x0 -> x2, local copies, waits for them, and re-layouts: none -> 4.74 us  [the longest x1 2.38 us: on_device(): relayed = lax.ppermute(held, 'tm', [(1, 0), (0, 1)])]
    ppermute x14, starting transfers between devices: 24.5 us -> 20.7 us  [exchange(): return lax.ppermute(value, axis, pairs)]
    optimization_barrier x0 -> x1, local copies, waits for them, and re-layouts: none -> 2.35 us  [on_device(): held, state_in = lax.optimization_barrier((along_y[half_rows:], state_in))]
    dot_general x1, matrix products: 1.31 us -> 3.41 us  [on_device(): jnp.einsum('hts,thp->shp', weights, grad_heads, preferred_element_type=fl)]
    dot_general x1, matrix products: 2.39 us -> 0.29 us  [on_device(): jnp.einsum('tn,hpn->thp', c_proj, state_half, preferred_element_type=fl)]
    dot_general x1, matrix products: 1.29 us -> 3.33 us  [on_device(): jnp.einsum('hts,shp->thp', weights, x_heads, preferred_element_type=fl)]
  transfers between devices with their start and end apart: 18 -> 19, of which waited for: 11 -> 12; matrix products, arithmetic and copies ran while one was open for 42% -> 46% of each run, Pallas kernels for 0% -> 0%
where the time goes in v22:
time: 147 us; the launch traced here: 145 us
  local copies, waits for them, and re-layouts  43.8 us (30%)
  starting transfers between devices  37 us (25%)
  matrix products  23.3 us (16%)
  waiting for transfers between devices  20.1 us (14%)
  other arithmetic  19.9 us (14%)
    ppermute x14, starting transfers between devices, exchange(): return lax.ppermute(value, axis, pairs)  20.7 us
    ppermute x14, waiting for transfers between devices, exchange(): return lax.ppermute(value, axis, pairs)  17.3 us
    all_to_all x1, starting transfers between devices, on_device(): lax.all_to_all(outgoing, ('tm', 'series'), split_axis=0, concat_axis=1, t...  7.1 us
    mul x4, local copies, waits for them, and re-layouts, on_device(): later_weighted = (later * head_all[k][:, :, None]).astype(half)  6.13 us
    unnamed x71, local copies, waits for them, and re-layouts  5.33 us
    ppermute x1, starting transfers between devices, on_device(): relayed = lax.ppermute(held, 'tm', [(1, 0), (0, 1)])  5.07 us
    convert_element_type x1, local copies, waits for them, and re-layouts, on_device(): xw_all = (x_all[:earlier] * tail_all[:earlier, :, :, None]).astype(half)  3.53 us
    dot_general x1, matrix products, on_device(): jnp.einsum('hts,thp->shp', weights, grad_heads, preferred_element_type=fl)  3.41 us
  transfers between devices with their start and end apart: 19, of which 12 were waited for; matrix products, arithmetic and copies ran while one was open for 46% of the time, Pallas kernels for 0%

profile of v22, /device:TPU:1, one launch (start us, length us, event | category | flops | bytes accessed | tf_op | source)
XLA Modules:
  0.0 145.4 jit_solution(9058269609875848147)
XLA Ops:
  1.6 1.3 gather_fusion
  3.6 7.1 %all-to-all-start = ((f32[32,1,16]{2,1,0:T(1,128)}), f32[32,1,16]{2,1,0:T(1,128)S(1)}, u32[]{:S(2)}, u32[]{:S(2)}) async-start(f32[32,1,16]{2,1,0:T(1,128)} %copy.120), calls=%async_computation | async-start | bytes 32768 | tf_op jit(solution)/shard_map/all_to_all | solution.py:91
  12.1 1.3 copy.121
  14.7 2.7 %all-to-all-done = f32[32,1,16]{2,1,0:T(1,128)S(1)} async-done(((f32[32,1,16]{2,1,0:T(1,128)}), f32[32,1,16]{2,1,0:T(1,128)S(1)}, u32[]{:S(2)}, u32[]{:S(2)}) %all-to-all-start) | async-done | bytes 2080 | tf_op jit(solution)/shard_map/all_to_all | solution.py:91
  18.7 1.5 convert_reduce_fusion
  20.9 1.3 fusion
  25.4 1.4 collective-permute-start
  26.8 1.5 %collective-permute-start.1 = (f32[128,2048]{0,1:T(8,128)}, f32[128,2048]{0,1:T(8,128)}, u32[]{:S(2)}, u32[]{:S(2)}) collective-permute-start(f32[128,2048]{0,1:T(8,128)} %bitcast_convert_fusion), channel_id=1, source_target_pairs={{24,16},{8,0},{25,17},{9,1},{26,18},{10,2},{27,19},{11,3},{28,20},... | collective-permute-start | bytes 3145736 | tf_op jit(solution)/shard_map/ppermute | solution.py:155
  28.3 1.6 %convolution_convert_fusion = bf16[512,2304]{1,0:T(8,128)(2,1)S(1)} fusion(bf16[128,2304]{1,0:T(8,128)(2,1)S(1)} %copy-done, f32[128]{0:T(128)S(1)} %add_multiply_fusion, f32[512]{0:T(512)S(1)} %bitcast.236), kind=kOutput, calls=%fused_computation.4 | convolution fusion | flops 303300608 | bytes 2951680 | tf_op jit(solution)/shard_map/dot_general | solution.py:128
  35.1 1.6 %copy.131 = f32[3,128,32]{1,2,0:T(8,128)} copy(f32[3,128,32]{2,1,0:T(8,128)} %slice_multiply_fusion) | data formatting | bytes 98304 | tf_op jit(solution)/shard_map/slice | solution.py:140
  36.7 2.1 %slice_convert_fusion = f32[3,128,2048]{2,1,0:T(8,128)} fusion(bf16[4,128,2304]{2,1,0:T(8,128)(2,1)S(1)} %bitcast.201), kind=kLoop, calls=%fused_computation.14 | loop fusion | flops 786432 | bytes 4718592 | tf_op jit(solution)/shard_map/convert_element_type | solution.py:140
  38.8 3.5 %copy.129 = f32[3,128,2048]{1,2,0:T(8,128)} copy(f32[3,128,2048]{2,1,0:T(8,128)} %slice_convert_fusion) | data formatting | bytes 6291456 | tf_op jit(solution)/shard_map/convert_element_type | solution.py:140
  42.4 1.4 multiply_bitcast_fusion
  43.8 1.6 %slice_bitcast_fusion.5 = (f32[128,32]{1,0:T(8,128)}, f32[128,32]{1,0:T(8,128)}, f32[128,32]{1,0:T(8,128)}) fusion(f32[4,128,32]{2,1,0:T(8,128)} %exp.40), kind=kLoop, calls=%fused_computation.104 | loop fusion | bytes 98304 | tf_op jit(solution)/shard_map/mul | solution.py:170
  45.4 1.3 negate_multiply_fusion.1
  46.7 1.4 copy.124
  48.1 1.6 %reduce_window_sum.39 = f32[128,32]{1,0:T(8,128)} reduce-window(f32[128,32]{1,0:T(8,128)} %copy.124, f32[]{:T(128)} %constant.174.clone.1), window={size=128x1 pad=127_0x0_0}, to_apply=%region_3.4 | reduce-window | flops 520192 | bytes 32772 | tf_op jit(solution)/shard_map/jit(cumsum)/reduce_window_sum | solution.py:123
  50.6 2.1 %copy.122 = bf16[128,2048]{0,1:T(8,128)(2,1)} copy(bf16[128,2048]{1,0:T(8,128)(2,1)} %slice.157) | data formatting | bytes 1048576 | tf_op jit(solution)/shard_map/slice | solution.py:119
  52.7 2.8 %fusion.2 = bf16[128,128]{0,1:T(8,128)(2,1)S(1)} fusion(bf16[128,32,64]{0,2,1:T(8,128)(2,1)} %bitcast.217, bf16[128,32,64]{0,2,1:T(8,128)(2,1)} %bitcast.207, f32[32,128]{1,0:T(8,128)} %get-tuple-element.57, f32[32,128]{1,0:T(8,128)S(1)} %copy.125, pred[128,128]{0,1:T(8,128)(4,1)} %iota_compare_fusion), kind=kOutput, calls=%fused_computation.10 | convolution fusion | flops 70238208 | bytes 1130496 | tf_op jit(solution)/shard_map/thp,shp->hts/dot_general | solution.py:198
  57.0 1.6 %fusion.19 = bf16[32,64,128]{2,1,0:T(8,128)(2,1)} fusion(f32[3,32,64,128]{3,2,1,0:T(8,128)S(1)} %fusion.3, f32[32]{0:T(128)S(1)} %copy-done.30, f32[32]{0:T(128)S(1)} %copy-done.24, f32[32]{0:T(128)S(1)} %copy-done.22, pred[]{:T(512)S(6)} %gt.24, pred[]{:T(512)S(6)} %gt.23, pred[]{:T(512)S(6)} %gt.22), kind=kLoop, calls=%fused_computation.47 | loop fusion | flops 2097152 | bytes 3670403 | tf_op jit(solution)/shard_map/jit(_where)/select_n | solution.py:148
  59.5 2.3 %copy.135 = f32[64,2048]{1,0:T(8,128)} copy(f32[64,2048]{0,1:T(8,128)} %bitcast.199) | data formatting | bytes 1048576 | tf_op jit(solution)/shard_map/slice | solution.py:158
  61.8 1.3 collective-permute-start.2
  65.2 2.6 %slice.160 = f32[64,2048]{0,1:T(8,128)} slice(f32[128,2048]{0,1:T(8,128)} %collective-permute-done), slice={[64:128], [0:2048]} | slice | bytes 1048576 | tf_op jit(solution)/shard_map/slice | solution.py:159
  67.8 2.3 %copy.136 = f32[64,2048]{1,0:T(8,128)} copy(f32[64,2048]{0,1:T(8,128)} %slice.160) | data formatting | bytes 1048576 | tf_op jit(solution)/shard_map/optimization_barrier | solution.py:159
  70.1 5.1 %collective-permute-start.3 = (f32[64,2048]{1,0:T(8,128)}, f32[64,2048]{1,0:T(8,128)}, u32[]{:S(2)}, u32[]{:S(2)}) collective-permute-start(f32[64,2048]{1,0:T(8,128)} %copy.136), channel_id=1, source_target_pairs={{8,0},{0,8},{9,1},{1,9},{10,2},{2,10},{11,3},{3,11},{12,4},{4,12},... | collective-permute-start | bytes 1572872 | tf_op jit(solution)/shard_map/ppermute | solution.py:160
  75.2 1.4 exponential_multiply_fusion
  76.6 1.5 %exp.39 = f32[128,32]{1,0:T(8,128)} exponential(f32[128,32]{1,0:T(8,128)} %reduce_window_sum.39) | non-fusion elementwise | bytes 32768 | tf_op jit(solution)/shard_map/exp | solution.py:125
  78.1 1.5 %copy.139 = f32[128,32]{0,1:T(8,128)} copy(f32[128,32]{1,0:T(8,128)} %get-tuple-element.38) | data formatting | bytes 32768 | tf_op jit(solution)/shard_map/mul | solution.py:170
  79.6 1.5 %copy.140 = f32[128,32]{0,1:T(8,128)} copy(f32[128,32]{1,0:T(8,128)} %get-tuple-element.37) | data formatting | bytes 32768 | tf_op jit(solution)/shard_map/mul | solution.py:170
  81.1 1.5 %copy.141 = f32[128,32]{0,1:T(8,128)} copy(f32[128,32]{1,0:T(8,128)} %get-tuple-element.36) | data formatting | bytes 32768 | tf_op jit(solution)/shard_map/mul | solution.py:170
  83.5 3.4 %convolution_bitcast_fusion = f32[128,32,64]{0,2,1:T(8,128)} fusion(bf16[128,32,64]{0,2,1:T(8,128)(2,1)} %bitcast.208, f32[32,128]{1,0:T(8,128)} %get-tuple-element.57, f32[32,128]{1,0:T(8,128)} %copy-done.17, f32[128,128]{0,1:T(8,128)} %fusion.69, pred[128,128]{0,1:T(8,128)(4,1)} %iota_compare_fusion), kind=kOutput, calls=%fused_computation.28 | convolution fusion | flops 70254592 | bytes 1687552 | tf_op jit(solution)/shard_map/hts,thp->shp/dot_general | solution.py:192
  86.9 2.4 %copy.137 = f32[64,2048]{0,1:T(8,128)} copy(f32[64,2048]{1,0:T(8,128)} %collective-permute-done.2) | data formatting | bytes 1048576 | tf_op jit(solution)/shard_map/ppermute | solution.py:158
  89.3 2.2 %fusion.17 = bf16[128,128]{0,1:T(8,128)(2,1)} fusion(f32[128,128]{0,1:T(8,128)} %fusion.66, bf16[128,32,64]{0,2,1:T(8,128)(2,1)} %bitcast.209, f32[128,32]{0,1:T(8,128)S(1)} %copy.132, bf16[32,64,128]{2,1,0:T(8,128)(2,1)} %fusion.19), kind=kOutput, calls=%fused_computation.43 | convolution fusion | flops 67928064 | bytes 1163264 | tf_op jit(solution)/shard_map/thp,hpn->tn/dot_general | solution.py:203
  91.5 2.4 %copy.138 = f32[64,2048]{0,1:T(8,128)} copy(f32[64,2048]{1,0:T(8,128)} %collective-permute-done.3) | data formatting | bytes 1048576 | tf_op jit(solution)/shard_map/ppermute | solution.py:160
  93.9 2.7 %fusion.25 = (bf16[128,2048]{0,1:T(8,128)(2,1)S(1)}, bf16[128,2048]{0,1:T(8,128)(2,1)S(1)}, bf16[128,2048]{0,1:T(8,128)(2,1)S(1)}) fusion(f32[128,2048]{0,1:T(8,128)} %collective-permute-done, f32[128,32]{0,1:T(8,128)} %copy.140, pred[]{:T(512)S(6)} %eq.19, f32[64,2048]{0,1:T(8,128)} %copy.138, f32[64,2048]{0,1:T(8,128)} %copy.137, f32[128,32]{0,1:T(8,128)} %copy.139, ...), kind=kLoop, calls=%fused_computation.58 | loop fusion | flops 2621440 | bytes 4767746 | tf_op jit(solution)/shard_map/convert_element_type | solution.py:170
  100.8 1.6 %collective-permute-done.4 = f32[1152,128]{1,0:T(8,128)S(1)} collective-permute-done((f32[1152,128]{1,0:T(8,128)S(1)}, f32[1152,128]{1,0:T(8,128)S(1)}, u32[]{:S(2)}, u32[]{:S(2)}) %collective-permute-start.4) | collective-permute-done | bytes 589856 | tf_op jit(solution)/shard_map/ppermute | solution.py:26
  102.6 3.2 %collective-permute-start.6 = (f32[288,128]{1,0:T(8,128)S(1)}, f32[288,128]{1,0:T(8,128)S(1)}, u32[]{:S(2)}, u32[]{:S(2)}) collective-permute-start(f32[288,128]{1,0:T(8,128)S(1)} %get-tuple-element.35), channel_id=1, source_target_pairs={{0,16},{8,24},{16,0},{24,8},{1,17},{9,25},{17,1},{25,9},{2,18},{10... | collective-permute-start | bytes 442376 | tf_op jit(solution)/shard_map/ppermute | solution.py:26
  105.8 1.9 %collective-permute-done.5 = f32[288,128]{1,0:T(8,128)S(1)} collective-permute-done((f32[288,128]{1,0:T(8,128)S(1)}, f32[288,128]{1,0:T(8,128)S(1)}, u32[]{:S(2)}, u32[]{:S(2)}) %collective-permute-start.5) | collective-permute-done | bytes 147488 | tf_op jit(solution)/shard_map/ppermute | solution.py:26
  107.6 3.9 %collective-permute-done.6 = f32[288,128]{1,0:T(8,128)S(1)} collective-permute-done((f32[288,128]{1,0:T(8,128)S(1)}, f32[288,128]{1,0:T(8,128)S(1)}, u32[]{:S(2)}, u32[]{:S(2)}) %collective-permute-start.6) | collective-permute-done | bytes 147488 | tf_op jit(solution)/shard_map/ppermute | solution.py:26
  113.2 3.0 %collective-permute-start.9 = (f32[72,128]{1,0:T(8,128)S(1)}, f32[72,128]{1,0:T(8,128)S(1)}, u32[]{:S(2)}, u32[]{:S(2)}) collective-permute-start(f32[72,128]{1,0:T(8,128)S(1)} %get-tuple-element.47), channel_id=1, source_target_pairs={{0,4},{1,5},{2,6},{3,7},{4,0},{5,1},{6,2},{7,3},{8,12},{9,13},{10,... | collective-permute-start | bytes 110600 | tf_op jit(solution)/shard_map/ppermute | solution.py:26
  118.5 1.7 %collective-permute-start.12 = (f32[72,128]{1,0:T(8,128)S(1)}, f32[72,128]{1,0:T(8,128)S(1)}, u32[]{:S(2)}, u32[]{:S(2)}) collective-permute-start(f32[72,128]{1,0:T(8,128)S(1)} %add_add_fusion.1), channel_id=1, source_target_pairs={{0,4},{1,5},{2,6},{3,7},{4,0},{5,1},{6,2},{7,3},{8,12},{9,13},{10,... | collective-permute-start | bytes 110600 | tf_op jit(solution)/shard_map/ppermute | solution.py:26
  120.1 1.8 %collective-permute-start.13 = (f32[72,128]{1,0:T(8,128)S(1)}, f32[72,128]{1,0:T(8,128)S(1)}, u32[]{:S(2)}, u32[]{:S(2)}) collective-permute-start(f32[72,128]{1,0:T(8,128)S(1)} %add_add_fusion.1), channel_id=1, source_target_pairs={{0,6},{1,7},{2,4},{3,5},{4,2},{5,3},{6,0},{7,1},{8,14},{9,15},{10,... | collective-permute-start | bytes 110600 | tf_op jit(solution)/shard_map/ppermute | solution.py:26
  122.2 2.5 %collective-permute-done.13 = f32[72,128]{1,0:T(8,128)S(1)} collective-permute-done((f32[72,128]{1,0:T(8,128)S(1)}, f32[72,128]{1,0:T(8,128)S(1)}, u32[]{:S(2)}, u32[]{:S(2)}) %collective-permute-start.13) | collective-permute-done | bytes 36896 | tf_op jit(solution)/shard_map/ppermute | solution.py:26
  127.6 1.3 collective-permute-done.14
  130.0 1.6 %collective-permute-done.16 = f32[288,128]{1,0:T(8,128)S(1)} collective-permute-done((f32[288,128]{1,0:T(8,128)S(1)}, f32[288,128]{1,0:T(8,128)S(1)}, u32[]{:S(2)}, u32[]{:S(2)}) %collective-permute-start.16) | collective-permute-done | bytes 147488 | tf_op jit(solution)/shard_map/ppermute | solution.py:26
  131.8 6.2 %collective-permute-start.17 = (f32[1152,128]{1,0:T(8,128)S(1)}, f32[1152,128]{1,0:T(8,128)}, u32[]{:S(2)}, u32[]{:S(2)}) collective-permute-start(f32[1152,128]{1,0:T(8,128)S(1)} %get-tuple-element.27), channel_id=1, source_target_pairs={{0,1},{1,0},{2,3},{3,2},{4,5},{5,4},{6,7},{7,6},{8,9},{9,8},{10,11... | collective-permute-start | bytes 1769480 | tf_op jit(solution)/shard_map/ppermute | solution.py:26
  138.0 3.3 %convolution_bitcast_fusion.1 = f32[128,32,64]{0,2,1:T(8,128)S(1)} fusion(bf16[128,32,64]{0,2,1:T(8,128)(2,1)} %bitcast.218, f32[32,128]{1,0:T(8,128)S(1)} %copy-done.33, f32[32,128]{1,0:T(8,128)S(1)} %copy-done.18, f32[128,128]{0,1:T(8,128)S(1)} %copy-done.13, pred[128,128]{0,1:T(8,128)(4,1)S(1)} %copy-done.19), kind=kOutput, calls=%fused_computation.31 | convolution fusion | flops 70254592 | bytes 1687552 | tf_op jit(solution)/shard_map/hts,shp->thp/dot_general | solution.py:185
  144.0 1.4 copy.144
  (158 shorter events, 36.0 us)
Async XLA Ops:
  0.6 27.6 %copy-start = (bf16[128,2304]{1,0:T(8,128)(2,1)S(1)}, bf16[128,2304]{1,0:T(8,128)(2,1)}, u32[]{:S(2)}) copy-start(bf16[128,2304]{1,0:T(8,128)(2,1)} %param.11) | copy-start | bytes 1769476
  0.6 13.9 %copy-start.15 = (s32[4096]{0:T(1024)S(1)}, s32[4096]{0:T(1024)}, u32[]{:S(2)}) copy-start(s32[4096]{0:T(1024)} %param.10) | copy-start | bytes 49156
  3.6 13.8 %all-to-all-start = ((f32[32,1,16]{2,1,0:T(1,128)}), f32[32,1,16]{2,1,0:T(1,128)S(1)}, u32[]{:S(2)}, u32[]{:S(2)}) async-start(f32[32,1,16]{2,1,0:T(1,128)} %copy.120), calls=%async_computation | async-start | bytes 32768 | tf_op jit(solution)/shard_map/all_to_all | solution.py:91
  13.4 8.8 %copy-start.2 = (bf16[1,128,2048]{1,2,0:T(8,128)(2,1)}, bf16[1,128,2048]{1,2,0:T(8,128)(2,1)S(1)}, u32[]{:S(2)}) copy-start(bf16[1,128,2048]{1,2,0:T(8,128)(2,1)S(1)} %copy.121) | copy-start | bytes 1572868
  14.6 15.3 %copy-start.20 = (f32[128]{0:T(128)}, f32[128]{0:T(128)S(1)}, u32[]{:S(2)}) copy-start(f32[128]{0:T(128)S(1)} %add_multiply_fusion) | copy-start | bytes 1540
  20.9 1.4 copy-start.31
  20.9 1.4 copy-start.32
  20.9 3.4 %copy-start.26 = (f32[32]{0:T(128)S(1)}, f32[32]{0:T(128)}, u32[]{:S(2)}) copy-start(f32[32]{0:T(128)} %param.14) | copy-start | bytes 388
  24.6 2.2 %copy-start.4 = (f32[4,128,32]{2,1,0:T(8,128)}, f32[4,128,32]{2,1,0:T(8,128)S(1)}, u32[]{:S(2)}) copy-start(f32[4,128,32]{2,1,0:T(8,128)S(1)} %reduce_window_sum.40) | copy-start | bytes 196612
  25.4 9.0 %copy-start.7 = (f32[512,32]{1,0:T(8,128)S(1)}, f32[512,32]{1,0:T(8,128)}, u32[]{:S(2)}) copy-start(f32[512,32]{1,0:T(8,128)} %copy-done.6) | copy-start | bytes 196612
  25.4 39.9 %collective-permute-start = (f32[128,2048]{0,1:T(8,128)}, f32[128,2048]{0,1:T(8,128)}, u32[]{:S(2)}, u32[]{:S(2)}) collective-permute-start(f32[128,2048]{0,1:T(8,128)} %bitcast_convert_fusion), channel_id=1, source_target_pairs={{24,8},{16,0},{25,9},{17,1},{26,10},{18,2},{27,11},{19,3},{28,12},... | collective-permute-start | bytes 3145736 | tf_op jit(solution)/shard_map/ppermute | solution.py:156
  26.8 67.1 %collective-permute-start.1 = (f32[128,2048]{0,1:T(8,128)}, f32[128,2048]{0,1:T(8,128)}, u32[]{:S(2)}, u32[]{:S(2)}) collective-permute-start(f32[128,2048]{0,1:T(8,128)} %bitcast_convert_fusion), channel_id=1, source_target_pairs={{24,16},{8,0},{25,17},{9,1},{26,18},{10,2},{27,19},{11,3},{28,20},... | collective-permute-start | bytes 3145736 | tf_op jit(solution)/shard_map/ppermute | solution.py:155
  28.3 6.1 %copy-start.5 = (f32[4,128,32]{2,1,0:T(8,128)S(1)}, f32[4,128,32]{2,1,0:T(8,128)}, u32[]{:S(2)}) copy-start(f32[4,128,32]{2,1,0:T(8,128)} %copy-done.4) | copy-start | bytes 196612
  29.9 1.0 copy-start.27
  31.0 14.4 %copy-start.12 = (f32[128,32]{0,1:T(8,128)}, f32[128,32]{0,1:T(8,128)S(1)}, u32[]{:S(2)}) copy-start(f32[128,32]{0,1:T(8,128)S(1)} %get-tuple-element.58) | copy-start | bytes 49156
  50.6 4.9 %copy-start.17 = (f32[32,128]{1,0:T(8,128)}, f32[32,128]{1,0:T(8,128)S(1)}, u32[]{:S(2)}) copy-start(f32[32,128]{1,0:T(8,128)S(1)} %copy.125) | copy-start | bytes 49156
  52.7 3.7 %copy-start.1 = (f32[3,128,2048]{1,2,0:T(8,128)S(1)}, f32[3,128,2048]{1,2,0:T(8,128)}, u32[]{:S(2)}) copy-start(f32[3,128,2048]{1,2,0:T(8,128)} %copy.129) | copy-start | bytes 9437188
  52.7 3.7 %copy-start.10 = (f32[3,128,32]{1,2,0:T(8,128)S(1)}, f32[3,128,32]{1,2,0:T(8,128)}, u32[]{:S(2)}) copy-start(f32[3,128,32]{1,2,0:T(8,128)} %copy.131) | copy-start | bytes 147460
  61.8 25.1 %collective-permute-start.2 = (f32[64,2048]{1,0:T(8,128)}, f32[64,2048]{1,0:T(8,128)}, u32[]{:S(2)}, u32[]{:S(2)}) collective-permute-start(f32[64,2048]{1,0:T(8,128)} %copy.135), channel_id=1, source_target_pairs={{16,8},{24,0},{17,9},{25,1},{18,10},{26,2},{19,11},{27,3},{20,12},... | collective-permute-start | bytes 1572872 | tf_op jit(solution)/shard_map/ppermute | solution.py:158
  70.1 21.3 %collective-permute-start.3 = (f32[64,2048]{1,0:T(8,128)}, f32[64,2048]{1,0:T(8,128)}, u32[]{:S(2)}, u32[]{:S(2)}) collective-permute-start(f32[64,2048]{1,0:T(8,128)} %copy.136), channel_id=1, source_target_pairs={{8,0},{0,8},{9,1},{1,9},{10,2},{2,10},{11,3},{3,11},{12,4},{4,12},... | collective-permute-start | bytes 1572872 | tf_op jit(solution)/shard_map/ppermute | solution.py:160
  93.8 2.7 %copy-start.29 = (f32[32]{0:T(128)S(1)}, f32[32]{0:T(128)}, u32[]{:S(2)}) copy-start(f32[32]{0:T(128)} %get-tuple-element.53) | copy-start | bytes 388
  93.8 3.0 %copy-start.23 = (f32[32]{0:T(128)S(1)}, f32[32]{0:T(128)}, u32[]{:S(2)}) copy-start(f32[32]{0:T(128)} %get-tuple-element.56) | copy-start | bytes 388
  96.8 1.2 copy-start.8
  96.8 1.2 copy-start.11
  97.2 1.2 copy-start.9
  97.2 1.2 copy-start.14
  98.1 0.8 copy-start.16
  98.1 0.8 copy-start.21
  98.1 0.8 copy-start.28
  99.5 2.9 %collective-permute-start.4 = (f32[1152,128]{1,0:T(8,128)S(1)}, f32[1152,128]{1,0:T(8,128)S(1)}, u32[]{:S(2)}, u32[]{:S(2)}) collective-permute-start(f32[1152,128]{1,0:T(8,128)S(1)} %constant_dynamic-slice_fusion.6), channel_id=1, source_target_pairs={{0,1},{1,0},{2,3},{3,2},{4,5},{5,4},{6,7},{7,6},{8,9},{9,8},{10,11... | collective-permute-start | bytes 1769480 | tf_op jit(solution)/shard_map/ppermute | solution.py:26
  102.5 5.1 %collective-permute-start.5 = (f32[288,128]{1,0:T(8,128)S(1)}, f32[288,128]{1,0:T(8,128)S(1)}, u32[]{:S(2)}, u32[]{:S(2)}) collective-permute-start(f32[288,128]{1,0:T(8,128)S(1)} %get-tuple-element.33), channel_id=1, source_target_pairs={{0,8},{8,0},{16,24},{24,16},{1,9},{9,1},{17,25},{25,17},{2,10},{10... | collective-permute-start | bytes 442376 | tf_op jit(solution)/shard_map/ppermute | solution.py:26
  102.6 8.9 %collective-permute-start.6 = (f32[288,128]{1,0:T(8,128)S(1)}, f32[288,128]{1,0:T(8,128)S(1)}, u32[]{:S(2)}, u32[]{:S(2)}) collective-permute-start(f32[288,128]{1,0:T(8,128)S(1)} %get-tuple-element.35), channel_id=1, source_target_pairs={{0,16},{8,24},{16,0},{24,8},{1,17},{9,25},{17,1},{25,9},{2,18},{10... | collective-permute-start | bytes 442376 | tf_op jit(solution)/shard_map/ppermute | solution.py:26
  105.8 6.8 %collective-permute-start.7 = (f32[288,128]{1,0:T(8,128)S(1)}, f32[288,128]{1,0:T(8,128)S(1)}, u32[]{:S(2)}, u32[]{:S(2)}) collective-permute-start(f32[288,128]{1,0:T(8,128)S(1)} %get-tuple-element.34), channel_id=1, source_target_pairs={{0,24},{8,16},{16,8},{24,0},{1,25},{9,17},{17,9},{25,1},{2,26},{10... | collective-permute-start | bytes 442376 | tf_op jit(solution)/shard_map/ppermute | solution.py:26
  112.7 4.8 %collective-permute-start.10 = (f32[72,128]{1,0:T(8,128)S(1)}, f32[72,128]{1,0:T(8,128)S(1)}, u32[]{:S(2)}, u32[]{:S(2)}) collective-permute-start(f32[72,128]{1,0:T(8,128)S(1)} %get-tuple-element.46), channel_id=1, source_target_pairs={{0,6},{1,7},{2,4},{3,5},{4,2},{5,3},{6,0},{7,1},{8,14},{9,15},{10,... | collective-permute-start | bytes 110600 | tf_op jit(solution)/shard_map/ppermute | solution.py:26
  113.0 4.4 %collective-permute-start.8 = (f32[72,128]{1,0:T(8,128)S(1)}, f32[72,128]{1,0:T(8,128)S(1)}, u32[]{:S(2)}, u32[]{:S(2)}) collective-permute-start(f32[72,128]{1,0:T(8,128)S(1)} %get-tuple-element.45), channel_id=1, source_target_pairs={{0,2},{1,3},{2,0},{3,1},{4,6},{5,7},{6,4},{7,5},{8,10},{9,11},{10,... | collective-permute-start | bytes 110600 | tf_op jit(solution)/shard_map/ppermute | solution.py:26
  113.2 5.0 %collective-permute-start.9 = (f32[72,128]{1,0:T(8,128)S(1)}, f32[72,128]{1,0:T(8,128)S(1)}, u32[]{:S(2)}, u32[]{:S(2)}) collective-permute-start(f32[72,128]{1,0:T(8,128)S(1)} %get-tuple-element.47), channel_id=1, source_target_pairs={{0,4},{1,5},{2,6},{3,7},{4,0},{5,1},{6,2},{7,3},{8,12},{9,13},{10,... | collective-permute-start | bytes 110600 | tf_op jit(solution)/shard_map/ppermute | solution.py:26
  118.3 3.6 %collective-permute-start.11 = (f32[72,128]{1,0:T(8,128)S(1)}, f32[72,128]{1,0:T(8,128)S(1)}, u32[]{:S(2)}, u32[]{:S(2)}) collective-permute-start(f32[72,128]{1,0:T(8,128)S(1)} %add_add_fusion.1), channel_id=1, source_target_pairs={{0,2},{1,3},{2,0},{3,1},{4,6},{5,7},{6,4},{7,5},{8,10},{9,11},{10,... | collective-permute-start | bytes 110600 | tf_op jit(solution)/shard_map/ppermute | solution.py:26
  118.5 3.7 %collective-permute-start.12 = (f32[72,128]{1,0:T(8,128)S(1)}, f32[72,128]{1,0:T(8,128)S(1)}, u32[]{:S(2)}, u32[]{:S(2)}) collective-permute-start(f32[72,128]{1,0:T(8,128)S(1)} %add_add_fusion.1), channel_id=1, source_target_pairs={{0,4},{1,5},{2,6},{3,7},{4,0},{5,1},{6,2},{7,3},{8,12},{9,13},{10,... | collective-permute-start | bytes 110600 | tf_op jit(solution)/shard_map/ppermute | solution.py:26
  120.1 4.6 %collective-permute-start.13 = (f32[72,128]{1,0:T(8,128)S(1)}, f32[72,128]{1,0:T(8,128)S(1)}, u32[]{:S(2)}, u32[]{:S(2)}) collective-permute-start(f32[72,128]{1,0:T(8,128)S(1)} %add_add_fusion.1), channel_id=1, source_target_pairs={{0,6},{1,7},{2,4},{3,5},{4,2},{5,3},{6,0},{7,1},{8,14},{9,15},{10,... | collective-permute-start | bytes 110600 | tf_op jit(solution)/shard_map/ppermute | solution.py:26
  124.8 13.2 %copy-start.13 = (f32[128,128]{0,1:T(8,128)S(1)}, f32[128,128]{0,1:T(8,128)}, u32[]{:S(2)}) copy-start(f32[128,128]{0,1:T(8,128)} %fusion.69) | copy-start | bytes 196612
  124.8 13.2 %copy-start.18 = (f32[32,128]{1,0:T(8,128)S(1)}, f32[32,128]{1,0:T(8,128)}, u32[]{:S(2)}) copy-start(f32[32,128]{1,0:T(8,128)} %copy-done.17) | copy-start | bytes 49156
  124.8 13.2 %copy-start.19 = (pred[128,128]{0,1:T(8,128)(4,1)S(1)}, pred[128,128]{0,1:T(8,128)(4,1)}, u32[]{:S(2)}) copy-start(pred[128,128]{0,1:T(8,128)(4,1)} %iota_compare_fusion) | copy-start | bytes 49156
  124.9 13.2 %copy-start.33 = (f32[32,128]{1,0:T(8,128)S(1)}, f32[32,128]{1,0:T(8,128)}, u32[]{:S(2)}) copy-start(f32[32,128]{1,0:T(8,128)} %get-tuple-element.57) | copy-start | bytes 49156
  124.9 4.1 %collective-permute-start.14 = (f32[288,128]{1,0:T(8,128)S(1)}, f32[288,128]{1,0:T(8,128)S(1)}, u32[]{:S(2)}, u32[]{:S(2)}) collective-permute-start(f32[288,128]{1,0:T(8,128)S(1)} %get-tuple-element.40), channel_id=1, source_target_pairs={{0,8},{8,0},{16,24},{24,16},{1,9},{9,1},{17,25},{25,17},{2,10},{10... | collective-permute-start | bytes 442376 | tf_op jit(solution)/shard_map/ppermute | solution.py:26
  126.0 4.0 %collective-permute-start.15 = (f32[288,128]{1,0:T(8,128)S(1)}, f32[288,128]{1,0:T(8,128)S(1)}, u32[]{:S(2)}, u32[]{:S(2)}) collective-permute-start(f32[288,128]{1,0:T(8,128)S(1)} %get-tuple-element.40), channel_id=1, source_target_pairs={{0,16},{8,24},{16,0},{24,8},{1,17},{9,25},{17,1},{25,9},{2,18},{10... | collective-permute-start | bytes 442376 | tf_op jit(solution)/shard_map/ppermute | solution.py:26
  126.5 5.1 %collective-permute-start.16 = (f32[288,128]{1,0:T(8,128)S(1)}, f32[288,128]{1,0:T(8,128)S(1)}, u32[]{:S(2)}, u32[]{:S(2)}) collective-permute-start(f32[288,128]{1,0:T(8,128)S(1)} %get-tuple-element.40), channel_id=1, source_target_pairs={{0,24},{8,16},{16,8},{24,0},{1,25},{9,17},{17,9},{25,1},{2,26},{10... | collective-permute-start | bytes 442376 | tf_op jit(solution)/shard_map/ppermute | solution.py:26
  131.8 10.9 %collective-permute-start.17 = (f32[1152,128]{1,0:T(8,128)S(1)}, f32[1152,128]{1,0:T(8,128)}, u32[]{:S(2)}, u32[]{:S(2)}) collective-permute-start(f32[1152,128]{1,0:T(8,128)S(1)} %get-tuple-element.27), channel_id=1, source_target_pairs={{0,1},{1,0},{2,3},{3,2},{4,5},{5,4},{6,7},{7,6},{8,9},{9,8},{10,11... | collective-permute-start | bytes 1769480 | tf_op jit(solution)/shard_map/ppermute | solution.py:26
  138.0 3.3 %copy-start.3 = (bf16[32,64,128]{2,1,0:T(8,128)(2,1)S(1)}, bf16[32,64,128]{2,1,0:T(8,128)(2,1)}, u32[]{:S(2)}) copy-start(bf16[32,64,128]{2,1,0:T(8,128)(2,1)} %fusion.19) | copy-start | bytes 1572868
  (5 other events, 3.4 us)

commit v23 on v20

--- a/solution.py
+++ b/solution.py
@@ -58,7 +58,7 @@
     return [lax.dynamic_index_in_dim(stacked, coord ^ q, 0, keepdims=False) for q in range(size)]
 
 
-def tree_psum(value):
+def tree_psum(value, finish):
     done = []
     for axis, bits in bit_groups():
         if value.shape[0] % (8 << len(bits)) == 0:
@@ -69,9 +69,10 @@
             value = pieces[0]
             for piece in pieces[1:]:
                 value = value + piece
-    for axis, bits in reversed(done):
+    for axis, bits in reversed(done[1:]):
         value = jnp.concatenate(group_round(value, axis, bits, False))
-    return value
+    axis, bits = done[0]
+    return jnp.concatenate(group_round(finish(value).T, axis, bits, False), axis=1)
 
 
 def on_device(codes, owner_slot, edges, w_in, w_dt, dt_bias, decay_rate, grad_out):
@@ -208,8 +209,8 @@
         axis=1,
     )
     local_grad = jnp.einsum("tw,tf->wf", grad_rows, features, preferred_element_type=fl)
-    total_grad = tree_psum(local_grad).T
-    grad_in = total_grad / math.sqrt(series_count * seq_len)
+    scale = math.sqrt(series_count * seq_len)
+    grad_in = tree_psum(local_grad, lambda share: share / scale)
     return (ssd_output, grad_in)
 
 

time: 127 us -> 127 us (level)
    unnamed x73 -> x72, local copies, waits for them, and re-layouts: 5.53 us -> 4.14 us
where the time goes in v23:
time: 127 us; the launch traced here: 126 us
  starting transfers between devices  35.5 us (28%)
  local copies, waits for them, and re-layouts  27 us (21%)
  matrix products  24.8 us (20%)
  waiting for transfers between devices  21.3 us (17%)
  other arithmetic  15.9 us (13%)
  between operations  1.37 us (1%)
    ppermute x14, starting transfers between devices, exchange(): return lax.ppermute(value, axis, pairs)  24.5 us
    ppermute x14, waiting for transfers between devices, exchange(): return lax.ppermute(value, axis, pairs)  18.5 us
    all_to_all x1, starting transfers between devices, on_device(): lax.all_to_all(outgoing, ('tm', 'series'), split_axis=0, concat_axis=1, t...  7.1 us
    mul x4, local copies, waits for them, and re-layouts, on_device(): later_weighted = (later * head_all[k][:, :, None]).astype(half)  4.34 us
    unnamed x72, local copies, waits for them, and re-layouts  4.14 us
    slice x2, local copies, waits for them, and re-layouts, on_device(): x_heads = projected[:, :inner_width].reshape(tok_rows, head_count, head_dim)  3.92 us
    convert_element_type x1, local copies, waits for them, and re-layouts, on_device(): xw_all = (x_all[:earlier] * tail_all[:earlier, :, :, None]).astype(half)  3.56 us
    all_to_all x1, waiting for transfers between devices, on_device(): lax.all_to_all(outgoing, ('tm', 'series'), split_axis=0, concat_axis=1, t...  2.82 us
  transfers between devices with their start and end apart: 18, of which 11 were waited for; matrix products, arithmetic and copies ran while one was open for 42% of the time, Pallas kernels for 0%

profile of v23, /device:TPU:1, one launch (start us, length us, event | category | flops | bytes accessed | tf_op | source)
XLA Modules:
  0.0 125.9 jit_solution(2419207235713545378)
XLA Ops:
  1.6 1.3 %gather_fusion = s32[32,16]{1,0:T(8,128)S(1)} fusion(s32[8,16]{1,0:T(8,128)} %param.8, s32[1024]{0:T(1024)S(1)} %pad_clamp_fusion), kind=kCustom, calls=%fused_computation | custom fusion | bytes 4224 | tf_op jit(solution)/shard_map/jit(_take)/gather | solution.py:91
  3.6 7.1 %all-to-all-start = ((f32[32,1,16]{2,1,0:T(1,128)}), f32[32,1,16]{2,1,0:T(1,128)S(1)}, u32[]{:S(2)}, u32[]{:S(2)}) async-start(f32[32,1,16]{2,1,0:T(1,128)} %copy.117), calls=%async_computation | async-start | bytes 32768 | tf_op jit(solution)/shard_map/all_to_all | solution.py:92
  12.1 1.3 %copy.118 = bf16[1,128,2048]{1,2,0:T(8,128)(2,1)S(1)} copy(bf16[1,128,2048]{2,1,0:T(8,128)(2,1)} %param.15) | data formatting | bytes 1048576 | tf_op args[7]
  13.4 1.0 convert_bitcast_fusion
  14.6 2.8 %all-to-all-done = f32[32,1,16]{2,1,0:T(1,128)S(1)} async-done(((f32[32,1,16]{2,1,0:T(1,128)}), f32[32,1,16]{2,1,0:T(1,128)S(1)}, u32[]{:S(2)}, u32[]{:S(2)}) %all-to-all-start) | async-done | bytes 2080 | tf_op jit(solution)/shard_map/all_to_all | solution.py:92
  18.7 1.5 %convert_reduce_fusion = f32[4096]{0:T(1024)S(1)} fusion(f32[4096]{0:T(1024)S(1)} %get-tuple-element.48, f32[4096]{0:T(1024)S(1)} %convert_element_type.124, f32[512]{0:T(512)S(1)} %le.29), kind=kLoop, calls=%fused_computation.1 | loop fusion | flops 10481664 | bytes 51200 | tf_op jit(solution)/shard_map/reduce_sum | solution.py:98
  20.1 1.3 %collective-permute-start = (f32[128,2048]{0,1:T(8,128)}, f32[128,2048]{0,1:T(8,128)}, u32[]{:S(2)}, u32[]{:S(2)}) collective-permute-start(f32[128,2048]{0,1:T(8,128)} %convert_bitcast_fusion), channel_id=1, source_target_pairs={{24,16},{8,0},{25,17},{9,1},{26,18},{10,2},{27,19},{11,3},{28,20},... | collective-permute-start | bytes 3145736 | tf_op jit(solution)/shard_map/ppermute | solution.py:156
  21.4 1.3 %collective-permute-start.1 = (f32[128,2048]{0,1:T(8,128)}, f32[128,2048]{0,1:T(8,128)}, u32[]{:S(2)}, u32[]{:S(2)}) collective-permute-start(f32[128,2048]{0,1:T(8,128)} %convert_bitcast_fusion), channel_id=1, source_target_pairs={{24,8},{16,0},{25,9},{17,1},{26,10},{18,2},{27,11},{19,3},{28,12},... | collective-permute-start | bytes 3145736 | tf_op jit(solution)/shard_map/ppermute | solution.py:157
  22.7 1.3 %collective-permute-start.2 = (f32[128,2048]{0,1:T(8,128)}, f32[128,2048]{0,1:T(8,128)}, u32[]{:S(2)}, u32[]{:S(2)}) collective-permute-start(f32[128,2048]{0,1:T(8,128)} %convert_bitcast_fusion), channel_id=1, source_target_pairs={{16,8},{24,0},{17,9},{25,1},{18,10},{26,2},{19,11},{27,3},{20,12},... | collective-permute-start | bytes 3145736 | tf_op jit(solution)/shard_map/ppermute | solution.py:158
  24.8 1.3 %fusion = f32[512,12]{0,1:T(8,128)S(1)} fusion(f32[4096]{0:T(1024)S(1)} %get-tuple-element.48, f32[4096]{0:T(1024)S(1)} %convert_element_type.124, f32[512]{0:T(512)S(1)} %le.29, bf16[4096,4]{0,1:T(4,128)(2,1)S(1)} %get-tuple-element.46, bf16[4096,4]{0,1:T(4,128)(2,1)S(1)} %get-tuple-element.45, bf16[4096,4]{0,1:T(4,128)(2,1)S(1)} %get-tuple-element.44), kind=kOutput, calls=%fused_computation.5 | convolution fusion | flops 61112320 | bytes 157696 | tf_op jit(solution)/shard_map/dot_general | solution.py:106
  26.2 1.1 compare_select_fusion
  29.3 1.6 %convolution_convert_fusion = bf16[512,2304]{1,0:T(8,128)(2,1)S(1)} fusion(bf16[128,2304]{1,0:T(8,128)(2,1)S(1)} %copy-done, f32[128]{0:T(128)S(1)} %add_multiply_fusion, f32[512]{0:T(512)S(1)} %bitcast.240), kind=kOutput, calls=%fused_computation.4 | convolution fusion | flops 303300608 | bytes 2951680 | tf_op jit(solution)/shard_map/dot_general | solution.py:129
  30.9 1.0 compare_select_fusion.1
  32.0 1.4 %convolution_convert_fusion.1 = bf16[128,2304]{1,0:T(8,128)(2,1)} fusion(bf16[128,2304]{1,0:T(8,128)(2,1)S(1)} %copy-done, f32[128]{0:T(128)S(1)} %add_multiply_fusion, f32[1,128]{1,0:T(1,128)S(1)} %constant_dynamic-slice_fusion.7), kind=kOutput, calls=%fused_computation.7 | convolution fusion | flops 75825152 | bytes 1180672 | tf_op jit(solution)/shard_map/dot_general | solution.py:119
  36.4 1.5 %fusion.73 = f32[128,128]{0,1:T(8,128)} fusion(bf16[128,2304]{1,0:T(8,128)(2,1)} %convolution_convert_fusion.1), kind=kOutput, calls=%fused_computation.141 | convolution fusion | flops 4194304 | bytes 131072 | tf_op jit(solution)/shard_map/dot_general | solution.py:178
  38.0 1.9 %slice.149 = bf16[128,2048]{1,0:T(8,128)(2,1)} slice(bf16[128,2304]{1,0:T(8,128)(2,1)} %convolution_convert_fusion.1), slice={[0:128], [0:2048]} | slice | bytes 1048576 | tf_op jit(solution)/shard_map/slice | solution.py:120
  40.5 2.0 %copy.119 = bf16[128,2048]{0,1:T(8,128)(2,1)} copy(bf16[128,2048]{1,0:T(8,128)(2,1)} %slice.149) | data formatting | bytes 1048576 | tf_op jit(solution)/shard_map/slice | solution.py:120
  42.6 2.8 %fusion.2 = bf16[128,128]{0,1:T(8,128)(2,1)S(1)} fusion(bf16[128,32,64]{0,2,1:T(8,128)(2,1)} %bitcast.219, bf16[128,32,64]{0,2,1:T(8,128)(2,1)S(1)} %bitcast.207, f32[32,128]{1,0:T(8,128)} %get-tuple-element.53, f32[32,128]{1,0:T(8,128)} %copy.122, pred[128,128]{0,1:T(8,128)(4,1)} %iota_compare_fusion), kind=kOutput, calls=%fused_computation.10 | convolution fusion | flops 70238208 | bytes 1130496 | tf_op jit(solution)/shard_map/thp,shp->hts/dot_general | solution.py:195
  45.3 1.6 %fusion.75 = f32[128,128]{0,1:T(8,128)} fusion(bf16[128,2304]{1,0:T(8,128)(2,1)} %convolution_convert_fusion.1, bf16[128,128]{0,1:T(8,128)(2,1)S(1)} %fusion.2), kind=kOutput, calls=%fused_computation.143 | convolution fusion | flops 4194304 | bytes 131072 | tf_op jit(solution)/shard_map/dot_general | solution.py:197
  46.9 1.6 %fusion.70 = f32[128,128]{0,1:T(8,128)} fusion(bf16[128,2304]{1,0:T(8,128)(2,1)} %convolution_convert_fusion.1, bf16[128,128]{0,1:T(8,128)(2,1)S(1)} %fusion.2), kind=kOutput, calls=%fused_computation.138 | convolution fusion | flops 4194304 | bytes 131072 | tf_op jit(solution)/shard_map/dot_general | solution.py:199
  49.8 1.5 %copy.132 = f32[128,32]{0,1:T(8,128)} copy(f32[128,32]{1,0:T(8,128)} %get-tuple-element.34) | data formatting | bytes 32768 | tf_op jit(solution)/shard_map/mul | solution.py:167
  51.3 1.5 %copy.133 = f32[128,32]{0,1:T(8,128)} copy(f32[128,32]{1,0:T(8,128)} %get-tuple-element.33) | data formatting | bytes 32768 | tf_op jit(solution)/shard_map/mul | solution.py:167
  54.1 1.7 %slice_multiply_fusion = f32[3,128,32]{2,1,0:T(8,128)} fusion(f32[4,128,32]{2,1,0:T(8,128)} %bitcast.216, f32[4,128,32]{2,1,0:T(8,128)} %copy-done.2, f32[3,32]{1,0:T(4,128)S(1)} %bitcast.238), kind=kLoop, calls=%fused_computation.86 | loop fusion | flops 24576 | bytes 147840 | tf_op jit(solution)/shard_map/mul | solution.py:138
  55.8 1.7 %copy.128 = f32[3,128,32]{1,2,0:T(8,128)} copy(f32[3,128,32]{2,1,0:T(8,128)} %slice_multiply_fusion) | data formatting | bytes 98304 | tf_op jit(solution)/shard_map/slice | solution.py:141
  57.5 2.1 %slice_convert_fusion = f32[3,128,2048]{2,1,0:T(8,128)} fusion(bf16[4,128,2304]{2,1,0:T(8,128)(2,1)S(1)} %bitcast.202), kind=kLoop, calls=%fused_computation.14 | loop fusion | flops 786432 | bytes 4718592 | tf_op jit(solution)/shard_map/convert_element_type | solution.py:141
  59.6 3.6 %copy.126 = f32[3,128,2048]{1,2,0:T(8,128)} copy(f32[3,128,2048]{2,1,0:T(8,128)} %slice_convert_fusion) | data formatting | bytes 6291456 | tf_op jit(solution)/shard_map/convert_element_type | solution.py:141
  65.0 2.5 %fusion.3 = f32[3,32,64,128]{3,2,1,0:T(8,128)S(1)} fusion(f32[3,128,32,64]{1,3,2,0:T(8,128)} %bitcast.201, f32[3,128,32]{1,2,0:T(8,128)} %copy.128, bf16[4,128,2304]{2,1,0:T(8,128)(2,1)S(1)} %bitcast.203), kind=kOutput, calls=%fused_computation.13 | convolution fusion | flops 202899456 | bytes 6438912 | tf_op jit(solution)/shard_map/bthp,btn->bhpn/dot_general | solution.py:142
  69.2 1.3 %convolution_bitcast_fusion = f32[128,32,64]{0,2,1:T(8,128)S(1)} fusion(bf16[128,32,64]{0,2,1:T(8,128)(2,1)S(1)} %bitcast.208, f32[32,128]{1,0:T(8,128)S(1)} %copy-done.33, f32[32,128]{1,0:T(8,128)S(1)} %copy-done.17, f32[128,128]{0,1:T(8,128)S(1)} %copy-done.12, pred[128,128]{0,1:T(8,128)(4,1)S(1)} %copy-done.18), kind=kOutput, calls=%fused_computation.28 | convolution fusion | flops 70254592 | bytes 1687552 | tf_op jit(solution)/shard_map/hts,thp->shp/dot_general | solution.py:189
  70.5 2.2 %fusion.19 = (bf16[128,2048]{0,1:T(8,128)(2,1)S(1)}, bf16[128,2048]{0,1:T(8,128)(2,1)S(1)}, bf16[128,2048]{0,1:T(8,128)(2,1)S(1)}) fusion(f32[128,2048]{0,1:T(8,128)} %collective-permute-done.2, f32[128,2048]{0,1:T(8,128)} %collective-permute-done.1, f32[128,32]{0,1:T(8,128)S(1)} %copy-done.9, pred[]{:T(512)S(6)} %eq.19, f32[128,32]{0,1:T(8,128)S(1)} %copy-done.8, ...), kind=kLoop, calls=%fused_computation.50 | loop fusion | flops 2359296 | bytes 4767746 | tf_op jit(solution)/shard_map/convert_element_type | solution.py:167
  73.7 1.1 fusion.12
  75.8 1.2 collective-permute-start.3
  77.0 1.6 %collective-permute-done.3 = f32[1152,128]{1,0:T(8,128)S(1)} collective-permute-done((f32[1152,128]{1,0:T(8,128)S(1)}, f32[1152,128]{1,0:T(8,128)S(1)}, u32[]{:S(2)}, u32[]{:S(2)}) %collective-permute-start.3) | collective-permute-done | bytes 589856 | tf_op jit(solution)/shard_map/ppermute | solution.py:26
  78.8 3.1 %collective-permute-start.4 = (f32[288,128]{1,0:T(8,128)S(1)}, f32[288,128]{1,0:T(8,128)S(1)}, u32[]{:S(2)}, u32[]{:S(2)}) collective-permute-start(f32[288,128]{1,0:T(8,128)S(1)} %get-tuple-element.29), channel_id=1, source_target_pairs={{0,8},{8,0},{16,24},{24,16},{1,9},{9,1},{17,25},{25,17},{2,10},{10... | collective-permute-start | bytes 442376 | tf_op jit(solution)/shard_map/ppermute | solution.py:26
  81.9 4.1 %collective-permute-start.5 = (f32[288,128]{1,0:T(8,128)S(1)}, f32[288,128]{1,0:T(8,128)S(1)}, u32[]{:S(2)}, u32[]{:S(2)}) collective-permute-start(f32[288,128]{1,0:T(8,128)S(1)} %get-tuple-element.31), channel_id=1, source_target_pairs={{0,16},{8,24},{16,0},{24,8},{1,17},{9,25},{17,1},{25,9},{2,18},{10... | collective-permute-start | bytes 442376 | tf_op jit(solution)/shard_map/ppermute | solution.py:26
  86.0 5.8 %collective-permute-done.5 = f32[288,128]{1,0:T(8,128)S(1)} collective-permute-done((f32[288,128]{1,0:T(8,128)S(1)}, f32[288,128]{1,0:T(8,128)S(1)}, u32[]{:S(2)}, u32[]{:S(2)}) %collective-permute-start.5) | collective-permute-done | bytes 147488 | tf_op jit(solution)/shard_map/ppermute | solution.py:26
  93.3 3.0 %collective-permute-start.9 = (f32[72,128]{1,0:T(8,128)S(1)}, f32[72,128]{1,0:T(8,128)S(1)}, u32[]{:S(2)}, u32[]{:S(2)}) collective-permute-start(f32[72,128]{1,0:T(8,128)S(1)} %get-tuple-element.42), channel_id=1, source_target_pairs={{0,6},{1,7},{2,4},{3,5},{4,2},{5,3},{6,0},{7,1},{8,14},{9,15},{10,... | collective-permute-start | bytes 110600 | tf_op jit(solution)/shard_map/ppermute | solution.py:26
  96.7 1.4 %collective-permute-done.9 = f32[72,128]{1,0:T(8,128)S(1)} collective-permute-done((f32[72,128]{1,0:T(8,128)S(1)}, f32[72,128]{1,0:T(8,128)S(1)}, u32[]{:S(2)}, u32[]{:S(2)}) %collective-permute-start.9) | collective-permute-done | bytes 36896 | tf_op jit(solution)/shard_map/ppermute | solution.py:26
  98.2 3.1 %collective-permute-start.11 = (f32[72,128]{1,0:T(8,128)S(1)}, f32[72,128]{1,0:T(8,128)S(1)}, u32[]{:S(2)}, u32[]{:S(2)}) collective-permute-start(f32[72,128]{1,0:T(8,128)S(1)} %add_add_fusion.1), channel_id=1, source_target_pairs={{0,4},{1,5},{2,6},{3,7},{4,0},{5,1},{6,2},{7,3},{8,12},{9,13},{10,... | collective-permute-start | bytes 110600 | tf_op jit(solution)/shard_map/ppermute | solution.py:26
  102.6 3.4 %collective-permute-done.12 = f32[72,128]{1,0:T(8,128)S(1)} collective-permute-done((f32[72,128]{1,0:T(8,128)S(1)}, f32[72,128]{1,0:T(8,128)S(1)}, u32[]{:S(2)}, u32[]{:S(2)}) %collective-permute-start.12) | collective-permute-done | bytes 36896 | tf_op jit(solution)/shard_map/ppermute | solution.py:26
  106.1 1.3 %collective-permute-start.13 = (f32[288,128]{1,0:T(8,128)S(1)}, f32[288,128]{1,0:T(8,128)S(1)}, u32[]{:S(2)}, u32[]{:S(2)}) collective-permute-start(f32[288,128]{1,0:T(8,128)S(1)} %get-tuple-element.36), channel_id=1, source_target_pairs={{0,8},{8,0},{16,24},{24,16},{1,9},{9,1},{17,25},{25,17},{2,10},{10... | collective-permute-start | bytes 442376 | tf_op jit(solution)/shard_map/ppermute | solution.py:26
  108.8 1.4 %collective-permute-done.13 = f32[288,128]{1,0:T(8,128)S(1)} collective-permute-done((f32[288,128]{1,0:T(8,128)S(1)}, f32[288,128]{1,0:T(8,128)S(1)}, u32[]{:S(2)}, u32[]{:S(2)}) %collective-permute-start.13) | collective-permute-done | bytes 147488 | tf_op jit(solution)/shard_map/ppermute | solution.py:26
  110.3 1.2 collective-permute-done.14
  111.4 1.6 %collective-permute-done.15 = f32[288,128]{1,0:T(8,128)S(1)} collective-permute-done((f32[288,128]{1,0:T(8,128)S(1)}, f32[288,128]{1,0:T(8,128)S(1)}, u32[]{:S(2)}, u32[]{:S(2)}) %collective-permute-start.15) | collective-permute-done | bytes 147488 | tf_op jit(solution)/shard_map/ppermute | solution.py:26
  113.2 6.1 %collective-permute-start.16 = (f32[128,1152]{0,1:T(8,128)S(1)}, f32[128,1152]{0,1:T(8,128)S(1)}, u32[]{:S(2)}, u32[]{:S(2)}) collective-permute-start(f32[128,1152]{0,1:T(8,128)S(1)} %get-tuple-element.23), channel_id=1, source_target_pairs={{0,1},{1,0},{2,3},{3,2},{4,5},{5,4},{6,7},{7,6},{8,9},{9,8},{10,11... | collective-permute-start | bytes 1769480 | tf_op jit(solution)/shard_map/ppermute | solution.py:26
  119.3 1.3 %convolution_bitcast_fusion.1 = f32[128,32,64]{0,2,1:T(8,128)S(1)} fusion(bf16[128,32,64]{0,2,1:T(8,128)(2,1)S(1)} %bitcast.221, f32[32,128]{1,0:T(8,128)S(1)} %copy-done.34, f32[32,128]{1,0:T(8,128)S(1)} %copy-done.17, f32[128,128]{0,1:T(8,128)S(1)} %copy-done.13, pred[128,128]{0,1:T(8,128)(4,1)S(1)} %copy-done.19), kind=kOutput, calls=%fused_computation.31 | convolution fusion | flops 70254592 | bytes 1687552 | tf_op jit(solution)/shard_map/hts,shp->thp/dot_general | solution.py:182
  120.6 2.4 %fusion.10 = bf16[128,32,64]{0,2,1:T(8,128)(2,1)S(1)} fusion(f32[128,32,64]{0,2,1:T(8,128)S(1)} %convolution_bitcast_fusion.1, f32[3,32,64,128]{3,2,1,0:T(8,128)} %copy-done.1, f32[128,32]{0,1:T(8,128)S(1)} %copy.129, f32[32]{0:T(128)S(1)} %copy-done.30, f32[32]{0:T(128)S(1)} %copy-done.28, f32[32]{0:T(128)S(1)} %copy-done.26, pred[]{:T(512)S(6)} %gt.24, ...), kind=kOutput, calls=%fused_computation.34 | convolution fusion | flops 70254592 | bytes 4768131 | tf_op jit(solution)/shard_map/tn,hpn->thp/dot_general | solution.py:185
  123.0 1.0 copy.138
  124.8 1.1 pad_maximum_fusion
  (154 shorter events, 24.6 us)
Async XLA Ops:
  0.6 28.6 %copy-start = (bf16[128,2304]{1,0:T(8,128)(2,1)S(1)}, bf16[128,2304]{1,0:T(8,128)(2,1)}, u32[]{:S(2)}) copy-start(bf16[128,2304]{1,0:T(8,128)(2,1)} %param.11) | copy-start | bytes 1769476
  0.6 13.8 %copy-start.16 = (s32[4096]{0:T(1024)S(1)}, s32[4096]{0:T(1024)}, u32[]{:S(2)}) copy-start(s32[4096]{0:T(1024)} %param.10) | copy-start | bytes 49156
  3.6 13.8 %all-to-all-start = ((f32[32,1,16]{2,1,0:T(1,128)}), f32[32,1,16]{2,1,0:T(1,128)S(1)}, u32[]{:S(2)}, u32[]{:S(2)}) async-start(f32[32,1,16]{2,1,0:T(1,128)} %copy.117), calls=%async_computation | async-start | bytes 32768 | tf_op jit(solution)/shard_map/all_to_all | solution.py:92
  14.6 17.4 %copy-start.20 = (f32[128]{0:T(128)}, f32[128]{0:T(128)S(1)}, u32[]{:S(2)}) copy-start(f32[128]{0:T(128)S(1)} %add_multiply_fusion) | copy-start | bytes 1540
  20.1 50.3 %collective-permute-start = (f32[128,2048]{0,1:T(8,128)}, f32[128,2048]{0,1:T(8,128)}, u32[]{:S(2)}, u32[]{:S(2)}) collective-permute-start(f32[128,2048]{0,1:T(8,128)} %convert_bitcast_fusion), channel_id=1, source_target_pairs={{24,16},{8,0},{25,17},{9,1},{26,18},{10,2},{27,19},{11,3},{28,20},... | collective-permute-start | bytes 3145736 | tf_op jit(solution)/shard_map/ppermute | solution.py:156
  21.4 49.1 %collective-permute-start.1 = (f32[128,2048]{0,1:T(8,128)}, f32[128,2048]{0,1:T(8,128)}, u32[]{:S(2)}, u32[]{:S(2)}) collective-permute-start(f32[128,2048]{0,1:T(8,128)} %convert_bitcast_fusion), channel_id=1, source_target_pairs={{24,8},{16,0},{25,9},{17,1},{26,10},{18,2},{27,11},{19,3},{28,12},... | collective-permute-start | bytes 3145736 | tf_op jit(solution)/shard_map/ppermute | solution.py:157
  22.7 47.8 %collective-permute-start.2 = (f32[128,2048]{0,1:T(8,128)}, f32[128,2048]{0,1:T(8,128)}, u32[]{:S(2)}, u32[]{:S(2)}) collective-permute-start(f32[128,2048]{0,1:T(8,128)} %convert_bitcast_fusion), channel_id=1, source_target_pairs={{16,8},{24,0},{17,9},{25,1},{18,10},{26,2},{19,11},{27,3},{20,12},... | collective-permute-start | bytes 3145736 | tf_op jit(solution)/shard_map/ppermute | solution.py:158
  24.8 1.4 %copy-start.31 = (bf16[128,32]{0,1:T(8,128)(2,1)S(1)}, bf16[128,32]{0,1:T(8,128)(2,1)}, u32[]{:S(2)}) copy-start(bf16[128,32]{0,1:T(8,128)(2,1)} %param.12) | copy-start | bytes 24580
  24.8 1.4 %copy-start.32 = (f32[32]{0:T(128)S(1)}, f32[32]{0:T(128)}, u32[]{:S(2)}) copy-start(f32[32]{0:T(128)} %param.13) | copy-start | bytes 388
  24.8 3.4 %copy-start.22 = (f32[32]{0:T(128)S(1)}, f32[32]{0:T(128)}, u32[]{:S(2)}) copy-start(f32[32]{0:T(128)} %param.14) | copy-start | bytes 388
  30.9 2.4 %copy-start.23 = (f32[1,128]{1,0:T(1,128)}, f32[1,128]{1,0:T(1,128)S(1)}, u32[]{:S(2)}) copy-start(f32[1,128]{1,0:T(1,128)S(1)} %constant_dynamic-slice_fusion.7) | copy-start | bytes 1540
  32.0 1.4 %copy-start.11 = (f32[128,32]{0,1:T(8,128)}, f32[128,32]{0,1:T(8,128)S(1)}, u32[]{:S(2)}) copy-start(f32[128,32]{0,1:T(8,128)S(1)} %get-tuple-element.54) | copy-start | bytes 49156
  42.6 6.6 %copy-start.4 = (f32[4,128,32]{2,1,0:T(8,128)S(1)}, f32[4,128,32]{2,1,0:T(8,128)}, u32[]{:S(2)}) copy-start(f32[4,128,32]{2,1,0:T(8,128)} %exp.40) | copy-start | bytes 196612
  59.6 3.6 %copy-start.7 = (f32[128,32]{1,0:T(8,128)S(1)}, f32[128,32]{1,0:T(8,128)}, u32[]{:S(2)}) copy-start(f32[128,32]{1,0:T(8,128)} %exp.39) | copy-start | bytes 49156
  65.0 2.5 %copy-start.29 = (f32[32]{0:T(128)}, f32[32]{0:T(128)S(1)}, u32[]{:S(2)}) copy-start(f32[32]{0:T(128)S(1)} %get-tuple-element.50) | copy-start | bytes 388
  65.0 8.1 %copy-start.25 = (f32[32]{0:T(128)}, f32[32]{0:T(128)S(1)}, u32[]{:S(2)}) copy-start(f32[32]{0:T(128)S(1)} %get-tuple-element.52) | copy-start | bytes 388
  65.0 8.4 %copy-start.27 = (f32[32]{0:T(128)}, f32[32]{0:T(128)S(1)}, u32[]{:S(2)}) copy-start(f32[32]{0:T(128)S(1)} %get-tuple-element.51) | copy-start | bytes 388
  65.0 2.5 %copy-start.15 = (f32[128,128]{0,1:T(8,128)S(1)}, f32[128,128]{0,1:T(8,128)}, u32[]{:S(2)}) copy-start(f32[128,128]{0,1:T(8,128)} %fusion.70) | copy-start | bytes 196612
  67.5 1.6 %copy-start.1 = (f32[3,32,64,128]{3,2,1,0:T(8,128)}, f32[3,32,64,128]{3,2,1,0:T(8,128)S(1)}, u32[]{:S(2)}) copy-start(f32[3,32,64,128]{3,2,1,0:T(8,128)S(1)} %fusion.3) | copy-start | bytes 9437188
  67.5 1.6 %copy-start.12 = (f32[128,128]{0,1:T(8,128)S(1)}, f32[128,128]{0,1:T(8,128)}, u32[]{:S(2)}) copy-start(f32[128,128]{0,1:T(8,128)} %fusion.73) | copy-start | bytes 196612
  67.5 1.6 %copy-start.17 = (f32[32,128]{1,0:T(8,128)S(1)}, f32[32,128]{1,0:T(8,128)}, u32[]{:S(2)}) copy-start(f32[32,128]{1,0:T(8,128)} %copy.122) | copy-start | bytes 49156
  67.5 1.6 %copy-start.18 = (pred[128,128]{0,1:T(8,128)(4,1)S(1)}, pred[128,128]{0,1:T(8,128)(4,1)}, u32[]{:S(2)}) copy-start(pred[128,128]{0,1:T(8,128)(4,1)} %iota_compare_fusion) | copy-start | bytes 49156
  67.5 1.6 %copy-start.33 = (f32[32,128]{1,0:T(8,128)S(1)}, f32[32,128]{1,0:T(8,128)}, u32[]{:S(2)}) copy-start(f32[32,128]{1,0:T(8,128)} %get-tuple-element.53) | copy-start | bytes 49156
  69.1 1.4 %copy-start.8 = (f32[128,32]{0,1:T(8,128)S(1)}, f32[128,32]{0,1:T(8,128)}, u32[]{:S(2)}) copy-start(f32[128,32]{0,1:T(8,128)} %copy.132) | copy-start | bytes 49156
  69.2 1.4 %copy-start.9 = (f32[128,32]{0,1:T(8,128)S(1)}, f32[128,32]{0,1:T(8,128)}, u32[]{:S(2)}) copy-start(f32[128,32]{0,1:T(8,128)} %copy.133) | copy-start | bytes 49156
  69.2 1.4 %copy-start.10 = (f32[128,32]{0,1:T(8,128)S(1)}, f32[128,32]{0,1:T(8,128)}, u32[]{:S(2)}) copy-start(f32[128,32]{0,1:T(8,128)} %copy.134) | copy-start | bytes 49156
  73.4 1.4 %copy-start.5 = (bf16[128,2048]{0,1:T(8,128)(2,1)S(1)}, bf16[128,2048]{0,1:T(8,128)(2,1)}, u32[]{:S(2)}) copy-start(bf16[128,2048]{0,1:T(8,128)(2,1)} %copy.119) | copy-start | bytes 1572868
  73.4 1.4 %copy-start.14 = (f32[128,128]{0,1:T(8,128)S(1)}, f32[128,128]{0,1:T(8,128)}, u32[]{:S(2)}) copy-start(f32[128,128]{0,1:T(8,128)} %fusion.75) | copy-start | bytes 196612
  73.7 1.5 %copy-start.21 = (f32[128]{0:T(128)S(1)}, f32[128]{0:T(128)}, u32[]{:S(2)}) copy-start(f32[128]{0:T(128)} %copy-done.20) | copy-start | bytes 1540
  73.7 1.5 %copy-start.24 = (f32[1,128]{1,0:T(1,128)S(1)}, f32[1,128]{1,0:T(1,128)}, u32[]{:S(2)}) copy-start(f32[1,128]{1,0:T(1,128)} %copy-done.23) | copy-start | bytes 1540
  75.8 2.9 %collective-permute-start.3 = (f32[1152,128]{1,0:T(8,128)S(1)}, f32[1152,128]{1,0:T(8,128)S(1)}, u32[]{:S(2)}, u32[]{:S(2)}) collective-permute-start(f32[1152,128]{1,0:T(8,128)S(1)} %constant_dynamic-slice_fusion.6), channel_id=1, source_target_pairs={{0,1},{1,0},{2,3},{3,2},{4,5},{5,4},{6,7},{7,6},{8,9},{9,8},{10,11... | collective-permute-start | bytes 1769480 | tf_op jit(solution)/shard_map/ppermute | solution.py:26
  78.8 7.3 %collective-permute-start.4 = (f32[288,128]{1,0:T(8,128)S(1)}, f32[288,128]{1,0:T(8,128)S(1)}, u32[]{:S(2)}, u32[]{:S(2)}) collective-permute-start(f32[288,128]{1,0:T(8,128)S(1)} %get-tuple-element.29), channel_id=1, source_target_pairs={{0,8},{8,0},{16,24},{24,16},{1,9},{9,1},{17,25},{25,17},{2,10},{10... | collective-permute-start | bytes 442376 | tf_op jit(solution)/shard_map/ppermute | solution.py:26
  81.9 10.0 %collective-permute-start.5 = (f32[288,128]{1,0:T(8,128)S(1)}, f32[288,128]{1,0:T(8,128)S(1)}, u32[]{:S(2)}, u32[]{:S(2)}) collective-permute-start(f32[288,128]{1,0:T(8,128)S(1)} %get-tuple-element.31), channel_id=1, source_target_pairs={{0,16},{8,24},{16,0},{24,8},{1,17},{9,25},{17,1},{25,9},{2,18},{10... | collective-permute-start | bytes 442376 | tf_op jit(solution)/shard_map/ppermute | solution.py:26
  86.0 6.6 %collective-permute-start.6 = (f32[288,128]{1,0:T(8,128)S(1)}, f32[288,128]{1,0:T(8,128)S(1)}, u32[]{:S(2)}, u32[]{:S(2)}) collective-permute-start(f32[288,128]{1,0:T(8,128)S(1)} %get-tuple-element.30), channel_id=1, source_target_pairs={{0,24},{8,16},{16,8},{24,0},{1,25},{9,17},{17,9},{25,1},{2,26},{10... | collective-permute-start | bytes 442376 | tf_op jit(solution)/shard_map/ppermute | solution.py:26
  92.7 3.6 %collective-permute-start.7 = (f32[72,128]{1,0:T(8,128)S(1)}, f32[72,128]{1,0:T(8,128)S(1)}, u32[]{:S(2)}, u32[]{:S(2)}) collective-permute-start(f32[72,128]{1,0:T(8,128)S(1)} %get-tuple-element.41), channel_id=1, source_target_pairs={{0,2},{1,3},{2,0},{3,1},{4,6},{5,7},{6,4},{7,5},{8,10},{9,11},{10,... | collective-permute-start | bytes 110600 | tf_op jit(solution)/shard_map/ppermute | solution.py:26
  93.0 3.7 %collective-permute-start.8 = (f32[72,128]{1,0:T(8,128)S(1)}, f32[72,128]{1,0:T(8,128)S(1)}, u32[]{:S(2)}, u32[]{:S(2)}) collective-permute-start(f32[72,128]{1,0:T(8,128)S(1)} %get-tuple-element.43), channel_id=1, source_target_pairs={{0,4},{1,5},{2,6},{3,7},{4,0},{5,1},{6,2},{7,3},{8,12},{9,13},{10,... | collective-permute-start | bytes 110600 | tf_op jit(solution)/shard_map/ppermute | solution.py:26
  93.3 4.8 %collective-permute-start.9 = (f32[72,128]{1,0:T(8,128)S(1)}, f32[72,128]{1,0:T(8,128)S(1)}, u32[]{:S(2)}, u32[]{:S(2)}) collective-permute-start(f32[72,128]{1,0:T(8,128)S(1)} %get-tuple-element.42), channel_id=1, source_target_pairs={{0,6},{1,7},{2,4},{3,5},{4,2},{5,3},{6,0},{7,1},{8,14},{9,15},{10,... | collective-permute-start | bytes 110600 | tf_op jit(solution)/shard_map/ppermute | solution.py:26
  98.1 3.6 %collective-permute-start.10 = (f32[72,128]{1,0:T(8,128)S(1)}, f32[72,128]{1,0:T(8,128)S(1)}, u32[]{:S(2)}, u32[]{:S(2)}) collective-permute-start(f32[72,128]{1,0:T(8,128)S(1)} %add_add_fusion.1), channel_id=1, source_target_pairs={{0,2},{1,3},{2,0},{3,1},{4,6},{5,7},{6,4},{7,5},{8,10},{9,11},{10,... | collective-permute-start | bytes 110600 | tf_op jit(solution)/shard_map/ppermute | solution.py:26
  98.2 4.4 %collective-permute-start.11 = (f32[72,128]{1,0:T(8,128)S(1)}, f32[72,128]{1,0:T(8,128)S(1)}, u32[]{:S(2)}, u32[]{:S(2)}) collective-permute-start(f32[72,128]{1,0:T(8,128)S(1)} %add_add_fusion.1), channel_id=1, source_target_pairs={{0,4},{1,5},{2,6},{3,7},{4,0},{5,1},{6,2},{7,3},{8,12},{9,13},{10,... | collective-permute-start | bytes 110600 | tf_op jit(solution)/shard_map/ppermute | solution.py:26
  101.3 4.7 %collective-permute-start.12 = (f32[72,128]{1,0:T(8,128)S(1)}, f32[72,128]{1,0:T(8,128)S(1)}, u32[]{:S(2)}, u32[]{:S(2)}) collective-permute-start(f32[72,128]{1,0:T(8,128)S(1)} %add_add_fusion.1), channel_id=1, source_target_pairs={{0,6},{1,7},{2,4},{3,5},{4,2},{5,3},{6,0},{7,1},{8,14},{9,15},{10,... | collective-permute-start | bytes 110600 | tf_op jit(solution)/shard_map/ppermute | solution.py:26
  106.1 13.2 %copy-start.6 = (bf16[128,2048]{0,1:T(8,128)(2,1)S(1)}, bf16[128,2048]{0,1:T(8,128)(2,1)}, u32[]{:S(2)}) copy-start(bf16[128,2048]{0,1:T(8,128)(2,1)} %copy.119) | copy-start | bytes 1572868
  106.1 13.2 %copy-start.13 = (f32[128,128]{0,1:T(8,128)S(1)}, f32[128,128]{0,1:T(8,128)}, u32[]{:S(2)}) copy-start(f32[128,128]{0,1:T(8,128)} %fusion.73) | copy-start | bytes 196612
  106.1 13.2 %copy-start.19 = (pred[128,128]{0,1:T(8,128)(4,1)S(1)}, pred[128,128]{0,1:T(8,128)(4,1)}, u32[]{:S(2)}) copy-start(pred[128,128]{0,1:T(8,128)(4,1)} %iota_compare_fusion) | copy-start | bytes 49156
  106.1 13.2 %copy-start.34 = (f32[32,128]{1,0:T(8,128)S(1)}, f32[32,128]{1,0:T(8,128)}, u32[]{:S(2)}) copy-start(f32[32,128]{1,0:T(8,128)} %get-tuple-element.53) | copy-start | bytes 49156
  106.1 4.1 %collective-permute-start.13 = (f32[288,128]{1,0:T(8,128)S(1)}, f32[288,128]{1,0:T(8,128)S(1)}, u32[]{:S(2)}, u32[]{:S(2)}) collective-permute-start(f32[288,128]{1,0:T(8,128)S(1)} %get-tuple-element.36), channel_id=1, source_target_pairs={{0,8},{8,0},{16,24},{24,16},{1,9},{9,1},{17,25},{25,17},{2,10},{10... | collective-permute-start | bytes 442376 | tf_op jit(solution)/shard_map/ppermute | solution.py:26
  107.4 4.0 %collective-permute-start.14 = (f32[288,128]{1,0:T(8,128)S(1)}, f32[288,128]{1,0:T(8,128)S(1)}, u32[]{:S(2)}, u32[]{:S(2)}) collective-permute-start(f32[288,128]{1,0:T(8,128)S(1)} %get-tuple-element.36), channel_id=1, source_target_pairs={{0,16},{8,24},{16,0},{24,8},{1,17},{9,25},{17,1},{25,9},{2,18},{10... | collective-permute-start | bytes 442376 | tf_op jit(solution)/shard_map/ppermute | solution.py:26
  107.8 5.1 %collective-permute-start.15 = (f32[288,128]{1,0:T(8,128)S(1)}, f32[288,128]{1,0:T(8,128)S(1)}, u32[]{:S(2)}, u32[]{:S(2)}) collective-permute-start(f32[288,128]{1,0:T(8,128)S(1)} %get-tuple-element.36), channel_id=1, source_target_pairs={{0,24},{8,16},{16,8},{24,0},{1,25},{9,17},{17,9},{25,1},{2,26},{10... | collective-permute-start | bytes 442376 | tf_op jit(solution)/shard_map/ppermute | solution.py:26
  113.2 10.9 %collective-permute-start.16 = (f32[128,1152]{0,1:T(8,128)S(1)}, f32[128,1152]{0,1:T(8,128)S(1)}, u32[]{:S(2)}, u32[]{:S(2)}) collective-permute-start(f32[128,1152]{0,1:T(8,128)S(1)} %get-tuple-element.23), channel_id=1, source_target_pairs={{0,1},{1,0},{2,3},{3,2},{4,5},{5,4},{6,7},{7,6},{8,9},{9,8},{10,11... | collective-permute-start | bytes 1769480 | tf_op jit(solution)/shard_map/ppermute | solution.py:26
  (5 other events, 5.5 us)

commit v24 on v20

--- a/solution.py
+++ b/solution.py
@@ -29,8 +29,8 @@
 def bit_groups():
     tm_bits, series_bits = axis_bits("tm"), axis_bits("series")
     groups = [("series", series_bits[:1])] if series_bits else []
-    for axis, bits in (("tm", tm_bits), ("series", series_bits[1:])):
-        groups += [(axis, bits[i : i + 2]) for i in range(0, len(bits), 2)]
+    groups += [("tm", tm_bits[i : i + 2]) for i in range(0, len(tm_bits), 2)]
+    groups += [("series", [b]) for b in series_bits[1:]]
     return groups
 
 

time: 127 us -> 130 us (1.024)
  waiting for transfers between devices: 21.3 us -> 29 us
  starting transfers between devices: 35.5 us -> 30.7 us
    ppermute x14 -> x12, waiting for transfers between devices: 18.5 us -> 26.1 us  [exchange(): return lax.ppermute(value, axis, pairs)]
    ppermute x14 -> x12, starting transfers between devices: 24.5 us -> 19.7 us  [exchange(): return lax.ppermute(value, axis, pairs)]
    unnamed x73 -> x72, local copies, waits for them, and re-layouts: 5.53 us -> 4.14 us
  transfers between devices with their start and end apart: 18 -> 16, of which waited for: 11 -> 10; matrix products, arithmetic and copies ran while one was open for 42% -> 41% of each run, Pallas kernels for 0% -> 0%
where the time goes in v24:
time: 130 us; the launch traced here: 129 us
  starting transfers between devices  30.7 us (24%)
  waiting for transfers between devices  29 us (22%)
  local copies, waits for them, and re-layouts  27 us (21%)
  matrix products  24.8 us (19%)
  other arithmetic  16 us (12%)
  between operations  1.42 us (1%)
    ppermute x12, waiting for transfers between devices, exchange(): return lax.ppermute(value, axis, pairs)  26.1 us
    ppermute x12, starting transfers between devices, exchange(): return lax.ppermute(value, axis, pairs)  19.7 us
    all_to_all x1, starting transfers between devices, on_device(): lax.all_to_all(outgoing, ('tm', 'series'), split_axis=0, concat_axis=1, t...  7.1 us
    mul x4, local copies, waits for them, and re-layouts, on_device(): later_weighted = (later * head_all[k][:, :, None]).astype(half)  4.36 us
    unnamed x72, local copies, waits for them, and re-layouts  4.14 us
    slice x2, local copies, waits for them, and re-layouts, on_device(): x_heads = projected[:, :inner_width].reshape(tok_rows, head_count, head_dim)  3.92 us
    convert_element_type x1, local copies, waits for them, and re-layouts, on_device(): xw_all = (x_all[:earlier] * tail_all[:earlier, :, :, None]).astype(half)  3.56 us
    all_to_all x1, waiting for transfers between devices, on_device(): lax.all_to_all(outgoing, ('tm', 'series'), split_axis=0, concat_axis=1, t...  2.82 us
  transfers between devices with their start and end apart: 16, of which 10 were waited for; matrix products, arithmetic and copies ran while one was open for 41% of the time, Pallas kernels for 0%

profile of v24, /device:TPU:1, one launch (start us, length us, event | category | flops | bytes accessed | tf_op | source)
XLA Modules:
  0.0 128.8 jit_solution(305845553178877701)
XLA Ops:
  1.6 1.3 gather_fusion
  3.6 7.1 %all-to-all-start = ((f32[32,1,16]{2,1,0:T(1,128)}), f32[32,1,16]{2,1,0:T(1,128)S(1)}, u32[]{:S(2)}, u32[]{:S(2)}) async-start(f32[32,1,16]{2,1,0:T(1,128)} %copy.100), calls=%async_computation | async-start | bytes 32768 | tf_op jit(solution)/shard_map/all_to_all | solution.py:91
  12.1 1.3 %copy.101 = bf16[1,128,2048]{1,2,0:T(8,128)(2,1)S(1)} copy(bf16[1,128,2048]{2,1,0:T(8,128)(2,1)} %param.15) | data formatting | bytes 1048576 | tf_op args[7]
  13.4 1.0 convert_bitcast_fusion
  14.6 2.8 %all-to-all-done = f32[32,1,16]{2,1,0:T(1,128)S(1)} async-done(((f32[32,1,16]{2,1,0:T(1,128)}), f32[32,1,16]{2,1,0:T(1,128)S(1)}, u32[]{:S(2)}, u32[]{:S(2)}) %all-to-all-start) | async-done | bytes 2080 | tf_op jit(solution)/shard_map/all_to_all | solution.py:91
  18.7 1.5 %convert_reduce_fusion = f32[4096]{0:T(1024)S(1)} fusion(f32[4096]{0:T(1024)S(1)} %get-tuple-element.45, f32[4096]{0:T(1024)S(1)} %convert_element_type.124, f32[512]{0:T(512)S(1)} %le.29), kind=kLoop, calls=%fused_computation.1 | loop fusion | flops 10481664 | bytes 51200 | tf_op jit(solution)/shard_map/reduce_sum | solution.py:97
  20.1 1.3 %collective-permute-start = (f32[128,2048]{0,1:T(8,128)}, f32[128,2048]{0,1:T(8,128)}, u32[]{:S(2)}, u32[]{:S(2)}) collective-permute-start(f32[128,2048]{0,1:T(8,128)} %convert_bitcast_fusion), channel_id=1, source_target_pairs={{24,16},{8,0},{25,17},{9,1},{26,18},{10,2},{27,19},{11,3},{28,20},... | collective-permute-start | bytes 3145736 | tf_op jit(solution)/shard_map/ppermute | solution.py:155
  21.4 1.3 %collective-permute-start.1 = (f32[128,2048]{0,1:T(8,128)}, f32[128,2048]{0,1:T(8,128)}, u32[]{:S(2)}, u32[]{:S(2)}) collective-permute-start(f32[128,2048]{0,1:T(8,128)} %convert_bitcast_fusion), channel_id=1, source_target_pairs={{24,8},{16,0},{25,9},{17,1},{26,10},{18,2},{27,11},{19,3},{28,12},... | collective-permute-start | bytes 3145736 | tf_op jit(solution)/shard_map/ppermute | solution.py:156
  22.7 1.3 %collective-permute-start.2 = (f32[128,2048]{0,1:T(8,128)}, f32[128,2048]{0,1:T(8,128)}, u32[]{:S(2)}, u32[]{:S(2)}) collective-permute-start(f32[128,2048]{0,1:T(8,128)} %convert_bitcast_fusion), channel_id=1, source_target_pairs={{16,8},{24,0},{17,9},{25,1},{18,10},{26,2},{19,11},{27,3},{20,12},... | collective-permute-start | bytes 3145736 | tf_op jit(solution)/shard_map/ppermute | solution.py:157
  24.8 1.3 fusion
  26.2 1.1 compare_select_fusion
  29.3 1.6 %convolution_convert_fusion = bf16[512,2304]{1,0:T(8,128)(2,1)S(1)} fusion(bf16[128,2304]{1,0:T(8,128)(2,1)S(1)} %copy-done, f32[128]{0:T(128)S(1)} %add_multiply_fusion, f32[512]{0:T(512)S(1)} %bitcast.239), kind=kOutput, calls=%fused_computation.4 | convolution fusion | flops 303300608 | bytes 2951680 | tf_op jit(solution)/shard_map/dot_general | solution.py:128
  30.9 1.0 compare_select_fusion.1
  31.9 1.4 %convolution_convert_fusion.1 = bf16[128,2304]{1,0:T(8,128)(2,1)} fusion(bf16[128,2304]{1,0:T(8,128)(2,1)S(1)} %copy-done, f32[128]{0:T(128)S(1)} %add_multiply_fusion, f32[1,128]{1,0:T(1,128)S(1)} %constant_dynamic-slice_fusion.6), kind=kOutput, calls=%fused_computation.7 | convolution fusion | flops 75825152 | bytes 1180672 | tf_op jit(solution)/shard_map/dot_general | solution.py:118
  36.4 1.6 %fusion.80 = f32[128,128]{0,1:T(8,128)} fusion(bf16[128,2304]{1,0:T(8,128)(2,1)} %convolution_convert_fusion.1), kind=kOutput, calls=%fused_computation.153 | convolution fusion | flops 4194304 | bytes 131072 | tf_op jit(solution)/shard_map/dot_general | solution.py:177
  38.0 1.9 %slice.149 = bf16[128,2048]{1,0:T(8,128)(2,1)} slice(bf16[128,2304]{1,0:T(8,128)(2,1)} %convolution_convert_fusion.1), slice={[0:128], [0:2048]} | slice | bytes 1048576 | tf_op jit(solution)/shard_map/slice | solution.py:119
  40.5 2.0 %copy.102 = bf16[128,2048]{0,1:T(8,128)(2,1)} copy(bf16[128,2048]{1,0:T(8,128)(2,1)} %slice.149) | data formatting | bytes 1048576 | tf_op jit(solution)/shard_map/slice | solution.py:119
  42.6 2.8 %fusion.2 = bf16[128,128]{0,1:T(8,128)(2,1)S(1)} fusion(bf16[128,32,64]{0,2,1:T(8,128)(2,1)} %bitcast.219, bf16[128,32,64]{0,2,1:T(8,128)(2,1)S(1)} %bitcast.207, f32[32,128]{1,0:T(8,128)} %get-tuple-element.50, f32[32,128]{1,0:T(8,128)} %copy.105, pred[128,128]{0,1:T(8,128)(4,1)} %iota_compare_fusion), kind=kOutput, calls=%fused_computation.10 | convolution fusion | flops 70238208 | bytes 1130496 | tf_op jit(solution)/shard_map/thp,shp->hts/dot_general | solution.py:194
  45.3 1.6 %fusion.82 = f32[128,128]{0,1:T(8,128)} fusion(bf16[128,2304]{1,0:T(8,128)(2,1)} %convolution_convert_fusion.1, bf16[128,128]{0,1:T(8,128)(2,1)S(1)} %fusion.2), kind=kOutput, calls=%fused_computation.155 | convolution fusion | flops 4194304 | bytes 131072 | tf_op jit(solution)/shard_map/dot_general | solution.py:196
  46.9 1.6 %fusion.77 = f32[128,128]{0,1:T(8,128)} fusion(bf16[128,2304]{1,0:T(8,128)(2,1)} %convolution_convert_fusion.1, bf16[128,128]{0,1:T(8,128)(2,1)S(1)} %fusion.2), kind=kOutput, calls=%fused_computation.150 | convolution fusion | flops 4194304 | bytes 131072 | tf_op jit(solution)/shard_map/dot_general | solution.py:198
  49.8 1.5 %copy.115 = f32[128,32]{0,1:T(8,128)} copy(f32[128,32]{1,0:T(8,128)} %get-tuple-element.32) | data formatting | bytes 32768 | tf_op jit(solution)/shard_map/mul | solution.py:166
  51.3 1.5 %copy.116 = f32[128,32]{0,1:T(8,128)} copy(f32[128,32]{1,0:T(8,128)} %get-tuple-element.31) | data formatting | bytes 32768 | tf_op jit(solution)/shard_map/mul | solution.py:166
  54.1 1.7 %slice_multiply_fusion = f32[3,128,32]{2,1,0:T(8,128)} fusion(f32[4,128,32]{2,1,0:T(8,128)} %bitcast.216, f32[4,128,32]{2,1,0:T(8,128)} %copy-done.2, f32[3,32]{1,0:T(4,128)S(1)} %bitcast.237), kind=kLoop, calls=%fused_computation.85 | loop fusion | flops 24576 | bytes 147840 | tf_op jit(solution)/shard_map/mul | solution.py:137
  55.8 1.6 %copy.111 = f32[3,128,32]{1,2,0:T(8,128)} copy(f32[3,128,32]{2,1,0:T(8,128)} %slice_multiply_fusion) | data formatting | bytes 98304 | tf_op jit(solution)/shard_map/slice | solution.py:140
  57.5 2.1 %slice_convert_fusion = f32[3,128,2048]{2,1,0:T(8,128)} fusion(bf16[4,128,2304]{2,1,0:T(8,128)(2,1)S(1)} %bitcast.202), kind=kLoop, calls=%fused_computation.14 | loop fusion | flops 786432 | bytes 4718592 | tf_op jit(solution)/shard_map/convert_element_type | solution.py:140
  59.6 3.6 %copy.109 = f32[3,128,2048]{1,2,0:T(8,128)} copy(f32[3,128,2048]{2,1,0:T(8,128)} %slice_convert_fusion) | data formatting | bytes 6291456 | tf_op jit(solution)/shard_map/convert_element_type | solution.py:140
  65.0 2.5 %fusion.3 = f32[3,32,64,128]{3,2,1,0:T(8,128)S(1)} fusion(f32[3,128,32,64]{1,3,2,0:T(8,128)} %bitcast.201, f32[3,128,32]{1,2,0:T(8,128)} %copy.111, bf16[4,128,2304]{2,1,0:T(8,128)(2,1)S(1)} %bitcast.203), kind=kOutput, calls=%fused_computation.13 | convolution fusion | flops 202899456 | bytes 6438912 | tf_op jit(solution)/shard_map/bthp,btn->bhpn/dot_general | solution.py:141
  69.1 1.3 %convolution_bitcast_fusion = f32[128,32,64]{0,2,1:T(8,128)S(1)} fusion(bf16[128,32,64]{0,2,1:T(8,128)(2,1)S(1)} %bitcast.208, f32[32,128]{1,0:T(8,128)S(1)} %copy-done.33, f32[32,128]{1,0:T(8,128)S(1)} %copy-done.17, f32[128,128]{0,1:T(8,128)S(1)} %copy-done.12, pred[128,128]{0,1:T(8,128)(4,1)S(1)} %copy-done.18), kind=kOutput, calls=%fused_computation.28 | convolution fusion | flops 70254592 | bytes 1687552 | tf_op jit(solution)/shard_map/hts,thp->shp/dot_general | solution.py:188
  70.5 2.2 %fusion.20 = (bf16[128,2048]{0,1:T(8,128)(2,1)S(1)}, bf16[128,2048]{0,1:T(8,128)(2,1)S(1)}, bf16[128,2048]{0,1:T(8,128)(2,1)S(1)}) fusion(f32[128,2048]{0,1:T(8,128)} %collective-permute-done.2, f32[128,2048]{0,1:T(8,128)} %collective-permute-done.1, f32[128,32]{0,1:T(8,128)S(1)} %copy-done.9, pred[]{:T(512)S(6)} %eq.19, f32[128,32]{0,1:T(8,128)S(1)} %copy-done.8, ...), kind=kLoop, calls=%fused_computation.51 | loop fusion | flops 2359296 | bytes 4767746 | tf_op jit(solution)/shard_map/convert_element_type | solution.py:166
  73.7 1.1 fusion.12
  75.8 1.2 collective-permute-start.3
  77.0 1.6 %collective-permute-done.3 = f32[1152,128]{1,0:T(8,128)S(1)} collective-permute-done((f32[1152,128]{1,0:T(8,128)S(1)}, f32[1152,128]{1,0:T(8,128)S(1)}, u32[]{:S(2)}, u32[]{:S(2)}) %collective-permute-start.3) | collective-permute-done | bytes 589856 | tf_op jit(solution)/shard_map/ppermute | solution.py:26
  78.8 3.1 %collective-permute-start.4 = (f32[288,128]{1,0:T(8,128)S(1)}, f32[288,128]{1,0:T(8,128)S(1)}, u32[]{:S(2)}, u32[]{:S(2)}) collective-permute-start(f32[288,128]{1,0:T(8,128)S(1)} %get-tuple-element.27), channel_id=1, source_target_pairs={{0,8},{8,0},{16,24},{24,16},{1,9},{9,1},{17,25},{25,17},{2,10},{10... | collective-permute-start | bytes 442376 | tf_op jit(solution)/shard_map/ppermute | solution.py:26
  81.9 4.1 %collective-permute-start.5 = (f32[288,128]{1,0:T(8,128)S(1)}, f32[288,128]{1,0:T(8,128)S(1)}, u32[]{:S(2)}, u32[]{:S(2)}) collective-permute-start(f32[288,128]{1,0:T(8,128)S(1)} %get-tuple-element.29), channel_id=1, source_target_pairs={{0,16},{8,24},{16,0},{24,8},{1,17},{9,25},{17,1},{25,9},{2,18},{10... | collective-permute-start | bytes 442376 | tf_op jit(solution)/shard_map/ppermute | solution.py:26
  86.0 5.8 %collective-permute-done.5 = f32[288,128]{1,0:T(8,128)S(1)} collective-permute-done((f32[288,128]{1,0:T(8,128)S(1)}, f32[288,128]{1,0:T(8,128)S(1)}, u32[]{:S(2)}, u32[]{:S(2)}) %collective-permute-start.5) | collective-permute-done | bytes 147488 | tf_op jit(solution)/shard_map/ppermute | solution.py:26
  93.0 2.9 %collective-permute-done.7 = f32[144,128]{1,0:T(8,128)S(1)} collective-permute-done((f32[144,128]{1,0:T(8,128)S(1)}, f32[144,128]{1,0:T(8,128)S(1)}, u32[]{:S(2)}, u32[]{:S(2)}) %collective-permute-start.7) | collective-permute-done | bytes 73760 | tf_op jit(solution)/shard_map/ppermute | solution.py:26
  96.3 3.9 %collective-permute-done.8 = f32[72,128]{1,0:T(8,128)S(1)} collective-permute-done((f32[72,128]{1,0:T(8,128)S(1)}, f32[72,128]{1,0:T(8,128)S(1)}, u32[]{:S(2)}, u32[]{:S(2)}) %collective-permute-start.8) | collective-permute-done | bytes 36896 | tf_op jit(solution)/shard_map/ppermute | solution.py:26
  100.2 3.7 %collective-permute-done.9 = f32[72,128]{1,0:T(8,128)S(1)} collective-permute-done((f32[72,128]{1,0:T(8,128)S(1)}, f32[72,128]{1,0:T(8,128)S(1)}, u32[]{:S(2)}, u32[]{:S(2)}) %collective-permute-start.9) | collective-permute-done | bytes 36896 | tf_op jit(solution)/shard_map/ppermute | solution.py:26
  104.0 3.2 %collective-permute-done.10 = f32[144,128]{1,0:T(8,128)S(1)} collective-permute-done((f32[144,128]{1,0:T(8,128)S(1)}, f32[144,128]{1,0:T(8,128)S(1)}, u32[]{:S(2)}, u32[]{:S(2)}) %collective-permute-start.10) | collective-permute-done | bytes 73760 | tf_op jit(solution)/shard_map/ppermute | solution.py:26
  107.3 1.4 %collective-permute-start.11 = (f32[288,128]{1,0:T(8,128)S(1)}, f32[288,128]{1,0:T(8,128)S(1)}, u32[]{:S(2)}, u32[]{:S(2)}) collective-permute-start(f32[288,128]{1,0:T(8,128)S(1)} %get-tuple-element.34), channel_id=1, source_target_pairs={{0,8},{8,0},{16,24},{24,16},{1,9},{9,1},{17,25},{25,17},{2,10},{10... | collective-permute-start | bytes 442376 | tf_op jit(solution)/shard_map/ppermute | solution.py:26
  109.0 1.0 collective-permute-start.13
  110.0 1.3 %collective-permute-done.11 = f32[288,128]{1,0:T(8,128)S(1)} collective-permute-done((f32[288,128]{1,0:T(8,128)S(1)}, f32[288,128]{1,0:T(8,128)S(1)}, u32[]{:S(2)}, u32[]{:S(2)}) %collective-permute-start.11) | collective-permute-done | bytes 147488 | tf_op jit(solution)/shard_map/ppermute | solution.py:26
  111.4 2.9 %collective-permute-done.12 = f32[288,128]{1,0:T(8,128)S(1)} collective-permute-done((f32[288,128]{1,0:T(8,128)S(1)}, f32[288,128]{1,0:T(8,128)S(1)}, u32[]{:S(2)}, u32[]{:S(2)}) %collective-permute-start.12) | collective-permute-done | bytes 147488 | tf_op jit(solution)/shard_map/ppermute | solution.py:26
  114.5 7.8 %collective-permute-start.14 = (f32[1152,128]{1,0:T(8,128)S(1)}, f32[1152,128]{1,0:T(8,128)S(1)}, u32[]{:S(2)}, u32[]{:S(2)}) collective-permute-start(f32[1152,128]{1,0:T(8,128)S(1)} %get-tuple-element.21), channel_id=1, source_target_pairs={{0,1},{1,0},{2,3},{3,2},{4,5},{5,4},{6,7},{7,6},{8,9},{9,8},{10,11... | collective-permute-start | bytes 1769480 | tf_op jit(solution)/shard_map/ppermute | solution.py:26
  122.3 1.3 convolution_bitcast_fusion.1
  123.6 2.4 %fusion.10 = bf16[128,32,64]{0,2,1:T(8,128)(2,1)S(1)} fusion(f32[128,32,64]{0,2,1:T(8,128)S(1)} %convolution_bitcast_fusion.1, f32[3,32,64,128]{3,2,1,0:T(8,128)} %copy-done.1, f32[128,32]{0,1:T(8,128)S(1)} %copy.112, f32[32]{0:T(128)S(1)} %copy-done.30, f32[32]{0:T(128)S(1)} %copy-done.28, f32[32]{0:T(128)S(1)} %copy-done.26, pred[]{:T(512)S(6)} %gt.24, ...), kind=kOutput, calls=%fused_computation.34 | convolution fusion | flops 70254592 | bytes 4768131 | tf_op jit(solution)/shard_map/tn,hpn->thp/dot_general | solution.py:184
  126.0 1.0 copy.121
  127.7 1.1 fusion.13
  (153 shorter events, 21.8 us)
Async XLA Ops:
  0.6 28.6 %copy-start = (bf16[128,2304]{1,0:T(8,128)(2,1)S(1)}, bf16[128,2304]{1,0:T(8,128)(2,1)}, u32[]{:S(2)}) copy-start(bf16[128,2304]{1,0:T(8,128)(2,1)} %param.11) | copy-start | bytes 1769476
  0.6 13.8 %copy-start.16 = (s32[4096]{0:T(1024)S(1)}, s32[4096]{0:T(1024)}, u32[]{:S(2)}) copy-start(s32[4096]{0:T(1024)} %param.10) | copy-start | bytes 49156
  3.6 13.8 %all-to-all-start = ((f32[32,1,16]{2,1,0:T(1,128)}), f32[32,1,16]{2,1,0:T(1,128)S(1)}, u32[]{:S(2)}, u32[]{:S(2)}) async-start(f32[32,1,16]{2,1,0:T(1,128)} %copy.100), calls=%async_computation | async-start | bytes 32768 | tf_op jit(solution)/shard_map/all_to_all | solution.py:91
  14.6 17.4 %copy-start.20 = (f32[128]{0:T(128)}, f32[128]{0:T(128)S(1)}, u32[]{:S(2)}) copy-start(f32[128]{0:T(128)S(1)} %add_multiply_fusion) | copy-start | bytes 1540
  20.1 50.3 %collective-permute-start = (f32[128,2048]{0,1:T(8,128)}, f32[128,2048]{0,1:T(8,128)}, u32[]{:S(2)}, u32[]{:S(2)}) collective-permute-start(f32[128,2048]{0,1:T(8,128)} %convert_bitcast_fusion), channel_id=1, source_target_pairs={{24,16},{8,0},{25,17},{9,1},{26,18},{10,2},{27,19},{11,3},{28,20},... | collective-permute-start | bytes 3145736 | tf_op jit(solution)/shard_map/ppermute | solution.py:155
  21.4 49.0 %collective-permute-start.1 = (f32[128,2048]{0,1:T(8,128)}, f32[128,2048]{0,1:T(8,128)}, u32[]{:S(2)}, u32[]{:S(2)}) collective-permute-start(f32[128,2048]{0,1:T(8,128)} %convert_bitcast_fusion), channel_id=1, source_target_pairs={{24,8},{16,0},{25,9},{17,1},{26,10},{18,2},{27,11},{19,3},{28,12},... | collective-permute-start | bytes 3145736 | tf_op jit(solution)/shard_map/ppermute | solution.py:156
  22.7 47.7 %collective-permute-start.2 = (f32[128,2048]{0,1:T(8,128)}, f32[128,2048]{0,1:T(8,128)}, u32[]{:S(2)}, u32[]{:S(2)}) collective-permute-start(f32[128,2048]{0,1:T(8,128)} %convert_bitcast_fusion), channel_id=1, source_target_pairs={{16,8},{24,0},{17,9},{25,1},{18,10},{26,2},{19,11},{27,3},{20,12},... | collective-permute-start | bytes 3145736 | tf_op jit(solution)/shard_map/ppermute | solution.py:157
  24.8 1.4 %copy-start.31 = (bf16[128,32]{0,1:T(8,128)(2,1)S(1)}, bf16[128,32]{0,1:T(8,128)(2,1)}, u32[]{:S(2)}) copy-start(bf16[128,32]{0,1:T(8,128)(2,1)} %param.12) | copy-start | bytes 24580
  24.8 1.4 %copy-start.32 = (f32[32]{0:T(128)S(1)}, f32[32]{0:T(128)}, u32[]{:S(2)}) copy-start(f32[32]{0:T(128)} %param.13) | copy-start | bytes 388
  24.8 3.4 %copy-start.22 = (f32[32]{0:T(128)S(1)}, f32[32]{0:T(128)}, u32[]{:S(2)}) copy-start(f32[32]{0:T(128)} %param.14) | copy-start | bytes 388
  30.9 2.4 %copy-start.23 = (f32[1,128]{1,0:T(1,128)}, f32[1,128]{1,0:T(1,128)S(1)}, u32[]{:S(2)}) copy-start(f32[1,128]{1,0:T(1,128)S(1)} %constant_dynamic-slice_fusion.6) | copy-start | bytes 1540
  31.9 1.4 %copy-start.11 = (f32[128,32]{0,1:T(8,128)}, f32[128,32]{0,1:T(8,128)S(1)}, u32[]{:S(2)}) copy-start(f32[128,32]{0,1:T(8,128)S(1)} %get-tuple-element.51) | copy-start | bytes 49156
  42.6 6.6 %copy-start.4 = (f32[4,128,32]{2,1,0:T(8,128)S(1)}, f32[4,128,32]{2,1,0:T(8,128)}, u32[]{:S(2)}) copy-start(f32[4,128,32]{2,1,0:T(8,128)} %exp.40) | copy-start | bytes 196612
  59.6 3.6 %copy-start.7 = (f32[128,32]{1,0:T(8,128)S(1)}, f32[128,32]{1,0:T(8,128)}, u32[]{:S(2)}) copy-start(f32[128,32]{1,0:T(8,128)} %exp.39) | copy-start | bytes 49156
  64.9 2.5 %copy-start.29 = (f32[32]{0:T(128)}, f32[32]{0:T(128)S(1)}, u32[]{:S(2)}) copy-start(f32[32]{0:T(128)S(1)} %get-tuple-element.47) | copy-start | bytes 388
  64.9 8.1 %copy-start.25 = (f32[32]{0:T(128)}, f32[32]{0:T(128)S(1)}, u32[]{:S(2)}) copy-start(f32[32]{0:T(128)S(1)} %get-tuple-element.49) | copy-start | bytes 388
  65.0 8.4 %copy-start.27 = (f32[32]{0:T(128)}, f32[32]{0:T(128)S(1)}, u32[]{:S(2)}) copy-start(f32[32]{0:T(128)S(1)} %get-tuple-element.48) | copy-start | bytes 388
  65.0 2.5 %copy-start.15 = (f32[128,128]{0,1:T(8,128)S(1)}, f32[128,128]{0,1:T(8,128)}, u32[]{:S(2)}) copy-start(f32[128,128]{0,1:T(8,128)} %fusion.77) | copy-start | bytes 196612
  67.5 1.7 %copy-start.1 = (f32[3,32,64,128]{3,2,1,0:T(8,128)}, f32[3,32,64,128]{3,2,1,0:T(8,128)S(1)}, u32[]{:S(2)}) copy-start(f32[3,32,64,128]{3,2,1,0:T(8,128)S(1)} %fusion.3) | copy-start | bytes 9437188
  67.5 1.6 %copy-start.12 = (f32[128,128]{0,1:T(8,128)S(1)}, f32[128,128]{0,1:T(8,128)}, u32[]{:S(2)}) copy-start(f32[128,128]{0,1:T(8,128)} %fusion.80) | copy-start | bytes 196612
  67.5 1.6 %copy-start.17 = (f32[32,128]{1,0:T(8,128)S(1)}, f32[32,128]{1,0:T(8,128)}, u32[]{:S(2)}) copy-start(f32[32,128]{1,0:T(8,128)} %copy.105) | copy-start | bytes 49156
  67.5 1.6 %copy-start.18 = (pred[128,128]{0,1:T(8,128)(4,1)S(1)}, pred[128,128]{0,1:T(8,128)(4,1)}, u32[]{:S(2)}) copy-start(pred[128,128]{0,1:T(8,128)(4,1)} %iota_compare_fusion) | copy-start | bytes 49156
  67.5 1.6 %copy-start.33 = (f32[32,128]{1,0:T(8,128)S(1)}, f32[32,128]{1,0:T(8,128)}, u32[]{:S(2)}) copy-start(f32[32,128]{1,0:T(8,128)} %get-tuple-element.50) | copy-start | bytes 49156
  69.1 1.4 %copy-start.8 = (f32[128,32]{0,1:T(8,128)S(1)}, f32[128,32]{0,1:T(8,128)}, u32[]{:S(2)}) copy-start(f32[128,32]{0,1:T(8,128)} %copy.115) | copy-start | bytes 49156
  69.1 1.4 %copy-start.9 = (f32[128,32]{0,1:T(8,128)S(1)}, f32[128,32]{0,1:T(8,128)}, u32[]{:S(2)}) copy-start(f32[128,32]{0,1:T(8,128)} %copy.116) | copy-start | bytes 49156
  69.1 1.4 %copy-start.10 = (f32[128,32]{0,1:T(8,128)S(1)}, f32[128,32]{0,1:T(8,128)}, u32[]{:S(2)}) copy-start(f32[128,32]{0,1:T(8,128)} %copy.117) | copy-start | bytes 49156
  73.3 1.4 %copy-start.5 = (bf16[128,2048]{0,1:T(8,128)(2,1)S(1)}, bf16[128,2048]{0,1:T(8,128)(2,1)}, u32[]{:S(2)}) copy-start(bf16[128,2048]{0,1:T(8,128)(2,1)} %copy.102) | copy-start | bytes 1572868
  73.4 1.4 %copy-start.14 = (f32[128,128]{0,1:T(8,128)S(1)}, f32[128,128]{0,1:T(8,128)}, u32[]{:S(2)}) copy-start(f32[128,128]{0,1:T(8,128)} %fusion.82) | copy-start | bytes 196612
  73.7 1.5 %copy-start.21 = (f32[128]{0:T(128)S(1)}, f32[128]{0:T(128)}, u32[]{:S(2)}) copy-start(f32[128]{0:T(128)} %copy-done.20) | copy-start | bytes 1540
  73.7 1.5 %copy-start.24 = (f32[1,128]{1,0:T(1,128)S(1)}, f32[1,128]{1,0:T(1,128)}, u32[]{:S(2)}) copy-start(f32[1,128]{1,0:T(1,128)} %copy-done.23) | copy-start | bytes 1540
  75.8 2.9 %collective-permute-start.3 = (f32[1152,128]{1,0:T(8,128)S(1)}, f32[1152,128]{1,0:T(8,128)S(1)}, u32[]{:S(2)}, u32[]{:S(2)}) collective-permute-start(f32[1152,128]{1,0:T(8,128)S(1)} %constant_dynamic-slice_fusion.5), channel_id=1, source_target_pairs={{0,1},{1,0},{2,3},{3,2},{4,5},{5,4},{6,7},{7,6},{8,9},{9,8},{10,11... | collective-permute-start | bytes 1769480 | tf_op jit(solution)/shard_map/ppermute | solution.py:26
  78.8 7.2 %collective-permute-start.4 = (f32[288,128]{1,0:T(8,128)S(1)}, f32[288,128]{1,0:T(8,128)S(1)}, u32[]{:S(2)}, u32[]{:S(2)}) collective-permute-start(f32[288,128]{1,0:T(8,128)S(1)} %get-tuple-element.27), channel_id=1, source_target_pairs={{0,8},{8,0},{16,24},{24,16},{1,9},{9,1},{17,25},{25,17},{2,10},{10... | collective-permute-start | bytes 442376 | tf_op jit(solution)/shard_map/ppermute | solution.py:26
  81.9 9.9 %collective-permute-start.5 = (f32[288,128]{1,0:T(8,128)S(1)}, f32[288,128]{1,0:T(8,128)S(1)}, u32[]{:S(2)}, u32[]{:S(2)}) collective-permute-start(f32[288,128]{1,0:T(8,128)S(1)} %get-tuple-element.29), channel_id=1, source_target_pairs={{0,16},{8,24},{16,0},{24,8},{1,17},{9,25},{17,1},{25,9},{2,18},{10... | collective-permute-start | bytes 442376 | tf_op jit(solution)/shard_map/ppermute | solution.py:26
  86.0 6.6 %collective-permute-start.6 = (f32[288,128]{1,0:T(8,128)S(1)}, f32[288,128]{1,0:T(8,128)S(1)}, u32[]{:S(2)}, u32[]{:S(2)}) collective-permute-start(f32[288,128]{1,0:T(8,128)S(1)} %get-tuple-element.28), channel_id=1, source_target_pairs={{0,24},{8,16},{16,8},{24,0},{1,25},{9,17},{17,9},{25,1},{2,26},{10... | collective-permute-start | bytes 442376 | tf_op jit(solution)/shard_map/ppermute | solution.py:26
  92.7 3.3 %collective-permute-start.7 = (f32[144,128]{1,0:T(8,128)S(1)}, f32[144,128]{1,0:T(8,128)S(1)}, u32[]{:S(2)}, u32[]{:S(2)}) collective-permute-start(f32[144,128]{1,0:T(8,128)S(1)} %constant_dynamic-slice_fusion.1), channel_id=1, source_target_pairs={{0,2},{1,3},{2,0},{3,1},{4,6},{5,7},{6,4},{7,5},{8,10},{9,11},{10,... | collective-permute-start | bytes 221192 | tf_op jit(solution)/shard_map/ppermute | solution.py:26
  96.0 4.2 %collective-permute-start.8 = (f32[72,128]{1,0:T(8,128)S(1)}, f32[72,128]{1,0:T(8,128)S(1)}, u32[]{:S(2)}, u32[]{:S(2)}) collective-permute-start(f32[72,128]{1,0:T(8,128)S(1)} %constant_dynamic-slice_fusion), channel_id=1, source_target_pairs={{0,4},{1,5},{2,6},{3,7},{4,0},{5,1},{6,2},{7,3},{8,12},{9,13},{10,... | collective-permute-start | bytes 110600 | tf_op jit(solution)/shard_map/ppermute | solution.py:26
  100.2 3.7 %collective-permute-start.9 = (f32[72,128]{1,0:T(8,128)S(1)}, f32[72,128]{1,0:T(8,128)S(1)}, u32[]{:S(2)}, u32[]{:S(2)}) collective-permute-start(f32[72,128]{1,0:T(8,128)S(1)} %dynamic-slice_add_fusion.2), channel_id=1, source_target_pairs={{0,4},{1,5},{2,6},{3,7},{4,0},{5,1},{6,2},{7,3},{8,12},{9,13},{10,... | collective-permute-start | bytes 110600 | tf_op jit(solution)/shard_map/ppermute | solution.py:26
  103.9 3.3 %collective-permute-start.10 = (f32[144,128]{1,0:T(8,128)S(1)}, f32[144,128]{1,0:T(8,128)S(1)}, u32[]{:S(2)}, u32[]{:S(2)}) collective-permute-start(f32[144,128]{1,0:T(8,128)S(1)} %get-tuple-element.37), channel_id=1, source_target_pairs={{0,2},{1,3},{2,0},{3,1},{4,6},{5,7},{6,4},{7,5},{8,10},{9,11},{10,... | collective-permute-start | bytes 221192 | tf_op jit(solution)/shard_map/ppermute | solution.py:26
  107.3 15.0 %copy-start.6 = (bf16[128,2048]{0,1:T(8,128)(2,1)S(1)}, bf16[128,2048]{0,1:T(8,128)(2,1)}, u32[]{:S(2)}) copy-start(bf16[128,2048]{0,1:T(8,128)(2,1)} %copy.102) | copy-start | bytes 1572868
  107.3 15.0 %copy-start.13 = (f32[128,128]{0,1:T(8,128)S(1)}, f32[128,128]{0,1:T(8,128)}, u32[]{:S(2)}) copy-start(f32[128,128]{0,1:T(8,128)} %fusion.80) | copy-start | bytes 196612
  107.3 15.0 %copy-start.19 = (pred[128,128]{0,1:T(8,128)(4,1)S(1)}, pred[128,128]{0,1:T(8,128)(4,1)}, u32[]{:S(2)}) copy-start(pred[128,128]{0,1:T(8,128)(4,1)} %iota_compare_fusion) | copy-start | bytes 49156
  107.3 15.0 %copy-start.34 = (f32[32,128]{1,0:T(8,128)S(1)}, f32[32,128]{1,0:T(8,128)}, u32[]{:S(2)}) copy-start(f32[32,128]{1,0:T(8,128)} %get-tuple-element.50) | copy-start | bytes 49156
  107.3 4.1 %collective-permute-start.11 = (f32[288,128]{1,0:T(8,128)S(1)}, f32[288,128]{1,0:T(8,128)S(1)}, u32[]{:S(2)}, u32[]{:S(2)}) collective-permute-start(f32[288,128]{1,0:T(8,128)S(1)} %get-tuple-element.34), channel_id=1, source_target_pairs={{0,8},{8,0},{16,24},{24,16},{1,9},{9,1},{17,25},{25,17},{2,10},{10... | collective-permute-start | bytes 442376 | tf_op jit(solution)/shard_map/ppermute | solution.py:26
  108.7 5.6 %collective-permute-start.12 = (f32[288,128]{1,0:T(8,128)S(1)}, f32[288,128]{1,0:T(8,128)S(1)}, u32[]{:S(2)}, u32[]{:S(2)}) collective-permute-start(f32[288,128]{1,0:T(8,128)S(1)} %get-tuple-element.34), channel_id=1, source_target_pairs={{0,16},{8,24},{16,0},{24,8},{1,17},{9,25},{17,1},{25,9},{2,18},{10... | collective-permute-start | bytes 442376 | tf_op jit(solution)/shard_map/ppermute | solution.py:26
  109.0 5.3 %collective-permute-start.13 = (f32[288,128]{1,0:T(8,128)S(1)}, f32[288,128]{1,0:T(8,128)S(1)}, u32[]{:S(2)}, u32[]{:S(2)}) collective-permute-start(f32[288,128]{1,0:T(8,128)S(1)} %get-tuple-element.34), channel_id=1, source_target_pairs={{0,24},{8,16},{16,8},{24,0},{1,25},{9,17},{17,9},{25,1},{2,26},{10... | collective-permute-start | bytes 442376 | tf_op jit(solution)/shard_map/ppermute | solution.py:26
  114.5 12.6 %collective-permute-start.14 = (f32[1152,128]{1,0:T(8,128)S(1)}, f32[1152,128]{1,0:T(8,128)S(1)}, u32[]{:S(2)}, u32[]{:S(2)}) collective-permute-start(f32[1152,128]{1,0:T(8,128)S(1)} %get-tuple-element.21), channel_id=1, source_target_pairs={{0,1},{1,0},{2,3},{3,2},{4,5},{5,4},{6,7},{7,6},{8,9},{9,8},{10,11... | collective-permute-start | bytes 1769480 | tf_op jit(solution)/shard_map/ppermute | solution.py:26
  122.3 1.3 %copy-start.26 = (f32[32]{0:T(128)S(1)}, f32[32]{0:T(128)}, u32[]{:S(2)}) copy-start(f32[32]{0:T(128)} %copy-done.25) | copy-start | bytes 388
  122.3 1.3 %copy-start.28 = (f32[32]{0:T(128)S(1)}, f32[32]{0:T(128)}, u32[]{:S(2)}) copy-start(f32[32]{0:T(128)} %copy-done.27) | copy-start | bytes 388
  (3 other events, 2.8 us)
